TPU v7x, 32 devices: a whole 2x2x4 slice. The times are simulated.
32 devices in a mesh: videos: 2 (over y), ha: 4 (over z), wa: 2 (over x), ta: 2 (over core).
Axes of the slice: x: 2, y: 2, z: 4, core: 2. Of those that a mesh axis runs over, the one named last changes fastest.
Arguments:
- latents: bfloat16 [12, 8, 64, 512], P(('videos', 'ta'), 'ha', 'wa'), parts along dimension 0, may hold values from -200 to 200
- norm1_gain: float32 [512], replicated, may hold values from 0.25 to 1.75
- norm1_shift: float32 [512], replicated, may hold values from -2.5 to 2.5
- up_weight: bfloat16 [3, 3, 512, 256], replicated, may hold values from -0.1875 to 0.1875
- norm2_gain: float32 [256], replicated, may hold values from 0.25 to 1.75
- norm2_shift: float32 [256], replicated, may hold values from -2.5 to 2.5
- conv_a: bfloat16 [3, 3, 3, 256, 256], replicated, may hold values from -0.078125 to 0.078125
- norm3_gain: float32 [256], replicated, may hold values from 0.25 to 1.75
- norm3_shift: float32 [256], replicated, may hold values from -2.5 to 2.5
- conv_b: bfloat16 [3, 3, 3, 256, 256], replicated, may hold values from -0.078125 to 0.078125
Outputs:
- decoded: bfloat16 [12, 16, 128, 256], P(('videos', 'ta'), 'ha', 'wa'), parts along dimension 0
There are 2 independent parts, one for each index of `videos`. A program takes and returns all parts, laid end to end along the dimension named above; an argument that names none is the same for every part. Nothing has to cross between parts.
All inputs are finite; a program needn't handle non-finite values.
Results may differ from a plain program's by a relative error of at most 0.008.
Values may be sent and summed in bfloat16 or wider, within the bound.
No kernel may reach another device: no remote copies, remote signals or barrier semaphores. Data moves between devices by JAX's collectives and lax.ppermute only.
A program may use at most 64 MiB of HBM per device.

v0:
```python
import jax
import jax.numpy as jnp
from jax import lax
from jax.sharding import PartitionSpec as P

GROUPS = 32


EPSILON = 1e-06


def passed_along(block, axis, distance):
    devices = range(lax.axis_size(axis))
    route = [(i - distance, i) for i in devices if i - distance in devices]
    return lax.ppermute(block, axis, route)


def padded_2(x, sides, width):
    for axis, dim in sides:
        size, length = (lax.axis_size(axis), x.shape[dim])
        up = [(i, (i + 1) % size) for i in range(size - 1)]
        down = [(j, i) for i, j in up]
        last = lax.slice_in_dim(x, length - width, length, axis=dim)
        initial = lax.slice_in_dim(x, 0, width, axis=dim)
        before = lax.ppermute(last, axis, up)
        after = lax.ppermute(initial, axis, down)
        x = jnp.concatenate([before, x, after], axis=dim)
    return x


def activate(values, sample, scale_vec, shift_vec):
    channels = values.shape[-1]
    group_width = channels // GROUPS
    grouped = sample.reshape(-1, GROUPS, group_width)
    entries = (
        grouped.shape[0]
        * group_width
        * lax.axis_size("ha")
        * lax.axis_size("wa")
        * lax.axis_size("ta")
    )
    totals, squares = lax.psum(
        (jnp.sum(grouped, axis=(0, 2)), jnp.sum(grouped * grouped, axis=(0, 2))), ("ha", "wa", "ta")
    )
    average = totals / entries
    spread = squares / entries - average * average
    scaling = lax.rsqrt(spread + EPSILON)
    normed = (values - jnp.repeat(average, group_width)) * jnp.repeat(
        scaling, group_width
    ) * scale_vec + shift_vec
    return jax.nn.silu(normed).astype(jnp.bfloat16)


def parity_merge(lead_part, mid_part, tail_part, axis_pos):
    pad_end = [(0, 0)] * lead_part.ndim
    pad_front = [(0, 0)] * lead_part.ndim
    pad_end[axis_pos] = (0, 1)
    pad_front[axis_pos] = (1, 0)
    even_part = jnp.pad(lead_part, pad_end) + jnp.pad(tail_part, pad_front)
    odd_part = jnp.pad(mid_part, pad_end)
    stacked = jnp.stack([even_part, odd_part], axis=axis_pos + 1)
    new_shape = list(even_part.shape)
    new_shape[axis_pos] = new_shape[axis_pos] * 2
    return stacked.reshape(new_shape)


def spread_taps(source, kernel):
    frames, height, across, channels = source.shape
    flattened = source.reshape(-1, channels)
    products = [
        [
            jnp.dot(flattened, kernel[tap_y, tap_x], preferred_element_type=jnp.float32).reshape(
                frames, height, across, -1
            )
            for tap_x in range(3)
        ]
        for tap_y in range(3)
    ]
    columns = [
        parity_merge(products[0][tap_x], products[1][tap_x], products[2][tap_x], 1)
        for tap_x in range(3)
    ]
    return parity_merge(columns[0], columns[1], columns[2], 2)


def valid_conv(padded, kernel, frames, height, across):
    result = jnp.zeros((frames * height * across, kernel.shape[-1]), jnp.float32)
    for step_t in range(3):
        for step_y in range(3):
            for step_x in range(3):
                window = padded[
                    step_t : step_t + frames, step_y : step_y + height, step_x : step_x + across
                ]
                result = result + jnp.dot(
                    window.reshape(-1, window.shape[-1]),
                    kernel[step_t, step_y, step_x],
                    preferred_element_type=jnp.float32,
                )
    return result.reshape(frames, height, across, -1)


def causal_extend(values):
    earlier = passed_along(values[-2:], "ta", 1)
    opening = jnp.concatenate([values[:1], values[:1]], axis=0)
    earlier = jnp.where(lax.axis_index("ta") == 0, opening, earlier)
    return jnp.concatenate([earlier, values], axis=0)


def bordered_one(values):
    return padded_2(values, (("ha", 1), ("wa", 2)), 1)


def per_device(
    latents,
    norm1_gain,
    norm1_shift,
    up_weight,
    norm2_gain,
    norm2_shift,
    conv_a,
    norm3_gain,
    norm3_shift,
    conv_b,
):
    frames, height, across, channels = latents.shape
    latent_f = latents.astype(jnp.float32)
    activated = activate(latent_f, latent_f, norm1_gain, norm1_shift)
    spilled = spread_taps(activated, up_weight)
    from_below = passed_along(spilled[:, 0], "ha", -1)
    row_fixed = spilled[:, 1 : 2 * height + 1]
    row_fixed = jnp.concatenate(
        [row_fixed[:, :-1], row_fixed[:, -1:] + from_below[:, None]], axis=1
    )
    beside = passed_along(row_fixed[:, :, 0], "wa", -1)
    lifted = jnp.concatenate(
        [
            row_fixed[:, :, 1 : 2 * across],
            row_fixed[:, :, 2 * across : 2 * across + 1] + beside[:, :, None],
        ],
        axis=2,
    )
    lifted = lifted.astype(jnp.bfloat16)
    lifted_f = lifted.astype(jnp.float32)
    first_act = activate(lifted_f, lifted_f, norm2_gain, norm2_shift)
    out_h = 2 * height
    out_w = 2 * across
    hidden = valid_conv(
        bordered_one(causal_extend(first_act)), conv_a, frames, out_h, out_w
    ).astype(jnp.bfloat16)
    hidden_f = hidden.astype(jnp.float32)
    second_act = activate(hidden_f, hidden_f, norm3_gain, norm3_shift)
    framed = bordered_one(causal_extend(second_act))
    branch = valid_conv(framed, conv_b, frames, out_h, out_w)
    return (lifted_f + branch).astype(jnp.bfloat16)


def solution(mesh):
    return jax.shard_map(
        per_device,
        mesh=mesh,
        in_specs=(
            P(("videos", "ta"), "ha", "wa", None),
            P(),
            P(),
            P(),
            P(),
            P(),
            P(),
            P(),
            P(),
            P(),
        ),
        out_specs=P(("videos", "ta"), "ha", "wa", None),
        check_vma=False,
    )
```

profile of v0, /device:TPU:0, one launch (start us, length us, event | category | flops | bytes accessed | tf_op | source)
XLA Modules:
  0.0 204.1 jit_solution(1638593344820532898)
XLA Ops:
  0.0 1.0 convert_reduce_fusion.1
  1.4 34.9 %all-reduce.14 = (f32[32]{0:T(128)S(1)}, f32[32]{0:T(128)S(1)}) all-reduce(f32[32]{0:T(128)S(1)} %reduce_sum.77, f32[32]{0:T(128)S(1)} %reduce_sum.74), channel_id=1, replica_groups=mesh['videos'=2,'ha'=4,'wa'=2,'ta'=2] {'ha','wa','ta'}, use_global_device_ids=true, to_apply=%region_5.6 | all-reduce | flops 64 | bytes 512 | tf_op jit(solution)/shard_map/psum | solution.py:42
  36.6 1.1 fusion.25
  37.7 1.2 fusion.38
  38.9 1.2 fusion.41
  40.1 1.2 fusion.43
  41.2 1.2 fusion.46
  42.4 1.2 fusion.48
  43.6 1.2 fusion.51
  44.8 1.2 fusion.2
  46.1 1.2 fusion.3
  47.4 1.2 fusion.4
  49.0 0.9 copy.94
  50.9 1.3 collective-permute-start
  52.6 6.2 %collective-permute-done = f32[3,66,256]{2,1,0:T(8,128)S(1)} collective-permute-done((f32[3,66,256]{2,1,0:T(8,128)S(1)}, f32[3,66,256]{2,1,0:T(8,128)S(1)}, u32[]{:S(2)}, u32[]{:S(2)}) %collective-permute-start) | collective-permute-done | bytes 202784 | tf_op jit(solution)/shard_map/ppermute | solution.py:15
  59.0 1.3 collective-permute-start.1
  60.7 3.9 %collective-permute-done.1 = f32[3,4,256]{2,1,0:T(4,128)S(1)} collective-permute-done((f32[3,4,256]{2,1,0:T(4,128)S(1)}, f32[3,4,256]{2,1,0:T(4,128)S(1)}, u32[]{:S(2)}, u32[]{:S(2)}) %collective-permute-start.1) | collective-permute-done | bytes 12320 | tf_op jit(solution)/shard_map/ppermute | solution.py:15
  65.5 29.5 %all-reduce.13 = (f32[32]{0:T(128)S(1)}, f32[32]{0:T(128)S(1)}) all-reduce(f32[32]{0:T(128)S(1)} %reduce_sum.89, f32[32]{0:T(128)S(1)} %reduce_sum.83), channel_id=1, replica_groups=mesh['videos'=2,'ha'=4,'wa'=2,'ta'=2] {'ha','wa','ta'}, use_global_device_ids=true, to_apply=%region_11.12 | all-reduce | flops 64 | bytes 512 | tf_op jit(solution)/shard_map/psum | solution.py:42
  96.0 1.8 collective-permute-start.2
  97.9 1.1 collective-permute-done.2
  99.1 0.8 fusion.36
  100.0 1.3 collective-permute-start.4
  101.3 4.6 %collective-permute-start.3 = (bf16[5,1,64,256]{3,1,2,0:T(2,128)(2,1)S(1)}, bf16[5,1,64,256]{3,1,2,0:T(2,128)(2,1)S(1)}, u32[]{:S(2)}, u32[]{:S(2)}) collective-permute-start(bf16[5,1,64,256]{3,1,2,0:T(2,128)(2,1)S(1)} %get-tuple-element.81), channel_id=1, source_target_pairs={{0,4},{4,8},{8,12},{1,5},{5,9},{9,13},{2,6},{6,10},{10,14},{3,7},{... | collective-permute-start | bytes 491528 | tf_op jit(solution)/shard_map/ppermute | solution.py:25
  105.9 5.9 %collective-permute-done.4 = bf16[5,1,64,256]{3,1,2,0:T(2,128)(2,1)S(1)} collective-permute-done((bf16[5,1,64,256]{3,1,2,0:T(2,128)(2,1)S(1)}, bf16[5,1,64,256]{3,1,2,0:T(2,128)(2,1)S(1)}, u32[]{:S(2)}, u32[]{:S(2)}) %collective-permute-start.4) | collective-permute-done | bytes 163872 | tf_op jit(solution)/shard_map/ppermute | solution.py:26
  111.9 1.2 collective-permute-done.3
  113.1 1.3 collective-permute-start.5
  114.4 1.5 collective-permute-start.6
  115.9 1.0 pad_maximum_fusion.17
  117.2 1.7 pad_maximum_fusion.15
  120.1 2.3 %maximum_maximum_fusion = (bf16[5,6,65,256]{3,1,2,0:T(8,128)(2,1)S(1)}, bf16[5,6,65,256]{3,1,2,0:T(8,128)(2,1)S(1)}) fusion(bf16[5,1,64,256]{3,1,2,0:T(2,128)(2,1)S(1)} %collective-permute-done.4, bf16[3,4,64,256]{3,1,2,0:T(4,128)(2,1)S(1)} %fusion.13, bf16[2,4,64,256]{3,1,2,0:T(4,128)(2,1)S(1)} %maximum_select_fusion, ...), kind=kLoop, calls=%fused_computation.5 | loop fusion | flops 9984000 | bytes 3010560 | tf_op jit(solution)/shard_map/concatenate | solution.py:27
  122.4 1.6 fusion.182
  124.0 1.3 fusion.183
  133.7 30.7 %all-reduce.12 = (f32[32]{0:T(128)S(1)}, f32[32]{0:T(128)S(1)}) all-reduce(f32[32]{0:T(128)S(1)} %reduce_sum.113, f32[32]{0:T(128)S(1)} %reduce_sum.110), channel_id=1, replica_groups=mesh['videos'=2,'ha'=4,'wa'=2,'ta'=2] {'ha','wa','ta'}, use_global_device_ids=true, to_apply=%region_17.18 | all-reduce | flops 64 | bytes 512 | tf_op jit(solution)/shard_map/psum | solution.py:42
  165.6 1.8 collective-permute-start.7
  167.5 0.9 collective-permute-done.7
  168.5 0.8 fusion.34
  169.4 1.3 collective-permute-start.9
  170.7 4.6 %collective-permute-start.8 = (bf16[5,1,64,256]{3,1,2,0:T(2,128)(2,1)S(1)}, bf16[5,1,64,256]{3,1,2,0:T(2,128)(2,1)S(1)}, u32[]{:S(2)}, u32[]{:S(2)}) collective-permute-start(bf16[5,1,64,256]{3,1,2,0:T(2,128)(2,1)S(1)} %get-tuple-element.77), channel_id=1, source_target_pairs={{0,4},{4,8},{8,12},{1,5},{5,9},{9,13},{2,6},{6,10},{10,14},{3,7},{... | collective-permute-start | bytes 491528 | tf_op jit(solution)/shard_map/ppermute | solution.py:25
  175.3 6.0 %collective-permute-done.9 = bf16[5,1,64,256]{3,1,2,0:T(2,128)(2,1)S(1)} collective-permute-done((bf16[5,1,64,256]{3,1,2,0:T(2,128)(2,1)S(1)}, bf16[5,1,64,256]{3,1,2,0:T(2,128)(2,1)S(1)}, u32[]{:S(2)}, u32[]{:S(2)}) %collective-permute-start.9) | collective-permute-done | bytes 163872 | tf_op jit(solution)/shard_map/ppermute | solution.py:26
  181.3 1.2 collective-permute-done.8
  182.5 1.3 collective-permute-start.10
  183.8 1.3 collective-permute-start.11
  185.1 1.0 pad_maximum_fusion.8
  186.4 1.7 pad_maximum_fusion.6
  188.5 1.0 collective-permute-done.11
  189.5 2.3 %maximum_maximum_fusion.1 = (bf16[5,6,65,256]{3,1,2,0:T(8,128)(2,1)S(1)}, bf16[5,6,65,256]{3,1,2,0:T(8,128)(2,1)S(1)}) fusion(bf16[5,1,64,256]{3,1,2,0:T(2,128)(2,1)S(1)} %collective-permute-done.9, bf16[3,4,64,256]{3,1,2,0:T(4,128)(2,1)S(1)} %fusion.14, bf16[2,4,64,256]{3,1,2,0:T(4,128)(2,1)S(1)} %maximum_select_fusion.1, ...), kind=kLoop, calls=%fused_computation.7 | loop fusion | flops 9984000 | bytes 3010560 | tf_op jit(solution)/shard_map/concatenate | solution.py:27
  191.8 1.6 fusion.180
  193.4 1.2 fusion.181
  (181 shorter events, 26.1 us)
Async XLA Ops:
  50.9 44.4 %copy-start.2 = (f32[256]{0:T(256)S(1)}, f32[256]{0:T(256)}, u32[]{:S(2)}) copy-start(f32[256]{0:T(256)} %param.15) | copy-start | bytes 3076
  50.9 44.4 %copy-start.3 = (f32[256]{0:T(256)S(1)}, f32[256]{0:T(256)}, u32[]{:S(2)}) copy-start(f32[256]{0:T(256)} %param.14) | copy-start | bytes 3076
  50.9 7.8 %collective-permute-start = (f32[3,66,256]{2,1,0:T(8,128)S(1)}, f32[3,66,256]{2,1,0:T(8,128)S(1)}, u32[]{:S(2)}, u32[]{:S(2)}) collective-permute-start(f32[3,66,256]{2,1,0:T(8,128)S(1)} %get-tuple-element.53), channel_id=1, source_target_pairs={{4,0},{8,4},{12,8},{5,1},{9,5},{13,9},{6,2},{10,6},{14,10},{7,3},{... | collective-permute-start | bytes 608264 | tf_op jit(solution)/shard_map/ppermute | solution.py:15
  59.0 5.6 %collective-permute-start.1 = (f32[3,4,256]{2,1,0:T(4,128)S(1)}, f32[3,4,256]{2,1,0:T(4,128)S(1)}, u32[]{:S(2)}, u32[]{:S(2)}) collective-permute-start(f32[3,4,256]{2,1,0:T(4,128)S(1)} %fusion.176), channel_id=1, source_target_pairs={{2,0},{3,1},{6,4},{7,5},{10,8},{11,9},{14,12},{15,13},{18,16},{19,... | collective-permute-start | bytes 36872 | tf_op jit(solution)/shard_map/ppermute | solution.py:15
  96.0 2.9 %collective-permute-start.2 = (bf16[2,4,64,256]{3,1,2,0:T(4,128)(2,1)S(1)}, bf16[2,4,64,256]{3,1,2,0:T(4,128)(2,1)S(1)}, u32[]{:S(2)}, u32[]{:S(2)}) collective-permute-start(bf16[2,4,64,256]{3,1,2,0:T(4,128)(2,1)S(1)} %slice.594), channel_id=1, source_target_pairs={{0,1},{2,3},{4,5},{6,7},{8,9},{10,11},{12,13},{14,15},{16,17},{18,... | collective-permute-start | bytes 786440 | tf_op jit(solution)/shard_map/ppermute | solution.py:15
  97.9 19.0 %copy-start = (bf16[3,3,3,256,256]{4,3,2,1,0:T(8,128)(2,1)S(1)}, bf16[3,3,3,256,256]{4,3,2,1,0:T(8,128)(2,1)}, u32[]{:S(2)}) copy-start(bf16[3,3,3,256,256]{4,3,2,1,0:T(8,128)(2,1)} %param.16) | copy-start | bytes 10616836
  100.0 11.9 %collective-permute-start.4 = (bf16[5,1,64,256]{3,1,2,0:T(2,128)(2,1)S(1)}, bf16[5,1,64,256]{3,1,2,0:T(2,128)(2,1)S(1)}, u32[]{:S(2)}, u32[]{:S(2)}) collective-permute-start(bf16[5,1,64,256]{3,1,2,0:T(2,128)(2,1)S(1)} %get-tuple-element.82), channel_id=1, source_target_pairs={{4,0},{8,4},{12,8},{5,1},{9,5},{13,9},{6,2},{10,6},{14,10},{7,3},{... | collective-permute-start | bytes 491528 | tf_op jit(solution)/shard_map/ppermute | solution.py:26
  101.3 11.8 %collective-permute-start.3 = (bf16[5,1,64,256]{3,1,2,0:T(2,128)(2,1)S(1)}, bf16[5,1,64,256]{3,1,2,0:T(2,128)(2,1)S(1)}, u32[]{:S(2)}, u32[]{:S(2)}) collective-permute-start(bf16[5,1,64,256]{3,1,2,0:T(2,128)(2,1)S(1)} %get-tuple-element.81), channel_id=1, source_target_pairs={{0,4},{4,8},{8,12},{1,5},{5,9},{9,13},{2,6},{6,10},{10,14},{3,7},{... | collective-permute-start | bytes 491528 | tf_op jit(solution)/shard_map/ppermute | solution.py:25
  113.1 6.2 %collective-permute-start.5 = (bf16[5,6,1,256]{3,1,2,0:T(8,128)(2,1)S(1)}, bf16[5,6,1,256]{3,1,2,0:T(8,128)(2,1)S(1)}, u32[]{:S(2)}, u32[]{:S(2)}) collective-permute-start(bf16[5,6,1,256]{3,1,2,0:T(8,128)(2,1)S(1)} %get-tuple-element.61), channel_id=1, source_target_pairs={{0,2},{1,3},{4,6},{5,7},{8,10},{9,11},{12,14},{13,15},{16,18},{17,... | collective-permute-start | bytes 46088 | tf_op jit(solution)/shard_map/ppermute | solution.py:25
  114.4 5.7 %collective-permute-start.6 = (bf16[5,6,1,256]{3,1,2,0:T(8,128)(2,1)S(1)}, bf16[5,6,1,256]{3,1,2,0:T(8,128)(2,1)S(1)}, u32[]{:S(2)}, u32[]{:S(2)}) collective-permute-start(bf16[5,6,1,256]{3,1,2,0:T(8,128)(2,1)S(1)} %get-tuple-element.62), channel_id=1, source_target_pairs={{2,0},{3,1},{6,4},{7,5},{10,8},{11,9},{14,12},{15,13},{18,16},{19,... | collective-permute-start | bytes 46088 | tf_op jit(solution)/shard_map/ppermute | solution.py:26
  132.4 32.4 %copy-start.4 = (f32[256]{0:T(256)S(1)}, f32[256]{0:T(256)}, u32[]{:S(2)}) copy-start(f32[256]{0:T(256)} %param.18) | copy-start | bytes 3076
  132.4 32.4 %copy-start.5 = (f32[256]{0:T(256)S(1)}, f32[256]{0:T(256)}, u32[]{:S(2)}) copy-start(f32[256]{0:T(256)} %param.17) | copy-start | bytes 3076
  165.5 20.6 %copy-start.1 = (bf16[3,3,3,256,256]{4,3,2,1,0:T(8,128)(2,1)S(1)}, bf16[3,3,3,256,256]{4,3,2,1,0:T(8,128)(2,1)}, u32[]{:S(2)}) copy-start(bf16[3,3,3,256,256]{4,3,2,1,0:T(8,128)(2,1)} %param.19) | copy-start | bytes 10616836
  165.6 2.7 %collective-permute-start.7 = (bf16[2,4,64,256]{3,1,2,0:T(4,128)(2,1)S(1)}, bf16[2,4,64,256]{3,1,2,0:T(4,128)(2,1)S(1)}, u32[]{:S(2)}, u32[]{:S(2)}) collective-permute-start(bf16[2,4,64,256]{3,1,2,0:T(4,128)(2,1)S(1)} %slice.620), channel_id=1, source_target_pairs={{0,1},{2,3},{4,5},{6,7},{8,9},{10,11},{12,13},{14,15},{16,17},{18,... | collective-permute-start | bytes 786440 | tf_op jit(solution)/shard_map/ppermute | solution.py:15
  169.4 11.9 %collective-permute-start.9 = (bf16[5,1,64,256]{3,1,2,0:T(2,128)(2,1)S(1)}, bf16[5,1,64,256]{3,1,2,0:T(2,128)(2,1)S(1)}, u32[]{:S(2)}, u32[]{:S(2)}) collective-permute-start(bf16[5,1,64,256]{3,1,2,0:T(2,128)(2,1)S(1)} %get-tuple-element.78), channel_id=1, source_target_pairs={{4,0},{8,4},{12,8},{5,1},{9,5},{13,9},{6,2},{10,6},{14,10},{7,3},{... | collective-permute-start | bytes 491528 | tf_op jit(solution)/shard_map/ppermute | solution.py:26
  170.7 11.8 %collective-permute-start.8 = (bf16[5,1,64,256]{3,1,2,0:T(2,128)(2,1)S(1)}, bf16[5,1,64,256]{3,1,2,0:T(2,128)(2,1)S(1)}, u32[]{:S(2)}, u32[]{:S(2)}) collective-permute-start(bf16[5,1,64,256]{3,1,2,0:T(2,128)(2,1)S(1)} %get-tuple-element.77), channel_id=1, source_target_pairs={{0,4},{4,8},{8,12},{1,5},{5,9},{9,13},{2,6},{6,10},{10,14},{3,7},{... | collective-permute-start | bytes 491528 | tf_op jit(solution)/shard_map/ppermute | solution.py:25
  182.5 6.0 %collective-permute-start.10 = (bf16[5,6,1,256]{3,1,2,0:T(8,128)(2,1)S(1)}, bf16[5,6,1,256]{3,1,2,0:T(8,128)(2,1)S(1)}, u32[]{:S(2)}, u32[]{:S(2)}) collective-permute-start(bf16[5,6,1,256]{3,1,2,0:T(8,128)(2,1)S(1)} %get-tuple-element.57), channel_id=1, source_target_pairs={{0,2},{1,3},{4,6},{5,7},{8,10},{9,11},{12,14},{13,15},{16,18},{17,... | collective-permute-start | bytes 46088 | tf_op jit(solution)/shard_map/ppermute | solution.py:25
  183.8 5.7 %collective-permute-start.11 = (bf16[5,6,1,256]{3,1,2,0:T(8,128)(2,1)S(1)}, bf16[5,6,1,256]{3,1,2,0:T(8,128)(2,1)S(1)}, u32[]{:S(2)}, u32[]{:S(2)}) collective-permute-start(bf16[5,6,1,256]{3,1,2,0:T(8,128)(2,1)S(1)} %get-tuple-element.58), channel_id=1, source_target_pairs={{2,0},{3,1},{6,4},{7,5},{10,8},{11,9},{14,12},{15,13},{18,16},{19,... | collective-permute-start | bytes 46088 | tf_op jit(solution)/shard_map/ppermute | solution.py:26
where the time goes:
time: 205 us; the launch traced here: 204 us
  blocking collectives  95.1 us (46%)
  waiting for transfers between devices  28 us (14%)
  matrix products  24.9 us (12%)
  starting transfers between devices  23.2 us (11%)
  other arithmetic  18.4 us (9%)
  local copies, waits for them, and re-layouts  13 us (6%)
    psum x3, blocking collectives, activate(): lax.psum((jnp.sum(grouped, axis=(0, 2)), jnp.sum(grouped * grouped, axis=...  95.1 us
    dot_general x54, matrix products, valid_conv(): jnp.dot(window.reshape(-1, window.shape[-1]), kernel[step_t, step_y, step...  14.4 us
    ppermute x4, waiting for transfers between devices, padded_2(): after = lax.ppermute(initial, axis, down)  13.7 us
    ppermute x4, waiting for transfers between devices, passed_along(): return lax.ppermute(block, axis, route)  12 us
    ppermute x4, starting transfers between devices, padded_2(): before = lax.ppermute(last, axis, up)  11.7 us
    concatenate x6, other arithmetic, padded_2(): x = jnp.concatenate([before, x, after], axis=dim)  10.1 us
    slice x56, local copies, waits for them, and re-layouts, valid_conv(): padded[step_t:step_t + frames, step_y:step_y + height, step_x:step_x + ac...  8.07 us
    dot_general x6, matrix products, spread_taps(): jnp.dot(flattened, kernel[tap_y, tap_x], preferred_element_type=jnp.float32)  6.97 us
  transfers between devices with their start and end apart: 12, of which 10 were waited for; matrix products, arithmetic and copies ran while one was open for 4% of the time, Pallas kernels for 0%

commit v1 on v0

--- a/solution.py
+++ b/solution.py
@@ -28,6 +28,38 @@
     return x
 
 
+def group_allreduce(x, axes):
+    sizes = [lax.axis_size(a) for a in axes]
+    count = 1
+    for s in sizes:
+        count *= s
+    if count & (count - 1):
+        return lax.psum(x, axes)
+    index = 0
+    for a, s in zip(axes, sizes):
+        index = index * s + lax.axis_index(a)
+    shift = 0
+    while (1 << shift) < count:
+        width = min(2, (count.bit_length() - 1) - shift)
+        slots = 1 << width
+        position = (index >> shift) % slots
+        received = [x] + [
+            lax.ppermute(x, axes, [(i, i ^ (d << shift)) for i in range(count)])
+            for d in range(1, slots)
+        ]
+        ordered = []
+        for j in range(slots):
+            value = jnp.zeros_like(x)
+            for d in range(slots):
+                value = jnp.where((position ^ d) == j, received[d], value)
+            ordered.append(value)
+        while len(ordered) > 1:
+            ordered = [ordered[k] + ordered[k + 1] for k in range(0, len(ordered), 2)]
+        x = ordered[0]
+        shift += width
+    return x
+
+
 def activate(values, sample, scale_vec, shift_vec):
     channels = values.shape[-1]
     group_width = channels // GROUPS
@@ -39,8 +71,9 @@
         * lax.axis_size("wa")
         * lax.axis_size("ta")
     )
-    totals, squares = lax.psum(
-        (jnp.sum(grouped, axis=(0, 2)), jnp.sum(grouped * grouped, axis=(0, 2))), ("ha", "wa", "ta")
+    totals, squares = group_allreduce(
+        jnp.stack([jnp.sum(grouped, axis=(0, 2)), jnp.sum(grouped * grouped, axis=(0, 2))]),
+        ("ha", "wa", "ta"),
     )
     average = totals / entries
     spread = squares / entries - average * average

time: 205 us -> 143 us (0.70)
  blocking collectives: 95.1 us -> 0 us
  starting transfers between devices: 23.2 us -> 45.9 us
  waiting for transfers between devices: 28 us -> 43.6 us
  matrix products: 24.9 us -> 20.1 us
    psum x3 -> x0, blocking collectives: 95.1 us -> none  [activate(): lax.psum((jnp.sum(grouped, axis=(0, 2)), jnp.sum(grouped * grouped, axis=...]
    ppermute x0 -> x18, starting transfers between devices: none -> 20.5 us  [group_allreduce(): lax.ppermute(x, axes, [(i, i ^ d << shift) for i in range(count)])]
    ppermute x0 -> x18, waiting for transfers between devices: none -> 15.3 us  [group_allreduce(): lax.ppermute(x, axes, [(i, i ^ d << shift) for i in range(count)])]
    pad x3, matrix products: 3.55 us -> 0.7 us  [parity_merge(): even_part = jnp.pad(lead_part, pad_end) + jnp.pad(tail_part, pad_front)]
    ppermute x4, starting transfers between devices: 11.7 us -> 14.6 us  [padded_2(): before = lax.ppermute(last, axis, up)]
  transfers between devices with their start and end apart: 12 -> 30, of which waited for: 10 -> 23; matrix products, arithmetic and copies ran while one was open for 4% -> 5% of each run, Pallas kernels for 0% -> 0%
where the time goes in v1:
time: 143 us
  starting transfers between devices  45.9 us (32%)
  waiting for transfers between devices  43.6 us (30%)
  matrix products  20.1 us (14%)
  other arithmetic  18.9 us (13%)
  local copies, waits for them, and re-layouts  13 us (9%)
  between operations  1.51 us (1%)
    ppermute x18, starting transfers between devices, group_allreduce(): lax.ppermute(x, axes, [(i, i ^ d << shift) for i in range(count)])  20.5 us
    ppermute x18, waiting for transfers between devices, group_allreduce(): lax.ppermute(x, axes, [(i, i ^ d << shift) for i in range(count)])  15.3 us
    ppermute x4, starting transfers between devices, padded_2(): before = lax.ppermute(last, axis, up)  14.6 us
    dot_general x54, matrix products, valid_conv(): jnp.dot(window.reshape(-1, window.shape[-1]), kernel[step_t, step_y, step...  14.3 us
    ppermute x4, waiting for transfers between devices, padded_2(): after = lax.ppermute(initial, axis, down)  13.7 us
    ppermute x4, waiting for transfers between devices, passed_along(): return lax.ppermute(block, axis, route)  12.2 us
    concatenate x6, other arithmetic, padded_2(): x = jnp.concatenate([before, x, after], axis=dim)  10.2 us
    slice x56, local copies, waits for them, and re-layouts, valid_conv(): padded[step_t:step_t + frames, step_y:step_y + height, step_x:step_x + ac...  8.07 us
  transfers between devices with their start and end apart: 30, of which 23 were waited for; matrix products, arithmetic and copies ran while one was open for 5% of the time, Pallas kernels for 0%

profile of v1, /device:TPU:0, one launch (start us, length us, event | category | flops | bytes accessed | tf_op | source)
XLA Modules:
  0.0 143.0 jit_solution(1656186673751575803)
XLA Ops:
  0.0 1.2 convert_reduce_fusion.1
  1.6 2.4 %collective-permute-start = (f32[2,32]{1,0:T(2,128)S(1)}, f32[2,32]{1,0:T(2,128)S(1)}, u32[]{:S(2)}, u32[]{:S(2)}) collective-permute-start(f32[2,32]{1,0:T(2,128)S(1)} %pad_maximum_fusion.34), channel_id=1, source_target_pairs={{0,3},{1,2},{2,1},{3,0},{4,7},{5,6},{6,5},{7,4},{8,11},{9,10},{10,... | collective-permute-start | bytes 776 | tf_op jit(solution)/shard_map/ppermute | solution.py:47
  5.3 2.3 %collective-permute-done.1 = f32[2,32]{1,0:T(2,128)S(1)} collective-permute-done((f32[2,32]{1,0:T(2,128)S(1)}, f32[2,32]{1,0:T(2,128)S(1)}, u32[]{:S(2)}, u32[]{:S(2)}) %collective-permute-start.1) | collective-permute-done | bytes 288 | tf_op jit(solution)/shard_map/ppermute | solution.py:47
  7.6 3.7 %collective-permute-start.3 = (f32[2,32]{1,0:T(2,128)S(1)}, f32[2,32]{1,0:T(2,128)S(1)}, u32[]{:S(2)}, u32[]{:S(2)}) collective-permute-start(f32[2,32]{1,0:T(2,128)S(1)} %add_add_fusion.5), channel_id=1, source_target_pairs={{0,12},{1,13},{2,14},{3,15},{4,8},{5,9},{6,10},{7,11},{8,4},{9,5},... | collective-permute-start | bytes 776 | tf_op jit(solution)/shard_map/ppermute | solution.py:47
  12.1 1.0 collective-permute-done.3
  13.0 2.7 %collective-permute-done.4 = f32[2,32]{1,0:T(2,128)S(1)} collective-permute-done((f32[2,32]{1,0:T(2,128)S(1)}, f32[2,32]{1,0:T(2,128)S(1)}, u32[]{:S(2)}, u32[]{:S(2)}) %collective-permute-start.4) | collective-permute-done | bytes 288 | tf_op jit(solution)/shard_map/ppermute | solution.py:47
  16.1 1.1 fusion.26
  17.2 1.2 fusion.38
  18.4 1.2 fusion.41
  19.5 1.2 fusion.43
  20.7 1.2 fusion.46
  25.6 1.3 collective-permute-start.6
  27.3 6.2 %collective-permute-done.6 = f32[3,66,256]{2,1,0:T(8,128)S(1)} collective-permute-done((f32[3,66,256]{2,1,0:T(8,128)S(1)}, f32[3,66,256]{2,1,0:T(8,128)S(1)}, u32[]{:S(2)}, u32[]{:S(2)}) %collective-permute-start.6) | collective-permute-done | bytes 202784 | tf_op jit(solution)/shard_map/ppermute | solution.py:15
  33.8 1.3 collective-permute-start.7
  35.4 3.9 %collective-permute-done.7 = f32[3,4,256]{2,1,0:T(4,128)S(1)} collective-permute-done((f32[3,4,256]{2,1,0:T(4,128)S(1)}, f32[3,4,256]{2,1,0:T(4,128)S(1)}, u32[]{:S(2)}, u32[]{:S(2)}) %collective-permute-start.7) | collective-permute-done | bytes 12320 | tf_op jit(solution)/shard_map/ppermute | solution.py:15
  40.4 1.8 %collective-permute-start.10 = (f32[2,32]{1,0:T(2,128)S(1)}, f32[2,32]{1,0:T(2,128)S(1)}, u32[]{:S(2)}, u32[]{:S(2)}) collective-permute-start(f32[2,32]{1,0:T(2,128)S(1)} %pad_maximum_fusion.35), channel_id=1, source_target_pairs={{0,1},{1,0},{2,3},{3,2},{4,5},{5,4},{6,7},{7,6},{8,9},{9,8},{10,11... | collective-permute-start | bytes 776 | tf_op jit(solution)/shard_map/ppermute | solution.py:47
  42.1 1.1 collective-permute-done.8
  43.9 1.1 collective-permute-start.11
  45.0 1.1 collective-permute-start.12
  46.1 2.3 %collective-permute-start.13 = (f32[2,32]{1,0:T(2,128)S(1)}, f32[2,32]{1,0:T(2,128)S(1)}, u32[]{:S(2)}, u32[]{:S(2)}) collective-permute-start(f32[2,32]{1,0:T(2,128)S(1)} %add_add_fusion.3), channel_id=1, source_target_pairs={{0,4},{1,5},{2,6},{3,7},{4,0},{5,1},{6,2},{7,3},{8,12},{9,13},{10,... | collective-permute-start | bytes 776 | tf_op jit(solution)/shard_map/ppermute | solution.py:47
  51.0 1.3 collective-permute-start.14
  52.4 1.1 collective-permute-done.14
  54.5 1.3 collective-permute-start.16
  55.8 4.6 %collective-permute-start.15 = (bf16[5,1,64,256]{3,1,2,0:T(2,128)(2,1)S(1)}, bf16[5,1,64,256]{3,1,2,0:T(2,128)(2,1)S(1)}, u32[]{:S(2)}, u32[]{:S(2)}) collective-permute-start(bf16[5,1,64,256]{3,1,2,0:T(2,128)(2,1)S(1)} %get-tuple-element.75), channel_id=1, source_target_pairs={{0,4},{4,8},{8,12},{1,5},{5,9},{9,13},{2,6},{6,10},{10,14},{3,7},{... | collective-permute-start | bytes 491528 | tf_op jit(solution)/shard_map/ppermute | solution.py:25
  60.5 6.2 %collective-permute-done.16 = bf16[5,1,64,256]{3,1,2,0:T(2,128)(2,1)S(1)} collective-permute-done((bf16[5,1,64,256]{3,1,2,0:T(2,128)(2,1)S(1)}, bf16[5,1,64,256]{3,1,2,0:T(2,128)(2,1)S(1)}, u32[]{:S(2)}, u32[]{:S(2)}) %collective-permute-start.16) | collective-permute-done | bytes 163872 | tf_op jit(solution)/shard_map/ppermute | solution.py:26
  66.7 1.2 collective-permute-done.15
  67.9 1.9 %collective-permute-start.17 = (bf16[5,6,1,256]{3,1,2,0:T(8,128)(2,1)S(1)}, bf16[5,6,1,256]{3,1,2,0:T(8,128)(2,1)S(1)}, u32[]{:S(2)}, u32[]{:S(2)}) collective-permute-start(bf16[5,6,1,256]{3,1,2,0:T(8,128)(2,1)S(1)} %get-tuple-element.55), channel_id=1, source_target_pairs={{0,2},{1,3},{4,6},{5,7},{8,10},{9,11},{12,14},{13,15},{16,18},{17,... | collective-permute-start | bytes 46088 | tf_op jit(solution)/shard_map/ppermute | solution.py:25
  69.8 1.3 collective-permute-start.18
  72.4 1.9 %pad_maximum_fusion.15 = (bf16[3,4,64,256]{3,1,2,0:T(4,128)(2,1)S(1)}, bf16[3,4,64,256]{3,1,2,0:T(4,128)(2,1)S(1)}, bf16[3,4,64,256]{3,1,2,0:T(4,128)(2,1)S(1)},...) fusion(bf16[5,1,64,256]{3,1,2,0:T(2,128)(2,1)S(1)} %collective-permute-done.16, ...), kind=kLoop, calls=%fused_computation.128 | loop fusion | flops 5111808 | bytes 2785280 | tf_op jit(solution)/shard_map/concatenate | solution.py:27
  75.5 2.3 %maximum_maximum_fusion = (bf16[5,6,65,256]{3,1,2,0:T(8,128)(2,1)S(1)}, bf16[5,6,65,256]{3,1,2,0:T(8,128)(2,1)S(1)}) fusion(bf16[5,1,64,256]{3,1,2,0:T(2,128)(2,1)S(1)} %collective-permute-done.16, bf16[3,4,64,256]{3,1,2,0:T(4,128)(2,1)S(1)} %fusion.13, bf16[2,4,64,256]{3,1,2,0:T(4,128)(2,1)S(1)} %maximum_select_fusion, ...), kind=kLoop, calls=%fused_computation.5 | loop fusion | flops 9984000 | bytes 3010560 | tf_op jit(solution)/shard_map/concatenate | solution.py:27
  77.8 1.6 %fusion.188 = (bf16[3,4,64,256]{3,1,2,0:T(4,128)(2,1)S(1)}, bf16[3,4,64,256]{3,1,2,0:T(4,128)(2,1)S(1)}, bf16[3,4,64,256]{3,1,2,0:T(4,128)(2,1)S(1)}, bf16[3,4,6...) fusion(bf16[5,6,65,256]{3,1,2,0:T(8,128)(2,1)S(1)} %get-tuple-e, ...), kind=kLoop, calls=%fused_computation.328 | loop fusion | bytes 7077888 | tf_op jit(solution)/shard_map/slice | solution.py:124
  79.5 1.3 fusion.189
  89.5 1.8 %collective-permute-start.20 = (f32[2,32]{1,0:T(2,128)S(1)}, f32[2,32]{1,0:T(2,128)S(1)}, u32[]{:S(2)}, u32[]{:S(2)}) collective-permute-start(f32[2,32]{1,0:T(2,128)S(1)} %pad_maximum_fusion.36), channel_id=1, source_target_pairs={{0,2},{1,3},{2,0},{3,1},{4,6},{5,7},{6,4},{7,5},{8,10},{9,11},{10,... | collective-permute-start | bytes 776 | tf_op jit(solution)/shard_map/ppermute | solution.py:47
  91.3 1.0 collective-permute-done.19
  93.1 3.6 %collective-permute-start.22 = (f32[2,32]{1,0:T(2,128)S(1)}, f32[2,32]{1,0:T(2,128)S(1)}, u32[]{:S(2)}, u32[]{:S(2)}) collective-permute-start(f32[2,32]{1,0:T(2,128)S(1)} %add_add_fusion.1), channel_id=1, source_target_pairs={{0,12},{1,13},{2,14},{3,15},{4,8},{5,9},{6,10},{7,11},{8,4},{9,5},... | collective-permute-start | bytes 776 | tf_op jit(solution)/shard_map/ppermute | solution.py:47
  98.5 2.7 %collective-permute-done.23 = f32[2,32]{1,0:T(2,128)S(1)} collective-permute-done((f32[2,32]{1,0:T(2,128)S(1)}, f32[2,32]{1,0:T(2,128)S(1)}, u32[]{:S(2)}, u32[]{:S(2)}) %collective-permute-start.23) | collective-permute-done | bytes 288 | tf_op jit(solution)/shard_map/ppermute | solution.py:47
  102.3 1.6 %collective-permute-start.25 = (bf16[2,4,64,256]{3,1,2,0:T(4,128)(2,1)S(1)}, bf16[2,4,64,256]{3,1,2,0:T(4,128)(2,1)S(1)}, u32[]{:S(2)}, u32[]{:S(2)}) collective-permute-start(bf16[2,4,64,256]{3,1,2,0:T(4,128)(2,1)S(1)} %slice.620), channel_id=1, source_target_pairs={{0,1},{2,3},{4,5},{6,7},{8,9},{10,11},{12,13},{14,15},{16,17},{18,... | collective-permute-start | bytes 786440 | tf_op jit(solution)/shard_map/ppermute | solution.py:15
  104.0 1.1 collective-permute-done.25
  106.1 1.3 collective-permute-start.27
  107.4 4.6 %collective-permute-start.26 = (bf16[5,1,64,256]{3,1,2,0:T(2,128)(2,1)S(1)}, bf16[5,1,64,256]{3,1,2,0:T(2,128)(2,1)S(1)}, u32[]{:S(2)}, u32[]{:S(2)}) collective-permute-start(bf16[5,1,64,256]{3,1,2,0:T(2,128)(2,1)S(1)} %get-tuple-element.71), channel_id=1, source_target_pairs={{0,4},{4,8},{8,12},{1,5},{5,9},{9,13},{2,6},{6,10},{10,14},{3,7},{... | collective-permute-start | bytes 491528 | tf_op jit(solution)/shard_map/ppermute | solution.py:25
  112.0 6.0 %collective-permute-done.27 = bf16[5,1,64,256]{3,1,2,0:T(2,128)(2,1)S(1)} collective-permute-done((bf16[5,1,64,256]{3,1,2,0:T(2,128)(2,1)S(1)}, bf16[5,1,64,256]{3,1,2,0:T(2,128)(2,1)S(1)}, u32[]{:S(2)}, u32[]{:S(2)}) %collective-permute-start.27) | collective-permute-done | bytes 163872 | tf_op jit(solution)/shard_map/ppermute | solution.py:26
  117.9 1.2 collective-permute-done.26
  119.2 3.5 %collective-permute-start.28 = (bf16[5,6,1,256]{3,1,2,0:T(8,128)(2,1)S(1)}, bf16[5,6,1,256]{3,1,2,0:T(8,128)(2,1)S(1)}, u32[]{:S(2)}, u32[]{:S(2)}) collective-permute-start(bf16[5,6,1,256]{3,1,2,0:T(8,128)(2,1)S(1)} %get-tuple-element.51), channel_id=1, source_target_pairs={{0,2},{1,3},{4,6},{5,7},{8,10},{9,11},{12,14},{13,15},{16,18},{17,... | collective-permute-start | bytes 46088 | tf_op jit(solution)/shard_map/ppermute | solution.py:25
  122.7 1.5 %collective-permute-start.29 = (bf16[5,6,1,256]{3,1,2,0:T(8,128)(2,1)S(1)}, bf16[5,6,1,256]{3,1,2,0:T(8,128)(2,1)S(1)}, u32[]{:S(2)}, u32[]{:S(2)}) collective-permute-start(bf16[5,6,1,256]{3,1,2,0:T(8,128)(2,1)S(1)} %get-tuple-element.52), channel_id=1, source_target_pairs={{2,0},{3,1},{6,4},{7,5},{10,8},{11,9},{14,12},{15,13},{18,16},{19,... | collective-permute-start | bytes 46088 | tf_op jit(solution)/shard_map/ppermute | solution.py:26
  125.5 1.7 %pad_maximum_fusion.6 = (bf16[3,4,64,256]{3,1,2,0:T(4,128)(2,1)S(1)}, bf16[3,4,64,256]{3,1,2,0:T(4,128)(2,1)S(1)}, bf16[3,4,64,256]{3,1,2,0:T(4,128)(2,1)S(1)}, ...) fusion(bf16[5,1,64,256]{3,1,2,0:T(2,128)(2,1)S(1)} %collective-permute-done.27, ...), kind=kLoop, calls=%fused_computation.119 | loop fusion | flops 5111808 | bytes 2785280 | tf_op jit(solution)/shard_map/concatenate | solution.py:27
  128.4 2.3 %maximum_maximum_fusion.1 = (bf16[5,6,65,256]{3,1,2,0:T(8,128)(2,1)S(1)}, bf16[5,6,65,256]{3,1,2,0:T(8,128)(2,1)S(1)}) fusion(bf16[5,1,64,256]{3,1,2,0:T(2,128)(2,1)S(1)} %collective-permute-done.27, bf16[3,4,64,256]{3,1,2,0:T(4,128)(2,1)S(1)} %fusion.14, bf16[2,4,64,256]{3,1,2,0:T(4,128)(2,1)S(1)} %maximum_select_fusion.1, ...), kind=kLoop, calls=%fused_computation.7 | loop fusion | flops 9984000 | bytes 3010560 | tf_op jit(solution)/shard_map/concatenate | solution.py:27
  130.7 1.6 %fusion.186 = (bf16[3,4,64,256]{3,1,2,0:T(4,128)(2,1)S(1)}, bf16[3,4,64,256]{3,1,2,0:T(4,128)(2,1)S(1)}, bf16[3,4,64,256]{3,1,2,0:T(4,128)(2,1)S(1)}, bf16[3,4,6...) fusion(bf16[5,6,65,256]{3,1,2,0:T(8,128)(2,1)S(1)} %get-tuple-e, ...), kind=kLoop, calls=%fused_computation.326 | loop fusion | bytes 7077888 | tf_op jit(solution)/shard_map/slice | solution.py:124
  132.4 1.2 fusion.187
  (228 shorter events, 39.9 us)
Async XLA Ops:
  0.0 21.9 %copy-start.2 = (bf16[3,3,512,256]{3,2,1,0:T(8,128)(2,1)S(1)}, bf16[3,3,512,256]{3,2,1,0:T(8,128)(2,1)}, u32[]{:S(2)}) copy-start(bf16[3,3,512,256]{3,2,1,0:T(8,128)(2,1)} %param.13) | copy-start | bytes 7077892
  1.6 3.7 %collective-permute-start = (f32[2,32]{1,0:T(2,128)S(1)}, f32[2,32]{1,0:T(2,128)S(1)}, u32[]{:S(2)}, u32[]{:S(2)}) collective-permute-start(f32[2,32]{1,0:T(2,128)S(1)} %pad_maximum_fusion.34), channel_id=1, source_target_pairs={{0,3},{1,2},{2,1},{3,0},{4,7},{5,6},{6,5},{7,4},{8,11},{9,10},{10,... | collective-permute-start | bytes 776 | tf_op jit(solution)/shard_map/ppermute | solution.py:47
  4.0 3.6 %collective-permute-start.1 = (f32[2,32]{1,0:T(2,128)S(1)}, f32[2,32]{1,0:T(2,128)S(1)}, u32[]{:S(2)}, u32[]{:S(2)}) collective-permute-start(f32[2,32]{1,0:T(2,128)S(1)} %pad_maximum_fusion.34), channel_id=1, source_target_pairs={{0,2},{1,3},{2,0},{3,1},{4,6},{5,7},{6,4},{7,5},{8,10},{9,11},{10,... | collective-permute-start | bytes 776 | tf_op jit(solution)/shard_map/ppermute | solution.py:47
  4.6 2.9 %collective-permute-start.2 = (f32[2,32]{1,0:T(2,128)S(1)}, f32[2,32]{1,0:T(2,128)S(1)}, u32[]{:S(2)}, u32[]{:S(2)}) collective-permute-start(f32[2,32]{1,0:T(2,128)S(1)} %pad_maximum_fusion.34), channel_id=1, source_target_pairs={{0,1},{1,0},{2,3},{3,2},{4,5},{5,4},{6,7},{7,6},{8,9},{9,8},{10,11... | collective-permute-start | bytes 776 | tf_op jit(solution)/shard_map/ppermute | solution.py:47
  7.6 5.4 %collective-permute-start.3 = (f32[2,32]{1,0:T(2,128)S(1)}, f32[2,32]{1,0:T(2,128)S(1)}, u32[]{:S(2)}, u32[]{:S(2)}) collective-permute-start(f32[2,32]{1,0:T(2,128)S(1)} %add_add_fusion.5), channel_id=1, source_target_pairs={{0,12},{1,13},{2,14},{3,15},{4,8},{5,9},{6,10},{7,11},{8,4},{9,5},... | collective-permute-start | bytes 776 | tf_op jit(solution)/shard_map/ppermute | solution.py:47
  11.3 4.5 %collective-permute-start.4 = (f32[2,32]{1,0:T(2,128)S(1)}, f32[2,32]{1,0:T(2,128)S(1)}, u32[]{:S(2)}, u32[]{:S(2)}) collective-permute-start(f32[2,32]{1,0:T(2,128)S(1)} %add_add_fusion.5), channel_id=1, source_target_pairs={{0,8},{1,9},{2,10},{3,11},{4,12},{5,13},{6,14},{7,15},{8,0},{9,1},... | collective-permute-start | bytes 776 | tf_op jit(solution)/shard_map/ppermute | solution.py:47
  11.3 4.5 %collective-permute-start.5 = (f32[2,32]{1,0:T(2,128)S(1)}, f32[2,32]{1,0:T(2,128)S(1)}, u32[]{:S(2)}, u32[]{:S(2)}) collective-permute-start(f32[2,32]{1,0:T(2,128)S(1)} %add_add_fusion.5), channel_id=1, source_target_pairs={{0,4},{1,5},{2,6},{3,7},{4,0},{5,1},{6,2},{7,3},{8,12},{9,13},{10,... | collective-permute-start | bytes 776 | tf_op jit(solution)/shard_map/ppermute | solution.py:47
  25.6 24.7 %copy-start.3 = (f32[256]{0:T(256)S(1)}, f32[256]{0:T(256)}, u32[]{:S(2)}) copy-start(f32[256]{0:T(256)} %param.15) | copy-start | bytes 3076
  25.6 24.7 %copy-start.4 = (f32[256]{0:T(256)S(1)}, f32[256]{0:T(256)}, u32[]{:S(2)}) copy-start(f32[256]{0:T(256)} %param.14) | copy-start | bytes 3076
  25.6 7.8 %collective-permute-start.6 = (f32[3,66,256]{2,1,0:T(8,128)S(1)}, f32[3,66,256]{2,1,0:T(8,128)S(1)}, u32[]{:S(2)}, u32[]{:S(2)}) collective-permute-start(f32[3,66,256]{2,1,0:T(8,128)S(1)} %get-tuple-element.47), channel_id=1, source_target_pairs={{4,0},{8,4},{12,8},{5,1},{9,5},{13,9},{6,2},{10,6},{14,10},{7,3},{... | collective-permute-start | bytes 608264 | tf_op jit(solution)/shard_map/ppermute | solution.py:15
  33.8 5.6 %collective-permute-start.7 = (f32[3,4,256]{2,1,0:T(4,128)S(1)}, f32[3,4,256]{2,1,0:T(4,128)S(1)}, u32[]{:S(2)}, u32[]{:S(2)}) collective-permute-start(f32[3,4,256]{2,1,0:T(4,128)S(1)} %fusion.176), channel_id=1, source_target_pairs={{2,0},{3,1},{6,4},{7,5},{10,8},{11,9},{14,12},{15,13},{18,16},{19,... | collective-permute-start | bytes 36872 | tf_op jit(solution)/shard_map/ppermute | solution.py:15
  40.2 3.1 %collective-permute-start.8 = (f32[2,32]{1,0:T(2,128)S(1)}, f32[2,32]{1,0:T(2,128)S(1)}, u32[]{:S(2)}, u32[]{:S(2)}) collective-permute-start(f32[2,32]{1,0:T(2,128)S(1)} %pad_maximum_fusion.35), channel_id=1, source_target_pairs={{0,3},{1,2},{2,1},{3,0},{4,7},{5,6},{6,5},{7,4},{8,11},{9,10},{10,... | collective-permute-start | bytes 776 | tf_op jit(solution)/shard_map/ppermute | solution.py:47
  40.3 3.6 %collective-permute-start.9 = (f32[2,32]{1,0:T(2,128)S(1)}, f32[2,32]{1,0:T(2,128)S(1)}, u32[]{:S(2)}, u32[]{:S(2)}) collective-permute-start(f32[2,32]{1,0:T(2,128)S(1)} %pad_maximum_fusion.35), channel_id=1, source_target_pairs={{0,2},{1,3},{2,0},{3,1},{4,6},{5,7},{6,4},{7,5},{8,10},{9,11},{10,... | collective-permute-start | bytes 776 | tf_op jit(solution)/shard_map/ppermute | solution.py:47
  40.4 3.6 %collective-permute-start.10 = (f32[2,32]{1,0:T(2,128)S(1)}, f32[2,32]{1,0:T(2,128)S(1)}, u32[]{:S(2)}, u32[]{:S(2)}) collective-permute-start(f32[2,32]{1,0:T(2,128)S(1)} %pad_maximum_fusion.35), channel_id=1, source_target_pairs={{0,1},{1,0},{2,3},{3,2},{4,5},{5,4},{6,7},{7,6},{8,9},{9,8},{10,11... | collective-permute-start | bytes 776 | tf_op jit(solution)/shard_map/ppermute | solution.py:47
  43.9 5.4 %collective-permute-start.11 = (f32[2,32]{1,0:T(2,128)S(1)}, f32[2,32]{1,0:T(2,128)S(1)}, u32[]{:S(2)}, u32[]{:S(2)}) collective-permute-start(f32[2,32]{1,0:T(2,128)S(1)} %add_add_fusion.3), channel_id=1, source_target_pairs={{0,12},{1,13},{2,14},{3,15},{4,8},{5,9},{6,10},{7,11},{8,4},{9,5},... | collective-permute-start | bytes 776 | tf_op jit(solution)/shard_map/ppermute | solution.py:47
  45.0 4.5 %collective-permute-start.12 = (f32[2,32]{1,0:T(2,128)S(1)}, f32[2,32]{1,0:T(2,128)S(1)}, u32[]{:S(2)}, u32[]{:S(2)}) collective-permute-start(f32[2,32]{1,0:T(2,128)S(1)} %add_add_fusion.3), channel_id=1, source_target_pairs={{0,8},{1,9},{2,10},{3,11},{4,12},{5,13},{6,14},{7,15},{8,0},{9,1},... | collective-permute-start | bytes 776 | tf_op jit(solution)/shard_map/ppermute | solution.py:47
  46.1 3.8 %collective-permute-start.13 = (f32[2,32]{1,0:T(2,128)S(1)}, f32[2,32]{1,0:T(2,128)S(1)}, u32[]{:S(2)}, u32[]{:S(2)}) collective-permute-start(f32[2,32]{1,0:T(2,128)S(1)} %add_add_fusion.3), channel_id=1, source_target_pairs={{0,4},{1,5},{2,6},{3,7},{4,0},{5,1},{6,2},{7,3},{8,12},{9,13},{10,... | collective-permute-start | bytes 776 | tf_op jit(solution)/shard_map/ppermute | solution.py:47
  51.0 2.4 %collective-permute-start.14 = (bf16[2,4,64,256]{3,1,2,0:T(4,128)(2,1)S(1)}, bf16[2,4,64,256]{3,1,2,0:T(4,128)(2,1)S(1)}, u32[]{:S(2)}, u32[]{:S(2)}) collective-permute-start(bf16[2,4,64,256]{3,1,2,0:T(4,128)(2,1)S(1)} %slice.594), channel_id=1, source_target_pairs={{0,1},{2,3},{4,5},{6,7},{8,9},{10,11},{12,13},{14,15},{16,17},{18,... | collective-permute-start | bytes 786440 | tf_op jit(solution)/shard_map/ppermute | solution.py:15
  52.4 19.7 %copy-start = (bf16[3,3,3,256,256]{4,3,2,1,0:T(8,128)(2,1)S(1)}, bf16[3,3,3,256,256]{4,3,2,1,0:T(8,128)(2,1)}, u32[]{:S(2)}) copy-start(bf16[3,3,3,256,256]{4,3,2,1,0:T(8,128)(2,1)} %param.16) | copy-start | bytes 10616836
  54.5 12.2 %collective-permute-start.16 = (bf16[5,1,64,256]{3,1,2,0:T(2,128)(2,1)S(1)}, bf16[5,1,64,256]{3,1,2,0:T(2,128)(2,1)S(1)}, u32[]{:S(2)}, u32[]{:S(2)}) collective-permute-start(bf16[5,1,64,256]{3,1,2,0:T(2,128)(2,1)S(1)} %get-tuple-element.76), channel_id=1, source_target_pairs={{4,0},{8,4},{12,8},{5,1},{9,5},{13,9},{6,2},{10,6},{14,10},{7,3},{... | collective-permute-start | bytes 491528 | tf_op jit(solution)/shard_map/ppermute | solution.py:26
  55.8 12.1 %collective-permute-start.15 = (bf16[5,1,64,256]{3,1,2,0:T(2,128)(2,1)S(1)}, bf16[5,1,64,256]{3,1,2,0:T(2,128)(2,1)S(1)}, u32[]{:S(2)}, u32[]{:S(2)}) collective-permute-start(bf16[5,1,64,256]{3,1,2,0:T(2,128)(2,1)S(1)} %get-tuple-element.75), channel_id=1, source_target_pairs={{0,4},{4,8},{8,12},{1,5},{5,9},{9,13},{2,6},{6,10},{10,14},{3,7},{... | collective-permute-start | bytes 491528 | tf_op jit(solution)/shard_map/ppermute | solution.py:25
  67.9 6.8 %collective-permute-start.17 = (bf16[5,6,1,256]{3,1,2,0:T(8,128)(2,1)S(1)}, bf16[5,6,1,256]{3,1,2,0:T(8,128)(2,1)S(1)}, u32[]{:S(2)}, u32[]{:S(2)}) collective-permute-start(bf16[5,6,1,256]{3,1,2,0:T(8,128)(2,1)S(1)} %get-tuple-element.55), channel_id=1, source_target_pairs={{0,2},{1,3},{4,6},{5,7},{8,10},{9,11},{12,14},{13,15},{16,18},{17,... | collective-permute-start | bytes 46088 | tf_op jit(solution)/shard_map/ppermute | solution.py:25
  69.8 5.7 %collective-permute-start.18 = (bf16[5,6,1,256]{3,1,2,0:T(8,128)(2,1)S(1)}, bf16[5,6,1,256]{3,1,2,0:T(8,128)(2,1)S(1)}, u32[]{:S(2)}, u32[]{:S(2)}) collective-permute-start(bf16[5,6,1,256]{3,1,2,0:T(8,128)(2,1)S(1)} %get-tuple-element.56), channel_id=1, source_target_pairs={{2,0},{3,1},{6,4},{7,5},{10,8},{11,9},{14,12},{15,13},{18,16},{19,... | collective-permute-start | bytes 46088 | tf_op jit(solution)/shard_map/ppermute | solution.py:26
  87.9 13.6 %copy-start.5 = (f32[256]{0:T(256)S(1)}, f32[256]{0:T(256)}, u32[]{:S(2)}) copy-start(f32[256]{0:T(256)} %param.18) | copy-start | bytes 3076
  87.9 13.6 %copy-start.6 = (f32[256]{0:T(256)S(1)}, f32[256]{0:T(256)}, u32[]{:S(2)}) copy-start(f32[256]{0:T(256)} %param.17) | copy-start | bytes 3076
  89.2 3.1 %collective-permute-start.19 = (f32[2,32]{1,0:T(2,128)S(1)}, f32[2,32]{1,0:T(2,128)S(1)}, u32[]{:S(2)}, u32[]{:S(2)}) collective-permute-start(f32[2,32]{1,0:T(2,128)S(1)} %pad_maximum_fusion.36), channel_id=1, source_target_pairs={{0,3},{1,2},{2,1},{3,0},{4,7},{5,6},{6,5},{7,4},{8,11},{9,10},{10,... | collective-permute-start | bytes 776 | tf_op jit(solution)/shard_map/ppermute | solution.py:47
  89.5 3.6 %collective-permute-start.20 = (f32[2,32]{1,0:T(2,128)S(1)}, f32[2,32]{1,0:T(2,128)S(1)}, u32[]{:S(2)}, u32[]{:S(2)}) collective-permute-start(f32[2,32]{1,0:T(2,128)S(1)} %pad_maximum_fusion.36), channel_id=1, source_target_pairs={{0,2},{1,3},{2,0},{3,1},{4,6},{5,7},{6,4},{7,5},{8,10},{9,11},{10,... | collective-permute-start | bytes 776 | tf_op jit(solution)/shard_map/ppermute | solution.py:47
  91.2 1.8 %collective-permute-start.21 = (f32[2,32]{1,0:T(2,128)S(1)}, f32[2,32]{1,0:T(2,128)S(1)}, u32[]{:S(2)}, u32[]{:S(2)}) collective-permute-start(f32[2,32]{1,0:T(2,128)S(1)} %pad_maximum_fusion.36), channel_id=1, source_target_pairs={{0,1},{1,0},{2,3},{3,2},{4,5},{5,4},{6,7},{7,6},{8,9},{9,8},{10,11... | collective-permute-start | bytes 776 | tf_op jit(solution)/shard_map/ppermute | solution.py:47
  93.1 5.4 %collective-permute-start.22 = (f32[2,32]{1,0:T(2,128)S(1)}, f32[2,32]{1,0:T(2,128)S(1)}, u32[]{:S(2)}, u32[]{:S(2)}) collective-permute-start(f32[2,32]{1,0:T(2,128)S(1)} %add_add_fusion.1), channel_id=1, source_target_pairs={{0,12},{1,13},{2,14},{3,15},{4,8},{5,9},{6,10},{7,11},{8,4},{9,5},... | collective-permute-start | bytes 776 | tf_op jit(solution)/shard_map/ppermute | solution.py:47
  96.7 4.5 %collective-permute-start.23 = (f32[2,32]{1,0:T(2,128)S(1)}, f32[2,32]{1,0:T(2,128)S(1)}, u32[]{:S(2)}, u32[]{:S(2)}) collective-permute-start(f32[2,32]{1,0:T(2,128)S(1)} %add_add_fusion.1), channel_id=1, source_target_pairs={{0,8},{1,9},{2,10},{3,11},{4,12},{5,13},{6,14},{7,15},{8,0},{9,1},... | collective-permute-start | bytes 776 | tf_op jit(solution)/shard_map/ppermute | solution.py:47
  97.1 4.1 %collective-permute-start.24 = (f32[2,32]{1,0:T(2,128)S(1)}, f32[2,32]{1,0:T(2,128)S(1)}, u32[]{:S(2)}, u32[]{:S(2)}) collective-permute-start(f32[2,32]{1,0:T(2,128)S(1)} %add_add_fusion.1), channel_id=1, source_target_pairs={{0,4},{1,5},{2,6},{3,7},{4,0},{5,1},{6,2},{7,3},{8,12},{9,13},{10,... | collective-permute-start | bytes 776 | tf_op jit(solution)/shard_map/ppermute | solution.py:47
  102.2 23.0 %copy-start.1 = (bf16[3,3,3,256,256]{4,3,2,1,0:T(8,128)(2,1)S(1)}, bf16[3,3,3,256,256]{4,3,2,1,0:T(8,128)(2,1)}, u32[]{:S(2)}) copy-start(bf16[3,3,3,256,256]{4,3,2,1,0:T(8,128)(2,1)} %param.19) | copy-start | bytes 10616836
  102.3 2.7 %collective-permute-start.25 = (bf16[2,4,64,256]{3,1,2,0:T(4,128)(2,1)S(1)}, bf16[2,4,64,256]{3,1,2,0:T(4,128)(2,1)S(1)}, u32[]{:S(2)}, u32[]{:S(2)}) collective-permute-start(bf16[2,4,64,256]{3,1,2,0:T(4,128)(2,1)S(1)} %slice.620), channel_id=1, source_target_pairs={{0,1},{2,3},{4,5},{6,7},{8,9},{10,11},{12,13},{14,15},{16,17},{18,... | collective-permute-start | bytes 786440 | tf_op jit(solution)/shard_map/ppermute | solution.py:15
  106.1 11.9 %collective-permute-start.27 = (bf16[5,1,64,256]{3,1,2,0:T(2,128)(2,1)S(1)}, bf16[5,1,64,256]{3,1,2,0:T(2,128)(2,1)S(1)}, u32[]{:S(2)}, u32[]{:S(2)}) collective-permute-start(bf16[5,1,64,256]{3,1,2,0:T(2,128)(2,1)S(1)} %get-tuple-element.72), channel_id=1, source_target_pairs={{4,0},{8,4},{12,8},{5,1},{9,5},{13,9},{6,2},{10,6},{14,10},{7,3},{... | collective-permute-start | bytes 491528 | tf_op jit(solution)/shard_map/ppermute | solution.py:26
  107.4 11.8 %collective-permute-start.26 = (bf16[5,1,64,256]{3,1,2,0:T(2,128)(2,1)S(1)}, bf16[5,1,64,256]{3,1,2,0:T(2,128)(2,1)S(1)}, u32[]{:S(2)}, u32[]{:S(2)}) collective-permute-start(bf16[5,1,64,256]{3,1,2,0:T(2,128)(2,1)S(1)} %get-tuple-element.71), channel_id=1, source_target_pairs={{0,4},{4,8},{8,12},{1,5},{5,9},{9,13},{2,6},{6,10},{10,14},{3,7},{... | collective-permute-start | bytes 491528 | tf_op jit(solution)/shard_map/ppermute | solution.py:25
  119.2 8.5 %collective-permute-start.28 = (bf16[5,6,1,256]{3,1,2,0:T(8,128)(2,1)S(1)}, bf16[5,6,1,256]{3,1,2,0:T(8,128)(2,1)S(1)}, u32[]{:S(2)}, u32[]{:S(2)}) collective-permute-start(bf16[5,6,1,256]{3,1,2,0:T(8,128)(2,1)S(1)} %get-tuple-element.51), channel_id=1, source_target_pairs={{0,2},{1,3},{4,6},{5,7},{8,10},{9,11},{12,14},{13,15},{16,18},{17,... | collective-permute-start | bytes 46088 | tf_op jit(solution)/shard_map/ppermute | solution.py:25
  122.7 5.7 %collective-permute-start.29 = (bf16[5,6,1,256]{3,1,2,0:T(8,128)(2,1)S(1)}, bf16[5,6,1,256]{3,1,2,0:T(8,128)(2,1)S(1)}, u32[]{:S(2)}, u32[]{:S(2)}) collective-permute-start(bf16[5,6,1,256]{3,1,2,0:T(8,128)(2,1)S(1)} %get-tuple-element.52), channel_id=1, source_target_pairs={{2,0},{3,1},{6,4},{7,5},{10,8},{11,9},{14,12},{15,13},{18,16},{19,... | collective-permute-start | bytes 46088 | tf_op jit(solution)/shard_map/ppermute | solution.py:26

commit v2 on v1

v2 whole, which is shorter than its diff:
```python
import jax
import jax.numpy as jnp
from jax import lax
from jax.sharding import PartitionSpec as P

GROUPS = 32


EPSILON = 1e-06


def passed_along(block, axis, distance):
    devices = range(lax.axis_size(axis))
    route = [(i - distance, i) for i in devices if i - distance in devices]
    return lax.ppermute(block, axis, route)


def padded_2(x, sides, width):
    for axis, dim in sides:
        size, length = (lax.axis_size(axis), x.shape[dim])
        up = [(i, (i + 1) % size) for i in range(size - 1)]
        down = [(j, i) for i, j in up]
        last = lax.slice_in_dim(x, length - width, length, axis=dim)
        initial = lax.slice_in_dim(x, 0, width, axis=dim)
        before = lax.ppermute(last, axis, up)
        after = lax.ppermute(initial, axis, down)
        x = jnp.concatenate([before, x, after], axis=dim)
    return x


def group_allreduce(x, axes):
    sizes = [lax.axis_size(a) for a in axes]
    count = 1
    for s in sizes:
        count *= s
    if count & (count - 1):
        return lax.psum(x, axes)
    index = 0
    for a, s in zip(axes, sizes):
        index = index * s + lax.axis_index(a)
    shift = 0
    while (1 << shift) < count:
        width = min(2, (count.bit_length() - 1) - shift)
        slots = 1 << width
        position = (index >> shift) % slots
        received = [x] + [
            lax.ppermute(x, axes, [(i, i ^ (d << shift)) for i in range(count)])
            for d in range(1, slots)
        ]
        ordered = []
        for j in range(slots):
            value = jnp.zeros_like(x)
            for d in range(slots):
                value = jnp.where((position ^ d) == j, received[d], value)
            ordered.append(value)
        while len(ordered) > 1:
            ordered = [ordered[k] + ordered[k + 1] for k in range(0, len(ordered), 2)]
        x = ordered[0]
        shift += width
    return x


def group_stats(values):
    channels = values.shape[-1]
    group_width = channels // GROUPS
    grouped = values.reshape(-1, GROUPS, group_width)
    entries = (
        grouped.shape[0]
        * group_width
        * lax.axis_size("ha")
        * lax.axis_size("wa")
        * lax.axis_size("ta")
    )
    totals, squares = group_allreduce(
        jnp.stack([jnp.sum(grouped, axis=(0, 2)), jnp.sum(grouped * grouped, axis=(0, 2))]),
        ("ha", "wa", "ta"),
    )
    average = totals / entries
    spread = squares / entries - average * average
    scaling = lax.rsqrt(spread + EPSILON)
    return jnp.repeat(average, group_width), jnp.repeat(scaling, group_width)


def activate(values, stats, scale_vec, shift_vec):
    average, scaling = stats
    normed = (values - average) * scaling * scale_vec + shift_vec
    return jax.nn.silu(normed)


def inside_mask(rows, cols, low_pad):
    h, h_last = lax.axis_index("ha"), lax.axis_size("ha") - 1
    w, w_last = lax.axis_index("wa"), lax.axis_size("wa") - 1
    r = jnp.arange(rows)
    c = jnp.arange(cols)
    row_ok = jnp.logical_and(
        jnp.logical_or(r >= low_pad, h > 0), jnp.logical_or(r < rows - 1, h < h_last)
    )
    col_ok = jnp.logical_and(
        jnp.logical_or(c >= low_pad, w > 0), jnp.logical_or(c < cols - 1, w < w_last)
    )
    return jnp.logical_and(row_ok[:, None], col_ok[None, :])[None, :, :, None]


def latent_halo(x):
    h_size, w_size = lax.axis_size("ha"), lax.axis_size("wa")
    below = passed_along(x[:, :1], "ha", -1)
    right = passed_along(x[:, :, :1], "wa", -1)
    corner_route = [
        ((h + 1) * w_size + w + 1, h * w_size + w)
        for h in range(h_size - 1)
        for w in range(w_size - 1)
    ]
    corner = lax.ppermute(x[:, :1, :1], ("ha", "wa"), corner_route)
    top = jnp.concatenate([x, right], axis=2)
    bottom = jnp.concatenate([below, corner], axis=2)
    return jnp.concatenate([top, bottom], axis=1)


def upsample(act, kernel):
    frames, rows, cols, channels = act.shape
    height, across = rows - 1, cols - 1
    flat = lambda v: v.reshape(-1, channels)
    dot = lambda v, w: jnp.dot(flat(v), w, preferred_element_type=jnp.float32)
    a = act[:, :height, :across]
    b = act[:, :height, 1:]
    c = act[:, 1:, :across]
    d = act[:, 1:, 1:]
    out = kernel.shape[-1]
    pa = dot(a, jnp.concatenate([kernel[1, 1], kernel[1, 2], kernel[2, 1], kernel[2, 2]], axis=1))
    pb = dot(b, jnp.concatenate([kernel[1, 0], kernel[2, 0]], axis=1))
    pc = dot(c, jnp.concatenate([kernel[0, 1], kernel[0, 2]], axis=1))
    pd = dot(d, kernel[0, 0])
    ee = pa[:, :out]
    eo = pa[:, out : 2 * out] + pb[:, :out]
    oe = pa[:, 2 * out : 3 * out] + pc[:, :out]
    oo = pa[:, 3 * out :] + pb[:, out:] + pc[:, out:] + pd
    shape = (frames, height, across, 1, out)
    even = jnp.concatenate([ee.reshape(shape), eo.reshape(shape)], axis=3)
    odd = jnp.concatenate([oe.reshape(shape), oo.reshape(shape)], axis=3)
    even = even.reshape(frames, height, 1, 2 * across, out)
    odd = odd.reshape(frames, height, 1, 2 * across, out)
    return jnp.concatenate([even, odd], axis=2).reshape(frames, 2 * height, 2 * across, out)


def valid_conv(padded, kernel, frames, height, across):
    result = jnp.zeros((frames * height * across, kernel.shape[-1]), jnp.float32)
    for step_t in range(3):
        for step_y in range(3):
            for step_x in range(3):
                window = padded[
                    step_t : step_t + frames, step_y : step_y + height, step_x : step_x + across
                ]
                result = result + jnp.dot(
                    window.reshape(-1, window.shape[-1]),
                    kernel[step_t, step_y, step_x],
                    preferred_element_type=jnp.float32,
                )
    return result.reshape(frames, height, across, -1)


def conv_halo(values):
    x = padded_2(values, (("ha", 1), ("wa", 2)), 1)
    earlier = passed_along(x[-2:], "ta", 1)
    opening = jnp.concatenate([x[:1], x[:1]], axis=0)
    earlier = jnp.where(lax.axis_index("ta") == 0, opening, earlier)
    return jnp.concatenate([earlier, x], axis=0)


def norm_conv(values, gain, shift, kernel):
    frames, height, across, _ = values.shape
    values_f = values.astype(jnp.float32)
    stats = group_stats(values_f)
    extended = conv_halo(values).astype(jnp.float32)
    act = activate(extended, stats, gain, shift)
    act = jnp.where(inside_mask(height + 2, across + 2, 1), act, 0.0).astype(jnp.bfloat16)
    return valid_conv(act, kernel, frames, height, across)


def per_device(
    latents,
    norm1_gain,
    norm1_shift,
    up_weight,
    norm2_gain,
    norm2_shift,
    conv_a,
    norm3_gain,
    norm3_shift,
    conv_b,
):
    frames, height, across, channels = latents.shape
    stats = group_stats(latents.astype(jnp.float32))
    extended = latent_halo(latents).astype(jnp.float32)
    activated = activate(extended, stats, norm1_gain, norm1_shift)
    activated = jnp.where(inside_mask(height + 1, across + 1, 0), activated, 0.0)
    lifted = upsample(activated.astype(jnp.bfloat16), up_weight).astype(jnp.bfloat16)
    hidden = norm_conv(lifted, norm2_gain, norm2_shift, conv_a).astype(jnp.bfloat16)
    branch = norm_conv(hidden, norm3_gain, norm3_shift, conv_b)
    return (lifted.astype(jnp.float32) + branch).astype(jnp.bfloat16)


def solution(mesh):
    return jax.shard_map(
        per_device,
        mesh=mesh,
        in_specs=(
            P(("videos", "ta"), "ha", "wa", None),
            P(),
            P(),
            P(),
            P(),
            P(),
            P(),
            P(),
            P(),
            P(),
        ),
        out_specs=P(("videos", "ta"), "ha", "wa", None),
        check_vma=False,
    )
```

time: 143 us -> 99.3 us (0.69)
  waiting for transfers between devices: 43.6 us -> 15.4 us
  other arithmetic: 18.9 us -> 8.73 us
  matrix products: 20.1 us -> 16.3 us
  local copies, waits for them, and re-layouts: 13 us -> 10.2 us
    ppermute x18, waiting for transfers between devices: 15.3 us -> 3.9 us  [group_allreduce(): lax.ppermute(x, axes, [(i, i ^ d << shift) for i in range(count)])]
    concatenate x6 -> x2, other arithmetic: 10.2 us -> 0.31 us  [padded_2(): x = jnp.concatenate([before, x, after], axis=dim)]
    ppermute x4, waiting for transfers between devices: 12.2 us -> 2.9 us  [passed_along(): return lax.ppermute(block, axis, route)]
    ppermute x4, waiting for transfers between devices: 13.7 us -> 8.54 us  [padded_2(): after = lax.ppermute(initial, axis, down)]
    slice x56 -> x4, local copies, waits for them, and re-layouts: 8.07 us -> 4.76 us  [valid_conv(): padded[step_t:step_t + frames, step_y:step_y + height, step_x:step_x + ac...]
    dot_general x6 -> x4, matrix products: 5.07 us -> 2.06 us  [upsample(): dot = lambda v, w: jnp.dot(flat(v), w, preferred_element_type=jnp.float32)]
    ppermute x4, starting transfers between devices: 14.6 us -> 12.1 us  [padded_2(): before = lax.ppermute(last, axis, up)]
    ppermute x4, waiting for transfers between devices: 2.37 us -> 0.09 us  [padded_2(): before = lax.ppermute(last, axis, up)]
  transfers between devices with their start and end apart: 30 -> 31, of which waited for: 23 -> 10; matrix products, arithmetic and copies ran while one was open for 5% -> 5% of each run, Pallas kernels for 0% -> 0%
where the time goes in v2:
time: 99.3 us; the launch traced here: 98.7 us
  starting transfers between devices  46.9 us (47%)
  matrix products  16.3 us (16%)
  waiting for transfers between devices  15.4 us (16%)
  local copies, waits for them, and re-layouts  10.2 us (10%)
  other arithmetic  8.73 us (9%)
  between operations  1.14 us (1%)
    ppermute x18, starting transfers between devices, group_allreduce(): lax.ppermute(x, axes, [(i, i ^ d << shift) for i in range(count)])  22.7 us
    dot_general x54, matrix products, valid_conv(): jnp.dot(window.reshape(-1, window.shape[-1]), kernel[step_t, step_y, step...  14.2 us
    ppermute x4, starting transfers between devices, padded_2(): before = lax.ppermute(last, axis, up)  12.1 us
    ppermute x4, waiting for transfers between devices, padded_2(): after = lax.ppermute(initial, axis, down)  8.54 us
    ppermute x4, starting transfers between devices, passed_along(): return lax.ppermute(block, axis, route)  5.62 us
    ppermute x4, starting transfers between devices, padded_2(): after = lax.ppermute(initial, axis, down)  5.17 us
    slice x4, local copies, waits for them, and re-layouts, valid_conv(): padded[step_t:step_t + frames, step_y:step_y + height, step_x:step_x + ac...  4.76 us
    ppermute x18, waiting for transfers between devices, group_allreduce(): lax.ppermute(x, axes, [(i, i ^ d << shift) for i in range(count)])  3.9 us
  transfers between devices with their start and end apart: 31, of which 10 were waited for; matrix products, arithmetic and copies ran while one was open for 5% of the time, Pallas kernels for 0%

profile of v2, /device:TPU:0, one launch (start us, length us, event | category | flops | bytes accessed | tf_op | source)
XLA Modules:
  0.0 98.7 jit_solution(10026948767929639997)
XLA Ops:
  0.0 1.1 %convert_reduce_fusion.2 = (f32[512]{0:T(512)S(1)}, f32[512]{0:T(512)S(1)}) fusion(bf16[3,2,32,512]{3,2,1,0:T(8,128)(2,1)} %param.10), kind=kLoop, calls=%fused_computation.82 | loop fusion | flops 392192 | bytes 200704 | tf_op jit(solution)/shard_map/reduce_sum | solution.py:75
  1.5 0.5 collective-permute-start.5
  2.0 2.6 %collective-permute-start.4 = (f32[2,32]{1,0:T(2,128)S(1)}, f32[2,32]{1,0:T(2,128)S(1)}, u32[]{:S(2)}, u32[]{:S(2)}) collective-permute-start(f32[2,32]{1,0:T(2,128)S(1)} %pad_maximum_fusion.18), channel_id=1, source_target_pairs={{0,2},{1,3},{2,0},{3,1},{4,6},{5,7},{6,4},{7,5},{8,10},{9,11},{10,... | collective-permute-start | bytes 776 | tf_op jit(solution)/shard_map/ppermute | solution.py:47
  4.6 0.7 slice.436
  5.4 1.3 %collective-permute-start.2 = (bf16[3,1,1,512]{3,2,1,0:T(2,128)(2,1)S(1)}, bf16[3,1,1,512]{3,2,1,0:T(2,128)(2,1)S(1)}, u32[]{:S(2)}, u32[]{:S(2)}) collective-permute-start(bf16[3,1,1,512]{3,2,1,0:T(2,128)(2,1)S(1)} %slice.436), channel_id=1, source_target_pairs={{6,0},{10,4},{14,8},{7,1},{11,5},{15,9},{22,16},{26,20},{30,24},{2... | collective-permute-start | bytes 9224 | tf_op jit(solution)/shard_map/ppermute | solution.py:113
  6.7 0.8 slice.434
  7.5 1.3 %collective-permute-start = (bf16[3,2,1,512]{3,2,1,0:T(2,128)(2,1)S(1)}, bf16[3,2,1,512]{3,2,1,0:T(2,128)(2,1)S(1)}, u32[]{:S(2)}, u32[]{:S(2)}) collective-permute-start(bf16[3,2,1,512]{3,2,1,0:T(2,128)(2,1)S(1)} %slice.434), channel_id=1, source_target_pairs={{2,0},{3,1},{6,4},{7,5},{10,8},{11,9},{14,12},{15,13},{18,16},{19,... | collective-permute-start | bytes 18440 | tf_op jit(solution)/shard_map/ppermute | solution.py:15
  8.9 1.6 %slice_bitcast_fusion.7 = (bf16[512,256]{1,0:T(8,128)(2,1)S(1)}, bf16[512,256]{1,0:T(8,128)(2,1)S(1)}, bf16[512,256]{1,0:T(8,128)(2,1)S(1)}, bf16[512,256]{1,0:T...) fusion(bf16[3,3,512,256]{3,2,1,0:T(8,128)(2,1)} %param.13), kind=kLoop, calls=%fused_computation.105 | loop fusion | bytes 4194304 | tf_op jit(solution)/shard_map/squeeze | solution.py:129
  10.8 1.9 %collective-permute-start.8 = (f32[2,32]{1,0:T(2,128)S(1)}, f32[2,32]{1,0:T(2,128)S(1)}, u32[]{:S(2)}, u32[]{:S(2)}) collective-permute-start(f32[2,32]{1,0:T(2,128)S(1)} %add_add_fusion.5), channel_id=1, source_target_pairs={{0,4},{1,5},{2,6},{3,7},{4,0},{5,1},{6,2},{7,3},{8,12},{9,13},{10,... | collective-permute-start | bytes 776 | tf_op jit(solution)/shard_map/ppermute | solution.py:47
  12.6 2.0 %collective-permute-start.7 = (f32[2,32]{1,0:T(2,128)S(1)}, f32[2,32]{1,0:T(2,128)S(1)}, u32[]{:S(2)}, u32[]{:S(2)}) collective-permute-start(f32[2,32]{1,0:T(2,128)S(1)} %add_add_fusion.5), channel_id=1, source_target_pairs={{0,8},{1,9},{2,10},{3,11},{4,12},{5,13},{6,14},{7,15},{8,0},{9,1},... | collective-permute-start | bytes 776 | tf_op jit(solution)/shard_map/ppermute | solution.py:47
  14.6 0.6 collective-permute-start.6
  15.2 1.3 %collective-permute-start.1 = (bf16[3,1,32,512]{3,2,1,0:T(8,128)(2,1)S(1)}, bf16[3,1,32,512]{3,2,1,0:T(8,128)(2,1)S(1)}, u32[]{:S(2)}, u32[]{:S(2)}) collective-permute-start(bf16[3,1,32,512]{3,2,1,0:T(8,128)(2,1)S(1)} %slice.435), channel_id=1, source_target_pairs={{4,0},{8,4},{12,8},{5,1},{9,5},{13,9},{6,2},{10,6},{14,10},{7,3},{... | collective-permute-start | bytes 294920 | tf_op jit(solution)/shard_map/ppermute | solution.py:15
  16.5 0.6 collective-permute-done.7
  17.1 2.9 %collective-permute-done.6 = f32[2,32]{1,0:T(2,128)S(1)} collective-permute-done((f32[2,32]{1,0:T(2,128)S(1)}, f32[2,32]{1,0:T(2,128)S(1)}, u32[]{:S(2)}, u32[]{:S(2)}) %collective-permute-start.6) | collective-permute-done | bytes 288 | tf_op jit(solution)/shard_map/ppermute | solution.py:47
  20.3 1.4 %collective-permute-done.1 = bf16[3,1,32,512]{3,2,1,0:T(8,128)(2,1)S(1)} collective-permute-done((bf16[3,1,32,512]{3,2,1,0:T(8,128)(2,1)S(1)}, bf16[3,1,32,512]{3,2,1,0:T(8,128)(2,1)S(1)}, u32[]{:S(2)}, u32[]{:S(2)}) %collective-permute-start.1) | collective-permute-done | bytes 98336 | tf_op jit(solution)/shard_map/ppermute | solution.py:15
  23.2 1.2 %convolution_add_fusion.52 = bf16[192,256]{1,0:T(8,128)(2,1)S(1)} fusion(bf16[192,512]{1,0:T(8,128)(2,1)S(1)} %bitcast.410, bf16[3,3,512,256]{3,2,1,0:T(8,128)(2,1)} %param.13, f32[192,512]{1,0:T(8,128)S(1)} %fusion.15, f32[192,512]{1,0:T(8,128)S(1)} %fusion.11, f32[192,1024]{1,0:T(8,128)S(1)} %fusion.1), kind=kOutput, calls=%fused_computation.55 | convolution fusion | flops 50528256 | bytes 1146880 | tf_op jit(solution)/shard_map/dot_general | solution.py:123
  25.4 0.8 convert_reduce_fusion.1
  26.7 2.7 %collective-permute-start.15 = (f32[2,32]{1,0:T(2,128)S(1)}, f32[2,32]{1,0:T(2,128)S(1)}, u32[]{:S(2)}, u32[]{:S(2)}) collective-permute-start(f32[2,32]{1,0:T(2,128)S(1)} %pad_maximum_fusion.19), channel_id=1, source_target_pairs={{0,2},{1,3},{2,0},{3,1},{4,6},{5,7},{6,4},{7,5},{8,10},{9,11},{10,... | collective-permute-start | bytes 776 | tf_op jit(solution)/shard_map/ppermute | solution.py:47
  29.5 2.9 %collective-permute-start.9 = (bf16[3,1,64,256]{3,2,1,0:T(8,128)(2,1)S(1)}, bf16[3,1,64,256]{3,2,1,0:T(8,128)(2,1)S(1)}, u32[]{:S(2)}, u32[]{:S(2)}) collective-permute-start(bf16[3,1,64,256]{3,2,1,0:T(8,128)(2,1)S(1)} %get-tuple-element.83), channel_id=1, source_target_pairs={{0,4},{4,8},{8,12},{1,5},{5,9},{9,13},{2,6},{6,10},{10,14},{3,7},{... | collective-permute-start | bytes 294920 | tf_op jit(solution)/shard_map/ppermute | solution.py:25
  32.4 1.3 %collective-permute-start.10 = (bf16[3,1,64,256]{3,2,1,0:T(8,128)(2,1)S(1)}, bf16[3,1,64,256]{3,2,1,0:T(8,128)(2,1)S(1)}, u32[]{:S(2)}, u32[]{:S(2)}) collective-permute-start(bf16[3,1,64,256]{3,2,1,0:T(8,128)(2,1)S(1)} %get-tuple-element.84), channel_id=1, source_target_pairs={{4,0},{8,4},{12,8},{5,1},{9,5},{13,9},{6,2},{10,6},{14,10},{7,3},{... | collective-permute-start | bytes 294920 | tf_op jit(solution)/shard_map/ppermute | solution.py:26
  33.8 2.7 %collective-permute-start.19 = (f32[2,32]{1,0:T(2,128)S(1)}, f32[2,32]{1,0:T(2,128)S(1)}, u32[]{:S(2)}, u32[]{:S(2)}) collective-permute-start(f32[2,32]{1,0:T(2,128)S(1)} %add_add_fusion.3), channel_id=1, source_target_pairs={{0,4},{1,5},{2,6},{3,7},{4,0},{5,1},{6,2},{7,3},{8,12},{9,13},{10,... | collective-permute-start | bytes 776 | tf_op jit(solution)/shard_map/ppermute | solution.py:47
  36.5 1.1 %collective-permute-start.18 = (f32[2,32]{1,0:T(2,128)S(1)}, f32[2,32]{1,0:T(2,128)S(1)}, u32[]{:S(2)}, u32[]{:S(2)}) collective-permute-start(f32[2,32]{1,0:T(2,128)S(1)} %add_add_fusion.3), channel_id=1, source_target_pairs={{0,8},{1,9},{2,10},{3,11},{4,12},{5,13},{6,14},{7,15},{8,0},{9,1},... | collective-permute-start | bytes 776 | tf_op jit(solution)/shard_map/ppermute | solution.py:47
  37.6 1.4 %collective-permute-start.17 = (f32[2,32]{1,0:T(2,128)S(1)}, f32[2,32]{1,0:T(2,128)S(1)}, u32[]{:S(2)}, u32[]{:S(2)}) collective-permute-start(f32[2,32]{1,0:T(2,128)S(1)} %add_add_fusion.3), channel_id=1, source_target_pairs={{0,12},{1,13},{2,14},{3,15},{4,8},{5,9},{6,10},{7,11},{8,4},{9,5},... | collective-permute-start | bytes 776 | tf_op jit(solution)/shard_map/ppermute | solution.py:47
  39.0 3.8 %collective-permute-start.11 = (bf16[3,6,1,256]{3,2,1,0:T(2,128)(2,1)S(1)}, bf16[3,6,1,256]{3,2,1,0:T(2,128)(2,1)S(1)}, u32[]{:S(2)}, u32[]{:S(2)}) collective-permute-start(bf16[3,6,1,256]{3,2,1,0:T(2,128)(2,1)S(1)} %get-tuple-element.79), channel_id=1, source_target_pairs={{0,2},{1,3},{4,6},{5,7},{8,10},{9,11},{12,14},{13,15},{16,18},{17,... | collective-permute-start | bytes 27656 | tf_op jit(solution)/shard_map/ppermute | solution.py:25
  42.8 1.3 %collective-permute-start.12 = (bf16[3,6,1,256]{3,2,1,0:T(2,128)(2,1)S(1)}, bf16[3,6,1,256]{3,2,1,0:T(2,128)(2,1)S(1)}, u32[]{:S(2)}, u32[]{:S(2)}) collective-permute-start(bf16[3,6,1,256]{3,2,1,0:T(2,128)(2,1)S(1)} %get-tuple-element.80), channel_id=1, source_target_pairs={{2,0},{3,1},{6,4},{7,5},{10,8},{11,9},{14,12},{15,13},{18,16},{19,... | collective-permute-start | bytes 27656 | tf_op jit(solution)/shard_map/ppermute | solution.py:26
  44.2 4.2 %collective-permute-done.12 = bf16[3,6,1,256]{3,2,1,0:T(2,128)(2,1)S(1)} collective-permute-done((bf16[3,6,1,256]{3,2,1,0:T(2,128)(2,1)S(1)}, bf16[3,6,1,256]{3,2,1,0:T(2,128)(2,1)S(1)}, u32[]{:S(2)}, u32[]{:S(2)}) %collective-permute-start.12) | collective-permute-done | bytes 9248 | tf_op jit(solution)/shard_map/ppermute | solution.py:26
  48.6 1.5 %collective-permute-start.13 = (bf16[2,6,66,256]{3,2,1,0:T(8,128)(2,1)S(1)}, bf16[2,6,66,256]{3,2,1,0:T(8,128)(2,1)S(1)}, u32[]{:S(2)}, u32[]{:S(2)}) collective-permute-start(bf16[2,6,66,256]{3,2,1,0:T(8,128)(2,1)S(1)} %pad_maximum_fusion.4), channel_id=1, source_target_pairs={{0,1},{2,3},{4,5},{6,7},{8,9},{10,11},{12,13},{14,15},{16,17},{18,... | collective-permute-start | bytes 1216520 | tf_op jit(solution)/shard_map/ppermute | solution.py:15
  50.5 0.8 collective-permute-done.13
  51.4 1.7 %select_convert_fusion.1 = bf16[5,6,66,256]{3,2,1,0:T(8,128)(2,1)S(1)} fusion(bf16[3,6,1,256]{3,2,1,0:T(2,128)(2,1)S(1)} %collective-permute-done.12, bf16[3,1,64,256]{3,2,1,0:T(8,128)(2,1)S(1)} %collective-permute-done.10, bf16[3,4,64,256]{3,2,1,0:T(8,128)(2,1)S(1)} %bitcast.348, bf16[3,1,64,256]{3,2,1,0:T(8,128)(2,1)S(1)} %collective-permute-done.9, ...), kind=kLoop, calls=%fused_computation.1 | loop fusion | flops 11151360 | bytes 2032012 | tf_op jit(solution)/shard_map/convert_element_type | solution.py:175
  53.1 0.5 fusion.144
  53.6 1.9 %fusion.143 = (bf16[3,4,64,256]{3,2,1,0:T(8,128)(2,1)S(1)}, bf16[3,4,64,256]{3,2,1,0:T(8,128)(2,1)S(1)}, bf16[3,4,64,256]{3,2,1,0:T(8,128)(2,1)S(1)}, bf16[3,4,6...) fusion(bf16[5,6,66,256]{3,2,1,0:T(8,128)(2,1)S(1)} %select_conv, ...), kind=kLoop, calls=%fused_computation.260 | loop fusion | bytes 14942208 | tf_op jit(solution)/shard_map/slice | solution.py:150
  63.4 0.4 collective-permute-start.27
  63.8 1.5 %collective-permute-start.25 = (f32[2,32]{1,0:T(2,128)S(1)}, f32[2,32]{1,0:T(2,128)S(1)}, u32[]{:S(2)}, u32[]{:S(2)}) collective-permute-start(f32[2,32]{1,0:T(2,128)S(1)} %pad_maximum_fusion.20), channel_id=1, source_target_pairs={{0,3},{1,2},{2,1},{3,0},{4,7},{5,6},{6,5},{7,4},{8,11},{9,10},{10,... | collective-permute-start | bytes 776 | tf_op jit(solution)/shard_map/ppermute | solution.py:47
  65.3 3.5 %collective-permute-start.20 = (bf16[3,1,64,256]{3,2,1,0:T(8,128)(2,1)S(1)}, bf16[3,1,64,256]{3,2,1,0:T(8,128)(2,1)S(1)}, u32[]{:S(2)}, u32[]{:S(2)}) collective-permute-start(bf16[3,1,64,256]{3,2,1,0:T(8,128)(2,1)S(1)} %get-tuple-element.81), channel_id=1, source_target_pairs={{0,4},{4,8},{8,12},{1,5},{5,9},{9,13},{2,6},{6,10},{10,14},{3,7},{... | collective-permute-start | bytes 294920 | tf_op jit(solution)/shard_map/ppermute | solution.py:25
  68.8 1.3 %collective-permute-start.21 = (bf16[3,1,64,256]{3,2,1,0:T(8,128)(2,1)S(1)}, bf16[3,1,64,256]{3,2,1,0:T(8,128)(2,1)S(1)}, u32[]{:S(2)}, u32[]{:S(2)}) collective-permute-start(bf16[3,1,64,256]{3,2,1,0:T(8,128)(2,1)S(1)} %get-tuple-element.82), channel_id=1, source_target_pairs={{4,0},{8,4},{12,8},{5,1},{9,5},{13,9},{6,2},{10,6},{14,10},{7,3},{... | collective-permute-start | bytes 294920 | tf_op jit(solution)/shard_map/ppermute | solution.py:26
  70.2 2.7 %collective-permute-start.30 = (f32[2,32]{1,0:T(2,128)S(1)}, f32[2,32]{1,0:T(2,128)S(1)}, u32[]{:S(2)}, u32[]{:S(2)}) collective-permute-start(f32[2,32]{1,0:T(2,128)S(1)} %add_add_fusion.1), channel_id=1, source_target_pairs={{0,4},{1,5},{2,6},{3,7},{4,0},{5,1},{6,2},{7,3},{8,12},{9,13},{10,... | collective-permute-start | bytes 776 | tf_op jit(solution)/shard_map/ppermute | solution.py:47
  72.9 1.3 %collective-permute-start.29 = (f32[2,32]{1,0:T(2,128)S(1)}, f32[2,32]{1,0:T(2,128)S(1)}, u32[]{:S(2)}, u32[]{:S(2)}) collective-permute-start(f32[2,32]{1,0:T(2,128)S(1)} %add_add_fusion.1), channel_id=1, source_target_pairs={{0,8},{1,9},{2,10},{3,11},{4,12},{5,13},{6,14},{7,15},{8,0},{9,1},... | collective-permute-start | bytes 776 | tf_op jit(solution)/shard_map/ppermute | solution.py:47
  74.2 1.1 %collective-permute-start.28 = (f32[2,32]{1,0:T(2,128)S(1)}, f32[2,32]{1,0:T(2,128)S(1)}, u32[]{:S(2)}, u32[]{:S(2)}) collective-permute-start(f32[2,32]{1,0:T(2,128)S(1)} %add_add_fusion.1), channel_id=1, source_target_pairs={{0,12},{1,13},{2,14},{3,15},{4,8},{5,9},{6,10},{7,11},{8,4},{9,5},... | collective-permute-start | bytes 776 | tf_op jit(solution)/shard_map/ppermute | solution.py:47
  75.3 0.4 collective-permute-done.21
  75.8 2.0 %collective-permute-start.22 = (bf16[3,6,1,256]{3,2,1,0:T(2,128)(2,1)S(1)}, bf16[3,6,1,256]{3,2,1,0:T(2,128)(2,1)S(1)}, u32[]{:S(2)}, u32[]{:S(2)}) collective-permute-start(bf16[3,6,1,256]{3,2,1,0:T(2,128)(2,1)S(1)} %get-tuple-element.77), channel_id=1, source_target_pairs={{0,2},{1,3},{4,6},{5,7},{8,10},{9,11},{12,14},{13,15},{16,18},{17,... | collective-permute-start | bytes 27656 | tf_op jit(solution)/shard_map/ppermute | solution.py:25
  77.8 1.3 %collective-permute-start.23 = (bf16[3,6,1,256]{3,2,1,0:T(2,128)(2,1)S(1)}, bf16[3,6,1,256]{3,2,1,0:T(2,128)(2,1)S(1)}, u32[]{:S(2)}, u32[]{:S(2)}) collective-permute-start(bf16[3,6,1,256]{3,2,1,0:T(2,128)(2,1)S(1)} %get-tuple-element.78), channel_id=1, source_target_pairs={{2,0},{3,1},{6,4},{7,5},{10,8},{11,9},{14,12},{15,13},{18,16},{19,... | collective-permute-start | bytes 27656 | tf_op jit(solution)/shard_map/ppermute | solution.py:26
  79.6 3.9 %collective-permute-done.23 = bf16[3,6,1,256]{3,2,1,0:T(2,128)(2,1)S(1)} collective-permute-done((bf16[3,6,1,256]{3,2,1,0:T(2,128)(2,1)S(1)}, bf16[3,6,1,256]{3,2,1,0:T(2,128)(2,1)S(1)}, u32[]{:S(2)}, u32[]{:S(2)}) %collective-permute-start.23) | collective-permute-done | bytes 9248 | tf_op jit(solution)/shard_map/ppermute | solution.py:26
  83.6 1.5 %collective-permute-start.24 = (bf16[2,6,66,256]{3,2,1,0:T(8,128)(2,1)S(1)}, bf16[2,6,66,256]{3,2,1,0:T(8,128)(2,1)S(1)}, u32[]{:S(2)}, u32[]{:S(2)}) collective-permute-start(bf16[2,6,66,256]{3,2,1,0:T(8,128)(2,1)S(1)} %pad_maximum_fusion), channel_id=1, source_target_pairs={{0,1},{2,3},{4,5},{6,7},{8,9},{10,11},{12,13},{14,15},{16,17},{18,... | collective-permute-start | bytes 1216520 | tf_op jit(solution)/shard_map/ppermute | solution.py:15
  85.6 0.7 collective-permute-done.24
  86.4 1.7 %select_convert_fusion = bf16[5,6,66,256]{3,2,1,0:T(8,128)(2,1)S(1)} fusion(bf16[3,6,1,256]{3,2,1,0:T(2,128)(2,1)S(1)} %collective-permute-done.23, bf16[3,1,64,256]{3,2,1,0:T(8,128)(2,1)S(1)} %collective-permute-done.21, bf16[3,4,64,256]{3,2,1,0:T(8,128)(2,1)S(1)} %bitcast.354, bf16[3,1,64,256]{3,2,1,0:T(8,128)(2,1)S(1)} %collective-permute-done.20, ...), kind=kLoop, calls=%fused_computation | loop fusion | flops 11151360 | bytes 2032012 | tf_op jit(solution)/shard_map/convert_element_type | solution.py:175
  88.1 0.5 fusion.142
  88.6 1.9 %fusion.141 = (bf16[3,4,64,256]{3,2,1,0:T(8,128)(2,1)S(1)}, bf16[3,4,64,256]{3,2,1,0:T(8,128)(2,1)S(1)}, bf16[3,4,64,256]{3,2,1,0:T(8,128)(2,1)S(1)}, bf16[3,4,6...) fusion(bf16[5,6,66,256]{3,2,1,0:T(8,128)(2,1)S(1)} %select_conv, ...), kind=kLoop, calls=%fused_computation.258 | loop fusion | bytes 14942208 | tf_op jit(solution)/shard_map/slice | solution.py:150
  97.9 0.8 add_convert_fusion
  (168 shorter events, 20.8 us)
Async XLA Ops:
  0.0 15.2 %copy-start.2 = (bf16[3,2,32,512]{3,2,1,0:T(8,128)(2,1)S(1)}, bf16[3,2,32,512]{3,2,1,0:T(8,128)(2,1)}, u32[]{:S(2)}) copy-start(bf16[3,2,32,512]{3,2,1,0:T(8,128)(2,1)} %param.10) | copy-start | bytes 589828
  0.0 21.8 %copy-start.3 = (f32[512]{0:T(512)S(1)}, f32[512]{0:T(512)}, u32[]{:S(2)}) copy-start(f32[512]{0:T(512)} %param.12) | copy-start | bytes 6148
  0.0 21.8 %copy-start.4 = (f32[512]{0:T(512)S(1)}, f32[512]{0:T(512)}, u32[]{:S(2)}) copy-start(f32[512]{0:T(512)} %param.11) | copy-start | bytes 6148
  1.5 9.2 %collective-permute-start.5 = (f32[2,32]{1,0:T(2,128)S(1)}, f32[2,32]{1,0:T(2,128)S(1)}, u32[]{:S(2)}, u32[]{:S(2)}) collective-permute-start(f32[2,32]{1,0:T(2,128)S(1)} %pad_maximum_fusion.18), channel_id=1, source_target_pairs={{0,1},{1,0},{2,3},{3,2},{4,5},{5,4},{6,7},{7,6},{8,9},{9,8},{10,11... | collective-permute-start | bytes 776 | tf_op jit(solution)/shard_map/ppermute | solution.py:47
  2.0 8.7 %collective-permute-start.4 = (f32[2,32]{1,0:T(2,128)S(1)}, f32[2,32]{1,0:T(2,128)S(1)}, u32[]{:S(2)}, u32[]{:S(2)}) collective-permute-start(f32[2,32]{1,0:T(2,128)S(1)} %pad_maximum_fusion.18), channel_id=1, source_target_pairs={{0,2},{1,3},{2,0},{3,1},{4,6},{5,7},{6,4},{7,5},{8,10},{9,11},{10,... | collective-permute-start | bytes 776 | tf_op jit(solution)/shard_map/ppermute | solution.py:47
  4.6 6.2 %collective-permute-start.3 = (f32[2,32]{1,0:T(2,128)S(1)}, f32[2,32]{1,0:T(2,128)S(1)}, u32[]{:S(2)}, u32[]{:S(2)}) collective-permute-start(f32[2,32]{1,0:T(2,128)S(1)} %pad_maximum_fusion.18), channel_id=1, source_target_pairs={{0,3},{1,2},{2,1},{3,0},{4,7},{5,6},{6,5},{7,4},{8,11},{9,10},{10,... | collective-permute-start | bytes 776 | tf_op jit(solution)/shard_map/ppermute | solution.py:47
  5.4 15.0 %collective-permute-start.2 = (bf16[3,1,1,512]{3,2,1,0:T(2,128)(2,1)S(1)}, bf16[3,1,1,512]{3,2,1,0:T(2,128)(2,1)S(1)}, u32[]{:S(2)}, u32[]{:S(2)}) collective-permute-start(bf16[3,1,1,512]{3,2,1,0:T(2,128)(2,1)S(1)} %slice.436), channel_id=1, source_target_pairs={{6,0},{10,4},{14,8},{7,1},{11,5},{15,9},{22,16},{26,20},{30,24},{2... | collective-permute-start | bytes 9224 | tf_op jit(solution)/shard_map/ppermute | solution.py:113
  7.5 12.9 %collective-permute-start = (bf16[3,2,1,512]{3,2,1,0:T(2,128)(2,1)S(1)}, bf16[3,2,1,512]{3,2,1,0:T(2,128)(2,1)S(1)}, u32[]{:S(2)}, u32[]{:S(2)}) collective-permute-start(bf16[3,2,1,512]{3,2,1,0:T(2,128)(2,1)S(1)} %slice.434), channel_id=1, source_target_pairs={{2,0},{3,1},{6,4},{7,5},{10,8},{11,9},{14,12},{15,13},{18,16},{19,... | collective-permute-start | bytes 18440 | tf_op jit(solution)/shard_map/ppermute | solution.py:15
  10.8 4.5 %collective-permute-start.8 = (f32[2,32]{1,0:T(2,128)S(1)}, f32[2,32]{1,0:T(2,128)S(1)}, u32[]{:S(2)}, u32[]{:S(2)}) collective-permute-start(f32[2,32]{1,0:T(2,128)S(1)} %add_add_fusion.5), channel_id=1, source_target_pairs={{0,4},{1,5},{2,6},{3,7},{4,0},{5,1},{6,2},{7,3},{8,12},{9,13},{10,... | collective-permute-start | bytes 776 | tf_op jit(solution)/shard_map/ppermute | solution.py:47
  12.6 4.5 %collective-permute-start.7 = (f32[2,32]{1,0:T(2,128)S(1)}, f32[2,32]{1,0:T(2,128)S(1)}, u32[]{:S(2)}, u32[]{:S(2)}) collective-permute-start(f32[2,32]{1,0:T(2,128)S(1)} %add_add_fusion.5), channel_id=1, source_target_pairs={{0,8},{1,9},{2,10},{3,11},{4,12},{5,13},{6,14},{7,15},{8,0},{9,1},... | collective-permute-start | bytes 776 | tf_op jit(solution)/shard_map/ppermute | solution.py:47
  14.6 5.4 %collective-permute-start.6 = (f32[2,32]{1,0:T(2,128)S(1)}, f32[2,32]{1,0:T(2,128)S(1)}, u32[]{:S(2)}, u32[]{:S(2)}) collective-permute-start(f32[2,32]{1,0:T(2,128)S(1)} %add_add_fusion.5), channel_id=1, source_target_pairs={{0,12},{1,13},{2,14},{3,15},{4,8},{5,9},{6,10},{7,11},{8,4},{9,5},... | collective-permute-start | bytes 776 | tf_op jit(solution)/shard_map/ppermute | solution.py:47
  15.2 6.5 %collective-permute-start.1 = (bf16[3,1,32,512]{3,2,1,0:T(8,128)(2,1)S(1)}, bf16[3,1,32,512]{3,2,1,0:T(8,128)(2,1)S(1)}, u32[]{:S(2)}, u32[]{:S(2)}) collective-permute-start(bf16[3,1,32,512]{3,2,1,0:T(8,128)(2,1)S(1)} %slice.435), channel_id=1, source_target_pairs={{4,0},{8,4},{12,8},{5,1},{9,5},{13,9},{6,2},{10,6},{14,10},{7,3},{... | collective-permute-start | bytes 294920 | tf_op jit(solution)/shard_map/ppermute | solution.py:15
  24.6 26.8 %copy-start.5 = (f32[256]{0:T(256)S(1)}, f32[256]{0:T(256)}, u32[]{:S(2)}) copy-start(f32[256]{0:T(256)} %param.15) | copy-start | bytes 3076
  24.6 26.8 %copy-start.6 = (f32[256]{0:T(256)S(1)}, f32[256]{0:T(256)}, u32[]{:S(2)}) copy-start(f32[256]{0:T(256)} %param.14) | copy-start | bytes 3076
  26.6 7.1 %collective-permute-start.16 = (f32[2,32]{1,0:T(2,128)S(1)}, f32[2,32]{1,0:T(2,128)S(1)}, u32[]{:S(2)}, u32[]{:S(2)}) collective-permute-start(f32[2,32]{1,0:T(2,128)S(1)} %pad_maximum_fusion.19), channel_id=1, source_target_pairs={{0,1},{1,0},{2,3},{3,2},{4,5},{5,4},{6,7},{7,6},{8,9},{9,8},{10,11... | collective-permute-start | bytes 776 | tf_op jit(solution)/shard_map/ppermute | solution.py:47
  26.7 7.0 %collective-permute-start.15 = (f32[2,32]{1,0:T(2,128)S(1)}, f32[2,32]{1,0:T(2,128)S(1)}, u32[]{:S(2)}, u32[]{:S(2)}) collective-permute-start(f32[2,32]{1,0:T(2,128)S(1)} %pad_maximum_fusion.19), channel_id=1, source_target_pairs={{0,2},{1,3},{2,0},{3,1},{4,6},{5,7},{6,4},{7,5},{8,10},{9,11},{10,... | collective-permute-start | bytes 776 | tf_op jit(solution)/shard_map/ppermute | solution.py:47
  29.4 4.3 %collective-permute-start.14 = (f32[2,32]{1,0:T(2,128)S(1)}, f32[2,32]{1,0:T(2,128)S(1)}, u32[]{:S(2)}, u32[]{:S(2)}) collective-permute-start(f32[2,32]{1,0:T(2,128)S(1)} %pad_maximum_fusion.19), channel_id=1, source_target_pairs={{0,3},{1,2},{2,1},{3,0},{4,7},{5,6},{6,5},{7,4},{8,11},{9,10},{10,... | collective-permute-start | bytes 776 | tf_op jit(solution)/shard_map/ppermute | solution.py:47
  29.5 9.4 %collective-permute-start.9 = (bf16[3,1,64,256]{3,2,1,0:T(8,128)(2,1)S(1)}, bf16[3,1,64,256]{3,2,1,0:T(8,128)(2,1)S(1)}, u32[]{:S(2)}, u32[]{:S(2)}) collective-permute-start(bf16[3,1,64,256]{3,2,1,0:T(8,128)(2,1)S(1)} %get-tuple-element.83), channel_id=1, source_target_pairs={{0,4},{4,8},{8,12},{1,5},{5,9},{9,13},{2,6},{6,10},{10,14},{3,7},{... | collective-permute-start | bytes 294920 | tf_op jit(solution)/shard_map/ppermute | solution.py:25
  32.4 6.5 %collective-permute-start.10 = (bf16[3,1,64,256]{3,2,1,0:T(8,128)(2,1)S(1)}, bf16[3,1,64,256]{3,2,1,0:T(8,128)(2,1)S(1)}, u32[]{:S(2)}, u32[]{:S(2)}) collective-permute-start(bf16[3,1,64,256]{3,2,1,0:T(8,128)(2,1)S(1)} %get-tuple-element.84), channel_id=1, source_target_pairs={{4,0},{8,4},{12,8},{5,1},{9,5},{13,9},{6,2},{10,6},{14,10},{7,3},{... | collective-permute-start | bytes 294920 | tf_op jit(solution)/shard_map/ppermute | solution.py:26
  33.8 10.3 %collective-permute-start.19 = (f32[2,32]{1,0:T(2,128)S(1)}, f32[2,32]{1,0:T(2,128)S(1)}, u32[]{:S(2)}, u32[]{:S(2)}) collective-permute-start(f32[2,32]{1,0:T(2,128)S(1)} %add_add_fusion.3), channel_id=1, source_target_pairs={{0,4},{1,5},{2,6},{3,7},{4,0},{5,1},{6,2},{7,3},{8,12},{9,13},{10,... | collective-permute-start | bytes 776 | tf_op jit(solution)/shard_map/ppermute | solution.py:47
  36.5 7.6 %collective-permute-start.18 = (f32[2,32]{1,0:T(2,128)S(1)}, f32[2,32]{1,0:T(2,128)S(1)}, u32[]{:S(2)}, u32[]{:S(2)}) collective-permute-start(f32[2,32]{1,0:T(2,128)S(1)} %add_add_fusion.3), channel_id=1, source_target_pairs={{0,8},{1,9},{2,10},{3,11},{4,12},{5,13},{6,14},{7,15},{8,0},{9,1},... | collective-permute-start | bytes 776 | tf_op jit(solution)/shard_map/ppermute | solution.py:47
  37.6 6.5 %collective-permute-start.17 = (f32[2,32]{1,0:T(2,128)S(1)}, f32[2,32]{1,0:T(2,128)S(1)}, u32[]{:S(2)}, u32[]{:S(2)}) collective-permute-start(f32[2,32]{1,0:T(2,128)S(1)} %add_add_fusion.3), channel_id=1, source_target_pairs={{0,12},{1,13},{2,14},{3,15},{4,8},{5,9},{6,10},{7,11},{8,4},{9,5},... | collective-permute-start | bytes 776 | tf_op jit(solution)/shard_map/ppermute | solution.py:47
  39.0 5.2 %collective-permute-start.11 = (bf16[3,6,1,256]{3,2,1,0:T(2,128)(2,1)S(1)}, bf16[3,6,1,256]{3,2,1,0:T(2,128)(2,1)S(1)}, u32[]{:S(2)}, u32[]{:S(2)}) collective-permute-start(bf16[3,6,1,256]{3,2,1,0:T(2,128)(2,1)S(1)} %get-tuple-element.79), channel_id=1, source_target_pairs={{0,2},{1,3},{4,6},{5,7},{8,10},{9,11},{12,14},{13,15},{16,18},{17,... | collective-permute-start | bytes 27656 | tf_op jit(solution)/shard_map/ppermute | solution.py:25
  42.8 5.7 %collective-permute-start.12 = (bf16[3,6,1,256]{3,2,1,0:T(2,128)(2,1)S(1)}, bf16[3,6,1,256]{3,2,1,0:T(2,128)(2,1)S(1)}, u32[]{:S(2)}, u32[]{:S(2)}) collective-permute-start(bf16[3,6,1,256]{3,2,1,0:T(2,128)(2,1)S(1)} %get-tuple-element.80), channel_id=1, source_target_pairs={{2,0},{3,1},{6,4},{7,5},{10,8},{11,9},{14,12},{15,13},{18,16},{19,... | collective-permute-start | bytes 27656 | tf_op jit(solution)/shard_map/ppermute | solution.py:26
  48.6 2.7 %collective-permute-start.13 = (bf16[2,6,66,256]{3,2,1,0:T(8,128)(2,1)S(1)}, bf16[2,6,66,256]{3,2,1,0:T(8,128)(2,1)S(1)}, u32[]{:S(2)}, u32[]{:S(2)}) collective-permute-start(bf16[2,6,66,256]{3,2,1,0:T(8,128)(2,1)S(1)} %pad_maximum_fusion.4), channel_id=1, source_target_pairs={{0,1},{2,3},{4,5},{6,7},{8,9},{10,11},{12,13},{14,15},{16,17},{18,... | collective-permute-start | bytes 1216520 | tf_op jit(solution)/shard_map/ppermute | solution.py:15
  53.6 2.0 %copy-start = (bf16[3,3,3,256,256]{4,3,2,1,0:T(8,128)(2,1)S(1)}, bf16[3,3,3,256,256]{4,3,2,1,0:T(8,128)(2,1)}, u32[]{:S(2)}) copy-start(bf16[3,3,3,256,256]{4,3,2,1,0:T(8,128)(2,1)} %param.16) | copy-start | bytes 10616836
  62.3 24.1 %copy-start.7 = (f32[256]{0:T(256)S(1)}, f32[256]{0:T(256)}, u32[]{:S(2)}) copy-start(f32[256]{0:T(256)} %param.18) | copy-start | bytes 3076
  62.3 24.1 %copy-start.8 = (f32[256]{0:T(256)S(1)}, f32[256]{0:T(256)}, u32[]{:S(2)}) copy-start(f32[256]{0:T(256)} %param.17) | copy-start | bytes 3076
  63.4 6.8 %collective-permute-start.27 = (f32[2,32]{1,0:T(2,128)S(1)}, f32[2,32]{1,0:T(2,128)S(1)}, u32[]{:S(2)}, u32[]{:S(2)}) collective-permute-start(f32[2,32]{1,0:T(2,128)S(1)} %pad_maximum_fusion.20), channel_id=1, source_target_pairs={{0,1},{1,0},{2,3},{3,2},{4,5},{5,4},{6,7},{7,6},{8,9},{9,8},{10,11... | collective-permute-start | bytes 776 | tf_op jit(solution)/shard_map/ppermute | solution.py:47
  63.8 6.3 %collective-permute-start.26 = (f32[2,32]{1,0:T(2,128)S(1)}, f32[2,32]{1,0:T(2,128)S(1)}, u32[]{:S(2)}, u32[]{:S(2)}) collective-permute-start(f32[2,32]{1,0:T(2,128)S(1)} %pad_maximum_fusion.20), channel_id=1, source_target_pairs={{0,2},{1,3},{2,0},{3,1},{4,6},{5,7},{6,4},{7,5},{8,10},{9,11},{10,... | collective-permute-start | bytes 776 | tf_op jit(solution)/shard_map/ppermute | solution.py:47
  63.8 6.3 %collective-permute-start.25 = (f32[2,32]{1,0:T(2,128)S(1)}, f32[2,32]{1,0:T(2,128)S(1)}, u32[]{:S(2)}, u32[]{:S(2)}) collective-permute-start(f32[2,32]{1,0:T(2,128)S(1)} %pad_maximum_fusion.20), channel_id=1, source_target_pairs={{0,3},{1,2},{2,1},{3,0},{4,7},{5,6},{6,5},{7,4},{8,11},{9,10},{10,... | collective-permute-start | bytes 776 | tf_op jit(solution)/shard_map/ppermute | solution.py:47
  65.3 10.0 %collective-permute-start.20 = (bf16[3,1,64,256]{3,2,1,0:T(8,128)(2,1)S(1)}, bf16[3,1,64,256]{3,2,1,0:T(8,128)(2,1)S(1)}, u32[]{:S(2)}, u32[]{:S(2)}) collective-permute-start(bf16[3,1,64,256]{3,2,1,0:T(8,128)(2,1)S(1)} %get-tuple-element.81), channel_id=1, source_target_pairs={{0,4},{4,8},{8,12},{1,5},{5,9},{9,13},{2,6},{6,10},{10,14},{3,7},{... | collective-permute-start | bytes 294920 | tf_op jit(solution)/shard_map/ppermute | solution.py:25
  68.8 7.0 %collective-permute-start.21 = (bf16[3,1,64,256]{3,2,1,0:T(8,128)(2,1)S(1)}, bf16[3,1,64,256]{3,2,1,0:T(8,128)(2,1)S(1)}, u32[]{:S(2)}, u32[]{:S(2)}) collective-permute-start(bf16[3,1,64,256]{3,2,1,0:T(8,128)(2,1)S(1)} %get-tuple-element.82), channel_id=1, source_target_pairs={{4,0},{8,4},{12,8},{5,1},{9,5},{13,9},{6,2},{10,6},{14,10},{7,3},{... | collective-permute-start | bytes 294920 | tf_op jit(solution)/shard_map/ppermute | solution.py:26
  70.2 8.9 %collective-permute-start.30 = (f32[2,32]{1,0:T(2,128)S(1)}, f32[2,32]{1,0:T(2,128)S(1)}, u32[]{:S(2)}, u32[]{:S(2)}) collective-permute-start(f32[2,32]{1,0:T(2,128)S(1)} %add_add_fusion.1), channel_id=1, source_target_pairs={{0,4},{1,5},{2,6},{3,7},{4,0},{5,1},{6,2},{7,3},{8,12},{9,13},{10,... | collective-permute-start | bytes 776 | tf_op jit(solution)/shard_map/ppermute | solution.py:47
  72.9 6.2 %collective-permute-start.29 = (f32[2,32]{1,0:T(2,128)S(1)}, f32[2,32]{1,0:T(2,128)S(1)}, u32[]{:S(2)}, u32[]{:S(2)}) collective-permute-start(f32[2,32]{1,0:T(2,128)S(1)} %add_add_fusion.1), channel_id=1, source_target_pairs={{0,8},{1,9},{2,10},{3,11},{4,12},{5,13},{6,14},{7,15},{8,0},{9,1},... | collective-permute-start | bytes 776 | tf_op jit(solution)/shard_map/ppermute | solution.py:47
  74.2 5.4 %collective-permute-start.28 = (f32[2,32]{1,0:T(2,128)S(1)}, f32[2,32]{1,0:T(2,128)S(1)}, u32[]{:S(2)}, u32[]{:S(2)}) collective-permute-start(f32[2,32]{1,0:T(2,128)S(1)} %add_add_fusion.1), channel_id=1, source_target_pairs={{0,12},{1,13},{2,14},{3,15},{4,8},{5,9},{6,10},{7,11},{8,4},{9,5},... | collective-permute-start | bytes 776 | tf_op jit(solution)/shard_map/ppermute | solution.py:47
  75.8 3.8 %collective-permute-start.22 = (bf16[3,6,1,256]{3,2,1,0:T(2,128)(2,1)S(1)}, bf16[3,6,1,256]{3,2,1,0:T(2,128)(2,1)S(1)}, u32[]{:S(2)}, u32[]{:S(2)}) collective-permute-start(bf16[3,6,1,256]{3,2,1,0:T(2,128)(2,1)S(1)} %get-tuple-element.77), channel_id=1, source_target_pairs={{0,2},{1,3},{4,6},{5,7},{8,10},{9,11},{12,14},{13,15},{16,18},{17,... | collective-permute-start | bytes 27656 | tf_op jit(solution)/shard_map/ppermute | solution.py:25
  77.8 5.7 %collective-permute-start.23 = (bf16[3,6,1,256]{3,2,1,0:T(2,128)(2,1)S(1)}, bf16[3,6,1,256]{3,2,1,0:T(2,128)(2,1)S(1)}, u32[]{:S(2)}, u32[]{:S(2)}) collective-permute-start(bf16[3,6,1,256]{3,2,1,0:T(2,128)(2,1)S(1)} %get-tuple-element.78), channel_id=1, source_target_pairs={{2,0},{3,1},{6,4},{7,5},{10,8},{11,9},{14,12},{15,13},{18,16},{19,... | collective-permute-start | bytes 27656 | tf_op jit(solution)/shard_map/ppermute | solution.py:26
  83.6 2.7 %collective-permute-start.24 = (bf16[2,6,66,256]{3,2,1,0:T(8,128)(2,1)S(1)}, bf16[2,6,66,256]{3,2,1,0:T(8,128)(2,1)S(1)}, u32[]{:S(2)}, u32[]{:S(2)}) collective-permute-start(bf16[2,6,66,256]{3,2,1,0:T(8,128)(2,1)S(1)} %pad_maximum_fusion), channel_id=1, source_target_pairs={{0,1},{2,3},{4,5},{6,7},{8,9},{10,11},{12,13},{14,15},{16,17},{18,... | collective-permute-start | bytes 1216520 | tf_op jit(solution)/shard_map/ppermute | solution.py:15
  88.6 2.0 %copy-start.1 = (bf16[3,3,3,256,256]{4,3,2,1,0:T(8,128)(2,1)S(1)}, bf16[3,3,3,256,256]{4,3,2,1,0:T(8,128)(2,1)}, u32[]{:S(2)}) copy-start(bf16[3,3,3,256,256]{4,3,2,1,0:T(8,128)(2,1)} %param.19) | copy-start | bytes 10616836

commit v3 on v2

--- a/solution.py
+++ b/solution.py
@@ -166,12 +166,83 @@
     return jnp.concatenate([earlier, x], axis=0)
 
 
+def swap(x, axis, distance):
+    size = lax.axis_size(axis)
+    return lax.ppermute(x, axis, [(i, i ^ distance) for i in range(size)])
+
+
+def fast_mesh():
+    return lax.axis_size("ta") == 2 and lax.axis_size("wa") == 2 and lax.axis_size("ha") == 4
+
+
+def local_sums(values):
+    grouped = values.reshape(-1, GROUPS, values.shape[-1] // GROUPS)
+    return jnp.stack([jnp.sum(grouped, axis=(0, 2)), jnp.sum(grouped * grouped, axis=(0, 2))])
+
+
+def finish_stats(sums, values):
+    channels = values.shape[-1]
+    group_width = channels // GROUPS
+    entries = (
+        values.size // GROUPS
+        * lax.axis_size("ha")
+        * lax.axis_size("wa")
+        * lax.axis_size("ta")
+    )
+    average = sums[0] / entries
+    spread = sums[1] / entries - average * average
+    scaling = lax.rsqrt(spread + EPSILON)
+    return jnp.repeat(average, group_width), jnp.repeat(scaling, group_width)
+
+
+def ha_round(sums, upper, lower):
+    h = lax.axis_index("ha")
+    to_first = jnp.where(h % 2 == 1, upper, lower)
+    to_third = jnp.where(h == 2, upper, lower)
+    s1, got_first = swap((sums, to_first), "ha", 1)
+    s2 = swap(sums, "ha", 2)
+    s3, got_third = swap((sums, to_third), "ha", 3)
+    sums = (sums + s1) + (s2 + s3)
+    above = jnp.where(h % 2 == 1, got_first, got_third)
+    below = jnp.where(h % 2 == 0, got_first, got_third)
+    return sums, above, below
+
+
+def fast_conv_input(values):
+    sums = local_sums(values.astype(jnp.float32))
+    s_t, earlier = swap((sums, values[-2:]), "ta", 1)
+    sums = sums + s_t
+    opening = jnp.concatenate([values[:1], values[:1]], axis=0)
+    earlier = jnp.where(lax.axis_index("ta") == 0, opening, earlier)
+    x = jnp.concatenate([earlier, values], axis=0)
+    w = lax.axis_index("wa")
+    s_w, beside = swap((sums, jnp.where(w == 0, x[:, :, -1:], x[:, :, :1])), "wa", 1)
+    sums = sums + s_w
+    x = jnp.concatenate([beside, x, beside], axis=2)
+    sums, above, below = ha_round(sums, x[:, :1], x[:, -1:])
+    x = jnp.concatenate([above, x, below], axis=1)
+    return finish_stats(sums, values), x
+
+
+def fast_latent_input(values):
+    sums = local_sums(values.astype(jnp.float32))
+    sums = sums + swap(sums, "ta", 1)
+    s_w, beside = swap((sums, values[:, :, :1]), "wa", 1)
+    sums = sums + s_w
+    x = jnp.concatenate([values, beside], axis=2)
+    sums, _, below = ha_round(sums, x[:, :1], x[:, :1])
+    x = jnp.concatenate([x, below], axis=1)
+    return finish_stats(sums, values), x
+
+
 def norm_conv(values, gain, shift, kernel):
     frames, height, across, _ = values.shape
-    values_f = values.astype(jnp.float32)
-    stats = group_stats(values_f)
-    extended = conv_halo(values).astype(jnp.float32)
-    act = activate(extended, stats, gain, shift)
+    if fast_mesh():
+        stats, extended = fast_conv_input(values)
+    else:
+        stats = group_stats(values.astype(jnp.float32))
+        extended = conv_halo(values)
+    act = activate(extended.astype(jnp.float32), stats, gain, shift)
     act = jnp.where(inside_mask(height + 2, across + 2, 1), act, 0.0).astype(jnp.bfloat16)
     return valid_conv(act, kernel, frames, height, across)
 
@@ -189,9 +260,12 @@
     conv_b,
 ):
     frames, height, across, channels = latents.shape
-    stats = group_stats(latents.astype(jnp.float32))
-    extended = latent_halo(latents).astype(jnp.float32)
-    activated = activate(extended, stats, norm1_gain, norm1_shift)
+    if fast_mesh():
+        stats, extended = fast_latent_input(latents)
+    else:
+        stats = group_stats(latents.astype(jnp.float32))
+        extended = latent_halo(latents)
+    activated = activate(extended.astype(jnp.float32), stats, norm1_gain, norm1_shift)
     activated = jnp.where(inside_mask(height + 1, across + 1, 0), activated, 0.0)
     lifted = upsample(activated.astype(jnp.bfloat16), up_weight).astype(jnp.bfloat16)
     hidden = norm_conv(lifted, norm2_gain, norm2_shift, conv_a).astype(jnp.bfloat16)

time: 99.3 us -> 107 us (1.078)
  waiting for transfers between devices: 15.4 us -> 40.5 us
  starting transfers between devices: 46.9 us -> 29 us
    ppermute x31 -> x26, waiting for transfers between devices: 15.4 us -> 40.5 us  [swap(): return lax.ppermute(x, axis, [(i, i ^ distance) for i in range(size)])]
    ppermute x31 -> x26, starting transfers between devices: 46.9 us -> 29 us  [swap(): return lax.ppermute(x, axis, [(i, i ^ distance) for i in range(size)])]
  transfers between devices with their start and end apart: 31 -> 26, of which waited for: 10 -> 19; matrix products, arithmetic and copies ran while one was open for 5% -> 5% of each run, Pallas kernels for 0% -> 0%
where the time goes in v3:
time: 107 us
  waiting for transfers between devices  40.5 us (38%)
  starting transfers between devices  29 us (27%)
  matrix products  16.3 us (15%)
  local copies, waits for them, and re-layouts  10.9 us (10%)
  other arithmetic  9.2 us (9%)
    ppermute x26, waiting for transfers between devices, swap(): return lax.ppermute(x, axis, [(i, i ^ distance) for i in range(size)])  40.5 us
    ppermute x26, starting transfers between devices, swap(): return lax.ppermute(x, axis, [(i, i ^ distance) for i in range(size)])  29 us
    dot_general x54, matrix products, valid_conv(): jnp.dot(window.reshape(-1, window.shape[-1]), kernel[step_t, step_y, step...  14.3 us
    slice x4, local copies, waits for them, and re-layouts, valid_conv(): padded[step_t:step_t + frames, step_y:step_y + height, step_x:step_x + ac...  4.98 us
    convert_element_type x2, other arithmetic, norm_conv(): jnp.where(inside_mask(height + 2, across + 2, 1), act, 0.0)  3.99 us
    reduce_sum x5, other arithmetic, local_sums(): jnp.sum(grouped, axis=(0, 2))  2.21 us
  transfers between devices with their start and end apart: 26, of which 19 were waited for; matrix products, arithmetic and copies ran while one was open for 5% of the time, Pallas kernels for 0%

profile of v3, /device:TPU:0, one launch (start us, length us, event | category | flops | bytes accessed | tf_op | source)
XLA Modules:
  0.0 106.8 jit_solution(16371858359486462409)
XLA Ops:
  0.0 1.0 convert_reduce_fusion.2
  1.4 0.5 collective-permute-start.3
  2.0 0.8 slice.462
  2.8 2.6 %collective-permute-start = (bf16[3,2,1,512]{3,2,1,0:T(2,128)(2,1)S(1)}, bf16[3,2,1,512]{3,2,1,0:T(2,128)(2,1)S(1)}, u32[]{:S(2)}, u32[]{:S(2)}) collective-permute-start(bf16[3,2,1,512]{3,2,1,0:T(2,128)(2,1)S(1)} %slice.462), channel_id=1, source_target_pairs={{0,2},{2,0},{1,3},{3,1},{4,6},{6,4},{5,7},{7,5},{8,10},{10,8},{9,1... | collective-permute-start | bytes 18440 | tf_op jit(solution)/shard_map/ppermute | solution.py:171
  5.3 0.9 constant_dynamic-update-slice_fusion.1
  6.4 1.6 %slice_bitcast_fusion.7 = (bf16[512,256]{1,0:T(8,128)(2,1)S(1)}, bf16[512,256]{1,0:T(8,128)(2,1)S(1)}, bf16[512,256]{1,0:T(8,128)(2,1)S(1)}, bf16[512,256]{1,0:T...) fusion(bf16[3,3,512,256]{3,2,1,0:T(8,128)(2,1)} %param.13), kind=kLoop, calls=%fused_computation.97 | loop fusion | bytes 4194304 | tf_op jit(solution)/shard_map/squeeze | solution.py:129
  8.2 3.5 %collective-permute-done.4 = f32[2,32]{1,0:T(2,128)S(1)} collective-permute-done((f32[2,32]{1,0:T(2,128)S(1)}, f32[2,32]{1,0:T(2,128)S(1)}, u32[]{:S(2)}, u32[]{:S(2)}) %collective-permute-start.4) | collective-permute-done | bytes 288 | tf_op jit(solution)/shard_map/ppermute | solution.py:171
  11.8 3.7 %collective-permute-start.7 = (f32[2,32]{1,0:T(2,128)S(1)}, f32[2,32]{1,0:T(2,128)S(1)}, u32[]{:S(2)}, u32[]{:S(2)}) collective-permute-start(f32[2,32]{1,0:T(2,128)S(1)} %fusion.210), channel_id=1, source_target_pairs={{0,12},{4,8},{8,4},{12,0},{1,13},{5,9},{9,5},{13,1},{2,14},{6,10},... | collective-permute-start | bytes 776 | tf_op jit(solution)/shard_map/ppermute | solution.py:171
  15.5 0.8 collective-permute-start.5
  16.3 1.0 collective-permute-done.7
  17.2 2.7 %collective-permute-done.6 = f32[2,32]{1,0:T(2,128)S(1)} collective-permute-done((f32[2,32]{1,0:T(2,128)S(1)}, f32[2,32]{1,0:T(2,128)S(1)}, u32[]{:S(2)}, u32[]{:S(2)}) %collective-permute-start.6) | collective-permute-done | bytes 288 | tf_op jit(solution)/shard_map/ppermute | solution.py:171
  20.0 1.5 %collective-permute-start.2 = (bf16[3,1,33,512]{3,2,1,0:T(8,128)(2,1)S(1)}, bf16[3,1,33,512]{3,2,1,0:T(8,128)(2,1)S(1)}, u32[]{:S(2)}, u32[]{:S(2)}) collective-permute-start(bf16[3,1,33,512]{3,2,1,0:T(8,128)(2,1)S(1)} %slice.615), channel_id=1, source_target_pairs={{0,12},{4,8},{8,4},{12,0},{1,13},{5,9},{9,5},{13,1},{2,14},{6,10},... | collective-permute-start | bytes 304136 | tf_op jit(solution)/shard_map/ppermute | solution.py:171
  21.6 1.1 %collective-permute-start.1 = (bf16[3,1,33,512]{3,2,1,0:T(8,128)(2,1)S(1)}, bf16[3,1,33,512]{3,2,1,0:T(8,128)(2,1)S(1)}, u32[]{:S(2)}, u32[]{:S(2)}) collective-permute-start(bf16[3,1,33,512]{3,2,1,0:T(8,128)(2,1)S(1)} %slice.615), channel_id=1, source_target_pairs={{0,4},{4,0},{8,12},{12,8},{1,5},{5,1},{9,13},{13,9},{2,6},{6,2},{1... | collective-permute-start | bytes 304136 | tf_op jit(solution)/shard_map/ppermute | solution.py:171
  23.0 3.9 %collective-permute-done.2 = bf16[3,1,33,512]{3,2,1,0:T(8,128)(2,1)S(1)} collective-permute-done((bf16[3,1,33,512]{3,2,1,0:T(8,128)(2,1)S(1)}, bf16[3,1,33,512]{3,2,1,0:T(8,128)(2,1)S(1)}, u32[]{:S(2)}, u32[]{:S(2)}) %collective-permute-start.2) | collective-permute-done | bytes 101408 | tf_op jit(solution)/shard_map/ppermute | solution.py:171
  26.9 0.9 collective-permute-done.1
  29.2 1.2 %convolution_add_fusion.52 = bf16[192,256]{1,0:T(8,128)(2,1)S(1)} fusion(bf16[192,512]{1,0:T(8,128)(2,1)S(1)} %bitcast.410, bf16[3,3,512,256]{3,2,1,0:T(8,128)(2,1)} %param.13, f32[192,512]{1,0:T(8,128)S(1)} %fusion.15, f32[192,512]{1,0:T(8,128)S(1)} %fusion.11, f32[192,1024]{1,0:T(8,128)S(1)} %fusion.1), kind=kOutput, calls=%fused_computation.55 | convolution fusion | flops 50528256 | bytes 1146880 | tf_op jit(solution)/shard_map/dot_general | solution.py:123
  31.4 0.8 convert_reduce_fusion.1
  32.7 1.1 %collective-permute-done.12 = f32[2,32]{1,0:T(2,128)S(1)} collective-permute-done((f32[2,32]{1,0:T(2,128)S(1)}, f32[2,32]{1,0:T(2,128)S(1)}, u32[]{:S(2)}, u32[]{:S(2)}) %collective-permute-start.12) | collective-permute-done | bytes 288 | tf_op jit(solution)/shard_map/ppermute | solution.py:171
  33.9 0.6 collective-permute-start.13
  34.8 2.7 %collective-permute-done.13 = f32[2,32]{1,0:T(2,128)S(1)} collective-permute-done((f32[2,32]{1,0:T(2,128)S(1)}, f32[2,32]{1,0:T(2,128)S(1)}, u32[]{:S(2)}, u32[]{:S(2)}) %collective-permute-start.13) | collective-permute-done | bytes 288 | tf_op jit(solution)/shard_map/ppermute | solution.py:171
  37.5 2.0 %collective-permute-start.16 = (f32[2,32]{1,0:T(2,128)S(1)}, f32[2,32]{1,0:T(2,128)S(1)}, u32[]{:S(2)}, u32[]{:S(2)}) collective-permute-start(f32[2,32]{1,0:T(2,128)S(1)} %fusion.209), channel_id=1, source_target_pairs={{0,12},{4,8},{8,4},{12,0},{1,13},{5,9},{9,5},{13,1},{2,14},{6,10},... | collective-permute-start | bytes 776 | tf_op jit(solution)/shard_map/ppermute | solution.py:171
  39.5 2.5 %collective-permute-start.14 = (f32[2,32]{1,0:T(2,128)S(1)}, f32[2,32]{1,0:T(2,128)S(1)}, u32[]{:S(2)}, u32[]{:S(2)}) collective-permute-start(f32[2,32]{1,0:T(2,128)S(1)} %fusion.209), channel_id=1, source_target_pairs={{0,4},{4,0},{8,12},{12,8},{1,5},{5,1},{9,13},{13,9},{2,6},{6,2},{1... | collective-permute-start | bytes 776 | tf_op jit(solution)/shard_map/ppermute | solution.py:171
  42.1 0.8 collective-permute-done.16
  42.9 1.0 collective-permute-done.15
  44.0 0.6 collective-permute-start.9
  44.8 3.1 %collective-permute-done.9 = bf16[5,4,1,256]{3,2,1,0:T(2,128)(2,1)S(1)} collective-permute-done((bf16[5,4,1,256]{3,2,1,0:T(2,128)(2,1)S(1)}, bf16[5,4,1,256]{3,2,1,0:T(2,128)(2,1)S(1)}, u32[]{:S(2)}, u32[]{:S(2)}) %collective-permute-start.9) | collective-permute-done | bytes 10272 | tf_op jit(solution)/shard_map/ppermute | solution.py:171
  48.1 1.7 %collective-permute-start.10 = (bf16[5,1,66,256]{3,2,1,0:T(8,128)(2,1)S(1)}, bf16[5,1,66,256]{3,2,1,0:T(8,128)(2,1)S(1)}, u32[]{:S(2)}, u32[]{:S(2)}) collective-permute-start(bf16[5,1,66,256]{3,2,1,0:T(8,128)(2,1)S(1)} %broadcast_select_fusion.7), channel_id=1, source_target_pairs={{0,4},{4,0},{8,12},{12,8},{1,5},{5,1},{9,13},{13,9},{2,6},{6,2},{1... | collective-permute-start | bytes 506888 | tf_op jit(solution)/shard_map/ppermute | solution.py:171
  49.7 1.9 %collective-permute-start.11 = (bf16[5,1,66,256]{3,2,1,0:T(8,128)(2,1)S(1)}, bf16[5,1,66,256]{3,2,1,0:T(8,128)(2,1)S(1)}, u32[]{:S(2)}, u32[]{:S(2)}) collective-permute-start(bf16[5,1,66,256]{3,2,1,0:T(8,128)(2,1)S(1)} %get-tuple-element.15), channel_id=1, source_target_pairs={{0,12},{4,8},{8,4},{12,0},{1,13},{5,9},{9,5},{13,1},{2,14},{6,10},... | collective-permute-start | bytes 506888 | tf_op jit(solution)/shard_map/ppermute | solution.py:171
  51.8 2.5 %collective-permute-done.10 = bf16[5,1,66,256]{3,2,1,0:T(8,128)(2,1)S(1)} collective-permute-done((bf16[5,1,66,256]{3,2,1,0:T(8,128)(2,1)S(1)}, bf16[5,1,66,256]{3,2,1,0:T(8,128)(2,1)S(1)}, u32[]{:S(2)}, u32[]{:S(2)}) %collective-permute-start.10) | collective-permute-done | bytes 168992 | tf_op jit(solution)/shard_map/ppermute | solution.py:171
  54.3 2.8 %collective-permute-done.11 = bf16[5,1,66,256]{3,2,1,0:T(8,128)(2,1)S(1)} collective-permute-done((bf16[5,1,66,256]{3,2,1,0:T(8,128)(2,1)S(1)}, bf16[5,1,66,256]{3,2,1,0:T(8,128)(2,1)S(1)}, u32[]{:S(2)}, u32[]{:S(2)}) %collective-permute-start.11) | collective-permute-done | bytes 168992 | tf_op jit(solution)/shard_map/ppermute | solution.py:171
  57.2 2.1 %select_convert_fusion.1 = bf16[5,6,66,256]{3,2,1,0:T(8,128)(2,1)S(1)} fusion(bf16[5,1,66,256]{3,2,1,0:T(8,128)(2,1)S(1)} %get-tuple-element.86, bf16[5,4,1,256]{3,2,1,0:T(2,128)(2,1)S(1)} %collective-permute-done.9, bf16[3,4,64,256]{3,2,1,0:T(8,128)(2,1)S(1)} %bitcast.350, bf16[2,4,64,256]{3,2,1,0:T(8,128)(2,1)S(1)} %maximum_select_fusion, ...), kind=kLoop, calls=%fused_computation.1 | loop fusion | flops 11151360 | bytes 2021772 | tf_op jit(solution)/shard_map/convert_element_type | solution.py:246
  59.8 1.9 %fusion.146 = (bf16[3,4,64,256]{3,2,1,0:T(8,128)(2,1)S(1)}, bf16[3,4,64,256]{3,2,1,0:T(8,128)(2,1)S(1)}, bf16[3,4,64,256]{3,2,1,0:T(8,128)(2,1)S(1)}, bf16[3,4,6...) fusion(bf16[5,6,66,256]{3,2,1,0:T(8,128)(2,1)S(1)} %select_conv, ...), kind=kLoop, calls=%fused_computation.267 | loop fusion | bytes 14942208 | tf_op jit(solution)/shard_map/slice | solution.py:150
  69.7 1.1 %collective-permute-done.21 = f32[2,32]{1,0:T(2,128)S(1)} collective-permute-done((f32[2,32]{1,0:T(2,128)S(1)}, f32[2,32]{1,0:T(2,128)S(1)}, u32[]{:S(2)}, u32[]{:S(2)}) %collective-permute-start.21) | collective-permute-done | bytes 288 | tf_op jit(solution)/shard_map/ppermute | solution.py:171
  70.8 0.6 collective-permute-start.22
  71.5 2.9 %collective-permute-done.22 = f32[2,32]{1,0:T(2,128)S(1)} collective-permute-done((f32[2,32]{1,0:T(2,128)S(1)}, f32[2,32]{1,0:T(2,128)S(1)}, u32[]{:S(2)}, u32[]{:S(2)}) %collective-permute-start.22) | collective-permute-done | bytes 288 | tf_op jit(solution)/shard_map/ppermute | solution.py:171
  74.4 2.0 %collective-permute-start.25 = (f32[2,32]{1,0:T(2,128)S(1)}, f32[2,32]{1,0:T(2,128)S(1)}, u32[]{:S(2)}, u32[]{:S(2)}) collective-permute-start(f32[2,32]{1,0:T(2,128)S(1)} %fusion.208), channel_id=1, source_target_pairs={{0,12},{4,8},{8,4},{12,0},{1,13},{5,9},{9,5},{13,1},{2,14},{6,10},... | collective-permute-start | bytes 776 | tf_op jit(solution)/shard_map/ppermute | solution.py:171
  76.4 2.5 %collective-permute-start.23 = (f32[2,32]{1,0:T(2,128)S(1)}, f32[2,32]{1,0:T(2,128)S(1)}, u32[]{:S(2)}, u32[]{:S(2)}) collective-permute-start(f32[2,32]{1,0:T(2,128)S(1)} %fusion.208), channel_id=1, source_target_pairs={{0,4},{4,0},{8,12},{12,8},{1,5},{5,1},{9,13},{13,9},{2,6},{6,2},{1... | collective-permute-start | bytes 776 | tf_op jit(solution)/shard_map/ppermute | solution.py:171
  78.9 1.0 collective-permute-done.25
  79.9 1.0 collective-permute-done.24
  81.0 0.6 collective-permute-start.18
  81.8 3.1 %collective-permute-done.18 = bf16[5,4,1,256]{3,2,1,0:T(2,128)(2,1)S(1)} collective-permute-done((bf16[5,4,1,256]{3,2,1,0:T(2,128)(2,1)S(1)}, bf16[5,4,1,256]{3,2,1,0:T(2,128)(2,1)S(1)}, u32[]{:S(2)}, u32[]{:S(2)}) %collective-permute-start.18) | collective-permute-done | bytes 10272 | tf_op jit(solution)/shard_map/ppermute | solution.py:171
  85.0 1.6 %collective-permute-start.19 = (bf16[5,1,66,256]{3,2,1,0:T(8,128)(2,1)S(1)}, bf16[5,1,66,256]{3,2,1,0:T(8,128)(2,1)S(1)}, u32[]{:S(2)}, u32[]{:S(2)}) collective-permute-start(bf16[5,1,66,256]{3,2,1,0:T(8,128)(2,1)S(1)} %broadcast_select_fusion.5), channel_id=1, source_target_pairs={{0,4},{4,0},{8,12},{12,8},{1,5},{5,1},{9,13},{13,9},{2,6},{6,2},{1... | collective-permute-start | bytes 506888 | tf_op jit(solution)/shard_map/ppermute | solution.py:171
  86.7 1.9 %collective-permute-start.20 = (bf16[5,1,66,256]{3,2,1,0:T(8,128)(2,1)S(1)}, bf16[5,1,66,256]{3,2,1,0:T(8,128)(2,1)S(1)}, u32[]{:S(2)}, u32[]{:S(2)}) collective-permute-start(bf16[5,1,66,256]{3,2,1,0:T(8,128)(2,1)S(1)} %get-tuple-element.11), channel_id=1, source_target_pairs={{0,12},{4,8},{8,4},{12,0},{1,13},{5,9},{9,5},{13,1},{2,14},{6,10},... | collective-permute-start | bytes 506888 | tf_op jit(solution)/shard_map/ppermute | solution.py:171
  88.8 2.5 %collective-permute-done.19 = bf16[5,1,66,256]{3,2,1,0:T(8,128)(2,1)S(1)} collective-permute-done((bf16[5,1,66,256]{3,2,1,0:T(8,128)(2,1)S(1)}, bf16[5,1,66,256]{3,2,1,0:T(8,128)(2,1)S(1)}, u32[]{:S(2)}, u32[]{:S(2)}) %collective-permute-start.19) | collective-permute-done | bytes 168992 | tf_op jit(solution)/shard_map/ppermute | solution.py:171
  91.3 2.8 %collective-permute-done.20 = bf16[5,1,66,256]{3,2,1,0:T(8,128)(2,1)S(1)} collective-permute-done((bf16[5,1,66,256]{3,2,1,0:T(8,128)(2,1)S(1)}, bf16[5,1,66,256]{3,2,1,0:T(8,128)(2,1)S(1)}, u32[]{:S(2)}, u32[]{:S(2)}) %collective-permute-start.20) | collective-permute-done | bytes 168992 | tf_op jit(solution)/shard_map/ppermute | solution.py:171
  94.1 1.9 %select_convert_fusion = bf16[5,6,66,256]{3,2,1,0:T(8,128)(2,1)S(1)} fusion(bf16[5,1,66,256]{3,2,1,0:T(8,128)(2,1)S(1)} %get-tuple-element.84, bf16[5,4,1,256]{3,2,1,0:T(2,128)(2,1)S(1)} %collective-permute-done.18, bf16[3,4,64,256]{3,2,1,0:T(8,128)(2,1)S(1)} %bitcast.354, bf16[2,4,64,256]{3,2,1,0:T(8,128)(2,1)S(1)} %maximum_select_fusion.1, ...), kind=kLoop, calls=%fused_computation | loop fusion | flops 11151360 | bytes 2021772 | tf_op jit(solution)/shard_map/convert_element_type | solution.py:246
  96.6 2.1 %fusion.144 = (bf16[3,4,64,256]{3,2,1,0:T(8,128)(2,1)S(1)}, bf16[3,4,64,256]{3,2,1,0:T(8,128)(2,1)S(1)}, bf16[3,4,64,256]{3,2,1,0:T(8,128)(2,1)S(1)}, bf16[3,4,6...) fusion(bf16[5,6,66,256]{3,2,1,0:T(8,128)(2,1)S(1)} %select_conv, ...), kind=kLoop, calls=%fused_computation.265 | loop fusion | bytes 14942208 | tf_op jit(solution)/shard_map/slice | solution.py:150
  106.0 0.8 add_convert_fusion
  (167 shorter events, 21.6 us)
Async XLA Ops:
  0.0 27.8 %copy-start.2 = (f32[512]{0:T(512)S(1)}, f32[512]{0:T(512)}, u32[]{:S(2)}) copy-start(f32[512]{0:T(512)} %param.12) | copy-start | bytes 6148
  0.0 27.8 %copy-start.3 = (f32[512]{0:T(512)S(1)}, f32[512]{0:T(512)}, u32[]{:S(2)}) copy-start(f32[512]{0:T(512)} %param.11) | copy-start | bytes 6148
  1.4 6.7 %collective-permute-start.3 = (f32[2,32]{1,0:T(2,128)S(1)}, f32[2,32]{1,0:T(2,128)S(1)}, u32[]{:S(2)}, u32[]{:S(2)}) collective-permute-start(f32[2,32]{1,0:T(2,128)S(1)} %pad_maximum_fusion.12), channel_id=1, source_target_pairs={{0,1},{1,0},{2,3},{3,2},{4,5},{5,4},{6,7},{7,6},{8,9},{9,8},{10,11... | collective-permute-start | bytes 776 | tf_op jit(solution)/shard_map/ppermute | solution.py:171
  2.8 17.2 %collective-permute-start = (bf16[3,2,1,512]{3,2,1,0:T(2,128)(2,1)S(1)}, bf16[3,2,1,512]{3,2,1,0:T(2,128)(2,1)S(1)}, u32[]{:S(2)}, u32[]{:S(2)}) collective-permute-start(bf16[3,2,1,512]{3,2,1,0:T(2,128)(2,1)S(1)} %slice.462), channel_id=1, source_target_pairs={{0,2},{2,0},{1,3},{3,1},{4,6},{6,4},{5,7},{7,5},{8,10},{10,8},{9,1... | collective-permute-start | bytes 18440 | tf_op jit(solution)/shard_map/ppermute | solution.py:171
  8.2 3.6 %collective-permute-start.4 = (f32[2,32]{1,0:T(2,128)S(1)}, f32[2,32]{1,0:T(2,128)S(1)}, u32[]{:S(2)}, u32[]{:S(2)}) collective-permute-start(f32[2,32]{1,0:T(2,128)S(1)} %fusion.143), channel_id=1, source_target_pairs={{0,2},{2,0},{1,3},{3,1},{4,6},{6,4},{5,7},{7,5},{8,10},{10,8},{9,1... | collective-permute-start | bytes 776 | tf_op jit(solution)/shard_map/ppermute | solution.py:171
  11.8 5.4 %collective-permute-start.7 = (f32[2,32]{1,0:T(2,128)S(1)}, f32[2,32]{1,0:T(2,128)S(1)}, u32[]{:S(2)}, u32[]{:S(2)}) collective-permute-start(f32[2,32]{1,0:T(2,128)S(1)} %fusion.210), channel_id=1, source_target_pairs={{0,12},{4,8},{8,4},{12,0},{1,13},{5,9},{9,5},{13,1},{2,14},{6,10},... | collective-permute-start | bytes 776 | tf_op jit(solution)/shard_map/ppermute | solution.py:171
  15.5 4.5 %collective-permute-start.6 = (f32[2,32]{1,0:T(2,128)S(1)}, f32[2,32]{1,0:T(2,128)S(1)}, u32[]{:S(2)}, u32[]{:S(2)}) collective-permute-start(f32[2,32]{1,0:T(2,128)S(1)} %fusion.210), channel_id=1, source_target_pairs={{0,8},{4,12},{8,0},{12,4},{1,9},{5,13},{9,1},{13,5},{2,10},{6,14},... | collective-permute-start | bytes 776 | tf_op jit(solution)/shard_map/ppermute | solution.py:171
  15.5 4.5 %collective-permute-start.5 = (f32[2,32]{1,0:T(2,128)S(1)}, f32[2,32]{1,0:T(2,128)S(1)}, u32[]{:S(2)}, u32[]{:S(2)}) collective-permute-start(f32[2,32]{1,0:T(2,128)S(1)} %fusion.210), channel_id=1, source_target_pairs={{0,4},{4,0},{8,12},{12,8},{1,5},{5,1},{9,13},{13,9},{2,6},{6,2},{1... | collective-permute-start | bytes 776 | tf_op jit(solution)/shard_map/ppermute | solution.py:171
  20.0 6.9 %collective-permute-start.2 = (bf16[3,1,33,512]{3,2,1,0:T(8,128)(2,1)S(1)}, bf16[3,1,33,512]{3,2,1,0:T(8,128)(2,1)S(1)}, u32[]{:S(2)}, u32[]{:S(2)}) collective-permute-start(bf16[3,1,33,512]{3,2,1,0:T(8,128)(2,1)S(1)} %slice.615), channel_id=1, source_target_pairs={{0,12},{4,8},{8,4},{12,0},{1,13},{5,9},{9,5},{13,1},{2,14},{6,10},... | collective-permute-start | bytes 304136 | tf_op jit(solution)/shard_map/ppermute | solution.py:171
  21.6 6.2 %collective-permute-start.1 = (bf16[3,1,33,512]{3,2,1,0:T(8,128)(2,1)S(1)}, bf16[3,1,33,512]{3,2,1,0:T(8,128)(2,1)S(1)}, u32[]{:S(2)}, u32[]{:S(2)}) collective-permute-start(bf16[3,1,33,512]{3,2,1,0:T(8,128)(2,1)S(1)} %slice.615), channel_id=1, source_target_pairs={{0,4},{4,0},{8,12},{12,8},{1,5},{5,1},{9,13},{13,9},{2,6},{6,2},{1... | collective-permute-start | bytes 304136 | tf_op jit(solution)/shard_map/ppermute | solution.py:171
  31.4 25.8 %copy-start.4 = (f32[256]{0:T(256)S(1)}, f32[256]{0:T(256)}, u32[]{:S(2)}) copy-start(f32[256]{0:T(256)} %param.15) | copy-start | bytes 3076
  31.4 25.8 %copy-start.5 = (f32[256]{0:T(256)S(1)}, f32[256]{0:T(256)}, u32[]{:S(2)}) copy-start(f32[256]{0:T(256)} %param.14) | copy-start | bytes 3076
  32.6 1.2 %collective-permute-start.12 = (f32[2,32]{1,0:T(2,128)S(1)}, f32[2,32]{1,0:T(2,128)S(1)}, u32[]{:S(2)}, u32[]{:S(2)}) collective-permute-start(f32[2,32]{1,0:T(2,128)S(1)} %pad_maximum_fusion.13), channel_id=1, source_target_pairs={{0,1},{1,0},{2,3},{3,2},{4,5},{5,4},{6,7},{7,6},{8,9},{9,8},{10,11... | collective-permute-start | bytes 776 | tf_op jit(solution)/shard_map/ppermute | solution.py:171
  33.9 3.6 %collective-permute-start.13 = (f32[2,32]{1,0:T(2,128)S(1)}, f32[2,32]{1,0:T(2,128)S(1)}, u32[]{:S(2)}, u32[]{:S(2)}) collective-permute-start(f32[2,32]{1,0:T(2,128)S(1)} %fusion.142), channel_id=1, source_target_pairs={{0,2},{2,0},{1,3},{3,1},{4,6},{6,4},{5,7},{7,5},{8,10},{10,8},{9,1... | collective-permute-start | bytes 776 | tf_op jit(solution)/shard_map/ppermute | solution.py:171
  34.7 9.3 %collective-permute-start.8 = (bf16[2,4,64,256]{3,2,1,0:T(8,128)(2,1)S(1)}, bf16[2,4,64,256]{3,2,1,0:T(8,128)(2,1)S(1)}, u32[]{:S(2)}, u32[]{:S(2)}) collective-permute-start(bf16[2,4,64,256]{3,2,1,0:T(8,128)(2,1)S(1)} %bitcast.419), channel_id=1, source_target_pairs={{0,1},{1,0},{2,3},{3,2},{4,5},{5,4},{6,7},{7,6},{8,9},{9,8},{10,11... | collective-permute-start | bytes 786440 | tf_op jit(solution)/shard_map/ppermute | solution.py:171
  37.5 5.4 %collective-permute-start.16 = (f32[2,32]{1,0:T(2,128)S(1)}, f32[2,32]{1,0:T(2,128)S(1)}, u32[]{:S(2)}, u32[]{:S(2)}) collective-permute-start(f32[2,32]{1,0:T(2,128)S(1)} %fusion.209), channel_id=1, source_target_pairs={{0,12},{4,8},{8,4},{12,0},{1,13},{5,9},{9,5},{13,1},{2,14},{6,10},... | collective-permute-start | bytes 776 | tf_op jit(solution)/shard_map/ppermute | solution.py:171
  39.5 4.5 %collective-permute-start.15 = (f32[2,32]{1,0:T(2,128)S(1)}, f32[2,32]{1,0:T(2,128)S(1)}, u32[]{:S(2)}, u32[]{:S(2)}) collective-permute-start(f32[2,32]{1,0:T(2,128)S(1)} %fusion.209), channel_id=1, source_target_pairs={{0,8},{4,12},{8,0},{12,4},{1,9},{5,13},{9,1},{13,5},{2,10},{6,14},... | collective-permute-start | bytes 776 | tf_op jit(solution)/shard_map/ppermute | solution.py:171
  39.5 4.5 %collective-permute-start.14 = (f32[2,32]{1,0:T(2,128)S(1)}, f32[2,32]{1,0:T(2,128)S(1)}, u32[]{:S(2)}, u32[]{:S(2)}) collective-permute-start(f32[2,32]{1,0:T(2,128)S(1)} %fusion.209), channel_id=1, source_target_pairs={{0,4},{4,0},{8,12},{12,8},{1,5},{5,1},{9,13},{13,9},{2,6},{6,2},{1... | collective-permute-start | bytes 776 | tf_op jit(solution)/shard_map/ppermute | solution.py:171
  44.0 3.8 %collective-permute-start.9 = (bf16[5,4,1,256]{3,2,1,0:T(2,128)(2,1)S(1)}, bf16[5,4,1,256]{3,2,1,0:T(2,128)(2,1)S(1)}, u32[]{:S(2)}, u32[]{:S(2)}) collective-permute-start(bf16[5,4,1,256]{3,2,1,0:T(2,128)(2,1)S(1)} %broadcast_select_fusion.10), channel_id=1, source_target_pairs={{0,2},{2,0},{1,3},{3,1},{4,6},{6,4},{5,7},{7,5},{8,10},{10,8},{9,1... | collective-permute-start | bytes 30728 | tf_op jit(solution)/shard_map/ppermute | solution.py:171
  48.1 6.2 %collective-permute-start.10 = (bf16[5,1,66,256]{3,2,1,0:T(8,128)(2,1)S(1)}, bf16[5,1,66,256]{3,2,1,0:T(8,128)(2,1)S(1)}, u32[]{:S(2)}, u32[]{:S(2)}) collective-permute-start(bf16[5,1,66,256]{3,2,1,0:T(8,128)(2,1)S(1)} %broadcast_select_fusion.7), channel_id=1, source_target_pairs={{0,4},{4,0},{8,12},{12,8},{1,5},{5,1},{9,13},{13,9},{2,6},{6,2},{1... | collective-permute-start | bytes 506888 | tf_op jit(solution)/shard_map/ppermute | solution.py:171
  49.7 7.4 %collective-permute-start.11 = (bf16[5,1,66,256]{3,2,1,0:T(8,128)(2,1)S(1)}, bf16[5,1,66,256]{3,2,1,0:T(8,128)(2,1)S(1)}, u32[]{:S(2)}, u32[]{:S(2)}) collective-permute-start(bf16[5,1,66,256]{3,2,1,0:T(8,128)(2,1)S(1)} %get-tuple-element.15), channel_id=1, source_target_pairs={{0,12},{4,8},{8,4},{12,0},{1,13},{5,9},{9,5},{13,1},{2,14},{6,10},... | collective-permute-start | bytes 506888 | tf_op jit(solution)/shard_map/ppermute | solution.py:171
  59.8 2.0 %copy-start = (bf16[3,3,3,256,256]{4,3,2,1,0:T(8,128)(2,1)S(1)}, bf16[3,3,3,256,256]{4,3,2,1,0:T(8,128)(2,1)}, u32[]{:S(2)}) copy-start(bf16[3,3,3,256,256]{4,3,2,1,0:T(8,128)(2,1)} %param.16) | copy-start | bytes 10616836
  68.8 25.3 %copy-start.6 = (f32[256]{0:T(256)S(1)}, f32[256]{0:T(256)}, u32[]{:S(2)}) copy-start(f32[256]{0:T(256)} %param.18) | copy-start | bytes 3076
  68.8 25.3 %copy-start.7 = (f32[256]{0:T(256)S(1)}, f32[256]{0:T(256)}, u32[]{:S(2)}) copy-start(f32[256]{0:T(256)} %param.17) | copy-start | bytes 3076
  69.6 1.2 %collective-permute-start.21 = (f32[2,32]{1,0:T(2,128)S(1)}, f32[2,32]{1,0:T(2,128)S(1)}, u32[]{:S(2)}, u32[]{:S(2)}) collective-permute-start(f32[2,32]{1,0:T(2,128)S(1)} %pad_maximum_fusion.14), channel_id=1, source_target_pairs={{0,1},{1,0},{2,3},{3,2},{4,5},{5,4},{6,7},{7,6},{8,9},{9,8},{10,11... | collective-permute-start | bytes 776 | tf_op jit(solution)/shard_map/ppermute | solution.py:171
  70.8 3.6 %collective-permute-start.22 = (f32[2,32]{1,0:T(2,128)S(1)}, f32[2,32]{1,0:T(2,128)S(1)}, u32[]{:S(2)}, u32[]{:S(2)}) collective-permute-start(f32[2,32]{1,0:T(2,128)S(1)} %fusion.141), channel_id=1, source_target_pairs={{0,2},{2,0},{1,3},{3,1},{4,6},{6,4},{5,7},{7,5},{8,10},{10,8},{9,1... | collective-permute-start | bytes 776 | tf_op jit(solution)/shard_map/ppermute | solution.py:171
  71.4 9.5 %collective-permute-start.17 = (bf16[2,4,64,256]{3,2,1,0:T(8,128)(2,1)S(1)}, bf16[2,4,64,256]{3,2,1,0:T(8,128)(2,1)S(1)}, u32[]{:S(2)}, u32[]{:S(2)}) collective-permute-start(bf16[2,4,64,256]{3,2,1,0:T(8,128)(2,1)S(1)} %bitcast.420), channel_id=1, source_target_pairs={{0,1},{1,0},{2,3},{3,2},{4,5},{5,4},{6,7},{7,6},{8,9},{9,8},{10,11... | collective-permute-start | bytes 786440 | tf_op jit(solution)/shard_map/ppermute | solution.py:171
  74.4 5.4 %collective-permute-start.25 = (f32[2,32]{1,0:T(2,128)S(1)}, f32[2,32]{1,0:T(2,128)S(1)}, u32[]{:S(2)}, u32[]{:S(2)}) collective-permute-start(f32[2,32]{1,0:T(2,128)S(1)} %fusion.208), channel_id=1, source_target_pairs={{0,12},{4,8},{8,4},{12,0},{1,13},{5,9},{9,5},{13,1},{2,14},{6,10},... | collective-permute-start | bytes 776 | tf_op jit(solution)/shard_map/ppermute | solution.py:171
  76.4 4.5 %collective-permute-start.24 = (f32[2,32]{1,0:T(2,128)S(1)}, f32[2,32]{1,0:T(2,128)S(1)}, u32[]{:S(2)}, u32[]{:S(2)}) collective-permute-start(f32[2,32]{1,0:T(2,128)S(1)} %fusion.208), channel_id=1, source_target_pairs={{0,8},{4,12},{8,0},{12,4},{1,9},{5,13},{9,1},{13,5},{2,10},{6,14},... | collective-permute-start | bytes 776 | tf_op jit(solution)/shard_map/ppermute | solution.py:171
  76.4 4.5 %collective-permute-start.23 = (f32[2,32]{1,0:T(2,128)S(1)}, f32[2,32]{1,0:T(2,128)S(1)}, u32[]{:S(2)}, u32[]{:S(2)}) collective-permute-start(f32[2,32]{1,0:T(2,128)S(1)} %fusion.208), channel_id=1, source_target_pairs={{0,4},{4,0},{8,12},{12,8},{1,5},{5,1},{9,13},{13,9},{2,6},{6,2},{1... | collective-permute-start | bytes 776 | tf_op jit(solution)/shard_map/ppermute | solution.py:171
  81.0 3.8 %collective-permute-start.18 = (bf16[5,4,1,256]{3,2,1,0:T(2,128)(2,1)S(1)}, bf16[5,4,1,256]{3,2,1,0:T(2,128)(2,1)S(1)}, u32[]{:S(2)}, u32[]{:S(2)}) collective-permute-start(bf16[5,4,1,256]{3,2,1,0:T(2,128)(2,1)S(1)} %broadcast_select_fusion.9), channel_id=1, source_target_pairs={{0,2},{2,0},{1,3},{3,1},{4,6},{6,4},{5,7},{7,5},{8,10},{10,8},{9,1... | collective-permute-start | bytes 30728 | tf_op jit(solution)/shard_map/ppermute | solution.py:171
  85.0 6.2 %collective-permute-start.19 = (bf16[5,1,66,256]{3,2,1,0:T(8,128)(2,1)S(1)}, bf16[5,1,66,256]{3,2,1,0:T(8,128)(2,1)S(1)}, u32[]{:S(2)}, u32[]{:S(2)}) collective-permute-start(bf16[5,1,66,256]{3,2,1,0:T(8,128)(2,1)S(1)} %broadcast_select_fusion.5), channel_id=1, source_target_pairs={{0,4},{4,0},{8,12},{12,8},{1,5},{5,1},{9,13},{13,9},{2,6},{6,2},{1... | collective-permute-start | bytes 506888 | tf_op jit(solution)/shard_map/ppermute | solution.py:171
  86.7 7.4 %collective-permute-start.20 = (bf16[5,1,66,256]{3,2,1,0:T(8,128)(2,1)S(1)}, bf16[5,1,66,256]{3,2,1,0:T(8,128)(2,1)S(1)}, u32[]{:S(2)}, u32[]{:S(2)}) collective-permute-start(bf16[5,1,66,256]{3,2,1,0:T(8,128)(2,1)S(1)} %get-tuple-element.11), channel_id=1, source_target_pairs={{0,12},{4,8},{8,4},{12,0},{1,13},{5,9},{9,5},{13,1},{2,14},{6,10},... | collective-permute-start | bytes 506888 | tf_op jit(solution)/shard_map/ppermute | solution.py:171
  96.6 2.1 %copy-start.1 = (bf16[3,3,3,256,256]{4,3,2,1,0:T(8,128)(2,1)S(1)}, bf16[3,3,3,256,256]{4,3,2,1,0:T(8,128)(2,1)}, u32[]{:S(2)}) copy-start(bf16[3,3,3,256,256]{4,3,2,1,0:T(8,128)(2,1)} %param.19) | copy-start | bytes 10616836

commit v4 on v2

--- a/solution.py
+++ b/solution.py
@@ -143,18 +143,17 @@
 
 
 def valid_conv(padded, kernel, frames, height, across):
-    result = jnp.zeros((frames * height * across, kernel.shape[-1]), jnp.float32)
+    channels = padded.shape[-1]
+    wide = jnp.concatenate(
+        [padded[:, dy : dy + height, dx : dx + across] for dy in range(3) for dx in range(3)], axis=-1
+    )
+    result = None
     for step_t in range(3):
-        for step_y in range(3):
-            for step_x in range(3):
-                window = padded[
-                    step_t : step_t + frames, step_y : step_y + height, step_x : step_x + across
-                ]
-                result = result + jnp.dot(
-                    window.reshape(-1, window.shape[-1]),
-                    kernel[step_t, step_y, step_x],
-                    preferred_element_type=jnp.float32,
-                )
+        window = wide[step_t : step_t + frames].reshape(-1, 9 * channels)
+        part = jnp.dot(
+            window, kernel[step_t].reshape(9 * channels, -1), preferred_element_type=jnp.float32
+        )
+        result = part if result is None else result + part
     return result.reshape(frames, height, across, -1)
 
 

time: 99.3 us -> 107 us (1.078); the launches traced: 98.7 us -> 105 us
  local copies, waits for them, and re-layouts: 10.2 us -> 18.1 us
  matrix products: 16.3 us -> 8.59 us
  other arithmetic: 8.73 us -> 12.4 us
  starting transfers between devices: 46.9 us -> 49.3 us
    dot_general x54 -> x6, matrix products: 14.2 us -> 6.52 us  [valid_conv(): jnp.dot(window, kernel[step_t].reshape(9 * channels, -1), preferred_eleme...]
    unnamed x18 -> x62, local copies, waits for them, and re-layouts: 0.27 us -> 5.24 us
    ppermute x1, waiting for transfers between devices: 0.01 us -> 3.1 us  [latent_halo(): corner = lax.ppermute(x[:, :1, :1], ('ha', 'wa'), corner_route)]
    ppermute x4, waiting for transfers between devices: 2.9 us -> 1.12 us  [passed_along(): return lax.ppermute(block, axis, route)]
    slice x1, local copies, waits for them, and re-layouts: 0.01 us -> 1.53 us  [latent_halo(): below = passed_along(x[:, :1], 'ha', -1)]
    concatenate x2, other arithmetic: 0.31 us -> 1.84 us  [padded_2(): x = jnp.concatenate([before, x, after], axis=dim)]
    ppermute x18, starting transfers between devices: 22.7 us -> 24.2 us  [group_allreduce(): lax.ppermute(x, axes, [(i, i ^ d << shift) for i in range(count)])]
    ppermute x4, starting transfers between devices: 5.62 us -> 6.93 us  [passed_along(): return lax.ppermute(block, axis, route)]
  transfers between devices with their start and end apart: 31 -> 31, of which waited for: 10 -> 10; matrix products, arithmetic and copies ran while one was open for 5% -> 10% of each run, Pallas kernels for 0% -> 0%
where the time goes in v4:
time: 107 us; the launch traced here: 105 us
  starting transfers between devices  49.3 us (46%)
  local copies, waits for them, and re-layouts  18.1 us (17%)
  waiting for transfers between devices  15.6 us (15%)
  other arithmetic  12.4 us (12%)
  matrix products  8.59 us (8%)
    ppermute x18, starting transfers between devices, group_allreduce(): lax.ppermute(x, axes, [(i, i ^ d << shift) for i in range(count)])  24.2 us
    ppermute x4, starting transfers between devices, padded_2(): before = lax.ppermute(last, axis, up)  11.7 us
    ppermute x4, waiting for transfers between devices, padded_2(): after = lax.ppermute(initial, axis, down)  8.41 us
    ppermute x4, starting transfers between devices, passed_along(): return lax.ppermute(block, axis, route)  6.93 us
    dot_general x6, matrix products, valid_conv(): jnp.dot(window, kernel[step_t].reshape(9 * channels, -1), preferred_eleme...  6.52 us
    unnamed x62, local copies, waits for them, and re-layouts  5.24 us
    ppermute x4, starting transfers between devices, padded_2(): after = lax.ppermute(initial, axis, down)  5.17 us
    convert_element_type x2, other arithmetic, norm_conv(): jnp.where(inside_mask(height + 2, across + 2, 1), act, 0.0)  3.38 us
  transfers between devices with their start and end apart: 31, of which 10 were waited for; matrix products, arithmetic and copies ran while one was open for 10% of the time, Pallas kernels for 0%

profile of v4, /device:TPU:0, one launch (start us, length us, event | category | flops | bytes accessed | tf_op | source)
XLA Modules:
  0.0 105.0 jit_solution(11592844609714158947)
XLA Ops:
  0.0 1.0 convert_reduce_fusion.2
  2.0 2.4 %collective-permute-start.3 = (f32[2,32]{1,0:T(2,128)}, f32[2,32]{1,0:T(2,128)}, u32[]{:S(2)}, u32[]{:S(2)}) collective-permute-start(f32[2,32]{1,0:T(2,128)} %pad_maximum_fusion.18), channel_id=1, source_target_pairs={{0,3},{1,2},{2,1},{3,0},{4,7},{5,6},{6,5},{7,4},{8,11},{9,10},{10,... | collective-permute-start | bytes 776 | tf_op jit(solution)/shard_map/ppermute | solution.py:47
  5.0 1.5 %slice.201 = bf16[3,1,32,512]{3,2,1,0:T(8,128)(2,1)} slice(bf16[3,2,32,512]{3,2,1,0:T(8,128)(2,1)} %param.10), slice={[0:3], [0:1], [0:32], [0:512]} | slice | bytes 196608 | tf_op jit(solution)/shard_map/slice | solution.py:106
  6.6 1.5 %collective-permute-start.1 = (bf16[3,1,32,512]{3,2,1,0:T(8,128)(2,1)}, bf16[3,1,32,512]{3,2,1,0:T(8,128)(2,1)}, u32[]{:S(2)}, u32[]{:S(2)}) collective-permute-start(bf16[3,1,32,512]{3,2,1,0:T(8,128)(2,1)} %slice.201), channel_id=1, source_target_pairs={{4,0},{8,4},{12,8},{5,1},{9,5},{13,9},{6,2},{10,6},{14,10},{7,3},{... | collective-permute-start | bytes 294920 | tf_op jit(solution)/shard_map/ppermute | solution.py:15
  8.9 1.3 %collective-permute-start = (bf16[3,2,1,512]{3,2,1,0:T(2,128)(2,1)S(1)}, bf16[3,2,1,512]{3,2,1,0:T(2,128)(2,1)}, u32[]{:S(2)}, u32[]{:S(2)}) collective-permute-start(bf16[3,2,1,512]{3,2,1,0:T(2,128)(2,1)S(1)} %slice.200), channel_id=1, source_target_pairs={{2,0},{3,1},{6,4},{7,5},{10,8},{11,9},{14,12},{15,13},{18,16},{19,... | collective-permute-start | bytes 18440 | tf_op jit(solution)/shard_map/ppermute | solution.py:15
  10.3 2.9 %slice_bitcast_fusion.7 = (bf16[512,256]{1,0:T(8,128)(2,1)}, bf16[512,256]{1,0:T(8,128)(2,1)}, bf16[512,256]{1,0:T(8,128)(2,1)}, bf16[512,256]{1,0:T(8,128)(2,1)...) fusion(bf16[3,3,512,256]{3,2,1,0:T(8,128)(2,1)} %param.13), kind=kLoop, calls=%fused_computation.75 | loop fusion | bytes 4194304 | tf_op jit(solution)/shard_map/squeeze | solution.py:129
  13.3 1.9 %fusion.34 = (bf16[1,3,3,256,256]{4,3,2,1,0:T(8,128)(2,1)}, bf16[1,3,3,256,256]{4,3,2,1,0:T(8,128)(2,1)}, bf16[1,3,3,256,256]{4,3,2,1,0:T(8,128)(2,1)}) fusion(bf16[3,3,3,256,256]{4,3,2,1,0:T(8,128)(2,1)S(1)} %copy-done), kind=kLoop, calls=%fused_computation.121 | loop fusion | bytes 7077888 | tf_op jit(solution)/shard_map/slice | solution.py:154
  15.1 1.4 %copy-done.1 = bf16[3,3,3,256,256]{4,3,2,1,0:T(8,128)(2,1)S(1)} copy-done((bf16[3,3,3,256,256]{4,3,2,1,0:T(8,128)(2,1)S(1)}, bf16[3,3,3,256,256]{4,3,2,1,0:T(8,128)(2,1)}, u32[]{:S(2)}) %copy-start.1) | copy-done | bytes 3538968
  16.5 1.3 %fusion.33 = (bf16[1,3,3,256,256]{4,3,2,1,0:T(8,128)(2,1)S(1)}, bf16[1,3,3,256,256]{4,3,2,1,0:T(8,128)(2,1)}, bf16[1,3,3,256,256]{4,3,2,1,0:T(8,128)(2,1)S(1)}) fusion(bf16[3,3,3,256,256]{4,3,2,1,0:T(8,128)(2,1)S(1)} %copy-done.1), kind=kLoop, calls=%fused_computation.120 | loop fusion | bytes 7077888 | tf_op jit(solution)/shard_map/slice | solution.py:154
  18.8 5.6 %collective-permute-start.6 = (f32[2,32]{1,0:T(2,128)S(1)}, f32[2,32]{1,0:T(2,128)S(1)}, u32[]{:S(2)}, u32[]{:S(2)}) collective-permute-start(f32[2,32]{1,0:T(2,128)S(1)} %add_add_fusion.5), channel_id=1, source_target_pairs={{0,12},{1,13},{2,14},{3,15},{4,8},{5,9},{6,10},{7,11},{8,4},{9,5},... | collective-permute-start | bytes 776 | tf_op jit(solution)/shard_map/ppermute | solution.py:47
  25.1 0.9 collective-permute-done.6
  26.0 1.3 %collective-permute-start.2 = (bf16[3,1,1,512]{3,2,1,0:T(2,128)(2,1)S(1)}, bf16[3,1,1,512]{3,2,1,0:T(2,128)(2,1)S(1)}, u32[]{:S(2)}, u32[]{:S(2)}) collective-permute-start(bf16[3,1,1,512]{3,2,1,0:T(2,128)(2,1)S(1)} %slice.202), channel_id=1, source_target_pairs={{6,0},{10,4},{14,8},{7,1},{11,5},{15,9},{22,16},{26,20},{30,24},{2... | collective-permute-start | bytes 9224 | tf_op jit(solution)/shard_map/ppermute | solution.py:113
  27.3 1.6 %collective-permute-done.7 = f32[2,32]{1,0:T(2,128)S(1)} collective-permute-done((f32[2,32]{1,0:T(2,128)S(1)}, f32[2,32]{1,0:T(2,128)S(1)}, u32[]{:S(2)}, u32[]{:S(2)}) %collective-permute-start.7) | collective-permute-done | bytes 288 | tf_op jit(solution)/shard_map/ppermute | solution.py:47
  29.3 3.1 %collective-permute-done.2 = bf16[3,1,1,512]{3,2,1,0:T(2,128)(2,1)S(1)} collective-permute-done((bf16[3,1,1,512]{3,2,1,0:T(2,128)(2,1)S(1)}, bf16[3,1,1,512]{3,2,1,0:T(2,128)(2,1)S(1)}, u32[]{:S(2)}, u32[]{:S(2)}) %collective-permute-start.2) | collective-permute-done | bytes 3104 | tf_op jit(solution)/shard_map/ppermute | solution.py:113
  32.4 1.2 %select_convert_fusion.2 = bf16[3,3,33,512]{3,2,1,0:T(8,128)(2,1)S(1)} fusion(bf16[3,1,1,512]{3,2,1,0:T(2,128)(2,1)S(1)} %collective-permute-done.2, bf16[3,1,32,512]{3,2,1,0:T(8,128)(2,1)} %collective-permute-done.1, bf16[3,2,1,512]{3,2,1,0:T(2,128)(2,1)} %collective-permute-done, bf16[3,2,32,512]{3,2,1,0:T(8,128)(2,1)S(1)} %copy-done.2, ...), kind=kLoop, calls=%fused_computation.24 | loop fusion | flops 2737152 | bytes 616547 | tf_op jit(solution)/shard_map/convert_element_type | solution.py:195
  35.2 1.2 %convolution_add_fusion.4 = bf16[192,256]{1,0:T(8,128)(2,1)S(1)} fusion(bf16[192,512]{1,0:T(8,128)(2,1)S(1)} %bitcast.119, bf16[3,3,512,256]{3,2,1,0:T(8,128)(2,1)} %param.13, f32[192,512]{1,0:T(8,128)S(1)} %fusion.15, f32[192,512]{1,0:T(8,128)S(1)} %fusion.11, f32[192,1024]{1,0:T(8,128)S(1)} %fusion.1), kind=kOutput, calls=%fused_computation.7 | convolution fusion | flops 50528256 | bytes 1146880 | tf_op jit(solution)/shard_map/dot_general | solution.py:123
  37.0 0.8 convert_reduce_fusion.1
  38.5 1.6 %collective-permute-start.16 = (f32[2,32]{1,0:T(2,128)S(1)}, f32[2,32]{1,0:T(2,128)S(1)}, u32[]{:S(2)}, u32[]{:S(2)}) collective-permute-start(f32[2,32]{1,0:T(2,128)S(1)} %pad_maximum_fusion.19), channel_id=1, source_target_pairs={{0,1},{1,0},{2,3},{3,2},{4,5},{5,4},{6,7},{7,6},{8,9},{9,8},{10,11... | collective-permute-start | bytes 776 | tf_op jit(solution)/shard_map/ppermute | solution.py:47
  40.3 1.3 %collective-permute-start.10 = (bf16[3,1,64,256]{3,2,1,0:T(8,128)(2,1)S(1)}, bf16[3,1,64,256]{3,2,1,0:T(8,128)(2,1)S(1)}, u32[]{:S(2)}, u32[]{:S(2)}) collective-permute-start(bf16[3,1,64,256]{3,2,1,0:T(8,128)(2,1)S(1)} %get-tuple-element.42), channel_id=1, source_target_pairs={{4,0},{8,4},{12,8},{5,1},{9,5},{13,9},{6,2},{10,6},{14,10},{7,3},{... | collective-permute-start | bytes 294920 | tf_op jit(solution)/shard_map/ppermute | solution.py:26
  41.6 4.6 %collective-permute-start.9 = (bf16[3,1,64,256]{3,2,1,0:T(8,128)(2,1)S(1)}, bf16[3,1,64,256]{3,2,1,0:T(8,128)(2,1)S(1)}, u32[]{:S(2)}, u32[]{:S(2)}) collective-permute-start(bf16[3,1,64,256]{3,2,1,0:T(8,128)(2,1)S(1)} %get-tuple-element.41), channel_id=1, source_target_pairs={{0,4},{4,8},{8,12},{1,5},{5,9},{9,13},{2,6},{6,10},{10,14},{3,7},{... | collective-permute-start | bytes 294920 | tf_op jit(solution)/shard_map/ppermute | solution.py:25
  46.2 2.3 %collective-permute-start.17 = (f32[2,32]{1,0:T(2,128)S(1)}, f32[2,32]{1,0:T(2,128)S(1)}, u32[]{:S(2)}, u32[]{:S(2)}) collective-permute-start(f32[2,32]{1,0:T(2,128)S(1)} %add_add_fusion.3), channel_id=1, source_target_pairs={{0,12},{1,13},{2,14},{3,15},{4,8},{5,9},{6,10},{7,11},{8,4},{9,5},... | collective-permute-start | bytes 776 | tf_op jit(solution)/shard_map/ppermute | solution.py:47
  48.5 1.3 %collective-permute-start.18 = (f32[2,32]{1,0:T(2,128)S(1)}, f32[2,32]{1,0:T(2,128)S(1)}, u32[]{:S(2)}, u32[]{:S(2)}) collective-permute-start(f32[2,32]{1,0:T(2,128)S(1)} %add_add_fusion.3), channel_id=1, source_target_pairs={{0,8},{1,9},{2,10},{3,11},{4,12},{5,13},{6,14},{7,15},{8,0},{9,1},... | collective-permute-start | bytes 776 | tf_op jit(solution)/shard_map/ppermute | solution.py:47
  49.7 0.9 collective-permute-start.19
  50.7 2.2 %collective-permute-start.11 = (bf16[3,6,1,256]{3,2,1,0:T(2,128)(2,1)S(1)}, bf16[3,6,1,256]{3,2,1,0:T(2,128)(2,1)S(1)}, u32[]{:S(2)}, u32[]{:S(2)}) collective-permute-start(bf16[3,6,1,256]{3,2,1,0:T(2,128)(2,1)S(1)} %get-tuple-element.37), channel_id=1, source_target_pairs={{0,2},{1,3},{4,6},{5,7},{8,10},{9,11},{12,14},{13,15},{16,18},{17,... | collective-permute-start | bytes 27656 | tf_op jit(solution)/shard_map/ppermute | solution.py:25
  52.9 1.3 %collective-permute-start.12 = (bf16[3,6,1,256]{3,2,1,0:T(2,128)(2,1)S(1)}, bf16[3,6,1,256]{3,2,1,0:T(2,128)(2,1)S(1)}, u32[]{:S(2)}, u32[]{:S(2)}) collective-permute-start(bf16[3,6,1,256]{3,2,1,0:T(2,128)(2,1)S(1)} %get-tuple-element.38), channel_id=1, source_target_pairs={{2,0},{3,1},{6,4},{7,5},{10,8},{11,9},{14,12},{15,13},{18,16},{19,... | collective-permute-start | bytes 27656 | tf_op jit(solution)/shard_map/ppermute | solution.py:26
  54.3 4.2 %collective-permute-done.12 = bf16[3,6,1,256]{3,2,1,0:T(2,128)(2,1)S(1)} collective-permute-done((bf16[3,6,1,256]{3,2,1,0:T(2,128)(2,1)S(1)}, bf16[3,6,1,256]{3,2,1,0:T(2,128)(2,1)S(1)}, u32[]{:S(2)}, u32[]{:S(2)}) %collective-permute-start.12) | collective-permute-done | bytes 9248 | tf_op jit(solution)/shard_map/ppermute | solution.py:26
  58.5 0.9 pad_maximum_fusion.4
  59.4 2.0 %collective-permute-start.13 = (bf16[2,6,66,256]{3,2,1,0:T(8,128)(2,1)}, bf16[2,6,66,256]{3,2,1,0:T(8,128)(2,1)}, u32[]{:S(2)}, u32[]{:S(2)}) collective-permute-start(bf16[2,6,66,256]{3,2,1,0:T(8,128)(2,1)} %pad_maximum_fusion.4), channel_id=1, source_target_pairs={{0,1},{2,3},{4,5},{6,7},{8,9},{10,11},{12,13},{14,15},{16,17},{18,... | collective-permute-start | bytes 1216520 | tf_op jit(solution)/shard_map/ppermute | solution.py:15
  62.6 1.7 %select_convert_fusion.1 = bf16[5,6,66,256]{3,2,1,0:T(8,128)(2,1)S(1)} fusion(bf16[3,6,1,256]{3,2,1,0:T(2,128)(2,1)S(1)} %collective-permute-done.12, bf16[3,1,64,256]{3,2,1,0:T(8,128)(2,1)S(1)} %collective-permute-done.10, bf16[3,4,64,256]{3,2,1,0:T(8,128)(2,1)S(1)} %bitcast.100, bf16[3,1,64,256]{3,2,1,0:T(8,128)(2,1)S(1)} %collective-permute-done.9, ...), kind=kLoop, calls=%fused_computation.1 | loop fusion | flops 11151360 | bytes 2032012 | tf_op jit(solution)/shard_map/convert_element_type | solution.py:174
  66.0 1.0 fusion.32
  67.3 1.1 %fusion.39 = f32[768,256]{1,0:T(8,128)S(1)} fusion(bf16[768,2304]{1,0:T(8,128)(2,1)S(1)} %bitcast.111, bf16[2304,256]{1,0:T(8,128)(2,1)S(1)} %bitcast.118), kind=kOutput, calls=%fused_computation.126 | convolution fusion | flops 905969664 | bytes 5505024 | tf_op jit(solution)/shard_map/dot_general | solution.py:153
  68.5 1.1 %convolution_add_fusion.3 = f32[768,256]{1,0:T(8,128)S(1)} fusion(f32[768,256]{1,0:T(8,128)S(1)} %fusion.39, bf16[768,2304]{1,0:T(8,128)(2,1)S(1)} %bitcast.109, bf16[2304,256]{1,0:T(8,128)(2,1)S(1)} %bitcast.117), kind=kOutput, calls=%fused_computation.5 | convolution fusion | flops 906166272 | bytes 6291456 | tf_op jit(solution)/shard_map/dot_general | solution.py:153
  69.8 1.1 %convert_reduce_fusion = (f32[256]{0:T(256)S(1)}, f32[256]{0:T(256)S(1)}, bf16[768,256]{1,0:T(8,128)(2,1)S(1)}) fusion(f32[768,256]{1,0:T(8,128)S(1)} %convolution_add_fusion.3, bf16[768,2304]{1,0:T(8,128)(2,1)S(1)} %bitcast.107, bf16[2304,256]{1,0:T(8,128)(2,1)S(1)} %bitcast.116), kind=kOutput, calls=%fused_computation.17 | convolution fusion | flops 907148800 | bytes 5900288 | tf_op jit(solution)/shard_map/dot_general | solution.py:153
  72.2 2.3 %collective-permute-start.26 = (f32[2,32]{1,0:T(2,128)S(1)}, f32[2,32]{1,0:T(2,128)S(1)}, u32[]{:S(2)}, u32[]{:S(2)}) collective-permute-start(f32[2,32]{1,0:T(2,128)S(1)} %pad_maximum_fusion.20), channel_id=1, source_target_pairs={{0,2},{1,3},{2,0},{3,1},{4,6},{5,7},{6,4},{7,5},{8,10},{9,11},{10,... | collective-permute-start | bytes 776 | tf_op jit(solution)/shard_map/ppermute | solution.py:47
  74.5 3.0 %collective-permute-start.20 = (bf16[3,1,64,256]{3,2,1,0:T(8,128)(2,1)S(1)}, bf16[3,1,64,256]{3,2,1,0:T(8,128)(2,1)S(1)}, u32[]{:S(2)}, u32[]{:S(2)}) collective-permute-start(bf16[3,1,64,256]{3,2,1,0:T(8,128)(2,1)S(1)} %get-tuple-element.39), channel_id=1, source_target_pairs={{0,4},{4,8},{8,12},{1,5},{5,9},{9,13},{2,6},{6,10},{10,14},{3,7},{... | collective-permute-start | bytes 294920 | tf_op jit(solution)/shard_map/ppermute | solution.py:25
  77.5 1.3 %collective-permute-start.21 = (bf16[3,1,64,256]{3,2,1,0:T(8,128)(2,1)S(1)}, bf16[3,1,64,256]{3,2,1,0:T(8,128)(2,1)S(1)}, u32[]{:S(2)}, u32[]{:S(2)}) collective-permute-start(bf16[3,1,64,256]{3,2,1,0:T(8,128)(2,1)S(1)} %get-tuple-element.40), channel_id=1, source_target_pairs={{4,0},{8,4},{12,8},{5,1},{9,5},{13,9},{6,2},{10,6},{14,10},{7,3},{... | collective-permute-start | bytes 294920 | tf_op jit(solution)/shard_map/ppermute | solution.py:26
  78.9 4.8 %collective-permute-start.28 = (f32[2,32]{1,0:T(2,128)S(1)}, f32[2,32]{1,0:T(2,128)S(1)}, u32[]{:S(2)}, u32[]{:S(2)}) collective-permute-start(f32[2,32]{1,0:T(2,128)S(1)} %add_add_fusion.1), channel_id=1, source_target_pairs={{0,12},{1,13},{2,14},{3,15},{4,8},{5,9},{6,10},{7,11},{8,4},{9,5},... | collective-permute-start | bytes 776 | tf_op jit(solution)/shard_map/ppermute | solution.py:47
  84.6 1.9 %collective-permute-start.22 = (bf16[3,6,1,256]{3,2,1,0:T(2,128)(2,1)S(1)}, bf16[3,6,1,256]{3,2,1,0:T(2,128)(2,1)S(1)}, u32[]{:S(2)}, u32[]{:S(2)}) collective-permute-start(bf16[3,6,1,256]{3,2,1,0:T(2,128)(2,1)S(1)} %get-tuple-element.35), channel_id=1, source_target_pairs={{0,2},{1,3},{4,6},{5,7},{8,10},{9,11},{12,14},{13,15},{16,18},{17,... | collective-permute-start | bytes 27656 | tf_op jit(solution)/shard_map/ppermute | solution.py:25
  86.5 1.3 %collective-permute-start.23 = (bf16[3,6,1,256]{3,2,1,0:T(2,128)(2,1)S(1)}, bf16[3,6,1,256]{3,2,1,0:T(2,128)(2,1)S(1)}, u32[]{:S(2)}, u32[]{:S(2)}) collective-permute-start(bf16[3,6,1,256]{3,2,1,0:T(2,128)(2,1)S(1)} %get-tuple-element.36), channel_id=1, source_target_pairs={{2,0},{3,1},{6,4},{7,5},{10,8},{11,9},{14,12},{15,13},{18,16},{19,... | collective-permute-start | bytes 27656 | tf_op jit(solution)/shard_map/ppermute | solution.py:26
  88.2 4.0 %collective-permute-done.23 = bf16[3,6,1,256]{3,2,1,0:T(2,128)(2,1)S(1)} collective-permute-done((bf16[3,6,1,256]{3,2,1,0:T(2,128)(2,1)S(1)}, bf16[3,6,1,256]{3,2,1,0:T(2,128)(2,1)S(1)}, u32[]{:S(2)}, u32[]{:S(2)}) %collective-permute-start.23) | collective-permute-done | bytes 9248 | tf_op jit(solution)/shard_map/ppermute | solution.py:26
  92.1 0.9 pad_maximum_fusion
  93.1 2.1 %collective-permute-start.24 = (bf16[2,6,66,256]{3,2,1,0:T(8,128)(2,1)}, bf16[2,6,66,256]{3,2,1,0:T(8,128)(2,1)}, u32[]{:S(2)}, u32[]{:S(2)}) collective-permute-start(bf16[2,6,66,256]{3,2,1,0:T(8,128)(2,1)} %pad_maximum_fusion), channel_id=1, source_target_pairs={{0,1},{2,3},{4,5},{6,7},{8,9},{10,11},{12,13},{14,15},{16,17},{18,... | collective-permute-start | bytes 1216520 | tf_op jit(solution)/shard_map/ppermute | solution.py:15
  96.2 1.7 %select_convert_fusion = bf16[5,6,66,256]{3,2,1,0:T(8,128)(2,1)S(1)} fusion(bf16[3,6,1,256]{3,2,1,0:T(2,128)(2,1)S(1)} %collective-permute-done.23, bf16[3,1,64,256]{3,2,1,0:T(8,128)(2,1)S(1)} %collective-permute-done.21, bf16[3,4,64,256]{3,2,1,0:T(8,128)(2,1)S(1)} %bitcast.106, bf16[3,1,64,256]{3,2,1,0:T(8,128)(2,1)S(1)} %collective-permute-done.20, ...), kind=kLoop, calls=%fused_computation | loop fusion | flops 11151360 | bytes 2032012 | tf_op jit(solution)/shard_map/convert_element_type | solution.py:174
  99.6 1.0 fusion.31
  100.9 1.1 %fusion.40 = f32[768,256]{1,0:T(8,128)S(1)} fusion(bf16[768,2304]{1,0:T(8,128)(2,1)S(1)} %bitcast.112, bf16[2304,256]{1,0:T(8,128)(2,1)S(1)} %bitcast.115), kind=kOutput, calls=%fused_computation.127 | convolution fusion | flops 905969664 | bytes 5505024 | tf_op jit(solution)/shard_map/dot_general | solution.py:153
  102.0 1.1 %convolution_add_fusion.1 = f32[768,256]{1,0:T(8,128)S(1)} fusion(f32[768,256]{1,0:T(8,128)S(1)} %fusion.40, bf16[768,2304]{1,0:T(8,128)(2,1)S(1)} %bitcast.110, bf16[2304,256]{1,0:T(8,128)(2,1)S(1)} %bitcast.114), kind=kOutput, calls=%fused_computation.3 | convolution fusion | flops 906166272 | bytes 6291456 | tf_op jit(solution)/shard_map/dot_general | solution.py:153
  103.1 1.1 %convolution_add_fusion = f32[768,256]{1,0:T(8,128)S(1)} fusion(f32[768,256]{1,0:T(8,128)S(1)} %convolution_add_fusion.1, bf16[768,2304]{1,0:T(8,128)(2,1)S(1)} %bitcast.108, bf16[2304,256]{1,0:T(8,128)(2,1)S(1)} %bitcast.113), kind=kOutput, calls=%fused_computation.2 | convolution fusion | flops 906166272 | bytes 6291456 | tf_op jit(solution)/shard_map/dot_general | solution.py:153
  104.2 0.8 add_convert_fusion
  (166 shorter events, 16.2 us)
Async XLA Ops:
  1.4 3.6 %copy-start.15 = (f32[32]{0:T(128)}, f32[32]{0:T(128)S(1)}, u32[]{:S(2)}) copy-start(f32[32]{0:T(128)S(1)} %reduce_sum.77) | copy-start | bytes 388
  2.0 16.1 %collective-permute-start.3 = (f32[2,32]{1,0:T(2,128)}, f32[2,32]{1,0:T(2,128)}, u32[]{:S(2)}, u32[]{:S(2)}) collective-permute-start(f32[2,32]{1,0:T(2,128)} %pad_maximum_fusion.18), channel_id=1, source_target_pairs={{0,3},{1,2},{2,1},{3,0},{4,7},{5,6},{6,5},{7,4},{8,11},{9,10},{10,... | collective-permute-start | bytes 776 | tf_op jit(solution)/shard_map/ppermute | solution.py:47
  4.3 13.7 %collective-permute-start.4 = (f32[2,32]{1,0:T(2,128)}, f32[2,32]{1,0:T(2,128)}, u32[]{:S(2)}, u32[]{:S(2)}) collective-permute-start(f32[2,32]{1,0:T(2,128)} %pad_maximum_fusion.18), channel_id=1, source_target_pairs={{0,2},{1,3},{2,0},{3,1},{4,6},{5,7},{6,4},{7,5},{8,10},{9,11},{10,... | collective-permute-start | bytes 776 | tf_op jit(solution)/shard_map/ppermute | solution.py:47
  4.9 13.1 %collective-permute-start.5 = (f32[2,32]{1,0:T(2,128)}, f32[2,32]{1,0:T(2,128)}, u32[]{:S(2)}, u32[]{:S(2)}) collective-permute-start(f32[2,32]{1,0:T(2,128)} %pad_maximum_fusion.18), channel_id=1, source_target_pairs={{0,1},{1,0},{2,3},{3,2},{4,5},{5,4},{6,7},{7,6},{8,9},{9,8},{10,11... | collective-permute-start | bytes 776 | tf_op jit(solution)/shard_map/ppermute | solution.py:47
  6.6 6.7 %copy-start = (bf16[3,3,3,256,256]{4,3,2,1,0:T(8,128)(2,1)S(1)}, bf16[3,3,3,256,256]{4,3,2,1,0:T(8,128)(2,1)}, u32[]{:S(2)}) copy-start(bf16[3,3,3,256,256]{4,3,2,1,0:T(8,128)(2,1)} %param.16) | copy-start | bytes 10616836
  6.6 25.9 %collective-permute-start.1 = (bf16[3,1,32,512]{3,2,1,0:T(8,128)(2,1)}, bf16[3,1,32,512]{3,2,1,0:T(8,128)(2,1)}, u32[]{:S(2)}, u32[]{:S(2)}) collective-permute-start(bf16[3,1,32,512]{3,2,1,0:T(8,128)(2,1)} %slice.201), channel_id=1, source_target_pairs={{4,0},{8,4},{12,8},{5,1},{9,5},{13,9},{6,2},{10,6},{14,10},{7,3},{... | collective-permute-start | bytes 294920 | tf_op jit(solution)/shard_map/ppermute | solution.py:15
  8.9 23.5 %collective-permute-start = (bf16[3,2,1,512]{3,2,1,0:T(2,128)(2,1)S(1)}, bf16[3,2,1,512]{3,2,1,0:T(2,128)(2,1)}, u32[]{:S(2)}, u32[]{:S(2)}) collective-permute-start(bf16[3,2,1,512]{3,2,1,0:T(2,128)(2,1)S(1)} %slice.200), channel_id=1, source_target_pairs={{2,0},{3,1},{6,4},{7,5},{10,8},{11,9},{14,12},{15,13},{18,16},{19,... | collective-permute-start | bytes 18440 | tf_op jit(solution)/shard_map/ppermute | solution.py:15
  16.5 8.6 %copy-start.2 = (bf16[3,2,32,512]{3,2,1,0:T(8,128)(2,1)S(1)}, bf16[3,2,32,512]{3,2,1,0:T(8,128)(2,1)}, u32[]{:S(2)}) copy-start(bf16[3,2,32,512]{3,2,1,0:T(8,128)(2,1)} %param.10) | copy-start | bytes 589828
  16.5 15.9 %copy-start.17 = (f32[512]{0:T(512)S(1)}, f32[512]{0:T(512)}, u32[]{:S(2)}) copy-start(f32[512]{0:T(512)} %param.12) | copy-start | bytes 6148
  16.5 15.9 %copy-start.18 = (f32[512]{0:T(512)S(1)}, f32[512]{0:T(512)}, u32[]{:S(2)}) copy-start(f32[512]{0:T(512)} %param.11) | copy-start | bytes 6148
  17.9 15.8 %copy-start.13 = (bf16[512,256]{1,0:T(8,128)(2,1)S(1)}, bf16[512,256]{1,0:T(8,128)(2,1)}, u32[]{:S(2)}) copy-start(bf16[512,256]{1,0:T(8,128)(2,1)} %get-tuple-element.26) | copy-start | bytes 786436
  17.9 16.1 %copy-start.11 = (bf16[512,256]{1,0:T(8,128)(2,1)S(1)}, bf16[512,256]{1,0:T(8,128)(2,1)}, u32[]{:S(2)}) copy-start(bf16[512,256]{1,0:T(8,128)(2,1)} %get-tuple-element.25) | copy-start | bytes 786436
  17.9 16.1 %copy-start.12 = (bf16[512,256]{1,0:T(8,128)(2,1)S(1)}, bf16[512,256]{1,0:T(8,128)(2,1)}, u32[]{:S(2)}) copy-start(bf16[512,256]{1,0:T(8,128)(2,1)} %get-tuple-element.31) | copy-start | bytes 786436
  18.8 7.2 %collective-permute-start.6 = (f32[2,32]{1,0:T(2,128)S(1)}, f32[2,32]{1,0:T(2,128)S(1)}, u32[]{:S(2)}, u32[]{:S(2)}) collective-permute-start(f32[2,32]{1,0:T(2,128)S(1)} %add_add_fusion.5), channel_id=1, source_target_pairs={{0,12},{1,13},{2,14},{3,15},{4,8},{5,9},{6,10},{7,11},{8,4},{9,5},... | collective-permute-start | bytes 776 | tf_op jit(solution)/shard_map/ppermute | solution.py:47
  24.4 4.5 %collective-permute-start.7 = (f32[2,32]{1,0:T(2,128)S(1)}, f32[2,32]{1,0:T(2,128)S(1)}, u32[]{:S(2)}, u32[]{:S(2)}) collective-permute-start(f32[2,32]{1,0:T(2,128)S(1)} %add_add_fusion.5), channel_id=1, source_target_pairs={{0,8},{1,9},{2,10},{3,11},{4,12},{5,13},{6,14},{7,15},{8,0},{9,1},... | collective-permute-start | bytes 776 | tf_op jit(solution)/shard_map/ppermute | solution.py:47
  24.4 4.5 %collective-permute-start.8 = (f32[2,32]{1,0:T(2,128)S(1)}, f32[2,32]{1,0:T(2,128)S(1)}, u32[]{:S(2)}, u32[]{:S(2)}) collective-permute-start(f32[2,32]{1,0:T(2,128)S(1)} %add_add_fusion.5), channel_id=1, source_target_pairs={{0,4},{1,5},{2,6},{3,7},{4,0},{5,1},{6,2},{7,3},{8,12},{9,13},{10,... | collective-permute-start | bytes 776 | tf_op jit(solution)/shard_map/ppermute | solution.py:47
  26.0 6.4 %collective-permute-start.2 = (bf16[3,1,1,512]{3,2,1,0:T(2,128)(2,1)S(1)}, bf16[3,1,1,512]{3,2,1,0:T(2,128)(2,1)S(1)}, u32[]{:S(2)}, u32[]{:S(2)}) collective-permute-start(bf16[3,1,1,512]{3,2,1,0:T(2,128)(2,1)S(1)} %slice.202), channel_id=1, source_target_pairs={{6,0},{10,4},{14,8},{7,1},{11,5},{15,9},{22,16},{26,20},{30,24},{2... | collective-permute-start | bytes 9224 | tf_op jit(solution)/shard_map/ppermute | solution.py:113
  29.3 4.5 %copy-start.14 = (bf16[512,256]{1,0:T(8,128)(2,1)S(1)}, bf16[512,256]{1,0:T(8,128)(2,1)}, u32[]{:S(2)}) copy-start(bf16[512,256]{1,0:T(8,128)(2,1)} %get-tuple-element.27) | copy-start | bytes 786436
  29.3 5.0 %copy-start.7 = (bf16[512,256]{1,0:T(8,128)(2,1)S(1)}, bf16[512,256]{1,0:T(8,128)(2,1)}, u32[]{:S(2)}) copy-start(bf16[512,256]{1,0:T(8,128)(2,1)} %get-tuple-element.24) | copy-start | bytes 786436
  29.3 5.0 %copy-start.8 = (bf16[512,256]{1,0:T(8,128)(2,1)S(1)}, bf16[512,256]{1,0:T(8,128)(2,1)}, u32[]{:S(2)}) copy-start(bf16[512,256]{1,0:T(8,128)(2,1)} %get-tuple-element.28) | copy-start | bytes 786436
  29.3 5.0 %copy-start.9 = (bf16[512,256]{1,0:T(8,128)(2,1)S(1)}, bf16[512,256]{1,0:T(8,128)(2,1)}, u32[]{:S(2)}) copy-start(bf16[512,256]{1,0:T(8,128)(2,1)} %get-tuple-element.29) | copy-start | bytes 786436
  29.3 5.0 %copy-start.10 = (bf16[512,256]{1,0:T(8,128)(2,1)S(1)}, bf16[512,256]{1,0:T(8,128)(2,1)}, u32[]{:S(2)}) copy-start(bf16[512,256]{1,0:T(8,128)(2,1)} %get-tuple-element.30) | copy-start | bytes 786436
  38.2 7.9 %collective-permute-start.14 = (f32[2,32]{1,0:T(2,128)S(1)}, f32[2,32]{1,0:T(2,128)S(1)}, u32[]{:S(2)}, u32[]{:S(2)}) collective-permute-start(f32[2,32]{1,0:T(2,128)S(1)} %pad_maximum_fusion.19), channel_id=1, source_target_pairs={{0,3},{1,2},{2,1},{3,0},{4,7},{5,6},{6,5},{7,4},{8,11},{9,10},{10,... | collective-permute-start | bytes 776 | tf_op jit(solution)/shard_map/ppermute | solution.py:47
  38.3 7.8 %collective-permute-start.15 = (f32[2,32]{1,0:T(2,128)S(1)}, f32[2,32]{1,0:T(2,128)S(1)}, u32[]{:S(2)}, u32[]{:S(2)}) collective-permute-start(f32[2,32]{1,0:T(2,128)S(1)} %pad_maximum_fusion.19), channel_id=1, source_target_pairs={{0,2},{1,3},{2,0},{3,1},{4,6},{5,7},{6,4},{7,5},{8,10},{9,11},{10,... | collective-permute-start | bytes 776 | tf_op jit(solution)/shard_map/ppermute | solution.py:47
  38.5 7.6 %collective-permute-start.16 = (f32[2,32]{1,0:T(2,128)S(1)}, f32[2,32]{1,0:T(2,128)S(1)}, u32[]{:S(2)}, u32[]{:S(2)}) collective-permute-start(f32[2,32]{1,0:T(2,128)S(1)} %pad_maximum_fusion.19), channel_id=1, source_target_pairs={{0,1},{1,0},{2,3},{3,2},{4,5},{5,4},{6,7},{7,6},{8,9},{9,8},{10,11... | collective-permute-start | bytes 776 | tf_op jit(solution)/shard_map/ppermute | solution.py:47
  40.2 22.3 %copy-start.19 = (f32[256]{0:T(256)S(1)}, f32[256]{0:T(256)}, u32[]{:S(2)}) copy-start(f32[256]{0:T(256)} %param.15) | copy-start | bytes 3076
  40.2 22.3 %copy-start.20 = (f32[256]{0:T(256)S(1)}, f32[256]{0:T(256)}, u32[]{:S(2)}) copy-start(f32[256]{0:T(256)} %param.14) | copy-start | bytes 3076
  40.3 10.4 %collective-permute-start.10 = (bf16[3,1,64,256]{3,2,1,0:T(8,128)(2,1)S(1)}, bf16[3,1,64,256]{3,2,1,0:T(8,128)(2,1)S(1)}, u32[]{:S(2)}, u32[]{:S(2)}) collective-permute-start(bf16[3,1,64,256]{3,2,1,0:T(8,128)(2,1)S(1)} %get-tuple-element.42), channel_id=1, source_target_pairs={{4,0},{8,4},{12,8},{5,1},{9,5},{13,9},{6,2},{10,6},{14,10},{7,3},{... | collective-permute-start | bytes 294920 | tf_op jit(solution)/shard_map/ppermute | solution.py:26
  41.6 9.1 %collective-permute-start.9 = (bf16[3,1,64,256]{3,2,1,0:T(8,128)(2,1)S(1)}, bf16[3,1,64,256]{3,2,1,0:T(8,128)(2,1)S(1)}, u32[]{:S(2)}, u32[]{:S(2)}) collective-permute-start(bf16[3,1,64,256]{3,2,1,0:T(8,128)(2,1)S(1)} %get-tuple-element.41), channel_id=1, source_target_pairs={{0,4},{4,8},{8,12},{1,5},{5,9},{9,13},{2,6},{6,10},{10,14},{3,7},{... | collective-permute-start | bytes 294920 | tf_op jit(solution)/shard_map/ppermute | solution.py:25
  46.2 8.0 %collective-permute-start.17 = (f32[2,32]{1,0:T(2,128)S(1)}, f32[2,32]{1,0:T(2,128)S(1)}, u32[]{:S(2)}, u32[]{:S(2)}) collective-permute-start(f32[2,32]{1,0:T(2,128)S(1)} %add_add_fusion.3), channel_id=1, source_target_pairs={{0,12},{1,13},{2,14},{3,15},{4,8},{5,9},{6,10},{7,11},{8,4},{9,5},... | collective-permute-start | bytes 776 | tf_op jit(solution)/shard_map/ppermute | solution.py:47
  48.5 5.7 %collective-permute-start.18 = (f32[2,32]{1,0:T(2,128)S(1)}, f32[2,32]{1,0:T(2,128)S(1)}, u32[]{:S(2)}, u32[]{:S(2)}) collective-permute-start(f32[2,32]{1,0:T(2,128)S(1)} %add_add_fusion.3), channel_id=1, source_target_pairs={{0,8},{1,9},{2,10},{3,11},{4,12},{5,13},{6,14},{7,15},{8,0},{9,1},... | collective-permute-start | bytes 776 | tf_op jit(solution)/shard_map/ppermute | solution.py:47
  49.7 4.5 %collective-permute-start.19 = (f32[2,32]{1,0:T(2,128)S(1)}, f32[2,32]{1,0:T(2,128)S(1)}, u32[]{:S(2)}, u32[]{:S(2)}) collective-permute-start(f32[2,32]{1,0:T(2,128)S(1)} %add_add_fusion.3), channel_id=1, source_target_pairs={{0,4},{1,5},{2,6},{3,7},{4,0},{5,1},{6,2},{7,3},{8,12},{9,13},{10,... | collective-permute-start | bytes 776 | tf_op jit(solution)/shard_map/ppermute | solution.py:47
  50.7 3.6 %collective-permute-start.11 = (bf16[3,6,1,256]{3,2,1,0:T(2,128)(2,1)S(1)}, bf16[3,6,1,256]{3,2,1,0:T(2,128)(2,1)S(1)}, u32[]{:S(2)}, u32[]{:S(2)}) collective-permute-start(bf16[3,6,1,256]{3,2,1,0:T(2,128)(2,1)S(1)} %get-tuple-element.37), channel_id=1, source_target_pairs={{0,2},{1,3},{4,6},{5,7},{8,10},{9,11},{12,14},{13,15},{16,18},{17,... | collective-permute-start | bytes 27656 | tf_op jit(solution)/shard_map/ppermute | solution.py:25
  52.9 5.7 %collective-permute-start.12 = (bf16[3,6,1,256]{3,2,1,0:T(2,128)(2,1)S(1)}, bf16[3,6,1,256]{3,2,1,0:T(2,128)(2,1)S(1)}, u32[]{:S(2)}, u32[]{:S(2)}) collective-permute-start(bf16[3,6,1,256]{3,2,1,0:T(2,128)(2,1)S(1)} %get-tuple-element.38), channel_id=1, source_target_pairs={{2,0},{3,1},{6,4},{7,5},{10,8},{11,9},{14,12},{15,13},{18,16},{19,... | collective-permute-start | bytes 27656 | tf_op jit(solution)/shard_map/ppermute | solution.py:26
  59.4 3.0 %collective-permute-start.13 = (bf16[2,6,66,256]{3,2,1,0:T(8,128)(2,1)}, bf16[2,6,66,256]{3,2,1,0:T(8,128)(2,1)}, u32[]{:S(2)}, u32[]{:S(2)}) collective-permute-start(bf16[2,6,66,256]{3,2,1,0:T(8,128)(2,1)} %pad_maximum_fusion.4), channel_id=1, source_target_pairs={{0,1},{2,3},{4,5},{6,7},{8,9},{10,11},{12,13},{14,15},{16,17},{18,... | collective-permute-start | bytes 1216520 | tf_op jit(solution)/shard_map/ppermute | solution.py:15
  70.9 25.2 %copy-start.21 = (f32[256]{0:T(256)S(1)}, f32[256]{0:T(256)}, u32[]{:S(2)}) copy-start(f32[256]{0:T(256)} %param.18) | copy-start | bytes 3076
  70.9 25.2 %copy-start.22 = (f32[256]{0:T(256)S(1)}, f32[256]{0:T(256)}, u32[]{:S(2)}) copy-start(f32[256]{0:T(256)} %param.17) | copy-start | bytes 3076
  71.4 7.4 %collective-permute-start.25 = (f32[2,32]{1,0:T(2,128)S(1)}, f32[2,32]{1,0:T(2,128)S(1)}, u32[]{:S(2)}, u32[]{:S(2)}) collective-permute-start(f32[2,32]{1,0:T(2,128)S(1)} %pad_maximum_fusion.20), channel_id=1, source_target_pairs={{0,3},{1,2},{2,1},{3,0},{4,7},{5,6},{6,5},{7,4},{8,11},{9,10},{10,... | collective-permute-start | bytes 776 | tf_op jit(solution)/shard_map/ppermute | solution.py:47
  72.2 6.7 %collective-permute-start.26 = (f32[2,32]{1,0:T(2,128)S(1)}, f32[2,32]{1,0:T(2,128)S(1)}, u32[]{:S(2)}, u32[]{:S(2)}) collective-permute-start(f32[2,32]{1,0:T(2,128)S(1)} %pad_maximum_fusion.20), channel_id=1, source_target_pairs={{0,2},{1,3},{2,0},{3,1},{4,6},{5,7},{6,4},{7,5},{8,10},{9,11},{10,... | collective-permute-start | bytes 776 | tf_op jit(solution)/shard_map/ppermute | solution.py:47
  74.5 4.4 %collective-permute-start.27 = (f32[2,32]{1,0:T(2,128)S(1)}, f32[2,32]{1,0:T(2,128)S(1)}, u32[]{:S(2)}, u32[]{:S(2)}) collective-permute-start(f32[2,32]{1,0:T(2,128)S(1)} %pad_maximum_fusion.20), channel_id=1, source_target_pairs={{0,1},{1,0},{2,3},{3,2},{4,5},{5,4},{6,7},{7,6},{8,9},{9,8},{10,11... | collective-permute-start | bytes 776 | tf_op jit(solution)/shard_map/ppermute | solution.py:47
  74.5 9.8 %collective-permute-start.20 = (bf16[3,1,64,256]{3,2,1,0:T(8,128)(2,1)S(1)}, bf16[3,1,64,256]{3,2,1,0:T(8,128)(2,1)S(1)}, u32[]{:S(2)}, u32[]{:S(2)}) collective-permute-start(bf16[3,1,64,256]{3,2,1,0:T(8,128)(2,1)S(1)} %get-tuple-element.39), channel_id=1, source_target_pairs={{0,4},{4,8},{8,12},{1,5},{5,9},{9,13},{2,6},{6,10},{10,14},{3,7},{... | collective-permute-start | bytes 294920 | tf_op jit(solution)/shard_map/ppermute | solution.py:25
  77.5 7.0 %collective-permute-start.21 = (bf16[3,1,64,256]{3,2,1,0:T(8,128)(2,1)S(1)}, bf16[3,1,64,256]{3,2,1,0:T(8,128)(2,1)S(1)}, u32[]{:S(2)}, u32[]{:S(2)}) collective-permute-start(bf16[3,1,64,256]{3,2,1,0:T(8,128)(2,1)S(1)} %get-tuple-element.40), channel_id=1, source_target_pairs={{4,0},{8,4},{12,8},{5,1},{9,5},{13,9},{6,2},{10,6},{14,10},{7,3},{... | collective-permute-start | bytes 294920 | tf_op jit(solution)/shard_map/ppermute | solution.py:26
  78.9 8.9 %collective-permute-start.28 = (f32[2,32]{1,0:T(2,128)S(1)}, f32[2,32]{1,0:T(2,128)S(1)}, u32[]{:S(2)}, u32[]{:S(2)}) collective-permute-start(f32[2,32]{1,0:T(2,128)S(1)} %add_add_fusion.1), channel_id=1, source_target_pairs={{0,12},{1,13},{2,14},{3,15},{4,8},{5,9},{6,10},{7,11},{8,4},{9,5},... | collective-permute-start | bytes 776 | tf_op jit(solution)/shard_map/ppermute | solution.py:47
  83.7 4.5 %collective-permute-start.29 = (f32[2,32]{1,0:T(2,128)S(1)}, f32[2,32]{1,0:T(2,128)S(1)}, u32[]{:S(2)}, u32[]{:S(2)}) collective-permute-start(f32[2,32]{1,0:T(2,128)S(1)} %add_add_fusion.1), channel_id=1, source_target_pairs={{0,8},{1,9},{2,10},{3,11},{4,12},{5,13},{6,14},{7,15},{8,0},{9,1},... | collective-permute-start | bytes 776 | tf_op jit(solution)/shard_map/ppermute | solution.py:47
  83.7 4.5 %collective-permute-start.30 = (f32[2,32]{1,0:T(2,128)S(1)}, f32[2,32]{1,0:T(2,128)S(1)}, u32[]{:S(2)}, u32[]{:S(2)}) collective-permute-start(f32[2,32]{1,0:T(2,128)S(1)} %add_add_fusion.1), channel_id=1, source_target_pairs={{0,4},{1,5},{2,6},{3,7},{4,0},{5,1},{6,2},{7,3},{8,12},{9,13},{10,... | collective-permute-start | bytes 776 | tf_op jit(solution)/shard_map/ppermute | solution.py:47
  84.6 3.6 %collective-permute-start.22 = (bf16[3,6,1,256]{3,2,1,0:T(2,128)(2,1)S(1)}, bf16[3,6,1,256]{3,2,1,0:T(2,128)(2,1)S(1)}, u32[]{:S(2)}, u32[]{:S(2)}) collective-permute-start(bf16[3,6,1,256]{3,2,1,0:T(2,128)(2,1)S(1)} %get-tuple-element.35), channel_id=1, source_target_pairs={{0,2},{1,3},{4,6},{5,7},{8,10},{9,11},{12,14},{13,15},{16,18},{17,... | collective-permute-start | bytes 27656 | tf_op jit(solution)/shard_map/ppermute | solution.py:25
  86.5 5.7 %collective-permute-start.23 = (bf16[3,6,1,256]{3,2,1,0:T(2,128)(2,1)S(1)}, bf16[3,6,1,256]{3,2,1,0:T(2,128)(2,1)S(1)}, u32[]{:S(2)}, u32[]{:S(2)}) collective-permute-start(bf16[3,6,1,256]{3,2,1,0:T(2,128)(2,1)S(1)} %get-tuple-element.36), channel_id=1, source_target_pairs={{2,0},{3,1},{6,4},{7,5},{10,8},{11,9},{14,12},{15,13},{18,16},{19,... | collective-permute-start | bytes 27656 | tf_op jit(solution)/shard_map/ppermute | solution.py:26
  93.1 3.0 %collective-permute-start.24 = (bf16[2,6,66,256]{3,2,1,0:T(8,128)(2,1)}, bf16[2,6,66,256]{3,2,1,0:T(8,128)(2,1)}, u32[]{:S(2)}, u32[]{:S(2)}) collective-permute-start(bf16[2,6,66,256]{3,2,1,0:T(8,128)(2,1)} %pad_maximum_fusion), channel_id=1, source_target_pairs={{0,1},{2,3},{4,5},{6,7},{8,9},{10,11},{12,13},{14,15},{16,17},{18,... | collective-permute-start | bytes 1216520 | tf_op jit(solution)/shard_map/ppermute | solution.py:15
  (6 other events, 9.9 us)

commit v5 on v3

--- a/solution.py
+++ b/solution.py
@@ -143,18 +143,17 @@
 
 
 def valid_conv(padded, kernel, frames, height, across):
-    result = jnp.zeros((frames * height * across, kernel.shape[-1]), jnp.float32)
+    channels = padded.shape[-1]
+    wide = jnp.concatenate(
+        [padded[:, dy : dy + height, dx : dx + across] for dy in range(3) for dx in range(3)], axis=-1
+    )
+    result = None
     for step_t in range(3):
-        for step_y in range(3):
-            for step_x in range(3):
-                window = padded[
-                    step_t : step_t + frames, step_y : step_y + height, step_x : step_x + across
-                ]
-                result = result + jnp.dot(
-                    window.reshape(-1, window.shape[-1]),
-                    kernel[step_t, step_y, step_x],
-                    preferred_element_type=jnp.float32,
-                )
+        window = wide[step_t : step_t + frames].reshape(-1, 9 * channels)
+        part = jnp.dot(
+            window, kernel[step_t].reshape(9 * channels, -1), preferred_element_type=jnp.float32
+        )
+        result = part if result is None else result + part
     return result.reshape(frames, height, across, -1)
 
 
@@ -195,13 +194,37 @@
     return jnp.repeat(average, group_width), jnp.repeat(scaling, group_width)
 
 
+def pack_sums(sums, width):
+    high = sums.astype(jnp.bfloat16)
+    rest = sums - high.astype(jnp.float32)
+    middle = rest.astype(jnp.bfloat16)
+    low = (rest - middle.astype(jnp.float32)).astype(jnp.bfloat16)
+    flat = jnp.concatenate([high.reshape(-1), middle.reshape(-1), low.reshape(-1)])
+    rows = -(-flat.size // width)
+    return jnp.pad(flat, (0, rows * width - flat.size)).reshape(rows, width)
+
+
+def unpack_sums(rows, like):
+    flat = rows.reshape(-1)[: 3 * like.size].astype(jnp.float32).reshape(3, *like.shape)
+    return (flat[0] + flat[1]) + flat[2]
+
+
+def swap_with(sums, payload, axis, distance):
+    width = payload.shape[-1]
+    packed = pack_sums(sums, width)
+    message = jnp.concatenate([payload.reshape(-1, width), packed], axis=0)
+    got = swap(message, axis, distance)
+    cut = got.shape[0] - packed.shape[0]
+    return unpack_sums(got[cut:], sums), got[:cut].reshape(payload.shape)
+
+
 def ha_round(sums, upper, lower):
     h = lax.axis_index("ha")
     to_first = jnp.where(h % 2 == 1, upper, lower)
     to_third = jnp.where(h == 2, upper, lower)
-    s1, got_first = swap((sums, to_first), "ha", 1)
+    s1, got_first = swap_with(sums, to_first, "ha", 1)
     s2 = swap(sums, "ha", 2)
-    s3, got_third = swap((sums, to_third), "ha", 3)
+    s3, got_third = swap_with(sums, to_third, "ha", 3)
     sums = (sums + s1) + (s2 + s3)
     above = jnp.where(h % 2 == 1, got_first, got_third)
     below = jnp.where(h % 2 == 0, got_first, got_third)
@@ -210,13 +233,13 @@
 
 def fast_conv_input(values):
     sums = local_sums(values.astype(jnp.float32))
-    s_t, earlier = swap((sums, values[-2:]), "ta", 1)
+    s_t, earlier = swap_with(sums, values[-2:], "ta", 1)
     sums = sums + s_t
     opening = jnp.concatenate([values[:1], values[:1]], axis=0)
     earlier = jnp.where(lax.axis_index("ta") == 0, opening, earlier)
     x = jnp.concatenate([earlier, values], axis=0)
     w = lax.axis_index("wa")
-    s_w, beside = swap((sums, jnp.where(w == 0, x[:, :, -1:], x[:, :, :1])), "wa", 1)
+    s_w, beside = swap_with(sums, jnp.where(w == 0, x[:, :, -1:], x[:, :, :1]), "wa", 1)
     sums = sums + s_w
     x = jnp.concatenate([beside, x, beside], axis=2)
     sums, above, below = ha_round(sums, x[:, :1], x[:, -1:])
@@ -227,7 +250,7 @@
 def fast_latent_input(values):
     sums = local_sums(values.astype(jnp.float32))
     sums = sums + swap(sums, "ta", 1)
-    s_w, beside = swap((sums, values[:, :, :1]), "wa", 1)
+    s_w, beside = swap_with(sums, values[:, :, :1], "wa", 1)
     sums = sums + s_w
     x = jnp.concatenate([values, beside], axis=2)
     sums, _, below = ha_round(sums, x[:, :1], x[:, :1])

time: 107 us -> 97.1 us (0.907)
  waiting for transfers between devices: 40.5 us -> 22.1 us
  local copies, waits for them, and re-layouts: 10.9 us -> 26.6 us
  other arithmetic: 9.2 us -> 18.3 us
  starting transfers between devices: 29 us -> 20 us
  matrix products: 16.3 us -> 8.74 us
    ppermute x26 -> x15, waiting for transfers between devices: 40.5 us -> 22.1 us  [swap(): return lax.ppermute(x, axis, [(i, i ^ distance) for i in range(size)])]
    ppermute x26 -> x15, starting transfers between devices: 29 us -> 20 us  [swap(): return lax.ppermute(x, axis, [(i, i ^ distance) for i in range(size)])]
    dot_general x54 -> x6, matrix products: 14.3 us -> 6.52 us  [valid_conv(): jnp.dot(window, kernel[step_t].reshape(9 * channels, -1), preferred_eleme...]
    unnamed x17 -> x57, local copies, waits for them, and re-layouts: 1.1 us -> 6.36 us
    select_n x0 -> x5, local copies, waits for them, and re-layouts: none -> 3.38 us  [the longest x3 1.71 us: ha_round(): below = jnp.where(h % 2 == 0, got_first, got_third)]
    slice x8 -> x10, local copies, waits for them, and re-layouts: 6.01 us -> 8.3 us  [the longest x2 5.11 us: valid_conv(): kernel[step_t].reshape(9 * channels, -1)]
    reshape x0 -> x37, local copies, waits for them, and re-layouts: none -> 1.86 us  [the longest x6 0.51 us: pack_sums(): middle.reshape(-1)]
    concatenate x0 -> x16, other arithmetic: none -> 1.74 us  [the longest x8 1.11 us: swap_with(): message = jnp.concatenate([payload.reshape(-1, width), packed], axis=0)]
  transfers between devices with their start and end apart: 26 -> 15, of which waited for: 19 -> 8; matrix products, arithmetic and copies ran while one was open for 5% -> 9% of each run, Pallas kernels for 0% -> 0%
where the time goes in v5:
time: 97.1 us; the launch traced here: 96.6 us
  local copies, waits for them, and re-layouts  26.6 us (27%)
  waiting for transfers between devices  22.1 us (23%)
  starting transfers between devices  20 us (21%)
  other arithmetic  18.3 us (19%)
  matrix products  8.74 us (9%)
    ppermute x15, waiting for transfers between devices, swap(): return lax.ppermute(x, axis, [(i, i ^ distance) for i in range(size)])  22.1 us
    ppermute x15, starting transfers between devices, swap(): return lax.ppermute(x, axis, [(i, i ^ distance) for i in range(size)])  20 us
    dot_general x6, matrix products, valid_conv(): jnp.dot(window, kernel[step_t].reshape(9 * channels, -1), preferred_eleme...  6.52 us
    unnamed x57, local copies, waits for them, and re-layouts  6.36 us
    slice x2, local copies, waits for them, and re-layouts, valid_conv(): kernel[step_t].reshape(9 * channels, -1)  5.11 us
    convert_element_type x2, other arithmetic, norm_conv(): jnp.where(inside_mask(height + 2, across + 2, 1), act, 0.0)  4.99 us
    reduce_sum x5, other arithmetic, local_sums(): jnp.sum(grouped, axis=(0, 2))  3.32 us
    dot_general x4, matrix products, upsample(): dot = lambda v, w: jnp.dot(flat(v), w, preferred_element_type=jnp.float32)  2.22 us
  transfers between devices with their start and end apart: 15, of which 8 were waited for; matrix products, arithmetic and copies ran while one was open for 9% of the time, Pallas kernels for 0%

profile of v5, /device:TPU:0, one launch (start us, length us, event | category | flops | bytes accessed | tf_op | source)
XLA Modules:
  0.0 96.6 jit_solution(14987772056623497767)
XLA Ops:
  0.0 1.1 %convert_reduce_fusion.2 = (f32[512]{0:T(512)S(1)}, f32[512]{0:T(512)S(1)}) fusion(bf16[3,2,32,512]{3,2,1,0:T(8,128)(2,1)} %param.10), kind=kLoop, calls=%fused_computation.52 | loop fusion | flops 392192 | bytes 200704 | tf_op jit(solution)/shard_map/reduce_sum | solution.py:179
  2.0 1.6 %slice_bitcast_fusion.7 = (bf16[512,256]{1,0:T(8,128)(2,1)S(1)}, bf16[512,256]{1,0:T(8,128)(2,1)S(1)}, bf16[512,256]{1,0:T(8,128)(2,1)S(1)}, bf16[512,256]{1,0:T...) fusion(bf16[3,3,512,256]{3,2,1,0:T(8,128)(2,1)} %param.13), kind=kLoop, calls=%fused_computation.69 | loop fusion | bytes 4194304 | tf_op jit(solution)/shard_map/squeeze | solution.py:129
  4.2 2.6 %collective-permute-start.1 = (bf16[7,512]{1,0:T(8,128)(2,1)S(1)}, bf16[7,512]{1,0:T(8,128)(2,1)S(1)}, u32[]{:S(2)}, u32[]{:S(2)}) collective-permute-start(bf16[7,512]{1,0:T(8,128)(2,1)S(1)} %pad_maximum_fusion.21), channel_id=1, source_target_pairs={{0,2},{2,0},{1,3},{3,1},{4,6},{6,4},{5,7},{7,5},{8,10},{10,8},{9,1... | collective-permute-start | bytes 21512 | tf_op jit(solution)/shard_map/ppermute | solution.py:170
  6.9 1.6 %collective-permute-done.1 = bf16[7,512]{1,0:T(8,128)(2,1)S(1)} collective-permute-done((bf16[7,512]{1,0:T(8,128)(2,1)S(1)}, bf16[7,512]{1,0:T(8,128)(2,1)S(1)}, u32[]{:S(2)}, u32[]{:S(2)}) %collective-permute-start.1) | collective-permute-done | bytes 7200 | tf_op jit(solution)/shard_map/ppermute | solution.py:170
  9.1 2.2 %collective-permute-start.2 = (bf16[100,512]{1,0:T(8,128)(2,1)S(1)}, bf16[100,512]{1,0:T(8,128)(2,1)S(1)}, u32[]{:S(2)}, u32[]{:S(2)}) collective-permute-start(bf16[100,512]{1,0:T(8,128)(2,1)S(1)} %pad_maximum_fusion.16), channel_id=1, source_target_pairs={{0,4},{4,0},{8,12},{12,8},{1,5},{5,1},{9,13},{13,9},{2,6},{6,2},{1... | collective-permute-start | bytes 307208 | tf_op jit(solution)/shard_map/ppermute | solution.py:170
  11.8 2.5 %collective-permute-start.3 = (bf16[100,512]{1,0:T(8,128)(2,1)S(1)}, bf16[100,512]{1,0:T(8,128)(2,1)S(1)}, u32[]{:S(2)}, u32[]{:S(2)}) collective-permute-start(bf16[100,512]{1,0:T(8,128)(2,1)S(1)} %pad_maximum_fusion.16), channel_id=1, source_target_pairs={{0,12},{4,8},{8,4},{12,0},{1,13},{5,9},{9,5},{13,1},{2,14},{6,10},... | collective-permute-start | bytes 307208 | tf_op jit(solution)/shard_map/ppermute | solution.py:170
  14.5 4.2 %collective-permute-done.3 = bf16[100,512]{1,0:T(8,128)(2,1)S(1)} collective-permute-done((bf16[100,512]{1,0:T(8,128)(2,1)S(1)}, bf16[100,512]{1,0:T(8,128)(2,1)S(1)}, u32[]{:S(2)}, u32[]{:S(2)}) %collective-permute-start.3) | collective-permute-done | bytes 102432 | tf_op jit(solution)/shard_map/ppermute | solution.py:170
  21.2 1.3 %convolution_add_fusion.4 = bf16[192,256]{1,0:T(8,128)(2,1)S(1)} fusion(bf16[192,512]{1,0:T(8,128)(2,1)S(1)} %bitcast.126, bf16[3,3,512,256]{3,2,1,0:T(8,128)(2,1)} %param.13, f32[192,512]{1,0:T(8,128)S(1)} %fusion.15, f32[192,512]{1,0:T(8,128)S(1)} %fusion.11, f32[192,1024]{1,0:T(8,128)S(1)} %fusion.1), kind=kOutput, calls=%fused_computation.7 | convolution fusion | flops 50528256 | bytes 1146880 | tf_op jit(solution)/shard_map/dot_general | solution.py:123
  23.1 1.4 %convert_reduce_fusion.1 = (f32[256]{0:T(256)}, f32[256]{0:T(256)}, bf16[3,2,2,64,256]{4,1,3,0,2:T(2,128)(2,1)S(1)}) fusion(bf16[3,2,1,64,256]{4,1,3,0,2:T(2,128)(2,1)S(1)} %bitcast.129, bf16[3,2,1,64,256]{4,1,3,0,2:T(2,128)(2,1)S(1)} %bitcast.128), kind=kLoop, calls=%fused_computation.19 | loop fusion | flops 982528 | bytes 788480 | tf_op jit(solution)/shard_map/reduce_sum | solution.py:179
  24.6 0.7 copy-done.1
  25.5 0.7 copy.27
  26.2 0.7 reduce_sum.82
  27.0 0.6 reduce_sum.83
  27.6 0.7 reduce_sum.85
  29.7 1.0 %pad_maximum_fusion.2 = bf16[513,256]{1,0:T(8,128)(2,1)S(1)} fusion(bf16[1,256]{1,0:T(2,128)(2,1)S(1)} %reshape.701, bf16[512,256]{1,0:T(8,128)(2,1)} %bitcast.123), kind=kLoop, calls=%fused_computation.56 | loop fusion | flops 525312 | bytes 525312 | tf_op jit(solution)/shard_map/concatenate | solution.py:215
  30.8 1.8 %fusion.107 = (bf16[1,3,3,256,256]{4,3,2,1,0:T(8,128)(2,1)}, bf16[1,3,3,256,256]{4,3,2,1,0:T(8,128)(2,1)}, bf16[1,3,3,256,256]{4,3,2,1,0:T(8,128)(2,1)}) fusion(bf16[3,3,3,256,256]{4,3,2,1,0:T(8,128)(2,1)S(1)} %copy-done), kind=kLoop, calls=%fused_computation.257 | loop fusion | bytes 7077888 | tf_op jit(solution)/shard_map/slice | solution.py:154
  32.9 0.6 copy-done.8
  33.6 0.7 slice_convert_fusion.7
  34.8 1.5 %collective-permute-start.6 = (bf16[21,256]{1,0:T(8,128)(2,1)S(1)}, bf16[21,256]{1,0:T(8,128)(2,1)S(1)}, u32[]{:S(2)}, u32[]{:S(2)}) collective-permute-start(bf16[21,256]{1,0:T(8,128)(2,1)S(1)} %pad_maximum_fusion.19), channel_id=1, source_target_pairs={{0,2},{2,0},{1,3},{3,1},{4,6},{6,4},{5,7},{7,5},{8,10},{10,8},{9,1... | collective-permute-start | bytes 32264 | tf_op jit(solution)/shard_map/ppermute | solution.py:170
  36.4 2.2 %collective-permute-done.6 = bf16[21,256]{1,0:T(8,128)(2,1)S(1)} collective-permute-done((bf16[21,256]{1,0:T(8,128)(2,1)S(1)}, bf16[21,256]{1,0:T(8,128)(2,1)S(1)}, u32[]{:S(2)}, u32[]{:S(2)}) %collective-permute-start.6) | collective-permute-done | bytes 10784 | tf_op jit(solution)/shard_map/ppermute | solution.py:170
  39.5 0.9 collective-permute-start.7
  40.5 2.3 %collective-permute-start.9 = (f32[2,32]{1,0:T(2,128)S(1)}, f32[2,32]{1,0:T(2,128)S(1)}, u32[]{:S(2)}, u32[]{:S(2)}) collective-permute-start(f32[2,32]{1,0:T(2,128)S(1)} %get-tuple-element.22), channel_id=1, source_target_pairs={{0,8},{4,12},{8,0},{12,4},{1,9},{5,13},{9,1},{13,5},{2,10},{6,14},... | collective-permute-start | bytes 776 | tf_op jit(solution)/shard_map/ppermute | solution.py:170
  42.7 1.3 %collective-permute-start.8 = (bf16[331,256]{1,0:T(8,128)(2,1)S(1)}, bf16[331,256]{1,0:T(8,128)(2,1)S(1)}, u32[]{:S(2)}, u32[]{:S(2)}) collective-permute-start(bf16[331,256]{1,0:T(8,128)(2,1)S(1)} %get-tuple-element.68), channel_id=1, source_target_pairs={{0,12},{4,8},{8,4},{12,0},{1,13},{5,9},{9,5},{13,1},{2,14},{6,10},... | collective-permute-start | bytes 508424 | tf_op jit(solution)/shard_map/ppermute | solution.py:170
  44.0 1.2 %collective-permute-done.7 = bf16[331,256]{1,0:T(8,128)(2,1)S(1)} collective-permute-done((bf16[331,256]{1,0:T(8,128)(2,1)S(1)}, bf16[331,256]{1,0:T(8,128)(2,1)S(1)}, u32[]{:S(2)}, u32[]{:S(2)}) %collective-permute-start.7) | collective-permute-done | bytes 169504 | tf_op jit(solution)/shard_map/ppermute | solution.py:170
  45.3 5.0 %collective-permute-done.8 = bf16[331,256]{1,0:T(8,128)(2,1)S(1)} collective-permute-done((bf16[331,256]{1,0:T(8,128)(2,1)S(1)}, bf16[331,256]{1,0:T(8,128)(2,1)S(1)}, u32[]{:S(2)}, u32[]{:S(2)}) %collective-permute-start.8) | collective-permute-done | bytes 169504 | tf_op jit(solution)/shard_map/ppermute | solution.py:170
  51.1 2.1 %select_convert_fusion.1 = bf16[5,6,66,256]{3,2,1,0:T(8,128)(2,1)S(1)} fusion(bf16[5,1,66,256]{3,2,1,0:T(8,128)(2,1)S(1)} %select_n.183, bf16[5,4,1,256]{3,2,1,0:T(2,128)(2,1)S(1)} %reshape.737, bf16[3,4,64,256]{3,2,1,0:T(8,128)(2,1)S(1)} %bitcast.106, bf16[2,4,64,256]{3,2,1,0:T(8,128)(2,1)S(1)} %maximum_select_fusion, ...), kind=kLoop, calls=%fused_computation.1 | loop fusion | flops 11151360 | bytes 2021772 | tf_op jit(solution)/shard_map/convert_element_type | solution.py:269
  55.0 1.0 %fusion.105 = (bf16[3,4,64,2304]{3,2,1,0:T(8,128)(2,1)S(1)}, bf16[3,4,64,2304]{3,2,1,0:T(8,128)(2,1)S(1)}, bf16[3,4,64,2304]{3,2,1,0:T(8,128)(2,1)S(1)}) fusion(bf16[5,4,64,2304]{3,2,1,0:T(8,128)(2,1)S(1)} %slice_dynamic-update-slice_fusion.9), kind=kLoop, calls=%fused_computation.255 | loop fusion | bytes 21233664 | tf_op jit(solution)/shard_map/slice | solution.py:152
  56.2 1.1 %fusion.112 = f32[768,256]{1,0:T(8,128)S(1)} fusion(bf16[768,2304]{1,0:T(8,128)(2,1)S(1)} %bitcast.115, bf16[2304,256]{1,0:T(8,128)(2,1)S(1)} %bitcast.119), kind=kOutput, calls=%fused_computation.262 | convolution fusion | flops 905969664 | bytes 5505024 | tf_op jit(solution)/shard_map/dot_general | solution.py:153
  57.5 1.1 %convolution_add_fusion.3 = f32[768,256]{1,0:T(8,128)S(1)} fusion(f32[768,256]{1,0:T(8,128)S(1)} %fusion.112, bf16[768,2304]{1,0:T(8,128)(2,1)S(1)} %bitcast.113, bf16[2304,256]{1,0:T(8,128)(2,1)S(1)} %bitcast.118), kind=kOutput, calls=%fused_computation.5 | convolution fusion | flops 906166272 | bytes 6291456 | tf_op jit(solution)/shard_map/dot_general | solution.py:153
  58.8 1.1 %convert_reduce_fusion = (f32[256]{0:T(256)S(1)}, f32[256]{0:T(256)S(1)}, bf16[768,256]{1,0:T(8,128)(2,1)S(1)}) fusion(f32[768,256]{1,0:T(8,128)S(1)} %convolution_add_fusion.3, bf16[768,2304]{1,0:T(8,128)(2,1)S(1)} %bitcast.111, bf16[2304,256]{1,0:T(8,128)(2,1)S(1)} %bitcast.117), kind=kOutput, calls=%fused_computation.17 | convolution fusion | flops 907148800 | bytes 5900288 | tf_op jit(solution)/shard_map/dot_general | solution.py:153
  60.7 1.5 %collective-permute-done.10 = bf16[513,256]{1,0:T(8,128)(2,1)S(1)} collective-permute-done((bf16[513,256]{1,0:T(8,128)(2,1)S(1)}, bf16[513,256]{1,0:T(8,128)(2,1)S(1)}, u32[]{:S(2)}, u32[]{:S(2)}) %collective-permute-start.10) | collective-permute-done | bytes 262688 | tf_op jit(solution)/shard_map/ppermute | solution.py:170
  62.9 1.5 %collective-permute-start.11 = (bf16[21,256]{1,0:T(8,128)(2,1)S(1)}, bf16[21,256]{1,0:T(8,128)(2,1)S(1)}, u32[]{:S(2)}, u32[]{:S(2)}) collective-permute-start(bf16[21,256]{1,0:T(8,128)(2,1)S(1)} %pad_maximum_fusion.20), channel_id=1, source_target_pairs={{0,2},{2,0},{1,3},{3,1},{4,6},{6,4},{5,7},{7,5},{8,10},{10,8},{9,1... | collective-permute-start | bytes 32264 | tf_op jit(solution)/shard_map/ppermute | solution.py:170
  64.4 2.2 %collective-permute-done.11 = bf16[21,256]{1,0:T(8,128)(2,1)S(1)} collective-permute-done((bf16[21,256]{1,0:T(8,128)(2,1)S(1)}, bf16[21,256]{1,0:T(8,128)(2,1)S(1)}, u32[]{:S(2)}, u32[]{:S(2)}) %collective-permute-start.11) | collective-permute-done | bytes 10784 | tf_op jit(solution)/shard_map/ppermute | solution.py:170
  67.6 2.1 %collective-permute-start.12 = (bf16[331,256]{1,0:T(8,128)(2,1)S(1)}, bf16[331,256]{1,0:T(8,128)(2,1)S(1)}, u32[]{:S(2)}, u32[]{:S(2)}) collective-permute-start(bf16[331,256]{1,0:T(8,128)(2,1)S(1)} %get-tuple-element.61), channel_id=1, source_target_pairs={{0,4},{4,0},{8,12},{12,8},{1,5},{5,1},{9,13},{13,9},{2,6},{6,2},{1... | collective-permute-start | bytes 508424 | tf_op jit(solution)/shard_map/ppermute | solution.py:170
  69.7 3.3 %fusion.106 = (bf16[1,3,3,256,256]{4,3,2,1,0:T(8,128)(2,1)S(1)}, bf16[1,3,3,256,256]{4,3,2,1,0:T(8,128)(2,1)}, bf16[1,3,3,256,256]{4,3,2,1,0:T(8,128)(2,1)S(1)}) fusion(bf16[3,3,3,256,256]{4,3,2,1,0:T(8,128)(2,1)} %param.19), kind=kLoop, calls=%fused_computation.256 | loop fusion | bytes 7077888 | tf_op jit(solution)/shard_map/slice | solution.py:154
  72.9 2.4 %collective-permute-start.13 = (bf16[331,256]{1,0:T(8,128)(2,1)S(1)}, bf16[331,256]{1,0:T(8,128)(2,1)S(1)}, u32[]{:S(2)}, u32[]{:S(2)}) collective-permute-start(bf16[331,256]{1,0:T(8,128)(2,1)S(1)} %get-tuple-element.62), channel_id=1, source_target_pairs={{0,12},{4,8},{8,4},{12,0},{1,13},{5,9},{9,5},{13,1},{2,14},{6,10},... | collective-permute-start | bytes 508424 | tf_op jit(solution)/shard_map/ppermute | solution.py:170
  75.3 0.7 copy-done.9
  76.1 4.1 %collective-permute-done.13 = bf16[331,256]{1,0:T(8,128)(2,1)S(1)} collective-permute-done((bf16[331,256]{1,0:T(8,128)(2,1)S(1)}, bf16[331,256]{1,0:T(8,128)(2,1)S(1)}, u32[]{:S(2)}, u32[]{:S(2)}) %collective-permute-start.13) | collective-permute-done | bytes 169504 | tf_op jit(solution)/shard_map/ppermute | solution.py:170
  80.2 0.7 copy-done.10
  81.5 1.8 %broadcast_select_fusion.6 = (bf16[330,256]{1,0:T(8,128)(2,1)}, bf16[330,256]{1,0:T(8,128)(2,1)}) fusion(pred[]{:T(512)S(6)} %eq.35, bf16[331,256]{1,0:T(8,128)(2,1)} %copy-done.10, bf16[331,256]{1,0:T(8,128)(2,1)} %copy-done.9, pred[]{:T(512)S(6)} %eq.34), kind=kLoop, calls=%fused_computation.92 | loop fusion | flops 168960 | bytes 675842 | tf_op jit(solution)/shard_map/jit(_where)/select_n | solution.py:229
  83.2 1.6 %select_n.190 = bf16[5,1,66,256]{3,2,1,0:T(8,128)(2,1)} reshape(bf16[330,256]{1,0:T(8,128)(2,1)} %get-tuple-element.57) | data formatting | bytes 337920 | tf_op jit(solution)/shard_map/jit(_where)/select_n | solution.py:229
  84.9 1.6 %select_n.192 = bf16[5,1,66,256]{3,2,1,0:T(8,128)(2,1)} reshape(bf16[330,256]{1,0:T(8,128)(2,1)} %get-tuple-element.58) | data formatting | bytes 337920 | tf_op jit(solution)/shard_map/jit(_where)/select_n | solution.py:230
  86.5 2.9 %select_convert_fusion = bf16[5,6,66,256]{3,2,1,0:T(8,128)(2,1)S(1)} fusion(bf16[5,1,66,256]{3,2,1,0:T(8,128)(2,1)} %select_n.192, bf16[5,4,1,256]{3,2,1,0:T(2,128)(2,1)S(1)} %reshape.738, bf16[3,4,64,256]{3,2,1,0:T(8,128)(2,1)S(1)} %bitcast.110, bf16[2,4,64,256]{3,2,1,0:T(8,128)(2,1)S(1)} %maximum_select_fusion.1, bf16[5,1,66,256]{3,2,1,0:T(8,128)(2,1)} %select_n.190, ...), kind=kLoop, calls=%fused_computation | loop fusion | flops 11151360 | bytes 2021772 | tf_op jit(solution)/shard_map/convert_element_type | solution.py:269
  91.2 1.2 %fusion.104 = (bf16[3,4,64,2304]{3,2,1,0:T(8,128)(2,1)S(1)}, bf16[3,4,64,2304]{3,2,1,0:T(8,128)(2,1)S(1)}, bf16[3,4,64,2304]{3,2,1,0:T(8,128)(2,1)S(1)}) fusion(bf16[5,4,64,2304]{3,2,1,0:T(8,128)(2,1)S(1)} %slice_dynamic-update-slice_fusion), kind=kLoop, calls=%fused_computation.254 | loop fusion | bytes 21233664 | tf_op jit(solution)/shard_map/slice | solution.py:152
  92.5 1.1 %fusion.113 = f32[768,256]{1,0:T(8,128)S(1)} fusion(bf16[768,2304]{1,0:T(8,128)(2,1)S(1)} %bitcast.116, bf16[2304,256]{1,0:T(8,128)(2,1)S(1)} %bitcast.122), kind=kOutput, calls=%fused_computation.263 | convolution fusion | flops 905969664 | bytes 5505024 | tf_op jit(solution)/shard_map/dot_general | solution.py:153
  93.5 1.1 %convolution_add_fusion.1 = f32[768,256]{1,0:T(8,128)S(1)} fusion(f32[768,256]{1,0:T(8,128)S(1)} %fusion.113, bf16[768,2304]{1,0:T(8,128)(2,1)S(1)} %bitcast.114, bf16[2304,256]{1,0:T(8,128)(2,1)S(1)} %bitcast.121), kind=kOutput, calls=%fused_computation.3 | convolution fusion | flops 906166272 | bytes 6291456 | tf_op jit(solution)/shard_map/dot_general | solution.py:153
  94.6 1.1 %convolution_add_fusion = f32[768,256]{1,0:T(8,128)S(1)} fusion(f32[768,256]{1,0:T(8,128)S(1)} %convolution_add_fusion.1, bf16[768,2304]{1,0:T(8,128)(2,1)S(1)} %bitcast.112, bf16[2304,256]{1,0:T(8,128)(2,1)S(1)} %bitcast.120), kind=kOutput, calls=%fused_computation.2 | convolution fusion | flops 906166272 | bytes 6291456 | tf_op jit(solution)/shard_map/dot_general | solution.py:153
  95.7 0.9 add_convert_fusion
  (242 shorter events, 17.1 us)
Async XLA Ops:
  0.0 3.8 %copy-start.7 = (bf16[3,2,32,512]{3,2,1,0:T(8,128)(2,1)S(1)}, bf16[3,2,32,512]{3,2,1,0:T(8,128)(2,1)}, u32[]{:S(2)}) copy-start(bf16[3,2,32,512]{3,2,1,0:T(8,128)(2,1)} %param.10) | copy-start | bytes 589828
  1.5 2.3 %collective-permute-start = (f32[2,32]{1,0:T(2,128)S(1)}, f32[2,32]{1,0:T(2,128)S(1)}, u32[]{:S(2)}, u32[]{:S(2)}) collective-permute-start(f32[2,32]{1,0:T(2,128)S(1)} %pad_maximum_fusion.22), channel_id=1, source_target_pairs={{0,1},{1,0},{2,3},{3,2},{4,5},{5,4},{6,7},{7,6},{8,9},{9,8},{10,11... | collective-permute-start | bytes 776 | tf_op jit(solution)/shard_map/ppermute | solution.py:170
  2.0 17.4 %copy-start.13 = (f32[512]{0:T(512)S(1)}, f32[512]{0:T(512)}, u32[]{:S(2)}) copy-start(f32[512]{0:T(512)} %param.12) | copy-start | bytes 6148
  2.0 17.4 %copy-start.14 = (f32[512]{0:T(512)S(1)}, f32[512]{0:T(512)}, u32[]{:S(2)}) copy-start(f32[512]{0:T(512)} %param.11) | copy-start | bytes 6148
  4.2 4.2 %collective-permute-start.1 = (bf16[7,512]{1,0:T(8,128)(2,1)S(1)}, bf16[7,512]{1,0:T(8,128)(2,1)S(1)}, u32[]{:S(2)}, u32[]{:S(2)}) collective-permute-start(bf16[7,512]{1,0:T(8,128)(2,1)S(1)} %pad_maximum_fusion.21), channel_id=1, source_target_pairs={{0,2},{2,0},{1,3},{3,1},{4,6},{6,4},{5,7},{7,5},{8,10},{10,8},{9,1... | collective-permute-start | bytes 21512 | tf_op jit(solution)/shard_map/ppermute | solution.py:170
  9.1 5.3 %collective-permute-start.2 = (bf16[100,512]{1,0:T(8,128)(2,1)S(1)}, bf16[100,512]{1,0:T(8,128)(2,1)S(1)}, u32[]{:S(2)}, u32[]{:S(2)}) collective-permute-start(bf16[100,512]{1,0:T(8,128)(2,1)S(1)} %pad_maximum_fusion.16), channel_id=1, source_target_pairs={{0,4},{4,0},{8,12},{12,8},{1,5},{5,1},{9,13},{13,9},{2,6},{6,2},{1... | collective-permute-start | bytes 307208 | tf_op jit(solution)/shard_map/ppermute | solution.py:170
  11.8 6.9 %collective-permute-start.3 = (bf16[100,512]{1,0:T(8,128)(2,1)S(1)}, bf16[100,512]{1,0:T(8,128)(2,1)S(1)}, u32[]{:S(2)}, u32[]{:S(2)}) collective-permute-start(bf16[100,512]{1,0:T(8,128)(2,1)S(1)} %pad_maximum_fusion.16), channel_id=1, source_target_pairs={{0,12},{4,8},{8,4},{12,0},{1,13},{5,9},{9,5},{13,1},{2,14},{6,10},... | collective-permute-start | bytes 307208 | tf_op jit(solution)/shard_map/ppermute | solution.py:170
  14.3 4.7 %collective-permute-start.4 = (f32[2,32]{1,0:T(2,128)S(1)}, f32[2,32]{1,0:T(2,128)S(1)}, u32[]{:S(2)}, u32[]{:S(2)}) collective-permute-start(f32[2,32]{1,0:T(2,128)S(1)} %get-tuple-element.27), channel_id=1, source_target_pairs={{0,8},{4,12},{8,0},{12,4},{1,9},{5,13},{9,1},{13,5},{2,10},{6,14},... | collective-permute-start | bytes 776 | tf_op jit(solution)/shard_map/ppermute | solution.py:170
  21.2 9.6 %copy-start = (bf16[3,3,3,256,256]{4,3,2,1,0:T(8,128)(2,1)S(1)}, bf16[3,3,3,256,256]{4,3,2,1,0:T(8,128)(2,1)}, u32[]{:S(2)}) copy-start(bf16[3,3,3,256,256]{4,3,2,1,0:T(8,128)(2,1)} %param.16) | copy-start | bytes 10616836
  24.6 0.7 copy-start.1
  30.7 2.0 %copy-start.2 = (bf16[3,2,2,64,256]{4,1,3,0,2:T(2,128)(2,1)S(1)}, bf16[3,2,2,64,256]{4,1,3,0,2:T(2,128)(2,1)}, u32[]{:S(2)}) copy-start(bf16[3,2,2,64,256]{4,1,3,0,2:T(2,128)(2,1)} %copy-done.1) | copy-start | bytes 1179652
  30.7 2.1 %collective-permute-start.5 = (bf16[513,256]{1,0:T(8,128)(2,1)S(1)}, bf16[513,256]{1,0:T(8,128)(2,1)S(1)}, u32[]{:S(2)}, u32[]{:S(2)}) collective-permute-start(bf16[513,256]{1,0:T(8,128)(2,1)S(1)} %pad_maximum_fusion.2), channel_id=1, source_target_pairs={{0,1},{1,0},{2,3},{3,2},{4,5},{5,4},{6,7},{7,6},{8,9},{9,8},{10,11... | collective-permute-start | bytes 787976 | tf_op jit(solution)/shard_map/ppermute | solution.py:170
  32.6 1.9 %copy-start.11 = (f32[32]{0:T(128)S(1)}, f32[32]{0:T(128)}, u32[]{:S(2)}) copy-start(f32[32]{0:T(128)} %reduce_sum.83) | copy-start | bytes 388
  32.6 1.9 %copy-start.12 = (f32[32]{0:T(128)S(1)}, f32[32]{0:T(128)}, u32[]{:S(2)}) copy-start(f32[32]{0:T(128)} %reduce_sum.89) | copy-start | bytes 388
  32.8 0.7 copy-start.8
  32.8 7.6 %copy-start.19 = (pred[6]{0:T(512)(128)(4,1)S(1)}, pred[6]{0:T(512)(128)(4,1)}, u32[]{:S(2)}) copy-start(pred[6]{0:T(512)(128)(4,1)} %or_and_fusion.1) | copy-start | bytes 22
  34.8 3.8 %collective-permute-start.6 = (bf16[21,256]{1,0:T(8,128)(2,1)S(1)}, bf16[21,256]{1,0:T(8,128)(2,1)S(1)}, u32[]{:S(2)}, u32[]{:S(2)}) collective-permute-start(bf16[21,256]{1,0:T(8,128)(2,1)S(1)} %pad_maximum_fusion.19), channel_id=1, source_target_pairs={{0,2},{2,0},{1,3},{3,1},{4,6},{6,4},{5,7},{7,5},{8,10},{10,8},{9,1... | collective-permute-start | bytes 32264 | tf_op jit(solution)/shard_map/ppermute | solution.py:170
  38.6 12.5 %copy-start.15 = (f32[256]{0:T(256)S(1)}, f32[256]{0:T(256)}, u32[]{:S(2)}) copy-start(f32[256]{0:T(256)} %param.15) | copy-start | bytes 3076
  38.6 12.5 %copy-start.16 = (f32[256]{0:T(256)S(1)}, f32[256]{0:T(256)}, u32[]{:S(2)}) copy-start(f32[256]{0:T(256)} %param.14) | copy-start | bytes 3076
  39.5 5.7 %collective-permute-start.7 = (bf16[331,256]{1,0:T(8,128)(2,1)S(1)}, bf16[331,256]{1,0:T(8,128)(2,1)S(1)}, u32[]{:S(2)}, u32[]{:S(2)}) collective-permute-start(bf16[331,256]{1,0:T(8,128)(2,1)S(1)} %get-tuple-element.67), channel_id=1, source_target_pairs={{0,4},{4,0},{8,12},{12,8},{1,5},{5,1},{9,13},{13,9},{2,6},{6,2},{1... | collective-permute-start | bytes 508424 | tf_op jit(solution)/shard_map/ppermute | solution.py:170
  40.5 10.1 %collective-permute-start.9 = (f32[2,32]{1,0:T(2,128)S(1)}, f32[2,32]{1,0:T(2,128)S(1)}, u32[]{:S(2)}, u32[]{:S(2)}) collective-permute-start(f32[2,32]{1,0:T(2,128)S(1)} %get-tuple-element.22), channel_id=1, source_target_pairs={{0,8},{4,12},{8,0},{12,4},{1,9},{5,13},{9,1},{13,5},{2,10},{6,14},... | collective-permute-start | bytes 776 | tf_op jit(solution)/shard_map/ppermute | solution.py:170
  42.7 7.6 %collective-permute-start.8 = (bf16[331,256]{1,0:T(8,128)(2,1)S(1)}, bf16[331,256]{1,0:T(8,128)(2,1)S(1)}, u32[]{:S(2)}, u32[]{:S(2)}) collective-permute-start(bf16[331,256]{1,0:T(8,128)(2,1)S(1)} %get-tuple-element.68), channel_id=1, source_target_pairs={{0,12},{4,8},{8,4},{12,0},{1,13},{5,9},{9,5},{13,1},{2,14},{6,10},... | collective-permute-start | bytes 508424 | tf_op jit(solution)/shard_map/ppermute | solution.py:170
  55.0 1.3 %copy-start.5 = (bf16[1,3,3,256,256]{4,3,2,1,0:T(8,128)(2,1)S(1)}, bf16[1,3,3,256,256]{4,3,2,1,0:T(8,128)(2,1)}, u32[]{:S(2)}) copy-start(bf16[1,3,3,256,256]{4,3,2,1,0:T(8,128)(2,1)} %get-tuple-element.40) | copy-start | bytes 3538948
  56.2 1.3 %copy-start.4 = (bf16[1,3,3,256,256]{4,3,2,1,0:T(8,128)(2,1)S(1)}, bf16[1,3,3,256,256]{4,3,2,1,0:T(8,128)(2,1)}, u32[]{:S(2)}) copy-start(bf16[1,3,3,256,256]{4,3,2,1,0:T(8,128)(2,1)} %get-tuple-element.41) | copy-start | bytes 3538948
  57.5 1.3 %copy-start.3 = (bf16[1,3,3,256,256]{4,3,2,1,0:T(8,128)(2,1)S(1)}, bf16[1,3,3,256,256]{4,3,2,1,0:T(8,128)(2,1)}, u32[]{:S(2)}) copy-start(bf16[1,3,3,256,256]{4,3,2,1,0:T(8,128)(2,1)} %get-tuple-element.39) | copy-start | bytes 3538948
  60.6 1.6 %collective-permute-start.10 = (bf16[513,256]{1,0:T(8,128)(2,1)S(1)}, bf16[513,256]{1,0:T(8,128)(2,1)S(1)}, u32[]{:S(2)}, u32[]{:S(2)}) collective-permute-start(bf16[513,256]{1,0:T(8,128)(2,1)S(1)} %pad_maximum_fusion.3), channel_id=1, source_target_pairs={{0,1},{1,0},{2,3},{3,2},{4,5},{5,4},{6,7},{7,6},{8,9},{9,8},{10,11... | collective-permute-start | bytes 787976 | tf_op jit(solution)/shard_map/ppermute | solution.py:170
  62.9 3.8 %collective-permute-start.11 = (bf16[21,256]{1,0:T(8,128)(2,1)S(1)}, bf16[21,256]{1,0:T(8,128)(2,1)S(1)}, u32[]{:S(2)}, u32[]{:S(2)}) collective-permute-start(bf16[21,256]{1,0:T(8,128)(2,1)S(1)} %pad_maximum_fusion.20), channel_id=1, source_target_pairs={{0,2},{2,0},{1,3},{3,1},{4,6},{6,4},{5,7},{7,5},{8,10},{10,8},{9,1... | collective-permute-start | bytes 32264 | tf_op jit(solution)/shard_map/ppermute | solution.py:170
  67.5 19.0 %copy-start.17 = (f32[256]{0:T(256)S(1)}, f32[256]{0:T(256)}, u32[]{:S(2)}) copy-start(f32[256]{0:T(256)} %param.18) | copy-start | bytes 3076
  67.5 19.0 %copy-start.18 = (f32[256]{0:T(256)S(1)}, f32[256]{0:T(256)}, u32[]{:S(2)}) copy-start(f32[256]{0:T(256)} %param.17) | copy-start | bytes 3076
  67.6 7.8 %collective-permute-start.12 = (bf16[331,256]{1,0:T(8,128)(2,1)S(1)}, bf16[331,256]{1,0:T(8,128)(2,1)S(1)}, u32[]{:S(2)}, u32[]{:S(2)}) collective-permute-start(bf16[331,256]{1,0:T(8,128)(2,1)S(1)} %get-tuple-element.61), channel_id=1, source_target_pairs={{0,4},{4,0},{8,12},{12,8},{1,5},{5,1},{9,13},{13,9},{2,6},{6,2},{1... | collective-permute-start | bytes 508424 | tf_op jit(solution)/shard_map/ppermute | solution.py:170
  72.9 8.2 %collective-permute-start.14 = (f32[2,32]{1,0:T(2,128)S(1)}, f32[2,32]{1,0:T(2,128)S(1)}, u32[]{:S(2)}, u32[]{:S(2)}) collective-permute-start(f32[2,32]{1,0:T(2,128)S(1)} %get-tuple-element.15), channel_id=1, source_target_pairs={{0,8},{4,12},{8,0},{12,4},{1,9},{5,13},{9,1},{13,5},{2,10},{6,14},... | collective-permute-start | bytes 776 | tf_op jit(solution)/shard_map/ppermute | solution.py:170
  72.9 7.3 %collective-permute-start.13 = (bf16[331,256]{1,0:T(8,128)(2,1)S(1)}, bf16[331,256]{1,0:T(8,128)(2,1)S(1)}, u32[]{:S(2)}, u32[]{:S(2)}) collective-permute-start(bf16[331,256]{1,0:T(8,128)(2,1)S(1)} %get-tuple-element.62), channel_id=1, source_target_pairs={{0,12},{4,8},{8,4},{12,0},{1,13},{5,9},{9,5},{13,1},{2,14},{6,10},... | collective-permute-start | bytes 508424 | tf_op jit(solution)/shard_map/ppermute | solution.py:170
  75.3 0.7 copy-start.9
  80.2 0.7 copy-start.10
  91.2 1.3 %copy-start.6 = (bf16[1,3,3,256,256]{4,3,2,1,0:T(8,128)(2,1)S(1)}, bf16[1,3,3,256,256]{4,3,2,1,0:T(8,128)(2,1)}, u32[]{:S(2)}) copy-start(bf16[1,3,3,256,256]{4,3,2,1,0:T(8,128)(2,1)} %get-tuple-element.37) | copy-start | bytes 3538948

commit v6 on v5

--- a/solution.py
+++ b/solution.py
@@ -194,12 +194,18 @@
     return jnp.repeat(average, group_width), jnp.repeat(scaling, group_width)
 
 
+def split_high(value):
+    scaled = value * 65537.0
+    return scaled - (scaled - value)
+
+
 def pack_sums(sums, width):
-    high = sums.astype(jnp.bfloat16)
-    rest = sums - high.astype(jnp.float32)
-    middle = rest.astype(jnp.bfloat16)
-    low = (rest - middle.astype(jnp.float32)).astype(jnp.bfloat16)
+    high = split_high(sums)
+    rest = sums - high
+    middle = split_high(rest)
+    low = rest - middle
     flat = jnp.concatenate([high.reshape(-1), middle.reshape(-1), low.reshape(-1)])
+    flat = flat.astype(jnp.bfloat16)
     rows = -(-flat.size // width)
     return jnp.pad(flat, (0, rows * width - flat.size)).reshape(rows, width)
 

time: 97.1 us -> 97.2 us (level)
  no operation moved by 1% of the time
where the time goes in v6:
time: 97.2 us; the launch traced here: 96.7 us
  local copies, waits for them, and re-layouts  26.6 us (27%)
  waiting for transfers between devices  22.1 us (23%)
  starting transfers between devices  20.1 us (21%)
  other arithmetic  18.3 us (19%)
  matrix products  8.74 us (9%)
    ppermute x15, waiting for transfers between devices, swap(): return lax.ppermute(x, axis, [(i, i ^ distance) for i in range(size)])  22.1 us
    ppermute x15, starting transfers between devices, swap(): return lax.ppermute(x, axis, [(i, i ^ distance) for i in range(size)])  20.1 us
    dot_general x6, matrix products, valid_conv(): jnp.dot(window, kernel[step_t].reshape(9 * channels, -1), preferred_eleme...  6.52 us
    unnamed x57, local copies, waits for them, and re-layouts  6.36 us
    slice x2, local copies, waits for them, and re-layouts, valid_conv(): kernel[step_t].reshape(9 * channels, -1)  5.11 us
    convert_element_type x2, other arithmetic, norm_conv(): jnp.where(inside_mask(height + 2, across + 2, 1), act, 0.0)  4.99 us
    reduce_sum x5, other arithmetic, local_sums(): jnp.sum(grouped, axis=(0, 2))  3.32 us
    dot_general x4, matrix products, upsample(): dot = lambda v, w: jnp.dot(flat(v), w, preferred_element_type=jnp.float32)  2.22 us
  transfers between devices with their start and end apart: 15, of which 8 were waited for; matrix products, arithmetic and copies ran while one was open for 9% of the time, Pallas kernels for 0%

profile of v6, /device:TPU:0, one launch (start us, length us, event | category | flops | bytes accessed | tf_op | source)
XLA Modules:
  0.0 96.7 jit_solution(9139209012364739482)
XLA Ops:
  0.0 1.1 %convert_reduce_fusion.2 = (f32[512]{0:T(512)S(1)}, f32[512]{0:T(512)S(1)}) fusion(bf16[3,2,32,512]{3,2,1,0:T(8,128)(2,1)} %param.10), kind=kLoop, calls=%fused_computation.52 | loop fusion | flops 392192 | bytes 200704 | tf_op jit(solution)/shard_map/reduce_sum | solution.py:179
  2.0 1.6 %slice_bitcast_fusion.7 = (bf16[512,256]{1,0:T(8,128)(2,1)S(1)}, bf16[512,256]{1,0:T(8,128)(2,1)S(1)}, bf16[512,256]{1,0:T(8,128)(2,1)S(1)}, bf16[512,256]{1,0:T...) fusion(bf16[3,3,512,256]{3,2,1,0:T(8,128)(2,1)} %param.13), kind=kLoop, calls=%fused_computation.69 | loop fusion | bytes 4194304 | tf_op jit(solution)/shard_map/squeeze | solution.py:129
  4.2 2.6 %collective-permute-start.1 = (bf16[7,512]{1,0:T(8,128)(2,1)S(1)}, bf16[7,512]{1,0:T(8,128)(2,1)S(1)}, u32[]{:S(2)}, u32[]{:S(2)}) collective-permute-start(bf16[7,512]{1,0:T(8,128)(2,1)S(1)} %pad_maximum_fusion.21), channel_id=1, source_target_pairs={{0,2},{2,0},{1,3},{3,1},{4,6},{6,4},{5,7},{7,5},{8,10},{10,8},{9,1... | collective-permute-start | bytes 21512 | tf_op jit(solution)/shard_map/ppermute | solution.py:170
  6.9 1.6 %collective-permute-done.1 = bf16[7,512]{1,0:T(8,128)(2,1)S(1)} collective-permute-done((bf16[7,512]{1,0:T(8,128)(2,1)S(1)}, bf16[7,512]{1,0:T(8,128)(2,1)S(1)}, u32[]{:S(2)}, u32[]{:S(2)}) %collective-permute-start.1) | collective-permute-done | bytes 7200 | tf_op jit(solution)/shard_map/ppermute | solution.py:170
  9.1 2.2 %collective-permute-start.2 = (bf16[100,512]{1,0:T(8,128)(2,1)S(1)}, bf16[100,512]{1,0:T(8,128)(2,1)S(1)}, u32[]{:S(2)}, u32[]{:S(2)}) collective-permute-start(bf16[100,512]{1,0:T(8,128)(2,1)S(1)} %pad_maximum_fusion.16), channel_id=1, source_target_pairs={{0,4},{4,0},{8,12},{12,8},{1,5},{5,1},{9,13},{13,9},{2,6},{6,2},{1... | collective-permute-start | bytes 307208 | tf_op jit(solution)/shard_map/ppermute | solution.py:170
  11.8 2.5 %collective-permute-start.3 = (bf16[100,512]{1,0:T(8,128)(2,1)S(1)}, bf16[100,512]{1,0:T(8,128)(2,1)S(1)}, u32[]{:S(2)}, u32[]{:S(2)}) collective-permute-start(bf16[100,512]{1,0:T(8,128)(2,1)S(1)} %pad_maximum_fusion.16), channel_id=1, source_target_pairs={{0,12},{4,8},{8,4},{12,0},{1,13},{5,9},{9,5},{13,1},{2,14},{6,10},... | collective-permute-start | bytes 307208 | tf_op jit(solution)/shard_map/ppermute | solution.py:170
  14.5 4.2 %collective-permute-done.3 = bf16[100,512]{1,0:T(8,128)(2,1)S(1)} collective-permute-done((bf16[100,512]{1,0:T(8,128)(2,1)S(1)}, bf16[100,512]{1,0:T(8,128)(2,1)S(1)}, u32[]{:S(2)}, u32[]{:S(2)}) %collective-permute-start.3) | collective-permute-done | bytes 102432 | tf_op jit(solution)/shard_map/ppermute | solution.py:170
  21.2 1.3 %convolution_add_fusion.4 = bf16[192,256]{1,0:T(8,128)(2,1)S(1)} fusion(bf16[192,512]{1,0:T(8,128)(2,1)S(1)} %bitcast.126, bf16[3,3,512,256]{3,2,1,0:T(8,128)(2,1)} %param.13, f32[192,512]{1,0:T(8,128)S(1)} %fusion.15, f32[192,512]{1,0:T(8,128)S(1)} %fusion.11, f32[192,1024]{1,0:T(8,128)S(1)} %fusion.1), kind=kOutput, calls=%fused_computation.7 | convolution fusion | flops 50528256 | bytes 1146880 | tf_op jit(solution)/shard_map/dot_general | solution.py:123
  23.2 1.4 %convert_reduce_fusion.1 = (f32[256]{0:T(256)}, f32[256]{0:T(256)}, bf16[3,2,2,64,256]{4,1,3,0,2:T(2,128)(2,1)S(1)}) fusion(bf16[3,2,1,64,256]{4,1,3,0,2:T(2,128)(2,1)S(1)} %bitcast.129, bf16[3,2,1,64,256]{4,1,3,0,2:T(2,128)(2,1)S(1)} %bitcast.128), kind=kLoop, calls=%fused_computation.19 | loop fusion | flops 982528 | bytes 788480 | tf_op jit(solution)/shard_map/reduce_sum | solution.py:179
  24.6 0.7 copy-done.1
  25.5 0.7 copy.27
  26.2 0.7 reduce_sum.82
  27.0 0.6 reduce_sum.83
  27.6 0.7 reduce_sum.85
  29.7 1.0 %pad_maximum_fusion.2 = bf16[513,256]{1,0:T(8,128)(2,1)S(1)} fusion(bf16[1,256]{1,0:T(2,128)(2,1)S(1)} %reshape.719, bf16[512,256]{1,0:T(8,128)(2,1)} %bitcast.123), kind=kLoop, calls=%fused_computation.56 | loop fusion | flops 525312 | bytes 525312 | tf_op jit(solution)/shard_map/concatenate | solution.py:221
  30.8 1.8 %fusion.117 = (bf16[1,3,3,256,256]{4,3,2,1,0:T(8,128)(2,1)}, bf16[1,3,3,256,256]{4,3,2,1,0:T(8,128)(2,1)}, bf16[1,3,3,256,256]{4,3,2,1,0:T(8,128)(2,1)}) fusion(bf16[3,3,3,256,256]{4,3,2,1,0:T(8,128)(2,1)S(1)} %copy-done), kind=kLoop, calls=%fused_computation.275 | loop fusion | bytes 7077888 | tf_op jit(solution)/shard_map/slice | solution.py:154
  32.9 0.6 copy-done.8
  33.6 0.7 slice_convert_fusion.7
  34.9 1.5 %collective-permute-start.6 = (bf16[21,256]{1,0:T(8,128)(2,1)S(1)}, bf16[21,256]{1,0:T(8,128)(2,1)S(1)}, u32[]{:S(2)}, u32[]{:S(2)}) collective-permute-start(bf16[21,256]{1,0:T(8,128)(2,1)S(1)} %pad_maximum_fusion.19), channel_id=1, source_target_pairs={{0,2},{2,0},{1,3},{3,1},{4,6},{6,4},{5,7},{7,5},{8,10},{10,8},{9,1... | collective-permute-start | bytes 32264 | tf_op jit(solution)/shard_map/ppermute | solution.py:170
  36.4 2.2 %collective-permute-done.6 = bf16[21,256]{1,0:T(8,128)(2,1)S(1)} collective-permute-done((bf16[21,256]{1,0:T(8,128)(2,1)S(1)}, bf16[21,256]{1,0:T(8,128)(2,1)S(1)}, u32[]{:S(2)}, u32[]{:S(2)}) %collective-permute-start.6) | collective-permute-done | bytes 10784 | tf_op jit(solution)/shard_map/ppermute | solution.py:170
  39.5 0.9 collective-permute-start.7
  40.5 2.3 %collective-permute-start.9 = (f32[2,32]{1,0:T(2,128)S(1)}, f32[2,32]{1,0:T(2,128)S(1)}, u32[]{:S(2)}, u32[]{:S(2)}) collective-permute-start(f32[2,32]{1,0:T(2,128)S(1)} %get-tuple-element.22), channel_id=1, source_target_pairs={{0,8},{4,12},{8,0},{12,4},{1,9},{5,13},{9,1},{13,5},{2,10},{6,14},... | collective-permute-start | bytes 776 | tf_op jit(solution)/shard_map/ppermute | solution.py:170
  42.8 1.3 %collective-permute-start.8 = (bf16[331,256]{1,0:T(8,128)(2,1)S(1)}, bf16[331,256]{1,0:T(8,128)(2,1)S(1)}, u32[]{:S(2)}, u32[]{:S(2)}) collective-permute-start(bf16[331,256]{1,0:T(8,128)(2,1)S(1)} %get-tuple-element.68), channel_id=1, source_target_pairs={{0,12},{4,8},{8,4},{12,0},{1,13},{5,9},{9,5},{13,1},{2,14},{6,10},... | collective-permute-start | bytes 508424 | tf_op jit(solution)/shard_map/ppermute | solution.py:170
  44.1 1.2 %collective-permute-done.7 = bf16[331,256]{1,0:T(8,128)(2,1)S(1)} collective-permute-done((bf16[331,256]{1,0:T(8,128)(2,1)S(1)}, bf16[331,256]{1,0:T(8,128)(2,1)S(1)}, u32[]{:S(2)}, u32[]{:S(2)}) %collective-permute-start.7) | collective-permute-done | bytes 169504 | tf_op jit(solution)/shard_map/ppermute | solution.py:170
  45.3 5.0 %collective-permute-done.8 = bf16[331,256]{1,0:T(8,128)(2,1)S(1)} collective-permute-done((bf16[331,256]{1,0:T(8,128)(2,1)S(1)}, bf16[331,256]{1,0:T(8,128)(2,1)S(1)}, u32[]{:S(2)}, u32[]{:S(2)}) %collective-permute-start.8) | collective-permute-done | bytes 169504 | tf_op jit(solution)/shard_map/ppermute | solution.py:170
  51.1 2.1 %select_convert_fusion.1 = bf16[5,6,66,256]{3,2,1,0:T(8,128)(2,1)S(1)} fusion(bf16[5,1,66,256]{3,2,1,0:T(8,128)(2,1)S(1)} %select_n.183, bf16[5,4,1,256]{3,2,1,0:T(2,128)(2,1)S(1)} %reshape.755, bf16[3,4,64,256]{3,2,1,0:T(8,128)(2,1)S(1)} %bitcast.106, bf16[2,4,64,256]{3,2,1,0:T(8,128)(2,1)S(1)} %maximum_select_fusion, ...), kind=kLoop, calls=%fused_computation.1 | loop fusion | flops 11151360 | bytes 2021772 | tf_op jit(solution)/shard_map/convert_element_type | solution.py:275
  55.0 1.0 %fusion.115 = (bf16[3,4,64,2304]{3,2,1,0:T(8,128)(2,1)S(1)}, bf16[3,4,64,2304]{3,2,1,0:T(8,128)(2,1)S(1)}, bf16[3,4,64,2304]{3,2,1,0:T(8,128)(2,1)S(1)}) fusion(bf16[5,4,64,2304]{3,2,1,0:T(8,128)(2,1)S(1)} %slice_dynamic-update-slice_fusion.9), kind=kLoop, calls=%fused_computation.273 | loop fusion | bytes 21233664 | tf_op jit(solution)/shard_map/slice | solution.py:152
  56.3 1.1 %fusion.120 = f32[768,256]{1,0:T(8,128)S(1)} fusion(bf16[768,2304]{1,0:T(8,128)(2,1)S(1)} %bitcast.115, bf16[2304,256]{1,0:T(8,128)(2,1)S(1)} %bitcast.119), kind=kOutput, calls=%fused_computation.278 | convolution fusion | flops 905969664 | bytes 5505024 | tf_op jit(solution)/shard_map/dot_general | solution.py:153
  57.5 1.1 %convolution_add_fusion.3 = f32[768,256]{1,0:T(8,128)S(1)} fusion(f32[768,256]{1,0:T(8,128)S(1)} %fusion.120, bf16[768,2304]{1,0:T(8,128)(2,1)S(1)} %bitcast.113, bf16[2304,256]{1,0:T(8,128)(2,1)S(1)} %bitcast.118), kind=kOutput, calls=%fused_computation.5 | convolution fusion | flops 906166272 | bytes 6291456 | tf_op jit(solution)/shard_map/dot_general | solution.py:153
  58.8 1.1 %convert_reduce_fusion = (f32[256]{0:T(256)S(1)}, f32[256]{0:T(256)S(1)}, bf16[768,256]{1,0:T(8,128)(2,1)S(1)}) fusion(f32[768,256]{1,0:T(8,128)S(1)} %convolution_add_fusion.3, bf16[768,2304]{1,0:T(8,128)(2,1)S(1)} %bitcast.111, bf16[2304,256]{1,0:T(8,128)(2,1)S(1)} %bitcast.117), kind=kOutput, calls=%fused_computation.17 | convolution fusion | flops 907148800 | bytes 5900288 | tf_op jit(solution)/shard_map/dot_general | solution.py:153
  60.7 1.5 %collective-permute-done.10 = bf16[513,256]{1,0:T(8,128)(2,1)S(1)} collective-permute-done((bf16[513,256]{1,0:T(8,128)(2,1)S(1)}, bf16[513,256]{1,0:T(8,128)(2,1)S(1)}, u32[]{:S(2)}, u32[]{:S(2)}) %collective-permute-start.10) | collective-permute-done | bytes 262688 | tf_op jit(solution)/shard_map/ppermute | solution.py:170
  62.9 1.5 %collective-permute-start.11 = (bf16[21,256]{1,0:T(8,128)(2,1)S(1)}, bf16[21,256]{1,0:T(8,128)(2,1)S(1)}, u32[]{:S(2)}, u32[]{:S(2)}) collective-permute-start(bf16[21,256]{1,0:T(8,128)(2,1)S(1)} %pad_maximum_fusion.20), channel_id=1, source_target_pairs={{0,2},{2,0},{1,3},{3,1},{4,6},{6,4},{5,7},{7,5},{8,10},{10,8},{9,1... | collective-permute-start | bytes 32264 | tf_op jit(solution)/shard_map/ppermute | solution.py:170
  64.5 2.2 %collective-permute-done.11 = bf16[21,256]{1,0:T(8,128)(2,1)S(1)} collective-permute-done((bf16[21,256]{1,0:T(8,128)(2,1)S(1)}, bf16[21,256]{1,0:T(8,128)(2,1)S(1)}, u32[]{:S(2)}, u32[]{:S(2)}) %collective-permute-start.11) | collective-permute-done | bytes 10784 | tf_op jit(solution)/shard_map/ppermute | solution.py:170
  67.6 2.1 %collective-permute-start.12 = (bf16[331,256]{1,0:T(8,128)(2,1)S(1)}, bf16[331,256]{1,0:T(8,128)(2,1)S(1)}, u32[]{:S(2)}, u32[]{:S(2)}) collective-permute-start(bf16[331,256]{1,0:T(8,128)(2,1)S(1)} %get-tuple-element.61), channel_id=1, source_target_pairs={{0,4},{4,0},{8,12},{12,8},{1,5},{5,1},{9,13},{13,9},{2,6},{6,2},{1... | collective-permute-start | bytes 508424 | tf_op jit(solution)/shard_map/ppermute | solution.py:170
  69.7 3.3 %fusion.116 = (bf16[1,3,3,256,256]{4,3,2,1,0:T(8,128)(2,1)S(1)}, bf16[1,3,3,256,256]{4,3,2,1,0:T(8,128)(2,1)}, bf16[1,3,3,256,256]{4,3,2,1,0:T(8,128)(2,1)S(1)}) fusion(bf16[3,3,3,256,256]{4,3,2,1,0:T(8,128)(2,1)} %param.19), kind=kLoop, calls=%fused_computation.274 | loop fusion | bytes 7077888 | tf_op jit(solution)/shard_map/slice | solution.py:154
  73.0 2.4 %collective-permute-start.13 = (bf16[331,256]{1,0:T(8,128)(2,1)S(1)}, bf16[331,256]{1,0:T(8,128)(2,1)S(1)}, u32[]{:S(2)}, u32[]{:S(2)}) collective-permute-start(bf16[331,256]{1,0:T(8,128)(2,1)S(1)} %get-tuple-element.62), channel_id=1, source_target_pairs={{0,12},{4,8},{8,4},{12,0},{1,13},{5,9},{9,5},{13,1},{2,14},{6,10},... | collective-permute-start | bytes 508424 | tf_op jit(solution)/shard_map/ppermute | solution.py:170
  75.4 0.7 copy-done.9
  76.1 4.1 %collective-permute-done.13 = bf16[331,256]{1,0:T(8,128)(2,1)S(1)} collective-permute-done((bf16[331,256]{1,0:T(8,128)(2,1)S(1)}, bf16[331,256]{1,0:T(8,128)(2,1)S(1)}, u32[]{:S(2)}, u32[]{:S(2)}) %collective-permute-start.13) | collective-permute-done | bytes 169504 | tf_op jit(solution)/shard_map/ppermute | solution.py:170
  80.2 0.7 copy-done.10
  81.5 1.8 %broadcast_select_fusion.6 = (bf16[330,256]{1,0:T(8,128)(2,1)}, bf16[330,256]{1,0:T(8,128)(2,1)}) fusion(pred[]{:T(512)S(6)} %eq.35, bf16[331,256]{1,0:T(8,128)(2,1)} %copy-done.10, bf16[331,256]{1,0:T(8,128)(2,1)} %copy-done.9, pred[]{:T(512)S(6)} %eq.34), kind=kLoop, calls=%fused_computation.92 | loop fusion | flops 168960 | bytes 675842 | tf_op jit(solution)/shard_map/jit(_where)/select_n | solution.py:235
  83.3 1.6 %select_n.190 = bf16[5,1,66,256]{3,2,1,0:T(8,128)(2,1)} reshape(bf16[330,256]{1,0:T(8,128)(2,1)} %get-tuple-element.57) | data formatting | bytes 337920 | tf_op jit(solution)/shard_map/jit(_where)/select_n | solution.py:235
  84.9 1.6 %select_n.192 = bf16[5,1,66,256]{3,2,1,0:T(8,128)(2,1)} reshape(bf16[330,256]{1,0:T(8,128)(2,1)} %get-tuple-element.58) | data formatting | bytes 337920 | tf_op jit(solution)/shard_map/jit(_where)/select_n | solution.py:236
  86.6 2.9 %select_convert_fusion = bf16[5,6,66,256]{3,2,1,0:T(8,128)(2,1)S(1)} fusion(bf16[5,1,66,256]{3,2,1,0:T(8,128)(2,1)} %select_n.192, bf16[5,4,1,256]{3,2,1,0:T(2,128)(2,1)S(1)} %reshape.756, bf16[3,4,64,256]{3,2,1,0:T(8,128)(2,1)S(1)} %bitcast.110, bf16[2,4,64,256]{3,2,1,0:T(8,128)(2,1)S(1)} %maximum_select_fusion.1, bf16[5,1,66,256]{3,2,1,0:T(8,128)(2,1)} %select_n.190, ...), kind=kLoop, calls=%fused_computation | loop fusion | flops 11151360 | bytes 2021772 | tf_op jit(solution)/shard_map/convert_element_type | solution.py:275
  91.2 1.2 %fusion.114 = (bf16[3,4,64,2304]{3,2,1,0:T(8,128)(2,1)S(1)}, bf16[3,4,64,2304]{3,2,1,0:T(8,128)(2,1)S(1)}, bf16[3,4,64,2304]{3,2,1,0:T(8,128)(2,1)S(1)}) fusion(bf16[5,4,64,2304]{3,2,1,0:T(8,128)(2,1)S(1)} %slice_dynamic-update-slice_fusion), kind=kLoop, calls=%fused_computation.272 | loop fusion | bytes 21233664 | tf_op jit(solution)/shard_map/slice | solution.py:152
  92.5 1.1 %fusion.121 = f32[768,256]{1,0:T(8,128)S(1)} fusion(bf16[768,2304]{1,0:T(8,128)(2,1)S(1)} %bitcast.116, bf16[2304,256]{1,0:T(8,128)(2,1)S(1)} %bitcast.122), kind=kOutput, calls=%fused_computation.279 | convolution fusion | flops 905969664 | bytes 5505024 | tf_op jit(solution)/shard_map/dot_general | solution.py:153
  93.6 1.1 %convolution_add_fusion.1 = f32[768,256]{1,0:T(8,128)S(1)} fusion(f32[768,256]{1,0:T(8,128)S(1)} %fusion.121, bf16[768,2304]{1,0:T(8,128)(2,1)S(1)} %bitcast.114, bf16[2304,256]{1,0:T(8,128)(2,1)S(1)} %bitcast.121), kind=kOutput, calls=%fused_computation.3 | convolution fusion | flops 906166272 | bytes 6291456 | tf_op jit(solution)/shard_map/dot_general | solution.py:153
  94.7 1.1 %convolution_add_fusion = f32[768,256]{1,0:T(8,128)S(1)} fusion(f32[768,256]{1,0:T(8,128)S(1)} %convolution_add_fusion.1, bf16[768,2304]{1,0:T(8,128)(2,1)S(1)} %bitcast.112, bf16[2304,256]{1,0:T(8,128)(2,1)S(1)} %bitcast.120), kind=kOutput, calls=%fused_computation.2 | convolution fusion | flops 906166272 | bytes 6291456 | tf_op jit(solution)/shard_map/dot_general | solution.py:153
  95.8 0.9 add_convert_fusion
  (242 shorter events, 17.1 us)
Async XLA Ops:
  0.0 3.8 %copy-start.7 = (bf16[3,2,32,512]{3,2,1,0:T(8,128)(2,1)S(1)}, bf16[3,2,32,512]{3,2,1,0:T(8,128)(2,1)}, u32[]{:S(2)}) copy-start(bf16[3,2,32,512]{3,2,1,0:T(8,128)(2,1)} %param.10) | copy-start | bytes 589828
  1.5 2.3 %collective-permute-start = (f32[2,32]{1,0:T(2,128)S(1)}, f32[2,32]{1,0:T(2,128)S(1)}, u32[]{:S(2)}, u32[]{:S(2)}) collective-permute-start(f32[2,32]{1,0:T(2,128)S(1)} %pad_maximum_fusion.22), channel_id=1, source_target_pairs={{0,1},{1,0},{2,3},{3,2},{4,5},{5,4},{6,7},{7,6},{8,9},{9,8},{10,11... | collective-permute-start | bytes 776 | tf_op jit(solution)/shard_map/ppermute | solution.py:170
  2.0 17.4 %copy-start.13 = (f32[512]{0:T(512)S(1)}, f32[512]{0:T(512)}, u32[]{:S(2)}) copy-start(f32[512]{0:T(512)} %param.12) | copy-start | bytes 6148
  2.0 17.4 %copy-start.14 = (f32[512]{0:T(512)S(1)}, f32[512]{0:T(512)}, u32[]{:S(2)}) copy-start(f32[512]{0:T(512)} %param.11) | copy-start | bytes 6148
  4.2 4.2 %collective-permute-start.1 = (bf16[7,512]{1,0:T(8,128)(2,1)S(1)}, bf16[7,512]{1,0:T(8,128)(2,1)S(1)}, u32[]{:S(2)}, u32[]{:S(2)}) collective-permute-start(bf16[7,512]{1,0:T(8,128)(2,1)S(1)} %pad_maximum_fusion.21), channel_id=1, source_target_pairs={{0,2},{2,0},{1,3},{3,1},{4,6},{6,4},{5,7},{7,5},{8,10},{10,8},{9,1... | collective-permute-start | bytes 21512 | tf_op jit(solution)/shard_map/ppermute | solution.py:170
  9.1 5.3 %collective-permute-start.2 = (bf16[100,512]{1,0:T(8,128)(2,1)S(1)}, bf16[100,512]{1,0:T(8,128)(2,1)S(1)}, u32[]{:S(2)}, u32[]{:S(2)}) collective-permute-start(bf16[100,512]{1,0:T(8,128)(2,1)S(1)} %pad_maximum_fusion.16), channel_id=1, source_target_pairs={{0,4},{4,0},{8,12},{12,8},{1,5},{5,1},{9,13},{13,9},{2,6},{6,2},{1... | collective-permute-start | bytes 307208 | tf_op jit(solution)/shard_map/ppermute | solution.py:170
  11.8 6.9 %collective-permute-start.3 = (bf16[100,512]{1,0:T(8,128)(2,1)S(1)}, bf16[100,512]{1,0:T(8,128)(2,1)S(1)}, u32[]{:S(2)}, u32[]{:S(2)}) collective-permute-start(bf16[100,512]{1,0:T(8,128)(2,1)S(1)} %pad_maximum_fusion.16), channel_id=1, source_target_pairs={{0,12},{4,8},{8,4},{12,0},{1,13},{5,9},{9,5},{13,1},{2,14},{6,10},... | collective-permute-start | bytes 307208 | tf_op jit(solution)/shard_map/ppermute | solution.py:170
  14.3 4.7 %collective-permute-start.4 = (f32[2,32]{1,0:T(2,128)S(1)}, f32[2,32]{1,0:T(2,128)S(1)}, u32[]{:S(2)}, u32[]{:S(2)}) collective-permute-start(f32[2,32]{1,0:T(2,128)S(1)} %get-tuple-element.27), channel_id=1, source_target_pairs={{0,8},{4,12},{8,0},{12,4},{1,9},{5,13},{9,1},{13,5},{2,10},{6,14},... | collective-permute-start | bytes 776 | tf_op jit(solution)/shard_map/ppermute | solution.py:170
  21.2 9.6 %copy-start = (bf16[3,3,3,256,256]{4,3,2,1,0:T(8,128)(2,1)S(1)}, bf16[3,3,3,256,256]{4,3,2,1,0:T(8,128)(2,1)}, u32[]{:S(2)}) copy-start(bf16[3,3,3,256,256]{4,3,2,1,0:T(8,128)(2,1)} %param.16) | copy-start | bytes 10616836
  24.6 0.7 copy-start.1
  30.7 2.0 %copy-start.2 = (bf16[3,2,2,64,256]{4,1,3,0,2:T(2,128)(2,1)S(1)}, bf16[3,2,2,64,256]{4,1,3,0,2:T(2,128)(2,1)}, u32[]{:S(2)}) copy-start(bf16[3,2,2,64,256]{4,1,3,0,2:T(2,128)(2,1)} %copy-done.1) | copy-start | bytes 1179652
  30.7 2.1 %collective-permute-start.5 = (bf16[513,256]{1,0:T(8,128)(2,1)S(1)}, bf16[513,256]{1,0:T(8,128)(2,1)S(1)}, u32[]{:S(2)}, u32[]{:S(2)}) collective-permute-start(bf16[513,256]{1,0:T(8,128)(2,1)S(1)} %pad_maximum_fusion.2), channel_id=1, source_target_pairs={{0,1},{1,0},{2,3},{3,2},{4,5},{5,4},{6,7},{7,6},{8,9},{9,8},{10,11... | collective-permute-start | bytes 787976 | tf_op jit(solution)/shard_map/ppermute | solution.py:170
  32.6 1.9 %copy-start.11 = (f32[32]{0:T(128)S(1)}, f32[32]{0:T(128)}, u32[]{:S(2)}) copy-start(f32[32]{0:T(128)} %reduce_sum.83) | copy-start | bytes 388
  32.6 1.9 %copy-start.12 = (f32[32]{0:T(128)S(1)}, f32[32]{0:T(128)}, u32[]{:S(2)}) copy-start(f32[32]{0:T(128)} %reduce_sum.89) | copy-start | bytes 388
  32.8 0.7 copy-start.8
  32.9 7.6 %copy-start.19 = (pred[6]{0:T(512)(128)(4,1)S(1)}, pred[6]{0:T(512)(128)(4,1)}, u32[]{:S(2)}) copy-start(pred[6]{0:T(512)(128)(4,1)} %or_and_fusion.1) | copy-start | bytes 22
  34.9 3.8 %collective-permute-start.6 = (bf16[21,256]{1,0:T(8,128)(2,1)S(1)}, bf16[21,256]{1,0:T(8,128)(2,1)S(1)}, u32[]{:S(2)}, u32[]{:S(2)}) collective-permute-start(bf16[21,256]{1,0:T(8,128)(2,1)S(1)} %pad_maximum_fusion.19), channel_id=1, source_target_pairs={{0,2},{2,0},{1,3},{3,1},{4,6},{6,4},{5,7},{7,5},{8,10},{10,8},{9,1... | collective-permute-start | bytes 32264 | tf_op jit(solution)/shard_map/ppermute | solution.py:170
  38.6 12.5 %copy-start.15 = (f32[256]{0:T(256)S(1)}, f32[256]{0:T(256)}, u32[]{:S(2)}) copy-start(f32[256]{0:T(256)} %param.15) | copy-start | bytes 3076
  38.7 12.5 %copy-start.16 = (f32[256]{0:T(256)S(1)}, f32[256]{0:T(256)}, u32[]{:S(2)}) copy-start(f32[256]{0:T(256)} %param.14) | copy-start | bytes 3076
  39.5 5.7 %collective-permute-start.7 = (bf16[331,256]{1,0:T(8,128)(2,1)S(1)}, bf16[331,256]{1,0:T(8,128)(2,1)S(1)}, u32[]{:S(2)}, u32[]{:S(2)}) collective-permute-start(bf16[331,256]{1,0:T(8,128)(2,1)S(1)} %get-tuple-element.67), channel_id=1, source_target_pairs={{0,4},{4,0},{8,12},{12,8},{1,5},{5,1},{9,13},{13,9},{2,6},{6,2},{1... | collective-permute-start | bytes 508424 | tf_op jit(solution)/shard_map/ppermute | solution.py:170
  40.5 10.1 %collective-permute-start.9 = (f32[2,32]{1,0:T(2,128)S(1)}, f32[2,32]{1,0:T(2,128)S(1)}, u32[]{:S(2)}, u32[]{:S(2)}) collective-permute-start(f32[2,32]{1,0:T(2,128)S(1)} %get-tuple-element.22), channel_id=1, source_target_pairs={{0,8},{4,12},{8,0},{12,4},{1,9},{5,13},{9,1},{13,5},{2,10},{6,14},... | collective-permute-start | bytes 776 | tf_op jit(solution)/shard_map/ppermute | solution.py:170
  42.8 7.6 %collective-permute-start.8 = (bf16[331,256]{1,0:T(8,128)(2,1)S(1)}, bf16[331,256]{1,0:T(8,128)(2,1)S(1)}, u32[]{:S(2)}, u32[]{:S(2)}) collective-permute-start(bf16[331,256]{1,0:T(8,128)(2,1)S(1)} %get-tuple-element.68), channel_id=1, source_target_pairs={{0,12},{4,8},{8,4},{12,0},{1,13},{5,9},{9,5},{13,1},{2,14},{6,10},... | collective-permute-start | bytes 508424 | tf_op jit(solution)/shard_map/ppermute | solution.py:170
  55.0 1.3 %copy-start.5 = (bf16[1,3,3,256,256]{4,3,2,1,0:T(8,128)(2,1)S(1)}, bf16[1,3,3,256,256]{4,3,2,1,0:T(8,128)(2,1)}, u32[]{:S(2)}) copy-start(bf16[1,3,3,256,256]{4,3,2,1,0:T(8,128)(2,1)} %get-tuple-element.40) | copy-start | bytes 3538948
  56.3 1.3 %copy-start.4 = (bf16[1,3,3,256,256]{4,3,2,1,0:T(8,128)(2,1)S(1)}, bf16[1,3,3,256,256]{4,3,2,1,0:T(8,128)(2,1)}, u32[]{:S(2)}) copy-start(bf16[1,3,3,256,256]{4,3,2,1,0:T(8,128)(2,1)} %get-tuple-element.41) | copy-start | bytes 3538948
  57.5 1.3 %copy-start.3 = (bf16[1,3,3,256,256]{4,3,2,1,0:T(8,128)(2,1)S(1)}, bf16[1,3,3,256,256]{4,3,2,1,0:T(8,128)(2,1)}, u32[]{:S(2)}) copy-start(bf16[1,3,3,256,256]{4,3,2,1,0:T(8,128)(2,1)} %get-tuple-element.39) | copy-start | bytes 3538948
  60.6 1.6 %collective-permute-start.10 = (bf16[513,256]{1,0:T(8,128)(2,1)S(1)}, bf16[513,256]{1,0:T(8,128)(2,1)S(1)}, u32[]{:S(2)}, u32[]{:S(2)}) collective-permute-start(bf16[513,256]{1,0:T(8,128)(2,1)S(1)} %pad_maximum_fusion.3), channel_id=1, source_target_pairs={{0,1},{1,0},{2,3},{3,2},{4,5},{5,4},{6,7},{7,6},{8,9},{9,8},{10,11... | collective-permute-start | bytes 787976 | tf_op jit(solution)/shard_map/ppermute | solution.py:170
  62.9 3.8 %collective-permute-start.11 = (bf16[21,256]{1,0:T(8,128)(2,1)S(1)}, bf16[21,256]{1,0:T(8,128)(2,1)S(1)}, u32[]{:S(2)}, u32[]{:S(2)}) collective-permute-start(bf16[21,256]{1,0:T(8,128)(2,1)S(1)} %pad_maximum_fusion.20), channel_id=1, source_target_pairs={{0,2},{2,0},{1,3},{3,1},{4,6},{6,4},{5,7},{7,5},{8,10},{10,8},{9,1... | collective-permute-start | bytes 32264 | tf_op jit(solution)/shard_map/ppermute | solution.py:170
  67.6 19.0 %copy-start.17 = (f32[256]{0:T(256)S(1)}, f32[256]{0:T(256)}, u32[]{:S(2)}) copy-start(f32[256]{0:T(256)} %param.18) | copy-start | bytes 3076
  67.6 19.0 %copy-start.18 = (f32[256]{0:T(256)S(1)}, f32[256]{0:T(256)}, u32[]{:S(2)}) copy-start(f32[256]{0:T(256)} %param.17) | copy-start | bytes 3076
  67.6 7.8 %collective-permute-start.12 = (bf16[331,256]{1,0:T(8,128)(2,1)S(1)}, bf16[331,256]{1,0:T(8,128)(2,1)S(1)}, u32[]{:S(2)}, u32[]{:S(2)}) collective-permute-start(bf16[331,256]{1,0:T(8,128)(2,1)S(1)} %get-tuple-element.61), channel_id=1, source_target_pairs={{0,4},{4,0},{8,12},{12,8},{1,5},{5,1},{9,13},{13,9},{2,6},{6,2},{1... | collective-permute-start | bytes 508424 | tf_op jit(solution)/shard_map/ppermute | solution.py:170
  73.0 8.2 %collective-permute-start.14 = (f32[2,32]{1,0:T(2,128)S(1)}, f32[2,32]{1,0:T(2,128)S(1)}, u32[]{:S(2)}, u32[]{:S(2)}) collective-permute-start(f32[2,32]{1,0:T(2,128)S(1)} %get-tuple-element.15), channel_id=1, source_target_pairs={{0,8},{4,12},{8,0},{12,4},{1,9},{5,13},{9,1},{13,5},{2,10},{6,14},... | collective-permute-start | bytes 776 | tf_op jit(solution)/shard_map/ppermute | solution.py:170
  73.0 7.3 %collective-permute-start.13 = (bf16[331,256]{1,0:T(8,128)(2,1)S(1)}, bf16[331,256]{1,0:T(8,128)(2,1)S(1)}, u32[]{:S(2)}, u32[]{:S(2)}) collective-permute-start(bf16[331,256]{1,0:T(8,128)(2,1)S(1)} %get-tuple-element.62), channel_id=1, source_target_pairs={{0,12},{4,8},{8,4},{12,0},{1,13},{5,9},{9,5},{13,1},{2,14},{6,10},... | collective-permute-start | bytes 508424 | tf_op jit(solution)/shard_map/ppermute | solution.py:170
  75.4 0.7 copy-start.9
  80.2 0.7 copy-start.10
  91.2 1.3 %copy-start.6 = (bf16[1,3,3,256,256]{4,3,2,1,0:T(8,128)(2,1)S(1)}, bf16[1,3,3,256,256]{4,3,2,1,0:T(8,128)(2,1)}, u32[]{:S(2)}) copy-start(bf16[1,3,3,256,256]{4,3,2,1,0:T(8,128)(2,1)} %get-tuple-element.37) | copy-start | bytes 3538948

commit v7 on v6

--- a/solution.py
+++ b/solution.py
@@ -175,8 +175,10 @@
 
 
 def local_sums(values):
-    grouped = values.reshape(-1, GROUPS, values.shape[-1] // GROUPS)
-    return jnp.stack([jnp.sum(grouped, axis=(0, 2)), jnp.sum(grouped * grouped, axis=(0, 2))])
+    channels = values.shape[-1]
+    flat = values.reshape(-1, channels)
+    per_channel = jnp.stack([jnp.sum(flat, axis=0), jnp.sum(flat * flat, axis=0)])
+    return jnp.sum(per_channel.reshape(2, GROUPS, channels // GROUPS), axis=2)
 
 
 def finish_stats(sums, values):
@@ -226,14 +228,20 @@
 
 def ha_round(sums, upper, lower):
     h = lax.axis_index("ha")
-    to_first = jnp.where(h % 2 == 1, upper, lower)
-    to_third = jnp.where(h == 2, upper, lower)
-    s1, got_first = swap_with(sums, to_first, "ha", 1)
+    s1, got_first = swap_with(sums, jnp.where(h % 2 == 1, upper, lower), "ha", 1)
     s2 = swap(sums, "ha", 2)
-    s3, got_third = swap_with(sums, to_third, "ha", 3)
+    inner = jnp.where(h == 2, upper, lower)
+    width = inner.shape[-1]
+    packed = pack_sums(sums, width)
+    message = jnp.concatenate([inner.reshape(-1, width), packed], axis=0)
+    got = lax.ppermute(message, "ha", [(1, 2), (2, 1)])
+    cut = got.shape[0] - packed.shape[0]
+    got_inner = got[:cut].reshape(inner.shape)
+    s_outer = lax.ppermute(sums, "ha", [(0, 3), (3, 0)])
+    s3 = jnp.where(jnp.logical_or(h == 1, h == 2), unpack_sums(got[cut:], sums), s_outer)
     sums = (sums + s1) + (s2 + s3)
-    above = jnp.where(h % 2 == 1, got_first, got_third)
-    below = jnp.where(h % 2 == 0, got_first, got_third)
+    above = jnp.where(h % 2 == 1, got_first, got_inner)
+    below = jnp.where(h % 2 == 0, got_first, got_inner)
     return sums, above, below
 
 

time: 97.2 us -> 100 us (1.029)
  starting transfers between devices: 20.1 us -> 32.3 us
  waiting for transfers between devices: 22.1 us -> 12.8 us
  other arithmetic: 18.3 us -> 16.6 us
  local copies, waits for them, and re-layouts: 26.6 us -> 28.1 us
    ppermute x0 -> x6, starting transfers between devices: none -> 14.8 us  [the longest x3 12.4 us: ha_round(): s_outer = lax.ppermute(sums, 'ha', [(0, 3), (3, 0)])]
    ppermute x15 -> x12, waiting for transfers between devices: 22.1 us -> 7.5 us  [swap(): return lax.ppermute(x, axis, [(i, i ^ distance) for i in range(size)])]
    ppermute x0 -> x6, waiting for transfers between devices: none -> 5.25 us  [the longest x3 5.24 us: ha_round(): s_outer = lax.ppermute(sums, 'ha', [(0, 3), (3, 0)])]
    another operation x2 -> x10, local copies, waits for them, and re-layouts: 0.16 us -> 3.3 us  [local_sums(): jnp.stack([jnp.sum(flat, axis=0), jnp.sum(flat * flat, axis=0)])]
    ppermute x15 -> x12, starting transfers between devices: 20.1 us -> 17.4 us  [swap(): return lax.ppermute(x, axis, [(i, i ^ distance) for i in range(size)])]
    reduce_sum x6 -> x2, local copies, waits for them, and re-layouts: 1.8 us -> 0.17 us  [local_sums(): return jnp.sum(per_channel.reshape(2, GROUPS, channels // GROUPS), axis=2)]
    reduce_sum x8 -> x5, other arithmetic: 4.17 us -> 3.3 us  [the longest x2 2.48 us: local_sums(): jnp.sum(flat, axis=0)]
    unnamed x57 -> x53, local copies, waits for them, and re-layouts: 6.36 us -> 6.57 us
  transfers between devices with their start and end apart: 15 -> 18, of which waited for: 8 -> 6; matrix products, arithmetic and copies ran while one was open for 9% -> 9% of each run, Pallas kernels for 0% -> 0%
where the time goes in v7:
time: 100 us; the launch traced here: 99.5 us
  starting transfers between devices  32.3 us (32%)
  local copies, waits for them, and re-layouts  28.1 us (28%)
  other arithmetic  16.6 us (17%)
  waiting for transfers between devices  12.8 us (13%)
  matrix products  8.73 us (9%)
  between operations  1 us (1%)
    ppermute x12, starting transfers between devices, swap(): return lax.ppermute(x, axis, [(i, i ^ distance) for i in range(size)])  17.4 us
    ppermute x3, starting transfers between devices, ha_round(): s_outer = lax.ppermute(sums, 'ha', [(0, 3), (3, 0)])  12.4 us
    ppermute x12, waiting for transfers between devices, swap(): return lax.ppermute(x, axis, [(i, i ^ distance) for i in range(size)])  7.5 us
    unnamed x53, local copies, waits for them, and re-layouts  6.57 us
    dot_general x6, matrix products, valid_conv(): jnp.dot(window, kernel[step_t].reshape(9 * channels, -1), preferred_eleme...  6.51 us
    ppermute x3, waiting for transfers between devices, ha_round(): s_outer = lax.ppermute(sums, 'ha', [(0, 3), (3, 0)])  5.24 us
    slice x2, local copies, waits for them, and re-layouts, valid_conv(): kernel[step_t].reshape(9 * channels, -1)  5.11 us
    convert_element_type x2, other arithmetic, norm_conv(): jnp.where(inside_mask(height + 2, across + 2, 1), act, 0.0)  4.81 us
  transfers between devices with their start and end apart: 18, of which 6 were waited for; matrix products, arithmetic and copies ran while one was open for 9% of the time, Pallas kernels for 0%

profile of v7, /device:TPU:0, one launch (start us, length us, event | category | flops | bytes accessed | tf_op | source)
XLA Modules:
  0.0 99.5 jit_solution(13875648602784578185)
XLA Ops:
  0.0 1.1 %convert_reduce_fusion.2 = (f32[512]{0:T(512)S(1)}, f32[512]{0:T(512)S(1)}) fusion(bf16[3,2,32,512]{3,2,1,0:T(8,128)(2,1)} %param.10), kind=kLoop, calls=%fused_computation.52 | loop fusion | flops 392192 | bytes 200704 | tf_op jit(solution)/shard_map/reduce_sum | solution.py:180
  1.8 1.6 %slice_bitcast_fusion.7 = (bf16[512,256]{1,0:T(8,128)(2,1)S(1)}, bf16[512,256]{1,0:T(8,128)(2,1)S(1)}, bf16[512,256]{1,0:T(8,128)(2,1)S(1)}, bf16[512,256]{1,0:T...) fusion(bf16[3,3,512,256]{3,2,1,0:T(8,128)(2,1)} %param.13), kind=kLoop, calls=%fused_computation.69 | loop fusion | bytes 4194304 | tf_op jit(solution)/shard_map/squeeze | solution.py:129
  4.0 2.6 %collective-permute-start.1 = (bf16[7,512]{1,0:T(8,128)(2,1)S(1)}, bf16[7,512]{1,0:T(8,128)(2,1)S(1)}, u32[]{:S(2)}, u32[]{:S(2)}) collective-permute-start(bf16[7,512]{1,0:T(8,128)(2,1)S(1)} %pad_maximum_fusion.21), channel_id=1, source_target_pairs={{0,2},{2,0},{1,3},{3,1},{4,6},{6,4},{5,7},{7,5},{8,10},{10,8},{9,1... | collective-permute-start | bytes 21512 | tf_op jit(solution)/shard_map/ppermute | solution.py:170
  6.6 1.6 %collective-permute-done.1 = bf16[7,512]{1,0:T(8,128)(2,1)S(1)} collective-permute-done((bf16[7,512]{1,0:T(8,128)(2,1)S(1)}, bf16[7,512]{1,0:T(8,128)(2,1)S(1)}, u32[]{:S(2)}, u32[]{:S(2)}) %collective-permute-start.1) | collective-permute-done | bytes 7200 | tf_op jit(solution)/shard_map/ppermute | solution.py:170
  8.9 2.2 %collective-permute-start.2 = (bf16[100,512]{1,0:T(8,128)(2,1)S(1)}, bf16[100,512]{1,0:T(8,128)(2,1)S(1)}, u32[]{:S(2)}, u32[]{:S(2)}) collective-permute-start(bf16[100,512]{1,0:T(8,128)(2,1)S(1)} %pad_maximum_fusion.16), channel_id=1, source_target_pairs={{0,4},{4,0},{8,12},{12,8},{1,5},{5,1},{9,13},{13,9},{2,6},{6,2},{1... | collective-permute-start | bytes 307208 | tf_op jit(solution)/shard_map/ppermute | solution.py:170
  12.2 3.9 %collective-permute-start.4 = (f32[2,32]{1,0:T(2,128)S(1)}, f32[2,32]{1,0:T(2,128)S(1)}, u32[]{:S(2)}, u32[]{:S(2)}) collective-permute-start(f32[2,32]{1,0:T(2,128)S(1)} %get-tuple-element.27), channel_id=1, source_target_pairs={{0,8},{4,12},{8,0},{12,4},{1,9},{5,13},{9,1},{13,5},{2,10},{6,14},... | collective-permute-start | bytes 776 | tf_op jit(solution)/shard_map/ppermute | solution.py:170
  16.1 4.8 %collective-permute-start.5 = (f32[2,32]{1,0:T(2,128)S(1)}, f32[2,32]{1,0:T(2,128)S(1)}, u32[]{:S(2)}, u32[]{:S(2)}) collective-permute-start(f32[2,32]{1,0:T(2,128)S(1)} %get-tuple-element.27), channel_id=1, source_target_pairs={{0,12},{12,0},{1,13},{13,1},{2,14},{14,2},{3,15},{15,3},{16,28},{2... | collective-permute-start | bytes 776 | tf_op jit(solution)/shard_map/ppermute | solution.py:240
  21.3 2.1 %collective-permute-done.5 = f32[2,32]{1,0:T(2,128)S(1)} collective-permute-done((f32[2,32]{1,0:T(2,128)S(1)}, f32[2,32]{1,0:T(2,128)S(1)}, u32[]{:S(2)}, u32[]{:S(2)}) %collective-permute-start.5) | collective-permute-done | bytes 288 | tf_op jit(solution)/shard_map/ppermute | solution.py:240
  25.6 1.3 %convolution_add_fusion.4 = bf16[192,256]{1,0:T(8,128)(2,1)S(1)} fusion(bf16[192,512]{1,0:T(8,128)(2,1)S(1)} %bitcast.120, bf16[3,3,512,256]{3,2,1,0:T(8,128)(2,1)} %param.13, f32[192,512]{1,0:T(8,128)S(1)} %fusion.15, f32[192,512]{1,0:T(8,128)S(1)} %fusion.11, f32[192,1024]{1,0:T(8,128)S(1)} %fusion.1), kind=kOutput, calls=%fused_computation.7 | convolution fusion | flops 50528256 | bytes 1146880 | tf_op jit(solution)/shard_map/dot_general | solution.py:123
  27.5 1.4 %convert_reduce_fusion.1 = (f32[256]{0:T(256)}, f32[256]{0:T(256)}, bf16[3,2,2,64,256]{4,1,3,0,2:T(2,128)(2,1)S(1)}) fusion(bf16[3,2,1,64,256]{4,1,3,0,2:T(2,128)(2,1)S(1)} %bitcast.123, bf16[3,2,1,64,256]{4,1,3,0,2:T(2,128)(2,1)S(1)} %bitcast.122), kind=kLoop, calls=%fused_computation.19 | loop fusion | flops 982528 | bytes 788480 | tf_op jit(solution)/shard_map/reduce_sum | solution.py:180
  29.0 0.7 copy-done.1
  29.9 0.7 copy.39
  30.6 0.7 stack.30
  31.4 0.7 copy.40
  32.0 0.7 stack.31
  32.8 0.7 copy.41
  33.4 0.7 maximum_reduce_fusion.1
  34.3 1.0 pad_maximum_fusion.2
  35.4 1.8 %fusion.111 = (bf16[1,3,3,256,256]{4,3,2,1,0:T(8,128)(2,1)}, bf16[1,3,3,256,256]{4,3,2,1,0:T(8,128)(2,1)}, bf16[1,3,3,256,256]{4,3,2,1,0:T(8,128)(2,1)}) fusion(bf16[3,3,3,256,256]{4,3,2,1,0:T(8,128)(2,1)S(1)} %copy-done), kind=kLoop, calls=%fused_computation.272 | loop fusion | bytes 7077888 | tf_op jit(solution)/shard_map/slice | solution.py:154
  38.3 0.7 slice_convert_fusion.7
  39.5 1.5 %collective-permute-start.7 = (bf16[21,256]{1,0:T(8,128)(2,1)S(1)}, bf16[21,256]{1,0:T(8,128)(2,1)S(1)}, u32[]{:S(2)}, u32[]{:S(2)}) collective-permute-start(bf16[21,256]{1,0:T(8,128)(2,1)S(1)} %pad_maximum_fusion.19), channel_id=1, source_target_pairs={{0,2},{2,0},{1,3},{3,1},{4,6},{6,4},{5,7},{7,5},{8,10},{10,8},{9,1... | collective-permute-start | bytes 32264 | tf_op jit(solution)/shard_map/ppermute | solution.py:170
  41.1 2.2 %collective-permute-done.7 = bf16[21,256]{1,0:T(8,128)(2,1)S(1)} collective-permute-done((bf16[21,256]{1,0:T(8,128)(2,1)S(1)}, bf16[21,256]{1,0:T(8,128)(2,1)S(1)}, u32[]{:S(2)}, u32[]{:S(2)}) %collective-permute-start.7) | collective-permute-done | bytes 10784 | tf_op jit(solution)/shard_map/ppermute | solution.py:170
  44.3 3.4 %collective-permute-start.10 = (f32[2,32]{1,0:T(2,128)S(1)}, f32[2,32]{1,0:T(2,128)S(1)}, u32[]{:S(2)}, u32[]{:S(2)}) collective-permute-start(f32[2,32]{1,0:T(2,128)S(1)} %get-tuple-element.22), channel_id=1, source_target_pairs={{0,8},{4,12},{8,0},{12,4},{1,9},{5,13},{9,1},{13,5},{2,10},{6,14},... | collective-permute-start | bytes 776 | tf_op jit(solution)/shard_map/ppermute | solution.py:170
  47.8 2.8 %collective-permute-start.11 = (f32[2,32]{1,0:T(2,128)S(1)}, f32[2,32]{1,0:T(2,128)S(1)}, u32[]{:S(2)}, u32[]{:S(2)}) collective-permute-start(f32[2,32]{1,0:T(2,128)S(1)} %get-tuple-element.22), channel_id=1, source_target_pairs={{0,12},{12,0},{1,13},{13,1},{2,14},{14,2},{3,15},{15,3},{16,28},{2... | collective-permute-start | bytes 776 | tf_op jit(solution)/shard_map/ppermute | solution.py:240
  50.6 0.9 collective-permute-start.9
  51.8 3.2 %collective-permute-done.11 = f32[2,32]{1,0:T(2,128)S(1)} collective-permute-done((f32[2,32]{1,0:T(2,128)S(1)}, f32[2,32]{1,0:T(2,128)S(1)}, u32[]{:S(2)}, u32[]{:S(2)}) %collective-permute-start.11) | collective-permute-done | bytes 288 | tf_op jit(solution)/shard_map/ppermute | solution.py:240
  55.5 1.9 %select_convert_fusion.1 = bf16[5,6,66,256]{3,2,1,0:T(8,128)(2,1)S(1)} fusion(bf16[5,1,66,256]{3,2,1,0:T(8,128)(2,1)S(1)} %select_n.201, bf16[5,4,1,256]{3,2,1,0:T(2,128)(2,1)S(1)} %reshape.763, bf16[3,4,64,256]{3,2,1,0:T(8,128)(2,1)S(1)} %bitcast.100, bf16[2,4,64,256]{3,2,1,0:T(8,128)(2,1)S(1)} %maximum_select_fusion, ...), kind=kLoop, calls=%fused_computation.1 | loop fusion | flops 11151360 | bytes 2021772 | tf_op jit(solution)/shard_map/convert_element_type | solution.py:283
  59.2 1.0 fusion.109
  60.5 1.1 %fusion.114 = f32[768,256]{1,0:T(8,128)S(1)} fusion(bf16[768,2304]{1,0:T(8,128)(2,1)S(1)} %bitcast.109, bf16[2304,256]{1,0:T(8,128)(2,1)S(1)} %bitcast.113), kind=kOutput, calls=%fused_computation.275 | convolution fusion | flops 905969664 | bytes 5505024 | tf_op jit(solution)/shard_map/dot_general | solution.py:153
  61.8 1.1 %convolution_add_fusion.3 = f32[768,256]{1,0:T(8,128)S(1)} fusion(f32[768,256]{1,0:T(8,128)S(1)} %fusion.114, bf16[768,2304]{1,0:T(8,128)(2,1)S(1)} %bitcast.107, bf16[2304,256]{1,0:T(8,128)(2,1)S(1)} %bitcast.112), kind=kOutput, calls=%fused_computation.5 | convolution fusion | flops 906166272 | bytes 6291456 | tf_op jit(solution)/shard_map/dot_general | solution.py:153
  63.0 1.1 %convert_reduce_fusion = (f32[256]{0:T(256)S(1)}, f32[256]{0:T(256)S(1)}, bf16[768,256]{1,0:T(8,128)(2,1)S(1)}) fusion(f32[768,256]{1,0:T(8,128)S(1)} %convolution_add_fusion.3, bf16[768,2304]{1,0:T(8,128)(2,1)S(1)} %bitcast.105, bf16[2304,256]{1,0:T(8,128)(2,1)S(1)} %bitcast.111), kind=kOutput, calls=%fused_computation.17 | convolution fusion | flops 907148800 | bytes 5900288 | tf_op jit(solution)/shard_map/dot_general | solution.py:153
  64.8 1.5 %collective-permute-done.12 = bf16[513,256]{1,0:T(8,128)(2,1)S(1)} collective-permute-done((bf16[513,256]{1,0:T(8,128)(2,1)S(1)}, bf16[513,256]{1,0:T(8,128)(2,1)S(1)}, u32[]{:S(2)}, u32[]{:S(2)}) %collective-permute-start.12) | collective-permute-done | bytes 262688 | tf_op jit(solution)/shard_map/ppermute | solution.py:170
  67.1 1.6 %collective-permute-start.13 = (bf16[21,256]{1,0:T(8,128)(2,1)S(1)}, bf16[21,256]{1,0:T(8,128)(2,1)S(1)}, u32[]{:S(2)}, u32[]{:S(2)}) collective-permute-start(bf16[21,256]{1,0:T(8,128)(2,1)S(1)} %pad_maximum_fusion.20), channel_id=1, source_target_pairs={{0,2},{2,0},{1,3},{3,1},{4,6},{6,4},{5,7},{7,5},{8,10},{10,8},{9,1... | collective-permute-start | bytes 32264 | tf_op jit(solution)/shard_map/ppermute | solution.py:170
  68.6 2.2 %collective-permute-done.13 = bf16[21,256]{1,0:T(8,128)(2,1)S(1)} collective-permute-done((bf16[21,256]{1,0:T(8,128)(2,1)S(1)}, bf16[21,256]{1,0:T(8,128)(2,1)S(1)}, u32[]{:S(2)}, u32[]{:S(2)}) %collective-permute-start.13) | collective-permute-done | bytes 10784 | tf_op jit(solution)/shard_map/ppermute | solution.py:170
  71.7 1.1 %collective-permute-start.14 = (bf16[331,256]{1,0:T(8,128)(2,1)S(1)}, bf16[331,256]{1,0:T(8,128)(2,1)S(1)}, u32[]{:S(2)}, u32[]{:S(2)}) collective-permute-start(bf16[331,256]{1,0:T(8,128)(2,1)S(1)} %get-tuple-element.61), channel_id=1, source_target_pairs={{0,4},{4,0},{8,12},{12,8},{1,5},{5,1},{9,13},{13,9},{2,6},{6,2},{1... | collective-permute-start | bytes 508424 | tf_op jit(solution)/shard_map/ppermute | solution.py:170
  72.8 3.3 %fusion.110 = (bf16[1,3,3,256,256]{4,3,2,1,0:T(8,128)(2,1)S(1)}, bf16[1,3,3,256,256]{4,3,2,1,0:T(8,128)(2,1)}, bf16[1,3,3,256,256]{4,3,2,1,0:T(8,128)(2,1)S(1)}) fusion(bf16[3,3,3,256,256]{4,3,2,1,0:T(8,128)(2,1)} %param.19), kind=kLoop, calls=%fused_computation.271 | loop fusion | bytes 7077888 | tf_op jit(solution)/shard_map/slice | solution.py:154
  76.5 4.8 %collective-permute-start.17 = (f32[2,32]{1,0:T(2,128)S(1)}, f32[2,32]{1,0:T(2,128)S(1)}, u32[]{:S(2)}, u32[]{:S(2)}) collective-permute-start(f32[2,32]{1,0:T(2,128)S(1)} %get-tuple-element.15), channel_id=1, source_target_pairs={{0,12},{12,0},{1,13},{13,1},{2,14},{14,2},{3,15},{15,3},{16,28},{2... | collective-permute-start | bytes 776 | tf_op jit(solution)/shard_map/ppermute | solution.py:240
  81.3 0.9 collective-permute-start.15
  83.0 0.7 copy-done.10
  84.3 1.8 %broadcast_select_fusion.6 = (bf16[330,256]{1,0:T(8,128)(2,1)}, bf16[330,256]{1,0:T(8,128)(2,1)}) fusion(pred[]{:T(512)S(6)} %eq.45, bf16[331,256]{1,0:T(8,128)(2,1)} %copy-done.10, bf16[331,256]{1,0:T(8,128)(2,1)} %copy-done.9, pred[]{:T(512)S(6)} %eq.21), kind=kLoop, calls=%fused_computation.92 | loop fusion | flops 168960 | bytes 675842 | tf_op jit(solution)/shard_map/jit(_where)/select_n | solution.py:243
  86.1 1.6 %select_n.209 = bf16[5,1,66,256]{3,2,1,0:T(8,128)(2,1)} reshape(bf16[330,256]{1,0:T(8,128)(2,1)} %get-tuple-element.57) | data formatting | bytes 337920 | tf_op jit(solution)/shard_map/jit(_where)/select_n | solution.py:243
  87.7 1.6 %select_n.211 = bf16[5,1,66,256]{3,2,1,0:T(8,128)(2,1)} reshape(bf16[330,256]{1,0:T(8,128)(2,1)} %get-tuple-element.58) | data formatting | bytes 337920 | tf_op jit(solution)/shard_map/jit(_where)/select_n | solution.py:244
  89.4 2.9 %select_convert_fusion = bf16[5,6,66,256]{3,2,1,0:T(8,128)(2,1)S(1)} fusion(bf16[5,1,66,256]{3,2,1,0:T(8,128)(2,1)} %select_n.211, bf16[5,4,1,256]{3,2,1,0:T(2,128)(2,1)S(1)} %reshape.764, bf16[3,4,64,256]{3,2,1,0:T(8,128)(2,1)S(1)} %bitcast.104, bf16[2,4,64,256]{3,2,1,0:T(8,128)(2,1)S(1)} %maximum_select_fusion.1, bf16[5,1,66,256]{3,2,1,0:T(8,128)(2,1)} %select_n.209, ...), kind=kLoop, calls=%fused_computation | loop fusion | flops 11151360 | bytes 2021772 | tf_op jit(solution)/shard_map/convert_element_type | solution.py:283
  94.0 1.0 fusion.108
  95.3 1.1 %fusion.115 = f32[768,256]{1,0:T(8,128)S(1)} fusion(bf16[768,2304]{1,0:T(8,128)(2,1)S(1)} %bitcast.110, bf16[2304,256]{1,0:T(8,128)(2,1)S(1)} %bitcast.116), kind=kOutput, calls=%fused_computation.276 | convolution fusion | flops 905969664 | bytes 5505024 | tf_op jit(solution)/shard_map/dot_general | solution.py:153
  96.4 1.1 %convolution_add_fusion.1 = f32[768,256]{1,0:T(8,128)S(1)} fusion(f32[768,256]{1,0:T(8,128)S(1)} %fusion.115, bf16[768,2304]{1,0:T(8,128)(2,1)S(1)} %bitcast.108, bf16[2304,256]{1,0:T(8,128)(2,1)S(1)} %bitcast.115), kind=kOutput, calls=%fused_computation.3 | convolution fusion | flops 906166272 | bytes 6291456 | tf_op jit(solution)/shard_map/dot_general | solution.py:153
  97.5 1.1 %convolution_add_fusion = f32[768,256]{1,0:T(8,128)S(1)} fusion(f32[768,256]{1,0:T(8,128)S(1)} %convolution_add_fusion.1, bf16[768,2304]{1,0:T(8,128)(2,1)S(1)} %bitcast.106, bf16[2304,256]{1,0:T(8,128)(2,1)S(1)} %bitcast.114), kind=kOutput, calls=%fused_computation.2 | convolution fusion | flops 906166272 | bytes 6291456 | tf_op jit(solution)/shard_map/dot_general | solution.py:153
  98.6 0.9 add_convert_fusion
  (242 shorter events, 18.2 us)
Async XLA Ops:
  0.0 3.6 %copy-start.7 = (bf16[3,2,32,512]{3,2,1,0:T(8,128)(2,1)S(1)}, bf16[3,2,32,512]{3,2,1,0:T(8,128)(2,1)}, u32[]{:S(2)}) copy-start(bf16[3,2,32,512]{3,2,1,0:T(8,128)(2,1)} %param.10) | copy-start | bytes 589828
  1.3 2.3 %collective-permute-start = (f32[2,32]{1,0:T(2,128)S(1)}, f32[2,32]{1,0:T(2,128)S(1)}, u32[]{:S(2)}, u32[]{:S(2)}) collective-permute-start(f32[2,32]{1,0:T(2,128)S(1)} %maximum_reduce_fusion), channel_id=1, source_target_pairs={{0,1},{1,0},{2,3},{3,2},{4,5},{5,4},{6,7},{7,6},{8,9},{9,8},{10,11... | collective-permute-start | bytes 776 | tf_op jit(solution)/shard_map/ppermute | solution.py:170
  1.8 22.0 %copy-start.11 = (f32[512]{0:T(512)S(1)}, f32[512]{0:T(512)}, u32[]{:S(2)}) copy-start(f32[512]{0:T(512)} %param.12) | copy-start | bytes 6148
  1.8 22.0 %copy-start.12 = (f32[512]{0:T(512)S(1)}, f32[512]{0:T(512)}, u32[]{:S(2)}) copy-start(f32[512]{0:T(512)} %param.11) | copy-start | bytes 6148
  4.0 4.2 %collective-permute-start.1 = (bf16[7,512]{1,0:T(8,128)(2,1)S(1)}, bf16[7,512]{1,0:T(8,128)(2,1)S(1)}, u32[]{:S(2)}, u32[]{:S(2)}) collective-permute-start(bf16[7,512]{1,0:T(8,128)(2,1)S(1)} %pad_maximum_fusion.21), channel_id=1, source_target_pairs={{0,2},{2,0},{1,3},{3,1},{4,6},{6,4},{5,7},{7,5},{8,10},{10,8},{9,1... | collective-permute-start | bytes 21512 | tf_op jit(solution)/shard_map/ppermute | solution.py:170
  8.9 12.1 %collective-permute-start.2 = (bf16[100,512]{1,0:T(8,128)(2,1)S(1)}, bf16[100,512]{1,0:T(8,128)(2,1)S(1)}, u32[]{:S(2)}, u32[]{:S(2)}) collective-permute-start(bf16[100,512]{1,0:T(8,128)(2,1)S(1)} %pad_maximum_fusion.16), channel_id=1, source_target_pairs={{0,4},{4,0},{8,12},{12,8},{1,5},{5,1},{9,13},{13,9},{2,6},{6,2},{1... | collective-permute-start | bytes 307208 | tf_op jit(solution)/shard_map/ppermute | solution.py:170
  11.6 9.5 %collective-permute-start.3 = (bf16[100,512]{1,0:T(8,128)(2,1)S(1)}, bf16[100,512]{1,0:T(8,128)(2,1)S(1)}, u32[]{:S(2)}, u32[]{:S(2)}) collective-permute-start(bf16[100,512]{1,0:T(8,128)(2,1)S(1)} %pad_maximum_fusion.16), channel_id=1, source_target_pairs={{4,8},{8,4},{5,9},{9,5},{6,10},{10,6},{7,11},{11,7},{20,24},{24,20... | collective-permute-start | bytes 307208 | tf_op jit(solution)/shard_map/ppermute | solution.py:237
  12.2 9.1 %collective-permute-start.4 = (f32[2,32]{1,0:T(2,128)S(1)}, f32[2,32]{1,0:T(2,128)S(1)}, u32[]{:S(2)}, u32[]{:S(2)}) collective-permute-start(f32[2,32]{1,0:T(2,128)S(1)} %get-tuple-element.27), channel_id=1, source_target_pairs={{0,8},{4,12},{8,0},{12,4},{1,9},{5,13},{9,1},{13,5},{2,10},{6,14},... | collective-permute-start | bytes 776 | tf_op jit(solution)/shard_map/ppermute | solution.py:170
  16.1 7.2 %collective-permute-start.5 = (f32[2,32]{1,0:T(2,128)S(1)}, f32[2,32]{1,0:T(2,128)S(1)}, u32[]{:S(2)}, u32[]{:S(2)}) collective-permute-start(f32[2,32]{1,0:T(2,128)S(1)} %get-tuple-element.27), channel_id=1, source_target_pairs={{0,12},{12,0},{1,13},{13,1},{2,14},{14,2},{3,15},{15,3},{16,28},{2... | collective-permute-start | bytes 776 | tf_op jit(solution)/shard_map/ppermute | solution.py:240
  25.6 9.8 %copy-start = (bf16[3,3,3,256,256]{4,3,2,1,0:T(8,128)(2,1)S(1)}, bf16[3,3,3,256,256]{4,3,2,1,0:T(8,128)(2,1)}, u32[]{:S(2)}) copy-start(bf16[3,3,3,256,256]{4,3,2,1,0:T(8,128)(2,1)} %param.16) | copy-start | bytes 10616836
  29.0 0.7 copy-start.1
  35.3 2.0 %copy-start.2 = (bf16[3,2,2,64,256]{4,1,3,0,2:T(2,128)(2,1)S(1)}, bf16[3,2,2,64,256]{4,1,3,0,2:T(2,128)(2,1)}, u32[]{:S(2)}) copy-start(bf16[3,2,2,64,256]{4,1,3,0,2:T(2,128)(2,1)} %copy-done.1) | copy-start | bytes 1179652
  35.3 2.1 %collective-permute-start.6 = (bf16[513,256]{1,0:T(8,128)(2,1)S(1)}, bf16[513,256]{1,0:T(8,128)(2,1)S(1)}, u32[]{:S(2)}, u32[]{:S(2)}) collective-permute-start(bf16[513,256]{1,0:T(8,128)(2,1)S(1)} %pad_maximum_fusion.2), channel_id=1, source_target_pairs={{0,1},{1,0},{2,3},{3,2},{4,5},{5,4},{6,7},{7,6},{8,9},{9,8},{10,11... | collective-permute-start | bytes 787976 | tf_op jit(solution)/shard_map/ppermute | solution.py:170
  37.4 0.7 copy-start.8
  37.5 6.8 %copy-start.17 = (pred[6]{0:T(512)(128)(4,1)S(1)}, pred[6]{0:T(512)(128)(4,1)}, u32[]{:S(2)}) copy-start(pred[6]{0:T(512)(128)(4,1)} %or_and_fusion.1) | copy-start | bytes 22
  39.5 3.8 %collective-permute-start.7 = (bf16[21,256]{1,0:T(8,128)(2,1)S(1)}, bf16[21,256]{1,0:T(8,128)(2,1)S(1)}, u32[]{:S(2)}, u32[]{:S(2)}) collective-permute-start(bf16[21,256]{1,0:T(8,128)(2,1)S(1)} %pad_maximum_fusion.19), channel_id=1, source_target_pairs={{0,2},{2,0},{1,3},{3,1},{4,6},{6,4},{5,7},{7,5},{8,10},{10,8},{9,1... | collective-permute-start | bytes 32264 | tf_op jit(solution)/shard_map/ppermute | solution.py:170
  43.3 12.3 %copy-start.13 = (f32[256]{0:T(256)S(1)}, f32[256]{0:T(256)}, u32[]{:S(2)}) copy-start(f32[256]{0:T(256)} %param.15) | copy-start | bytes 3076
  43.3 12.3 %copy-start.14 = (f32[256]{0:T(256)S(1)}, f32[256]{0:T(256)}, u32[]{:S(2)}) copy-start(f32[256]{0:T(256)} %param.14) | copy-start | bytes 3076
  44.2 7.3 %collective-permute-start.8 = (bf16[331,256]{1,0:T(8,128)(2,1)S(1)}, bf16[331,256]{1,0:T(8,128)(2,1)S(1)}, u32[]{:S(2)}, u32[]{:S(2)}) collective-permute-start(bf16[331,256]{1,0:T(8,128)(2,1)S(1)} %get-tuple-element.67), channel_id=1, source_target_pairs={{0,4},{4,0},{8,12},{12,8},{1,5},{5,1},{9,13},{13,9},{2,6},{6,2},{1... | collective-permute-start | bytes 508424 | tf_op jit(solution)/shard_map/ppermute | solution.py:170
  44.3 7.5 %collective-permute-start.10 = (f32[2,32]{1,0:T(2,128)S(1)}, f32[2,32]{1,0:T(2,128)S(1)}, u32[]{:S(2)}, u32[]{:S(2)}) collective-permute-start(f32[2,32]{1,0:T(2,128)S(1)} %get-tuple-element.22), channel_id=1, source_target_pairs={{0,8},{4,12},{8,0},{12,4},{1,9},{5,13},{9,1},{13,5},{2,10},{6,14},... | collective-permute-start | bytes 776 | tf_op jit(solution)/shard_map/ppermute | solution.py:170
  47.8 7.3 %collective-permute-start.11 = (f32[2,32]{1,0:T(2,128)S(1)}, f32[2,32]{1,0:T(2,128)S(1)}, u32[]{:S(2)}, u32[]{:S(2)}) collective-permute-start(f32[2,32]{1,0:T(2,128)S(1)} %get-tuple-element.22), channel_id=1, source_target_pairs={{0,12},{12,0},{1,13},{13,1},{2,14},{14,2},{3,15},{15,3},{16,28},{2... | collective-permute-start | bytes 776 | tf_op jit(solution)/shard_map/ppermute | solution.py:240
  50.6 1.0 collective-permute-start.9
  59.2 1.3 %copy-start.5 = (bf16[1,3,3,256,256]{4,3,2,1,0:T(8,128)(2,1)S(1)}, bf16[1,3,3,256,256]{4,3,2,1,0:T(8,128)(2,1)}, u32[]{:S(2)}) copy-start(bf16[1,3,3,256,256]{4,3,2,1,0:T(8,128)(2,1)} %get-tuple-element.40) | copy-start | bytes 3538948
  60.5 1.3 %copy-start.4 = (bf16[1,3,3,256,256]{4,3,2,1,0:T(8,128)(2,1)S(1)}, bf16[1,3,3,256,256]{4,3,2,1,0:T(8,128)(2,1)}, u32[]{:S(2)}) copy-start(bf16[1,3,3,256,256]{4,3,2,1,0:T(8,128)(2,1)} %get-tuple-element.41) | copy-start | bytes 3538948
  61.8 1.3 %copy-start.3 = (bf16[1,3,3,256,256]{4,3,2,1,0:T(8,128)(2,1)S(1)}, bf16[1,3,3,256,256]{4,3,2,1,0:T(8,128)(2,1)}, u32[]{:S(2)}) copy-start(bf16[1,3,3,256,256]{4,3,2,1,0:T(8,128)(2,1)} %get-tuple-element.39) | copy-start | bytes 3538948
  64.7 1.6 %collective-permute-start.12 = (bf16[513,256]{1,0:T(8,128)(2,1)S(1)}, bf16[513,256]{1,0:T(8,128)(2,1)S(1)}, u32[]{:S(2)}, u32[]{:S(2)}) collective-permute-start(bf16[513,256]{1,0:T(8,128)(2,1)S(1)} %pad_maximum_fusion.3), channel_id=1, source_target_pairs={{0,1},{1,0},{2,3},{3,2},{4,5},{5,4},{6,7},{7,6},{8,9},{9,8},{10,11... | collective-permute-start | bytes 787976 | tf_op jit(solution)/shard_map/ppermute | solution.py:170
  67.1 3.8 %collective-permute-start.13 = (bf16[21,256]{1,0:T(8,128)(2,1)S(1)}, bf16[21,256]{1,0:T(8,128)(2,1)S(1)}, u32[]{:S(2)}, u32[]{:S(2)}) collective-permute-start(bf16[21,256]{1,0:T(8,128)(2,1)S(1)} %pad_maximum_fusion.20), channel_id=1, source_target_pairs={{0,2},{2,0},{1,3},{3,1},{4,6},{6,4},{5,7},{7,5},{8,10},{10,8},{9,1... | collective-permute-start | bytes 32264 | tf_op jit(solution)/shard_map/ppermute | solution.py:170
  71.7 17.7 %copy-start.15 = (f32[256]{0:T(256)S(1)}, f32[256]{0:T(256)}, u32[]{:S(2)}) copy-start(f32[256]{0:T(256)} %param.18) | copy-start | bytes 3076
  71.7 17.6 %copy-start.16 = (f32[256]{0:T(256)S(1)}, f32[256]{0:T(256)}, u32[]{:S(2)}) copy-start(f32[256]{0:T(256)} %param.17) | copy-start | bytes 3076
  71.7 10.5 %collective-permute-start.14 = (bf16[331,256]{1,0:T(8,128)(2,1)S(1)}, bf16[331,256]{1,0:T(8,128)(2,1)S(1)}, u32[]{:S(2)}, u32[]{:S(2)}) collective-permute-start(bf16[331,256]{1,0:T(8,128)(2,1)S(1)} %get-tuple-element.61), channel_id=1, source_target_pairs={{0,4},{4,0},{8,12},{12,8},{1,5},{5,1},{9,13},{13,9},{2,6},{6,2},{1... | collective-permute-start | bytes 508424 | tf_op jit(solution)/shard_map/ppermute | solution.py:170
  76.1 7.9 %collective-permute-start.16 = (f32[2,32]{1,0:T(2,128)S(1)}, f32[2,32]{1,0:T(2,128)S(1)}, u32[]{:S(2)}, u32[]{:S(2)}) collective-permute-start(f32[2,32]{1,0:T(2,128)S(1)} %get-tuple-element.15), channel_id=1, source_target_pairs={{0,8},{4,12},{8,0},{12,4},{1,9},{5,13},{9,1},{13,5},{2,10},{6,14},... | collective-permute-start | bytes 776 | tf_op jit(solution)/shard_map/ppermute | solution.py:170
  76.5 7.4 %collective-permute-start.17 = (f32[2,32]{1,0:T(2,128)S(1)}, f32[2,32]{1,0:T(2,128)S(1)}, u32[]{:S(2)}, u32[]{:S(2)}) collective-permute-start(f32[2,32]{1,0:T(2,128)S(1)} %get-tuple-element.15), channel_id=1, source_target_pairs={{0,12},{12,0},{1,13},{13,1},{2,14},{14,2},{3,15},{15,3},{16,28},{2... | collective-permute-start | bytes 776 | tf_op jit(solution)/shard_map/ppermute | solution.py:240
  81.3 1.7 %collective-permute-start.15 = (bf16[331,256]{1,0:T(8,128)(2,1)S(1)}, bf16[331,256]{1,0:T(8,128)(2,1)S(1)}, u32[]{:S(2)}, u32[]{:S(2)}) collective-permute-start(bf16[331,256]{1,0:T(8,128)(2,1)S(1)} %get-tuple-element.62), channel_id=1, source_target_pairs={{4,8},{8,4},{5,9},{9,5},{6,10},{10,6},{7,11},{11,7},{20,24},{24,20... | collective-permute-start | bytes 508424 | tf_op jit(solution)/shard_map/ppermute | solution.py:237
  82.3 0.7 copy-start.9
  83.0 0.7 copy-start.10
  94.0 1.3 %copy-start.6 = (bf16[1,3,3,256,256]{4,3,2,1,0:T(8,128)(2,1)S(1)}, bf16[1,3,3,256,256]{4,3,2,1,0:T(8,128)(2,1)}, u32[]{:S(2)}) copy-start(bf16[1,3,3,256,256]{4,3,2,1,0:T(8,128)(2,1)} %get-tuple-element.37) | copy-start | bytes 3538948

commit v8 on v6

--- a/solution.py
+++ b/solution.py
@@ -147,12 +147,11 @@
     wide = jnp.concatenate(
         [padded[:, dy : dy + height, dx : dx + across] for dy in range(3) for dx in range(3)], axis=-1
     )
+    taps = kernel.reshape(3, 9 * channels, kernel.shape[-1])
     result = None
     for step_t in range(3):
         window = wide[step_t : step_t + frames].reshape(-1, 9 * channels)
-        part = jnp.dot(
-            window, kernel[step_t].reshape(9 * channels, -1), preferred_element_type=jnp.float32
-        )
+        part = jnp.dot(window, taps[step_t], preferred_element_type=jnp.float32)
         result = part if result is None else result + part
     return result.reshape(frames, height, across, -1)
 
@@ -215,22 +214,27 @@
     return (flat[0] + flat[1]) + flat[2]
 
 
-def swap_with(sums, payload, axis, distance):
-    width = payload.shape[-1]
-    packed = pack_sums(sums, width)
-    message = jnp.concatenate([payload.reshape(-1, width), packed], axis=0)
+def swap_with(sums, payload, axis, distance, along):
+    slot = list(payload.shape)
+    slot[along] = 1
+    size = 1
+    for s in slot:
+        size *= s
+    packed = pack_sums(sums, size).reshape(slot)
+    message = jnp.concatenate([payload, packed], axis=along)
     got = swap(message, axis, distance)
-    cut = got.shape[0] - packed.shape[0]
-    return unpack_sums(got[cut:], sums), got[:cut].reshape(payload.shape)
+    cut = payload.shape[along]
+    received = lax.slice_in_dim(got, 0, cut, axis=along)
+    return unpack_sums(lax.slice_in_dim(got, cut, cut + 1, axis=along), sums), received
 
 
 def ha_round(sums, upper, lower):
     h = lax.axis_index("ha")
     to_first = jnp.where(h % 2 == 1, upper, lower)
     to_third = jnp.where(h == 2, upper, lower)
-    s1, got_first = swap_with(sums, to_first, "ha", 1)
+    s1, got_first = swap_with(sums, to_first, "ha", 1, 0)
     s2 = swap(sums, "ha", 2)
-    s3, got_third = swap_with(sums, to_third, "ha", 3)
+    s3, got_third = swap_with(sums, to_third, "ha", 3, 0)
     sums = (sums + s1) + (s2 + s3)
     above = jnp.where(h % 2 == 1, got_first, got_third)
     below = jnp.where(h % 2 == 0, got_first, got_third)
@@ -239,13 +243,13 @@
 
 def fast_conv_input(values):
     sums = local_sums(values.astype(jnp.float32))
-    s_t, earlier = swap_with(sums, values[-2:], "ta", 1)
+    s_t, earlier = swap_with(sums, values[-2:], "ta", 1, 1)
     sums = sums + s_t
     opening = jnp.concatenate([values[:1], values[:1]], axis=0)
     earlier = jnp.where(lax.axis_index("ta") == 0, opening, earlier)
     x = jnp.concatenate([earlier, values], axis=0)
     w = lax.axis_index("wa")
-    s_w, beside = swap_with(sums, jnp.where(w == 0, x[:, :, -1:], x[:, :, :1]), "wa", 1)
+    s_w, beside = swap_with(sums, jnp.where(w == 0, x[:, :, -1:], x[:, :, :1]), "wa", 1, 1)
     sums = sums + s_w
     x = jnp.concatenate([beside, x, beside], axis=2)
     sums, above, below = ha_round(sums, x[:, :1], x[:, -1:])
@@ -256,7 +260,7 @@
 def fast_latent_input(values):
     sums = local_sums(values.astype(jnp.float32))
     sums = sums + swap(sums, "ta", 1)
-    s_w, beside = swap_with(sums, values[:, :, :1], "wa", 1)
+    s_w, beside = swap_with(sums, values[:, :, :1], "wa", 1, 1)
     sums = sums + s_w
     x = jnp.concatenate([values, beside], axis=2)
     sums, _, below = ha_round(sums, x[:, :1], x[:, :1])

time: 97.2 us -> 104 us (1.070)
  waiting for transfers between devices: 22.1 us -> 26.1 us
  local copies, waits for them, and re-layouts: 26.6 us -> 28.5 us
    slice x8 -> x31, local copies, waits for them, and re-layouts: 6.11 us -> 11.4 us  [the longest x2 5.17 us: valid_conv(): part = jnp.dot(window, taps[step_t], preferred_element_type=jnp.float32)]
    ppermute x15, waiting for transfers between devices: 22.1 us -> 26.1 us  [swap(): return lax.ppermute(x, axis, [(i, i ^ distance) for i in range(size)])]
    select_n x5 -> x0, local copies, waits for them, and re-layouts: 3.38 us -> none  [the longest x3 1.71 us: ha_round(): below = jnp.where(h % 2 == 0, got_first, got_third)]
    another operation x0 -> x8, local copies, waits for them, and re-layouts: none -> 1.66 us  [swap_with(): packed = pack_sums(sums, size).reshape(slot)]
    unnamed x57 -> x52, local copies, waits for them, and re-layouts: 6.36 us -> 6.02 us
  transfers between devices with their start and end apart: 15 -> 15, of which waited for: 8 -> 10; matrix products, arithmetic and copies ran while one was open for 9% -> 13% of each run, Pallas kernels for 0% -> 0%
where the time goes in v8:
time: 104 us; the launch traced here: 103 us
  local copies, waits for them, and re-layouts  28.5 us (27%)
  waiting for transfers between devices  26.1 us (25%)
  starting transfers between devices  19.9 us (19%)
  other arithmetic  18.7 us (18%)
  matrix products  8.74 us (8%)
    ppermute x15, waiting for transfers between devices, swap(): return lax.ppermute(x, axis, [(i, i ^ distance) for i in range(size)])  26.1 us
    ppermute x15, starting transfers between devices, swap(): return lax.ppermute(x, axis, [(i, i ^ distance) for i in range(size)])  19.9 us
    dot_general x6, matrix products, valid_conv(): part = jnp.dot(window, taps[step_t], preferred_element_type=jnp.float32)  6.51 us
    unnamed x52, local copies, waits for them, and re-layouts  6.02 us
    slice x2, local copies, waits for them, and re-layouts, valid_conv(): part = jnp.dot(window, taps[step_t], preferred_element_type=jnp.float32)  5.17 us
    convert_element_type x2, other arithmetic, norm_conv(): jnp.where(inside_mask(height + 2, across + 2, 1), act, 0.0)  3.99 us
    reduce_sum x5, other arithmetic, local_sums(): jnp.sum(grouped, axis=(0, 2))  3.28 us
    slice x11, local copies, waits for them, and re-layouts, unpack_sums(): rows.reshape(-1)[:3 * like.size].astype(jnp.float32).reshape(3, *like.shape)  2.72 us
  transfers between devices with their start and end apart: 15, of which 10 were waited for; matrix products, arithmetic and copies ran while one was open for 13% of the time, Pallas kernels for 0%

profile of v8, /device:TPU:0, one launch (start us, length us, event | category | flops | bytes accessed | tf_op | source)
XLA Modules:
  0.0 103.0 jit_solution(6722972672398064189)
XLA Ops:
  0.0 1.0 convert_reduce_fusion.2
  1.9 0.8 slice.553
  2.7 0.9 constant_dynamic-update-slice_fusion.1
  3.7 1.6 %slice_bitcast_fusion.7 = (bf16[512,256]{1,0:T(8,128)(2,1)S(1)}, bf16[512,256]{1,0:T(8,128)(2,1)S(1)}, bf16[512,256]{1,0:T(8,128)(2,1)S(1)}, bf16[512,256]{1,0:T...) fusion(bf16[3,3,512,256]{3,2,1,0:T(8,128)(2,1)} %param.13), kind=kLoop, calls=%fused_computation.73 | loop fusion | bytes 4194304 | tf_op jit(solution)/shard_map/squeeze | solution.py:129
  5.8 2.6 %collective-permute-start.1 = (bf16[3,3,1,512]{3,1,2,0:T(4,128)(2,1)S(1)}, bf16[3,3,1,512]{3,1,2,0:T(4,128)(2,1)S(1)}, u32[]{:S(2)}, u32[]{:S(2)}) collective-permute-start(bf16[3,3,1,512]{3,1,2,0:T(4,128)(2,1)S(1)} %pad_maximum_fusion.21), channel_id=1, source_target_pairs={{0,2},{2,0},{1,3},{3,1},{4,6},{6,4},{5,7},{7,5},{8,10},{10,8},{9,1... | collective-permute-start | bytes 27656 | tf_op jit(solution)/shard_map/ppermute | solution.py:169
  8.4 1.7 %collective-permute-done.1 = bf16[3,3,1,512]{3,1,2,0:T(4,128)(2,1)S(1)} collective-permute-done((bf16[3,3,1,512]{3,1,2,0:T(4,128)(2,1)S(1)}, bf16[3,3,1,512]{3,1,2,0:T(4,128)(2,1)S(1)}, u32[]{:S(2)}, u32[]{:S(2)}) %collective-permute-start.1) | collective-permute-done | bytes 9248 | tf_op jit(solution)/shard_map/ppermute | solution.py:169
  10.7 2.2 %collective-permute-start.2 = (bf16[4,1,33,512]{3,2,1,0:T(8,128)(2,1)S(1)}, bf16[4,1,33,512]{3,2,1,0:T(8,128)(2,1)S(1)}, u32[]{:S(2)}, u32[]{:S(2)}) collective-permute-start(bf16[4,1,33,512]{3,2,1,0:T(8,128)(2,1)S(1)} %pad_maximum_fusion.16), channel_id=1, source_target_pairs={{0,4},{4,0},{8,12},{12,8},{1,5},{5,1},{9,13},{13,9},{2,6},{6,2},{1... | collective-permute-start | bytes 405512 | tf_op jit(solution)/shard_map/ppermute | solution.py:169
  12.9 2.5 %collective-permute-start.3 = (bf16[4,1,33,512]{3,2,1,0:T(8,128)(2,1)S(1)}, bf16[4,1,33,512]{3,2,1,0:T(8,128)(2,1)S(1)}, u32[]{:S(2)}, u32[]{:S(2)}) collective-permute-start(bf16[4,1,33,512]{3,2,1,0:T(8,128)(2,1)S(1)} %pad_maximum_fusion.16), channel_id=1, source_target_pairs={{0,12},{4,8},{8,4},{12,0},{1,13},{5,9},{9,5},{13,1},{2,14},{6,10},... | collective-permute-start | bytes 405512 | tf_op jit(solution)/shard_map/ppermute | solution.py:169
  16.0 1.2 %collective-permute-done.2 = bf16[4,1,33,512]{3,2,1,0:T(8,128)(2,1)S(1)} collective-permute-done((bf16[4,1,33,512]{3,2,1,0:T(8,128)(2,1)S(1)}, bf16[4,1,33,512]{3,2,1,0:T(8,128)(2,1)S(1)}, u32[]{:S(2)}, u32[]{:S(2)}) %collective-permute-start.2) | collective-permute-done | bytes 135200 | tf_op jit(solution)/shard_map/ppermute | solution.py:169
  17.3 5.0 %collective-permute-done.3 = bf16[4,1,33,512]{3,2,1,0:T(8,128)(2,1)S(1)} collective-permute-done((bf16[4,1,33,512]{3,2,1,0:T(8,128)(2,1)S(1)}, bf16[4,1,33,512]{3,2,1,0:T(8,128)(2,1)S(1)}, u32[]{:S(2)}, u32[]{:S(2)}) %collective-permute-start.3) | collective-permute-done | bytes 135200 | tf_op jit(solution)/shard_map/ppermute | solution.py:169
  24.7 1.3 %convolution_add_fusion.4 = bf16[192,256]{1,0:T(8,128)(2,1)S(1)} fusion(bf16[192,512]{1,0:T(8,128)(2,1)S(1)} %bitcast.125, bf16[3,3,512,256]{3,2,1,0:T(8,128)(2,1)} %param.13, f32[192,512]{1,0:T(8,128)S(1)} %fusion.15, f32[192,512]{1,0:T(8,128)S(1)} %fusion.11, f32[192,1024]{1,0:T(8,128)S(1)} %fusion.1), kind=kOutput, calls=%fused_computation.7 | convolution fusion | flops 50528256 | bytes 1146880 | tf_op jit(solution)/shard_map/dot_general | solution.py:123
  26.7 1.4 %convert_reduce_fusion.1 = (f32[256]{0:T(256)}, f32[256]{0:T(256)}, bf16[3,2,2,64,256]{4,1,3,0,2:T(2,128)(2,1)S(1)}) fusion(bf16[3,2,1,64,256]{4,1,3,0,2:T(2,128)(2,1)S(1)} %bitcast.128, bf16[3,2,1,64,256]{4,1,3,0,2:T(2,128)(2,1)S(1)} %bitcast.127), kind=kLoop, calls=%fused_computation.19 | loop fusion | flops 982528 | bytes 788480 | tf_op jit(solution)/shard_map/reduce_sum | solution.py:178
  28.1 0.7 copy-done.1
  29.0 0.7 copy.37
  29.8 0.7 reduce_sum.82
  34.0 1.5 %reshape_reshape.29 = bf16[2,1,64,256]{3,2,1,0:T(8,128)(2,1)} reshape(bf16[32768]{0:T(1024)(128)(2,1)} %fusion.38) | data formatting | bytes 131072 | tf_op jit(solution)/shard_map/reshape;reshape | solution.py:223
  35.5 1.0 pad_maximum_fusion.2
  36.6 1.9 %fusion.100 = (bf16[1,3,3,256,256]{4,3,2,1,0:T(8,128)(2,1)}, bf16[1,3,3,256,256]{4,3,2,1,0:T(8,128)(2,1)}, bf16[1,3,3,256,256]{4,3,2,1,0:T(8,128)(2,1)}) fusion(bf16[3,3,3,256,256]{4,3,2,1,0:T(8,128)(2,1)S(1)} %copy-done), kind=kLoop, calls=%fused_computation.247 | loop fusion | bytes 7077888 | tf_op jit(solution)/shard_map/slice | solution.py:154
  38.7 0.8 slice.730
  40.1 1.0 slice_select_fusion.1
  41.2 1.6 %collective-permute-start.6 = (bf16[5,5,1,256]{3,2,1,0:T(2,128)(2,1)S(1)}, bf16[5,5,1,256]{3,2,1,0:T(2,128)(2,1)S(1)}, u32[]{:S(2)}, u32[]{:S(2)}) collective-permute-start(bf16[5,5,1,256]{3,2,1,0:T(2,128)(2,1)S(1)} %pad_maximum_fusion.17), channel_id=1, source_target_pairs={{0,2},{2,0},{1,3},{3,1},{4,6},{6,4},{5,7},{7,5},{8,10},{10,8},{9,1... | collective-permute-start | bytes 38408 | tf_op jit(solution)/shard_map/ppermute | solution.py:169
  42.8 2.3 %collective-permute-done.6 = bf16[5,5,1,256]{3,2,1,0:T(2,128)(2,1)S(1)} collective-permute-done((bf16[5,5,1,256]{3,2,1,0:T(2,128)(2,1)S(1)}, bf16[5,5,1,256]{3,2,1,0:T(2,128)(2,1)S(1)}, u32[]{:S(2)}, u32[]{:S(2)}) %collective-permute-start.6) | collective-permute-done | bytes 12832 | tf_op jit(solution)/shard_map/ppermute | solution.py:169
  45.9 2.6 %collective-permute-start.8 = (bf16[6,1,66,256]{3,2,1,0:T(8,128)(2,1)S(1)}, bf16[6,1,66,256]{3,2,1,0:T(8,128)(2,1)S(1)}, u32[]{:S(2)}, u32[]{:S(2)}) collective-permute-start(bf16[6,1,66,256]{3,2,1,0:T(8,128)(2,1)S(1)} %get-tuple-element.64), channel_id=1, source_target_pairs={{0,12},{4,8},{8,4},{12,0},{1,13},{5,9},{9,5},{13,1},{2,14},{6,10},... | collective-permute-start | bytes 608264 | tf_op jit(solution)/shard_map/ppermute | solution.py:169
  48.6 1.9 %collective-permute-start.7 = (bf16[6,1,66,256]{3,2,1,0:T(8,128)(2,1)S(1)}, bf16[6,1,66,256]{3,2,1,0:T(8,128)(2,1)S(1)}, u32[]{:S(2)}, u32[]{:S(2)}) collective-permute-start(bf16[6,1,66,256]{3,2,1,0:T(8,128)(2,1)S(1)} %get-tuple-element.63), channel_id=1, source_target_pairs={{0,4},{4,0},{8,12},{12,8},{1,5},{5,1},{9,13},{13,9},{2,6},{6,2},{1... | collective-permute-start | bytes 608264 | tf_op jit(solution)/shard_map/ppermute | solution.py:169
  50.4 5.7 %collective-permute-done.8 = bf16[6,1,66,256]{3,2,1,0:T(8,128)(2,1)S(1)} collective-permute-done((bf16[6,1,66,256]{3,2,1,0:T(8,128)(2,1)S(1)}, bf16[6,1,66,256]{3,2,1,0:T(8,128)(2,1)S(1)}, u32[]{:S(2)}, u32[]{:S(2)}) %collective-permute-start.8) | collective-permute-done | bytes 202784 | tf_op jit(solution)/shard_map/ppermute | solution.py:169
  56.3 3.0 %collective-permute-done.7 = bf16[6,1,66,256]{3,2,1,0:T(8,128)(2,1)S(1)} collective-permute-done((bf16[6,1,66,256]{3,2,1,0:T(8,128)(2,1)S(1)}, bf16[6,1,66,256]{3,2,1,0:T(8,128)(2,1)S(1)}, u32[]{:S(2)}, u32[]{:S(2)}) %collective-permute-start.7) | collective-permute-done | bytes 202784 | tf_op jit(solution)/shard_map/ppermute | solution.py:169
  59.9 2.1 %select_convert_fusion.1 = bf16[5,6,66,256]{3,2,1,0:T(8,128)(2,1)S(1)} fusion(bf16[5,1,66,256]{3,2,1,0:T(8,128)(2,1)S(1)} %get-tuple-element.56, bf16[5,4,1,256]{3,2,1,0:T(2,128)(2,1)S(1)} %slice.732, bf16[3,4,64,256]{3,2,1,0:T(8,128)(2,1)S(1)} %bitcast.106, bf16[2,4,64,256]{3,2,1,0:T(8,128)(2,1)S(1)} %slice_select_fusion.1, ...), kind=kLoop, calls=%fused_computation.1 | loop fusion | flops 11151360 | bytes 2021772 | tf_op jit(solution)/shard_map/convert_element_type | solution.py:279
  63.8 1.0 fusion.98
  65.0 1.1 %fusion.103 = f32[768,256]{1,0:T(8,128)S(1)} fusion(bf16[768,2304]{1,0:T(8,128)(2,1)S(1)} %bitcast.115, bf16[2304,256]{1,0:T(8,128)(2,1)S(1)} %bitcast.119), kind=kOutput, calls=%fused_computation.250 | convolution fusion | flops 905969664 | bytes 5505024 | tf_op jit(solution)/shard_map/dot_general | solution.py:154
  66.3 1.1 %convolution_add_fusion.3 = f32[768,256]{1,0:T(8,128)S(1)} fusion(f32[768,256]{1,0:T(8,128)S(1)} %fusion.103, bf16[768,2304]{1,0:T(8,128)(2,1)S(1)} %bitcast.113, bf16[2304,256]{1,0:T(8,128)(2,1)S(1)} %bitcast.118), kind=kOutput, calls=%fused_computation.5 | convolution fusion | flops 906166272 | bytes 6291456 | tf_op jit(solution)/shard_map/dot_general | solution.py:154
  67.6 1.1 %convert_reduce_fusion = (f32[256]{0:T(256)S(1)}, f32[256]{0:T(256)S(1)}, bf16[768,256]{1,0:T(8,128)(2,1)S(1)}) fusion(f32[768,256]{1,0:T(8,128)S(1)} %convolution_add_fusion.3, bf16[768,2304]{1,0:T(8,128)(2,1)S(1)} %bitcast.111, bf16[2304,256]{1,0:T(8,128)(2,1)S(1)} %bitcast.117), kind=kOutput, calls=%fused_computation.17 | convolution fusion | flops 907148800 | bytes 5900288 | tf_op jit(solution)/shard_map/dot_general | solution.py:154
  69.5 1.6 %collective-permute-done.10 = bf16[2,5,64,256]{3,2,1,0:T(8,128)(2,1)S(1)} collective-permute-done((bf16[2,5,64,256]{3,2,1,0:T(8,128)(2,1)S(1)}, bf16[2,5,64,256]{3,2,1,0:T(8,128)(2,1)S(1)}, u32[]{:S(2)}, u32[]{:S(2)}) %collective-permute-start.10) | collective-permute-done | bytes 327712 | tf_op jit(solution)/shard_map/ppermute | solution.py:169
  71.8 1.6 %collective-permute-start.11 = (bf16[5,5,1,256]{3,2,1,0:T(2,128)(2,1)S(1)}, bf16[5,5,1,256]{3,2,1,0:T(2,128)(2,1)S(1)}, u32[]{:S(2)}, u32[]{:S(2)}) collective-permute-start(bf16[5,5,1,256]{3,2,1,0:T(2,128)(2,1)S(1)} %pad_maximum_fusion.18), channel_id=1, source_target_pairs={{0,2},{2,0},{1,3},{3,1},{4,6},{6,4},{5,7},{7,5},{8,10},{10,8},{9,1... | collective-permute-start | bytes 38408 | tf_op jit(solution)/shard_map/ppermute | solution.py:169
  73.3 2.4 %collective-permute-done.11 = bf16[5,5,1,256]{3,2,1,0:T(2,128)(2,1)S(1)} collective-permute-done((bf16[5,5,1,256]{3,2,1,0:T(2,128)(2,1)S(1)}, bf16[5,5,1,256]{3,2,1,0:T(2,128)(2,1)S(1)}, u32[]{:S(2)}, u32[]{:S(2)}) %collective-permute-start.11) | collective-permute-done | bytes 12832 | tf_op jit(solution)/shard_map/ppermute | solution.py:169
  77.2 2.5 %collective-permute-start.13 = (bf16[6,1,66,256]{3,2,1,0:T(8,128)(2,1)S(1)}, bf16[6,1,66,256]{3,2,1,0:T(8,128)(2,1)S(1)}, u32[]{:S(2)}, u32[]{:S(2)}) collective-permute-start(bf16[6,1,66,256]{3,2,1,0:T(8,128)(2,1)S(1)} %get-tuple-element.62), channel_id=1, source_target_pairs={{0,12},{4,8},{8,4},{12,0},{1,13},{5,9},{9,5},{13,1},{2,14},{6,10},... | collective-permute-start | bytes 608264 | tf_op jit(solution)/shard_map/ppermute | solution.py:169
  79.7 3.3 %fusion.99 = (bf16[1,3,3,256,256]{4,3,2,1,0:T(8,128)(2,1)S(1)}, bf16[1,3,3,256,256]{4,3,2,1,0:T(8,128)(2,1)}, bf16[1,3,3,256,256]{4,3,2,1,0:T(8,128)(2,1)S(1)}) fusion(bf16[3,3,3,256,256]{4,3,2,1,0:T(8,128)(2,1)} %param.19), kind=kLoop, calls=%fused_computation.246 | loop fusion | bytes 7077888 | tf_op jit(solution)/shard_map/slice | solution.py:154
  83.0 1.9 %collective-permute-start.12 = (bf16[6,1,66,256]{3,2,1,0:T(8,128)(2,1)}, bf16[6,1,66,256]{3,2,1,0:T(8,128)(2,1)}, u32[]{:S(2)}, u32[]{:S(2)}) collective-permute-start(bf16[6,1,66,256]{3,2,1,0:T(8,128)(2,1)} %get-tuple-element.61), channel_id=1, source_target_pairs={{0,4},{4,0},{8,12},{12,8},{1,5},{5,1},{9,13},{13,9},{2,6},{6,2},{1... | collective-permute-start | bytes 608264 | tf_op jit(solution)/shard_map/ppermute | solution.py:169
  86.2 0.8 slice.683
  87.7 2.6 %collective-permute-done.12 = bf16[6,1,66,256]{3,2,1,0:T(8,128)(2,1)} collective-permute-done((bf16[6,1,66,256]{3,2,1,0:T(8,128)(2,1)}, bf16[6,1,66,256]{3,2,1,0:T(8,128)(2,1)}, u32[]{:S(2)}, u32[]{:S(2)}) %collective-permute-start.12) | collective-permute-done | bytes 202784 | tf_op jit(solution)/shard_map/ppermute | solution.py:169
  90.3 0.8 slice.763
  91.0 0.8 slice.677
  92.9 1.0 %broadcast_select_fusion.4 = (bf16[5,1,66,256]{3,2,1,0:T(8,128)(2,1)S(1)}, bf16[5,1,66,256]{3,2,1,0:T(8,128)(2,1)S(1)}) fusion(pred[]{:T(512)S(6)} %eq.35, bf16[6,1,66,256]{3,2,1,0:T(8,128)(2,1)} %copy-done.7, bf16[6,1,66,256]{3,2,1,0:T(8,128)(2,1)} %collective-permute-done.12, pred[]{:T(512)S(6)} %eq.34), kind=kLoop, calls=%fused_computation.90 | loop fusion | flops 168960 | bytes 675842 | tf_op jit(solution)/shard_map/jit(_where)/select_n | solution.py:239
  93.9 1.9 %select_convert_fusion = bf16[5,6,66,256]{3,2,1,0:T(8,128)(2,1)S(1)} fusion(bf16[5,1,66,256]{3,2,1,0:T(8,128)(2,1)S(1)} %get-tuple-element.54, bf16[5,4,1,256]{3,2,1,0:T(2,128)(2,1)S(1)} %slice.758, bf16[3,4,64,256]{3,2,1,0:T(8,128)(2,1)S(1)} %bitcast.110, bf16[2,4,64,256]{3,2,1,0:T(8,128)(2,1)S(1)} %slice_select_fusion, ...), kind=kLoop, calls=%fused_computation | loop fusion | flops 11151360 | bytes 2021772 | tf_op jit(solution)/shard_map/convert_element_type | solution.py:279
  97.6 1.2 %fusion.97 = (bf16[3,4,64,2304]{3,2,1,0:T(8,128)(2,1)S(1)}, bf16[3,4,64,2304]{3,2,1,0:T(8,128)(2,1)S(1)}, bf16[3,4,64,2304]{3,2,1,0:T(8,128)(2,1)S(1)}) fusion(bf16[5,4,64,2304]{3,2,1,0:T(8,128)(2,1)S(1)} %slice_dynamic-update-slice_fusion), kind=kLoop, calls=%fused_computation.244 | loop fusion | bytes 21233664 | tf_op jit(solution)/shard_map/slice | solution.py:153
  98.9 1.1 %fusion.104 = f32[768,256]{1,0:T(8,128)S(1)} fusion(bf16[768,2304]{1,0:T(8,128)(2,1)S(1)} %bitcast.116, bf16[2304,256]{1,0:T(8,128)(2,1)S(1)} %bitcast.122), kind=kOutput, calls=%fused_computation.251 | convolution fusion | flops 905969664 | bytes 5505024 | tf_op jit(solution)/shard_map/dot_general | solution.py:154
  100.0 1.1 %convolution_add_fusion.1 = f32[768,256]{1,0:T(8,128)S(1)} fusion(f32[768,256]{1,0:T(8,128)S(1)} %fusion.104, bf16[768,2304]{1,0:T(8,128)(2,1)S(1)} %bitcast.114, bf16[2304,256]{1,0:T(8,128)(2,1)S(1)} %bitcast.121), kind=kOutput, calls=%fused_computation.3 | convolution fusion | flops 906166272 | bytes 6291456 | tf_op jit(solution)/shard_map/dot_general | solution.py:154
  101.1 1.1 %convolution_add_fusion = f32[768,256]{1,0:T(8,128)S(1)} fusion(f32[768,256]{1,0:T(8,128)S(1)} %convolution_add_fusion.1, bf16[768,2304]{1,0:T(8,128)(2,1)S(1)} %bitcast.112, bf16[2304,256]{1,0:T(8,128)(2,1)S(1)} %bitcast.120), kind=kOutput, calls=%fused_computation.2 | convolution fusion | flops 906166272 | bytes 6291456 | tf_op jit(solution)/shard_map/dot_general | solution.py:154
  102.2 0.9 add_convert_fusion
  (221 shorter events, 21.6 us)
Async XLA Ops:
  1.4 4.0 %collective-permute-start = (f32[2,32]{1,0:T(2,128)S(1)}, f32[2,32]{1,0:T(2,128)S(1)}, u32[]{:S(2)}, u32[]{:S(2)}) collective-permute-start(f32[2,32]{1,0:T(2,128)S(1)} %pad_maximum_fusion.22), channel_id=1, source_target_pairs={{0,1},{1,0},{2,3},{3,2},{4,5},{5,4},{6,7},{7,6},{8,9},{9,8},{10,11... | collective-permute-start | bytes 776 | tf_op jit(solution)/shard_map/ppermute | solution.py:169
  3.7 19.2 %copy-start.10 = (f32[512]{0:T(512)S(1)}, f32[512]{0:T(512)}, u32[]{:S(2)}) copy-start(f32[512]{0:T(512)} %param.12) | copy-start | bytes 6148
  3.7 19.2 %copy-start.11 = (f32[512]{0:T(512)S(1)}, f32[512]{0:T(512)}, u32[]{:S(2)}) copy-start(f32[512]{0:T(512)} %param.11) | copy-start | bytes 6148
  5.8 4.2 %collective-permute-start.1 = (bf16[3,3,1,512]{3,1,2,0:T(4,128)(2,1)S(1)}, bf16[3,3,1,512]{3,1,2,0:T(4,128)(2,1)S(1)}, u32[]{:S(2)}, u32[]{:S(2)}) collective-permute-start(bf16[3,3,1,512]{3,1,2,0:T(4,128)(2,1)S(1)} %pad_maximum_fusion.21), channel_id=1, source_target_pairs={{0,2},{2,0},{1,3},{3,1},{4,6},{6,4},{5,7},{7,5},{8,10},{10,8},{9,1... | collective-permute-start | bytes 27656 | tf_op jit(solution)/shard_map/ppermute | solution.py:169
  10.7 6.5 %collective-permute-start.2 = (bf16[4,1,33,512]{3,2,1,0:T(8,128)(2,1)S(1)}, bf16[4,1,33,512]{3,2,1,0:T(8,128)(2,1)S(1)}, u32[]{:S(2)}, u32[]{:S(2)}) collective-permute-start(bf16[4,1,33,512]{3,2,1,0:T(8,128)(2,1)S(1)} %pad_maximum_fusion.16), channel_id=1, source_target_pairs={{0,4},{4,0},{8,12},{12,8},{1,5},{5,1},{9,13},{13,9},{2,6},{6,2},{1... | collective-permute-start | bytes 405512 | tf_op jit(solution)/shard_map/ppermute | solution.py:169
  12.9 9.5 %collective-permute-start.3 = (bf16[4,1,33,512]{3,2,1,0:T(8,128)(2,1)S(1)}, bf16[4,1,33,512]{3,2,1,0:T(8,128)(2,1)S(1)}, u32[]{:S(2)}, u32[]{:S(2)}) collective-permute-start(bf16[4,1,33,512]{3,2,1,0:T(8,128)(2,1)S(1)} %pad_maximum_fusion.16), channel_id=1, source_target_pairs={{0,12},{4,8},{8,4},{12,0},{1,13},{5,9},{9,5},{13,1},{2,14},{6,10},... | collective-permute-start | bytes 405512 | tf_op jit(solution)/shard_map/ppermute | solution.py:169
  15.9 6.6 %collective-permute-start.4 = (f32[2,32]{1,0:T(2,128)S(1)}, f32[2,32]{1,0:T(2,128)S(1)}, u32[]{:S(2)}, u32[]{:S(2)}) collective-permute-start(f32[2,32]{1,0:T(2,128)S(1)} %get-tuple-element.27), channel_id=1, source_target_pairs={{0,8},{4,12},{8,0},{12,4},{1,9},{5,13},{9,1},{13,5},{2,10},{6,14},... | collective-permute-start | bytes 776 | tf_op jit(solution)/shard_map/ppermute | solution.py:169
  24.7 11.9 %copy-start = (bf16[3,3,3,256,256]{4,3,2,1,0:T(8,128)(2,1)S(1)}, bf16[3,3,3,256,256]{4,3,2,1,0:T(8,128)(2,1)}, u32[]{:S(2)}) copy-start(bf16[3,3,3,256,256]{4,3,2,1,0:T(8,128)(2,1)} %param.16) | copy-start | bytes 10616836
  28.1 0.7 copy-start.1
  36.5 2.0 %copy-start.2 = (bf16[3,2,2,64,256]{4,1,3,0,2:T(2,128)(2,1)S(1)}, bf16[3,2,2,64,256]{4,1,3,0,2:T(2,128)(2,1)}, u32[]{:S(2)}) copy-start(bf16[3,2,2,64,256]{4,1,3,0,2:T(2,128)(2,1)} %copy-done.1) | copy-start | bytes 1179652
  36.5 3.2 %copy-start.8 = (f32[32]{0:T(128)S(1)}, f32[32]{0:T(128)}, u32[]{:S(2)}) copy-start(f32[32]{0:T(128)} %reduce_sum.83) | copy-start | bytes 388
  36.5 3.2 %copy-start.9 = (f32[32]{0:T(128)S(1)}, f32[32]{0:T(128)}, u32[]{:S(2)}) copy-start(f32[32]{0:T(128)} %reduce_sum.89) | copy-start | bytes 388
  36.5 2.1 %collective-permute-start.5 = (bf16[2,5,64,256]{3,2,1,0:T(8,128)(2,1)S(1)}, bf16[2,5,64,256]{3,2,1,0:T(8,128)(2,1)}, u32[]{:S(2)}, u32[]{:S(2)}) collective-permute-start(bf16[2,5,64,256]{3,2,1,0:T(8,128)(2,1)S(1)} %pad_maximum_fusion.2), channel_id=1, source_target_pairs={{0,1},{1,0},{2,3},{3,2},{4,5},{5,4},{6,7},{7,6},{8,9},{9,8},{10,11... | collective-permute-start | bytes 983048 | tf_op jit(solution)/shard_map/ppermute | solution.py:169
  39.7 8.8 %copy-start.16 = (pred[6]{0:T(512)(128)(4,1)S(1)}, pred[6]{0:T(512)(128)(4,1)}, u32[]{:S(2)}) copy-start(pred[6]{0:T(512)(128)(4,1)} %or_and_fusion.1) | copy-start | bytes 22
  41.1 18.7 %copy-start.12 = (f32[256]{0:T(256)S(1)}, f32[256]{0:T(256)}, u32[]{:S(2)}) copy-start(f32[256]{0:T(256)} %param.15) | copy-start | bytes 3076
  41.2 18.7 %copy-start.13 = (f32[256]{0:T(256)S(1)}, f32[256]{0:T(256)}, u32[]{:S(2)}) copy-start(f32[256]{0:T(256)} %param.14) | copy-start | bytes 3076
  41.2 3.9 %collective-permute-start.6 = (bf16[5,5,1,256]{3,2,1,0:T(2,128)(2,1)S(1)}, bf16[5,5,1,256]{3,2,1,0:T(2,128)(2,1)S(1)}, u32[]{:S(2)}, u32[]{:S(2)}) collective-permute-start(bf16[5,5,1,256]{3,2,1,0:T(2,128)(2,1)S(1)} %pad_maximum_fusion.17), channel_id=1, source_target_pairs={{0,2},{2,0},{1,3},{3,1},{4,6},{6,4},{5,7},{7,5},{8,10},{10,8},{9,1... | collective-permute-start | bytes 38408 | tf_op jit(solution)/shard_map/ppermute | solution.py:169
  45.9 10.3 %collective-permute-start.8 = (bf16[6,1,66,256]{3,2,1,0:T(8,128)(2,1)S(1)}, bf16[6,1,66,256]{3,2,1,0:T(8,128)(2,1)S(1)}, u32[]{:S(2)}, u32[]{:S(2)}) collective-permute-start(bf16[6,1,66,256]{3,2,1,0:T(8,128)(2,1)S(1)} %get-tuple-element.64), channel_id=1, source_target_pairs={{0,12},{4,8},{8,4},{12,0},{1,13},{5,9},{9,5},{13,1},{2,14},{6,10},... | collective-permute-start | bytes 608264 | tf_op jit(solution)/shard_map/ppermute | solution.py:169
  48.5 10.9 %collective-permute-start.9 = (f32[2,32]{1,0:T(2,128)S(1)}, f32[2,32]{1,0:T(2,128)S(1)}, u32[]{:S(2)}, u32[]{:S(2)}) collective-permute-start(f32[2,32]{1,0:T(2,128)S(1)} %get-tuple-element.22), channel_id=1, source_target_pairs={{0,8},{4,12},{8,0},{12,4},{1,9},{5,13},{9,1},{13,5},{2,10},{6,14},... | collective-permute-start | bytes 776 | tf_op jit(solution)/shard_map/ppermute | solution.py:169
  48.6 10.7 %collective-permute-start.7 = (bf16[6,1,66,256]{3,2,1,0:T(8,128)(2,1)S(1)}, bf16[6,1,66,256]{3,2,1,0:T(8,128)(2,1)S(1)}, u32[]{:S(2)}, u32[]{:S(2)}) collective-permute-start(bf16[6,1,66,256]{3,2,1,0:T(8,128)(2,1)S(1)} %get-tuple-element.63), channel_id=1, source_target_pairs={{0,4},{4,0},{8,12},{12,8},{1,5},{5,1},{9,13},{13,9},{2,6},{6,2},{1... | collective-permute-start | bytes 608264 | tf_op jit(solution)/shard_map/ppermute | solution.py:169
  63.8 1.3 %copy-start.5 = (bf16[1,3,3,256,256]{4,3,2,1,0:T(8,128)(2,1)S(1)}, bf16[1,3,3,256,256]{4,3,2,1,0:T(8,128)(2,1)}, u32[]{:S(2)}) copy-start(bf16[1,3,3,256,256]{4,3,2,1,0:T(8,128)(2,1)} %get-tuple-element.40) | copy-start | bytes 3538948
  65.0 1.3 %copy-start.4 = (bf16[1,3,3,256,256]{4,3,2,1,0:T(8,128)(2,1)S(1)}, bf16[1,3,3,256,256]{4,3,2,1,0:T(8,128)(2,1)}, u32[]{:S(2)}) copy-start(bf16[1,3,3,256,256]{4,3,2,1,0:T(8,128)(2,1)} %get-tuple-element.41) | copy-start | bytes 3538948
  66.3 1.3 %copy-start.3 = (bf16[1,3,3,256,256]{4,3,2,1,0:T(8,128)(2,1)S(1)}, bf16[1,3,3,256,256]{4,3,2,1,0:T(8,128)(2,1)}, u32[]{:S(2)}) copy-start(bf16[1,3,3,256,256]{4,3,2,1,0:T(8,128)(2,1)} %get-tuple-element.39) | copy-start | bytes 3538948
  69.4 1.7 %collective-permute-start.10 = (bf16[2,5,64,256]{3,2,1,0:T(8,128)(2,1)S(1)}, bf16[2,5,64,256]{3,2,1,0:T(8,128)(2,1)S(1)}, u32[]{:S(2)}, u32[]{:S(2)}) collective-permute-start(bf16[2,5,64,256]{3,2,1,0:T(8,128)(2,1)S(1)} %pad_maximum_fusion.3), channel_id=1, source_target_pairs={{0,1},{1,0},{2,3},{3,2},{4,5},{5,4},{6,7},{7,6},{8,9},{9,8},{10,11... | collective-permute-start | bytes 983048 | tf_op jit(solution)/shard_map/ppermute | solution.py:169
  71.8 3.9 %collective-permute-start.11 = (bf16[5,5,1,256]{3,2,1,0:T(2,128)(2,1)S(1)}, bf16[5,5,1,256]{3,2,1,0:T(2,128)(2,1)S(1)}, u32[]{:S(2)}, u32[]{:S(2)}) collective-permute-start(bf16[5,5,1,256]{3,2,1,0:T(2,128)(2,1)S(1)} %pad_maximum_fusion.18), channel_id=1, source_target_pairs={{0,2},{2,0},{1,3},{3,1},{4,6},{6,4},{5,7},{7,5},{8,10},{10,8},{9,1... | collective-permute-start | bytes 38408 | tf_op jit(solution)/shard_map/ppermute | solution.py:169
  77.1 16.8 %copy-start.14 = (f32[256]{0:T(256)S(1)}, f32[256]{0:T(256)}, u32[]{:S(2)}) copy-start(f32[256]{0:T(256)} %param.18) | copy-start | bytes 3076
  77.1 16.8 %copy-start.15 = (f32[256]{0:T(256)S(1)}, f32[256]{0:T(256)}, u32[]{:S(2)}) copy-start(f32[256]{0:T(256)} %param.17) | copy-start | bytes 3076
  77.2 8.3 %collective-permute-start.13 = (bf16[6,1,66,256]{3,2,1,0:T(8,128)(2,1)S(1)}, bf16[6,1,66,256]{3,2,1,0:T(8,128)(2,1)S(1)}, u32[]{:S(2)}, u32[]{:S(2)}) collective-permute-start(bf16[6,1,66,256]{3,2,1,0:T(8,128)(2,1)S(1)} %get-tuple-element.62), channel_id=1, source_target_pairs={{0,12},{4,8},{8,4},{12,0},{1,13},{5,9},{9,5},{13,1},{2,14},{6,10},... | collective-permute-start | bytes 608264 | tf_op jit(solution)/shard_map/ppermute | solution.py:169
  83.0 9.5 %collective-permute-start.14 = (f32[2,32]{1,0:T(2,128)S(1)}, f32[2,32]{1,0:T(2,128)S(1)}, u32[]{:S(2)}, u32[]{:S(2)}) collective-permute-start(f32[2,32]{1,0:T(2,128)S(1)} %get-tuple-element.15), channel_id=1, source_target_pairs={{0,8},{4,12},{8,0},{12,4},{1,9},{5,13},{9,1},{13,5},{2,10},{6,14},... | collective-permute-start | bytes 776 | tf_op jit(solution)/shard_map/ppermute | solution.py:169
  83.0 7.3 %collective-permute-start.12 = (bf16[6,1,66,256]{3,2,1,0:T(8,128)(2,1)}, bf16[6,1,66,256]{3,2,1,0:T(8,128)(2,1)}, u32[]{:S(2)}, u32[]{:S(2)}) collective-permute-start(bf16[6,1,66,256]{3,2,1,0:T(8,128)(2,1)} %get-tuple-element.61), channel_id=1, source_target_pairs={{0,4},{4,0},{8,12},{12,8},{1,5},{5,1},{9,13},{13,9},{2,6},{6,2},{1... | collective-permute-start | bytes 608264 | tf_op jit(solution)/shard_map/ppermute | solution.py:169
  85.5 0.7 copy-start.7
  97.6 1.3 %copy-start.6 = (bf16[1,3,3,256,256]{4,3,2,1,0:T(8,128)(2,1)S(1)}, bf16[1,3,3,256,256]{4,3,2,1,0:T(8,128)(2,1)}, u32[]{:S(2)}) copy-start(bf16[1,3,3,256,256]{4,3,2,1,0:T(8,128)(2,1)} %get-tuple-element.37) | copy-start | bytes 3538948

commit v9 on v6

--- a/solution.py
+++ b/solution.py
@@ -143,18 +143,15 @@
 
 
 def valid_conv(padded, kernel, frames, height, across):
-    channels = padded.shape[-1]
-    wide = jnp.concatenate(
-        [padded[:, dy : dy + height, dx : dx + across] for dy in range(3) for dx in range(3)], axis=-1
-    )
-    result = None
-    for step_t in range(3):
-        window = wide[step_t : step_t + frames].reshape(-1, 9 * channels)
-        part = jnp.dot(
-            window, kernel[step_t].reshape(9 * channels, -1), preferred_element_type=jnp.float32
-        )
-        result = part if result is None else result + part
-    return result.reshape(frames, height, across, -1)
+    out = lax.conv_general_dilated(
+        padded[None],
+        kernel,
+        (1, 1, 1),
+        "VALID",
+        dimension_numbers=("NDHWC", "DHWIO", "NDHWC"),
+        preferred_element_type=jnp.float32,
+    )
+    return out[0]
 
 
 def conv_halo(values):
@@ -175,8 +172,11 @@
 
 
 def local_sums(values):
-    grouped = values.reshape(-1, GROUPS, values.shape[-1] // GROUPS)
-    return jnp.stack([jnp.sum(grouped, axis=(0, 2)), jnp.sum(grouped * grouped, axis=(0, 2))])
+    channels = values.shape[-1]
+    flat = values.reshape(-1, channels)
+    per_channel = jnp.stack([jnp.sum(flat, axis=0), jnp.sum(flat * flat, axis=0)])
+    member = jnp.arange(channels)[:, None] // (channels // GROUPS) == jnp.arange(GROUPS)[None, :]
+    return jnp.dot(per_channel, member.astype(jnp.float32), precision=lax.Precision.HIGHEST)
 
 
 def finish_stats(sums, values):

time: 97.2 us -> 184 us (1.89)
  local copies, waits for them, and re-layouts: 26.6 us -> 80 us
  other arithmetic: 18.3 us -> 51 us
  matrix products: 8.74 us -> 12 us
  waiting for transfers between devices: 22.1 us -> 19.2 us
    reshape x8, local copies, waits for them, and re-layouts: 0.25 us -> 9.52 us  [swap_with(): message = jnp.concatenate([payload.reshape(-1, width), packed], axis=0)]
    unnamed x57 -> x69, local copies, waits for them, and re-layouts: 6.36 us -> 13.7 us
    slice x4 -> x0, local copies, waits for them, and re-layouts: 7.3 us -> none  [the longest x2 5.11 us: valid_conv(): kernel[step_t].reshape(9 * channels, -1)]
    conv_general_dilated x0 -> x2, matrix products: none -> 7.28 us  [valid_conv(): lax.conv_general_dilated(padded[None], kernel, (1, 1, 1), 'VALID', dimens...]
    concatenate x2 -> x4, local copies, waits for them, and re-layouts: 0.5 us -> 6.54 us  [fast_conv_input(): x = jnp.concatenate([above, x, below], axis=1)]
    another operation x17 -> x12, other arithmetic: 0.78 us -> 6.63 us  [the longest x3 0.61 us: local_sums(): jnp.stack([jnp.sum(grouped, axis=(0, 2)), jnp.sum(grouped * grouped, axis...]
    reshape x6 -> x8, local copies, waits for them, and re-layouts: 0.5 us -> 5.93 us  [pack_sums(): high.reshape(-1)]
    reshape x6 -> x8, local copies, waits for them, and re-layouts: 0.5 us -> 5.42 us  [pack_sums(): low.reshape(-1)]
  transfers between devices with their start and end apart: 15 -> 15, of which waited for: 8 -> 9; matrix products, arithmetic and copies ran while one was open for 9% -> 10% of each run, Pallas kernels for 0% -> 0%
where the time goes in v9:
time: 184 us; the launch traced here: 183 us
  local copies, waits for them, and re-layouts  80 us (43%)
  other arithmetic  51 us (28%)
  starting transfers between devices  19.9 us (11%)
  waiting for transfers between devices  19.2 us (10%)
  matrix products  12 us (7%)
    ppermute x15, starting transfers between devices, swap(): return lax.ppermute(x, axis, [(i, i ^ distance) for i in range(size)])  19.9 us
    ppermute x15, waiting for transfers between devices, swap(): return lax.ppermute(x, axis, [(i, i ^ distance) for i in range(size)])  19.2 us
    unnamed x69, local copies, waits for them, and re-layouts  13.7 us
    reshape x8, local copies, waits for them, and re-layouts, swap_with(): message = jnp.concatenate([payload.reshape(-1, width), packed], axis=0)  9.52 us
    conv_general_dilated x2, matrix products, valid_conv(): lax.conv_general_dilated(padded[None], kernel, (1, 1, 1), 'VALID', dimens...  7.28 us
    another operation x12, other arithmetic  6.63 us
    concatenate x4, local copies, waits for them, and re-layouts, fast_conv_input(): x = jnp.concatenate([above, x, below], axis=1)  6.54 us
    reshape x8, local copies, waits for them, and re-layouts, pack_sums(): high.reshape(-1)  5.93 us
  transfers between devices with their start and end apart: 15, of which 9 were waited for; matrix products, arithmetic and copies ran while one was open for 10% of the time, Pallas kernels for 0%

profile of v9, /device:TPU:0, one launch (start us, length us, event | category | flops | bytes accessed | tf_op | source)
XLA Modules:
  0.0 182.5 jit_solution(8001288536047963173)
XLA Ops:
  2.5 2.8 %slice_bitcast_fusion.7 = (bf16[512,256]{1,0:T(8,128)(2,1)}, bf16[512,256]{1,0:T(8,128)(2,1)}, bf16[512,256]{1,0:T(8,128)(2,1)}, bf16[512,256]{1,0:T(8,128)(2,1)...) fusion(bf16[3,3,512,256]{3,2,1,0:T(8,128)(2,1)} %param.13), kind=kLoop, calls=%fused_computation.75 | loop fusion | bytes 4194304 | tf_op jit(solution)/shard_map/squeeze | solution.py:129
  12.5 2.5 %collective-permute-start.1 = (bf16[7,512]{1,0:T(8,128)(2,1)}, bf16[7,512]{1,0:T(8,128)(2,1)S(1)}, u32[]{:S(2)}, u32[]{:S(2)}) collective-permute-start(bf16[7,512]{1,0:T(8,128)(2,1)} %pad_maximum_fusion.15), channel_id=1, source_target_pairs={{0,2},{2,0},{1,3},{3,1},{4,6},{6,4},{5,7},{7,5},{8,10},{10,8},{9,1... | collective-permute-start | bytes 21512 | tf_op jit(solution)/shard_map/ppermute | solution.py:167
  15.0 1.6 constant_dynamic-update-slice_fusion.1
  19.3 1.3 reshape.944
  25.1 1.6 slice.538
  26.6 1.6 reshape.941
  29.1 4.2 %collective-permute-start.3 = (bf16[100,512]{1,0:T(8,128)(2,1)S(1)}, bf16[100,512]{1,0:T(8,128)(2,1)S(1)}, u32[]{:S(2)}, u32[]{:S(2)}) collective-permute-start(bf16[100,512]{1,0:T(8,128)(2,1)S(1)} %pad_maximum_fusion.10), channel_id=1, source_target_pairs={{0,12},{4,8},{8,4},{12,0},{1,13},{5,9},{9,5},{13,1},{2,14},{6,10},... | collective-permute-start | bytes 307208 | tf_op jit(solution)/shard_map/ppermute | solution.py:167
  34.5 2.6 %collective-permute-done.3 = bf16[100,512]{1,0:T(8,128)(2,1)S(1)} collective-permute-done((bf16[100,512]{1,0:T(8,128)(2,1)S(1)}, bf16[100,512]{1,0:T(8,128)(2,1)S(1)}, u32[]{:S(2)}, u32[]{:S(2)}) %collective-permute-start.3) | collective-permute-done | bytes 102432 | tf_op jit(solution)/shard_map/ppermute | solution.py:167
  42.0 1.6 slice_select_fusion
  43.5 1.6 select_n.222
  47.9 1.4 select_convert_fusion.2
  53.1 1.6 convert_reduce_fusion
  59.0 1.8 copy.34
  66.9 1.5 fusion.60
  69.7 1.5 collective-permute-start.6
  71.9 1.8 collective-permute-done.6
  76.2 1.3 reshape.971
  81.9 2.4 %fusion.168 = (bf16[1,5,4,66,256]{4,3,2,1,0:T(8,128)(2,1)}, bf16[5,4,66,256]{3,2,1,0:T(8,128)(2,1)S(1)}) fusion(bf16[5,4,1,256]{3,2,1,0:T(2,128)(2,1)} %reshape.1031, bf16[3,4,64,256]{3,2,1,0:T(8,128)(2,1)} %bitcast.125, bf16[2,4,64,256]{3,2,1,0:T(8,128)(2,1)} %copy-done.2), kind=kLoop, calls=%fused_computation.303 | loop fusion | flops 2703360 | bytes 2017280 | tf_op jit(solution)/shard_map/concatenate | solution.py:252
  85.0 1.6 reshape.968
  86.7 1.6 reshape.973
  89.3 2.8 %collective-permute-start.8 = (bf16[331,256]{1,0:T(8,128)(2,1)S(1)}, bf16[331,256]{1,0:T(8,128)(2,1)S(1)}, u32[]{:S(2)}, u32[]{:S(2)}) collective-permute-start(bf16[331,256]{1,0:T(8,128)(2,1)S(1)} %get-tuple-element.61), channel_id=1, source_target_pairs={{0,12},{4,8},{8,4},{12,0},{1,13},{5,9},{9,5},{13,1},{2,14},{6,10},... | collective-permute-start | bytes 508424 | tf_op jit(solution)/shard_map/ppermute | solution.py:167
  92.8 1.6 collective-permute-start.7
  94.4 2.8 %collective-permute-done.8 = bf16[331,256]{1,0:T(8,128)(2,1)S(1)} collective-permute-done((bf16[331,256]{1,0:T(8,128)(2,1)S(1)}, bf16[331,256]{1,0:T(8,128)(2,1)S(1)}, u32[]{:S(2)}, u32[]{:S(2)}) %collective-permute-start.8) | collective-permute-done | bytes 169504 | tf_op jit(solution)/shard_map/ppermute | solution.py:167
  98.0 2.7 %collective-permute-done.7 = bf16[331,256]{1,0:T(8,128)(2,1)S(1)} collective-permute-done((bf16[331,256]{1,0:T(8,128)(2,1)S(1)}, bf16[331,256]{1,0:T(8,128)(2,1)S(1)}, u32[]{:S(2)}, u32[]{:S(2)}) %collective-permute-start.7) | collective-permute-done | bytes 169504 | tf_op jit(solution)/shard_map/ppermute | solution.py:167
  103.9 1.8 broadcast_select_fusion.7
  105.6 1.6 concatenate.164
  107.3 1.6 concatenate.162
  111.7 2.1 %fusion.25 = bf16[5,6,1,66,256]{4,3,1,0,2:T(8,128)(2,1)S(1)} fusion(bf16[1,5,1,66,256]{4,3,2,1,0:T(8,128)(2,1)} %bitcast.142, bf16[1,5,4,66,256]{4,3,2,1,0:T(8,128)(2,1)} %get-tuple-element.41, bf16[1,5,1,66,256]{4,3,2,1,0:T(8,128)(2,1)} %bitcast.144, f32[256]{0:T(256)} %param.15, f32[256]{0:T(256)} %param.14, f32[256]{0:T(256)} %mul.202, f32[256]{0:T(256)} %sub.267, ...), kind=kLoop, calls=%fused_computation.21 | loop fusion | flops 6589440 | bytes 2032012 | tf_op jit(solution)/shard_map/convert_element_type | solution.py:275
  115.0 4.0 %fusion.35 = (f32[256]{0:T(256)S(1)}, f32[256]{0:T(256)S(1)}, bf16[3,4,8,9,256]{4,2,3,1,0:T(8,128)(2,1)}) fusion(pred[8,9]{0,1:T(8,128)(4,1)S(1)} %copy-done.30, bf16[3,3,3,256,256]{4,3,2,1,0:T(8,128)(2,1)S(1)} %copy-done, bf16[5,6,1,7,2,256]{5,3,4,1,0,2:T(8,128)(2,1)S(1)} %slice.589, bf16[5,6,1,8,9,256]{5,3,4,1,0,2:T(8,128)(2,1)S(1)} %copy.43), kind=kOutput, calls=%fused_computation.35 | convolution fusion | flops 3063471616 | bytes 5304392 | tf_op jit(solution)/shard_map/conv_general_dilated | solution.py:146
  128.9 1.5 fusion.61
  131.1 1.6 collective-permute-start.11
  132.7 2.2 %collective-permute-done.11 = bf16[21,256]{1,0:T(8,128)(2,1)S(1)} collective-permute-done((bf16[21,256]{1,0:T(8,128)(2,1)S(1)}, bf16[21,256]{1,0:T(8,128)(2,1)S(1)}, u32[]{:S(2)}, u32[]{:S(2)}) %collective-permute-start.11) | collective-permute-done | bytes 10784 | tf_op jit(solution)/shard_map/ppermute | solution.py:167
  135.6 1.3 fusion.124
  137.4 1.3 reshape.989
  139.9 1.3 reshape.987
  143.2 2.4 %fusion.167 = (bf16[1,5,4,66,256]{4,3,2,1,0:T(8,128)(2,1)}, bf16[5,4,66,256]{3,2,1,0:T(8,128)(2,1)S(1)}) fusion(bf16[5,4,1,256]{3,2,1,0:T(2,128)(2,1)} %reshape.1032, bf16[3,4,64,256]{3,2,1,0:T(8,128)(2,1)} %bitcast.130, bf16[2,4,64,256]{3,2,1,0:T(8,128)(2,1)} %copy-done.3), kind=kLoop, calls=%fused_computation.302 | loop fusion | flops 2703360 | bytes 2017280 | tf_op jit(solution)/shard_map/concatenate | solution.py:252
  146.3 1.6 reshape.986
  148.0 1.6 reshape.991
  150.6 2.8 %collective-permute-start.13 = (bf16[331,256]{1,0:T(8,128)(2,1)S(1)}, bf16[331,256]{1,0:T(8,128)(2,1)S(1)}, u32[]{:S(2)}, u32[]{:S(2)}) collective-permute-start(bf16[331,256]{1,0:T(8,128)(2,1)S(1)} %get-tuple-element.52), channel_id=1, source_target_pairs={{0,12},{4,8},{8,4},{12,0},{1,13},{5,9},{9,5},{13,1},{2,14},{6,10},... | collective-permute-start | bytes 508424 | tf_op jit(solution)/shard_map/ppermute | solution.py:167
  153.4 1.7 collective-permute-start.12
  155.1 4.1 %collective-permute-done.13 = bf16[331,256]{1,0:T(8,128)(2,1)S(1)} collective-permute-done((bf16[331,256]{1,0:T(8,128)(2,1)S(1)}, bf16[331,256]{1,0:T(8,128)(2,1)S(1)}, u32[]{:S(2)}, u32[]{:S(2)}) %collective-permute-start.13) | collective-permute-done | bytes 169504 | tf_op jit(solution)/shard_map/ppermute | solution.py:167
  160.0 1.9 %collective-permute-done.12 = bf16[331,256]{1,0:T(8,128)(2,1)S(1)} collective-permute-done((bf16[331,256]{1,0:T(8,128)(2,1)S(1)}, bf16[331,256]{1,0:T(8,128)(2,1)S(1)}, u32[]{:S(2)}, u32[]{:S(2)}) %collective-permute-start.12) | collective-permute-done | bytes 169504 | tf_op jit(solution)/shard_map/ppermute | solution.py:167
  165.2 1.8 broadcast_select_fusion.6
  166.9 1.6 concatenate.178
  168.6 1.6 concatenate.176
  173.0 2.1 %fusion.26 = bf16[5,6,1,66,256]{4,3,1,0,2:T(8,128)(2,1)S(1)} fusion(bf16[1,5,1,66,256]{4,3,2,1,0:T(8,128)(2,1)} %bitcast.141, bf16[1,5,4,66,256]{4,3,2,1,0:T(8,128)(2,1)} %get-tuple-element.39, bf16[1,5,1,66,256]{4,3,2,1,0:T(8,128)(2,1)} %bitcast.143, f32[256]{0:T(256)} %param.18, f32[256]{0:T(256)} %param.17, f32[256]{0:T(256)} %mul.216, f32[256]{0:T(256)} %sub.289, ...), kind=kLoop, calls=%fused_computation.22 | loop fusion | flops 6589440 | bytes 2032012 | tf_op jit(solution)/shard_map/convert_element_type | solution.py:275
  175.9 1.4 copy-done.27
  177.4 3.2 %fusion.16 = f32[3,4,8,9,256]{4,2,3,1,0:T(8,128)S(1)} fusion(bf16[3,3,3,256,256]{4,3,2,1,0:T(8,128)(2,1)S(1)} %copy-done.27, bf16[5,6,1,7,2,256]{5,3,4,1,0,2:T(8,128)(2,1)S(1)} %slice.617, bf16[5,6,1,8,9,256]{5,3,4,1,0,2:T(8,128)(2,1)S(1)} %copy.56, pred[8,9]{0,1:T(8,128)(4,1)S(1)} %copy-done.31), kind=kOutput, calls=%fused_computation.17 | convolution fusion | flops 3061923840 | bytes 5744712 | tf_op jit(solution)/shard_map/conv_general_dilated | solution.py:146
  (251 shorter events, 86.0 us)
Async XLA Ops:
  0.0 114.6 %copy-start = (bf16[3,3,3,256,256]{4,3,2,1,0:T(8,128)(2,1)S(1)}, bf16[3,3,3,256,256]{4,3,2,1,0:T(8,128)(2,1)}, u32[]{:S(2)}) copy-start(bf16[3,3,3,256,256]{4,3,2,1,0:T(8,128)(2,1)} %param.16) | copy-start | bytes 10616836
  2.0 4.8 %collective-permute-start = (f32[2,32]{1,0:T(2,128)}, f32[2,32]{1,0:T(2,128)}, u32[]{:S(2)}, u32[]{:S(2)}) collective-permute-start(f32[2,32]{1,0:T(2,128)} %fusion.54), channel_id=1, source_target_pairs={{0,1},{1,0},{2,3},{3,2},{4,5},{5,4},{6,7},{7,6},{8,9},{9,8},{10,11... | collective-permute-start | bytes 776 | tf_op jit(solution)/shard_map/ppermute | solution.py:167
  12.5 4.3 %collective-permute-start.1 = (bf16[7,512]{1,0:T(8,128)(2,1)}, bf16[7,512]{1,0:T(8,128)(2,1)S(1)}, u32[]{:S(2)}, u32[]{:S(2)}) collective-permute-start(bf16[7,512]{1,0:T(8,128)(2,1)} %pad_maximum_fusion.15), channel_id=1, source_target_pairs={{0,2},{2,0},{1,3},{3,1},{4,6},{6,4},{5,7},{7,5},{8,10},{10,8},{9,1... | collective-permute-start | bytes 21512 | tf_op jit(solution)/shard_map/ppermute | solution.py:167
  16.9 6.9 %copy-start.20 = (bf16[7,512]{1,0:T(8,128)(2,1)}, bf16[7,512]{1,0:T(8,128)(2,1)S(1)}, u32[]{:S(2)}) copy-start(bf16[7,512]{1,0:T(8,128)(2,1)S(1)} %collective-permute-done.1) | copy-start | bytes 21508
  29.1 8.0 %collective-permute-start.3 = (bf16[100,512]{1,0:T(8,128)(2,1)S(1)}, bf16[100,512]{1,0:T(8,128)(2,1)S(1)}, u32[]{:S(2)}, u32[]{:S(2)}) collective-permute-start(bf16[100,512]{1,0:T(8,128)(2,1)S(1)} %pad_maximum_fusion.10), channel_id=1, source_target_pairs={{0,12},{4,8},{8,4},{12,0},{1,13},{5,9},{9,5},{13,1},{2,14},{6,10},... | collective-permute-start | bytes 307208 | tf_op jit(solution)/shard_map/ppermute | solution.py:167
  33.9 4.8 %collective-permute-start.2 = (bf16[100,512]{1,0:T(8,128)(2,1)S(1)}, bf16[100,512]{1,0:T(8,128)(2,1)S(1)}, u32[]{:S(2)}, u32[]{:S(2)}) collective-permute-start(bf16[100,512]{1,0:T(8,128)(2,1)S(1)} %pad_maximum_fusion.10), channel_id=1, source_target_pairs={{0,4},{4,0},{8,12},{12,8},{1,5},{5,1},{9,13},{13,9},{2,6},{6,2},{1... | collective-permute-start | bytes 307208 | tf_op jit(solution)/shard_map/ppermute | solution.py:167
  33.9 6.9 %collective-permute-start.4 = (f32[2,32]{1,0:T(2,128)S(1)}, f32[2,32]{1,0:T(2,128)S(1)}, u32[]{:S(2)}, u32[]{:S(2)}) collective-permute-start(f32[2,32]{1,0:T(2,128)S(1)} %get-tuple-element.21), channel_id=1, source_target_pairs={{0,8},{4,12},{8,0},{12,4},{1,9},{5,13},{9,1},{13,5},{2,10},{6,14},... | collective-permute-start | bytes 776 | tf_op jit(solution)/shard_map/ppermute | solution.py:167
  37.1 0.6 copy-start.18
  38.7 0.6 copy-start.19
  47.9 1.5 copy-start.11
  47.9 1.6 copy-start.12
  47.9 1.8 %copy-start.9 = (bf16[512,256]{1,0:T(8,128)(2,1)S(1)}, bf16[512,256]{1,0:T(8,128)(2,1)}, u32[]{:S(2)}) copy-start(bf16[512,256]{1,0:T(8,128)(2,1)} %get-tuple-element.26) | copy-start | bytes 786436
  47.9 1.8 %copy-start.10 = (bf16[512,256]{1,0:T(8,128)(2,1)S(1)}, bf16[512,256]{1,0:T(8,128)(2,1)}, u32[]{:S(2)}) copy-start(bf16[512,256]{1,0:T(8,128)(2,1)} %get-tuple-element.27) | copy-start | bytes 786436
  49.3 1.0 copy-start.5
  49.3 1.0 copy-start.6
  49.3 1.1 copy-start.7
  49.3 1.2 copy-start.8
  50.9 3.8 %copy-start.28 = (s32[256]{0:T(256)S(1)}, s32[256]{0:T(256)}, u32[]{:S(2)}) copy-start(s32[256]{0:T(256)} %and_select_fusion) | copy-start | bytes 3076
  58.4 4.0 %collective-permute-start.5 = (bf16[513,256]{1,0:T(8,128)(2,1)}, bf16[513,256]{1,0:T(8,128)(2,1)}, u32[]{:S(2)}, u32[]{:S(2)}) collective-permute-start(bf16[513,256]{1,0:T(8,128)(2,1)} %pad_maximum_fusion.4), channel_id=1, source_target_pairs={{0,1},{1,0},{2,3},{3,2},{4,5},{5,4},{6,7},{7,6},{8,9},{9,8},{10,11... | collective-permute-start | bytes 787976 | tf_op jit(solution)/shard_map/ppermute | solution.py:167
  63.3 0.5 copy-start.21
  66.2 0.7 copy-start.2
  69.7 3.9 %collective-permute-start.6 = (bf16[21,256]{1,0:T(8,128)(2,1)}, bf16[21,256]{1,0:T(8,128)(2,1)S(1)}, u32[]{:S(2)}, u32[]{:S(2)}) collective-permute-start(bf16[21,256]{1,0:T(8,128)(2,1)} %pad_maximum_fusion.13), channel_id=1, source_target_pairs={{0,2},{2,0},{1,3},{3,1},{4,6},{6,4},{5,7},{7,5},{8,10},{10,8},{9,1... | collective-permute-start | bytes 32264 | tf_op jit(solution)/shard_map/ppermute | solution.py:167
  81.9 6.4 %copy-start.24 = (bf16[1,256]{1,0:T(2,128)(2,1)S(1)}, bf16[1,256]{1,0:T(2,128)(2,1)}, u32[]{:S(2)}) copy-start(bf16[1,256]{1,0:T(2,128)(2,1)} %reshape.972) | copy-start | bytes 1540
  81.9 10.2 %copy-start.25 = (pred[66]{0:T(512)(128)(4,1)S(1)}, pred[66]{0:T(512)(128)(4,1)}, u32[]{:S(2)}) copy-start(pred[66]{0:T(512)(128)(4,1)} %or_and_fusion) | copy-start | bytes 202
  81.9 10.2 %copy-start.26 = (pred[6]{0:T(512)(128)(4,1)S(1)}, pred[6]{0:T(512)(128)(4,1)}, u32[]{:S(2)}) copy-start(pred[6]{0:T(512)(128)(4,1)} %or_and_fusion.1) | copy-start | bytes 22
  89.3 7.9 %collective-permute-start.8 = (bf16[331,256]{1,0:T(8,128)(2,1)S(1)}, bf16[331,256]{1,0:T(8,128)(2,1)S(1)}, u32[]{:S(2)}, u32[]{:S(2)}) collective-permute-start(bf16[331,256]{1,0:T(8,128)(2,1)S(1)} %get-tuple-element.61), channel_id=1, source_target_pairs={{0,12},{4,8},{8,4},{12,0},{1,13},{5,9},{9,5},{13,1},{2,14},{6,10},... | collective-permute-start | bytes 508424 | tf_op jit(solution)/shard_map/ppermute | solution.py:167
  92.8 10.0 %collective-permute-start.9 = (f32[2,32]{1,0:T(2,128)S(1)}, f32[2,32]{1,0:T(2,128)S(1)}, u32[]{:S(2)}, u32[]{:S(2)}) collective-permute-start(f32[2,32]{1,0:T(2,128)S(1)} %get-tuple-element.16), channel_id=1, source_target_pairs={{0,8},{4,12},{8,0},{12,4},{1,9},{5,13},{9,1},{13,5},{2,10},{6,14},... | collective-permute-start | bytes 776 | tf_op jit(solution)/shard_map/ppermute | solution.py:167
  92.8 7.9 %collective-permute-start.7 = (bf16[331,256]{1,0:T(8,128)(2,1)S(1)}, bf16[331,256]{1,0:T(8,128)(2,1)S(1)}, u32[]{:S(2)}, u32[]{:S(2)}) collective-permute-start(bf16[331,256]{1,0:T(8,128)(2,1)S(1)} %get-tuple-element.60), channel_id=1, source_target_pairs={{0,4},{4,0},{8,12},{12,8},{1,5},{5,1},{9,13},{13,9},{2,6},{6,2},{1... | collective-permute-start | bytes 508424 | tf_op jit(solution)/shard_map/ppermute | solution.py:167
  97.2 0.7 copy-start.14
  100.6 0.7 copy-start.17
  114.3 0.7 copy-start.30
  115.0 4.0 %copy-start.29 = (s32[256]{0:T(256)S(1)}, s32[256]{0:T(256)}, u32[]{:S(2)}) copy-start(s32[256]{0:T(256)} %and_select_fusion) | copy-start | bytes 3076
  120.9 1.5 copy-start.4
  122.3 2.0 %collective-permute-start.10 = (bf16[513,256]{1,0:T(8,128)(2,1)S(1)}, bf16[513,256]{1,0:T(8,128)(2,1)S(1)}, u32[]{:S(2)}, u32[]{:S(2)}) collective-permute-start(bf16[513,256]{1,0:T(8,128)(2,1)S(1)} %pad_maximum_fusion.5), channel_id=1, source_target_pairs={{0,1},{1,0},{2,3},{3,2},{4,5},{5,4},{6,7},{7,6},{8,9},{9,8},{10,11... | collective-permute-start | bytes 787976 | tf_op jit(solution)/shard_map/ppermute | solution.py:167
  124.3 0.7 copy-start.13
  125.2 0.6 copy-start.22
  128.1 0.7 copy-start.3
  131.1 3.8 %collective-permute-start.11 = (bf16[21,256]{1,0:T(8,128)(2,1)S(1)}, bf16[21,256]{1,0:T(8,128)(2,1)S(1)}, u32[]{:S(2)}, u32[]{:S(2)}) collective-permute-start(bf16[21,256]{1,0:T(8,128)(2,1)S(1)} %pad_maximum_fusion.14), channel_id=1, source_target_pairs={{0,2},{2,0},{1,3},{3,1},{4,6},{6,4},{5,7},{7,5},{8,10},{10,8},{9,1... | collective-permute-start | bytes 32264 | tf_op jit(solution)/shard_map/ppermute | solution.py:167
  143.2 6.4 %copy-start.23 = (bf16[1,256]{1,0:T(2,128)(2,1)S(1)}, bf16[1,256]{1,0:T(2,128)(2,1)}, u32[]{:S(2)}) copy-start(bf16[1,256]{1,0:T(2,128)(2,1)} %reshape.990) | copy-start | bytes 1540
  150.6 8.6 %collective-permute-start.13 = (bf16[331,256]{1,0:T(8,128)(2,1)S(1)}, bf16[331,256]{1,0:T(8,128)(2,1)S(1)}, u32[]{:S(2)}, u32[]{:S(2)}) collective-permute-start(bf16[331,256]{1,0:T(8,128)(2,1)S(1)} %get-tuple-element.52), channel_id=1, source_target_pairs={{0,12},{4,8},{8,4},{12,0},{1,13},{5,9},{9,5},{13,1},{2,14},{6,10},... | collective-permute-start | bytes 508424 | tf_op jit(solution)/shard_map/ppermute | solution.py:167
  153.4 10.6 %collective-permute-start.14 = (f32[2,32]{1,0:T(2,128)S(1)}, f32[2,32]{1,0:T(2,128)S(1)}, u32[]{:S(2)}, u32[]{:S(2)}) collective-permute-start(f32[2,32]{1,0:T(2,128)S(1)} %get-tuple-element.12), channel_id=1, source_target_pairs={{0,8},{4,12},{8,0},{12,4},{1,9},{5,13},{9,1},{13,5},{2,10},{6,14},... | collective-permute-start | bytes 776 | tf_op jit(solution)/shard_map/ppermute | solution.py:167
  153.4 8.5 %collective-permute-start.12 = (bf16[331,256]{1,0:T(8,128)(2,1)S(1)}, bf16[331,256]{1,0:T(8,128)(2,1)S(1)}, u32[]{:S(2)}, u32[]{:S(2)}) collective-permute-start(bf16[331,256]{1,0:T(8,128)(2,1)S(1)} %get-tuple-element.51), channel_id=1, source_target_pairs={{0,4},{4,0},{8,12},{12,8},{1,5},{5,1},{9,13},{13,9},{2,6},{6,2},{1... | collective-permute-start | bytes 508424 | tf_op jit(solution)/shard_map/ppermute | solution.py:167
  159.2 0.7 copy-start.15
  161.9 0.7 copy-start.16
  175.3 2.0 %copy-start.27 = (bf16[3,3,3,256,256]{4,3,2,1,0:T(8,128)(2,1)S(1)}, bf16[3,3,3,256,256]{4,3,2,1,0:T(8,128)(2,1)}, u32[]{:S(2)}) copy-start(bf16[3,3,3,256,256]{4,3,2,1,0:T(8,128)(2,1)} %param.19) | copy-start | bytes 10616836
  175.6 1.7 copy-start.31
  180.6 1.0 copy-start.1

commit v10 on v6

--- a/solution.py
+++ b/solution.py
@@ -239,17 +239,17 @@
 
 def fast_conv_input(values):
     sums = local_sums(values.astype(jnp.float32))
-    s_t, earlier = swap_with(sums, values[-2:], "ta", 1)
-    sums = sums + s_t
-    opening = jnp.concatenate([values[:1], values[:1]], axis=0)
-    earlier = jnp.where(lax.axis_index("ta") == 0, opening, earlier)
-    x = jnp.concatenate([earlier, values], axis=0)
     w = lax.axis_index("wa")
-    s_w, beside = swap_with(sums, jnp.where(w == 0, x[:, :, -1:], x[:, :, :1]), "wa", 1)
+    s_w, beside = swap_with(sums, jnp.where(w == 0, values[:, :, -1:], values[:, :, :1]), "wa", 1)
     sums = sums + s_w
-    x = jnp.concatenate([beside, x, beside], axis=2)
+    x = jnp.concatenate([beside, values, beside], axis=2)
     sums, above, below = ha_round(sums, x[:, :1], x[:, -1:])
     x = jnp.concatenate([above, x, below], axis=1)
+    s_t, earlier = swap_with(sums, x[-2:], "ta", 1)
+    sums = sums + s_t
+    opening = jnp.concatenate([x[:1], x[:1]], axis=0)
+    earlier = jnp.where(lax.axis_index("ta") == 0, opening, earlier)
+    x = jnp.concatenate([earlier, x], axis=0)
     return finish_stats(sums, values), x
 
 

time: 97.2 us -> 77.8 us (0.80)
  other arithmetic: 18.3 us -> 11 us
  local copies, waits for them, and re-layouts: 26.6 us -> 20.9 us
  waiting for transfers between devices: 22.1 us -> 17.7 us
  starting transfers between devices: 20.1 us -> 18.3 us
    ppermute x15, waiting for transfers between devices: 22.1 us -> 17.7 us  [swap(): return lax.ppermute(x, axis, [(i, i ^ distance) for i in range(size)])]
    unnamed x57 -> x39, local copies, waits for them, and re-layouts: 6.36 us -> 3.58 us
    slice x2, local copies, waits for them, and re-layouts: 5.11 us -> 7.42 us  [valid_conv(): kernel[step_t].reshape(9 * channels, -1)]
    ppermute x15, starting transfers between devices: 20.1 us -> 18.3 us  [swap(): return lax.ppermute(x, axis, [(i, i ^ distance) for i in range(size)])]
    select_n x2, other arithmetic: 1.8 us -> 0.05 us  [ha_round(): above = jnp.where(h % 2 == 1, got_first, got_third)]
    select_n x2, local copies, waits for them, and re-layouts: 1.67 us -> 0.06 us  [ha_round(): above = jnp.where(h % 2 == 1, got_first, got_third)]
    select_n x3, local copies, waits for them, and re-layouts: 1.71 us -> 0.09 us  [ha_round(): below = jnp.where(h % 2 == 0, got_first, got_third)]
    convert_element_type x2, other arithmetic: 4.99 us -> 3.58 us  [norm_conv(): jnp.where(inside_mask(height + 2, across + 2, 1), act, 0.0)]
  transfers between devices with their start and end apart: 15 -> 15, of which waited for: 8 -> 10; matrix products, arithmetic and copies ran while one was open for 9% -> 14% of each run, Pallas kernels for 0% -> 0%
where the time goes in v10:
time: 77.8 us; the launch traced here: 77.4 us
  local copies, waits for them, and re-layouts  20.9 us (27%)
  starting transfers between devices  18.3 us (24%)
  waiting for transfers between devices  17.7 us (23%)
  other arithmetic  11 us (14%)
  matrix products  8.59 us (11%)
  between operations  0.89 us (1%)
    ppermute x15, starting transfers between devices, swap(): return lax.ppermute(x, axis, [(i, i ^ distance) for i in range(size)])  18.3 us
    ppermute x15, waiting for transfers between devices, swap(): return lax.ppermute(x, axis, [(i, i ^ distance) for i in range(size)])  17.7 us
    slice x2, local copies, waits for them, and re-layouts, valid_conv(): kernel[step_t].reshape(9 * channels, -1)  7.42 us
    dot_general x6, matrix products, valid_conv(): jnp.dot(window, kernel[step_t].reshape(9 * channels, -1), preferred_eleme...  6.52 us
    unnamed x39, local copies, waits for them, and re-layouts  3.58 us
    convert_element_type x2, other arithmetic, norm_conv(): jnp.where(inside_mask(height + 2, across + 2, 1), act, 0.0)  3.58 us
    reduce_sum x5, other arithmetic, local_sums(): jnp.sum(grouped, axis=(0, 2))  2.25 us
    slice x2, local copies, waits for them, and re-layouts, valid_conv(): window = wide[step_t:step_t + frames].reshape(-1, 9 * channels)  2.19 us
  transfers between devices with their start and end apart: 15, of which 10 were waited for; matrix products, arithmetic and copies ran while one was open for 14% of the time, Pallas kernels for 0%

profile of v10, /device:TPU:0, one launch (start us, length us, event | category | flops | bytes accessed | tf_op | source)
XLA Modules:
  0.0 77.4 jit_solution(15521919190932012527)
XLA Ops:
  0.0 1.1 %convert_reduce_fusion.2 = (f32[512]{0:T(512)S(1)}, f32[512]{0:T(512)S(1)}) fusion(bf16[3,2,32,512]{3,2,1,0:T(8,128)(2,1)} %param.10), kind=kLoop, calls=%fused_computation.52 | loop fusion | flops 392192 | bytes 200704 | tf_op jit(solution)/shard_map/reduce_sum | solution.py:179
  1.5 0.5 collective-permute-start
  2.0 1.6 %slice_bitcast_fusion.7 = (bf16[512,256]{1,0:T(8,128)(2,1)S(1)}, bf16[512,256]{1,0:T(8,128)(2,1)S(1)}, bf16[512,256]{1,0:T(8,128)(2,1)S(1)}, bf16[512,256]{1,0:T...) fusion(bf16[3,3,512,256]{3,2,1,0:T(8,128)(2,1)} %param.13), kind=kLoop, calls=%fused_computation.77 | loop fusion | bytes 4194304 | tf_op jit(solution)/shard_map/squeeze | solution.py:129
  4.2 2.6 %collective-permute-start.1 = (bf16[7,512]{1,0:T(8,128)(2,1)S(1)}, bf16[7,512]{1,0:T(8,128)(2,1)S(1)}, u32[]{:S(2)}, u32[]{:S(2)}) collective-permute-start(bf16[7,512]{1,0:T(8,128)(2,1)S(1)} %pad_maximum_fusion.25), channel_id=1, source_target_pairs={{0,2},{2,0},{1,3},{3,1},{4,6},{6,4},{5,7},{7,5},{8,10},{10,8},{9,1... | collective-permute-start | bytes 21512 | tf_op jit(solution)/shard_map/ppermute | solution.py:170
  6.9 1.6 %collective-permute-done.1 = bf16[7,512]{1,0:T(8,128)(2,1)S(1)} collective-permute-done((bf16[7,512]{1,0:T(8,128)(2,1)S(1)}, bf16[7,512]{1,0:T(8,128)(2,1)S(1)}, u32[]{:S(2)}, u32[]{:S(2)}) %collective-permute-start.1) | collective-permute-done | bytes 7200 | tf_op jit(solution)/shard_map/ppermute | solution.py:170
  9.1 2.2 %collective-permute-start.2 = (bf16[100,512]{1,0:T(8,128)(2,1)S(1)}, bf16[100,512]{1,0:T(8,128)(2,1)S(1)}, u32[]{:S(2)}, u32[]{:S(2)}) collective-permute-start(bf16[100,512]{1,0:T(8,128)(2,1)S(1)} %pad_maximum_fusion.24), channel_id=1, source_target_pairs={{0,4},{4,0},{8,12},{12,8},{1,5},{5,1},{9,13},{13,9},{2,6},{6,2},{1... | collective-permute-start | bytes 307208 | tf_op jit(solution)/shard_map/ppermute | solution.py:170
  11.3 2.5 %collective-permute-start.3 = (bf16[100,512]{1,0:T(8,128)(2,1)S(1)}, bf16[100,512]{1,0:T(8,128)(2,1)S(1)}, u32[]{:S(2)}, u32[]{:S(2)}) collective-permute-start(bf16[100,512]{1,0:T(8,128)(2,1)S(1)} %pad_maximum_fusion.24), channel_id=1, source_target_pairs={{0,12},{4,8},{8,4},{12,0},{1,13},{5,9},{9,5},{13,1},{2,14},{6,10},... | collective-permute-start | bytes 307208 | tf_op jit(solution)/shard_map/ppermute | solution.py:170
  14.3 4.1 %collective-permute-done.3 = bf16[100,512]{1,0:T(8,128)(2,1)S(1)} collective-permute-done((bf16[100,512]{1,0:T(8,128)(2,1)S(1)}, bf16[100,512]{1,0:T(8,128)(2,1)S(1)}, u32[]{:S(2)}, u32[]{:S(2)}) %collective-permute-start.3) | collective-permute-done | bytes 102432 | tf_op jit(solution)/shard_map/ppermute | solution.py:170
  19.0 0.3 select_convert_fusion.2
  19.4 0.3 fusion.11
  19.7 0.3 fusion.15
  20.0 0.4 fusion.1
  20.8 1.2 %convolution_add_fusion.4 = bf16[192,256]{1,0:T(8,128)(2,1)S(1)} fusion(bf16[192,512]{1,0:T(8,128)(2,1)S(1)} %bitcast.122, bf16[3,3,512,256]{3,2,1,0:T(8,128)(2,1)} %param.13, f32[192,512]{1,0:T(8,128)S(1)} %fusion.15, f32[192,512]{1,0:T(8,128)S(1)} %fusion.11, f32[192,1024]{1,0:T(8,128)S(1)} %fusion.1), kind=kOutput, calls=%fused_computation.7 | convolution fusion | flops 50528256 | bytes 1146880 | tf_op jit(solution)/shard_map/dot_general | solution.py:123
  22.0 0.3 pad_maximum_fusion.10
  22.3 0.3 pad_maximum_fusion.11
  22.6 0.8 %convert_reduce_fusion.1 = (f32[256]{0:T(256)S(1)}, f32[256]{0:T(256)S(1)}, bf16[3,2,2,64,256]{4,1,3,0,2:T(2,128)(2,1)S(1)}) fusion(bf16[3,2,1,64,256]{4,1,3,0,2:T(2,128)(2,1)S(1)} %bitcast.125, bf16[3,2,1,64,256]{4,1,3,0,2:T(2,128)(2,1)S(1)} %bitcast.124), kind=kLoop, calls=%fused_computation.19 | loop fusion | flops 982528 | bytes 788480 | tf_op jit(solution)/shard_map/reduce_sum | solution.py:179
  24.2 1.6 %collective-permute-start.5 = (bf16[13,256]{1,0:T(8,128)(2,1)S(1)}, bf16[13,256]{1,0:T(8,128)(2,1)S(1)}, u32[]{:S(2)}, u32[]{:S(2)}) collective-permute-start(bf16[13,256]{1,0:T(8,128)(2,1)S(1)} %pad_maximum_fusion.26), channel_id=1, source_target_pairs={{0,2},{2,0},{1,3},{3,1},{4,6},{6,4},{5,7},{7,5},{8,10},{10,8},{9,1... | collective-permute-start | bytes 19976 | tf_op jit(solution)/shard_map/ppermute | solution.py:170
  25.7 2.2 %collective-permute-done.5 = bf16[13,256]{1,0:T(8,128)(2,1)S(1)} collective-permute-done((bf16[13,256]{1,0:T(8,128)(2,1)S(1)}, bf16[13,256]{1,0:T(8,128)(2,1)S(1)}, u32[]{:S(2)}, u32[]{:S(2)}) %collective-permute-start.5) | collective-permute-done | bytes 6688 | tf_op jit(solution)/shard_map/ppermute | solution.py:170
  28.7 0.7 collective-permute-start.6
  29.3 2.8 %collective-permute-start.7 = (bf16[199,256]{1,0:T(8,128)(2,1)S(1)}, bf16[199,256]{1,0:T(8,128)(2,1)S(1)}, u32[]{:S(2)}, u32[]{:S(2)}) collective-permute-start(bf16[199,256]{1,0:T(8,128)(2,1)S(1)} %get-tuple-element.70), channel_id=1, source_target_pairs={{0,12},{4,8},{8,4},{12,0},{1,13},{5,9},{9,5},{13,1},{2,14},{6,10},... | collective-permute-start | bytes 305672 | tf_op jit(solution)/shard_map/ppermute | solution.py:170
  32.3 1.1 %collective-permute-done.6 = bf16[199,256]{1,0:T(8,128)(2,1)S(1)} collective-permute-done((bf16[199,256]{1,0:T(8,128)(2,1)S(1)}, bf16[199,256]{1,0:T(8,128)(2,1)S(1)}, u32[]{:S(2)}, u32[]{:S(2)}) %collective-permute-start.6) | collective-permute-done | bytes 101920 | tf_op jit(solution)/shard_map/ppermute | solution.py:170
  33.4 2.6 %collective-permute-done.7 = bf16[199,256]{1,0:T(8,128)(2,1)S(1)} collective-permute-done((bf16[199,256]{1,0:T(8,128)(2,1)S(1)}, bf16[199,256]{1,0:T(8,128)(2,1)S(1)}, u32[]{:S(2)}, u32[]{:S(2)}) %collective-permute-start.7) | collective-permute-done | bytes 101920 | tf_op jit(solution)/shard_map/ppermute | solution.py:170
  37.2 3.7 %fusion.117 = (bf16[1,3,3,256,256]{4,3,2,1,0:T(8,128)(2,1)S(1)}, bf16[1,3,3,256,256]{4,3,2,1,0:T(8,128)(2,1)}, bf16[1,3,3,256,256]{4,3,2,1,0:T(8,128)(2,1)}) fusion(bf16[3,3,3,256,256]{4,3,2,1,0:T(8,128)(2,1)} %param.16), kind=kLoop, calls=%fused_computation.281 | loop fusion | bytes 7077888 | tf_op jit(solution)/shard_map/slice | solution.py:154
  41.7 1.9 %select_convert_fusion.1 = bf16[5,6,66,256]{3,2,1,0:T(8,128)(2,1)S(1)} fusion(bf16[3,1,66,256]{3,2,1,0:T(8,128)(2,1)S(1)} %select_n.182, bf16[3,4,1,256]{3,2,1,0:T(2,128)(2,1)S(1)} %reshape.752, bf16[3,4,64,256]{3,2,1,0:T(8,128)(2,1)S(1)} %bitcast.103, bf16[3,1,66,256]{3,2,1,0:T(8,128)(2,1)S(1)} %select_n.179, ...), kind=kLoop, calls=%fused_computation.1 | loop fusion | flops 11151360 | bytes 2025868 | tf_op jit(solution)/shard_map/convert_element_type | solution.py:275
  43.7 0.2 slice_dynamic-update-slice_fusion.16
  43.9 0.2 slice_dynamic-update-slice_fusion.15
  44.3 0.2 slice_dynamic-update-slice_fusion.13
  45.4 1.0 %fusion.115 = (bf16[3,4,64,2304]{3,2,1,0:T(8,128)(2,1)S(1)}, bf16[3,4,64,2304]{3,2,1,0:T(8,128)(2,1)S(1)}, bf16[3,4,64,2304]{3,2,1,0:T(8,128)(2,1)S(1)}) fusion(bf16[5,4,64,2304]{3,2,1,0:T(8,128)(2,1)S(1)} %slice_dynamic-update-slice_fusion.9), kind=kLoop, calls=%fused_computation.279 | loop fusion | bytes 21233664 | tf_op jit(solution)/shard_map/slice | solution.py:152
  46.3 0.3 copy-done.3
  46.6 1.1 %fusion.120 = f32[768,256]{1,0:T(8,128)S(1)} fusion(bf16[768,2304]{1,0:T(8,128)(2,1)S(1)} %bitcast.114, bf16[2304,256]{1,0:T(8,128)(2,1)S(1)} %bitcast.121), kind=kOutput, calls=%fused_computation.284 | convolution fusion | flops 905969664 | bytes 5505024 | tf_op jit(solution)/shard_map/dot_general | solution.py:153
  47.9 1.1 %convolution_add_fusion.3 = f32[768,256]{1,0:T(8,128)S(1)} fusion(f32[768,256]{1,0:T(8,128)S(1)} %fusion.120, bf16[768,2304]{1,0:T(8,128)(2,1)S(1)} %bitcast.112, bf16[2304,256]{1,0:T(8,128)(2,1)S(1)} %bitcast.120), kind=kOutput, calls=%fused_computation.5 | convolution fusion | flops 906166272 | bytes 6291456 | tf_op jit(solution)/shard_map/dot_general | solution.py:153
  49.0 1.1 %convert_reduce_fusion = (f32[256]{0:T(256)S(1)}, f32[256]{0:T(256)S(1)}, bf16[768,256]{1,0:T(8,128)(2,1)S(1)}) fusion(f32[768,256]{1,0:T(8,128)S(1)} %convolution_add_fusion.3, bf16[768,2304]{1,0:T(8,128)(2,1)S(1)} %bitcast.110, bf16[2304,256]{1,0:T(8,128)(2,1)S(1)} %bitcast.116), kind=kOutput, calls=%fused_computation.17 | convolution fusion | flops 907148800 | bytes 5900288 | tf_op jit(solution)/shard_map/dot_general | solution.py:153
  50.8 1.6 %collective-permute-start.10 = (bf16[13,256]{1,0:T(8,128)(2,1)S(1)}, bf16[13,256]{1,0:T(8,128)(2,1)S(1)}, u32[]{:S(2)}, u32[]{:S(2)}) collective-permute-start(bf16[13,256]{1,0:T(8,128)(2,1)S(1)} %pad_maximum_fusion.27), channel_id=1, source_target_pairs={{0,2},{2,0},{1,3},{3,1},{4,6},{6,4},{5,7},{7,5},{8,10},{10,8},{9,1... | collective-permute-start | bytes 19976 | tf_op jit(solution)/shard_map/ppermute | solution.py:170
  52.4 2.2 %collective-permute-done.10 = bf16[13,256]{1,0:T(8,128)(2,1)S(1)} collective-permute-done((bf16[13,256]{1,0:T(8,128)(2,1)S(1)}, bf16[13,256]{1,0:T(8,128)(2,1)S(1)}, u32[]{:S(2)}, u32[]{:S(2)}) %collective-permute-start.10) | collective-permute-done | bytes 6688 | tf_op jit(solution)/shard_map/ppermute | solution.py:170
  55.3 0.4 collective-permute-start.11
  55.7 2.4 %collective-permute-start.12 = (bf16[199,256]{1,0:T(8,128)(2,1)S(1)}, bf16[199,256]{1,0:T(8,128)(2,1)S(1)}, u32[]{:S(2)}, u32[]{:S(2)}) collective-permute-start(bf16[199,256]{1,0:T(8,128)(2,1)S(1)} %get-tuple-element.64), channel_id=1, source_target_pairs={{0,12},{4,8},{8,4},{12,0},{1,13},{5,9},{9,5},{13,1},{2,14},{6,10},... | collective-permute-start | bytes 305672 | tf_op jit(solution)/shard_map/ppermute | solution.py:170
  58.1 0.8 %collective-permute-start.13 = (f32[2,32]{1,0:T(2,128)S(1)}, f32[2,32]{1,0:T(2,128)S(1)}, u32[]{:S(2)}, u32[]{:S(2)}) collective-permute-start(f32[2,32]{1,0:T(2,128)S(1)} %get-tuple-element.17), channel_id=1, source_target_pairs={{0,8},{4,12},{8,0},{12,4},{1,9},{5,13},{9,1},{13,5},{2,10},{6,14},... | collective-permute-start | bytes 776 | tf_op jit(solution)/shard_map/ppermute | solution.py:170
  58.9 2.2 %collective-permute-done.11 = bf16[199,256]{1,0:T(8,128)(2,1)S(1)} collective-permute-done((bf16[199,256]{1,0:T(8,128)(2,1)S(1)}, bf16[199,256]{1,0:T(8,128)(2,1)S(1)}, u32[]{:S(2)}, u32[]{:S(2)}) %collective-permute-start.11) | collective-permute-done | bytes 101920 | tf_op jit(solution)/shard_map/ppermute | solution.py:170
  61.1 1.5 %collective-permute-done.12 = bf16[199,256]{1,0:T(8,128)(2,1)S(1)} collective-permute-done((bf16[199,256]{1,0:T(8,128)(2,1)S(1)}, bf16[199,256]{1,0:T(8,128)(2,1)S(1)}, u32[]{:S(2)}, u32[]{:S(2)}) %collective-permute-start.12) | collective-permute-done | bytes 101920 | tf_op jit(solution)/shard_map/ppermute | solution.py:170
  63.8 3.7 %fusion.116 = (bf16[1,3,3,256,256]{4,3,2,1,0:T(8,128)(2,1)S(1)}, bf16[1,3,3,256,256]{4,3,2,1,0:T(8,128)(2,1)}, bf16[1,3,3,256,256]{4,3,2,1,0:T(8,128)(2,1)}) fusion(bf16[3,3,3,256,256]{4,3,2,1,0:T(8,128)(2,1)} %param.19), kind=kLoop, calls=%fused_computation.280 | loop fusion | bytes 7077888 | tf_op jit(solution)/shard_map/slice | solution.py:154
  68.4 1.7 %select_convert_fusion = bf16[5,6,66,256]{3,2,1,0:T(8,128)(2,1)S(1)} fusion(bf16[3,1,66,256]{3,2,1,0:T(8,128)(2,1)S(1)} %select_n.191, bf16[3,4,1,256]{3,2,1,0:T(2,128)(2,1)S(1)} %reshape.753, bf16[3,4,64,256]{3,2,1,0:T(8,128)(2,1)S(1)} %bitcast.109, bf16[3,1,66,256]{3,2,1,0:T(8,128)(2,1)S(1)} %select_n.189, ...), kind=kLoop, calls=%fused_computation | loop fusion | flops 11151360 | bytes 2025868 | tf_op jit(solution)/shard_map/convert_element_type | solution.py:275
  70.1 0.2 slice_dynamic-update-slice_fusion.7
  70.4 0.2 slice_dynamic-update-slice_fusion.6
  71.8 1.2 %fusion.114 = (bf16[3,4,64,2304]{3,2,1,0:T(8,128)(2,1)S(1)}, bf16[3,4,64,2304]{3,2,1,0:T(8,128)(2,1)S(1)}, bf16[3,4,64,2304]{3,2,1,0:T(8,128)(2,1)S(1)}) fusion(bf16[5,4,64,2304]{3,2,1,0:T(8,128)(2,1)S(1)} %slice_dynamic-update-slice_fusion), kind=kLoop, calls=%fused_computation.278 | loop fusion | bytes 21233664 | tf_op jit(solution)/shard_map/slice | solution.py:152
  73.1 1.1 %fusion.121 = f32[768,256]{1,0:T(8,128)S(1)} fusion(bf16[768,2304]{1,0:T(8,128)(2,1)S(1)} %bitcast.115, bf16[2304,256]{1,0:T(8,128)(2,1)S(1)} %bitcast.119), kind=kOutput, calls=%fused_computation.285 | convolution fusion | flops 905969664 | bytes 5505024 | tf_op jit(solution)/shard_map/dot_general | solution.py:153
  74.3 1.1 %convolution_add_fusion.1 = f32[768,256]{1,0:T(8,128)S(1)} fusion(f32[768,256]{1,0:T(8,128)S(1)} %fusion.121, bf16[768,2304]{1,0:T(8,128)(2,1)S(1)} %bitcast.113, bf16[2304,256]{1,0:T(8,128)(2,1)S(1)} %bitcast.118), kind=kOutput, calls=%fused_computation.3 | convolution fusion | flops 906166272 | bytes 6291456 | tf_op jit(solution)/shard_map/dot_general | solution.py:153
  75.4 1.1 %convolution_add_fusion = f32[768,256]{1,0:T(8,128)S(1)} fusion(f32[768,256]{1,0:T(8,128)S(1)} %convolution_add_fusion.1, bf16[768,2304]{1,0:T(8,128)(2,1)S(1)} %bitcast.111, bf16[2304,256]{1,0:T(8,128)(2,1)S(1)} %bitcast.117), kind=kOutput, calls=%fused_computation.2 | convolution fusion | flops 906166272 | bytes 6291456 | tf_op jit(solution)/shard_map/dot_general | solution.py:153
  76.5 0.9 %add_convert_fusion = bf16[3,4,64,256]{3,2,1,0:T(8,128)(2,1)} fusion(f32[3,4,64,256]{3,2,1,0:T(8,128)S(1)} %bitcast.123, bf16[3,4,64,256]{3,2,1,0:T(8,128)(2,1)S(1)} %bitcast.104), kind=kLoop, calls=%fused_computation.23 | loop fusion | flops 589824 | bytes 1572864 | tf_op jit(solution)/shard_map/convert_element_type | solution.py:302
  (226 shorter events, 12.7 us)
Async XLA Ops:
  0.0 3.8 %copy-start.4 = (bf16[3,2,32,512]{3,2,1,0:T(8,128)(2,1)S(1)}, bf16[3,2,32,512]{3,2,1,0:T(8,128)(2,1)}, u32[]{:S(2)}) copy-start(bf16[3,2,32,512]{3,2,1,0:T(8,128)(2,1)} %param.10) | copy-start | bytes 589828
  1.5 2.3 %collective-permute-start = (f32[2,32]{1,0:T(2,128)S(1)}, f32[2,32]{1,0:T(2,128)S(1)}, u32[]{:S(2)}, u32[]{:S(2)}) collective-permute-start(f32[2,32]{1,0:T(2,128)S(1)} %pad_maximum_fusion.28), channel_id=1, source_target_pairs={{0,1},{1,0},{2,3},{3,2},{4,5},{5,4},{6,7},{7,6},{8,9},{9,8},{10,11... | collective-permute-start | bytes 776 | tf_op jit(solution)/shard_map/ppermute | solution.py:170
  2.0 17.0 %copy-start.5 = (f32[512]{0:T(512)S(1)}, f32[512]{0:T(512)}, u32[]{:S(2)}) copy-start(f32[512]{0:T(512)} %param.12) | copy-start | bytes 6148
  2.0 17.0 %copy-start.6 = (f32[512]{0:T(512)S(1)}, f32[512]{0:T(512)}, u32[]{:S(2)}) copy-start(f32[512]{0:T(512)} %param.11) | copy-start | bytes 6148
  4.2 4.2 %collective-permute-start.1 = (bf16[7,512]{1,0:T(8,128)(2,1)S(1)}, bf16[7,512]{1,0:T(8,128)(2,1)S(1)}, u32[]{:S(2)}, u32[]{:S(2)}) collective-permute-start(bf16[7,512]{1,0:T(8,128)(2,1)S(1)} %pad_maximum_fusion.25), channel_id=1, source_target_pairs={{0,2},{2,0},{1,3},{3,1},{4,6},{6,4},{5,7},{7,5},{8,10},{10,8},{9,1... | collective-permute-start | bytes 21512 | tf_op jit(solution)/shard_map/ppermute | solution.py:170
  9.1 5.0 %collective-permute-start.2 = (bf16[100,512]{1,0:T(8,128)(2,1)S(1)}, bf16[100,512]{1,0:T(8,128)(2,1)S(1)}, u32[]{:S(2)}, u32[]{:S(2)}) collective-permute-start(bf16[100,512]{1,0:T(8,128)(2,1)S(1)} %pad_maximum_fusion.24), channel_id=1, source_target_pairs={{0,4},{4,0},{8,12},{12,8},{1,5},{5,1},{9,13},{13,9},{2,6},{6,2},{1... | collective-permute-start | bytes 307208 | tf_op jit(solution)/shard_map/ppermute | solution.py:170
  11.3 7.0 %collective-permute-start.3 = (bf16[100,512]{1,0:T(8,128)(2,1)S(1)}, bf16[100,512]{1,0:T(8,128)(2,1)S(1)}, u32[]{:S(2)}, u32[]{:S(2)}) collective-permute-start(bf16[100,512]{1,0:T(8,128)(2,1)S(1)} %pad_maximum_fusion.24), channel_id=1, source_target_pairs={{0,12},{4,8},{8,4},{12,0},{1,13},{5,9},{9,5},{13,1},{2,14},{6,10},... | collective-permute-start | bytes 307208 | tf_op jit(solution)/shard_map/ppermute | solution.py:170
  13.8 4.8 %collective-permute-start.4 = (f32[2,32]{1,0:T(2,128)S(1)}, f32[2,32]{1,0:T(2,128)S(1)}, u32[]{:S(2)}, u32[]{:S(2)}) collective-permute-start(f32[2,32]{1,0:T(2,128)S(1)} %get-tuple-element.27), channel_id=1, source_target_pairs={{0,8},{4,12},{8,0},{12,4},{1,9},{5,13},{9,1},{13,5},{2,10},{6,14},... | collective-permute-start | bytes 776 | tf_op jit(solution)/shard_map/ppermute | solution.py:170
  24.2 3.7 %collective-permute-start.5 = (bf16[13,256]{1,0:T(8,128)(2,1)S(1)}, bf16[13,256]{1,0:T(8,128)(2,1)S(1)}, u32[]{:S(2)}, u32[]{:S(2)}) collective-permute-start(bf16[13,256]{1,0:T(8,128)(2,1)S(1)} %pad_maximum_fusion.26), channel_id=1, source_target_pairs={{0,2},{2,0},{1,3},{3,1},{4,6},{6,4},{5,7},{7,5},{8,10},{10,8},{9,1... | collective-permute-start | bytes 19976 | tf_op jit(solution)/shard_map/ppermute | solution.py:170
  28.7 4.7 %collective-permute-start.6 = (bf16[199,256]{1,0:T(8,128)(2,1)S(1)}, bf16[199,256]{1,0:T(8,128)(2,1)S(1)}, u32[]{:S(2)}, u32[]{:S(2)}) collective-permute-start(bf16[199,256]{1,0:T(8,128)(2,1)S(1)} %get-tuple-element.69), channel_id=1, source_target_pairs={{0,4},{4,0},{8,12},{12,8},{1,5},{5,1},{9,13},{13,9},{2,6},{6,2},{1... | collective-permute-start | bytes 305672 | tf_op jit(solution)/shard_map/ppermute | solution.py:170
  29.3 6.6 %collective-permute-start.7 = (bf16[199,256]{1,0:T(8,128)(2,1)S(1)}, bf16[199,256]{1,0:T(8,128)(2,1)S(1)}, u32[]{:S(2)}, u32[]{:S(2)}) collective-permute-start(bf16[199,256]{1,0:T(8,128)(2,1)S(1)} %get-tuple-element.70), channel_id=1, source_target_pairs={{0,12},{4,8},{8,4},{12,0},{1,13},{5,9},{9,5},{13,1},{2,14},{6,10},... | collective-permute-start | bytes 305672 | tf_op jit(solution)/shard_map/ppermute | solution.py:170
  32.2 4.5 %collective-permute-start.8 = (f32[2,32]{1,0:T(2,128)S(1)}, f32[2,32]{1,0:T(2,128)S(1)}, u32[]{:S(2)}, u32[]{:S(2)}) collective-permute-start(f32[2,32]{1,0:T(2,128)S(1)} %get-tuple-element.24), channel_id=1, source_target_pairs={{0,8},{4,12},{8,0},{12,4},{1,9},{5,13},{9,1},{13,5},{2,10},{6,14},... | collective-permute-start | bytes 776 | tf_op jit(solution)/shard_map/ppermute | solution.py:170
  37.1 3.8 %collective-permute-start.9 = (bf16[793,256]{1,0:T(8,128)(2,1)S(1)}, bf16[793,256]{1,0:T(8,128)(2,1)S(1)}, u32[]{:S(2)}, u32[]{:S(2)}) collective-permute-start(bf16[793,256]{1,0:T(8,128)(2,1)S(1)} %pad_maximum_fusion.8), channel_id=1, source_target_pairs={{0,1},{1,0},{2,3},{3,2},{4,5},{5,4},{6,7},{7,6},{8,9},{9,8},{10,11... | collective-permute-start | bytes 1218056 | tf_op jit(solution)/shard_map/ppermute | solution.py:170
  40.9 0.8 %copy-start.7 = (f32[256]{0:T(256)S(1)}, f32[256]{0:T(256)}, u32[]{:S(2)}) copy-start(f32[256]{0:T(256)} %param.15) | copy-start | bytes 3076
  40.9 0.8 %copy-start.8 = (f32[256]{0:T(256)S(1)}, f32[256]{0:T(256)}, u32[]{:S(2)}) copy-start(f32[256]{0:T(256)} %param.14) | copy-start | bytes 3076
  45.3 1.3 %copy-start.3 = (bf16[1,3,3,256,256]{4,3,2,1,0:T(8,128)(2,1)S(1)}, bf16[1,3,3,256,256]{4,3,2,1,0:T(8,128)(2,1)}, u32[]{:S(2)}) copy-start(bf16[1,3,3,256,256]{4,3,2,1,0:T(8,128)(2,1)} %get-tuple-element.40) | copy-start | bytes 3538948
  46.6 1.3 %copy-start.2 = (bf16[1,3,3,256,256]{4,3,2,1,0:T(8,128)(2,1)S(1)}, bf16[1,3,3,256,256]{4,3,2,1,0:T(8,128)(2,1)}, u32[]{:S(2)}) copy-start(bf16[1,3,3,256,256]{4,3,2,1,0:T(8,128)(2,1)} %get-tuple-element.41) | copy-start | bytes 3538948
  50.8 3.7 %collective-permute-start.10 = (bf16[13,256]{1,0:T(8,128)(2,1)S(1)}, bf16[13,256]{1,0:T(8,128)(2,1)S(1)}, u32[]{:S(2)}, u32[]{:S(2)}) collective-permute-start(bf16[13,256]{1,0:T(8,128)(2,1)S(1)} %pad_maximum_fusion.27), channel_id=1, source_target_pairs={{0,2},{2,0},{1,3},{3,1},{4,6},{6,4},{5,7},{7,5},{8,10},{10,8},{9,1... | collective-permute-start | bytes 19976 | tf_op jit(solution)/shard_map/ppermute | solution.py:170
  55.3 5.8 %collective-permute-start.11 = (bf16[199,256]{1,0:T(8,128)(2,1)S(1)}, bf16[199,256]{1,0:T(8,128)(2,1)S(1)}, u32[]{:S(2)}, u32[]{:S(2)}) collective-permute-start(bf16[199,256]{1,0:T(8,128)(2,1)S(1)} %get-tuple-element.63), channel_id=1, source_target_pairs={{0,4},{4,0},{8,12},{12,8},{1,5},{5,1},{9,13},{13,9},{2,6},{6,2},{1... | collective-permute-start | bytes 305672 | tf_op jit(solution)/shard_map/ppermute | solution.py:170
  55.7 7.0 %collective-permute-start.12 = (bf16[199,256]{1,0:T(8,128)(2,1)S(1)}, bf16[199,256]{1,0:T(8,128)(2,1)S(1)}, u32[]{:S(2)}, u32[]{:S(2)}) collective-permute-start(bf16[199,256]{1,0:T(8,128)(2,1)S(1)} %get-tuple-element.64), channel_id=1, source_target_pairs={{0,12},{4,8},{8,4},{12,0},{1,13},{5,9},{9,5},{13,1},{2,14},{6,10},... | collective-permute-start | bytes 305672 | tf_op jit(solution)/shard_map/ppermute | solution.py:170
  58.1 5.3 %collective-permute-start.13 = (f32[2,32]{1,0:T(2,128)S(1)}, f32[2,32]{1,0:T(2,128)S(1)}, u32[]{:S(2)}, u32[]{:S(2)}) collective-permute-start(f32[2,32]{1,0:T(2,128)S(1)} %get-tuple-element.17), channel_id=1, source_target_pairs={{0,8},{4,12},{8,0},{12,4},{1,9},{5,13},{9,1},{13,5},{2,10},{6,14},... | collective-permute-start | bytes 776 | tf_op jit(solution)/shard_map/ppermute | solution.py:170
  63.7 3.8 %collective-permute-start.14 = (bf16[793,256]{1,0:T(8,128)(2,1)S(1)}, bf16[793,256]{1,0:T(8,128)(2,1)S(1)}, u32[]{:S(2)}, u32[]{:S(2)}) collective-permute-start(bf16[793,256]{1,0:T(8,128)(2,1)S(1)} %pad_maximum_fusion.9), channel_id=1, source_target_pairs={{0,1},{1,0},{2,3},{3,2},{4,5},{5,4},{6,7},{7,6},{8,9},{9,8},{10,11... | collective-permute-start | bytes 1218056 | tf_op jit(solution)/shard_map/ppermute | solution.py:170
  67.5 0.8 %copy-start.9 = (f32[256]{0:T(256)S(1)}, f32[256]{0:T(256)}, u32[]{:S(2)}) copy-start(f32[256]{0:T(256)} %param.18) | copy-start | bytes 3076
  67.5 0.8 %copy-start.10 = (f32[256]{0:T(256)S(1)}, f32[256]{0:T(256)}, u32[]{:S(2)}) copy-start(f32[256]{0:T(256)} %param.17) | copy-start | bytes 3076
  71.8 1.3 %copy-start.1 = (bf16[1,3,3,256,256]{4,3,2,1,0:T(8,128)(2,1)S(1)}, bf16[1,3,3,256,256]{4,3,2,1,0:T(8,128)(2,1)}, u32[]{:S(2)}) copy-start(bf16[1,3,3,256,256]{4,3,2,1,0:T(8,128)(2,1)} %get-tuple-element.37) | copy-start | bytes 3538948
  73.1 1.3 %copy-start = (bf16[1,3,3,256,256]{4,3,2,1,0:T(8,128)(2,1)S(1)}, bf16[1,3,3,256,256]{4,3,2,1,0:T(8,128)(2,1)}, u32[]{:S(2)}) copy-start(bf16[1,3,3,256,256]{4,3,2,1,0:T(8,128)(2,1)} %get-tuple-element.38) | copy-start | bytes 3538948

commit v11 on v10

--- a/solution.py
+++ b/solution.py
@@ -142,7 +142,12 @@
     return jnp.concatenate([even, odd], axis=2).reshape(frames, 2 * height, 2 * across, out)
 
 
-def valid_conv(padded, kernel, frames, height, across):
+def conv_taps(kernel):
+    channels = kernel.shape[-2]
+    return [kernel[step_t].reshape(9 * channels, -1) for step_t in range(3)]
+
+
+def valid_conv(padded, taps, frames, height, across):
     channels = padded.shape[-1]
     wide = jnp.concatenate(
         [padded[:, dy : dy + height, dx : dx + across] for dy in range(3) for dx in range(3)], axis=-1
@@ -150,9 +155,7 @@
     result = None
     for step_t in range(3):
         window = wide[step_t : step_t + frames].reshape(-1, 9 * channels)
-        part = jnp.dot(
-            window, kernel[step_t].reshape(9 * channels, -1), preferred_element_type=jnp.float32
-        )
+        part = jnp.dot(window, taps[step_t], preferred_element_type=jnp.float32)
         result = part if result is None else result + part
     return result.reshape(frames, height, across, -1)
 
@@ -237,7 +240,7 @@
     return sums, above, below
 
 
-def fast_conv_input(values):
+def fast_conv_input(values, ready):
     sums = local_sums(values.astype(jnp.float32))
     w = lax.axis_index("wa")
     s_w, beside = swap_with(sums, jnp.where(w == 0, values[:, :, -1:], values[:, :, :1]), "wa", 1)
@@ -245,12 +248,13 @@
     x = jnp.concatenate([beside, values, beside], axis=2)
     sums, above, below = ha_round(sums, x[:, :1], x[:, -1:])
     x = jnp.concatenate([above, x, below], axis=1)
+    x, sums, ready = lax.optimization_barrier((x, sums, ready))
     s_t, earlier = swap_with(sums, x[-2:], "ta", 1)
     sums = sums + s_t
     opening = jnp.concatenate([x[:1], x[:1]], axis=0)
     earlier = jnp.where(lax.axis_index("ta") == 0, opening, earlier)
     x = jnp.concatenate([earlier, x], axis=0)
-    return finish_stats(sums, values), x
+    return finish_stats(sums, values), x, ready
 
 
 def fast_latent_input(values):
@@ -264,16 +268,16 @@
     return finish_stats(sums, values), x
 
 
-def norm_conv(values, gain, shift, kernel):
+def norm_conv(values, gain, shift, taps, ready):
     frames, height, across, _ = values.shape
     if fast_mesh():
-        stats, extended = fast_conv_input(values)
+        stats, extended, ready = fast_conv_input(values, ready)
     else:
         stats = group_stats(values.astype(jnp.float32))
         extended = conv_halo(values)
     act = activate(extended.astype(jnp.float32), stats, gain, shift)
     act = jnp.where(inside_mask(height + 2, across + 2, 1), act, 0.0).astype(jnp.bfloat16)
-    return valid_conv(act, kernel, frames, height, across)
+    return valid_conv(act, taps, frames, height, across), ready
 
 
 def per_device(
@@ -289,16 +293,18 @@
     conv_b,
 ):
     frames, height, across, channels = latents.shape
+    taps_a = conv_taps(conv_a)
     if fast_mesh():
         stats, extended = fast_latent_input(latents)
+        extended, stats, taps_a = lax.optimization_barrier((extended, stats, taps_a))
     else:
         stats = group_stats(latents.astype(jnp.float32))
         extended = latent_halo(latents)
     activated = activate(extended.astype(jnp.float32), stats, norm1_gain, norm1_shift)
     activated = jnp.where(inside_mask(height + 1, across + 1, 0), activated, 0.0)
     lifted = upsample(activated.astype(jnp.bfloat16), up_weight).astype(jnp.bfloat16)
-    hidden = norm_conv(lifted, norm2_gain, norm2_shift, conv_a).astype(jnp.bfloat16)
-    branch = norm_conv(hidden, norm3_gain, norm3_shift, conv_b)
+    hidden, taps_b = norm_conv(lifted, norm2_gain, norm2_shift, taps_a, conv_taps(conv_b))
+    branch, _ = norm_conv(hidden.astype(jnp.bfloat16), norm3_gain, norm3_shift, taps_b, None)
     return (lifted.astype(jnp.float32) + branch).astype(jnp.bfloat16)
 
 

time: 77.8 us -> 91.6 us (1.18)
  local copies, waits for them, and re-layouts: 20.9 us -> 25.9 us
  waiting for transfers between devices: 17.7 us -> 22.5 us
  other arithmetic: 11 us -> 13.2 us
  starting transfers between devices: 18.3 us -> 19.9 us
    ppermute x15, waiting for transfers between devices: 17.7 us -> 22.5 us  [swap(): return lax.ppermute(x, axis, [(i, i ^ distance) for i in range(size)])]
    unnamed x39 -> x57, local copies, waits for them, and re-layouts: 3.58 us -> 5.83 us
    convert_element_type x2, other arithmetic: 3.58 us -> 1.75 us  [norm_conv(): jnp.where(inside_mask(height + 2, across + 2, 1), act, 0.0)]
    slice x2 -> x6, local copies, waits for them, and re-layouts: 7.42 us -> 5.66 us  [the longest x2 5.57 us: conv_taps(): return [kernel[step_t].reshape(9 * channels, -1) for step_t in range(3)]]
    ppermute x15, starting transfers between devices: 18.3 us -> 19.9 us  [swap(): return lax.ppermute(x, axis, [(i, i ^ distance) for i in range(size)])]
    squeeze x1, local copies, waits for them, and re-layouts: 1.65 us -> 2.82 us  [upsample(): kernel[1, 1]]
    concatenate x0 -> x1, other arithmetic: none -> 1.03 us  [fast_latent_input(): x = jnp.concatenate([x, below], axis=1)]
    slice x2, local copies, waits for them, and re-layouts: 0.06 us -> 1.06 us  [swap_with(): return (unpack_sums(got[cut:], sums), got[:cut].reshape(payload.shape))]
  transfers between devices with their start and end apart: 15 -> 15, of which waited for: 10 -> 10; matrix products, arithmetic and copies ran while one was open for 14% -> 15% of each run, Pallas kernels for 0% -> 0%
where the time goes in v11:
time: 91.6 us; the launch traced here: 91 us
  local copies, waits for them, and re-layouts  25.9 us (28%)
  waiting for transfers between devices  22.5 us (25%)
  starting transfers between devices  19.9 us (22%)
  other arithmetic  13.2 us (14%)
  matrix products  8.57 us (9%)
  between operations  0.93 us (1%)
    ppermute x15, waiting for transfers between devices, swap(): return lax.ppermute(x, axis, [(i, i ^ distance) for i in range(size)])  22.5 us
    ppermute x15, starting transfers between devices, swap(): return lax.ppermute(x, axis, [(i, i ^ distance) for i in range(size)])  19.9 us
    dot_general x6, matrix products, valid_conv(): part = jnp.dot(window, taps[step_t], preferred_element_type=jnp.float32)  6.5 us
    unnamed x57, local copies, waits for them, and re-layouts  5.83 us
    slice x2, local copies, waits for them, and re-layouts, conv_taps(): return [kernel[step_t].reshape(9 * channels, -1) for step_t in range(3)]  5.57 us
    squeeze x1, local copies, waits for them, and re-layouts, upsample(): kernel[1, 1]  2.82 us
    reduce_sum x5, other arithmetic, local_sums(): jnp.sum(grouped, axis=(0, 2))  2.18 us
    slice x2, local copies, waits for them, and re-layouts, valid_conv(): window = wide[step_t:step_t + frames].reshape(-1, 9 * channels)  2.15 us
  transfers between devices with their start and end apart: 15, of which 10 were waited for; matrix products, arithmetic and copies ran while one was open for 15% of the time, Pallas kernels for 0%

profile of v11, /device:TPU:0, one launch (start us, length us, event | category | flops | bytes accessed | tf_op | source)
XLA Modules:
  0.0 91.0 jit_solution(7598163998340777427)
XLA Ops:
  0.0 1.0 %convert_reduce_fusion.2 = (f32[512]{0:T(512)S(1)}, f32[512]{0:T(512)S(1)}) fusion(bf16[3,2,32,512]{3,2,1,0:T(8,128)(2,1)} %param.10), kind=kLoop, calls=%fused_computation.54 | loop fusion | flops 392192 | bytes 200704 | tf_op jit(solution)/shard_map/reduce_sum | solution.py:182
  1.4 0.6 pad_maximum_fusion.21
  2.4 0.8 slice_reduce_fusion
  3.3 1.8 %constant_dynamic-update-slice_fusion.1 = bf16[3,2,33,512]{3,2,1,0:T(8,128)(2,1)} fusion(bf16[3,2,32,512]{3,2,1,0:T(8,128)(2,1)} %param.10), kind=kLoop, calls=%fused_computation.98 | loop fusion | bytes 393216
  5.0 0.5 compare_or_fusion.1
  5.6 2.8 %slice_bitcast_fusion.7 = (bf16[512,256]{1,0:T(8,128)(2,1)}, bf16[512,256]{1,0:T(8,128)(2,1)}, bf16[512,256]{1,0:T(8,128)(2,1)}, bf16[512,256]{1,0:T(8,128)(2,1)...) fusion(bf16[3,3,512,256]{3,2,1,0:T(8,128)(2,1)} %param.13), kind=kLoop, calls=%fused_computation.72 | loop fusion | bytes 4194304 | tf_op jit(solution)/shard_map/squeeze | solution.py:129
  8.4 1.8 %fusion.117 = (bf16[1,3,3,256,256]{4,3,2,1,0:T(8,128)(2,1)}, bf16[1,3,3,256,256]{4,3,2,1,0:T(8,128)(2,1)}, bf16[1,3,3,256,256]{4,3,2,1,0:T(8,128)(2,1)}) fusion(bf16[3,3,3,256,256]{4,3,2,1,0:T(8,128)(2,1)S(1)} %copy-done), kind=kLoop, calls=%fused_computation.274 | loop fusion | bytes 7077888 | tf_op jit(solution)/shard_map/slice | solution.py:147
  10.3 0.7 fusion.53
  11.3 2.6 %collective-permute-start.1 = (bf16[7,512]{1,0:T(8,128)(2,1)S(1)}, bf16[7,512]{1,0:T(8,128)(2,1)S(1)}, u32[]{:S(2)}, u32[]{:S(2)}) collective-permute-start(bf16[7,512]{1,0:T(8,128)(2,1)S(1)} %pad_maximum_fusion.18), channel_id=1, source_target_pairs={{0,2},{2,0},{1,3},{3,1},{4,6},{6,4},{5,7},{7,5},{8,10},{10,8},{9,1... | collective-permute-start | bytes 21512 | tf_op jit(solution)/shard_map/ppermute | solution.py:173
  13.9 1.6 %collective-permute-done.1 = bf16[7,512]{1,0:T(8,128)(2,1)S(1)} collective-permute-done((bf16[7,512]{1,0:T(8,128)(2,1)S(1)}, bf16[7,512]{1,0:T(8,128)(2,1)S(1)}, u32[]{:S(2)}, u32[]{:S(2)}) %collective-permute-start.1) | collective-permute-done | bytes 7200 | tf_op jit(solution)/shard_map/ppermute | solution.py:173
  16.1 0.6 constant_dynamic-update-slice_fusion
  16.7 1.0 %slice.640 = bf16[3,1,33,512]{3,2,1,0:T(8,128)(2,1)S(1)} slice(bf16[3,2,33,512]{3,2,1,0:T(8,128)(2,1)} %constant_dynamic-update-slice_fusion), slice={[0:3], [0:1], [0:33], [0:512]} | slice | bytes 202752 | tf_op jit(solution)/shard_map/slice | solution.py:266
  17.7 4.2 %collective-permute-start.3 = (bf16[100,512]{1,0:T(8,128)(2,1)S(1)}, bf16[100,512]{1,0:T(8,128)(2,1)S(1)}, u32[]{:S(2)}, u32[]{:S(2)}) collective-permute-start(bf16[100,512]{1,0:T(8,128)(2,1)S(1)} %pad_maximum_fusion.17), channel_id=1, source_target_pairs={{0,12},{4,8},{8,4},{12,0},{1,13},{5,9},{9,5},{13,1},{2,14},{6,10},... | collective-permute-start | bytes 307208 | tf_op jit(solution)/shard_map/ppermute | solution.py:173
  21.9 0.7 broadcast_and_fusion.1
  22.6 0.6 collective-permute-start.2
  23.2 1.7 %collective-permute-done.3 = bf16[100,512]{1,0:T(8,128)(2,1)S(1)} collective-permute-done((bf16[100,512]{1,0:T(8,128)(2,1)S(1)}, bf16[100,512]{1,0:T(8,128)(2,1)S(1)}, u32[]{:S(2)}, u32[]{:S(2)}) %collective-permute-start.3) | collective-permute-done | bytes 102432 | tf_op jit(solution)/shard_map/ppermute | solution.py:173
  25.0 2.3 %collective-permute-done.2 = bf16[100,512]{1,0:T(8,128)(2,1)S(1)} collective-permute-done((bf16[100,512]{1,0:T(8,128)(2,1)S(1)}, bf16[100,512]{1,0:T(8,128)(2,1)S(1)}, u32[]{:S(2)}, u32[]{:S(2)}) %collective-permute-start.2) | collective-permute-done | bytes 102432 | tf_op jit(solution)/shard_map/ppermute | solution.py:173
  28.0 1.0 %pad_maximum_fusion.6 = bf16[3,3,33,512]{3,2,1,0:T(8,128)(2,1)S(1)} fusion(bf16[3,1,33,512]{3,2,1,0:T(8,128)(2,1)S(1)} %select_n.168, bf16[3,2,33,512]{3,2,1,0:T(8,128)(2,1)} %constant_dynamic-update-slice_fusion), kind=kLoop, calls=%fused_computation.62 | loop fusion | flops 152064 | bytes 608256 | tf_op jit(solution)/shard_map/concatenate | solution.py:267
  30.7 1.2 %convolution_add_fusion.4 = bf16[192,256]{1,0:T(8,128)(2,1)S(1)} fusion(bf16[192,512]{1,0:T(8,128)(2,1)S(1)} %bitcast.118, bf16[3,3,512,256]{3,2,1,0:T(8,128)(2,1)} %param.13, f32[192,512]{1,0:T(8,128)S(1)} %fusion.15, f32[192,512]{1,0:T(8,128)S(1)} %fusion.11, f32[192,1024]{1,0:T(8,128)S(1)} %fusion.1), kind=kOutput, calls=%fused_computation.7 | convolution fusion | flops 50528256 | bytes 1146880 | tf_op jit(solution)/shard_map/dot_general | solution.py:123
  32.9 0.8 convert_reduce_fusion.1
  34.4 1.6 %collective-permute-start.5 = (bf16[13,256]{1,0:T(8,128)(2,1)S(1)}, bf16[13,256]{1,0:T(8,128)(2,1)S(1)}, u32[]{:S(2)}, u32[]{:S(2)}) collective-permute-start(bf16[13,256]{1,0:T(8,128)(2,1)S(1)} %pad_maximum_fusion.19), channel_id=1, source_target_pairs={{0,2},{2,0},{1,3},{3,1},{4,6},{6,4},{5,7},{7,5},{8,10},{10,8},{9,1... | collective-permute-start | bytes 19976 | tf_op jit(solution)/shard_map/ppermute | solution.py:173
  36.0 2.2 %collective-permute-done.5 = bf16[13,256]{1,0:T(8,128)(2,1)S(1)} collective-permute-done((bf16[13,256]{1,0:T(8,128)(2,1)S(1)}, bf16[13,256]{1,0:T(8,128)(2,1)S(1)}, u32[]{:S(2)}, u32[]{:S(2)}) %collective-permute-start.5) | collective-permute-done | bytes 6688 | tf_op jit(solution)/shard_map/ppermute | solution.py:173
  38.9 1.3 %collective-permute-start.6 = (bf16[199,256]{1,0:T(8,128)(2,1)S(1)}, bf16[199,256]{1,0:T(8,128)(2,1)S(1)}, u32[]{:S(2)}, u32[]{:S(2)}) collective-permute-start(bf16[199,256]{1,0:T(8,128)(2,1)S(1)} %get-tuple-element.93), channel_id=1, source_target_pairs={{0,4},{4,0},{8,12},{12,8},{1,5},{5,1},{9,13},{13,9},{2,6},{6,2},{1... | collective-permute-start | bytes 305672 | tf_op jit(solution)/shard_map/ppermute | solution.py:173
  40.2 3.7 %fusion.116 = (bf16[1,3,3,256,256]{4,3,2,1,0:T(8,128)(2,1)S(1)}, bf16[1,3,3,256,256]{4,3,2,1,0:T(8,128)(2,1)}, bf16[1,3,3,256,256]{4,3,2,1,0:T(8,128)(2,1)}) fusion(bf16[3,3,3,256,256]{4,3,2,1,0:T(8,128)(2,1)} %param.19), kind=kLoop, calls=%fused_computation.273 | loop fusion | bytes 7077888 | tf_op jit(solution)/shard_map/slice | solution.py:147
  43.9 2.4 %collective-permute-start.8 = (f32[2,32]{1,0:T(2,128)S(1)}, f32[2,32]{1,0:T(2,128)S(1)}, u32[]{:S(2)}, u32[]{:S(2)}) collective-permute-start(f32[2,32]{1,0:T(2,128)S(1)} %get-tuple-element.46), channel_id=1, source_target_pairs={{0,8},{4,12},{8,0},{12,4},{1,9},{5,13},{9,1},{13,5},{2,10},{6,14},... | collective-permute-start | bytes 776 | tf_op jit(solution)/shard_map/ppermute | solution.py:173
  46.3 0.8 collective-permute-start.7
  47.2 5.6 %collective-permute-done.7 = bf16[199,256]{1,0:T(8,128)(2,1)S(1)} collective-permute-done((bf16[199,256]{1,0:T(8,128)(2,1)S(1)}, bf16[199,256]{1,0:T(8,128)(2,1)S(1)}, u32[]{:S(2)}, u32[]{:S(2)}) %collective-permute-start.7) | collective-permute-done | bytes 101920 | tf_op jit(solution)/shard_map/ppermute | solution.py:173
  54.2 1.6 %collective-permute-done.9 = bf16[793,256]{1,0:T(8,128)(2,1)S(1)} collective-permute-done((bf16[793,256]{1,0:T(8,128)(2,1)S(1)}, bf16[793,256]{1,0:T(8,128)(2,1)S(1)}, u32[]{:S(2)}, u32[]{:S(2)}) %collective-permute-start.9) | collective-permute-done | bytes 406048 | tf_op jit(solution)/shard_map/ppermute | solution.py:173
  56.6 0.9 select_convert_fusion.1
  59.2 1.2 %fusion.115 = (bf16[3,4,64,2304]{3,2,1,0:T(8,128)(2,1)S(1)}, bf16[3,4,64,2304]{3,2,1,0:T(8,128)(2,1)S(1)}, bf16[3,4,64,2304]{3,2,1,0:T(8,128)(2,1)S(1)}) fusion(bf16[5,4,64,2304]{3,2,1,0:T(8,128)(2,1)S(1)} %slice_dynamic-update-slice_fusion.9), kind=kLoop, calls=%fused_computation.272 | loop fusion | bytes 21233664 | tf_op jit(solution)/shard_map/slice | solution.py:157
  60.5 1.1 %fusion.120 = f32[768,256]{1,0:T(8,128)S(1)} fusion(bf16[768,2304]{1,0:T(8,128)(2,1)S(1)} %bitcast.107, bf16[2304,256]{1,0:T(8,128)(2,1)S(1)} %bitcast.114), kind=kOutput, calls=%fused_computation.277 | convolution fusion | flops 905969664 | bytes 5505024 | tf_op jit(solution)/shard_map/dot_general | solution.py:158
  61.8 1.1 %convolution_add_fusion.3 = f32[768,256]{1,0:T(8,128)S(1)} fusion(f32[768,256]{1,0:T(8,128)S(1)} %fusion.120, bf16[768,2304]{1,0:T(8,128)(2,1)S(1)} %bitcast.105, bf16[2304,256]{1,0:T(8,128)(2,1)S(1)} %bitcast.113), kind=kOutput, calls=%fused_computation.5 | convolution fusion | flops 906166272 | bytes 6291456 | tf_op jit(solution)/shard_map/dot_general | solution.py:158
  63.0 1.1 %convert_reduce_fusion = (f32[256]{0:T(256)S(1)}, f32[256]{0:T(256)S(1)}, bf16[768,256]{1,0:T(8,128)(2,1)S(1)}) fusion(f32[768,256]{1,0:T(8,128)S(1)} %convolution_add_fusion.3, bf16[768,2304]{1,0:T(8,128)(2,1)S(1)} %bitcast.103, bf16[2304,256]{1,0:T(8,128)(2,1)S(1)} %bitcast.112), kind=kOutput, calls=%fused_computation.17 | convolution fusion | flops 907148800 | bytes 5900288 | tf_op jit(solution)/shard_map/dot_general | solution.py:158
  64.8 1.6 %collective-permute-start.10 = (bf16[13,256]{1,0:T(8,128)(2,1)S(1)}, bf16[13,256]{1,0:T(8,128)(2,1)S(1)}, u32[]{:S(2)}, u32[]{:S(2)}) collective-permute-start(bf16[13,256]{1,0:T(8,128)(2,1)S(1)} %pad_maximum_fusion.20), channel_id=1, source_target_pairs={{0,2},{2,0},{1,3},{3,1},{4,6},{6,4},{5,7},{7,5},{8,10},{10,8},{9,1... | collective-permute-start | bytes 19976 | tf_op jit(solution)/shard_map/ppermute | solution.py:173
  66.4 2.2 %collective-permute-done.10 = bf16[13,256]{1,0:T(8,128)(2,1)S(1)} collective-permute-done((bf16[13,256]{1,0:T(8,128)(2,1)S(1)}, bf16[13,256]{1,0:T(8,128)(2,1)S(1)}, u32[]{:S(2)}, u32[]{:S(2)}) %collective-permute-start.10) | collective-permute-done | bytes 6688 | tf_op jit(solution)/shard_map/ppermute | solution.py:173
  69.4 1.4 %collective-permute-start.13 = (f32[2,32]{1,0:T(2,128)S(1)}, f32[2,32]{1,0:T(2,128)S(1)}, u32[]{:S(2)}, u32[]{:S(2)}) collective-permute-start(f32[2,32]{1,0:T(2,128)S(1)} %get-tuple-element.41), channel_id=1, source_target_pairs={{0,8},{4,12},{8,0},{12,4},{1,9},{5,13},{9,1},{13,5},{2,10},{6,14},... | collective-permute-start | bytes 776 | tf_op jit(solution)/shard_map/ppermute | solution.py:173
  70.8 3.0 %collective-permute-start.12 = (bf16[199,256]{1,0:T(8,128)(2,1)S(1)}, bf16[199,256]{1,0:T(8,128)(2,1)S(1)}, u32[]{:S(2)}, u32[]{:S(2)}) collective-permute-start(bf16[199,256]{1,0:T(8,128)(2,1)S(1)} %get-tuple-element.87), channel_id=1, source_target_pairs={{0,12},{4,8},{8,4},{12,0},{1,13},{5,9},{9,5},{13,1},{2,14},{6,10},... | collective-permute-start | bytes 305672 | tf_op jit(solution)/shard_map/ppermute | solution.py:173
  73.8 1.4 %collective-permute-done.11 = bf16[199,256]{1,0:T(8,128)(2,1)S(1)} collective-permute-done((bf16[199,256]{1,0:T(8,128)(2,1)S(1)}, bf16[199,256]{1,0:T(8,128)(2,1)S(1)}, u32[]{:S(2)}, u32[]{:S(2)}) %collective-permute-start.11) | collective-permute-done | bytes 101920 | tf_op jit(solution)/shard_map/ppermute | solution.py:173
  75.3 2.0 %collective-permute-done.12 = bf16[199,256]{1,0:T(8,128)(2,1)S(1)} collective-permute-done((bf16[199,256]{1,0:T(8,128)(2,1)S(1)}, bf16[199,256]{1,0:T(8,128)(2,1)S(1)}, u32[]{:S(2)}, u32[]{:S(2)}) %collective-permute-start.12) | collective-permute-done | bytes 101920 | tf_op jit(solution)/shard_map/ppermute | solution.py:173
  78.5 1.8 %collective-permute-done.14 = bf16[793,256]{1,0:T(8,128)(2,1)} collective-permute-done((bf16[793,256]{1,0:T(8,128)(2,1)S(1)}, bf16[793,256]{1,0:T(8,128)(2,1)}, u32[]{:S(2)}, u32[]{:S(2)}) %collective-permute-start.14) | collective-permute-done | bytes 406048 | tf_op jit(solution)/shard_map/ppermute | solution.py:173
  80.3 0.7 slice_convert_fusion
  81.5 1.0 %slice.718 = bf16[792,256]{1,0:T(8,128)(2,1)S(1)} slice(bf16[793,256]{1,0:T(8,128)(2,1)} %collective-permute-done.14), slice={[0:792], [0:256]} | slice | bytes 811008 | tf_op jit(solution)/shard_map/slice | solution.py:227
  82.8 0.9 select_convert_fusion
  85.4 1.0 %fusion.114 = (bf16[3,4,64,2304]{3,2,1,0:T(8,128)(2,1)S(1)}, bf16[3,4,64,2304]{3,2,1,0:T(8,128)(2,1)S(1)}, bf16[3,4,64,2304]{3,2,1,0:T(8,128)(2,1)S(1)}) fusion(bf16[5,4,64,2304]{3,2,1,0:T(8,128)(2,1)S(1)} %slice_dynamic-update-slice_fusion), kind=kLoop, calls=%fused_computation.271 | loop fusion | bytes 21233664 | tf_op jit(solution)/shard_map/slice | solution.py:157
  86.7 1.1 %fusion.121 = f32[768,256]{1,0:T(8,128)S(1)} fusion(bf16[768,2304]{1,0:T(8,128)(2,1)S(1)} %bitcast.108, bf16[2304,256]{1,0:T(8,128)(2,1)S(1)} %bitcast.117), kind=kOutput, calls=%fused_computation.278 | convolution fusion | flops 905969664 | bytes 5505024 | tf_op jit(solution)/shard_map/dot_general | solution.py:158
  88.0 1.1 %convolution_add_fusion.1 = f32[768,256]{1,0:T(8,128)S(1)} fusion(f32[768,256]{1,0:T(8,128)S(1)} %fusion.121, bf16[768,2304]{1,0:T(8,128)(2,1)S(1)} %bitcast.106, bf16[2304,256]{1,0:T(8,128)(2,1)S(1)} %bitcast.116), kind=kOutput, calls=%fused_computation.3 | convolution fusion | flops 906166272 | bytes 6291456 | tf_op jit(solution)/shard_map/dot_general | solution.py:158
  89.1 1.1 %convolution_add_fusion = f32[768,256]{1,0:T(8,128)S(1)} fusion(f32[768,256]{1,0:T(8,128)S(1)} %convolution_add_fusion.1, bf16[768,2304]{1,0:T(8,128)(2,1)S(1)} %bitcast.104, bf16[2304,256]{1,0:T(8,128)(2,1)S(1)} %bitcast.115), kind=kOutput, calls=%fused_computation.2 | convolution fusion | flops 906166272 | bytes 6291456 | tf_op jit(solution)/shard_map/dot_general | solution.py:158
  90.1 0.9 add_convert_fusion
  (247 shorter events, 16.3 us)
Async XLA Ops:
  2.0 8.3 %collective-permute-start = (f32[2,32]{1,0:T(2,128)}, f32[2,32]{1,0:T(2,128)}, u32[]{:S(2)}, u32[]{:S(2)}) collective-permute-start(f32[2,32]{1,0:T(2,128)} %pad_maximum_fusion.21), channel_id=1, source_target_pairs={{0,1},{1,0},{2,3},{3,2},{4,5},{5,4},{6,7},{7,6},{8,9},{9,8},{10,11... | collective-permute-start | bytes 776 | tf_op jit(solution)/shard_map/ppermute | solution.py:173
  3.3 5.1 %copy-start = (bf16[3,3,3,256,256]{4,3,2,1,0:T(8,128)(2,1)S(1)}, bf16[3,3,3,256,256]{4,3,2,1,0:T(8,128)(2,1)}, u32[]{:S(2)}) copy-start(bf16[3,3,3,256,256]{4,3,2,1,0:T(8,128)(2,1)} %param.16) | copy-start | bytes 10616836
  10.2 18.8 %copy-start.14 = (f32[512]{0:T(512)S(1)}, f32[512]{0:T(512)}, u32[]{:S(2)}) copy-start(f32[512]{0:T(512)} %param.12) | copy-start | bytes 6148
  10.2 18.8 %copy-start.15 = (f32[512]{0:T(512)S(1)}, f32[512]{0:T(512)}, u32[]{:S(2)}) copy-start(f32[512]{0:T(512)} %param.11) | copy-start | bytes 6148
  11.3 4.2 %collective-permute-start.1 = (bf16[7,512]{1,0:T(8,128)(2,1)S(1)}, bf16[7,512]{1,0:T(8,128)(2,1)S(1)}, u32[]{:S(2)}, u32[]{:S(2)}) collective-permute-start(bf16[7,512]{1,0:T(8,128)(2,1)S(1)} %pad_maximum_fusion.18), channel_id=1, source_target_pairs={{0,2},{2,0},{1,3},{3,1},{4,6},{6,4},{5,7},{7,5},{8,10},{10,8},{9,1... | collective-permute-start | bytes 21512 | tf_op jit(solution)/shard_map/ppermute | solution.py:173
  16.7 12.8 %copy-start.12 = (bf16[512,256]{1,0:T(8,128)(2,1)S(1)}, bf16[512,256]{1,0:T(8,128)(2,1)}, u32[]{:S(2)}) copy-start(bf16[512,256]{1,0:T(8,128)(2,1)} %get-tuple-element.66) | copy-start | bytes 786436
  16.7 12.8 %copy-start.13 = (bf16[512,256]{1,0:T(8,128)(2,1)S(1)}, bf16[512,256]{1,0:T(8,128)(2,1)}, u32[]{:S(2)}) copy-start(bf16[512,256]{1,0:T(8,128)(2,1)} %get-tuple-element.67) | copy-start | bytes 786436
  17.7 7.1 %collective-permute-start.3 = (bf16[100,512]{1,0:T(8,128)(2,1)S(1)}, bf16[100,512]{1,0:T(8,128)(2,1)S(1)}, u32[]{:S(2)}, u32[]{:S(2)}) collective-permute-start(bf16[100,512]{1,0:T(8,128)(2,1)S(1)} %pad_maximum_fusion.17), channel_id=1, source_target_pairs={{0,12},{4,8},{8,4},{12,0},{1,13},{5,9},{9,5},{13,1},{2,14},{6,10},... | collective-permute-start | bytes 307208 | tf_op jit(solution)/shard_map/ppermute | solution.py:173
  22.6 5.0 %collective-permute-start.4 = (f32[2,32]{1,0:T(2,128)S(1)}, f32[2,32]{1,0:T(2,128)S(1)}, u32[]{:S(2)}, u32[]{:S(2)}) collective-permute-start(f32[2,32]{1,0:T(2,128)S(1)} %get-tuple-element.49), channel_id=1, source_target_pairs={{0,8},{4,12},{8,0},{12,4},{1,9},{5,13},{9,1},{13,5},{2,10},{6,14},... | collective-permute-start | bytes 776 | tf_op jit(solution)/shard_map/ppermute | solution.py:173
  22.6 4.7 %collective-permute-start.2 = (bf16[100,512]{1,0:T(8,128)(2,1)S(1)}, bf16[100,512]{1,0:T(8,128)(2,1)S(1)}, u32[]{:S(2)}, u32[]{:S(2)}) collective-permute-start(bf16[100,512]{1,0:T(8,128)(2,1)S(1)} %pad_maximum_fusion.17), channel_id=1, source_target_pairs={{0,4},{4,0},{8,12},{12,8},{1,5},{5,1},{9,13},{13,9},{2,6},{6,2},{1... | collective-permute-start | bytes 307208 | tf_op jit(solution)/shard_map/ppermute | solution.py:173
  27.9 1.8 %copy-start.10 = (bf16[512,256]{1,0:T(8,128)(2,1)S(1)}, bf16[512,256]{1,0:T(8,128)(2,1)}, u32[]{:S(2)}) copy-start(bf16[512,256]{1,0:T(8,128)(2,1)} %get-tuple-element.65) | copy-start | bytes 786436
  27.9 1.8 %copy-start.11 = (bf16[512,256]{1,0:T(8,128)(2,1)S(1)}, bf16[512,256]{1,0:T(8,128)(2,1)}, u32[]{:S(2)}) copy-start(bf16[512,256]{1,0:T(8,128)(2,1)} %get-tuple-element.71) | copy-start | bytes 786436
  29.0 1.0 %copy-start.6 = (bf16[512,256]{1,0:T(8,128)(2,1)S(1)}, bf16[512,256]{1,0:T(8,128)(2,1)}, u32[]{:S(2)}) copy-start(bf16[512,256]{1,0:T(8,128)(2,1)} %get-tuple-element.64) | copy-start | bytes 786436
  29.1 1.0 %copy-start.7 = (bf16[512,256]{1,0:T(8,128)(2,1)S(1)}, bf16[512,256]{1,0:T(8,128)(2,1)}, u32[]{:S(2)}) copy-start(bf16[512,256]{1,0:T(8,128)(2,1)} %get-tuple-element.68) | copy-start | bytes 786436
  29.1 1.1 %copy-start.8 = (bf16[512,256]{1,0:T(8,128)(2,1)S(1)}, bf16[512,256]{1,0:T(8,128)(2,1)}, u32[]{:S(2)}) copy-start(bf16[512,256]{1,0:T(8,128)(2,1)} %get-tuple-element.69) | copy-start | bytes 786436
  29.1 1.2 %copy-start.9 = (bf16[512,256]{1,0:T(8,128)(2,1)S(1)}, bf16[512,256]{1,0:T(8,128)(2,1)}, u32[]{:S(2)}) copy-start(bf16[512,256]{1,0:T(8,128)(2,1)} %get-tuple-element.70) | copy-start | bytes 786436
  34.4 3.7 %collective-permute-start.5 = (bf16[13,256]{1,0:T(8,128)(2,1)S(1)}, bf16[13,256]{1,0:T(8,128)(2,1)S(1)}, u32[]{:S(2)}, u32[]{:S(2)}) collective-permute-start(bf16[13,256]{1,0:T(8,128)(2,1)S(1)} %pad_maximum_fusion.19), channel_id=1, source_target_pairs={{0,2},{2,0},{1,3},{3,1},{4,6},{6,4},{5,7},{7,5},{8,10},{10,8},{9,1... | collective-permute-start | bytes 19976 | tf_op jit(solution)/shard_map/ppermute | solution.py:173
  38.9 8.2 %collective-permute-start.6 = (bf16[199,256]{1,0:T(8,128)(2,1)S(1)}, bf16[199,256]{1,0:T(8,128)(2,1)S(1)}, u32[]{:S(2)}, u32[]{:S(2)}) collective-permute-start(bf16[199,256]{1,0:T(8,128)(2,1)S(1)} %get-tuple-element.93), channel_id=1, source_target_pairs={{0,4},{4,0},{8,12},{12,8},{1,5},{5,1},{9,13},{13,9},{2,6},{6,2},{1... | collective-permute-start | bytes 305672 | tf_op jit(solution)/shard_map/ppermute | solution.py:173
  43.9 9.5 %collective-permute-start.8 = (f32[2,32]{1,0:T(2,128)S(1)}, f32[2,32]{1,0:T(2,128)S(1)}, u32[]{:S(2)}, u32[]{:S(2)}) collective-permute-start(f32[2,32]{1,0:T(2,128)S(1)} %get-tuple-element.46), channel_id=1, source_target_pairs={{0,8},{4,12},{8,0},{12,4},{1,9},{5,13},{9,1},{13,5},{2,10},{6,14},... | collective-permute-start | bytes 776 | tf_op jit(solution)/shard_map/ppermute | solution.py:173
  46.3 6.5 %collective-permute-start.7 = (bf16[199,256]{1,0:T(8,128)(2,1)S(1)}, bf16[199,256]{1,0:T(8,128)(2,1)S(1)}, u32[]{:S(2)}, u32[]{:S(2)}) collective-permute-start(bf16[199,256]{1,0:T(8,128)(2,1)S(1)} %get-tuple-element.94), channel_id=1, source_target_pairs={{0,12},{4,8},{8,4},{12,0},{1,13},{5,9},{9,5},{13,1},{2,14},{6,10},... | collective-permute-start | bytes 305672 | tf_op jit(solution)/shard_map/ppermute | solution.py:173
  53.9 2.6 %copy-start.16 = (f32[256]{0:T(256)S(1)}, f32[256]{0:T(256)}, u32[]{:S(2)}) copy-start(f32[256]{0:T(256)} %param.15) | copy-start | bytes 3076
  53.9 2.6 %copy-start.17 = (f32[256]{0:T(256)S(1)}, f32[256]{0:T(256)}, u32[]{:S(2)}) copy-start(f32[256]{0:T(256)} %param.14) | copy-start | bytes 3076
  54.0 1.8 %collective-permute-start.9 = (bf16[793,256]{1,0:T(8,128)(2,1)S(1)}, bf16[793,256]{1,0:T(8,128)(2,1)S(1)}, u32[]{:S(2)}, u32[]{:S(2)}) collective-permute-start(bf16[793,256]{1,0:T(8,128)(2,1)S(1)} %pad_maximum_fusion.2), channel_id=1, source_target_pairs={{0,1},{1,0},{2,3},{3,2},{4,5},{5,4},{6,7},{7,6},{8,9},{9,8},{10,11... | collective-permute-start | bytes 1218056 | tf_op jit(solution)/shard_map/ppermute | solution.py:173
  59.2 1.3 %copy-start.3 = (bf16[1,3,3,256,256]{4,3,2,1,0:T(8,128)(2,1)S(1)}, bf16[1,3,3,256,256]{4,3,2,1,0:T(8,128)(2,1)}, u32[]{:S(2)}) copy-start(bf16[1,3,3,256,256]{4,3,2,1,0:T(8,128)(2,1)} %get-tuple-element.62) | copy-start | bytes 3538948
  60.5 1.3 %copy-start.2 = (bf16[1,3,3,256,256]{4,3,2,1,0:T(8,128)(2,1)S(1)}, bf16[1,3,3,256,256]{4,3,2,1,0:T(8,128)(2,1)}, u32[]{:S(2)}) copy-start(bf16[1,3,3,256,256]{4,3,2,1,0:T(8,128)(2,1)} %get-tuple-element.63) | copy-start | bytes 3538948
  61.8 1.3 %copy-start.1 = (bf16[1,3,3,256,256]{4,3,2,1,0:T(8,128)(2,1)S(1)}, bf16[1,3,3,256,256]{4,3,2,1,0:T(8,128)(2,1)}, u32[]{:S(2)}) copy-start(bf16[1,3,3,256,256]{4,3,2,1,0:T(8,128)(2,1)} %get-tuple-element.61) | copy-start | bytes 3538948
  64.8 3.7 %collective-permute-start.10 = (bf16[13,256]{1,0:T(8,128)(2,1)S(1)}, bf16[13,256]{1,0:T(8,128)(2,1)S(1)}, u32[]{:S(2)}, u32[]{:S(2)}) collective-permute-start(bf16[13,256]{1,0:T(8,128)(2,1)S(1)} %pad_maximum_fusion.20), channel_id=1, source_target_pairs={{0,2},{2,0},{1,3},{3,1},{4,6},{6,4},{5,7},{7,5},{8,10},{10,8},{9,1... | collective-permute-start | bytes 19976 | tf_op jit(solution)/shard_map/ppermute | solution.py:173
  69.3 5.8 %collective-permute-start.11 = (bf16[199,256]{1,0:T(8,128)(2,1)S(1)}, bf16[199,256]{1,0:T(8,128)(2,1)S(1)}, u32[]{:S(2)}, u32[]{:S(2)}) collective-permute-start(bf16[199,256]{1,0:T(8,128)(2,1)S(1)} %get-tuple-element.86), channel_id=1, source_target_pairs={{0,4},{4,0},{8,12},{12,8},{1,5},{5,1},{9,13},{13,9},{2,6},{6,2},{1... | collective-permute-start | bytes 305672 | tf_op jit(solution)/shard_map/ppermute | solution.py:173
  69.4 8.4 %collective-permute-start.13 = (f32[2,32]{1,0:T(2,128)S(1)}, f32[2,32]{1,0:T(2,128)S(1)}, u32[]{:S(2)}, u32[]{:S(2)}) collective-permute-start(f32[2,32]{1,0:T(2,128)S(1)} %get-tuple-element.41), channel_id=1, source_target_pairs={{0,8},{4,12},{8,0},{12,4},{1,9},{5,13},{9,1},{13,5},{2,10},{6,14},... | collective-permute-start | bytes 776 | tf_op jit(solution)/shard_map/ppermute | solution.py:173
  70.8 6.5 %collective-permute-start.12 = (bf16[199,256]{1,0:T(8,128)(2,1)S(1)}, bf16[199,256]{1,0:T(8,128)(2,1)S(1)}, u32[]{:S(2)}, u32[]{:S(2)}) collective-permute-start(bf16[199,256]{1,0:T(8,128)(2,1)S(1)} %get-tuple-element.87), channel_id=1, source_target_pairs={{0,12},{4,8},{8,4},{12,0},{1,13},{5,9},{9,5},{13,1},{2,14},{6,10},... | collective-permute-start | bytes 305672 | tf_op jit(solution)/shard_map/ppermute | solution.py:173
  78.3 4.4 %copy-start.18 = (f32[256]{0:T(256)S(1)}, f32[256]{0:T(256)}, u32[]{:S(2)}) copy-start(f32[256]{0:T(256)} %param.18) | copy-start | bytes 3076
  78.3 4.4 %copy-start.19 = (f32[256]{0:T(256)S(1)}, f32[256]{0:T(256)}, u32[]{:S(2)}) copy-start(f32[256]{0:T(256)} %param.17) | copy-start | bytes 3076
  78.4 1.9 %collective-permute-start.14 = (bf16[793,256]{1,0:T(8,128)(2,1)S(1)}, bf16[793,256]{1,0:T(8,128)(2,1)}, u32[]{:S(2)}, u32[]{:S(2)}) collective-permute-start(bf16[793,256]{1,0:T(8,128)(2,1)S(1)} %pad_maximum_fusion.3), channel_id=1, source_target_pairs={{0,1},{1,0},{2,3},{3,2},{4,5},{5,4},{6,7},{7,6},{8,9},{9,8},{10,11... | collective-permute-start | bytes 1218056 | tf_op jit(solution)/shard_map/ppermute | solution.py:173
  85.4 1.3 %copy-start.5 = (bf16[1,3,3,256,256]{4,3,2,1,0:T(8,128)(2,1)S(1)}, bf16[1,3,3,256,256]{4,3,2,1,0:T(8,128)(2,1)}, u32[]{:S(2)}) copy-start(bf16[1,3,3,256,256]{4,3,2,1,0:T(8,128)(2,1)} %get-tuple-element.59) | copy-start | bytes 3538948
  86.7 1.3 %copy-start.4 = (bf16[1,3,3,256,256]{4,3,2,1,0:T(8,128)(2,1)S(1)}, bf16[1,3,3,256,256]{4,3,2,1,0:T(8,128)(2,1)}, u32[]{:S(2)}) copy-start(bf16[1,3,3,256,256]{4,3,2,1,0:T(8,128)(2,1)} %get-tuple-element.60) | copy-start | bytes 3538948

commit v12 on v10

--- a/solution.py
+++ b/solution.py
@@ -226,14 +226,20 @@
 
 def ha_round(sums, upper, lower):
     h = lax.axis_index("ha")
-    to_first = jnp.where(h % 2 == 1, upper, lower)
-    to_third = jnp.where(h == 2, upper, lower)
-    s1, got_first = swap_with(sums, to_first, "ha", 1)
+    s1, got_first = swap_with(sums, jnp.where(h % 2 == 1, upper, lower), "ha", 1)
     s2 = swap(sums, "ha", 2)
-    s3, got_third = swap_with(sums, to_third, "ha", 3)
+    inner = jnp.where(h == 2, upper, lower)
+    width = inner.shape[-1]
+    packed = pack_sums(sums, width)
+    message = jnp.concatenate([inner.reshape(-1, width), packed], axis=0)
+    got = lax.ppermute(message, "ha", [(1, 2), (2, 1)])
+    cut = got.shape[0] - packed.shape[0]
+    got_inner = got[:cut].reshape(inner.shape)
+    s_outer = lax.ppermute(sums, "ha", [(0, 3), (3, 0)])
+    s3 = jnp.where(jnp.logical_or(h == 1, h == 2), unpack_sums(got[cut:], sums), s_outer)
     sums = (sums + s1) + (s2 + s3)
-    above = jnp.where(h % 2 == 1, got_first, got_third)
-    below = jnp.where(h % 2 == 0, got_first, got_third)
+    above = jnp.where(h % 2 == 1, got_first, got_inner)
+    below = jnp.where(h % 2 == 0, got_first, got_inner)
     return sums, above, below
 
 

time: 77.8 us -> 89.4 us (1.15)
  starting transfers between devices: 18.3 us -> 32.8 us
  waiting for transfers between devices: 17.7 us -> 14.7 us
    ppermute x0 -> x6, starting transfers between devices: none -> 14.8 us  [the longest x3 12.8 us: ha_round(): s_outer = lax.ppermute(sums, 'ha', [(0, 3), (3, 0)])]
    ppermute x15 -> x12, waiting for transfers between devices: 17.7 us -> 8.18 us  [swap(): return lax.ppermute(x, axis, [(i, i ^ distance) for i in range(size)])]
    ppermute x0 -> x6, waiting for transfers between devices: none -> 6.51 us  [the longest x3 6.5 us: ha_round(): s_outer = lax.ppermute(sums, 'ha', [(0, 3), (3, 0)])]
    ppermute x15 -> x12, starting transfers between devices: 18.3 us -> 18 us  [swap(): return lax.ppermute(x, axis, [(i, i ^ distance) for i in range(size)])]
  transfers between devices with their start and end apart: 15 -> 18, of which waited for: 10 -> 7; matrix products, arithmetic and copies ran while one was open for 14% -> 13% of each run, Pallas kernels for 0% -> 0%
where the time goes in v12:
time: 89.4 us; the launch traced here: 88.9 us
  starting transfers between devices  32.8 us (37%)
  local copies, waits for them, and re-layouts  21 us (23%)
  waiting for transfers between devices  14.7 us (16%)
  other arithmetic  10.8 us (12%)
  matrix products  8.59 us (10%)
  between operations  0.98 us (1%)
    ppermute x12, starting transfers between devices, swap(): return lax.ppermute(x, axis, [(i, i ^ distance) for i in range(size)])  18 us
    ppermute x3, starting transfers between devices, ha_round(): s_outer = lax.ppermute(sums, 'ha', [(0, 3), (3, 0)])  12.8 us
    ppermute x12, waiting for transfers between devices, swap(): return lax.ppermute(x, axis, [(i, i ^ distance) for i in range(size)])  8.18 us
    slice x2, local copies, waits for them, and re-layouts, valid_conv(): kernel[step_t].reshape(9 * channels, -1)  7.49 us
    dot_general x6, matrix products, valid_conv(): jnp.dot(window, kernel[step_t].reshape(9 * channels, -1), preferred_eleme...  6.52 us
    ppermute x3, waiting for transfers between devices, ha_round(): s_outer = lax.ppermute(sums, 'ha', [(0, 3), (3, 0)])  6.5 us
    unnamed x39, local copies, waits for them, and re-layouts  3.81 us
    convert_element_type x2, other arithmetic, norm_conv(): jnp.where(inside_mask(height + 2, across + 2, 1), act, 0.0)  3.4 us
  transfers between devices with their start and end apart: 18, of which 7 were waited for; matrix products, arithmetic and copies ran while one was open for 13% of the time, Pallas kernels for 0%

profile of v12, /device:TPU:0, one launch (start us, length us, event | category | flops | bytes accessed | tf_op | source)
XLA Modules:
  0.0 88.9 jit_solution(3736151401702193527)
XLA Ops:
  0.0 1.1 %convert_reduce_fusion.2 = (f32[512]{0:T(512)S(1)}, f32[512]{0:T(512)S(1)}) fusion(bf16[3,2,32,512]{3,2,1,0:T(8,128)(2,1)} %param.10), kind=kLoop, calls=%fused_computation.52 | loop fusion | flops 392192 | bytes 200704 | tf_op jit(solution)/shard_map/reduce_sum | solution.py:179
  1.5 0.5 collective-permute-start
  2.0 1.6 %slice_bitcast_fusion.7 = (bf16[512,256]{1,0:T(8,128)(2,1)S(1)}, bf16[512,256]{1,0:T(8,128)(2,1)S(1)}, bf16[512,256]{1,0:T(8,128)(2,1)S(1)}, bf16[512,256]{1,0:T...) fusion(bf16[3,3,512,256]{3,2,1,0:T(8,128)(2,1)} %param.13), kind=kLoop, calls=%fused_computation.77 | loop fusion | bytes 4194304 | tf_op jit(solution)/shard_map/squeeze | solution.py:129
  4.2 2.6 %collective-permute-start.1 = (bf16[7,512]{1,0:T(8,128)(2,1)S(1)}, bf16[7,512]{1,0:T(8,128)(2,1)S(1)}, u32[]{:S(2)}, u32[]{:S(2)}) collective-permute-start(bf16[7,512]{1,0:T(8,128)(2,1)S(1)} %pad_maximum_fusion.25), channel_id=1, source_target_pairs={{0,2},{2,0},{1,3},{3,1},{4,6},{6,4},{5,7},{7,5},{8,10},{10,8},{9,1... | collective-permute-start | bytes 21512 | tf_op jit(solution)/shard_map/ppermute | solution.py:170
  6.9 1.6 %collective-permute-done.1 = bf16[7,512]{1,0:T(8,128)(2,1)S(1)} collective-permute-done((bf16[7,512]{1,0:T(8,128)(2,1)S(1)}, bf16[7,512]{1,0:T(8,128)(2,1)S(1)}, u32[]{:S(2)}, u32[]{:S(2)}) %collective-permute-start.1) | collective-permute-done | bytes 7200 | tf_op jit(solution)/shard_map/ppermute | solution.py:170
  9.1 2.2 %collective-permute-start.2 = (bf16[100,512]{1,0:T(8,128)(2,1)S(1)}, bf16[100,512]{1,0:T(8,128)(2,1)S(1)}, u32[]{:S(2)}, u32[]{:S(2)}) collective-permute-start(bf16[100,512]{1,0:T(8,128)(2,1)S(1)} %pad_maximum_fusion.24), channel_id=1, source_target_pairs={{0,4},{4,0},{8,12},{12,8},{1,5},{5,1},{9,13},{13,9},{2,6},{6,2},{1... | collective-permute-start | bytes 307208 | tf_op jit(solution)/shard_map/ppermute | solution.py:170
  11.3 0.7 collective-permute-start.3
  12.0 3.9 %collective-permute-start.4 = (f32[2,32]{1,0:T(2,128)S(1)}, f32[2,32]{1,0:T(2,128)S(1)}, u32[]{:S(2)}, u32[]{:S(2)}) collective-permute-start(f32[2,32]{1,0:T(2,128)S(1)} %get-tuple-element.27), channel_id=1, source_target_pairs={{0,8},{4,12},{8,0},{12,4},{1,9},{5,13},{9,1},{13,5},{2,10},{6,14},... | collective-permute-start | bytes 776 | tf_op jit(solution)/shard_map/ppermute | solution.py:170
  15.9 4.8 %collective-permute-start.5 = (f32[2,32]{1,0:T(2,128)S(1)}, f32[2,32]{1,0:T(2,128)S(1)}, u32[]{:S(2)}, u32[]{:S(2)}) collective-permute-start(f32[2,32]{1,0:T(2,128)S(1)} %get-tuple-element.27), channel_id=1, source_target_pairs={{0,12},{12,0},{1,13},{13,1},{2,14},{14,2},{3,15},{15,3},{16,28},{2... | collective-permute-start | bytes 776 | tf_op jit(solution)/shard_map/ppermute | solution.py:238
  21.1 2.1 %collective-permute-done.5 = f32[2,32]{1,0:T(2,128)S(1)} collective-permute-done((f32[2,32]{1,0:T(2,128)S(1)}, f32[2,32]{1,0:T(2,128)S(1)}, u32[]{:S(2)}, u32[]{:S(2)}) %collective-permute-start.5) | collective-permute-done | bytes 288 | tf_op jit(solution)/shard_map/ppermute | solution.py:238
  23.5 0.3 select_convert_fusion.2
  23.9 0.3 fusion.11
  24.2 0.3 fusion.15
  24.5 0.4 fusion.1
  25.3 1.2 %convolution_add_fusion.4 = bf16[192,256]{1,0:T(8,128)(2,1)S(1)} fusion(bf16[192,512]{1,0:T(8,128)(2,1)S(1)} %bitcast.122, bf16[3,3,512,256]{3,2,1,0:T(8,128)(2,1)} %param.13, f32[192,512]{1,0:T(8,128)S(1)} %fusion.15, f32[192,512]{1,0:T(8,128)S(1)} %fusion.11, f32[192,1024]{1,0:T(8,128)S(1)} %fusion.1), kind=kOutput, calls=%fused_computation.7 | convolution fusion | flops 50528256 | bytes 1146880 | tf_op jit(solution)/shard_map/dot_general | solution.py:123
  26.6 0.3 pad_maximum_fusion.10
  26.8 0.3 pad_maximum_fusion.11
  27.1 0.8 convert_reduce_fusion.1
  28.7 1.6 %collective-permute-start.6 = (bf16[13,256]{1,0:T(8,128)(2,1)S(1)}, bf16[13,256]{1,0:T(8,128)(2,1)S(1)}, u32[]{:S(2)}, u32[]{:S(2)}) collective-permute-start(bf16[13,256]{1,0:T(8,128)(2,1)S(1)} %pad_maximum_fusion.26), channel_id=1, source_target_pairs={{0,2},{2,0},{1,3},{3,1},{4,6},{6,4},{5,7},{7,5},{8,10},{10,8},{9,1... | collective-permute-start | bytes 19976 | tf_op jit(solution)/shard_map/ppermute | solution.py:170
  30.2 2.1 %collective-permute-done.6 = bf16[13,256]{1,0:T(8,128)(2,1)S(1)} collective-permute-done((bf16[13,256]{1,0:T(8,128)(2,1)S(1)}, bf16[13,256]{1,0:T(8,128)(2,1)S(1)}, u32[]{:S(2)}, u32[]{:S(2)}) %collective-permute-start.6) | collective-permute-done | bytes 6688 | tf_op jit(solution)/shard_map/ppermute | solution.py:170
  33.3 0.7 collective-permute-start.8
  34.0 5.0 %collective-permute-start.10 = (f32[2,32]{1,0:T(2,128)S(1)}, f32[2,32]{1,0:T(2,128)S(1)}, u32[]{:S(2)}, u32[]{:S(2)}) collective-permute-start(f32[2,32]{1,0:T(2,128)S(1)} %get-tuple-element.24), channel_id=1, source_target_pairs={{0,12},{12,0},{1,13},{13,1},{2,14},{14,2},{3,15},{15,3},{16,28},{2... | collective-permute-start | bytes 776 | tf_op jit(solution)/shard_map/ppermute | solution.py:238
  39.0 0.6 collective-permute-start.9
  40.3 1.0 %collective-permute-done.10 = f32[2,32]{1,0:T(2,128)S(1)} collective-permute-done((f32[2,32]{1,0:T(2,128)S(1)}, f32[2,32]{1,0:T(2,128)S(1)}, u32[]{:S(2)}, u32[]{:S(2)}) %collective-permute-start.10) | collective-permute-done | bytes 288 | tf_op jit(solution)/shard_map/ppermute | solution.py:238
  41.3 2.3 %collective-permute-done.9 = f32[2,32]{1,0:T(2,128)S(1)} collective-permute-done((f32[2,32]{1,0:T(2,128)S(1)}, f32[2,32]{1,0:T(2,128)S(1)}, u32[]{:S(2)}, u32[]{:S(2)}) %collective-permute-start.9) | collective-permute-done | bytes 288 | tf_op jit(solution)/shard_map/ppermute | solution.py:170
  44.0 3.7 %fusion.117 = (bf16[1,3,3,256,256]{4,3,2,1,0:T(8,128)(2,1)S(1)}, bf16[1,3,3,256,256]{4,3,2,1,0:T(8,128)(2,1)}, bf16[1,3,3,256,256]{4,3,2,1,0:T(8,128)(2,1)}) fusion(bf16[3,3,3,256,256]{4,3,2,1,0:T(8,128)(2,1)} %param.16), kind=kLoop, calls=%fused_computation.281 | loop fusion | bytes 7077888 | tf_op jit(solution)/shard_map/slice | solution.py:154
  48.6 1.7 %select_convert_fusion.1 = bf16[5,6,66,256]{3,2,1,0:T(8,128)(2,1)S(1)} fusion(bf16[3,1,66,256]{3,2,1,0:T(8,128)(2,1)S(1)} %select_n.200, bf16[3,4,1,256]{3,2,1,0:T(2,128)(2,1)S(1)} %reshape.752, bf16[3,4,64,256]{3,2,1,0:T(8,128)(2,1)S(1)} %bitcast.103, bf16[3,1,66,256]{3,2,1,0:T(8,128)(2,1)S(1)} %select_n.197, ...), kind=kLoop, calls=%fused_computation.1 | loop fusion | flops 11151360 | bytes 2025868 | tf_op jit(solution)/shard_map/convert_element_type | solution.py:281
  50.3 0.2 slice_dynamic-update-slice_fusion.16
  52.0 1.0 %fusion.115 = (bf16[3,4,64,2304]{3,2,1,0:T(8,128)(2,1)S(1)}, bf16[3,4,64,2304]{3,2,1,0:T(8,128)(2,1)S(1)}, bf16[3,4,64,2304]{3,2,1,0:T(8,128)(2,1)S(1)}) fusion(bf16[5,4,64,2304]{3,2,1,0:T(8,128)(2,1)S(1)} %slice_dynamic-update-slice_fusion.9), kind=kLoop, calls=%fused_computation.279 | loop fusion | bytes 21233664 | tf_op jit(solution)/shard_map/slice | solution.py:152
  53.0 0.3 copy-done.3
  53.3 1.1 %fusion.120 = f32[768,256]{1,0:T(8,128)S(1)} fusion(bf16[768,2304]{1,0:T(8,128)(2,1)S(1)} %bitcast.114, bf16[2304,256]{1,0:T(8,128)(2,1)S(1)} %bitcast.121), kind=kOutput, calls=%fused_computation.284 | convolution fusion | flops 905969664 | bytes 5505024 | tf_op jit(solution)/shard_map/dot_general | solution.py:153
  54.6 1.1 %convolution_add_fusion.3 = f32[768,256]{1,0:T(8,128)S(1)} fusion(f32[768,256]{1,0:T(8,128)S(1)} %fusion.120, bf16[768,2304]{1,0:T(8,128)(2,1)S(1)} %bitcast.112, bf16[2304,256]{1,0:T(8,128)(2,1)S(1)} %bitcast.120), kind=kOutput, calls=%fused_computation.5 | convolution fusion | flops 906166272 | bytes 6291456 | tf_op jit(solution)/shard_map/dot_general | solution.py:153
  55.6 1.1 %convert_reduce_fusion = (f32[256]{0:T(256)S(1)}, f32[256]{0:T(256)S(1)}, bf16[768,256]{1,0:T(8,128)(2,1)S(1)}) fusion(f32[768,256]{1,0:T(8,128)S(1)} %convolution_add_fusion.3, bf16[768,2304]{1,0:T(8,128)(2,1)S(1)} %bitcast.110, bf16[2304,256]{1,0:T(8,128)(2,1)S(1)} %bitcast.116), kind=kOutput, calls=%fused_computation.17 | convolution fusion | flops 907148800 | bytes 5900288 | tf_op jit(solution)/shard_map/dot_general | solution.py:153
  57.5 1.6 %collective-permute-start.12 = (bf16[13,256]{1,0:T(8,128)(2,1)S(1)}, bf16[13,256]{1,0:T(8,128)(2,1)S(1)}, u32[]{:S(2)}, u32[]{:S(2)}) collective-permute-start(bf16[13,256]{1,0:T(8,128)(2,1)S(1)} %pad_maximum_fusion.27), channel_id=1, source_target_pairs={{0,2},{2,0},{1,3},{3,1},{4,6},{6,4},{5,7},{7,5},{8,10},{10,8},{9,1... | collective-permute-start | bytes 19976 | tf_op jit(solution)/shard_map/ppermute | solution.py:170
  59.0 2.2 %collective-permute-done.12 = bf16[13,256]{1,0:T(8,128)(2,1)S(1)} collective-permute-done((bf16[13,256]{1,0:T(8,128)(2,1)S(1)}, bf16[13,256]{1,0:T(8,128)(2,1)S(1)}, u32[]{:S(2)}, u32[]{:S(2)}) %collective-permute-start.12) | collective-permute-done | bytes 6688 | tf_op jit(solution)/shard_map/ppermute | solution.py:170
  62.0 1.2 %collective-permute-start.13 = (bf16[199,256]{1,0:T(8,128)(2,1)S(1)}, bf16[199,256]{1,0:T(8,128)(2,1)S(1)}, u32[]{:S(2)}, u32[]{:S(2)}) collective-permute-start(bf16[199,256]{1,0:T(8,128)(2,1)S(1)} %get-tuple-element.63), channel_id=1, source_target_pairs={{0,4},{4,0},{8,12},{12,8},{1,5},{5,1},{9,13},{13,9},{2,6},{6,2},{1... | collective-permute-start | bytes 305672 | tf_op jit(solution)/shard_map/ppermute | solution.py:170
  63.1 0.7 collective-permute-start.14
  63.8 3.7 %collective-permute-start.15 = (f32[2,32]{1,0:T(2,128)S(1)}, f32[2,32]{1,0:T(2,128)S(1)}, u32[]{:S(2)}, u32[]{:S(2)}) collective-permute-start(f32[2,32]{1,0:T(2,128)S(1)} %get-tuple-element.17), channel_id=1, source_target_pairs={{0,8},{4,12},{8,0},{12,4},{1,9},{5,13},{9,1},{13,5},{2,10},{6,14},... | collective-permute-start | bytes 776 | tf_op jit(solution)/shard_map/ppermute | solution.py:170
  67.5 3.0 %collective-permute-start.16 = (f32[2,32]{1,0:T(2,128)S(1)}, f32[2,32]{1,0:T(2,128)S(1)}, u32[]{:S(2)}, u32[]{:S(2)}) collective-permute-start(f32[2,32]{1,0:T(2,128)S(1)} %get-tuple-element.17), channel_id=1, source_target_pairs={{0,12},{12,0},{1,13},{13,1},{2,14},{14,2},{3,15},{15,3},{16,28},{2... | collective-permute-start | bytes 776 | tf_op jit(solution)/shard_map/ppermute | solution.py:238
  71.2 3.5 %collective-permute-done.16 = f32[2,32]{1,0:T(2,128)S(1)} collective-permute-done((f32[2,32]{1,0:T(2,128)S(1)}, f32[2,32]{1,0:T(2,128)S(1)}, u32[]{:S(2)}, u32[]{:S(2)}) %collective-permute-start.16) | collective-permute-done | bytes 288 | tf_op jit(solution)/shard_map/ppermute | solution.py:238
  75.2 3.8 %fusion.116 = (bf16[1,3,3,256,256]{4,3,2,1,0:T(8,128)(2,1)S(1)}, bf16[1,3,3,256,256]{4,3,2,1,0:T(8,128)(2,1)}, bf16[1,3,3,256,256]{4,3,2,1,0:T(8,128)(2,1)}) fusion(bf16[3,3,3,256,256]{4,3,2,1,0:T(8,128)(2,1)} %param.19), kind=kLoop, calls=%fused_computation.280 | loop fusion | bytes 7077888 | tf_op jit(solution)/shard_map/slice | solution.py:154
  79.8 1.7 %select_convert_fusion = bf16[5,6,66,256]{3,2,1,0:T(8,128)(2,1)S(1)} fusion(bf16[3,1,66,256]{3,2,1,0:T(8,128)(2,1)S(1)} %select_n.210, bf16[3,4,1,256]{3,2,1,0:T(2,128)(2,1)S(1)} %reshape.753, bf16[3,4,64,256]{3,2,1,0:T(8,128)(2,1)S(1)} %bitcast.109, bf16[3,1,66,256]{3,2,1,0:T(8,128)(2,1)S(1)} %select_n.208, ...), kind=kLoop, calls=%fused_computation | loop fusion | flops 11151360 | bytes 2025868 | tf_op jit(solution)/shard_map/convert_element_type | solution.py:281
  83.3 1.0 %fusion.114 = (bf16[3,4,64,2304]{3,2,1,0:T(8,128)(2,1)S(1)}, bf16[3,4,64,2304]{3,2,1,0:T(8,128)(2,1)S(1)}, bf16[3,4,64,2304]{3,2,1,0:T(8,128)(2,1)S(1)}) fusion(bf16[5,4,64,2304]{3,2,1,0:T(8,128)(2,1)S(1)} %slice_dynamic-update-slice_fusion), kind=kLoop, calls=%fused_computation.278 | loop fusion | bytes 21233664 | tf_op jit(solution)/shard_map/slice | solution.py:152
  84.3 0.3 copy-done.1
  84.6 1.1 %fusion.121 = f32[768,256]{1,0:T(8,128)S(1)} fusion(bf16[768,2304]{1,0:T(8,128)(2,1)S(1)} %bitcast.115, bf16[2304,256]{1,0:T(8,128)(2,1)S(1)} %bitcast.119), kind=kOutput, calls=%fused_computation.285 | convolution fusion | flops 905969664 | bytes 5505024 | tf_op jit(solution)/shard_map/dot_general | solution.py:153
  85.8 1.1 %convolution_add_fusion.1 = f32[768,256]{1,0:T(8,128)S(1)} fusion(f32[768,256]{1,0:T(8,128)S(1)} %fusion.121, bf16[768,2304]{1,0:T(8,128)(2,1)S(1)} %bitcast.113, bf16[2304,256]{1,0:T(8,128)(2,1)S(1)} %bitcast.118), kind=kOutput, calls=%fused_computation.3 | convolution fusion | flops 906166272 | bytes 6291456 | tf_op jit(solution)/shard_map/dot_general | solution.py:153
  86.9 1.1 %convolution_add_fusion = f32[768,256]{1,0:T(8,128)S(1)} fusion(f32[768,256]{1,0:T(8,128)S(1)} %convolution_add_fusion.1, bf16[768,2304]{1,0:T(8,128)(2,1)S(1)} %bitcast.111, bf16[2304,256]{1,0:T(8,128)(2,1)S(1)} %bitcast.117), kind=kOutput, calls=%fused_computation.2 | convolution fusion | flops 906166272 | bytes 6291456 | tf_op jit(solution)/shard_map/dot_general | solution.py:153
  88.0 0.9 add_convert_fusion
  (232 shorter events, 13.2 us)
Async XLA Ops:
  0.0 3.8 %copy-start.4 = (bf16[3,2,32,512]{3,2,1,0:T(8,128)(2,1)S(1)}, bf16[3,2,32,512]{3,2,1,0:T(8,128)(2,1)}, u32[]{:S(2)}) copy-start(bf16[3,2,32,512]{3,2,1,0:T(8,128)(2,1)} %param.10) | copy-start | bytes 589828
  1.5 2.3 %collective-permute-start = (f32[2,32]{1,0:T(2,128)S(1)}, f32[2,32]{1,0:T(2,128)S(1)}, u32[]{:S(2)}, u32[]{:S(2)}) collective-permute-start(f32[2,32]{1,0:T(2,128)S(1)} %pad_maximum_fusion.28), channel_id=1, source_target_pairs={{0,1},{1,0},{2,3},{3,2},{4,5},{5,4},{6,7},{7,6},{8,9},{9,8},{10,11... | collective-permute-start | bytes 776 | tf_op jit(solution)/shard_map/ppermute | solution.py:170
  2.0 21.5 %copy-start.5 = (f32[512]{0:T(512)S(1)}, f32[512]{0:T(512)}, u32[]{:S(2)}) copy-start(f32[512]{0:T(512)} %param.12) | copy-start | bytes 6148
  2.0 21.5 %copy-start.6 = (f32[512]{0:T(512)S(1)}, f32[512]{0:T(512)}, u32[]{:S(2)}) copy-start(f32[512]{0:T(512)} %param.11) | copy-start | bytes 6148
  4.2 4.2 %collective-permute-start.1 = (bf16[7,512]{1,0:T(8,128)(2,1)S(1)}, bf16[7,512]{1,0:T(8,128)(2,1)S(1)}, u32[]{:S(2)}, u32[]{:S(2)}) collective-permute-start(bf16[7,512]{1,0:T(8,128)(2,1)S(1)} %pad_maximum_fusion.25), channel_id=1, source_target_pairs={{0,2},{2,0},{1,3},{3,1},{4,6},{6,4},{5,7},{7,5},{8,10},{10,8},{9,1... | collective-permute-start | bytes 21512 | tf_op jit(solution)/shard_map/ppermute | solution.py:170
  9.1 11.6 %collective-permute-start.2 = (bf16[100,512]{1,0:T(8,128)(2,1)S(1)}, bf16[100,512]{1,0:T(8,128)(2,1)S(1)}, u32[]{:S(2)}, u32[]{:S(2)}) collective-permute-start(bf16[100,512]{1,0:T(8,128)(2,1)S(1)} %pad_maximum_fusion.24), channel_id=1, source_target_pairs={{0,4},{4,0},{8,12},{12,8},{1,5},{5,1},{9,13},{13,9},{2,6},{6,2},{1... | collective-permute-start | bytes 307208 | tf_op jit(solution)/shard_map/ppermute | solution.py:170
  11.3 9.5 %collective-permute-start.3 = (bf16[100,512]{1,0:T(8,128)(2,1)S(1)}, bf16[100,512]{1,0:T(8,128)(2,1)S(1)}, u32[]{:S(2)}, u32[]{:S(2)}) collective-permute-start(bf16[100,512]{1,0:T(8,128)(2,1)S(1)} %pad_maximum_fusion.24), channel_id=1, source_target_pairs={{4,8},{8,4},{5,9},{9,5},{6,10},{10,6},{7,11},{11,7},{20,24},{24,20... | collective-permute-start | bytes 307208 | tf_op jit(solution)/shard_map/ppermute | solution.py:235
  12.0 9.1 %collective-permute-start.4 = (f32[2,32]{1,0:T(2,128)S(1)}, f32[2,32]{1,0:T(2,128)S(1)}, u32[]{:S(2)}, u32[]{:S(2)}) collective-permute-start(f32[2,32]{1,0:T(2,128)S(1)} %get-tuple-element.27), channel_id=1, source_target_pairs={{0,8},{4,12},{8,0},{12,4},{1,9},{5,13},{9,1},{13,5},{2,10},{6,14},... | collective-permute-start | bytes 776 | tf_op jit(solution)/shard_map/ppermute | solution.py:170
  15.9 7.2 %collective-permute-start.5 = (f32[2,32]{1,0:T(2,128)S(1)}, f32[2,32]{1,0:T(2,128)S(1)}, u32[]{:S(2)}, u32[]{:S(2)}) collective-permute-start(f32[2,32]{1,0:T(2,128)S(1)} %get-tuple-element.27), channel_id=1, source_target_pairs={{0,12},{12,0},{1,13},{13,1},{2,14},{14,2},{3,15},{15,3},{16,28},{2... | collective-permute-start | bytes 776 | tf_op jit(solution)/shard_map/ppermute | solution.py:238
  28.7 3.7 %collective-permute-start.6 = (bf16[13,256]{1,0:T(8,128)(2,1)S(1)}, bf16[13,256]{1,0:T(8,128)(2,1)S(1)}, u32[]{:S(2)}, u32[]{:S(2)}) collective-permute-start(bf16[13,256]{1,0:T(8,128)(2,1)S(1)} %pad_maximum_fusion.26), channel_id=1, source_target_pairs={{0,2},{2,0},{1,3},{3,1},{4,6},{6,4},{5,7},{7,5},{8,10},{10,8},{9,1... | collective-permute-start | bytes 19976 | tf_op jit(solution)/shard_map/ppermute | solution.py:170
  33.2 6.4 %collective-permute-start.7 = (bf16[199,256]{1,0:T(8,128)(2,1)S(1)}, bf16[199,256]{1,0:T(8,128)(2,1)S(1)}, u32[]{:S(2)}, u32[]{:S(2)}) collective-permute-start(bf16[199,256]{1,0:T(8,128)(2,1)S(1)} %get-tuple-element.69), channel_id=1, source_target_pairs={{0,4},{4,0},{8,12},{12,8},{1,5},{5,1},{9,13},{13,9},{2,6},{6,2},{1... | collective-permute-start | bytes 305672 | tf_op jit(solution)/shard_map/ppermute | solution.py:170
  33.3 6.4 %collective-permute-start.8 = (bf16[199,256]{1,0:T(8,128)(2,1)S(1)}, bf16[199,256]{1,0:T(8,128)(2,1)S(1)}, u32[]{:S(2)}, u32[]{:S(2)}) collective-permute-start(bf16[199,256]{1,0:T(8,128)(2,1)S(1)} %get-tuple-element.70), channel_id=1, source_target_pairs={{4,8},{8,4},{5,9},{9,5},{6,10},{10,6},{7,11},{11,7},{20,24},{24,20... | collective-permute-start | bytes 305672 | tf_op jit(solution)/shard_map/ppermute | solution.py:235
  34.0 7.2 %collective-permute-start.10 = (f32[2,32]{1,0:T(2,128)S(1)}, f32[2,32]{1,0:T(2,128)S(1)}, u32[]{:S(2)}, u32[]{:S(2)}) collective-permute-start(f32[2,32]{1,0:T(2,128)S(1)} %get-tuple-element.24), channel_id=1, source_target_pairs={{0,12},{12,0},{1,13},{13,1},{2,14},{14,2},{3,15},{15,3},{16,28},{2... | collective-permute-start | bytes 776 | tf_op jit(solution)/shard_map/ppermute | solution.py:238
  39.0 4.5 %collective-permute-start.9 = (f32[2,32]{1,0:T(2,128)S(1)}, f32[2,32]{1,0:T(2,128)S(1)}, u32[]{:S(2)}, u32[]{:S(2)}) collective-permute-start(f32[2,32]{1,0:T(2,128)S(1)} %get-tuple-element.24), channel_id=1, source_target_pairs={{0,8},{4,12},{8,0},{12,4},{1,9},{5,13},{9,1},{13,5},{2,10},{6,14},... | collective-permute-start | bytes 776 | tf_op jit(solution)/shard_map/ppermute | solution.py:170
  43.9 3.8 %collective-permute-start.11 = (bf16[793,256]{1,0:T(8,128)(2,1)S(1)}, bf16[793,256]{1,0:T(8,128)(2,1)S(1)}, u32[]{:S(2)}, u32[]{:S(2)}) collective-permute-start(bf16[793,256]{1,0:T(8,128)(2,1)S(1)} %pad_maximum_fusion.8), channel_id=1, source_target_pairs={{0,1},{1,0},{2,3},{3,2},{4,5},{5,4},{6,7},{7,6},{8,9},{9,8},{10,11... | collective-permute-start | bytes 1218056 | tf_op jit(solution)/shard_map/ppermute | solution.py:170
  47.7 0.8 copy-start.7
  47.7 0.8 copy-start.8
  52.0 1.3 %copy-start.3 = (bf16[1,3,3,256,256]{4,3,2,1,0:T(8,128)(2,1)S(1)}, bf16[1,3,3,256,256]{4,3,2,1,0:T(8,128)(2,1)}, u32[]{:S(2)}) copy-start(bf16[1,3,3,256,256]{4,3,2,1,0:T(8,128)(2,1)} %get-tuple-element.40) | copy-start | bytes 3538948
  53.3 1.3 %copy-start.2 = (bf16[1,3,3,256,256]{4,3,2,1,0:T(8,128)(2,1)S(1)}, bf16[1,3,3,256,256]{4,3,2,1,0:T(8,128)(2,1)}, u32[]{:S(2)}) copy-start(bf16[1,3,3,256,256]{4,3,2,1,0:T(8,128)(2,1)} %get-tuple-element.41) | copy-start | bytes 3538948
  57.5 3.7 %collective-permute-start.12 = (bf16[13,256]{1,0:T(8,128)(2,1)S(1)}, bf16[13,256]{1,0:T(8,128)(2,1)S(1)}, u32[]{:S(2)}, u32[]{:S(2)}) collective-permute-start(bf16[13,256]{1,0:T(8,128)(2,1)S(1)} %pad_maximum_fusion.27), channel_id=1, source_target_pairs={{0,2},{2,0},{1,3},{3,1},{4,6},{6,4},{5,7},{7,5},{8,10},{10,8},{9,1... | collective-permute-start | bytes 19976 | tf_op jit(solution)/shard_map/ppermute | solution.py:170
  62.0 8.6 %collective-permute-start.13 = (bf16[199,256]{1,0:T(8,128)(2,1)S(1)}, bf16[199,256]{1,0:T(8,128)(2,1)S(1)}, u32[]{:S(2)}, u32[]{:S(2)}) collective-permute-start(bf16[199,256]{1,0:T(8,128)(2,1)S(1)} %get-tuple-element.63), channel_id=1, source_target_pairs={{0,4},{4,0},{8,12},{12,8},{1,5},{5,1},{9,13},{13,9},{2,6},{6,2},{1... | collective-permute-start | bytes 305672 | tf_op jit(solution)/shard_map/ppermute | solution.py:170
  63.1 7.4 %collective-permute-start.14 = (bf16[199,256]{1,0:T(8,128)(2,1)S(1)}, bf16[199,256]{1,0:T(8,128)(2,1)S(1)}, u32[]{:S(2)}, u32[]{:S(2)}) collective-permute-start(bf16[199,256]{1,0:T(8,128)(2,1)S(1)} %get-tuple-element.64), channel_id=1, source_target_pairs={{4,8},{8,4},{5,9},{9,5},{6,10},{10,6},{7,11},{11,7},{20,24},{24,20... | collective-permute-start | bytes 305672 | tf_op jit(solution)/shard_map/ppermute | solution.py:235
  63.8 7.5 %collective-permute-start.15 = (f32[2,32]{1,0:T(2,128)S(1)}, f32[2,32]{1,0:T(2,128)S(1)}, u32[]{:S(2)}, u32[]{:S(2)}) collective-permute-start(f32[2,32]{1,0:T(2,128)S(1)} %get-tuple-element.17), channel_id=1, source_target_pairs={{0,8},{4,12},{8,0},{12,4},{1,9},{5,13},{9,1},{13,5},{2,10},{6,14},... | collective-permute-start | bytes 776 | tf_op jit(solution)/shard_map/ppermute | solution.py:170
  67.5 7.2 %collective-permute-start.16 = (f32[2,32]{1,0:T(2,128)S(1)}, f32[2,32]{1,0:T(2,128)S(1)}, u32[]{:S(2)}, u32[]{:S(2)}) collective-permute-start(f32[2,32]{1,0:T(2,128)S(1)} %get-tuple-element.17), channel_id=1, source_target_pairs={{0,12},{12,0},{1,13},{13,1},{2,14},{14,2},{3,15},{15,3},{16,28},{2... | collective-permute-start | bytes 776 | tf_op jit(solution)/shard_map/ppermute | solution.py:238
  75.1 3.9 %collective-permute-start.17 = (bf16[793,256]{1,0:T(8,128)(2,1)S(1)}, bf16[793,256]{1,0:T(8,128)(2,1)S(1)}, u32[]{:S(2)}, u32[]{:S(2)}) collective-permute-start(bf16[793,256]{1,0:T(8,128)(2,1)S(1)} %pad_maximum_fusion.9), channel_id=1, source_target_pairs={{0,1},{1,0},{2,3},{3,2},{4,5},{5,4},{6,7},{7,6},{8,9},{9,8},{10,11... | collective-permute-start | bytes 1218056 | tf_op jit(solution)/shard_map/ppermute | solution.py:170
  79.0 0.8 copy-start.9
  79.0 0.8 copy-start.10
  83.3 1.3 %copy-start.1 = (bf16[1,3,3,256,256]{4,3,2,1,0:T(8,128)(2,1)S(1)}, bf16[1,3,3,256,256]{4,3,2,1,0:T(8,128)(2,1)}, u32[]{:S(2)}) copy-start(bf16[1,3,3,256,256]{4,3,2,1,0:T(8,128)(2,1)} %get-tuple-element.37) | copy-start | bytes 3538948
  84.6 1.3 %copy-start = (bf16[1,3,3,256,256]{4,3,2,1,0:T(8,128)(2,1)S(1)}, bf16[1,3,3,256,256]{4,3,2,1,0:T(8,128)(2,1)}, u32[]{:S(2)}) copy-start(bf16[1,3,3,256,256]{4,3,2,1,0:T(8,128)(2,1)} %get-tuple-element.38) | copy-start | bytes 3538948

commit v13 on v10

--- a/solution.py
+++ b/solution.py
@@ -2,6 +2,8 @@
 import jax.numpy as jnp
 from jax import lax
 from jax.sharding import PartitionSpec as P
+from jax.experimental import pallas as pl
+from jax.experimental.pallas import tpu as pltpu
 
 GROUPS = 32
 
@@ -142,19 +144,43 @@
     return jnp.concatenate([even, odd], axis=2).reshape(frames, 2 * height, 2 * across, out)
 
 
+def tap_kernel(window_ref, weight_ref, out_ref):
+    step_t, frame = pl.program_id(0), pl.program_id(1)
+    part = jnp.dot(window_ref[0], weight_ref[0], preferred_element_type=jnp.float32)
+
+    @pl.when(step_t == 0)
+    def _():
+        out_ref[frame] = part
+
+    @pl.when(step_t > 0)
+    def _():
+        out_ref[frame] = out_ref[frame] + part
+
+
+def frame_tap_dots(wide, taps, frames):
+    _, rows, depth = wide.shape
+    outs = taps.shape[-1]
+    return pl.pallas_call(
+        tap_kernel,
+        grid=(3, frames),
+        in_specs=[
+            pl.BlockSpec((1, rows, depth), lambda t, f: (t + f, 0, 0)),
+            pl.BlockSpec((1, depth, outs), lambda t, f: (t, 0, 0)),
+        ],
+        out_specs=pl.BlockSpec((frames, rows, outs), lambda t, f: (0, 0, 0)),
+        out_shape=jax.ShapeDtypeStruct((frames, rows, outs), jnp.float32),
+        compiler_params=pltpu.CompilerParams(dimension_semantics=("arbitrary", "arbitrary")),
+    )(wide, taps)
+
+
 def valid_conv(padded, kernel, frames, height, across):
     channels = padded.shape[-1]
     wide = jnp.concatenate(
         [padded[:, dy : dy + height, dx : dx + across] for dy in range(3) for dx in range(3)], axis=-1
     )
-    result = None
-    for step_t in range(3):
-        window = wide[step_t : step_t + frames].reshape(-1, 9 * channels)
-        part = jnp.dot(
-            window, kernel[step_t].reshape(9 * channels, -1), preferred_element_type=jnp.float32
-        )
-        result = part if result is None else result + part
-    return result.reshape(frames, height, across, -1)
+    wide = wide.reshape(frames + 2, height * across, 9 * channels)
+    taps = kernel.reshape(3, 9 * channels, kernel.shape[-1])
+    return frame_tap_dots(wide, taps, frames).reshape(frames, height, across, -1)
 
 
 def conv_halo(values):

time: 77.8 us -> 98.2 us (1.26)
  Pallas kernels: 0 us -> 21.5 us
  matrix products: 8.59 us -> 2.06 us
  waiting for transfers between devices: 17.7 us -> 22.3 us
  local copies, waits for them, and re-layouts: 20.9 us -> 17.4 us
  other arithmetic: 11 us -> 13.4 us
  starting transfers between devices: 18.3 us -> 20.2 us
    pallas_call x0 -> x2, Pallas kernels: none -> 21.5 us  [frame_tap_dots(): pl.pallas_call(tap_kernel, grid=(3, frames), in_specs=[pl.BlockSpec((1, r...]
    slice x4 -> x0, local copies, waits for them, and re-layouts: 9.61 us -> none  [the longest x2 7.42 us: valid_conv(): kernel[step_t].reshape(9 * channels, -1)]
    dot_general x6 -> x0, matrix products: 6.52 us -> none  [valid_conv(): jnp.dot(window, kernel[step_t].reshape(9 * channels, -1), preferred_eleme...]
    unnamed x39 -> x33, local copies, waits for them, and re-layouts: 3.58 us -> 8.83 us
    ppermute x15, waiting for transfers between devices: 17.7 us -> 22.3 us  [swap(): return lax.ppermute(x, axis, [(i, i ^ distance) for i in range(size)])]
    ppermute x15, starting transfers between devices: 18.3 us -> 20.2 us  [swap(): return lax.ppermute(x, axis, [(i, i ^ distance) for i in range(size)])]
    reduce_sum x5 -> x6, other arithmetic: 2.25 us -> 3.45 us  [local_sums(): jnp.sum(grouped, axis=(0, 2))]
    convert_element_type x1, other arithmetic: 0.87 us -> 1.98 us  [per_device(): return (lifted.astype(jnp.float32) + branch).astype(jnp.bfloat16)]
  transfers between devices with their start and end apart: 15 -> 15, of which waited for: 10 -> 11; matrix products, arithmetic and copies ran while one was open for 14% -> 5% of each run, Pallas kernels for 0% -> 0%
where the time goes in v13:
time: 98.2 us; the launch traced here: 97.6 us
  waiting for transfers between devices  22.3 us (23%)
  Pallas kernels  21.5 us (22%)
  starting transfers between devices  20.2 us (21%)
  local copies, waits for them, and re-layouts  17.4 us (18%)
  other arithmetic  13.4 us (14%)
  matrix products  2.06 us (2%)
    ppermute x15, waiting for transfers between devices, swap(): return lax.ppermute(x, axis, [(i, i ^ distance) for i in range(size)])  22.3 us
    pallas_call x2, Pallas kernels, frame_tap_dots(): pl.pallas_call(tap_kernel, grid=(3, frames), in_specs=[pl.BlockSpec((1, r...  21.5 us
    ppermute x15, starting transfers between devices, swap(): return lax.ppermute(x, axis, [(i, i ^ distance) for i in range(size)])  20.2 us
    unnamed x33, local copies, waits for them, and re-layouts  8.83 us
    convert_element_type x2, other arithmetic, norm_conv(): jnp.where(inside_mask(height + 2, across + 2, 1), act, 0.0)  3.58 us
    reduce_sum x6, other arithmetic, local_sums(): jnp.sum(grouped, axis=(0, 2))  3.45 us
    dot_general x4, matrix products, upsample(): dot = lambda v, w: jnp.dot(flat(v), w, preferred_element_type=jnp.float32)  2.06 us
    convert_element_type x1, other arithmetic, per_device(): return (lifted.astype(jnp.float32) + branch).astype(jnp.bfloat16)  1.98 us
  transfers between devices with their start and end apart: 15, of which 11 were waited for; matrix products, arithmetic and copies ran while one was open for 5% of the time, Pallas kernels for 0%

profile of v13, /device:TPU:0, one launch (start us, length us, event | category | flops | bytes accessed | tf_op | source)
XLA Modules:
  0.0 97.6 jit_solution(15116250876876376625)
XLA Ops:
  0.0 1.0 %convert_reduce_fusion.2 = (f32[512]{0:T(512)S(1)}, f32[512]{0:T(512)S(1)}) fusion(bf16[3,2,32,512]{3,2,1,0:T(8,128)(2,1)} %param.10), kind=kLoop, calls=%fused_computation.47 | loop fusion | flops 392192 | bytes 200704 | tf_op jit(solution)/shard_map/reduce_sum | solution.py:205
  1.4 0.5 collective-permute-start
  1.9 0.8 slice_reduce_fusion
  2.8 0.9 constant_dynamic-update-slice_fusion.1
  3.8 1.6 %slice_bitcast_fusion.7 = (bf16[512,256]{1,0:T(8,128)(2,1)S(1)}, bf16[512,256]{1,0:T(8,128)(2,1)S(1)}, bf16[512,256]{1,0:T(8,128)(2,1)S(1)}, bf16[512,256]{1,0:T...) fusion(bf16[3,3,512,256]{3,2,1,0:T(8,128)(2,1)} %param.13), kind=kLoop, calls=%fused_computation.72 | loop fusion | bytes 4194304 | tf_op jit(solution)/shard_map/squeeze | solution.py:131
  5.8 2.6 %collective-permute-start.1 = (bf16[7,512]{1,0:T(8,128)(2,1)S(1)}, bf16[7,512]{1,0:T(8,128)(2,1)S(1)}, u32[]{:S(2)}, u32[]{:S(2)}) collective-permute-start(bf16[7,512]{1,0:T(8,128)(2,1)S(1)} %pad_maximum_fusion.25), channel_id=1, source_target_pairs={{0,2},{2,0},{1,3},{3,1},{4,6},{6,4},{5,7},{7,5},{8,10},{10,8},{9,1... | collective-permute-start | bytes 21512 | tf_op jit(solution)/shard_map/ppermute | solution.py:196
  8.4 1.6 %collective-permute-done.1 = bf16[7,512]{1,0:T(8,128)(2,1)S(1)} collective-permute-done((bf16[7,512]{1,0:T(8,128)(2,1)S(1)}, bf16[7,512]{1,0:T(8,128)(2,1)S(1)}, u32[]{:S(2)}, u32[]{:S(2)}) %collective-permute-start.1) | collective-permute-done | bytes 7200 | tf_op jit(solution)/shard_map/ppermute | solution.py:196
  10.7 4.2 %collective-permute-start.3 = (bf16[100,512]{1,0:T(8,128)(2,1)S(1)}, bf16[100,512]{1,0:T(8,128)(2,1)S(1)}, u32[]{:S(2)}, u32[]{:S(2)}) collective-permute-start(bf16[100,512]{1,0:T(8,128)(2,1)S(1)} %pad_maximum_fusion.24), channel_id=1, source_target_pairs={{0,12},{4,8},{8,4},{12,0},{1,13},{5,9},{9,5},{13,1},{2,14},{6,10},... | collective-permute-start | bytes 307208 | tf_op jit(solution)/shard_map/ppermute | solution.py:196
  15.0 0.6 collective-permute-start.2
  15.6 2.3 %collective-permute-done.3 = bf16[100,512]{1,0:T(8,128)(2,1)S(1)} collective-permute-done((bf16[100,512]{1,0:T(8,128)(2,1)S(1)}, bf16[100,512]{1,0:T(8,128)(2,1)S(1)}, u32[]{:S(2)}, u32[]{:S(2)}) %collective-permute-start.3) | collective-permute-done | bytes 102432 | tf_op jit(solution)/shard_map/ppermute | solution.py:196
  17.9 2.0 %collective-permute-done.2 = bf16[100,512]{1,0:T(8,128)(2,1)S(1)} collective-permute-done((bf16[100,512]{1,0:T(8,128)(2,1)S(1)}, bf16[100,512]{1,0:T(8,128)(2,1)S(1)}, u32[]{:S(2)}, u32[]{:S(2)}) %collective-permute-start.2) | collective-permute-done | bytes 102432 | tf_op jit(solution)/shard_map/ppermute | solution.py:196
  20.6 0.3 select_convert_fusion.2
  21.0 0.3 fusion.14
  21.3 0.3 fusion.10
  21.6 0.4 fusion
  22.0 1.2 %convolution_add_fusion = bf16[192,256]{1,0:T(8,128)(2,1)S(1)} fusion(bf16[192,512]{1,0:T(8,128)(2,1)S(1)} %bitcast.95, bf16[3,3,512,256]{3,2,1,0:T(8,128)(2,1)} %param.13, f32[192,512]{1,0:T(8,128)S(1)} %fusion.14, f32[192,512]{1,0:T(8,128)S(1)} %fusion.10, f32[192,1024]{1,0:T(8,128)S(1)} %fusion), kind=kOutput, calls=%fused_computation.2 | convolution fusion | flops 50528256 | bytes 1146880 | tf_op jit(solution)/shard_map/dot_general | solution.py:125
  23.6 0.3 pad_maximum_fusion.11
  23.9 0.3 pad_maximum_fusion.10
  24.2 0.8 convert_reduce_fusion.1
  25.8 1.7 %collective-permute-start.5 = (bf16[13,256]{1,0:T(8,128)(2,1)S(1)}, bf16[13,256]{1,0:T(8,128)(2,1)S(1)}, u32[]{:S(2)}, u32[]{:S(2)}) collective-permute-start(bf16[13,256]{1,0:T(8,128)(2,1)S(1)} %pad_maximum_fusion.26), channel_id=1, source_target_pairs={{0,2},{2,0},{1,3},{3,1},{4,6},{6,4},{5,7},{7,5},{8,10},{10,8},{9,1... | collective-permute-start | bytes 19976 | tf_op jit(solution)/shard_map/ppermute | solution.py:196
  27.5 2.0 %collective-permute-done.5 = bf16[13,256]{1,0:T(8,128)(2,1)S(1)} collective-permute-done((bf16[13,256]{1,0:T(8,128)(2,1)S(1)}, bf16[13,256]{1,0:T(8,128)(2,1)S(1)}, u32[]{:S(2)}, u32[]{:S(2)}) %collective-permute-start.5) | collective-permute-done | bytes 6688 | tf_op jit(solution)/shard_map/ppermute | solution.py:196
  30.3 1.6 %collective-permute-start.6 = (bf16[199,256]{1,0:T(8,128)(2,1)S(1)}, bf16[199,256]{1,0:T(8,128)(2,1)S(1)}, u32[]{:S(2)}, u32[]{:S(2)}) collective-permute-start(bf16[199,256]{1,0:T(8,128)(2,1)S(1)} %get-tuple-element.58), channel_id=1, source_target_pairs={{0,4},{4,0},{8,12},{12,8},{1,5},{5,1},{9,13},{13,9},{2,6},{6,2},{1... | collective-permute-start | bytes 305672 | tf_op jit(solution)/shard_map/ppermute | solution.py:196
  31.9 2.4 %collective-permute-start.8 = (f32[2,32]{1,0:T(2,128)S(1)}, f32[2,32]{1,0:T(2,128)S(1)}, u32[]{:S(2)}, u32[]{:S(2)}) collective-permute-start(f32[2,32]{1,0:T(2,128)S(1)} %get-tuple-element.25), channel_id=1, source_target_pairs={{0,8},{4,12},{8,0},{12,4},{1,9},{5,13},{9,1},{13,5},{2,10},{6,14},... | collective-permute-start | bytes 776 | tf_op jit(solution)/shard_map/ppermute | solution.py:196
  34.3 0.4 collective-permute-start.7
  34.7 0.3 collective-permute-done.6
  35.1 5.7 %collective-permute-done.7 = bf16[199,256]{1,0:T(8,128)(2,1)S(1)} collective-permute-done((bf16[199,256]{1,0:T(8,128)(2,1)S(1)}, bf16[199,256]{1,0:T(8,128)(2,1)S(1)}, u32[]{:S(2)}, u32[]{:S(2)}) %collective-permute-start.7) | collective-permute-done | bytes 101920 | tf_op jit(solution)/shard_map/ppermute | solution.py:196
  42.0 1.6 %collective-permute-done.9 = bf16[793,256]{1,0:T(8,128)(2,1)S(1)} collective-permute-done((bf16[793,256]{1,0:T(8,128)(2,1)S(1)}, bf16[793,256]{1,0:T(8,128)(2,1)S(1)}, u32[]{:S(2)}, u32[]{:S(2)}) %collective-permute-start.9) | collective-permute-done | bytes 406048 | tf_op jit(solution)/shard_map/ppermute | solution.py:196
  44.4 1.9 %select_convert_fusion.1 = bf16[5,6,66,256]{3,2,1,0:T(8,128)(2,1)S(1)} fusion(bf16[3,1,66,256]{3,2,1,0:T(8,128)(2,1)S(1)} %select_n.182, bf16[3,4,1,256]{3,2,1,0:T(2,128)(2,1)S(1)} %reshape.744, bf16[3,4,64,256]{3,2,1,0:T(8,128)(2,1)S(1)} %bitcast.83, bf16[3,1,66,256]{3,2,1,0:T(8,128)(2,1)S(1)} %select_n.179, ...), kind=kLoop, calls=%fused_computation.1 | loop fusion | flops 11151360 | bytes 2025868 | tf_op jit(solution)/shard_map/convert_element_type | solution.py:301
  46.6 0.2 slice_dynamic-update-slice_fusion.15
  46.9 0.2 slice_dynamic-update-slice_fusion.13
  47.5 0.2 slice_dynamic-update-slice_fusion.10
  48.0 2.5 %copy-done = bf16[5,4,64,2304]{3,2,1,0:T(8,128)(2,1)} copy-done((bf16[5,4,64,2304]{3,2,1,0:T(8,128)(2,1)}, bf16[5,4,64,2304]{3,2,1,0:T(8,128)(2,1)S(1)}, u32[]{:S(2)}) %copy-start) | copy-done | bytes 5898264
  50.5 10.7 %shard_map.100 = f32[3,256,256]{2,1,0:T(8,128)} custom-call(bf16[5,256,2304]{2,1,0:T(8,128)(2,1)} %bitcast.90, bf16[3,2304,256]{2,1,0:T(8,128)(2,1)} %bitcast.92), custom_call_target="tpu_custom_call" | custom-call | tf_op jit(solution)/shard_map/pallas_call | solution.py:163
  61.2 1.3 %convert_reduce_fusion = (f32[256]{0:T(256)S(1)}, f32[256]{0:T(256)S(1)}, bf16[3,256,256]{2,1,0:T(8,128)(2,1)S(1)}) fusion(f32[3,256,256]{2,1,0:T(8,128)} %shard_map.100), kind=kLoop, calls=%fused_computation.12 | loop fusion | flops 982528 | bytes 1181696 | tf_op jit(solution)/shard_map/reduce_sum | solution.py:205
  63.2 1.5 %collective-permute-start.10 = (bf16[13,256]{1,0:T(8,128)(2,1)S(1)}, bf16[13,256]{1,0:T(8,128)(2,1)S(1)}, u32[]{:S(2)}, u32[]{:S(2)}) collective-permute-start(bf16[13,256]{1,0:T(8,128)(2,1)S(1)} %pad_maximum_fusion.27), channel_id=1, source_target_pairs={{0,2},{2,0},{1,3},{3,1},{4,6},{6,4},{5,7},{7,5},{8,10},{10,8},{9,1... | collective-permute-start | bytes 19976 | tf_op jit(solution)/shard_map/ppermute | solution.py:196
  64.8 2.2 %collective-permute-done.10 = bf16[13,256]{1,0:T(8,128)(2,1)S(1)} collective-permute-done((bf16[13,256]{1,0:T(8,128)(2,1)S(1)}, bf16[13,256]{1,0:T(8,128)(2,1)S(1)}, u32[]{:S(2)}, u32[]{:S(2)}) %collective-permute-start.10) | collective-permute-done | bytes 6688 | tf_op jit(solution)/shard_map/ppermute | solution.py:196
  67.8 1.0 %collective-permute-start.13 = (f32[2,32]{1,0:T(2,128)S(1)}, f32[2,32]{1,0:T(2,128)S(1)}, u32[]{:S(2)}, u32[]{:S(2)}) collective-permute-start(f32[2,32]{1,0:T(2,128)S(1)} %get-tuple-element.17), channel_id=1, source_target_pairs={{0,8},{4,12},{8,0},{12,4},{1,9},{5,13},{9,1},{13,5},{2,10},{6,14},... | collective-permute-start | bytes 776 | tf_op jit(solution)/shard_map/ppermute | solution.py:196
  68.8 3.3 %collective-permute-start.12 = (bf16[199,256]{1,0:T(8,128)(2,1)S(1)}, bf16[199,256]{1,0:T(8,128)(2,1)S(1)}, u32[]{:S(2)}, u32[]{:S(2)}) collective-permute-start(bf16[199,256]{1,0:T(8,128)(2,1)S(1)} %get-tuple-element.53), channel_id=1, source_target_pairs={{0,12},{4,8},{8,4},{12,0},{1,13},{5,9},{9,5},{13,1},{2,14},{6,10},... | collective-permute-start | bytes 305672 | tf_op jit(solution)/shard_map/ppermute | solution.py:196
  72.2 1.4 %collective-permute-done.11 = bf16[199,256]{1,0:T(8,128)(2,1)S(1)} collective-permute-done((bf16[199,256]{1,0:T(8,128)(2,1)S(1)}, bf16[199,256]{1,0:T(8,128)(2,1)S(1)}, u32[]{:S(2)}, u32[]{:S(2)}) %collective-permute-start.11) | collective-permute-done | bytes 101920 | tf_op jit(solution)/shard_map/ppermute | solution.py:196
  73.6 1.6 %collective-permute-done.12 = bf16[199,256]{1,0:T(8,128)(2,1)S(1)} collective-permute-done((bf16[199,256]{1,0:T(8,128)(2,1)S(1)}, bf16[199,256]{1,0:T(8,128)(2,1)S(1)}, u32[]{:S(2)}, u32[]{:S(2)}) %collective-permute-start.12) | collective-permute-done | bytes 101920 | tf_op jit(solution)/shard_map/ppermute | solution.py:196
  76.4 1.7 %collective-permute-done.14 = bf16[793,256]{1,0:T(8,128)(2,1)S(1)} collective-permute-done((bf16[793,256]{1,0:T(8,128)(2,1)S(1)}, bf16[793,256]{1,0:T(8,128)(2,1)S(1)}, u32[]{:S(2)}, u32[]{:S(2)}) %collective-permute-start.14) | collective-permute-done | bytes 406048 | tf_op jit(solution)/shard_map/ppermute | solution.py:196
  78.9 1.7 %select_convert_fusion = bf16[5,6,66,256]{3,2,1,0:T(8,128)(2,1)S(1)} fusion(bf16[3,1,66,256]{3,2,1,0:T(8,128)(2,1)S(1)} %select_n.191, bf16[3,4,1,256]{3,2,1,0:T(2,128)(2,1)S(1)} %reshape.745, bf16[3,4,64,256]{3,2,1,0:T(8,128)(2,1)S(1)} %bitcast.89, bf16[3,1,66,256]{3,2,1,0:T(8,128)(2,1)S(1)} %select_n.189, ...), kind=kLoop, calls=%fused_computation | loop fusion | flops 11151360 | bytes 2025868 | tf_op jit(solution)/shard_map/convert_element_type | solution.py:301
  80.7 0.2 slice_dynamic-update-slice_fusion.7
  81.3 0.2 slice_dynamic-update-slice_fusion.4
  81.8 0.2 slice_dynamic-update-slice_fusion.1
  82.3 2.5 %copy-done.1 = bf16[5,4,64,2304]{3,2,1,0:T(8,128)(2,1)} copy-done((bf16[5,4,64,2304]{3,2,1,0:T(8,128)(2,1)}, bf16[5,4,64,2304]{3,2,1,0:T(8,128)(2,1)S(1)}, u32[]{:S(2)}) %copy-start.1) | copy-done | bytes 5898264
  84.9 10.7 %shard_map.101 = f32[3,256,256]{2,1,0:T(8,128)} custom-call(bf16[5,256,2304]{2,1,0:T(8,128)(2,1)} %bitcast.91, bf16[3,2304,256]{2,1,0:T(8,128)(2,1)} %bitcast.93), custom_call_target="tpu_custom_call" | custom-call | tf_op jit(solution)/shard_map/pallas_call | solution.py:163
  95.6 2.0 %add_convert_fusion = bf16[3,4,64,256]{3,2,1,0:T(8,128)(2,1)} fusion(f32[3,4,64,256]{3,2,1,0:T(8,128)} %bitcast.94, bf16[3,4,64,256]{3,2,1,0:T(8,128)(2,1)S(1)} %bitcast.84), kind=kLoop, calls=%fused_computation.18 | loop fusion | flops 589824 | bytes 1572864 | tf_op jit(solution)/shard_map/convert_element_type | solution.py:328
  (213 shorter events, 11.6 us)
Async XLA Ops:
  1.4 4.0 %collective-permute-start = (f32[2,32]{1,0:T(2,128)S(1)}, f32[2,32]{1,0:T(2,128)S(1)}, u32[]{:S(2)}, u32[]{:S(2)}) collective-permute-start(f32[2,32]{1,0:T(2,128)S(1)} %pad_maximum_fusion.28), channel_id=1, source_target_pairs={{0,1},{1,0},{2,3},{3,2},{4,5},{5,4},{6,7},{7,6},{8,9},{9,8},{10,11... | collective-permute-start | bytes 776 | tf_op jit(solution)/shard_map/ppermute | solution.py:196
  3.7 16.9 %copy-start.2 = (f32[512]{0:T(512)S(1)}, f32[512]{0:T(512)}, u32[]{:S(2)}) copy-start(f32[512]{0:T(512)} %param.12) | copy-start | bytes 6148
  3.7 16.9 %copy-start.3 = (f32[512]{0:T(512)S(1)}, f32[512]{0:T(512)}, u32[]{:S(2)}) copy-start(f32[512]{0:T(512)} %param.11) | copy-start | bytes 6148
  5.8 4.2 %collective-permute-start.1 = (bf16[7,512]{1,0:T(8,128)(2,1)S(1)}, bf16[7,512]{1,0:T(8,128)(2,1)S(1)}, u32[]{:S(2)}, u32[]{:S(2)}) collective-permute-start(bf16[7,512]{1,0:T(8,128)(2,1)S(1)} %pad_maximum_fusion.25), channel_id=1, source_target_pairs={{0,2},{2,0},{1,3},{3,1},{4,6},{6,4},{5,7},{7,5},{8,10},{10,8},{9,1... | collective-permute-start | bytes 21512 | tf_op jit(solution)/shard_map/ppermute | solution.py:196
  10.7 7.1 %collective-permute-start.3 = (bf16[100,512]{1,0:T(8,128)(2,1)S(1)}, bf16[100,512]{1,0:T(8,128)(2,1)S(1)}, u32[]{:S(2)}, u32[]{:S(2)}) collective-permute-start(bf16[100,512]{1,0:T(8,128)(2,1)S(1)} %pad_maximum_fusion.24), channel_id=1, source_target_pairs={{0,12},{4,8},{8,4},{12,0},{1,13},{5,9},{9,5},{13,1},{2,14},{6,10},... | collective-permute-start | bytes 307208 | tf_op jit(solution)/shard_map/ppermute | solution.py:196
  15.0 5.2 %collective-permute-start.4 = (f32[2,32]{1,0:T(2,128)S(1)}, f32[2,32]{1,0:T(2,128)S(1)}, u32[]{:S(2)}, u32[]{:S(2)}) collective-permute-start(f32[2,32]{1,0:T(2,128)S(1)} %get-tuple-element.28), channel_id=1, source_target_pairs={{0,8},{4,12},{8,0},{12,4},{1,9},{5,13},{9,1},{13,5},{2,10},{6,14},... | collective-permute-start | bytes 776 | tf_op jit(solution)/shard_map/ppermute | solution.py:196
  15.0 4.9 %collective-permute-start.2 = (bf16[100,512]{1,0:T(8,128)(2,1)S(1)}, bf16[100,512]{1,0:T(8,128)(2,1)S(1)}, u32[]{:S(2)}, u32[]{:S(2)}) collective-permute-start(bf16[100,512]{1,0:T(8,128)(2,1)S(1)} %pad_maximum_fusion.24), channel_id=1, source_target_pairs={{0,4},{4,0},{8,12},{12,8},{1,5},{5,1},{9,13},{13,9},{2,6},{6,2},{1... | collective-permute-start | bytes 307208 | tf_op jit(solution)/shard_map/ppermute | solution.py:196
  25.8 3.7 %collective-permute-start.5 = (bf16[13,256]{1,0:T(8,128)(2,1)S(1)}, bf16[13,256]{1,0:T(8,128)(2,1)S(1)}, u32[]{:S(2)}, u32[]{:S(2)}) collective-permute-start(bf16[13,256]{1,0:T(8,128)(2,1)S(1)} %pad_maximum_fusion.26), channel_id=1, source_target_pairs={{0,2},{2,0},{1,3},{3,1},{4,6},{6,4},{5,7},{7,5},{8,10},{10,8},{9,1... | collective-permute-start | bytes 19976 | tf_op jit(solution)/shard_map/ppermute | solution.py:196
  30.3 4.7 %collective-permute-start.6 = (bf16[199,256]{1,0:T(8,128)(2,1)S(1)}, bf16[199,256]{1,0:T(8,128)(2,1)S(1)}, u32[]{:S(2)}, u32[]{:S(2)}) collective-permute-start(bf16[199,256]{1,0:T(8,128)(2,1)S(1)} %get-tuple-element.58), channel_id=1, source_target_pairs={{0,4},{4,0},{8,12},{12,8},{1,5},{5,1},{9,13},{13,9},{2,6},{6,2},{1... | collective-permute-start | bytes 305672 | tf_op jit(solution)/shard_map/ppermute | solution.py:196
  31.9 9.1 %collective-permute-start.8 = (f32[2,32]{1,0:T(2,128)S(1)}, f32[2,32]{1,0:T(2,128)S(1)}, u32[]{:S(2)}, u32[]{:S(2)}) collective-permute-start(f32[2,32]{1,0:T(2,128)S(1)} %get-tuple-element.25), channel_id=1, source_target_pairs={{0,8},{4,12},{8,0},{12,4},{1,9},{5,13},{9,1},{13,5},{2,10},{6,14},... | collective-permute-start | bytes 776 | tf_op jit(solution)/shard_map/ppermute | solution.py:196
  34.3 6.5 %collective-permute-start.7 = (bf16[199,256]{1,0:T(8,128)(2,1)S(1)}, bf16[199,256]{1,0:T(8,128)(2,1)S(1)}, u32[]{:S(2)}, u32[]{:S(2)}) collective-permute-start(bf16[199,256]{1,0:T(8,128)(2,1)S(1)} %get-tuple-element.59), channel_id=1, source_target_pairs={{0,12},{4,8},{8,4},{12,0},{1,13},{5,9},{9,5},{13,1},{2,14},{6,10},... | collective-permute-start | bytes 305672 | tf_op jit(solution)/shard_map/ppermute | solution.py:196
  41.7 2.6 %copy-start.4 = (f32[256]{0:T(256)S(1)}, f32[256]{0:T(256)}, u32[]{:S(2)}) copy-start(f32[256]{0:T(256)} %param.15) | copy-start | bytes 3076
  41.7 2.6 %copy-start.5 = (f32[256]{0:T(256)S(1)}, f32[256]{0:T(256)}, u32[]{:S(2)}) copy-start(f32[256]{0:T(256)} %param.14) | copy-start | bytes 3076
  41.8 1.8 %collective-permute-start.9 = (bf16[793,256]{1,0:T(8,128)(2,1)S(1)}, bf16[793,256]{1,0:T(8,128)(2,1)S(1)}, u32[]{:S(2)}, u32[]{:S(2)}) collective-permute-start(bf16[793,256]{1,0:T(8,128)(2,1)S(1)} %pad_maximum_fusion.8), channel_id=1, source_target_pairs={{0,1},{1,0},{2,3},{3,2},{4,5},{5,4},{6,7},{7,6},{8,9},{9,8},{10,11... | collective-permute-start | bytes 1218056 | tf_op jit(solution)/shard_map/ppermute | solution.py:196
  48.0 2.5 %copy-start = (bf16[5,4,64,2304]{3,2,1,0:T(8,128)(2,1)}, bf16[5,4,64,2304]{3,2,1,0:T(8,128)(2,1)S(1)}, u32[]{:S(2)}) copy-start(bf16[5,4,64,2304]{3,2,1,0:T(8,128)(2,1)S(1)} %slice_dynamic-update-slice_fusion.9) | copy-start | bytes 17694724
  63.2 3.7 %collective-permute-start.10 = (bf16[13,256]{1,0:T(8,128)(2,1)S(1)}, bf16[13,256]{1,0:T(8,128)(2,1)S(1)}, u32[]{:S(2)}, u32[]{:S(2)}) collective-permute-start(bf16[13,256]{1,0:T(8,128)(2,1)S(1)} %pad_maximum_fusion.27), channel_id=1, source_target_pairs={{0,2},{2,0},{1,3},{3,1},{4,6},{6,4},{5,7},{7,5},{8,10},{10,8},{9,1... | collective-permute-start | bytes 19976 | tf_op jit(solution)/shard_map/ppermute | solution.py:196
  67.7 5.8 %collective-permute-start.11 = (bf16[199,256]{1,0:T(8,128)(2,1)S(1)}, bf16[199,256]{1,0:T(8,128)(2,1)S(1)}, u32[]{:S(2)}, u32[]{:S(2)}) collective-permute-start(bf16[199,256]{1,0:T(8,128)(2,1)S(1)} %get-tuple-element.52), channel_id=1, source_target_pairs={{0,4},{4,0},{8,12},{12,8},{1,5},{5,1},{9,13},{13,9},{2,6},{6,2},{1... | collective-permute-start | bytes 305672 | tf_op jit(solution)/shard_map/ppermute | solution.py:196
  67.8 7.8 %collective-permute-start.13 = (f32[2,32]{1,0:T(2,128)S(1)}, f32[2,32]{1,0:T(2,128)S(1)}, u32[]{:S(2)}, u32[]{:S(2)}) collective-permute-start(f32[2,32]{1,0:T(2,128)S(1)} %get-tuple-element.17), channel_id=1, source_target_pairs={{0,8},{4,12},{8,0},{12,4},{1,9},{5,13},{9,1},{13,5},{2,10},{6,14},... | collective-permute-start | bytes 776 | tf_op jit(solution)/shard_map/ppermute | solution.py:196
  68.8 6.5 %collective-permute-start.12 = (bf16[199,256]{1,0:T(8,128)(2,1)S(1)}, bf16[199,256]{1,0:T(8,128)(2,1)S(1)}, u32[]{:S(2)}, u32[]{:S(2)}) collective-permute-start(bf16[199,256]{1,0:T(8,128)(2,1)S(1)} %get-tuple-element.53), channel_id=1, source_target_pairs={{0,12},{4,8},{8,4},{12,0},{1,13},{5,9},{9,5},{13,1},{2,14},{6,10},... | collective-permute-start | bytes 305672 | tf_op jit(solution)/shard_map/ppermute | solution.py:196
  76.2 2.6 %copy-start.6 = (f32[256]{0:T(256)S(1)}, f32[256]{0:T(256)}, u32[]{:S(2)}) copy-start(f32[256]{0:T(256)} %param.18) | copy-start | bytes 3076
  76.3 2.6 %copy-start.7 = (f32[256]{0:T(256)S(1)}, f32[256]{0:T(256)}, u32[]{:S(2)}) copy-start(f32[256]{0:T(256)} %param.17) | copy-start | bytes 3076
  76.3 1.8 %collective-permute-start.14 = (bf16[793,256]{1,0:T(8,128)(2,1)S(1)}, bf16[793,256]{1,0:T(8,128)(2,1)S(1)}, u32[]{:S(2)}, u32[]{:S(2)}) collective-permute-start(bf16[793,256]{1,0:T(8,128)(2,1)S(1)} %pad_maximum_fusion.9), channel_id=1, source_target_pairs={{0,1},{1,0},{2,3},{3,2},{4,5},{5,4},{6,7},{7,6},{8,9},{9,8},{10,11... | collective-permute-start | bytes 1218056 | tf_op jit(solution)/shard_map/ppermute | solution.py:196
  82.3 2.5 %copy-start.1 = (bf16[5,4,64,2304]{3,2,1,0:T(8,128)(2,1)}, bf16[5,4,64,2304]{3,2,1,0:T(8,128)(2,1)S(1)}, u32[]{:S(2)}) copy-start(bf16[5,4,64,2304]{3,2,1,0:T(8,128)(2,1)S(1)} %slice_dynamic-update-slice_fusion) | copy-start | bytes 17694724

commit v14 on v10

--- a/solution.py
+++ b/solution.py
@@ -255,12 +255,12 @@
 
 def fast_latent_input(values):
     sums = local_sums(values.astype(jnp.float32))
-    sums = sums + swap(sums, "ta", 1)
     s_w, beside = swap_with(sums, values[:, :, :1], "wa", 1)
     sums = sums + s_w
     x = jnp.concatenate([values, beside], axis=2)
     sums, _, below = ha_round(sums, x[:, :1], x[:, :1])
     x = jnp.concatenate([x, below], axis=1)
+    sums = sums + swap(sums, "ta", 1)
     return finish_stats(sums, values), x
 
 

time: 77.8 us -> 78.3 us (level)
  starting transfers between devices: 18.3 us -> 17.5 us
    slice x1, local copies, waits for them, and re-layouts: 0.04 us -> 0.9 us  [fast_latent_input(): s_w, beside = swap_with(sums, values[:, :, :1], 'wa', 1)]
    ppermute x15, starting transfers between devices: 18.3 us -> 17.5 us  [swap(): return lax.ppermute(x, axis, [(i, i ^ distance) for i in range(size)])]
  transfers between devices with their start and end apart: 15 -> 15, of which waited for: 10 -> 9; matrix products, arithmetic and copies ran while one was open for 14% -> 14% of each run, Pallas kernels for 0% -> 0%
where the time goes in v14:
time: 78.3 us; the launch traced here: 77.9 us
  local copies, waits for them, and re-layouts  21.6 us (28%)
  waiting for transfers between devices  18.3 us (23%)
  starting transfers between devices  17.5 us (22%)
  other arithmetic  10.9 us (14%)
  matrix products  8.59 us (11%)
  between operations  0.91 us (1%)
    ppermute x15, waiting for transfers between devices, swap(): return lax.ppermute(x, axis, [(i, i ^ distance) for i in range(size)])  18.3 us
    ppermute x15, starting transfers between devices, swap(): return lax.ppermute(x, axis, [(i, i ^ distance) for i in range(size)])  17.5 us
    slice x2, local copies, waits for them, and re-layouts, valid_conv(): kernel[step_t].reshape(9 * channels, -1)  7.42 us
    dot_general x6, matrix products, valid_conv(): jnp.dot(window, kernel[step_t].reshape(9 * channels, -1), preferred_eleme...  6.52 us
    unnamed x39, local copies, waits for them, and re-layouts  3.59 us
    convert_element_type x2, other arithmetic, norm_conv(): jnp.where(inside_mask(height + 2, across + 2, 1), act, 0.0)  3.58 us
    slice x2, local copies, waits for them, and re-layouts, valid_conv(): window = wide[step_t:step_t + frames].reshape(-1, 9 * channels)  2.19 us
    reduce_sum x5, other arithmetic, local_sums(): jnp.sum(grouped, axis=(0, 2))  2.18 us
  transfers between devices with their start and end apart: 15, of which 9 were waited for; matrix products, arithmetic and copies ran while one was open for 14% of the time, Pallas kernels for 0%

profile of v14, /device:TPU:0, one launch (start us, length us, event | category | flops | bytes accessed | tf_op | source)
XLA Modules:
  0.0 77.9 jit_solution(14884290076796522180)
XLA Ops:
  0.0 1.0 %convert_reduce_fusion.2 = (f32[512]{0:T(512)S(1)}, f32[512]{0:T(512)S(1)}) fusion(bf16[3,2,32,512]{3,2,1,0:T(8,128)(2,1)} %param.10), kind=kLoop, calls=%fused_computation.52 | loop fusion | flops 392192 | bytes 200704 | tf_op jit(solution)/shard_map/reduce_sum | solution.py:179
  1.0 0.9 %slice_reduce_fusion = bf16[3,2,512]{2,1,0:T(2,128)(2,1)S(1)} fusion(bf16[3,2,32,512]{3,2,1,0:T(8,128)(2,1)} %param.10), kind=kLoop, calls=%fused_computation.110 | loop fusion | bytes 12288 | tf_op jit(solution)/shard_map/slice | solution.py:258
  2.5 3.0 %collective-permute-start = (bf16[7,512]{1,0:T(8,128)(2,1)S(1)}, bf16[7,512]{1,0:T(8,128)(2,1)S(1)}, u32[]{:S(2)}, u32[]{:S(2)}) collective-permute-start(bf16[7,512]{1,0:T(8,128)(2,1)S(1)} %pad_maximum_fusion.25), channel_id=1, source_target_pairs={{0,2},{2,0},{1,3},{3,1},{4,6},{6,4},{5,7},{7,5},{8,10},{10,8},{9,1... | collective-permute-start | bytes 21512 | tf_op jit(solution)/shard_map/ppermute | solution.py:170
  5.6 1.6 %slice_bitcast_fusion.7 = (bf16[512,256]{1,0:T(8,128)(2,1)S(1)}, bf16[512,256]{1,0:T(8,128)(2,1)S(1)}, bf16[512,256]{1,0:T(8,128)(2,1)S(1)}, bf16[512,256]{1,0:T...) fusion(bf16[3,3,512,256]{3,2,1,0:T(8,128)(2,1)} %param.13), kind=kLoop, calls=%fused_computation.77 | loop fusion | bytes 4194304 | tf_op jit(solution)/shard_map/squeeze | solution.py:129
  8.0 2.0 %collective-permute-start.1 = (bf16[100,512]{1,0:T(8,128)(2,1)S(1)}, bf16[100,512]{1,0:T(8,128)(2,1)S(1)}, u32[]{:S(2)}, u32[]{:S(2)}) collective-permute-start(bf16[100,512]{1,0:T(8,128)(2,1)S(1)} %pad_maximum_fusion.24), channel_id=1, source_target_pairs={{0,4},{4,0},{8,12},{12,8},{1,5},{5,1},{9,13},{13,9},{2,6},{6,2},{1... | collective-permute-start | bytes 307208 | tf_op jit(solution)/shard_map/ppermute | solution.py:170
  10.0 2.5 %collective-permute-start.2 = (bf16[100,512]{1,0:T(8,128)(2,1)S(1)}, bf16[100,512]{1,0:T(8,128)(2,1)S(1)}, u32[]{:S(2)}, u32[]{:S(2)}) collective-permute-start(bf16[100,512]{1,0:T(8,128)(2,1)S(1)} %pad_maximum_fusion.24), channel_id=1, source_target_pairs={{0,12},{4,8},{8,4},{12,0},{1,13},{5,9},{9,5},{13,1},{2,14},{6,10},... | collective-permute-start | bytes 307208 | tf_op jit(solution)/shard_map/ppermute | solution.py:170
  12.7 0.3 collective-permute-done.1
  13.1 3.9 %collective-permute-done.2 = bf16[100,512]{1,0:T(8,128)(2,1)S(1)} collective-permute-done((bf16[100,512]{1,0:T(8,128)(2,1)S(1)}, bf16[100,512]{1,0:T(8,128)(2,1)S(1)}, u32[]{:S(2)}, u32[]{:S(2)}) %collective-permute-start.2) | collective-permute-done | bytes 102432 | tf_op jit(solution)/shard_map/ppermute | solution.py:170
  17.4 1.1 %collective-permute-done.4 = f32[2,32]{1,0:T(2,128)S(1)} collective-permute-done((f32[2,32]{1,0:T(2,128)S(1)}, f32[2,32]{1,0:T(2,128)S(1)}, u32[]{:S(2)}, u32[]{:S(2)}) %collective-permute-start.4) | collective-permute-done | bytes 288 | tf_op jit(solution)/shard_map/ppermute | solution.py:170
  18.8 0.3 select_convert_fusion.2
  19.2 0.3 fusion.11
  19.4 0.3 fusion.15
  19.7 0.4 fusion.1
  20.5 1.2 %convolution_add_fusion.4 = bf16[192,256]{1,0:T(8,128)(2,1)S(1)} fusion(bf16[192,512]{1,0:T(8,128)(2,1)S(1)} %bitcast.122, bf16[3,3,512,256]{3,2,1,0:T(8,128)(2,1)} %param.13, f32[192,512]{1,0:T(8,128)S(1)} %fusion.15, f32[192,512]{1,0:T(8,128)S(1)} %fusion.11, f32[192,1024]{1,0:T(8,128)S(1)} %fusion.1), kind=kOutput, calls=%fused_computation.7 | convolution fusion | flops 50528256 | bytes 1146880 | tf_op jit(solution)/shard_map/dot_general | solution.py:123
  21.8 0.3 pad_maximum_fusion.10
  22.1 0.3 pad_maximum_fusion.11
  22.3 0.8 %convert_reduce_fusion.1 = (f32[256]{0:T(256)S(1)}, f32[256]{0:T(256)S(1)}, bf16[3,2,2,64,256]{4,1,3,0,2:T(2,128)(2,1)S(1)}) fusion(bf16[3,2,1,64,256]{4,1,3,0,2:T(2,128)(2,1)S(1)} %bitcast.125, bf16[3,2,1,64,256]{4,1,3,0,2:T(2,128)(2,1)S(1)} %bitcast.124), kind=kLoop, calls=%fused_computation.19 | loop fusion | flops 982528 | bytes 788480 | tf_op jit(solution)/shard_map/reduce_sum | solution.py:179
  23.9 1.2 %collective-permute-start.5 = (bf16[13,256]{1,0:T(8,128)(2,1)S(1)}, bf16[13,256]{1,0:T(8,128)(2,1)S(1)}, u32[]{:S(2)}, u32[]{:S(2)}) collective-permute-start(bf16[13,256]{1,0:T(8,128)(2,1)S(1)} %pad_maximum_fusion.26), channel_id=1, source_target_pairs={{0,2},{2,0},{1,3},{3,1},{4,6},{6,4},{5,7},{7,5},{8,10},{10,8},{9,1... | collective-permute-start | bytes 19976 | tf_op jit(solution)/shard_map/ppermute | solution.py:170
  25.2 2.5 %collective-permute-done.5 = bf16[13,256]{1,0:T(8,128)(2,1)S(1)} collective-permute-done((bf16[13,256]{1,0:T(8,128)(2,1)S(1)}, bf16[13,256]{1,0:T(8,128)(2,1)S(1)}, u32[]{:S(2)}, u32[]{:S(2)}) %collective-permute-start.5) | collective-permute-done | bytes 6688 | tf_op jit(solution)/shard_map/ppermute | solution.py:170
  28.4 0.7 collective-permute-start.6
  29.1 2.9 %collective-permute-start.7 = (bf16[199,256]{1,0:T(8,128)(2,1)S(1)}, bf16[199,256]{1,0:T(8,128)(2,1)S(1)}, u32[]{:S(2)}, u32[]{:S(2)}) collective-permute-start(bf16[199,256]{1,0:T(8,128)(2,1)S(1)} %get-tuple-element.68), channel_id=1, source_target_pairs={{0,12},{4,8},{8,4},{12,0},{1,13},{5,9},{9,5},{13,1},{2,14},{6,10},... | collective-permute-start | bytes 305672 | tf_op jit(solution)/shard_map/ppermute | solution.py:170
  32.0 2.2 %collective-permute-done.6 = bf16[199,256]{1,0:T(8,128)(2,1)S(1)} collective-permute-done((bf16[199,256]{1,0:T(8,128)(2,1)S(1)}, bf16[199,256]{1,0:T(8,128)(2,1)S(1)}, u32[]{:S(2)}, u32[]{:S(2)}) %collective-permute-start.6) | collective-permute-done | bytes 101920 | tf_op jit(solution)/shard_map/ppermute | solution.py:170
  34.2 1.7 %collective-permute-done.7 = bf16[199,256]{1,0:T(8,128)(2,1)S(1)} collective-permute-done((bf16[199,256]{1,0:T(8,128)(2,1)S(1)}, bf16[199,256]{1,0:T(8,128)(2,1)S(1)}, u32[]{:S(2)}, u32[]{:S(2)}) %collective-permute-start.7) | collective-permute-done | bytes 101920 | tf_op jit(solution)/shard_map/ppermute | solution.py:170
  37.1 3.7 %fusion.117 = (bf16[1,3,3,256,256]{4,3,2,1,0:T(8,128)(2,1)S(1)}, bf16[1,3,3,256,256]{4,3,2,1,0:T(8,128)(2,1)}, bf16[1,3,3,256,256]{4,3,2,1,0:T(8,128)(2,1)}) fusion(bf16[3,3,3,256,256]{4,3,2,1,0:T(8,128)(2,1)} %param.16), kind=kLoop, calls=%fused_computation.281 | loop fusion | bytes 7077888 | tf_op jit(solution)/shard_map/slice | solution.py:154
  41.7 1.9 %select_convert_fusion.1 = bf16[5,6,66,256]{3,2,1,0:T(8,128)(2,1)S(1)} fusion(bf16[3,1,66,256]{3,2,1,0:T(8,128)(2,1)S(1)} %select_n.182, bf16[3,4,1,256]{3,2,1,0:T(2,128)(2,1)S(1)} %reshape.743, bf16[3,4,64,256]{3,2,1,0:T(8,128)(2,1)S(1)} %bitcast.103, bf16[3,1,66,256]{3,2,1,0:T(8,128)(2,1)S(1)} %select_n.179, ...), kind=kLoop, calls=%fused_computation.1 | loop fusion | flops 11151360 | bytes 2025868 | tf_op jit(solution)/shard_map/convert_element_type | solution.py:275
  43.6 0.2 slice_dynamic-update-slice_fusion.16
  43.9 0.2 slice_dynamic-update-slice_fusion.15
  44.2 0.2 slice_dynamic-update-slice_fusion.13
  45.3 1.0 %fusion.115 = (bf16[3,4,64,2304]{3,2,1,0:T(8,128)(2,1)S(1)}, bf16[3,4,64,2304]{3,2,1,0:T(8,128)(2,1)S(1)}, bf16[3,4,64,2304]{3,2,1,0:T(8,128)(2,1)S(1)}) fusion(bf16[5,4,64,2304]{3,2,1,0:T(8,128)(2,1)S(1)} %slice_dynamic-update-slice_fusion.9), kind=kLoop, calls=%fused_computation.279 | loop fusion | bytes 21233664 | tf_op jit(solution)/shard_map/slice | solution.py:152
  46.3 0.3 copy-done.3
  46.6 1.1 %fusion.120 = f32[768,256]{1,0:T(8,128)S(1)} fusion(bf16[768,2304]{1,0:T(8,128)(2,1)S(1)} %bitcast.114, bf16[2304,256]{1,0:T(8,128)(2,1)S(1)} %bitcast.121), kind=kOutput, calls=%fused_computation.284 | convolution fusion | flops 905969664 | bytes 5505024 | tf_op jit(solution)/shard_map/dot_general | solution.py:153
  47.9 1.1 %convolution_add_fusion.3 = f32[768,256]{1,0:T(8,128)S(1)} fusion(f32[768,256]{1,0:T(8,128)S(1)} %fusion.120, bf16[768,2304]{1,0:T(8,128)(2,1)S(1)} %bitcast.112, bf16[2304,256]{1,0:T(8,128)(2,1)S(1)} %bitcast.120), kind=kOutput, calls=%fused_computation.5 | convolution fusion | flops 906166272 | bytes 6291456 | tf_op jit(solution)/shard_map/dot_general | solution.py:153
  48.9 1.1 %convert_reduce_fusion = (f32[256]{0:T(256)S(1)}, f32[256]{0:T(256)S(1)}, bf16[768,256]{1,0:T(8,128)(2,1)S(1)}) fusion(f32[768,256]{1,0:T(8,128)S(1)} %convolution_add_fusion.3, bf16[768,2304]{1,0:T(8,128)(2,1)S(1)} %bitcast.110, bf16[2304,256]{1,0:T(8,128)(2,1)S(1)} %bitcast.116), kind=kOutput, calls=%fused_computation.17 | convolution fusion | flops 907148800 | bytes 5900288 | tf_op jit(solution)/shard_map/dot_general | solution.py:153
  50.8 1.3 %collective-permute-start.10 = (bf16[13,256]{1,0:T(8,128)(2,1)S(1)}, bf16[13,256]{1,0:T(8,128)(2,1)S(1)}, u32[]{:S(2)}, u32[]{:S(2)}) collective-permute-start(bf16[13,256]{1,0:T(8,128)(2,1)S(1)} %pad_maximum_fusion.27), channel_id=1, source_target_pairs={{0,2},{2,0},{1,3},{3,1},{4,6},{6,4},{5,7},{7,5},{8,10},{10,8},{9,1... | collective-permute-start | bytes 19976 | tf_op jit(solution)/shard_map/ppermute | solution.py:170
  52.1 2.4 %collective-permute-done.10 = bf16[13,256]{1,0:T(8,128)(2,1)S(1)} collective-permute-done((bf16[13,256]{1,0:T(8,128)(2,1)S(1)}, bf16[13,256]{1,0:T(8,128)(2,1)S(1)}, u32[]{:S(2)}, u32[]{:S(2)}) %collective-permute-start.10) | collective-permute-done | bytes 6688 | tf_op jit(solution)/shard_map/ppermute | solution.py:170
  55.4 3.3 %collective-permute-start.12 = (bf16[199,256]{1,0:T(8,128)(2,1)S(1)}, bf16[199,256]{1,0:T(8,128)(2,1)S(1)}, u32[]{:S(2)}, u32[]{:S(2)}) collective-permute-start(bf16[199,256]{1,0:T(8,128)(2,1)S(1)} %get-tuple-element.62), channel_id=1, source_target_pairs={{0,12},{4,8},{8,4},{12,0},{1,13},{5,9},{9,5},{13,1},{2,14},{6,10},... | collective-permute-start | bytes 305672 | tf_op jit(solution)/shard_map/ppermute | solution.py:170
  58.8 2.0 %collective-permute-done.11 = bf16[199,256]{1,0:T(8,128)(2,1)S(1)} collective-permute-done((bf16[199,256]{1,0:T(8,128)(2,1)S(1)}, bf16[199,256]{1,0:T(8,128)(2,1)S(1)}, u32[]{:S(2)}, u32[]{:S(2)}) %collective-permute-start.11) | collective-permute-done | bytes 101920 | tf_op jit(solution)/shard_map/ppermute | solution.py:170
  60.8 2.3 %collective-permute-done.12 = bf16[199,256]{1,0:T(8,128)(2,1)S(1)} collective-permute-done((bf16[199,256]{1,0:T(8,128)(2,1)S(1)}, bf16[199,256]{1,0:T(8,128)(2,1)S(1)}, u32[]{:S(2)}, u32[]{:S(2)}) %collective-permute-start.12) | collective-permute-done | bytes 101920 | tf_op jit(solution)/shard_map/ppermute | solution.py:170
  64.3 3.7 %fusion.116 = (bf16[1,3,3,256,256]{4,3,2,1,0:T(8,128)(2,1)S(1)}, bf16[1,3,3,256,256]{4,3,2,1,0:T(8,128)(2,1)}, bf16[1,3,3,256,256]{4,3,2,1,0:T(8,128)(2,1)}) fusion(bf16[3,3,3,256,256]{4,3,2,1,0:T(8,128)(2,1)} %param.19), kind=kLoop, calls=%fused_computation.280 | loop fusion | bytes 7077888 | tf_op jit(solution)/shard_map/slice | solution.py:154
  68.8 1.7 %select_convert_fusion = bf16[5,6,66,256]{3,2,1,0:T(8,128)(2,1)S(1)} fusion(bf16[3,1,66,256]{3,2,1,0:T(8,128)(2,1)S(1)} %select_n.191, bf16[3,4,1,256]{3,2,1,0:T(2,128)(2,1)S(1)} %reshape.744, bf16[3,4,64,256]{3,2,1,0:T(8,128)(2,1)S(1)} %bitcast.109, bf16[3,1,66,256]{3,2,1,0:T(8,128)(2,1)S(1)} %select_n.189, ...), kind=kLoop, calls=%fused_computation | loop fusion | flops 11151360 | bytes 2025868 | tf_op jit(solution)/shard_map/convert_element_type | solution.py:275
  70.6 0.2 slice_dynamic-update-slice_fusion.7
  70.8 0.2 slice_dynamic-update-slice_fusion.6
  71.2 0.2 slice_dynamic-update-slice_fusion.4
  72.3 1.2 %fusion.114 = (bf16[3,4,64,2304]{3,2,1,0:T(8,128)(2,1)S(1)}, bf16[3,4,64,2304]{3,2,1,0:T(8,128)(2,1)S(1)}, bf16[3,4,64,2304]{3,2,1,0:T(8,128)(2,1)S(1)}) fusion(bf16[5,4,64,2304]{3,2,1,0:T(8,128)(2,1)S(1)} %slice_dynamic-update-slice_fusion), kind=kLoop, calls=%fused_computation.278 | loop fusion | bytes 21233664 | tf_op jit(solution)/shard_map/slice | solution.py:152
  73.5 1.1 %fusion.121 = f32[768,256]{1,0:T(8,128)S(1)} fusion(bf16[768,2304]{1,0:T(8,128)(2,1)S(1)} %bitcast.115, bf16[2304,256]{1,0:T(8,128)(2,1)S(1)} %bitcast.119), kind=kOutput, calls=%fused_computation.285 | convolution fusion | flops 905969664 | bytes 5505024 | tf_op jit(solution)/shard_map/dot_general | solution.py:153
  74.8 1.1 %convolution_add_fusion.1 = f32[768,256]{1,0:T(8,128)S(1)} fusion(f32[768,256]{1,0:T(8,128)S(1)} %fusion.121, bf16[768,2304]{1,0:T(8,128)(2,1)S(1)} %bitcast.113, bf16[2304,256]{1,0:T(8,128)(2,1)S(1)} %bitcast.118), kind=kOutput, calls=%fused_computation.3 | convolution fusion | flops 906166272 | bytes 6291456 | tf_op jit(solution)/shard_map/dot_general | solution.py:153
  75.9 1.1 %convolution_add_fusion = f32[768,256]{1,0:T(8,128)S(1)} fusion(f32[768,256]{1,0:T(8,128)S(1)} %convolution_add_fusion.1, bf16[768,2304]{1,0:T(8,128)(2,1)S(1)} %bitcast.111, bf16[2304,256]{1,0:T(8,128)(2,1)S(1)} %bitcast.117), kind=kOutput, calls=%fused_computation.2 | convolution fusion | flops 906166272 | bytes 6291456 | tf_op jit(solution)/shard_map/dot_general | solution.py:153
  77.0 0.9 %add_convert_fusion = bf16[3,4,64,256]{3,2,1,0:T(8,128)(2,1)} fusion(f32[3,4,64,256]{3,2,1,0:T(8,128)S(1)} %bitcast.123, bf16[3,4,64,256]{3,2,1,0:T(8,128)(2,1)S(1)} %bitcast.104), kind=kLoop, calls=%fused_computation.23 | loop fusion | flops 589824 | bytes 1572864 | tf_op jit(solution)/shard_map/convert_element_type | solution.py:302
  (224 shorter events, 12.2 us)
Async XLA Ops:
  1.0 6.3 %copy-start.4 = (bf16[3,2,32,512]{3,2,1,0:T(8,128)(2,1)S(1)}, bf16[3,2,32,512]{3,2,1,0:T(8,128)(2,1)}, u32[]{:S(2)}) copy-start(bf16[3,2,32,512]{3,2,1,0:T(8,128)(2,1)} %param.10) | copy-start | bytes 589828
  2.5 4.8 %collective-permute-start = (bf16[7,512]{1,0:T(8,128)(2,1)S(1)}, bf16[7,512]{1,0:T(8,128)(2,1)S(1)}, u32[]{:S(2)}, u32[]{:S(2)}) collective-permute-start(bf16[7,512]{1,0:T(8,128)(2,1)S(1)} %pad_maximum_fusion.25), channel_id=1, source_target_pairs={{0,2},{2,0},{1,3},{3,1},{4,6},{6,4},{5,7},{7,5},{8,10},{10,8},{9,1... | collective-permute-start | bytes 21512 | tf_op jit(solution)/shard_map/ppermute | solution.py:170
  5.6 13.2 %copy-start.5 = (f32[512]{0:T(512)S(1)}, f32[512]{0:T(512)}, u32[]{:S(2)}) copy-start(f32[512]{0:T(512)} %param.12) | copy-start | bytes 6148
  5.6 13.2 %copy-start.6 = (f32[512]{0:T(512)S(1)}, f32[512]{0:T(512)}, u32[]{:S(2)}) copy-start(f32[512]{0:T(512)} %param.11) | copy-start | bytes 6148
  8.0 5.0 %collective-permute-start.1 = (bf16[100,512]{1,0:T(8,128)(2,1)S(1)}, bf16[100,512]{1,0:T(8,128)(2,1)S(1)}, u32[]{:S(2)}, u32[]{:S(2)}) collective-permute-start(bf16[100,512]{1,0:T(8,128)(2,1)S(1)} %pad_maximum_fusion.24), channel_id=1, source_target_pairs={{0,4},{4,0},{8,12},{12,8},{1,5},{5,1},{9,13},{13,9},{2,6},{6,2},{1... | collective-permute-start | bytes 307208 | tf_op jit(solution)/shard_map/ppermute | solution.py:170
  10.0 6.9 %collective-permute-start.2 = (bf16[100,512]{1,0:T(8,128)(2,1)S(1)}, bf16[100,512]{1,0:T(8,128)(2,1)S(1)}, u32[]{:S(2)}, u32[]{:S(2)}) collective-permute-start(bf16[100,512]{1,0:T(8,128)(2,1)S(1)} %pad_maximum_fusion.24), channel_id=1, source_target_pairs={{0,12},{4,8},{8,4},{12,0},{1,13},{5,9},{9,5},{13,1},{2,14},{6,10},... | collective-permute-start | bytes 307208 | tf_op jit(solution)/shard_map/ppermute | solution.py:170
  12.5 4.7 %collective-permute-start.3 = (f32[2,32]{1,0:T(2,128)S(1)}, f32[2,32]{1,0:T(2,128)S(1)}, u32[]{:S(2)}, u32[]{:S(2)}) collective-permute-start(f32[2,32]{1,0:T(2,128)S(1)} %get-tuple-element.27), channel_id=1, source_target_pairs={{0,8},{4,12},{8,0},{12,4},{1,9},{5,13},{9,1},{13,5},{2,10},{6,14},... | collective-permute-start | bytes 776 | tf_op jit(solution)/shard_map/ppermute | solution.py:170
  17.2 1.2 %collective-permute-start.4 = (f32[2,32]{1,0:T(2,128)S(1)}, f32[2,32]{1,0:T(2,128)S(1)}, u32[]{:S(2)}, u32[]{:S(2)}) collective-permute-start(f32[2,32]{1,0:T(2,128)S(1)} %add_add_fusion.2), channel_id=1, source_target_pairs={{0,1},{1,0},{2,3},{3,2},{4,5},{5,4},{6,7},{7,6},{8,9},{9,8},{10,11... | collective-permute-start | bytes 776 | tf_op jit(solution)/shard_map/ppermute | solution.py:170
  23.9 3.7 %collective-permute-start.5 = (bf16[13,256]{1,0:T(8,128)(2,1)S(1)}, bf16[13,256]{1,0:T(8,128)(2,1)S(1)}, u32[]{:S(2)}, u32[]{:S(2)}) collective-permute-start(bf16[13,256]{1,0:T(8,128)(2,1)S(1)} %pad_maximum_fusion.26), channel_id=1, source_target_pairs={{0,2},{2,0},{1,3},{3,1},{4,6},{6,4},{5,7},{7,5},{8,10},{10,8},{9,1... | collective-permute-start | bytes 19976 | tf_op jit(solution)/shard_map/ppermute | solution.py:170
  28.4 5.8 %collective-permute-start.6 = (bf16[199,256]{1,0:T(8,128)(2,1)S(1)}, bf16[199,256]{1,0:T(8,128)(2,1)S(1)}, u32[]{:S(2)}, u32[]{:S(2)}) collective-permute-start(bf16[199,256]{1,0:T(8,128)(2,1)S(1)} %get-tuple-element.67), channel_id=1, source_target_pairs={{0,4},{4,0},{8,12},{12,8},{1,5},{5,1},{9,13},{13,9},{2,6},{6,2},{1... | collective-permute-start | bytes 305672 | tf_op jit(solution)/shard_map/ppermute | solution.py:170
  29.1 6.9 %collective-permute-start.7 = (bf16[199,256]{1,0:T(8,128)(2,1)S(1)}, bf16[199,256]{1,0:T(8,128)(2,1)S(1)}, u32[]{:S(2)}, u32[]{:S(2)}) collective-permute-start(bf16[199,256]{1,0:T(8,128)(2,1)S(1)} %get-tuple-element.68), channel_id=1, source_target_pairs={{0,12},{4,8},{8,4},{12,0},{1,13},{5,9},{9,5},{13,1},{2,14},{6,10},... | collective-permute-start | bytes 305672 | tf_op jit(solution)/shard_map/ppermute | solution.py:170
  32.0 4.6 %collective-permute-start.8 = (f32[2,32]{1,0:T(2,128)S(1)}, f32[2,32]{1,0:T(2,128)S(1)}, u32[]{:S(2)}, u32[]{:S(2)}) collective-permute-start(f32[2,32]{1,0:T(2,128)S(1)} %get-tuple-element.24), channel_id=1, source_target_pairs={{0,8},{4,12},{8,0},{12,4},{1,9},{5,13},{9,1},{13,5},{2,10},{6,14},... | collective-permute-start | bytes 776 | tf_op jit(solution)/shard_map/ppermute | solution.py:170
  37.0 3.8 %collective-permute-start.9 = (bf16[793,256]{1,0:T(8,128)(2,1)S(1)}, bf16[793,256]{1,0:T(8,128)(2,1)S(1)}, u32[]{:S(2)}, u32[]{:S(2)}) collective-permute-start(bf16[793,256]{1,0:T(8,128)(2,1)S(1)} %pad_maximum_fusion.8), channel_id=1, source_target_pairs={{0,1},{1,0},{2,3},{3,2},{4,5},{5,4},{6,7},{7,6},{8,9},{9,8},{10,11... | collective-permute-start | bytes 1218056 | tf_op jit(solution)/shard_map/ppermute | solution.py:170
  40.8 0.8 %copy-start.7 = (f32[256]{0:T(256)S(1)}, f32[256]{0:T(256)}, u32[]{:S(2)}) copy-start(f32[256]{0:T(256)} %param.15) | copy-start | bytes 3076
  40.8 0.8 %copy-start.8 = (f32[256]{0:T(256)S(1)}, f32[256]{0:T(256)}, u32[]{:S(2)}) copy-start(f32[256]{0:T(256)} %param.14) | copy-start | bytes 3076
  45.3 1.3 %copy-start.3 = (bf16[1,3,3,256,256]{4,3,2,1,0:T(8,128)(2,1)S(1)}, bf16[1,3,3,256,256]{4,3,2,1,0:T(8,128)(2,1)}, u32[]{:S(2)}) copy-start(bf16[1,3,3,256,256]{4,3,2,1,0:T(8,128)(2,1)} %get-tuple-element.38) | copy-start | bytes 3538948
  46.6 1.3 %copy-start.2 = (bf16[1,3,3,256,256]{4,3,2,1,0:T(8,128)(2,1)S(1)}, bf16[1,3,3,256,256]{4,3,2,1,0:T(8,128)(2,1)}, u32[]{:S(2)}) copy-start(bf16[1,3,3,256,256]{4,3,2,1,0:T(8,128)(2,1)} %get-tuple-element.39) | copy-start | bytes 3538948
  50.8 3.7 %collective-permute-start.10 = (bf16[13,256]{1,0:T(8,128)(2,1)S(1)}, bf16[13,256]{1,0:T(8,128)(2,1)S(1)}, u32[]{:S(2)}, u32[]{:S(2)}) collective-permute-start(bf16[13,256]{1,0:T(8,128)(2,1)S(1)} %pad_maximum_fusion.27), channel_id=1, source_target_pairs={{0,2},{2,0},{1,3},{3,1},{4,6},{6,4},{5,7},{7,5},{8,10},{10,8},{9,1... | collective-permute-start | bytes 19976 | tf_op jit(solution)/shard_map/ppermute | solution.py:170
  55.3 5.5 %collective-permute-start.11 = (bf16[199,256]{1,0:T(8,128)(2,1)S(1)}, bf16[199,256]{1,0:T(8,128)(2,1)S(1)}, u32[]{:S(2)}, u32[]{:S(2)}) collective-permute-start(bf16[199,256]{1,0:T(8,128)(2,1)S(1)} %get-tuple-element.61), channel_id=1, source_target_pairs={{0,4},{4,0},{8,12},{12,8},{1,5},{5,1},{9,13},{13,9},{2,6},{6,2},{1... | collective-permute-start | bytes 305672 | tf_op jit(solution)/shard_map/ppermute | solution.py:170
  55.4 7.7 %collective-permute-start.12 = (bf16[199,256]{1,0:T(8,128)(2,1)S(1)}, bf16[199,256]{1,0:T(8,128)(2,1)S(1)}, u32[]{:S(2)}, u32[]{:S(2)}) collective-permute-start(bf16[199,256]{1,0:T(8,128)(2,1)S(1)} %get-tuple-element.62), channel_id=1, source_target_pairs={{0,12},{4,8},{8,4},{12,0},{1,13},{5,9},{9,5},{13,1},{2,14},{6,10},... | collective-permute-start | bytes 305672 | tf_op jit(solution)/shard_map/ppermute | solution.py:170
  58.8 5.0 %collective-permute-start.13 = (f32[2,32]{1,0:T(2,128)S(1)}, f32[2,32]{1,0:T(2,128)S(1)}, u32[]{:S(2)}, u32[]{:S(2)}) collective-permute-start(f32[2,32]{1,0:T(2,128)S(1)} %get-tuple-element.17), channel_id=1, source_target_pairs={{0,8},{4,12},{8,0},{12,4},{1,9},{5,13},{9,1},{13,5},{2,10},{6,14},... | collective-permute-start | bytes 776 | tf_op jit(solution)/shard_map/ppermute | solution.py:170
  64.2 3.8 %collective-permute-start.14 = (bf16[793,256]{1,0:T(8,128)(2,1)S(1)}, bf16[793,256]{1,0:T(8,128)(2,1)S(1)}, u32[]{:S(2)}, u32[]{:S(2)}) collective-permute-start(bf16[793,256]{1,0:T(8,128)(2,1)S(1)} %pad_maximum_fusion.9), channel_id=1, source_target_pairs={{0,1},{1,0},{2,3},{3,2},{4,5},{5,4},{6,7},{7,6},{8,9},{9,8},{10,11... | collective-permute-start | bytes 1218056 | tf_op jit(solution)/shard_map/ppermute | solution.py:170
  68.0 0.8 %copy-start.9 = (f32[256]{0:T(256)S(1)}, f32[256]{0:T(256)}, u32[]{:S(2)}) copy-start(f32[256]{0:T(256)} %param.18) | copy-start | bytes 3076
  68.0 0.8 %copy-start.10 = (f32[256]{0:T(256)S(1)}, f32[256]{0:T(256)}, u32[]{:S(2)}) copy-start(f32[256]{0:T(256)} %param.17) | copy-start | bytes 3076
  72.3 1.3 %copy-start.1 = (bf16[1,3,3,256,256]{4,3,2,1,0:T(8,128)(2,1)S(1)}, bf16[1,3,3,256,256]{4,3,2,1,0:T(8,128)(2,1)}, u32[]{:S(2)}) copy-start(bf16[1,3,3,256,256]{4,3,2,1,0:T(8,128)(2,1)} %get-tuple-element.35) | copy-start | bytes 3538948
  73.5 1.3 %copy-start = (bf16[1,3,3,256,256]{4,3,2,1,0:T(8,128)(2,1)S(1)}, bf16[1,3,3,256,256]{4,3,2,1,0:T(8,128)(2,1)}, u32[]{:S(2)}) copy-start(bf16[1,3,3,256,256]{4,3,2,1,0:T(8,128)(2,1)} %get-tuple-element.36) | copy-start | bytes 3538948

commit v15 on v10

--- a/solution.py
+++ b/solution.py
@@ -144,16 +144,17 @@
 
 def valid_conv(padded, kernel, frames, height, across):
     channels = padded.shape[-1]
-    wide = jnp.concatenate(
-        [padded[:, dy : dy + height, dx : dx + across] for dy in range(3) for dx in range(3)], axis=-1
-    )
+    wide = jnp.concatenate([padded[:, :, dx : dx + across] for dx in range(3)], axis=-1)
     result = None
     for step_t in range(3):
-        window = wide[step_t : step_t + frames].reshape(-1, 9 * channels)
-        part = jnp.dot(
-            window, kernel[step_t].reshape(9 * channels, -1), preferred_element_type=jnp.float32
-        )
-        result = part if result is None else result + part
+        for step_y in range(3):
+            window = wide[step_t : step_t + frames, step_y : step_y + height]
+            part = jnp.dot(
+                window.reshape(-1, 3 * channels),
+                kernel[step_t, step_y].reshape(3 * channels, -1),
+                preferred_element_type=jnp.float32,
+            )
+            result = part if result is None else result + part
     return result.reshape(frames, height, across, -1)
 
 

time: 77.8 us -> 84.9 us (1.091)
  other arithmetic: 11 us -> 14.9 us
  matrix products: 8.59 us -> 10.8 us
    dot_general x6 -> x18, matrix products: 6.52 us -> 8.7 us  [valid_conv(): jnp.dot(window.reshape(-1, 3 * channels), kernel[step_t, step_y].reshape(...]
    select_n x2, other arithmetic: 0.12 us -> 2.22 us  [fast_conv_input(): earlier = jnp.where(lax.axis_index('ta') == 0, opening, earlier)]
    slice x2, other arithmetic: 0.1 us -> 1.46 us  [fast_conv_input(): opening = jnp.concatenate([x[:1], x[:1]], axis=0)]
    slice x4 -> x6, local copies, waits for them, and re-layouts: 9.61 us -> 10.9 us  [the longest x2 6.49 us: valid_conv(): kernel[step_t, step_y].reshape(3 * channels, -1)]
    unnamed x39 -> x33, local copies, waits for them, and re-layouts: 3.58 us -> 3.6 us
where the time goes in v15:
time: 84.9 us; the launch traced here: 84.3 us
  local copies, waits for them, and re-layouts  21.7 us (26%)
  starting transfers between devices  18.3 us (22%)
  waiting for transfers between devices  17.7 us (21%)
  other arithmetic  14.9 us (18%)
  matrix products  10.8 us (13%)
  between operations  0.9 us (1%)
    ppermute x15, starting transfers between devices, swap(): return lax.ppermute(x, axis, [(i, i ^ distance) for i in range(size)])  18.3 us
    ppermute x15, waiting for transfers between devices, swap(): return lax.ppermute(x, axis, [(i, i ^ distance) for i in range(size)])  17.7 us
    dot_general x18, matrix products, valid_conv(): jnp.dot(window.reshape(-1, 3 * channels), kernel[step_t, step_y].reshape(...  8.7 us
    slice x2, local copies, waits for them, and re-layouts, valid_conv(): kernel[step_t, step_y].reshape(3 * channels, -1)  6.49 us
    unnamed x33, local copies, waits for them, and re-layouts  3.6 us
    convert_element_type x2, other arithmetic, norm_conv(): jnp.where(inside_mask(height + 2, across + 2, 1), act, 0.0)  3.58 us
    slice x2, local copies, waits for them, and re-layouts, valid_conv(): window = wide[step_t:step_t + frames, step_y:step_y + height]  2.9 us
    select_n x2, other arithmetic, fast_conv_input(): earlier = jnp.where(lax.axis_index('ta') == 0, opening, earlier)  2.22 us
  transfers between devices with their start and end apart: 15, of which 10 were waited for; matrix products, arithmetic and copies ran while one was open for 14% of the time, Pallas kernels for 0%

profile of v15, /device:TPU:0, one launch (start us, length us, event | category | flops | bytes accessed | tf_op | source)
XLA Modules:
  0.0 84.3 jit_solution(7560372113988383142)
XLA Ops:
  0.0 1.0 %convert_reduce_fusion.2 = (f32[512]{0:T(512)S(1)}, f32[512]{0:T(512)S(1)}) fusion(bf16[3,2,32,512]{3,2,1,0:T(8,128)(2,1)} %param.10), kind=kLoop, calls=%fused_computation.48 | loop fusion | flops 392192 | bytes 200704 | tf_op jit(solution)/shard_map/reduce_sum | solution.py:180
  1.4 0.5 collective-permute-start
  2.0 1.7 %slice_bitcast_fusion.7 = (bf16[512,256]{1,0:T(8,128)(2,1)S(1)}, bf16[512,256]{1,0:T(8,128)(2,1)S(1)}, bf16[512,256]{1,0:T(8,128)(2,1)S(1)}, bf16[512,256]{1,0:T...) fusion(bf16[3,3,512,256]{3,2,1,0:T(8,128)(2,1)} %param.13), kind=kLoop, calls=%fused_computation.73 | loop fusion | bytes 4194304 | tf_op jit(solution)/shard_map/squeeze | solution.py:129
  4.2 2.6 %collective-permute-start.1 = (bf16[7,512]{1,0:T(8,128)(2,1)S(1)}, bf16[7,512]{1,0:T(8,128)(2,1)S(1)}, u32[]{:S(2)}, u32[]{:S(2)}) collective-permute-start(bf16[7,512]{1,0:T(8,128)(2,1)S(1)} %pad_maximum_fusion.27), channel_id=1, source_target_pairs={{0,2},{2,0},{1,3},{3,1},{4,6},{6,4},{5,7},{7,5},{8,10},{10,8},{9,1... | collective-permute-start | bytes 21512 | tf_op jit(solution)/shard_map/ppermute | solution.py:171
  6.8 1.6 %collective-permute-done.1 = bf16[7,512]{1,0:T(8,128)(2,1)S(1)} collective-permute-done((bf16[7,512]{1,0:T(8,128)(2,1)S(1)}, bf16[7,512]{1,0:T(8,128)(2,1)S(1)}, u32[]{:S(2)}, u32[]{:S(2)}) %collective-permute-start.1) | collective-permute-done | bytes 7200 | tf_op jit(solution)/shard_map/ppermute | solution.py:171
  9.1 2.2 %collective-permute-start.2 = (bf16[100,512]{1,0:T(8,128)(2,1)S(1)}, bf16[100,512]{1,0:T(8,128)(2,1)S(1)}, u32[]{:S(2)}, u32[]{:S(2)}) collective-permute-start(bf16[100,512]{1,0:T(8,128)(2,1)S(1)} %pad_maximum_fusion.26), channel_id=1, source_target_pairs={{0,4},{4,0},{8,12},{12,8},{1,5},{5,1},{9,13},{13,9},{2,6},{6,2},{1... | collective-permute-start | bytes 307208 | tf_op jit(solution)/shard_map/ppermute | solution.py:171
  11.3 2.5 %collective-permute-start.3 = (bf16[100,512]{1,0:T(8,128)(2,1)S(1)}, bf16[100,512]{1,0:T(8,128)(2,1)S(1)}, u32[]{:S(2)}, u32[]{:S(2)}) collective-permute-start(bf16[100,512]{1,0:T(8,128)(2,1)S(1)} %pad_maximum_fusion.26), channel_id=1, source_target_pairs={{0,12},{4,8},{8,4},{12,0},{1,13},{5,9},{9,5},{13,1},{2,14},{6,10},... | collective-permute-start | bytes 307208 | tf_op jit(solution)/shard_map/ppermute | solution.py:171
  14.2 4.1 %collective-permute-done.3 = bf16[100,512]{1,0:T(8,128)(2,1)S(1)} collective-permute-done((bf16[100,512]{1,0:T(8,128)(2,1)S(1)}, bf16[100,512]{1,0:T(8,128)(2,1)S(1)}, u32[]{:S(2)}, u32[]{:S(2)}) %collective-permute-start.3) | collective-permute-done | bytes 102432 | tf_op jit(solution)/shard_map/ppermute | solution.py:171
  20.7 1.2 %convolution_add_fusion.16 = bf16[192,256]{1,0:T(8,128)(2,1)S(1)} fusion(bf16[192,512]{1,0:T(8,128)(2,1)S(1)} %bitcast.194, bf16[3,3,512,256]{3,2,1,0:T(8,128)(2,1)} %param.13, f32[192,512]{1,0:T(8,128)S(1)} %fusion.15, f32[192,512]{1,0:T(8,128)S(1)} %fusion.11, f32[192,1024]{1,0:T(8,128)S(1)} %fusion.1), kind=kOutput, calls=%fused_computation.21 | convolution fusion | flops 50528256 | bytes 1146880 | tf_op jit(solution)/shard_map/dot_general | solution.py:123
  22.5 0.8 convert_reduce_fusion.1
  24.1 1.6 %collective-permute-start.5 = (bf16[13,256]{1,0:T(8,128)(2,1)S(1)}, bf16[13,256]{1,0:T(8,128)(2,1)S(1)}, u32[]{:S(2)}, u32[]{:S(2)}) collective-permute-start(bf16[13,256]{1,0:T(8,128)(2,1)S(1)} %pad_maximum_fusion.28), channel_id=1, source_target_pairs={{0,2},{2,0},{1,3},{3,1},{4,6},{6,4},{5,7},{7,5},{8,10},{10,8},{9,1... | collective-permute-start | bytes 19976 | tf_op jit(solution)/shard_map/ppermute | solution.py:171
  25.7 2.1 %collective-permute-done.5 = bf16[13,256]{1,0:T(8,128)(2,1)S(1)} collective-permute-done((bf16[13,256]{1,0:T(8,128)(2,1)S(1)}, bf16[13,256]{1,0:T(8,128)(2,1)S(1)}, u32[]{:S(2)}, u32[]{:S(2)}) %collective-permute-start.5) | collective-permute-done | bytes 6688 | tf_op jit(solution)/shard_map/ppermute | solution.py:171
  28.6 0.7 collective-permute-start.6
  29.3 2.8 %collective-permute-start.7 = (bf16[199,256]{1,0:T(8,128)(2,1)S(1)}, bf16[199,256]{1,0:T(8,128)(2,1)S(1)}, u32[]{:S(2)}, u32[]{:S(2)}) collective-permute-start(bf16[199,256]{1,0:T(8,128)(2,1)S(1)} %get-tuple-element.100), channel_id=1, source_target_pairs={{0,12},{4,8},{8,4},{12,0},{1,13},{5,9},{9,5},{13,1},{2,14},{6,10},... | collective-permute-start | bytes 305672 | tf_op jit(solution)/shard_map/ppermute | solution.py:171
  32.2 1.1 %collective-permute-done.6 = bf16[199,256]{1,0:T(8,128)(2,1)S(1)} collective-permute-done((bf16[199,256]{1,0:T(8,128)(2,1)S(1)}, bf16[199,256]{1,0:T(8,128)(2,1)S(1)}, u32[]{:S(2)}, u32[]{:S(2)}) %collective-permute-start.6) | collective-permute-done | bytes 101920 | tf_op jit(solution)/shard_map/ppermute | solution.py:171
  33.3 2.6 %collective-permute-done.7 = bf16[199,256]{1,0:T(8,128)(2,1)S(1)} collective-permute-done((bf16[199,256]{1,0:T(8,128)(2,1)S(1)}, bf16[199,256]{1,0:T(8,128)(2,1)S(1)}, u32[]{:S(2)}, u32[]{:S(2)}) %collective-permute-start.7) | collective-permute-done | bytes 101920 | tf_op jit(solution)/shard_map/ppermute | solution.py:171
  37.1 3.2 %fusion.115 = (bf16[1,1,3,256,256]{4,3,2,1,0:T(8,128)(2,1)}, bf16[1,1,3,256,256]{4,3,2,1,0:T(8,128)(2,1)S(1)}, bf16[1,1,3,256,256]{4,3,2,1,0:T(8,128)(2,1)S(1)},...) fusion(bf16[3,3,3,256,256]{4,3,2,1,0:T(8,128)(2,1)} %param.16), kind=kLoop, calls=%fused_computation.275 | loop fusion | bytes 7077888 | tf_op jit(solution)/shard_map/slice | solution.py:154
  40.3 0.7 pad_maximum_fusion.15
  41.8 1.1 %maximum_select_fusion = bf16[2,6,66,256]{3,2,1,0:T(8,128)(2,1)S(1)} fusion(bf16[2,6,66,256]{3,2,1,0:T(8,128)(2,1)S(1)} %reshape.764, bf16[1,6,66,256]{3,2,1,0:T(8,128)(2,1)} %pad_maximum_fusion.15, pred[]{:T(512)S(6)} %eq.35), kind=kLoop, calls=%fused_computation.57 | loop fusion | flops 405504 | bytes 1013761 | tf_op jit(solution)/shard_map/jit(_where)/select_n | solution.py:252
  42.9 1.9 %select_convert_fusion.1 = bf16[5,6,66,256]{3,2,1,0:T(8,128)(2,1)S(1)} fusion(bf16[3,1,66,256]{3,2,1,0:T(8,128)(2,1)S(1)} %select_n.182, bf16[3,4,1,256]{3,2,1,0:T(2,128)(2,1)S(1)} %reshape.800, bf16[3,4,64,256]{3,2,1,0:T(8,128)(2,1)S(1)} %bitcast.151, bf16[3,1,66,256]{3,2,1,0:T(8,128)(2,1)S(1)} %select_n.179, ...), kind=kLoop, calls=%fused_computation.3 | loop fusion | flops 11151360 | bytes 2025868 | tf_op jit(solution)/shard_map/convert_element_type | solution.py:276
  44.8 0.7 fusion.119
  45.8 1.3 %fusion.117 = (bf16[3,4,64,768]{3,2,1,0:T(8,128)(2,1)S(1)}, bf16[3,4,64,768]{3,2,1,0:T(8,128)(2,1)S(1)}, bf16[3,4,64,768]{3,2,1,0:T(8,128)(2,1)S(1)}, bf16[3,4,6...) fusion(bf16[5,6,64,768]{3,2,1,0:T(8,128)(2,1)S(1)} %pad_maximum, ...), kind=kLoop, calls=%fused_computation.277 | loop fusion | bytes 21233664 | tf_op jit(solution)/shard_map/slice | solution.py:151
  47.7 0.5 copy-done.6
  48.7 0.5 copy-done.3
  50.7 0.5 convolution_add_fusion.11
  51.2 0.5 convolution_add_fusion.10
  51.7 0.5 convolution_add_fusion.9
  52.2 0.5 copy-done.9
  52.6 0.5 convert_reduce_fusion
  53.9 1.6 %collective-permute-start.10 = (bf16[13,256]{1,0:T(8,128)(2,1)S(1)}, bf16[13,256]{1,0:T(8,128)(2,1)S(1)}, u32[]{:S(2)}, u32[]{:S(2)}) collective-permute-start(bf16[13,256]{1,0:T(8,128)(2,1)S(1)} %pad_maximum_fusion.29), channel_id=1, source_target_pairs={{0,2},{2,0},{1,3},{3,1},{4,6},{6,4},{5,7},{7,5},{8,10},{10,8},{9,1... | collective-permute-start | bytes 19976 | tf_op jit(solution)/shard_map/ppermute | solution.py:171
  55.4 2.2 %collective-permute-done.10 = bf16[13,256]{1,0:T(8,128)(2,1)S(1)} collective-permute-done((bf16[13,256]{1,0:T(8,128)(2,1)S(1)}, bf16[13,256]{1,0:T(8,128)(2,1)S(1)}, u32[]{:S(2)}, u32[]{:S(2)}) %collective-permute-start.10) | collective-permute-done | bytes 6688 | tf_op jit(solution)/shard_map/ppermute | solution.py:171
  58.7 2.4 %collective-permute-start.12 = (bf16[199,256]{1,0:T(8,128)(2,1)S(1)}, bf16[199,256]{1,0:T(8,128)(2,1)S(1)}, u32[]{:S(2)}, u32[]{:S(2)}) collective-permute-start(bf16[199,256]{1,0:T(8,128)(2,1)S(1)} %get-tuple-element.94), channel_id=1, source_target_pairs={{0,12},{4,8},{8,4},{12,0},{1,13},{5,9},{9,5},{13,1},{2,14},{6,10},... | collective-permute-start | bytes 305672 | tf_op jit(solution)/shard_map/ppermute | solution.py:171
  61.1 0.8 collective-permute-start.13
  61.9 2.3 %collective-permute-done.11 = bf16[199,256]{1,0:T(8,128)(2,1)S(1)} collective-permute-done((bf16[199,256]{1,0:T(8,128)(2,1)S(1)}, bf16[199,256]{1,0:T(8,128)(2,1)S(1)}, u32[]{:S(2)}, u32[]{:S(2)}) %collective-permute-start.11) | collective-permute-done | bytes 101920 | tf_op jit(solution)/shard_map/ppermute | solution.py:171
  64.2 1.5 %collective-permute-done.12 = bf16[199,256]{1,0:T(8,128)(2,1)S(1)} collective-permute-done((bf16[199,256]{1,0:T(8,128)(2,1)S(1)}, bf16[199,256]{1,0:T(8,128)(2,1)S(1)}, u32[]{:S(2)}, u32[]{:S(2)}) %collective-permute-start.12) | collective-permute-done | bytes 101920 | tf_op jit(solution)/shard_map/ppermute | solution.py:171
  66.8 3.3 %fusion.114 = (bf16[1,1,3,256,256]{4,3,2,1,0:T(8,128)(2,1)S(1)}, bf16[1,1,3,256,256]{4,3,2,1,0:T(8,128)(2,1)S(1)}, bf16[1,1,3,256,256]{4,3,2,1,0:T(8,128)(2,1)S(...) fusion(bf16[3,3,3,256,256]{4,3,2,1,0:T(8,128)(2,1)} %param.19), kind=kLoop, calls=%fused_computation.274 | loop fusion | bytes 7077888 | tf_op jit(solution)/shard_map/slice | solution.py:154
  70.1 0.7 pad_maximum_fusion.14
  71.6 1.1 %maximum_select_fusion.1 = bf16[2,6,66,256]{3,2,1,0:T(8,128)(2,1)S(1)} fusion(bf16[2,6,66,256]{3,2,1,0:T(8,128)(2,1)S(1)} %reshape.788, bf16[1,6,66,256]{3,2,1,0:T(8,128)(2,1)} %pad_maximum_fusion.14, pred[]{:T(512)S(6)} %eq.35), kind=kLoop, calls=%fused_computation.58 | loop fusion | flops 405504 | bytes 1013761 | tf_op jit(solution)/shard_map/jit(_where)/select_n | solution.py:252
  72.7 1.7 %select_convert_fusion = bf16[5,6,66,256]{3,2,1,0:T(8,128)(2,1)S(1)} fusion(bf16[3,1,66,256]{3,2,1,0:T(8,128)(2,1)S(1)} %select_n.191, bf16[3,4,1,256]{3,2,1,0:T(2,128)(2,1)S(1)} %reshape.801, bf16[3,4,64,256]{3,2,1,0:T(8,128)(2,1)S(1)} %bitcast.157, bf16[3,1,66,256]{3,2,1,0:T(8,128)(2,1)S(1)} %select_n.189, ...), kind=kLoop, calls=%fused_computation.2 | loop fusion | flops 11151360 | bytes 2025868 | tf_op jit(solution)/shard_map/convert_element_type | solution.py:276
  74.4 0.7 fusion.118
  75.4 1.6 %fusion.116 = (bf16[3,4,64,768]{3,2,1,0:T(8,128)(2,1)S(1)}, bf16[3,4,64,768]{3,2,1,0:T(8,128)(2,1)S(1)}, bf16[3,4,64,768]{3,2,1,0:T(8,128)(2,1)S(1)}, bf16[3,4,6...) fusion(bf16[5,6,64,768]{3,2,1,0:T(8,128)(2,1)S(1)} %pad_maximum, ...), kind=kLoop, calls=%fused_computation.276 | loop fusion | bytes 21233664 | tf_op jit(solution)/shard_map/slice | solution.py:151
  77.5 0.5 copy-done.4
  78.5 0.5 copy-done.2
  79.5 0.5 copy-done.1
  80.5 0.5 copy-done
  82.0 0.5 convolution_add_fusion.2
  82.5 0.5 convolution_add_fusion.1
  83.4 0.8 %add_convert_fusion = bf16[3,4,64,256]{3,2,1,0:T(8,128)(2,1)} fusion(f32[3,4,64,256]{3,2,1,0:T(8,128)S(1)} %bitcast.175, bf16[3,4,64,256]{3,2,1,0:T(8,128)(2,1)S(1)} %bitcast.152), kind=kLoop, calls=%fused_computation.37 | loop fusion | flops 589824 | bytes 1572864 | tf_op jit(solution)/shard_map/convert_element_type | solution.py:303
  (234 shorter events, 18.4 us)
Async XLA Ops:
  1.4 2.4 %collective-permute-start = (f32[2,32]{1,0:T(2,128)S(1)}, f32[2,32]{1,0:T(2,128)S(1)}, u32[]{:S(2)}, u32[]{:S(2)}) collective-permute-start(f32[2,32]{1,0:T(2,128)S(1)} %pad_maximum_fusion.30), channel_id=1, source_target_pairs={{0,1},{1,0},{2,3},{3,2},{4,5},{5,4},{6,7},{7,6},{8,9},{9,8},{10,11... | collective-permute-start | bytes 776 | tf_op jit(solution)/shard_map/ppermute | solution.py:171
  1.9 1.8 %copy-start.8 = (bf16[3,2,32,512]{3,2,1,0:T(8,128)(2,1)S(1)}, bf16[3,2,32,512]{3,2,1,0:T(8,128)(2,1)}, u32[]{:S(2)}) copy-start(bf16[3,2,32,512]{3,2,1,0:T(8,128)(2,1)} %param.10) | copy-start | bytes 589828
  3.6 15.3 %copy-start.10 = (f32[512]{0:T(512)S(1)}, f32[512]{0:T(512)}, u32[]{:S(2)}) copy-start(f32[512]{0:T(512)} %param.12) | copy-start | bytes 6148
  3.6 15.3 %copy-start.11 = (f32[512]{0:T(512)S(1)}, f32[512]{0:T(512)}, u32[]{:S(2)}) copy-start(f32[512]{0:T(512)} %param.11) | copy-start | bytes 6148
  4.2 4.2 %collective-permute-start.1 = (bf16[7,512]{1,0:T(8,128)(2,1)S(1)}, bf16[7,512]{1,0:T(8,128)(2,1)S(1)}, u32[]{:S(2)}, u32[]{:S(2)}) collective-permute-start(bf16[7,512]{1,0:T(8,128)(2,1)S(1)} %pad_maximum_fusion.27), channel_id=1, source_target_pairs={{0,2},{2,0},{1,3},{3,1},{4,6},{6,4},{5,7},{7,5},{8,10},{10,8},{9,1... | collective-permute-start | bytes 21512 | tf_op jit(solution)/shard_map/ppermute | solution.py:171
  9.1 5.0 %collective-permute-start.2 = (bf16[100,512]{1,0:T(8,128)(2,1)S(1)}, bf16[100,512]{1,0:T(8,128)(2,1)S(1)}, u32[]{:S(2)}, u32[]{:S(2)}) collective-permute-start(bf16[100,512]{1,0:T(8,128)(2,1)S(1)} %pad_maximum_fusion.26), channel_id=1, source_target_pairs={{0,4},{4,0},{8,12},{12,8},{1,5},{5,1},{9,13},{13,9},{2,6},{6,2},{1... | collective-permute-start | bytes 307208 | tf_op jit(solution)/shard_map/ppermute | solution.py:171
  11.3 7.0 %collective-permute-start.3 = (bf16[100,512]{1,0:T(8,128)(2,1)S(1)}, bf16[100,512]{1,0:T(8,128)(2,1)S(1)}, u32[]{:S(2)}, u32[]{:S(2)}) collective-permute-start(bf16[100,512]{1,0:T(8,128)(2,1)S(1)} %pad_maximum_fusion.26), channel_id=1, source_target_pairs={{0,12},{4,8},{8,4},{12,0},{1,13},{5,9},{9,5},{13,1},{2,14},{6,10},... | collective-permute-start | bytes 307208 | tf_op jit(solution)/shard_map/ppermute | solution.py:171
  13.7 4.8 %collective-permute-start.4 = (f32[2,32]{1,0:T(2,128)S(1)}, f32[2,32]{1,0:T(2,128)S(1)}, u32[]{:S(2)}, u32[]{:S(2)}) collective-permute-start(f32[2,32]{1,0:T(2,128)S(1)} %get-tuple-element.27), channel_id=1, source_target_pairs={{0,8},{4,12},{8,0},{12,4},{1,9},{5,13},{9,1},{13,5},{2,10},{6,14},... | collective-permute-start | bytes 776 | tf_op jit(solution)/shard_map/ppermute | solution.py:171
  24.1 3.7 %collective-permute-start.5 = (bf16[13,256]{1,0:T(8,128)(2,1)S(1)}, bf16[13,256]{1,0:T(8,128)(2,1)S(1)}, u32[]{:S(2)}, u32[]{:S(2)}) collective-permute-start(bf16[13,256]{1,0:T(8,128)(2,1)S(1)} %pad_maximum_fusion.28), channel_id=1, source_target_pairs={{0,2},{2,0},{1,3},{3,1},{4,6},{6,4},{5,7},{7,5},{8,10},{10,8},{9,1... | collective-permute-start | bytes 19976 | tf_op jit(solution)/shard_map/ppermute | solution.py:171
  28.6 4.7 %collective-permute-start.6 = (bf16[199,256]{1,0:T(8,128)(2,1)S(1)}, bf16[199,256]{1,0:T(8,128)(2,1)S(1)}, u32[]{:S(2)}, u32[]{:S(2)}) collective-permute-start(bf16[199,256]{1,0:T(8,128)(2,1)S(1)} %get-tuple-element.99), channel_id=1, source_target_pairs={{0,4},{4,0},{8,12},{12,8},{1,5},{5,1},{9,13},{13,9},{2,6},{6,2},{1... | collective-permute-start | bytes 305672 | tf_op jit(solution)/shard_map/ppermute | solution.py:171
  29.3 6.6 %collective-permute-start.7 = (bf16[199,256]{1,0:T(8,128)(2,1)S(1)}, bf16[199,256]{1,0:T(8,128)(2,1)S(1)}, u32[]{:S(2)}, u32[]{:S(2)}) collective-permute-start(bf16[199,256]{1,0:T(8,128)(2,1)S(1)} %get-tuple-element.100), channel_id=1, source_target_pairs={{0,12},{4,8},{8,4},{12,0},{1,13},{5,9},{9,5},{13,1},{2,14},{6,10},... | collective-permute-start | bytes 305672 | tf_op jit(solution)/shard_map/ppermute | solution.py:171
  32.2 4.5 %collective-permute-start.8 = (f32[2,32]{1,0:T(2,128)S(1)}, f32[2,32]{1,0:T(2,128)S(1)}, u32[]{:S(2)}, u32[]{:S(2)}) collective-permute-start(f32[2,32]{1,0:T(2,128)S(1)} %get-tuple-element.24), channel_id=1, source_target_pairs={{0,8},{4,12},{8,0},{12,4},{1,9},{5,13},{9,1},{13,5},{2,10},{6,14},... | collective-permute-start | bytes 776 | tf_op jit(solution)/shard_map/ppermute | solution.py:171
  37.0 4.0 %collective-permute-start.9 = (bf16[793,256]{1,0:T(8,128)(2,1)S(1)}, bf16[793,256]{1,0:T(8,128)(2,1)S(1)}, u32[]{:S(2)}, u32[]{:S(2)}) collective-permute-start(bf16[793,256]{1,0:T(8,128)(2,1)S(1)} %pad_maximum_fusion.10), channel_id=1, source_target_pairs={{0,1},{1,0},{2,3},{3,2},{4,5},{5,4},{6,7},{7,6},{8,9},{9,8},{10,11... | collective-permute-start | bytes 1218056 | tf_op jit(solution)/shard_map/ppermute | solution.py:171
  41.7 1.3 %copy-start.12 = (f32[256]{0:T(256)S(1)}, f32[256]{0:T(256)}, u32[]{:S(2)}) copy-start(f32[256]{0:T(256)} %param.15) | copy-start | bytes 3076
  41.7 1.3 %copy-start.13 = (f32[256]{0:T(256)S(1)}, f32[256]{0:T(256)}, u32[]{:S(2)}) copy-start(f32[256]{0:T(256)} %param.14) | copy-start | bytes 3076
  45.8 1.4 %copy-start.7 = (bf16[1,1,3,256,256]{4,3,2,1,0:T(8,128)(2,1)S(1)}, bf16[1,1,3,256,256]{4,3,2,1,0:T(8,128)(2,1)}, u32[]{:S(2)}) copy-start(bf16[1,1,3,256,256]{4,3,2,1,0:T(8,128)(2,1)} %get-tuple-element.46) | copy-start | bytes 1179652
  47.2 1.0 %copy-start.6 = (bf16[1,1,3,256,256]{4,3,2,1,0:T(8,128)(2,1)S(1)}, bf16[1,1,3,256,256]{4,3,2,1,0:T(8,128)(2,1)}, u32[]{:S(2)}) copy-start(bf16[1,1,3,256,256]{4,3,2,1,0:T(8,128)(2,1)} %get-tuple-element.45) | copy-start | bytes 1179652
  48.2 1.0 %copy-start.3 = (bf16[1,1,3,256,256]{4,3,2,1,0:T(8,128)(2,1)S(1)}, bf16[1,1,3,256,256]{4,3,2,1,0:T(8,128)(2,1)}, u32[]{:S(2)}) copy-start(bf16[1,1,3,256,256]{4,3,2,1,0:T(8,128)(2,1)} %get-tuple-element.44) | copy-start | bytes 1179652
  51.6 1.0 %copy-start.9 = (bf16[1,1,3,256,256]{4,3,2,1,0:T(8,128)(2,1)S(1)}, bf16[1,1,3,256,256]{4,3,2,1,0:T(8,128)(2,1)}, u32[]{:S(2)}) copy-start(bf16[1,1,3,256,256]{4,3,2,1,0:T(8,128)(2,1)} %get-tuple-element.39) | copy-start | bytes 1179652
  53.9 3.7 %collective-permute-start.10 = (bf16[13,256]{1,0:T(8,128)(2,1)S(1)}, bf16[13,256]{1,0:T(8,128)(2,1)S(1)}, u32[]{:S(2)}, u32[]{:S(2)}) collective-permute-start(bf16[13,256]{1,0:T(8,128)(2,1)S(1)} %pad_maximum_fusion.29), channel_id=1, source_target_pairs={{0,2},{2,0},{1,3},{3,1},{4,6},{6,4},{5,7},{7,5},{8,10},{10,8},{9,1... | collective-permute-start | bytes 19976 | tf_op jit(solution)/shard_map/ppermute | solution.py:171
  58.4 5.8 %collective-permute-start.11 = (bf16[199,256]{1,0:T(8,128)(2,1)S(1)}, bf16[199,256]{1,0:T(8,128)(2,1)S(1)}, u32[]{:S(2)}, u32[]{:S(2)}) collective-permute-start(bf16[199,256]{1,0:T(8,128)(2,1)S(1)} %get-tuple-element.93), channel_id=1, source_target_pairs={{0,4},{4,0},{8,12},{12,8},{1,5},{5,1},{9,13},{13,9},{2,6},{6,2},{1... | collective-permute-start | bytes 305672 | tf_op jit(solution)/shard_map/ppermute | solution.py:171
  58.7 7.0 %collective-permute-start.12 = (bf16[199,256]{1,0:T(8,128)(2,1)S(1)}, bf16[199,256]{1,0:T(8,128)(2,1)S(1)}, u32[]{:S(2)}, u32[]{:S(2)}) collective-permute-start(bf16[199,256]{1,0:T(8,128)(2,1)S(1)} %get-tuple-element.94), channel_id=1, source_target_pairs={{0,12},{4,8},{8,4},{12,0},{1,13},{5,9},{9,5},{13,1},{2,14},{6,10},... | collective-permute-start | bytes 305672 | tf_op jit(solution)/shard_map/ppermute | solution.py:171
  61.1 5.3 %collective-permute-start.13 = (f32[2,32]{1,0:T(2,128)S(1)}, f32[2,32]{1,0:T(2,128)S(1)}, u32[]{:S(2)}, u32[]{:S(2)}) collective-permute-start(f32[2,32]{1,0:T(2,128)S(1)} %get-tuple-element.17), channel_id=1, source_target_pairs={{0,8},{4,12},{8,0},{12,4},{1,9},{5,13},{9,1},{13,5},{2,10},{6,14},... | collective-permute-start | bytes 776 | tf_op jit(solution)/shard_map/ppermute | solution.py:171
  66.8 4.1 %collective-permute-start.14 = (bf16[793,256]{1,0:T(8,128)(2,1)S(1)}, bf16[793,256]{1,0:T(8,128)(2,1)S(1)}, u32[]{:S(2)}, u32[]{:S(2)}) collective-permute-start(bf16[793,256]{1,0:T(8,128)(2,1)S(1)} %pad_maximum_fusion.11), channel_id=1, source_target_pairs={{0,1},{1,0},{2,3},{3,2},{4,5},{5,4},{6,7},{7,6},{8,9},{9,8},{10,11... | collective-permute-start | bytes 1218056 | tf_op jit(solution)/shard_map/ppermute | solution.py:171
  71.4 1.3 %copy-start.14 = (f32[256]{0:T(256)S(1)}, f32[256]{0:T(256)}, u32[]{:S(2)}) copy-start(f32[256]{0:T(256)} %param.18) | copy-start | bytes 3076
  71.4 1.3 %copy-start.15 = (f32[256]{0:T(256)S(1)}, f32[256]{0:T(256)}, u32[]{:S(2)}) copy-start(f32[256]{0:T(256)} %param.17) | copy-start | bytes 3076
  75.4 1.6 %copy-start.5 = (bf16[1,1,3,256,256]{4,3,2,1,0:T(8,128)(2,1)S(1)}, bf16[1,1,3,256,256]{4,3,2,1,0:T(8,128)(2,1)}, u32[]{:S(2)}) copy-start(bf16[1,1,3,256,256]{4,3,2,1,0:T(8,128)(2,1)} %get-tuple-element.37) | copy-start | bytes 1179652
  77.0 1.0 %copy-start.4 = (bf16[1,1,3,256,256]{4,3,2,1,0:T(8,128)(2,1)S(1)}, bf16[1,1,3,256,256]{4,3,2,1,0:T(8,128)(2,1)}, u32[]{:S(2)}) copy-start(bf16[1,1,3,256,256]{4,3,2,1,0:T(8,128)(2,1)} %get-tuple-element.36) | copy-start | bytes 1179652
  78.0 1.0 %copy-start.2 = (bf16[1,1,3,256,256]{4,3,2,1,0:T(8,128)(2,1)S(1)}, bf16[1,1,3,256,256]{4,3,2,1,0:T(8,128)(2,1)}, u32[]{:S(2)}) copy-start(bf16[1,1,3,256,256]{4,3,2,1,0:T(8,128)(2,1)} %get-tuple-element.35) | copy-start | bytes 1179652
  79.0 1.0 %copy-start.1 = (bf16[1,1,3,256,256]{4,3,2,1,0:T(8,128)(2,1)S(1)}, bf16[1,1,3,256,256]{4,3,2,1,0:T(8,128)(2,1)}, u32[]{:S(2)}) copy-start(bf16[1,1,3,256,256]{4,3,2,1,0:T(8,128)(2,1)} %get-tuple-element.34) | copy-start | bytes 1179652
  80.0 1.0 %copy-start = (bf16[1,1,3,256,256]{4,3,2,1,0:T(8,128)(2,1)S(1)}, bf16[1,1,3,256,256]{4,3,2,1,0:T(8,128)(2,1)}, u32[]{:S(2)}) copy-start(bf16[1,1,3,256,256]{4,3,2,1,0:T(8,128)(2,1)} %get-tuple-element.33) | copy-start | bytes 1179652

commit v16 on v10

--- a/solution.py
+++ b/solution.py
@@ -84,7 +84,7 @@
 def activate(values, stats, scale_vec, shift_vec):
     average, scaling = stats
     normed = (values - average) * scaling * scale_vec + shift_vec
-    return jax.nn.silu(normed)
+    return 0.5 * normed * (1.0 + jnp.tanh(0.5 * normed))
 
 
 def inside_mask(rows, cols, low_pad):

time: 77.8 us -> 77.7 us (level)
  no operation moved by 1% of the time
where the time goes in v16:
time: 77.7 us; the launch traced here: 77.3 us
  local copies, waits for them, and re-layouts  20.9 us (27%)
  starting transfers between devices  18.3 us (24%)
  waiting for transfers between devices  17.7 us (23%)
  other arithmetic  11 us (14%)
  matrix products  8.6 us (11%)
  between operations  0.89 us (1%)
    ppermute x15, starting transfers between devices, swap(): return lax.ppermute(x, axis, [(i, i ^ distance) for i in range(size)])  18.3 us
    ppermute x15, waiting for transfers between devices, swap(): return lax.ppermute(x, axis, [(i, i ^ distance) for i in range(size)])  17.7 us
    slice x2, local copies, waits for them, and re-layouts, valid_conv(): kernel[step_t].reshape(9 * channels, -1)  7.42 us
    dot_general x6, matrix products, valid_conv(): jnp.dot(window, kernel[step_t].reshape(9 * channels, -1), preferred_eleme...  6.52 us
    unnamed x39, local copies, waits for them, and re-layouts  3.59 us
    convert_element_type x2, other arithmetic, norm_conv(): jnp.where(inside_mask(height + 2, across + 2, 1), act, 0.0)  3.54 us
    reduce_sum x5, other arithmetic, local_sums(): jnp.sum(grouped, axis=(0, 2))  2.25 us
    slice x2, local copies, waits for them, and re-layouts, valid_conv(): window = wide[step_t:step_t + frames].reshape(-1, 9 * channels)  2.19 us
  transfers between devices with their start and end apart: 15, of which 10 were waited for; matrix products, arithmetic and copies ran while one was open for 14% of the time, Pallas kernels for 0%

profile of v16, /device:TPU:0, one launch (start us, length us, event | category | flops | bytes accessed | tf_op | source)
XLA Modules:
  0.0 77.3 jit_solution(7859686256388778148)
XLA Ops:
  0.0 1.1 %convert_reduce_fusion.2 = (f32[512]{0:T(512)S(1)}, f32[512]{0:T(512)S(1)}) fusion(bf16[3,2,32,512]{3,2,1,0:T(8,128)(2,1)} %param.10), kind=kLoop, calls=%fused_computation.52 | loop fusion | flops 392192 | bytes 200704 | tf_op jit(solution)/shard_map/reduce_sum | solution.py:179
  1.5 0.5 collective-permute-start
  2.0 1.6 %slice_bitcast_fusion.7 = (bf16[512,256]{1,0:T(8,128)(2,1)S(1)}, bf16[512,256]{1,0:T(8,128)(2,1)S(1)}, bf16[512,256]{1,0:T(8,128)(2,1)S(1)}, bf16[512,256]{1,0:T...) fusion(bf16[3,3,512,256]{3,2,1,0:T(8,128)(2,1)} %param.13), kind=kLoop, calls=%fused_computation.77 | loop fusion | bytes 4194304 | tf_op jit(solution)/shard_map/squeeze | solution.py:129
  4.2 2.6 %collective-permute-start.1 = (bf16[7,512]{1,0:T(8,128)(2,1)S(1)}, bf16[7,512]{1,0:T(8,128)(2,1)S(1)}, u32[]{:S(2)}, u32[]{:S(2)}) collective-permute-start(bf16[7,512]{1,0:T(8,128)(2,1)S(1)} %pad_maximum_fusion.25), channel_id=1, source_target_pairs={{0,2},{2,0},{1,3},{3,1},{4,6},{6,4},{5,7},{7,5},{8,10},{10,8},{9,1... | collective-permute-start | bytes 21512 | tf_op jit(solution)/shard_map/ppermute | solution.py:170
  6.9 1.6 %collective-permute-done.1 = bf16[7,512]{1,0:T(8,128)(2,1)S(1)} collective-permute-done((bf16[7,512]{1,0:T(8,128)(2,1)S(1)}, bf16[7,512]{1,0:T(8,128)(2,1)S(1)}, u32[]{:S(2)}, u32[]{:S(2)}) %collective-permute-start.1) | collective-permute-done | bytes 7200 | tf_op jit(solution)/shard_map/ppermute | solution.py:170
  9.1 2.2 %collective-permute-start.2 = (bf16[100,512]{1,0:T(8,128)(2,1)S(1)}, bf16[100,512]{1,0:T(8,128)(2,1)S(1)}, u32[]{:S(2)}, u32[]{:S(2)}) collective-permute-start(bf16[100,512]{1,0:T(8,128)(2,1)S(1)} %pad_maximum_fusion.24), channel_id=1, source_target_pairs={{0,4},{4,0},{8,12},{12,8},{1,5},{5,1},{9,13},{13,9},{2,6},{6,2},{1... | collective-permute-start | bytes 307208 | tf_op jit(solution)/shard_map/ppermute | solution.py:170
  11.3 2.5 %collective-permute-start.3 = (bf16[100,512]{1,0:T(8,128)(2,1)S(1)}, bf16[100,512]{1,0:T(8,128)(2,1)S(1)}, u32[]{:S(2)}, u32[]{:S(2)}) collective-permute-start(bf16[100,512]{1,0:T(8,128)(2,1)S(1)} %pad_maximum_fusion.24), channel_id=1, source_target_pairs={{0,12},{4,8},{8,4},{12,0},{1,13},{5,9},{9,5},{13,1},{2,14},{6,10},... | collective-permute-start | bytes 307208 | tf_op jit(solution)/shard_map/ppermute | solution.py:170
  14.3 4.1 %collective-permute-done.3 = bf16[100,512]{1,0:T(8,128)(2,1)S(1)} collective-permute-done((bf16[100,512]{1,0:T(8,128)(2,1)S(1)}, bf16[100,512]{1,0:T(8,128)(2,1)S(1)}, u32[]{:S(2)}, u32[]{:S(2)}) %collective-permute-start.3) | collective-permute-done | bytes 102432 | tf_op jit(solution)/shard_map/ppermute | solution.py:170
  19.0 0.3 select_convert_fusion.2
  19.4 0.3 fusion.11
  19.7 0.3 fusion.15
  19.9 0.4 fusion.1
  20.7 1.2 %convolution_add_fusion.4 = bf16[192,256]{1,0:T(8,128)(2,1)S(1)} fusion(bf16[192,512]{1,0:T(8,128)(2,1)S(1)} %bitcast.122, bf16[3,3,512,256]{3,2,1,0:T(8,128)(2,1)} %param.13, f32[192,512]{1,0:T(8,128)S(1)} %fusion.15, f32[192,512]{1,0:T(8,128)S(1)} %fusion.11, f32[192,1024]{1,0:T(8,128)S(1)} %fusion.1), kind=kOutput, calls=%fused_computation.7 | convolution fusion | flops 50528256 | bytes 1146880 | tf_op jit(solution)/shard_map/dot_general | solution.py:123
  22.0 0.3 pad_maximum_fusion.10
  22.3 0.3 pad_maximum_fusion.11
  22.6 0.8 %convert_reduce_fusion.1 = (f32[256]{0:T(256)S(1)}, f32[256]{0:T(256)S(1)}, bf16[3,2,2,64,256]{4,1,3,0,2:T(2,128)(2,1)S(1)}) fusion(bf16[3,2,1,64,256]{4,1,3,0,2:T(2,128)(2,1)S(1)} %bitcast.125, bf16[3,2,1,64,256]{4,1,3,0,2:T(2,128)(2,1)S(1)} %bitcast.124), kind=kLoop, calls=%fused_computation.19 | loop fusion | flops 982528 | bytes 788480 | tf_op jit(solution)/shard_map/reduce_sum | solution.py:179
  24.1 1.6 %collective-permute-start.5 = (bf16[13,256]{1,0:T(8,128)(2,1)S(1)}, bf16[13,256]{1,0:T(8,128)(2,1)S(1)}, u32[]{:S(2)}, u32[]{:S(2)}) collective-permute-start(bf16[13,256]{1,0:T(8,128)(2,1)S(1)} %pad_maximum_fusion.26), channel_id=1, source_target_pairs={{0,2},{2,0},{1,3},{3,1},{4,6},{6,4},{5,7},{7,5},{8,10},{10,8},{9,1... | collective-permute-start | bytes 19976 | tf_op jit(solution)/shard_map/ppermute | solution.py:170
  25.7 2.2 %collective-permute-done.5 = bf16[13,256]{1,0:T(8,128)(2,1)S(1)} collective-permute-done((bf16[13,256]{1,0:T(8,128)(2,1)S(1)}, bf16[13,256]{1,0:T(8,128)(2,1)S(1)}, u32[]{:S(2)}, u32[]{:S(2)}) %collective-permute-start.5) | collective-permute-done | bytes 6688 | tf_op jit(solution)/shard_map/ppermute | solution.py:170
  28.6 0.7 collective-permute-start.6
  29.3 2.8 %collective-permute-start.7 = (bf16[199,256]{1,0:T(8,128)(2,1)S(1)}, bf16[199,256]{1,0:T(8,128)(2,1)S(1)}, u32[]{:S(2)}, u32[]{:S(2)}) collective-permute-start(bf16[199,256]{1,0:T(8,128)(2,1)S(1)} %get-tuple-element.70), channel_id=1, source_target_pairs={{0,12},{4,8},{8,4},{12,0},{1,13},{5,9},{9,5},{13,1},{2,14},{6,10},... | collective-permute-start | bytes 305672 | tf_op jit(solution)/shard_map/ppermute | solution.py:170
  32.3 1.1 %collective-permute-done.6 = bf16[199,256]{1,0:T(8,128)(2,1)S(1)} collective-permute-done((bf16[199,256]{1,0:T(8,128)(2,1)S(1)}, bf16[199,256]{1,0:T(8,128)(2,1)S(1)}, u32[]{:S(2)}, u32[]{:S(2)}) %collective-permute-start.6) | collective-permute-done | bytes 101920 | tf_op jit(solution)/shard_map/ppermute | solution.py:170
  33.4 2.6 %collective-permute-done.7 = bf16[199,256]{1,0:T(8,128)(2,1)S(1)} collective-permute-done((bf16[199,256]{1,0:T(8,128)(2,1)S(1)}, bf16[199,256]{1,0:T(8,128)(2,1)S(1)}, u32[]{:S(2)}, u32[]{:S(2)}) %collective-permute-start.7) | collective-permute-done | bytes 101920 | tf_op jit(solution)/shard_map/ppermute | solution.py:170
  37.1 3.7 %fusion.117 = (bf16[1,3,3,256,256]{4,3,2,1,0:T(8,128)(2,1)S(1)}, bf16[1,3,3,256,256]{4,3,2,1,0:T(8,128)(2,1)}, bf16[1,3,3,256,256]{4,3,2,1,0:T(8,128)(2,1)}) fusion(bf16[3,3,3,256,256]{4,3,2,1,0:T(8,128)(2,1)} %param.16), kind=kLoop, calls=%fused_computation.281 | loop fusion | bytes 7077888 | tf_op jit(solution)/shard_map/slice | solution.py:154
  41.7 1.9 %select_convert_fusion.1 = bf16[5,6,66,256]{3,2,1,0:T(8,128)(2,1)S(1)} fusion(bf16[3,1,66,256]{3,2,1,0:T(8,128)(2,1)S(1)} %select_n.182, bf16[3,4,1,256]{3,2,1,0:T(2,128)(2,1)S(1)} %reshape.752, bf16[3,4,64,256]{3,2,1,0:T(8,128)(2,1)S(1)} %bitcast.103, bf16[3,1,66,256]{3,2,1,0:T(8,128)(2,1)S(1)} %select_n.179, ...), kind=kLoop, calls=%fused_computation.1 | loop fusion | flops 10644480 | bytes 2025868 | tf_op jit(solution)/shard_map/convert_element_type | solution.py:275
  43.6 0.2 slice_dynamic-update-slice_fusion.16
  43.9 0.2 slice_dynamic-update-slice_fusion.15
  44.2 0.2 slice_dynamic-update-slice_fusion.13
  45.3 1.0 %fusion.115 = (bf16[3,4,64,2304]{3,2,1,0:T(8,128)(2,1)S(1)}, bf16[3,4,64,2304]{3,2,1,0:T(8,128)(2,1)S(1)}, bf16[3,4,64,2304]{3,2,1,0:T(8,128)(2,1)S(1)}) fusion(bf16[5,4,64,2304]{3,2,1,0:T(8,128)(2,1)S(1)} %slice_dynamic-update-slice_fusion.9), kind=kLoop, calls=%fused_computation.279 | loop fusion | bytes 21233664 | tf_op jit(solution)/shard_map/slice | solution.py:152
  46.3 0.3 copy-done.3
  46.6 1.1 %fusion.120 = f32[768,256]{1,0:T(8,128)S(1)} fusion(bf16[768,2304]{1,0:T(8,128)(2,1)S(1)} %bitcast.114, bf16[2304,256]{1,0:T(8,128)(2,1)S(1)} %bitcast.121), kind=kOutput, calls=%fused_computation.284 | convolution fusion | flops 905969664 | bytes 5505024 | tf_op jit(solution)/shard_map/dot_general | solution.py:153
  47.8 1.1 %convolution_add_fusion.3 = f32[768,256]{1,0:T(8,128)S(1)} fusion(f32[768,256]{1,0:T(8,128)S(1)} %fusion.120, bf16[768,2304]{1,0:T(8,128)(2,1)S(1)} %bitcast.112, bf16[2304,256]{1,0:T(8,128)(2,1)S(1)} %bitcast.120), kind=kOutput, calls=%fused_computation.5 | convolution fusion | flops 906166272 | bytes 6291456 | tf_op jit(solution)/shard_map/dot_general | solution.py:153
  48.9 1.1 %convert_reduce_fusion = (f32[256]{0:T(256)S(1)}, f32[256]{0:T(256)S(1)}, bf16[768,256]{1,0:T(8,128)(2,1)S(1)}) fusion(f32[768,256]{1,0:T(8,128)S(1)} %convolution_add_fusion.3, bf16[768,2304]{1,0:T(8,128)(2,1)S(1)} %bitcast.110, bf16[2304,256]{1,0:T(8,128)(2,1)S(1)} %bitcast.116), kind=kOutput, calls=%fused_computation.17 | convolution fusion | flops 907148800 | bytes 5900288 | tf_op jit(solution)/shard_map/dot_general | solution.py:153
  50.8 1.6 %collective-permute-start.10 = (bf16[13,256]{1,0:T(8,128)(2,1)S(1)}, bf16[13,256]{1,0:T(8,128)(2,1)S(1)}, u32[]{:S(2)}, u32[]{:S(2)}) collective-permute-start(bf16[13,256]{1,0:T(8,128)(2,1)S(1)} %pad_maximum_fusion.27), channel_id=1, source_target_pairs={{0,2},{2,0},{1,3},{3,1},{4,6},{6,4},{5,7},{7,5},{8,10},{10,8},{9,1... | collective-permute-start | bytes 19976 | tf_op jit(solution)/shard_map/ppermute | solution.py:170
  52.3 2.2 %collective-permute-done.10 = bf16[13,256]{1,0:T(8,128)(2,1)S(1)} collective-permute-done((bf16[13,256]{1,0:T(8,128)(2,1)S(1)}, bf16[13,256]{1,0:T(8,128)(2,1)S(1)}, u32[]{:S(2)}, u32[]{:S(2)}) %collective-permute-start.10) | collective-permute-done | bytes 6688 | tf_op jit(solution)/shard_map/ppermute | solution.py:170
  55.3 0.4 collective-permute-start.11
  55.6 2.4 %collective-permute-start.12 = (bf16[199,256]{1,0:T(8,128)(2,1)S(1)}, bf16[199,256]{1,0:T(8,128)(2,1)S(1)}, u32[]{:S(2)}, u32[]{:S(2)}) collective-permute-start(bf16[199,256]{1,0:T(8,128)(2,1)S(1)} %get-tuple-element.64), channel_id=1, source_target_pairs={{0,12},{4,8},{8,4},{12,0},{1,13},{5,9},{9,5},{13,1},{2,14},{6,10},... | collective-permute-start | bytes 305672 | tf_op jit(solution)/shard_map/ppermute | solution.py:170
  58.0 0.8 %collective-permute-start.13 = (f32[2,32]{1,0:T(2,128)S(1)}, f32[2,32]{1,0:T(2,128)S(1)}, u32[]{:S(2)}, u32[]{:S(2)}) collective-permute-start(f32[2,32]{1,0:T(2,128)S(1)} %get-tuple-element.17), channel_id=1, source_target_pairs={{0,8},{4,12},{8,0},{12,4},{1,9},{5,13},{9,1},{13,5},{2,10},{6,14},... | collective-permute-start | bytes 776 | tf_op jit(solution)/shard_map/ppermute | solution.py:170
  58.8 2.2 %collective-permute-done.11 = bf16[199,256]{1,0:T(8,128)(2,1)S(1)} collective-permute-done((bf16[199,256]{1,0:T(8,128)(2,1)S(1)}, bf16[199,256]{1,0:T(8,128)(2,1)S(1)}, u32[]{:S(2)}, u32[]{:S(2)}) %collective-permute-start.11) | collective-permute-done | bytes 101920 | tf_op jit(solution)/shard_map/ppermute | solution.py:170
  61.0 1.5 %collective-permute-done.12 = bf16[199,256]{1,0:T(8,128)(2,1)S(1)} collective-permute-done((bf16[199,256]{1,0:T(8,128)(2,1)S(1)}, bf16[199,256]{1,0:T(8,128)(2,1)S(1)}, u32[]{:S(2)}, u32[]{:S(2)}) %collective-permute-start.12) | collective-permute-done | bytes 101920 | tf_op jit(solution)/shard_map/ppermute | solution.py:170
  63.8 3.7 %fusion.116 = (bf16[1,3,3,256,256]{4,3,2,1,0:T(8,128)(2,1)S(1)}, bf16[1,3,3,256,256]{4,3,2,1,0:T(8,128)(2,1)}, bf16[1,3,3,256,256]{4,3,2,1,0:T(8,128)(2,1)}) fusion(bf16[3,3,3,256,256]{4,3,2,1,0:T(8,128)(2,1)} %param.19), kind=kLoop, calls=%fused_computation.280 | loop fusion | bytes 7077888 | tf_op jit(solution)/shard_map/slice | solution.py:154
  68.3 1.7 %select_convert_fusion = bf16[5,6,66,256]{3,2,1,0:T(8,128)(2,1)S(1)} fusion(bf16[3,1,66,256]{3,2,1,0:T(8,128)(2,1)S(1)} %select_n.191, bf16[3,4,1,256]{3,2,1,0:T(2,128)(2,1)S(1)} %reshape.753, bf16[3,4,64,256]{3,2,1,0:T(8,128)(2,1)S(1)} %bitcast.109, bf16[3,1,66,256]{3,2,1,0:T(8,128)(2,1)S(1)} %select_n.189, ...), kind=kLoop, calls=%fused_computation | loop fusion | flops 10644480 | bytes 2025868 | tf_op jit(solution)/shard_map/convert_element_type | solution.py:275
  70.1 0.2 slice_dynamic-update-slice_fusion.7
  70.3 0.2 slice_dynamic-update-slice_fusion.6
  71.7 1.2 %fusion.114 = (bf16[3,4,64,2304]{3,2,1,0:T(8,128)(2,1)S(1)}, bf16[3,4,64,2304]{3,2,1,0:T(8,128)(2,1)S(1)}, bf16[3,4,64,2304]{3,2,1,0:T(8,128)(2,1)S(1)}) fusion(bf16[5,4,64,2304]{3,2,1,0:T(8,128)(2,1)S(1)} %slice_dynamic-update-slice_fusion), kind=kLoop, calls=%fused_computation.278 | loop fusion | bytes 21233664 | tf_op jit(solution)/shard_map/slice | solution.py:152
  73.0 1.1 %fusion.121 = f32[768,256]{1,0:T(8,128)S(1)} fusion(bf16[768,2304]{1,0:T(8,128)(2,1)S(1)} %bitcast.115, bf16[2304,256]{1,0:T(8,128)(2,1)S(1)} %bitcast.119), kind=kOutput, calls=%fused_computation.285 | convolution fusion | flops 905969664 | bytes 5505024 | tf_op jit(solution)/shard_map/dot_general | solution.py:153
  74.3 1.1 %convolution_add_fusion.1 = f32[768,256]{1,0:T(8,128)S(1)} fusion(f32[768,256]{1,0:T(8,128)S(1)} %fusion.121, bf16[768,2304]{1,0:T(8,128)(2,1)S(1)} %bitcast.113, bf16[2304,256]{1,0:T(8,128)(2,1)S(1)} %bitcast.118), kind=kOutput, calls=%fused_computation.3 | convolution fusion | flops 906166272 | bytes 6291456 | tf_op jit(solution)/shard_map/dot_general | solution.py:153
  75.4 1.1 %convolution_add_fusion = f32[768,256]{1,0:T(8,128)S(1)} fusion(f32[768,256]{1,0:T(8,128)S(1)} %convolution_add_fusion.1, bf16[768,2304]{1,0:T(8,128)(2,1)S(1)} %bitcast.111, bf16[2304,256]{1,0:T(8,128)(2,1)S(1)} %bitcast.117), kind=kOutput, calls=%fused_computation.2 | convolution fusion | flops 906166272 | bytes 6291456 | tf_op jit(solution)/shard_map/dot_general | solution.py:153
  76.5 0.9 %add_convert_fusion = bf16[3,4,64,256]{3,2,1,0:T(8,128)(2,1)} fusion(f32[3,4,64,256]{3,2,1,0:T(8,128)S(1)} %bitcast.123, bf16[3,4,64,256]{3,2,1,0:T(8,128)(2,1)S(1)} %bitcast.104), kind=kLoop, calls=%fused_computation.23 | loop fusion | flops 589824 | bytes 1572864 | tf_op jit(solution)/shard_map/convert_element_type | solution.py:302
  (226 shorter events, 12.7 us)
Async XLA Ops:
  0.0 3.8 %copy-start.4 = (bf16[3,2,32,512]{3,2,1,0:T(8,128)(2,1)S(1)}, bf16[3,2,32,512]{3,2,1,0:T(8,128)(2,1)}, u32[]{:S(2)}) copy-start(bf16[3,2,32,512]{3,2,1,0:T(8,128)(2,1)} %param.10) | copy-start | bytes 589828
  1.5 2.3 %collective-permute-start = (f32[2,32]{1,0:T(2,128)S(1)}, f32[2,32]{1,0:T(2,128)S(1)}, u32[]{:S(2)}, u32[]{:S(2)}) collective-permute-start(f32[2,32]{1,0:T(2,128)S(1)} %pad_maximum_fusion.28), channel_id=1, source_target_pairs={{0,1},{1,0},{2,3},{3,2},{4,5},{5,4},{6,7},{7,6},{8,9},{9,8},{10,11... | collective-permute-start | bytes 776 | tf_op jit(solution)/shard_map/ppermute | solution.py:170
  2.0 17.0 %copy-start.5 = (f32[512]{0:T(512)S(1)}, f32[512]{0:T(512)}, u32[]{:S(2)}) copy-start(f32[512]{0:T(512)} %param.12) | copy-start | bytes 6148
  2.0 17.0 %copy-start.6 = (f32[512]{0:T(512)S(1)}, f32[512]{0:T(512)}, u32[]{:S(2)}) copy-start(f32[512]{0:T(512)} %param.11) | copy-start | bytes 6148
  4.2 4.2 %collective-permute-start.1 = (bf16[7,512]{1,0:T(8,128)(2,1)S(1)}, bf16[7,512]{1,0:T(8,128)(2,1)S(1)}, u32[]{:S(2)}, u32[]{:S(2)}) collective-permute-start(bf16[7,512]{1,0:T(8,128)(2,1)S(1)} %pad_maximum_fusion.25), channel_id=1, source_target_pairs={{0,2},{2,0},{1,3},{3,1},{4,6},{6,4},{5,7},{7,5},{8,10},{10,8},{9,1... | collective-permute-start | bytes 21512 | tf_op jit(solution)/shard_map/ppermute | solution.py:170
  9.1 5.0 %collective-permute-start.2 = (bf16[100,512]{1,0:T(8,128)(2,1)S(1)}, bf16[100,512]{1,0:T(8,128)(2,1)S(1)}, u32[]{:S(2)}, u32[]{:S(2)}) collective-permute-start(bf16[100,512]{1,0:T(8,128)(2,1)S(1)} %pad_maximum_fusion.24), channel_id=1, source_target_pairs={{0,4},{4,0},{8,12},{12,8},{1,5},{5,1},{9,13},{13,9},{2,6},{6,2},{1... | collective-permute-start | bytes 307208 | tf_op jit(solution)/shard_map/ppermute | solution.py:170
  11.3 7.0 %collective-permute-start.3 = (bf16[100,512]{1,0:T(8,128)(2,1)S(1)}, bf16[100,512]{1,0:T(8,128)(2,1)S(1)}, u32[]{:S(2)}, u32[]{:S(2)}) collective-permute-start(bf16[100,512]{1,0:T(8,128)(2,1)S(1)} %pad_maximum_fusion.24), channel_id=1, source_target_pairs={{0,12},{4,8},{8,4},{12,0},{1,13},{5,9},{9,5},{13,1},{2,14},{6,10},... | collective-permute-start | bytes 307208 | tf_op jit(solution)/shard_map/ppermute | solution.py:170
  13.8 4.8 %collective-permute-start.4 = (f32[2,32]{1,0:T(2,128)S(1)}, f32[2,32]{1,0:T(2,128)S(1)}, u32[]{:S(2)}, u32[]{:S(2)}) collective-permute-start(f32[2,32]{1,0:T(2,128)S(1)} %get-tuple-element.27), channel_id=1, source_target_pairs={{0,8},{4,12},{8,0},{12,4},{1,9},{5,13},{9,1},{13,5},{2,10},{6,14},... | collective-permute-start | bytes 776 | tf_op jit(solution)/shard_map/ppermute | solution.py:170
  24.1 3.7 %collective-permute-start.5 = (bf16[13,256]{1,0:T(8,128)(2,1)S(1)}, bf16[13,256]{1,0:T(8,128)(2,1)S(1)}, u32[]{:S(2)}, u32[]{:S(2)}) collective-permute-start(bf16[13,256]{1,0:T(8,128)(2,1)S(1)} %pad_maximum_fusion.26), channel_id=1, source_target_pairs={{0,2},{2,0},{1,3},{3,1},{4,6},{6,4},{5,7},{7,5},{8,10},{10,8},{9,1... | collective-permute-start | bytes 19976 | tf_op jit(solution)/shard_map/ppermute | solution.py:170
  28.6 4.7 %collective-permute-start.6 = (bf16[199,256]{1,0:T(8,128)(2,1)S(1)}, bf16[199,256]{1,0:T(8,128)(2,1)S(1)}, u32[]{:S(2)}, u32[]{:S(2)}) collective-permute-start(bf16[199,256]{1,0:T(8,128)(2,1)S(1)} %get-tuple-element.69), channel_id=1, source_target_pairs={{0,4},{4,0},{8,12},{12,8},{1,5},{5,1},{9,13},{13,9},{2,6},{6,2},{1... | collective-permute-start | bytes 305672 | tf_op jit(solution)/shard_map/ppermute | solution.py:170
  29.3 6.6 %collective-permute-start.7 = (bf16[199,256]{1,0:T(8,128)(2,1)S(1)}, bf16[199,256]{1,0:T(8,128)(2,1)S(1)}, u32[]{:S(2)}, u32[]{:S(2)}) collective-permute-start(bf16[199,256]{1,0:T(8,128)(2,1)S(1)} %get-tuple-element.70), channel_id=1, source_target_pairs={{0,12},{4,8},{8,4},{12,0},{1,13},{5,9},{9,5},{13,1},{2,14},{6,10},... | collective-permute-start | bytes 305672 | tf_op jit(solution)/shard_map/ppermute | solution.py:170
  32.2 4.5 %collective-permute-start.8 = (f32[2,32]{1,0:T(2,128)S(1)}, f32[2,32]{1,0:T(2,128)S(1)}, u32[]{:S(2)}, u32[]{:S(2)}) collective-permute-start(f32[2,32]{1,0:T(2,128)S(1)} %get-tuple-element.24), channel_id=1, source_target_pairs={{0,8},{4,12},{8,0},{12,4},{1,9},{5,13},{9,1},{13,5},{2,10},{6,14},... | collective-permute-start | bytes 776 | tf_op jit(solution)/shard_map/ppermute | solution.py:170
  37.1 3.8 %collective-permute-start.9 = (bf16[793,256]{1,0:T(8,128)(2,1)S(1)}, bf16[793,256]{1,0:T(8,128)(2,1)S(1)}, u32[]{:S(2)}, u32[]{:S(2)}) collective-permute-start(bf16[793,256]{1,0:T(8,128)(2,1)S(1)} %pad_maximum_fusion.8), channel_id=1, source_target_pairs={{0,1},{1,0},{2,3},{3,2},{4,5},{5,4},{6,7},{7,6},{8,9},{9,8},{10,11... | collective-permute-start | bytes 1218056 | tf_op jit(solution)/shard_map/ppermute | solution.py:170
  40.8 0.8 %copy-start.7 = (f32[256]{0:T(256)S(1)}, f32[256]{0:T(256)}, u32[]{:S(2)}) copy-start(f32[256]{0:T(256)} %param.15) | copy-start | bytes 3076
  40.9 0.8 %copy-start.8 = (f32[256]{0:T(256)S(1)}, f32[256]{0:T(256)}, u32[]{:S(2)}) copy-start(f32[256]{0:T(256)} %param.14) | copy-start | bytes 3076
  45.3 1.3 %copy-start.3 = (bf16[1,3,3,256,256]{4,3,2,1,0:T(8,128)(2,1)S(1)}, bf16[1,3,3,256,256]{4,3,2,1,0:T(8,128)(2,1)}, u32[]{:S(2)}) copy-start(bf16[1,3,3,256,256]{4,3,2,1,0:T(8,128)(2,1)} %get-tuple-element.40) | copy-start | bytes 3538948
  46.6 1.3 %copy-start.2 = (bf16[1,3,3,256,256]{4,3,2,1,0:T(8,128)(2,1)S(1)}, bf16[1,3,3,256,256]{4,3,2,1,0:T(8,128)(2,1)}, u32[]{:S(2)}) copy-start(bf16[1,3,3,256,256]{4,3,2,1,0:T(8,128)(2,1)} %get-tuple-element.41) | copy-start | bytes 3538948
  50.8 3.7 %collective-permute-start.10 = (bf16[13,256]{1,0:T(8,128)(2,1)S(1)}, bf16[13,256]{1,0:T(8,128)(2,1)S(1)}, u32[]{:S(2)}, u32[]{:S(2)}) collective-permute-start(bf16[13,256]{1,0:T(8,128)(2,1)S(1)} %pad_maximum_fusion.27), channel_id=1, source_target_pairs={{0,2},{2,0},{1,3},{3,1},{4,6},{6,4},{5,7},{7,5},{8,10},{10,8},{9,1... | collective-permute-start | bytes 19976 | tf_op jit(solution)/shard_map/ppermute | solution.py:170
  55.3 5.8 %collective-permute-start.11 = (bf16[199,256]{1,0:T(8,128)(2,1)S(1)}, bf16[199,256]{1,0:T(8,128)(2,1)S(1)}, u32[]{:S(2)}, u32[]{:S(2)}) collective-permute-start(bf16[199,256]{1,0:T(8,128)(2,1)S(1)} %get-tuple-element.63), channel_id=1, source_target_pairs={{0,4},{4,0},{8,12},{12,8},{1,5},{5,1},{9,13},{13,9},{2,6},{6,2},{1... | collective-permute-start | bytes 305672 | tf_op jit(solution)/shard_map/ppermute | solution.py:170
  55.6 7.0 %collective-permute-start.12 = (bf16[199,256]{1,0:T(8,128)(2,1)S(1)}, bf16[199,256]{1,0:T(8,128)(2,1)S(1)}, u32[]{:S(2)}, u32[]{:S(2)}) collective-permute-start(bf16[199,256]{1,0:T(8,128)(2,1)S(1)} %get-tuple-element.64), channel_id=1, source_target_pairs={{0,12},{4,8},{8,4},{12,0},{1,13},{5,9},{9,5},{13,1},{2,14},{6,10},... | collective-permute-start | bytes 305672 | tf_op jit(solution)/shard_map/ppermute | solution.py:170
  58.0 5.3 %collective-permute-start.13 = (f32[2,32]{1,0:T(2,128)S(1)}, f32[2,32]{1,0:T(2,128)S(1)}, u32[]{:S(2)}, u32[]{:S(2)}) collective-permute-start(f32[2,32]{1,0:T(2,128)S(1)} %get-tuple-element.17), channel_id=1, source_target_pairs={{0,8},{4,12},{8,0},{12,4},{1,9},{5,13},{9,1},{13,5},{2,10},{6,14},... | collective-permute-start | bytes 776 | tf_op jit(solution)/shard_map/ppermute | solution.py:170
  63.7 3.8 %collective-permute-start.14 = (bf16[793,256]{1,0:T(8,128)(2,1)S(1)}, bf16[793,256]{1,0:T(8,128)(2,1)S(1)}, u32[]{:S(2)}, u32[]{:S(2)}) collective-permute-start(bf16[793,256]{1,0:T(8,128)(2,1)S(1)} %pad_maximum_fusion.9), channel_id=1, source_target_pairs={{0,1},{1,0},{2,3},{3,2},{4,5},{5,4},{6,7},{7,6},{8,9},{9,8},{10,11... | collective-permute-start | bytes 1218056 | tf_op jit(solution)/shard_map/ppermute | solution.py:170
  67.5 0.8 %copy-start.9 = (f32[256]{0:T(256)S(1)}, f32[256]{0:T(256)}, u32[]{:S(2)}) copy-start(f32[256]{0:T(256)} %param.18) | copy-start | bytes 3076
  67.5 0.8 %copy-start.10 = (f32[256]{0:T(256)S(1)}, f32[256]{0:T(256)}, u32[]{:S(2)}) copy-start(f32[256]{0:T(256)} %param.17) | copy-start | bytes 3076
  71.7 1.3 %copy-start.1 = (bf16[1,3,3,256,256]{4,3,2,1,0:T(8,128)(2,1)S(1)}, bf16[1,3,3,256,256]{4,3,2,1,0:T(8,128)(2,1)}, u32[]{:S(2)}) copy-start(bf16[1,3,3,256,256]{4,3,2,1,0:T(8,128)(2,1)} %get-tuple-element.37) | copy-start | bytes 3538948
  73.0 1.3 %copy-start = (bf16[1,3,3,256,256]{4,3,2,1,0:T(8,128)(2,1)S(1)}, bf16[1,3,3,256,256]{4,3,2,1,0:T(8,128)(2,1)}, u32[]{:S(2)}) copy-start(bf16[1,3,3,256,256]{4,3,2,1,0:T(8,128)(2,1)} %get-tuple-element.38) | copy-start | bytes 3538948

commit v17 on v10

--- a/solution.py
+++ b/solution.py
@@ -239,12 +239,12 @@
 
 def fast_conv_input(values):
     sums = local_sums(values.astype(jnp.float32))
+    sums, above, below = ha_round(sums, values[:, :1], values[:, -1:])
+    x = jnp.concatenate([above, values, below], axis=1)
     w = lax.axis_index("wa")
-    s_w, beside = swap_with(sums, jnp.where(w == 0, values[:, :, -1:], values[:, :, :1]), "wa", 1)
+    s_w, beside = swap_with(sums, jnp.where(w == 0, x[:, :, -1:], x[:, :, :1]), "wa", 1)
     sums = sums + s_w
-    x = jnp.concatenate([beside, values, beside], axis=2)
-    sums, above, below = ha_round(sums, x[:, :1], x[:, -1:])
-    x = jnp.concatenate([above, x, below], axis=1)
+    x = jnp.concatenate([beside, x, beside], axis=2)
     s_t, earlier = swap_with(sums, x[-2:], "ta", 1)
     sums = sums + s_t
     opening = jnp.concatenate([x[:1], x[:1]], axis=0)
@@ -256,11 +256,11 @@
 def fast_latent_input(values):
     sums = local_sums(values.astype(jnp.float32))
     sums = sums + swap(sums, "ta", 1)
-    s_w, beside = swap_with(sums, values[:, :, :1], "wa", 1)
+    sums, _, below = ha_round(sums, values[:, :1], values[:, :1])
+    x = jnp.concatenate([values, below], axis=1)
+    s_w, beside = swap_with(sums, x[:, :, :1], "wa", 1)
     sums = sums + s_w
-    x = jnp.concatenate([values, beside], axis=2)
-    sums, _, below = ha_round(sums, x[:, :1], x[:, :1])
-    x = jnp.concatenate([x, below], axis=1)
+    x = jnp.concatenate([x, beside], axis=2)
     return finish_stats(sums, values), x
 
 

time: 77.8 us -> 83.2 us (1.069)
  waiting for transfers between devices: 17.7 us -> 21 us
  starting transfers between devices: 18.3 us -> 19.5 us
  local copies, waits for them, and re-layouts: 20.9 us -> 21.8 us
    ppermute x15, waiting for transfers between devices: 17.7 us -> 21 us  [swap(): return lax.ppermute(x, axis, [(i, i ^ distance) for i in range(size)])]
    ppermute x15, starting transfers between devices: 18.3 us -> 19.5 us  [swap(): return lax.ppermute(x, axis, [(i, i ^ distance) for i in range(size)])]
    slice x2, local copies, waits for them, and re-layouts: 0.06 us -> 1.06 us  [swap_with(): return (unpack_sums(got[cut:], sums), got[:cut].reshape(payload.shape))]
    unnamed x39 -> x40, local copies, waits for them, and re-layouts: 3.58 us -> 3.85 us
  transfers between devices with their start and end apart: 15 -> 15, of which waited for: 10 -> 9; matrix products, arithmetic and copies ran while one was open for 14% -> 13% of each run, Pallas kernels for 0% -> 0%
where the time goes in v17:
time: 83.2 us; the launch traced here: 82.7 us
  local copies, waits for them, and re-layouts  21.8 us (26%)
  waiting for transfers between devices  21 us (25%)
  starting transfers between devices  19.5 us (23%)
  other arithmetic  11 us (13%)
  matrix products  8.6 us (10%)
    ppermute x15, waiting for transfers between devices, swap(): return lax.ppermute(x, axis, [(i, i ^ distance) for i in range(size)])  21 us
    ppermute x15, starting transfers between devices, swap(): return lax.ppermute(x, axis, [(i, i ^ distance) for i in range(size)])  19.5 us
    slice x2, local copies, waits for them, and re-layouts, valid_conv(): kernel[step_t].reshape(9 * channels, -1)  7.42 us
    dot_general x6, matrix products, valid_conv(): jnp.dot(window, kernel[step_t].reshape(9 * channels, -1), preferred_eleme...  6.54 us
    unnamed x40, local copies, waits for them, and re-layouts  3.85 us
    convert_element_type x2, other arithmetic, norm_conv(): jnp.where(inside_mask(height + 2, across + 2, 1), act, 0.0)  3.53 us
    slice x2, local copies, waits for them, and re-layouts, valid_conv(): window = wide[step_t:step_t + frames].reshape(-1, 9 * channels)  2.19 us
    reduce_sum x5, other arithmetic, local_sums(): jnp.sum(grouped, axis=(0, 2))  2.18 us
  transfers between devices with their start and end apart: 15, of which 9 were waited for; matrix products, arithmetic and copies ran while one was open for 13% of the time, Pallas kernels for 0%

profile of v17, /device:TPU:0, one launch (start us, length us, event | category | flops | bytes accessed | tf_op | source)
XLA Modules:
  0.0 82.7 jit_solution(844182888844065542)
XLA Ops:
  0.0 1.0 %convert_reduce_fusion.2 = (f32[512]{0:T(512)S(1)}, f32[512]{0:T(512)S(1)}) fusion(bf16[3,2,32,512]{3,2,1,0:T(8,128)(2,1)} %param.10), kind=kLoop, calls=%fused_computation.52 | loop fusion | flops 392192 | bytes 200704 | tf_op jit(solution)/shard_map/reduce_sum | solution.py:179
  1.4 0.5 collective-permute-start
  2.0 1.7 %slice_bitcast_fusion.7 = (bf16[512,256]{1,0:T(8,128)(2,1)S(1)}, bf16[512,256]{1,0:T(8,128)(2,1)S(1)}, bf16[512,256]{1,0:T(8,128)(2,1)S(1)}, bf16[512,256]{1,0:T...) fusion(bf16[3,3,512,256]{3,2,1,0:T(8,128)(2,1)} %param.13), kind=kLoop, calls=%fused_computation.77 | loop fusion | bytes 4194304 | tf_op jit(solution)/shard_map/squeeze | solution.py:129
  4.1 2.7 %collective-permute-start.1 = (bf16[97,512]{1,0:T(8,128)(2,1)S(1)}, bf16[97,512]{1,0:T(8,128)(2,1)S(1)}, u32[]{:S(2)}, u32[]{:S(2)}) collective-permute-start(bf16[97,512]{1,0:T(8,128)(2,1)S(1)} %pad_maximum_fusion.18), channel_id=1, source_target_pairs={{0,4},{4,0},{8,12},{12,8},{1,5},{5,1},{9,13},{13,9},{2,6},{6,2},{1... | collective-permute-start | bytes 297992 | tf_op jit(solution)/shard_map/ppermute | solution.py:170
  6.9 2.5 %collective-permute-start.2 = (bf16[97,512]{1,0:T(8,128)(2,1)S(1)}, bf16[97,512]{1,0:T(8,128)(2,1)S(1)}, u32[]{:S(2)}, u32[]{:S(2)}) collective-permute-start(bf16[97,512]{1,0:T(8,128)(2,1)S(1)} %pad_maximum_fusion.18), channel_id=1, source_target_pairs={{0,12},{4,8},{8,4},{12,0},{1,13},{5,9},{9,5},{13,1},{2,14},{6,10},... | collective-permute-start | bytes 297992 | tf_op jit(solution)/shard_map/ppermute | solution.py:170
  9.5 0.9 %collective-permute-done.1 = bf16[97,512]{1,0:T(8,128)(2,1)S(1)} collective-permute-done((bf16[97,512]{1,0:T(8,128)(2,1)S(1)}, bf16[97,512]{1,0:T(8,128)(2,1)S(1)}, u32[]{:S(2)}, u32[]{:S(2)}) %collective-permute-start.1) | collective-permute-done | bytes 99360 | tf_op jit(solution)/shard_map/ppermute | solution.py:170
  10.5 4.5 %collective-permute-done.2 = bf16[97,512]{1,0:T(8,128)(2,1)S(1)} collective-permute-done((bf16[97,512]{1,0:T(8,128)(2,1)S(1)}, bf16[97,512]{1,0:T(8,128)(2,1)S(1)}, u32[]{:S(2)}, u32[]{:S(2)}) %collective-permute-start.2) | collective-permute-done | bytes 99360 | tf_op jit(solution)/shard_map/ppermute | solution.py:170
  15.7 1.6 %collective-permute-start.4 = (bf16[10,512]{1,0:T(8,128)(2,1)S(1)}, bf16[10,512]{1,0:T(8,128)(2,1)S(1)}, u32[]{:S(2)}, u32[]{:S(2)}) collective-permute-start(bf16[10,512]{1,0:T(8,128)(2,1)S(1)} %pad_maximum_fusion.24), channel_id=1, source_target_pairs={{0,2},{2,0},{1,3},{3,1},{4,6},{6,4},{5,7},{7,5},{8,10},{10,8},{9,1... | collective-permute-start | bytes 30728 | tf_op jit(solution)/shard_map/ppermute | solution.py:170
  17.3 2.2 %collective-permute-done.4 = bf16[10,512]{1,0:T(8,128)(2,1)S(1)} collective-permute-done((bf16[10,512]{1,0:T(8,128)(2,1)S(1)}, bf16[10,512]{1,0:T(8,128)(2,1)S(1)}, u32[]{:S(2)}, u32[]{:S(2)}) %collective-permute-start.4) | collective-permute-done | bytes 10272 | tf_op jit(solution)/shard_map/ppermute | solution.py:170
  20.1 0.3 select_convert_fusion.2
  20.5 0.3 fusion.11
  20.7 0.3 fusion.15
  21.0 0.4 fusion.1
  21.8 1.2 %convolution_add_fusion.4 = bf16[192,256]{1,0:T(8,128)(2,1)S(1)} fusion(bf16[192,512]{1,0:T(8,128)(2,1)S(1)} %bitcast.151, bf16[3,3,512,256]{3,2,1,0:T(8,128)(2,1)} %param.13, f32[192,512]{1,0:T(8,128)S(1)} %fusion.15, f32[192,512]{1,0:T(8,128)S(1)} %fusion.11, f32[192,1024]{1,0:T(8,128)S(1)} %fusion.1), kind=kOutput, calls=%fused_computation.7 | convolution fusion | flops 50528256 | bytes 1146880 | tf_op jit(solution)/shard_map/dot_general | solution.py:123
  23.1 0.3 pad_maximum_fusion.10
  23.4 0.3 pad_maximum_fusion.11
  23.6 0.8 convert_reduce_fusion.1
  25.2 0.7 collective-permute-start.5
  25.9 2.3 %collective-permute-start.7 = (f32[2,32]{1,0:T(2,128)S(1)}, f32[2,32]{1,0:T(2,128)S(1)}, u32[]{:S(2)}, u32[]{:S(2)}) collective-permute-start(f32[2,32]{1,0:T(2,128)S(1)} %pad_maximum_fusion.28), channel_id=1, source_target_pairs={{0,8},{4,12},{8,0},{12,4},{1,9},{5,13},{9,1},{13,5},{2,10},{6,14},... | collective-permute-start | bytes 776 | tf_op jit(solution)/shard_map/ppermute | solution.py:170
  28.2 1.4 %collective-permute-start.6 = (bf16[193,256]{1,0:T(8,128)(2,1)S(1)}, bf16[193,256]{1,0:T(8,128)(2,1)S(1)}, u32[]{:S(2)}, u32[]{:S(2)}) collective-permute-start(bf16[193,256]{1,0:T(8,128)(2,1)S(1)} %get-tuple-element.70), channel_id=1, source_target_pairs={{0,12},{4,8},{8,4},{12,0},{1,13},{5,9},{9,5},{13,1},{2,14},{6,10},... | collective-permute-start | bytes 296456 | tf_op jit(solution)/shard_map/ppermute | solution.py:170
  29.6 0.3 collective-permute-done.5
  30.0 4.7 %collective-permute-done.6 = bf16[193,256]{1,0:T(8,128)(2,1)S(1)} collective-permute-done((bf16[193,256]{1,0:T(8,128)(2,1)S(1)}, bf16[193,256]{1,0:T(8,128)(2,1)S(1)}, u32[]{:S(2)}, u32[]{:S(2)}) %collective-permute-start.6) | collective-permute-done | bytes 98848 | tf_op jit(solution)/shard_map/ppermute | solution.py:170
  35.4 1.5 %collective-permute-start.8 = (bf16[19,256]{1,0:T(8,128)(2,1)S(1)}, bf16[19,256]{1,0:T(8,128)(2,1)S(1)}, u32[]{:S(2)}, u32[]{:S(2)}) collective-permute-start(bf16[19,256]{1,0:T(8,128)(2,1)S(1)} %pad_maximum_fusion.25), channel_id=1, source_target_pairs={{0,2},{2,0},{1,3},{3,1},{4,6},{6,4},{5,7},{7,5},{8,10},{10,8},{9,1... | collective-permute-start | bytes 29192 | tf_op jit(solution)/shard_map/ppermute | solution.py:170
  37.1 2.1 %collective-permute-done.8 = bf16[19,256]{1,0:T(8,128)(2,1)S(1)} collective-permute-done((bf16[19,256]{1,0:T(8,128)(2,1)S(1)}, bf16[19,256]{1,0:T(8,128)(2,1)S(1)}, u32[]{:S(2)}, u32[]{:S(2)}) %collective-permute-start.8) | collective-permute-done | bytes 9760 | tf_op jit(solution)/shard_map/ppermute | solution.py:170
  40.2 3.7 %fusion.114 = (bf16[1,3,3,256,256]{4,3,2,1,0:T(8,128)(2,1)S(1)}, bf16[1,3,3,256,256]{4,3,2,1,0:T(8,128)(2,1)}, bf16[1,3,3,256,256]{4,3,2,1,0:T(8,128)(2,1)}) fusion(bf16[3,3,3,256,256]{4,3,2,1,0:T(8,128)(2,1)} %param.16), kind=kLoop, calls=%fused_computation.276 | loop fusion | bytes 7077888 | tf_op jit(solution)/shard_map/slice | solution.py:154
  44.7 1.9 %select_convert_fusion.1 = bf16[5,6,66,256]{3,2,1,0:T(8,128)(2,1)S(1)} fusion(bf16[3,6,1,256]{3,2,1,0:T(2,128)(2,1)S(1)} %reshape.752, bf16[3,1,64,256]{3,2,1,0:T(8,128)(2,1)S(1)} %bitcast.133, bf16[3,4,64,256]{3,2,1,0:T(8,128)(2,1)S(1)} %bitcast.113, bf16[3,1,64,256]{3,2,1,0:T(8,128)(2,1)S(1)} %bitcast.129, ...), kind=kLoop, calls=%fused_computation.1 | loop fusion | flops 11151360 | bytes 2022796 | tf_op jit(solution)/shard_map/convert_element_type | solution.py:275
  47.8 0.2 slice_dynamic-update-slice_fusion.10
  48.3 1.0 %fusion.112 = (bf16[3,4,64,2304]{3,2,1,0:T(8,128)(2,1)S(1)}, bf16[3,4,64,2304]{3,2,1,0:T(8,128)(2,1)S(1)}, bf16[3,4,64,2304]{3,2,1,0:T(8,128)(2,1)S(1)}) fusion(bf16[5,4,64,2304]{3,2,1,0:T(8,128)(2,1)S(1)} %slice_dynamic-update-slice_fusion.9), kind=kLoop, calls=%fused_computation.274 | loop fusion | bytes 21233664 | tf_op jit(solution)/shard_map/slice | solution.py:152
  49.3 0.3 copy-done.4
  49.6 1.1 %fusion.117 = f32[768,256]{1,0:T(8,128)S(1)} fusion(bf16[768,2304]{1,0:T(8,128)(2,1)S(1)} %bitcast.124, bf16[2304,256]{1,0:T(8,128)(2,1)S(1)} %bitcast.148), kind=kOutput, calls=%fused_computation.279 | convolution fusion | flops 905969664 | bytes 5505024 | tf_op jit(solution)/shard_map/dot_general | solution.py:153
  50.9 1.1 %convolution_add_fusion.3 = f32[768,256]{1,0:T(8,128)S(1)} fusion(f32[768,256]{1,0:T(8,128)S(1)} %fusion.117, bf16[768,2304]{1,0:T(8,128)(2,1)S(1)} %bitcast.122, bf16[2304,256]{1,0:T(8,128)(2,1)S(1)} %bitcast.147), kind=kOutput, calls=%fused_computation.5 | convolution fusion | flops 906166272 | bytes 6291456 | tf_op jit(solution)/shard_map/dot_general | solution.py:153
  52.0 1.1 %convert_reduce_fusion = (f32[256]{0:T(256)S(1)}, f32[256]{0:T(256)S(1)}, bf16[768,256]{1,0:T(8,128)(2,1)S(1)}) fusion(f32[768,256]{1,0:T(8,128)S(1)} %convolution_add_fusion.3, bf16[768,2304]{1,0:T(8,128)(2,1)S(1)} %bitcast.120, bf16[2304,256]{1,0:T(8,128)(2,1)S(1)} %bitcast.143), kind=kOutput, calls=%fused_computation.17 | convolution fusion | flops 907148800 | bytes 5900288 | tf_op jit(solution)/shard_map/dot_general | solution.py:153
  53.8 2.0 %collective-permute-start.12 = (f32[2,32]{1,0:T(2,128)S(1)}, f32[2,32]{1,0:T(2,128)S(1)}, u32[]{:S(2)}, u32[]{:S(2)}) collective-permute-start(f32[2,32]{1,0:T(2,128)S(1)} %pad_maximum_fusion.29), channel_id=1, source_target_pairs={{0,8},{4,12},{8,0},{12,4},{1,9},{5,13},{9,1},{13,5},{2,10},{6,14},... | collective-permute-start | bytes 776 | tf_op jit(solution)/shard_map/ppermute | solution.py:170
  55.8 2.4 %collective-permute-start.11 = (bf16[193,256]{1,0:T(8,128)(2,1)S(1)}, bf16[193,256]{1,0:T(8,128)(2,1)S(1)}, u32[]{:S(2)}, u32[]{:S(2)}) collective-permute-start(bf16[193,256]{1,0:T(8,128)(2,1)S(1)} %get-tuple-element.64), channel_id=1, source_target_pairs={{0,12},{4,8},{8,4},{12,0},{1,13},{5,9},{9,5},{13,1},{2,14},{6,10},... | collective-permute-start | bytes 296456 | tf_op jit(solution)/shard_map/ppermute | solution.py:170
  58.2 0.9 %collective-permute-done.10 = bf16[193,256]{1,0:T(8,128)(2,1)S(1)} collective-permute-done((bf16[193,256]{1,0:T(8,128)(2,1)S(1)}, bf16[193,256]{1,0:T(8,128)(2,1)S(1)}, u32[]{:S(2)}, u32[]{:S(2)}) %collective-permute-start.10) | collective-permute-done | bytes 98848 | tf_op jit(solution)/shard_map/ppermute | solution.py:170
  59.2 3.2 %collective-permute-done.11 = bf16[193,256]{1,0:T(8,128)(2,1)S(1)} collective-permute-done((bf16[193,256]{1,0:T(8,128)(2,1)S(1)}, bf16[193,256]{1,0:T(8,128)(2,1)S(1)}, u32[]{:S(2)}, u32[]{:S(2)}) %collective-permute-start.11) | collective-permute-done | bytes 98848 | tf_op jit(solution)/shard_map/ppermute | solution.py:170
  63.2 1.5 %collective-permute-start.13 = (bf16[19,256]{1,0:T(8,128)(2,1)S(1)}, bf16[19,256]{1,0:T(8,128)(2,1)S(1)}, u32[]{:S(2)}, u32[]{:S(2)}) collective-permute-start(bf16[19,256]{1,0:T(8,128)(2,1)S(1)} %pad_maximum_fusion.26), channel_id=1, source_target_pairs={{0,2},{2,0},{1,3},{3,1},{4,6},{6,4},{5,7},{7,5},{8,10},{10,8},{9,1... | collective-permute-start | bytes 29192 | tf_op jit(solution)/shard_map/ppermute | solution.py:170
  64.7 2.2 %collective-permute-done.13 = bf16[19,256]{1,0:T(8,128)(2,1)S(1)} collective-permute-done((bf16[19,256]{1,0:T(8,128)(2,1)S(1)}, bf16[19,256]{1,0:T(8,128)(2,1)S(1)}, u32[]{:S(2)}, u32[]{:S(2)}) %collective-permute-start.13) | collective-permute-done | bytes 9760 | tf_op jit(solution)/shard_map/ppermute | solution.py:170
  67.9 3.7 %fusion.113 = (bf16[1,3,3,256,256]{4,3,2,1,0:T(8,128)(2,1)S(1)}, bf16[1,3,3,256,256]{4,3,2,1,0:T(8,128)(2,1)}, bf16[1,3,3,256,256]{4,3,2,1,0:T(8,128)(2,1)}) fusion(bf16[3,3,3,256,256]{4,3,2,1,0:T(8,128)(2,1)} %param.19), kind=kLoop, calls=%fused_computation.275 | loop fusion | bytes 7077888 | tf_op jit(solution)/shard_map/slice | solution.py:154
  72.1 0.3 copy-done.5
  72.5 1.0 %slice.717 = bf16[792,256]{1,0:T(8,128)(2,1)S(1)} slice(bf16[793,256]{1,0:T(8,128)(2,1)} %copy-done.5), slice={[0:792], [0:256]} | slice | bytes 811008 | tf_op jit(solution)/shard_map/slice | solution.py:224
  73.7 1.7 %select_convert_fusion = bf16[5,6,66,256]{3,2,1,0:T(8,128)(2,1)S(1)} fusion(bf16[3,6,1,256]{3,2,1,0:T(2,128)(2,1)S(1)} %reshape.753, bf16[3,1,64,256]{3,2,1,0:T(8,128)(2,1)S(1)} %bitcast.141, bf16[3,4,64,256]{3,2,1,0:T(8,128)(2,1)S(1)} %bitcast.119, bf16[3,1,64,256]{3,2,1,0:T(8,128)(2,1)S(1)} %bitcast.137, bf16[2,6,66,256]{3,2,1,0:T(8,128)(2,1)S(1)} %maximum_select_fusion.1, ...), kind=kLoop, calls=%fused_computation | loop fusion | flops 11151360 | bytes 2022796 | tf_op jit(solution)/shard_map/convert_element_type | solution.py:275
  76.6 0.2 slice_dynamic-update-slice_fusion.1
  77.2 1.2 %fusion.111 = (bf16[3,4,64,2304]{3,2,1,0:T(8,128)(2,1)S(1)}, bf16[3,4,64,2304]{3,2,1,0:T(8,128)(2,1)S(1)}, bf16[3,4,64,2304]{3,2,1,0:T(8,128)(2,1)S(1)}) fusion(bf16[5,4,64,2304]{3,2,1,0:T(8,128)(2,1)S(1)} %slice_dynamic-update-slice_fusion), kind=kLoop, calls=%fused_computation.273 | loop fusion | bytes 21233664 | tf_op jit(solution)/shard_map/slice | solution.py:152
  78.4 1.1 %fusion.118 = f32[768,256]{1,0:T(8,128)S(1)} fusion(bf16[768,2304]{1,0:T(8,128)(2,1)S(1)} %bitcast.125, bf16[2304,256]{1,0:T(8,128)(2,1)S(1)} %bitcast.146), kind=kOutput, calls=%fused_computation.280 | convolution fusion | flops 905969664 | bytes 5505024 | tf_op jit(solution)/shard_map/dot_general | solution.py:153
  79.7 1.1 %convolution_add_fusion.1 = f32[768,256]{1,0:T(8,128)S(1)} fusion(f32[768,256]{1,0:T(8,128)S(1)} %fusion.118, bf16[768,2304]{1,0:T(8,128)(2,1)S(1)} %bitcast.123, bf16[2304,256]{1,0:T(8,128)(2,1)S(1)} %bitcast.145), kind=kOutput, calls=%fused_computation.3 | convolution fusion | flops 906166272 | bytes 6291456 | tf_op jit(solution)/shard_map/dot_general | solution.py:153
  80.8 1.1 %convolution_add_fusion = f32[768,256]{1,0:T(8,128)S(1)} fusion(f32[768,256]{1,0:T(8,128)S(1)} %convolution_add_fusion.1, bf16[768,2304]{1,0:T(8,128)(2,1)S(1)} %bitcast.121, bf16[2304,256]{1,0:T(8,128)(2,1)S(1)} %bitcast.144), kind=kOutput, calls=%fused_computation.2 | convolution fusion | flops 906166272 | bytes 6291456 | tf_op jit(solution)/shard_map/dot_general | solution.py:153
  81.9 0.8 %add_convert_fusion = bf16[3,4,64,256]{3,2,1,0:T(8,128)(2,1)} fusion(f32[3,4,64,256]{3,2,1,0:T(8,128)S(1)} %bitcast.152, bf16[3,4,64,256]{3,2,1,0:T(8,128)(2,1)S(1)} %bitcast.114), kind=kLoop, calls=%fused_computation.23 | loop fusion | flops 589824 | bytes 1572864 | tf_op jit(solution)/shard_map/convert_element_type | solution.py:302
  (215 shorter events, 12.8 us)
Async XLA Ops:
  1.4 2.3 %collective-permute-start = (f32[2,32]{1,0:T(2,128)S(1)}, f32[2,32]{1,0:T(2,128)S(1)}, u32[]{:S(2)}, u32[]{:S(2)}) collective-permute-start(f32[2,32]{1,0:T(2,128)S(1)} %pad_maximum_fusion.27), channel_id=1, source_target_pairs={{0,1},{1,0},{2,3},{3,2},{4,5},{5,4},{6,7},{7,6},{8,9},{9,8},{10,11... | collective-permute-start | bytes 776 | tf_op jit(solution)/shard_map/ppermute | solution.py:170
  1.9 2.1 %slice-start = ((bf16[3,2,32,512]{3,2,1,0:T(8,128)(2,1)}), bf16[3,1,32,512]{3,2,1,0:T(8,128)(2,1)S(1)}, s32[]{:S(2)}) async-start(bf16[3,2,32,512]{3,2,1,0:T(8,128)(2,1)} %param.10), calls=%async_computation | async-start | bytes 196608 | tf_op jit(solution)/shard_map/slice | solution.py:259
  1.9 13.1 %copy-start = (bf16[3,2,32,512]{3,2,1,0:T(8,128)(2,1)S(1)}, bf16[3,2,32,512]{3,2,1,0:T(8,128)(2,1)}, u32[]{:S(2)}) copy-start(bf16[3,2,32,512]{3,2,1,0:T(8,128)(2,1)} %param.10) | copy-start | bytes 589828
  1.9 18.1 %copy-start.6 = (f32[512]{0:T(512)S(1)}, f32[512]{0:T(512)}, u32[]{:S(2)}) copy-start(f32[512]{0:T(512)} %param.12) | copy-start | bytes 6148
  2.0 18.1 %copy-start.7 = (f32[512]{0:T(512)S(1)}, f32[512]{0:T(512)}, u32[]{:S(2)}) copy-start(f32[512]{0:T(512)} %param.11) | copy-start | bytes 6148
  4.1 6.3 %collective-permute-start.1 = (bf16[97,512]{1,0:T(8,128)(2,1)S(1)}, bf16[97,512]{1,0:T(8,128)(2,1)S(1)}, u32[]{:S(2)}, u32[]{:S(2)}) collective-permute-start(bf16[97,512]{1,0:T(8,128)(2,1)S(1)} %pad_maximum_fusion.18), channel_id=1, source_target_pairs={{0,4},{4,0},{8,12},{12,8},{1,5},{5,1},{9,13},{13,9},{2,6},{6,2},{1... | collective-permute-start | bytes 297992 | tf_op jit(solution)/shard_map/ppermute | solution.py:170
  6.9 8.1 %collective-permute-start.2 = (bf16[97,512]{1,0:T(8,128)(2,1)S(1)}, bf16[97,512]{1,0:T(8,128)(2,1)S(1)}, u32[]{:S(2)}, u32[]{:S(2)}) collective-permute-start(bf16[97,512]{1,0:T(8,128)(2,1)S(1)} %pad_maximum_fusion.18), channel_id=1, source_target_pairs={{0,12},{4,8},{8,4},{12,0},{1,13},{5,9},{9,5},{13,1},{2,14},{6,10},... | collective-permute-start | bytes 297992 | tf_op jit(solution)/shard_map/ppermute | solution.py:170
  9.3 6.0 %collective-permute-start.3 = (f32[2,32]{1,0:T(2,128)S(1)}, f32[2,32]{1,0:T(2,128)S(1)}, u32[]{:S(2)}, u32[]{:S(2)}) collective-permute-start(f32[2,32]{1,0:T(2,128)S(1)} %get-tuple-element.23), channel_id=1, source_target_pairs={{0,8},{4,12},{8,0},{12,4},{1,9},{5,13},{9,1},{13,5},{2,10},{6,14},... | collective-permute-start | bytes 776 | tf_op jit(solution)/shard_map/ppermute | solution.py:170
  15.7 3.8 %collective-permute-start.4 = (bf16[10,512]{1,0:T(8,128)(2,1)S(1)}, bf16[10,512]{1,0:T(8,128)(2,1)S(1)}, u32[]{:S(2)}, u32[]{:S(2)}) collective-permute-start(bf16[10,512]{1,0:T(8,128)(2,1)S(1)} %pad_maximum_fusion.24), channel_id=1, source_target_pairs={{0,2},{2,0},{1,3},{3,1},{4,6},{6,4},{5,7},{7,5},{8,10},{10,8},{9,1... | collective-permute-start | bytes 30728 | tf_op jit(solution)/shard_map/ppermute | solution.py:170
  25.2 4.7 %collective-permute-start.5 = (bf16[193,256]{1,0:T(8,128)(2,1)S(1)}, bf16[193,256]{1,0:T(8,128)(2,1)S(1)}, u32[]{:S(2)}, u32[]{:S(2)}) collective-permute-start(bf16[193,256]{1,0:T(8,128)(2,1)S(1)} %get-tuple-element.69), channel_id=1, source_target_pairs={{0,4},{4,0},{8,12},{12,8},{1,5},{5,1},{9,13},{13,9},{2,6},{6,2},{1... | collective-permute-start | bytes 296456 | tf_op jit(solution)/shard_map/ppermute | solution.py:170
  25.9 9.1 %collective-permute-start.7 = (f32[2,32]{1,0:T(2,128)S(1)}, f32[2,32]{1,0:T(2,128)S(1)}, u32[]{:S(2)}, u32[]{:S(2)}) collective-permute-start(f32[2,32]{1,0:T(2,128)S(1)} %pad_maximum_fusion.28), channel_id=1, source_target_pairs={{0,8},{4,12},{8,0},{12,4},{1,9},{5,13},{9,1},{13,5},{2,10},{6,14},... | collective-permute-start | bytes 776 | tf_op jit(solution)/shard_map/ppermute | solution.py:170
  28.2 6.5 %collective-permute-start.6 = (bf16[193,256]{1,0:T(8,128)(2,1)S(1)}, bf16[193,256]{1,0:T(8,128)(2,1)S(1)}, u32[]{:S(2)}, u32[]{:S(2)}) collective-permute-start(bf16[193,256]{1,0:T(8,128)(2,1)S(1)} %get-tuple-element.70), channel_id=1, source_target_pairs={{0,12},{4,8},{8,4},{12,0},{1,13},{5,9},{9,5},{13,1},{2,14},{6,10},... | collective-permute-start | bytes 296456 | tf_op jit(solution)/shard_map/ppermute | solution.py:170
  35.4 3.8 %collective-permute-start.8 = (bf16[19,256]{1,0:T(8,128)(2,1)S(1)}, bf16[19,256]{1,0:T(8,128)(2,1)S(1)}, u32[]{:S(2)}, u32[]{:S(2)}) collective-permute-start(bf16[19,256]{1,0:T(8,128)(2,1)S(1)} %pad_maximum_fusion.25), channel_id=1, source_target_pairs={{0,2},{2,0},{1,3},{3,1},{4,6},{6,4},{5,7},{7,5},{8,10},{10,8},{9,1... | collective-permute-start | bytes 29192 | tf_op jit(solution)/shard_map/ppermute | solution.py:170
  40.1 3.9 %collective-permute-start.9 = (bf16[793,256]{1,0:T(8,128)(2,1)S(1)}, bf16[793,256]{1,0:T(8,128)(2,1)S(1)}, u32[]{:S(2)}, u32[]{:S(2)}) collective-permute-start(bf16[793,256]{1,0:T(8,128)(2,1)S(1)} %pad_maximum_fusion.8), channel_id=1, source_target_pairs={{0,1},{1,0},{2,3},{3,2},{4,5},{5,4},{6,7},{7,6},{8,9},{9,8},{10,11... | collective-permute-start | bytes 1218056 | tf_op jit(solution)/shard_map/ppermute | solution.py:170
  43.9 0.8 %copy-start.8 = (f32[256]{0:T(256)S(1)}, f32[256]{0:T(256)}, u32[]{:S(2)}) copy-start(f32[256]{0:T(256)} %param.15) | copy-start | bytes 3076
  43.9 0.9 %copy-start.9 = (f32[256]{0:T(256)S(1)}, f32[256]{0:T(256)}, u32[]{:S(2)}) copy-start(f32[256]{0:T(256)} %param.14) | copy-start | bytes 3076
  48.3 1.3 %copy-start.4 = (bf16[1,3,3,256,256]{4,3,2,1,0:T(8,128)(2,1)S(1)}, bf16[1,3,3,256,256]{4,3,2,1,0:T(8,128)(2,1)}, u32[]{:S(2)}) copy-start(bf16[1,3,3,256,256]{4,3,2,1,0:T(8,128)(2,1)} %get-tuple-element.34) | copy-start | bytes 3538948
  49.6 1.3 %copy-start.3 = (bf16[1,3,3,256,256]{4,3,2,1,0:T(8,128)(2,1)S(1)}, bf16[1,3,3,256,256]{4,3,2,1,0:T(8,128)(2,1)}, u32[]{:S(2)}) copy-start(bf16[1,3,3,256,256]{4,3,2,1,0:T(8,128)(2,1)} %get-tuple-element.35) | copy-start | bytes 3538948
  53.7 5.4 %collective-permute-start.10 = (bf16[193,256]{1,0:T(8,128)(2,1)S(1)}, bf16[193,256]{1,0:T(8,128)(2,1)S(1)}, u32[]{:S(2)}, u32[]{:S(2)}) collective-permute-start(bf16[193,256]{1,0:T(8,128)(2,1)S(1)} %get-tuple-element.63), channel_id=1, source_target_pairs={{0,4},{4,0},{8,12},{12,8},{1,5},{5,1},{9,13},{13,9},{2,6},{6,2},{1... | collective-permute-start | bytes 296456 | tf_op jit(solution)/shard_map/ppermute | solution.py:170
  53.8 8.9 %collective-permute-start.12 = (f32[2,32]{1,0:T(2,128)S(1)}, f32[2,32]{1,0:T(2,128)S(1)}, u32[]{:S(2)}, u32[]{:S(2)}) collective-permute-start(f32[2,32]{1,0:T(2,128)S(1)} %pad_maximum_fusion.29), channel_id=1, source_target_pairs={{0,8},{4,12},{8,0},{12,4},{1,9},{5,13},{9,1},{13,5},{2,10},{6,14},... | collective-permute-start | bytes 776 | tf_op jit(solution)/shard_map/ppermute | solution.py:170
  55.8 6.6 %collective-permute-start.11 = (bf16[193,256]{1,0:T(8,128)(2,1)S(1)}, bf16[193,256]{1,0:T(8,128)(2,1)S(1)}, u32[]{:S(2)}, u32[]{:S(2)}) collective-permute-start(bf16[193,256]{1,0:T(8,128)(2,1)S(1)} %get-tuple-element.64), channel_id=1, source_target_pairs={{0,12},{4,8},{8,4},{12,0},{1,13},{5,9},{9,5},{13,1},{2,14},{6,10},... | collective-permute-start | bytes 296456 | tf_op jit(solution)/shard_map/ppermute | solution.py:170
  63.2 3.8 %collective-permute-start.13 = (bf16[19,256]{1,0:T(8,128)(2,1)S(1)}, bf16[19,256]{1,0:T(8,128)(2,1)S(1)}, u32[]{:S(2)}, u32[]{:S(2)}) collective-permute-start(bf16[19,256]{1,0:T(8,128)(2,1)S(1)} %pad_maximum_fusion.26), channel_id=1, source_target_pairs={{0,2},{2,0},{1,3},{3,1},{4,6},{6,4},{5,7},{7,5},{8,10},{10,8},{9,1... | collective-permute-start | bytes 29192 | tf_op jit(solution)/shard_map/ppermute | solution.py:170
  67.8 3.9 %collective-permute-start.14 = (bf16[793,256]{1,0:T(8,128)(2,1)S(1)}, bf16[793,256]{1,0:T(8,128)(2,1)S(1)}, u32[]{:S(2)}, u32[]{:S(2)}) collective-permute-start(bf16[793,256]{1,0:T(8,128)(2,1)S(1)} %pad_maximum_fusion.9), channel_id=1, source_target_pairs={{0,1},{1,0},{2,3},{3,2},{4,5},{5,4},{6,7},{7,6},{8,9},{9,8},{10,11... | collective-permute-start | bytes 1218056 | tf_op jit(solution)/shard_map/ppermute | solution.py:170
  71.6 2.1 %copy-start.10 = (f32[256]{0:T(256)S(1)}, f32[256]{0:T(256)}, u32[]{:S(2)}) copy-start(f32[256]{0:T(256)} %param.18) | copy-start | bytes 3076
  71.6 2.2 %copy-start.11 = (f32[256]{0:T(256)S(1)}, f32[256]{0:T(256)}, u32[]{:S(2)}) copy-start(f32[256]{0:T(256)} %param.17) | copy-start | bytes 3076
  71.7 0.8 copy-start.5
  77.2 1.3 %copy-start.2 = (bf16[1,3,3,256,256]{4,3,2,1,0:T(8,128)(2,1)S(1)}, bf16[1,3,3,256,256]{4,3,2,1,0:T(8,128)(2,1)}, u32[]{:S(2)}) copy-start(bf16[1,3,3,256,256]{4,3,2,1,0:T(8,128)(2,1)} %get-tuple-element.31) | copy-start | bytes 3538948
  78.4 1.3 %copy-start.1 = (bf16[1,3,3,256,256]{4,3,2,1,0:T(8,128)(2,1)S(1)}, bf16[1,3,3,256,256]{4,3,2,1,0:T(8,128)(2,1)}, u32[]{:S(2)}) copy-start(bf16[1,3,3,256,256]{4,3,2,1,0:T(8,128)(2,1)} %get-tuple-element.32) | copy-start | bytes 3538948

commit v18 on v10

--- a/solution.py
+++ b/solution.py
@@ -144,16 +144,20 @@
 
 def valid_conv(padded, kernel, frames, height, across):
     channels = padded.shape[-1]
-    wide = jnp.concatenate(
-        [padded[:, dy : dy + height, dx : dx + across] for dy in range(3) for dx in range(3)], axis=-1
-    )
-    result = None
-    for step_t in range(3):
-        window = wide[step_t : step_t + frames].reshape(-1, 9 * channels)
-        part = jnp.dot(
-            window, kernel[step_t].reshape(9 * channels, -1), preferred_element_type=jnp.float32
-        )
-        result = part if result is None else result + part
+    columns = jnp.concatenate(
+        [
+            padded[dt : dt + frames, dy : dy + height, dx : dx + across]
+            for dt in range(3)
+            for dy in range(3)
+            for dx in range(3)
+        ],
+        axis=-1,
+    )
+    result = jnp.dot(
+        columns.reshape(-1, 27 * channels),
+        kernel.reshape(27 * channels, kernel.shape[-1]),
+        preferred_element_type=jnp.float32,
+    )
     return result.reshape(frames, height, across, -1)
 
 

time: 77.8 us -> 221 us (2.84)
  local copies, waits for them, and re-layouts: 20.9 us -> 95.1 us
  other arithmetic: 11 us -> 74.6 us
  matrix products: 8.59 us -> 12.5 us
    another operation x14, other arithmetic: 0.18 us -> 12.1 us
    reshape x10, local copies, waits for them, and re-layouts: 0.42 us -> 12.2 us  [swap_with(): message = jnp.concatenate([payload.reshape(-1, width), packed], axis=0)]
    slice x4 -> x0, local copies, waits for them, and re-layouts: 9.61 us -> none  [the longest x2 7.42 us: valid_conv(): kernel[step_t].reshape(9 * channels, -1)]
    unnamed x39 -> x87, local copies, waits for them, and re-layouts: 3.58 us -> 11.7 us
    add x11, local copies, waits for them, and re-layouts: 0.91 us -> 8.62 us  [unpack_sums(): return flat[0] + flat[1] + flat[2]]
    reshape x6, local copies, waits for them, and re-layouts: 0.51 us -> 7.45 us  [pack_sums(): middle.reshape(-1)]
    concatenate x8, other arithmetic: 0.15 us -> 6.94 us  [swap_with(): message = jnp.concatenate([payload.reshape(-1, width), packed], axis=0)]
    reshape x6, local copies, waits for them, and re-layouts: 0.5 us -> 6.89 us  [pack_sums(): low.reshape(-1)]
  transfers between devices with their start and end apart: 15 -> 15, of which waited for: 10 -> 9; matrix products, arithmetic and copies ran while one was open for 14% -> 10% of each run, Pallas kernels for 0% -> 0%
where the time goes in v18:
time: 221 us; the launch traced here: 219 us
  local copies, waits for them, and re-layouts  95.1 us (43%)
  other arithmetic  74.6 us (34%)
  starting transfers between devices  19.7 us (9%)
  waiting for transfers between devices  15.9 us (7%)
  matrix products  12.5 us (6%)
    ppermute x15, starting transfers between devices, swap(): return lax.ppermute(x, axis, [(i, i ^ distance) for i in range(size)])  19.7 us
    ppermute x15, waiting for transfers between devices, swap(): return lax.ppermute(x, axis, [(i, i ^ distance) for i in range(size)])  15.9 us
    reshape x10, local copies, waits for them, and re-layouts, swap_with(): message = jnp.concatenate([payload.reshape(-1, width), packed], axis=0)  12.2 us
    another operation x14, other arithmetic  12.1 us
    unnamed x87, local copies, waits for them, and re-layouts  11.7 us
    add x11, local copies, waits for them, and re-layouts, unpack_sums(): return flat[0] + flat[1] + flat[2]  8.62 us
    reshape x6, local copies, waits for them, and re-layouts, pack_sums(): middle.reshape(-1)  7.45 us
    dot_general x2, matrix products, valid_conv(): jnp.dot(columns.reshape(-1, 27 * channels), kernel.reshape(27 * channels,...  7.16 us
  transfers between devices with their start and end apart: 15, of which 9 were waited for; matrix products, arithmetic and copies ran while one was open for 10% of the time, Pallas kernels for 0%

profile of v18, /device:TPU:0, one launch (start us, length us, event | category | flops | bytes accessed | tf_op | source)
XLA Modules:
  0.0 218.6 jit_solution(10831027990509956742)
XLA Ops:
  0.0 1.7 convert_reduce_fusion.2
  7.8 1.6 constant_dynamic-update-slice_fusion.1
  9.9 2.8 %slice_bitcast_fusion.7 = (bf16[512,256]{1,0:T(8,128)(2,1)}, bf16[512,256]{1,0:T(8,128)(2,1)}, bf16[512,256]{1,0:T(8,128)(2,1)}, bf16[512,256]{1,0:T(8,128)(2,1)...) fusion(bf16[3,3,512,256]{3,2,1,0:T(8,128)(2,1)} %param.13), kind=kLoop, calls=%fused_computation.110 | loop fusion | bytes 4194304 | tf_op jit(solution)/shard_map/squeeze | solution.py:129
  18.3 2.6 %collective-permute-start.1 = (bf16[7,512]{1,0:T(8,128)(2,1)S(1)}, bf16[7,512]{1,0:T(8,128)(2,1)S(1)}, u32[]{:S(2)}, u32[]{:S(2)}) collective-permute-start(bf16[7,512]{1,0:T(8,128)(2,1)S(1)} %pad_maximum_fusion.25), channel_id=1, source_target_pairs={{0,2},{2,0},{1,3},{3,1},{4,6},{6,4},{5,7},{7,5},{8,10},{10,8},{9,1... | collective-permute-start | bytes 21512 | tf_op jit(solution)/shard_map/ppermute | solution.py:174
  30.7 1.6 slice.736
  32.3 1.6 reshape.689
  33.9 1.6 pad_maximum_fusion.24
  35.4 4.1 %collective-permute-start.3 = (bf16[100,512]{1,0:T(8,128)(2,1)}, bf16[100,512]{1,0:T(8,128)(2,1)}, u32[]{:S(2)}, u32[]{:S(2)}) collective-permute-start(bf16[100,512]{1,0:T(8,128)(2,1)} %pad_maximum_fusion.24), channel_id=1, source_target_pairs={{0,12},{4,8},{8,4},{12,0},{1,13},{5,9},{9,5},{13,1},{2,14},{6,10},... | collective-permute-start | bytes 307208 | tf_op jit(solution)/shard_map/ppermute | solution.py:174
  41.3 1.8 collective-permute-done.3
  43.9 1.8 collective-permute-done.2
  50.4 1.6 slice_select_fusion
  51.9 1.6 select_n.168
  57.5 1.6 fusion.1
  61.4 2.2 convert_reduce_fusion.1
  71.8 2.2 collective-permute-done.5
  81.2 1.7 broadcast_select_fusion.3
  82.9 1.6 reshape.707
  84.5 1.6 broadcast_select_fusion.1
  86.0 1.6 reshape.712
  90.2 2.4 %collective-permute-start.8 = (f32[2,32]{1,0:T(2,128)S(1)}, f32[2,32]{1,0:T(2,128)}, u32[]{:S(2)}, u32[]{:S(2)}) collective-permute-start(f32[2,32]{1,0:T(2,128)S(1)} %get-tuple-element.24), channel_id=1, source_target_pairs={{0,8},{4,12},{8,0},{12,4},{1,9},{5,13},{9,1},{13,5},{2,10},{6,14},... | collective-permute-start | bytes 776 | tf_op jit(solution)/shard_map/ppermute | solution.py:174
  94.9 4.3 %collective-permute-done.7 = bf16[199,256]{1,0:T(8,128)(2,1)S(1)} collective-permute-done((bf16[199,256]{1,0:T(8,128)(2,1)S(1)}, bf16[199,256]{1,0:T(8,128)(2,1)S(1)}, u32[]{:S(2)}, u32[]{:S(2)}) %collective-permute-start.7) | collective-permute-done | bytes 101920 | tf_op jit(solution)/shard_map/ppermute | solution.py:174
  109.1 1.6 broadcast_select_fusion.7
  110.7 1.6 select_n.179
  112.3 1.6 select_n.182
  113.8 1.9 pad_maximum_fusion.4
  115.7 1.9 reshape.713
  119.5 1.7 pad_maximum_fusion.13
  129.9 1.8 slice.780
  131.7 1.9 reshape.718
  134.7 2.9 %select_convert_fusion.1 = bf16[5,6,66,256]{3,2,1,0:T(8,128)(2,1)S(1)} fusion(bf16[3,1,66,256]{3,2,1,0:T(8,128)(2,1)} %select_n.182, bf16[3,4,1,256]{3,2,1,0:T(2,128)(2,1)S(1)} %reshape.739, bf16[3,4,64,256]{3,2,1,0:T(8,128)(2,1)} %bitcast.92, bf16[3,1,66,256]{3,2,1,0:T(8,128)(2,1)} %select_n.179, bf16[2,6,66,256]{3,2,1,0:T(8,128)(2,1)S(1)} %maximum_select_fusion, ...), kind=kLoop, calls=%fused_computation.1 | loop fusion | flops 11151360 | bytes 2025868 | tf_op jit(solution)/shard_map/convert_element_type | solution.py:279
  139.8 3.5 %convert_reduce_fusion = (f32[256]{0:T(256)}, f32[256]{0:T(256)}, bf16[3,4,64,256]{3,2,1,0:T(8,128)(2,1)S(1)}) fusion(bf16[3,4,64,6912]{3,2,1,0:T(8,128)(2,1)S(1)} %slice_dynamic-update-slice_fusion.27, bf16[6912,256,1,1]{1,0,3,2:T(8,128)(2,1)S(1)} %bitcast.87), kind=kOutput, calls=%fused_computation.15 | convolution fusion | flops 2718891520 | bytes 14551040 | tf_op jit(solution)/shard_map/dot_general | solution.py:156
  150.7 2.2 collective-permute-done.10
  160.3 1.7 broadcast_select_fusion.2
  162.0 1.6 reshape.723
  163.6 1.6 broadcast_select_fusion
  165.1 1.6 reshape.728
  169.4 2.8 %collective-permute-start.12 = (bf16[199,256]{1,0:T(8,128)(2,1)S(1)}, bf16[199,256]{1,0:T(8,128)(2,1)S(1)}, u32[]{:S(2)}, u32[]{:S(2)}) collective-permute-start(bf16[199,256]{1,0:T(8,128)(2,1)S(1)} %get-tuple-element.52), channel_id=1, source_target_pairs={{0,12},{4,8},{8,4},{12,0},{1,13},{5,9},{9,5},{13,1},{2,14},{6,10},... | collective-permute-start | bytes 305672 | tf_op jit(solution)/shard_map/ppermute | solution.py:174
  173.6 2.3 %collective-permute-done.12 = bf16[199,256]{1,0:T(8,128)(2,1)S(1)} collective-permute-done((bf16[199,256]{1,0:T(8,128)(2,1)S(1)}, bf16[199,256]{1,0:T(8,128)(2,1)S(1)}, u32[]{:S(2)}, u32[]{:S(2)}) %collective-permute-start.12) | collective-permute-done | bytes 101920 | tf_op jit(solution)/shard_map/ppermute | solution.py:174
  186.1 1.6 broadcast_select_fusion.6
  187.7 1.6 select_n.189
  189.2 1.6 select_n.191
  190.8 1.9 pad_maximum_fusion
  192.7 1.9 reshape.729
  195.7 1.7 pad_maximum_fusion.12
  204.9 1.8 slice.829
  206.7 1.9 reshape.734
  209.7 3.0 %select_convert_fusion = bf16[5,6,66,256]{3,2,1,0:T(8,128)(2,1)S(1)} fusion(bf16[3,1,66,256]{3,2,1,0:T(8,128)(2,1)} %select_n.191, bf16[3,4,1,256]{3,2,1,0:T(2,128)(2,1)S(1)} %reshape.740, bf16[3,4,64,256]{3,2,1,0:T(8,128)(2,1)} %copy-done.3, bf16[3,1,66,256]{3,2,1,0:T(8,128)(2,1)} %select_n.189, bf16[2,6,66,256]{3,2,1,0:T(8,128)(2,1)S(1)} %maximum_select_fusion.1, ...), kind=kLoop, calls=%fused_computation | loop fusion | flops 11151360 | bytes 2025868 | tf_op jit(solution)/shard_map/convert_element_type | solution.py:279
  214.9 3.7 %fusion = bf16[3,4,64,256]{3,2,1,0:T(8,128)(2,1)} fusion(bf16[3,4,64,6912]{3,2,1,0:T(8,128)(2,1)S(1)} %slice_dynamic-update-slice_fusion, bf16[6912,256,1,1]{1,0,3,2:T(8,128)(2,1)S(1)} %bitcast.119, bf16[3,4,64,256]{3,2,1,0:T(8,128)(2,1)S(1)} %bitcast.93), kind=kOutput, calls=%fused_computation.4 | convolution fusion | flops 2718498816 | bytes 14942208 | tf_op jit(solution)/shard_map/dot_general | solution.py:156
  (265 shorter events, 120.2 us)
Async XLA Ops:
  0.0 139.8 %copy-start = (bf16[3,3,3,256,256]{4,3,2,1,0:T(8,128)(2,1)S(1)}, bf16[3,3,3,256,256]{4,3,2,1,0:T(8,128)(2,1)}, u32[]{:S(2)}) copy-start(bf16[3,3,3,256,256]{4,3,2,1,0:T(8,128)(2,1)} %param.16) | copy-start | bytes 10616836
  5.3 7.4 %copy-start.15 = (f32[32]{0:T(128)}, f32[32]{0:T(128)S(1)}, u32[]{:S(2)}) copy-start(f32[32]{0:T(128)S(1)} %reduce_sum.77) | copy-start | bytes 388
  6.5 6.3 %collective-permute-start = (f32[2,32]{1,0:T(2,128)}, f32[2,32]{1,0:T(2,128)}, u32[]{:S(2)}, u32[]{:S(2)}) collective-permute-start(f32[2,32]{1,0:T(2,128)} %pad_maximum_fusion.28), channel_id=1, source_target_pairs={{0,1},{1,0},{2,3},{3,2},{4,5},{5,4},{6,7},{7,6},{8,9},{9,8},{10,11... | collective-permute-start | bytes 776 | tf_op jit(solution)/shard_map/ppermute | solution.py:174
  18.3 4.2 %collective-permute-start.1 = (bf16[7,512]{1,0:T(8,128)(2,1)S(1)}, bf16[7,512]{1,0:T(8,128)(2,1)S(1)}, u32[]{:S(2)}, u32[]{:S(2)}) collective-permute-start(bf16[7,512]{1,0:T(8,128)(2,1)S(1)} %pad_maximum_fusion.25), channel_id=1, source_target_pairs={{0,2},{2,0},{1,3},{3,1},{4,6},{6,4},{5,7},{7,5},{8,10},{10,8},{9,1... | collective-permute-start | bytes 21512 | tf_op jit(solution)/shard_map/ppermute | solution.py:174
  22.5 6.9 %copy-start.12 = (bf16[7,512]{1,0:T(8,128)(2,1)}, bf16[7,512]{1,0:T(8,128)(2,1)S(1)}, u32[]{:S(2)}) copy-start(bf16[7,512]{1,0:T(8,128)(2,1)S(1)} %collective-permute-done.1) | copy-start | bytes 21508
  35.4 7.7 %collective-permute-start.3 = (bf16[100,512]{1,0:T(8,128)(2,1)}, bf16[100,512]{1,0:T(8,128)(2,1)}, u32[]{:S(2)}, u32[]{:S(2)}) collective-permute-start(bf16[100,512]{1,0:T(8,128)(2,1)} %pad_maximum_fusion.24), channel_id=1, source_target_pairs={{0,12},{4,8},{8,4},{12,0},{1,13},{5,9},{9,5},{13,1},{2,14},{6,10},... | collective-permute-start | bytes 307208 | tf_op jit(solution)/shard_map/ppermute | solution.py:174
  40.8 6.9 %collective-permute-start.4 = (f32[2,32]{1,0:T(2,128)S(1)}, f32[2,32]{1,0:T(2,128)S(1)}, u32[]{:S(2)}, u32[]{:S(2)}) collective-permute-start(f32[2,32]{1,0:T(2,128)S(1)} %get-tuple-element.27), channel_id=1, source_target_pairs={{0,8},{4,12},{8,0},{12,4},{1,9},{5,13},{9,1},{13,5},{2,10},{6,14},... | collective-permute-start | bytes 776 | tf_op jit(solution)/shard_map/ppermute | solution.py:174
  40.8 4.9 %collective-permute-start.2 = (bf16[100,512]{1,0:T(8,128)(2,1)}, bf16[100,512]{1,0:T(8,128)(2,1)S(1)}, u32[]{:S(2)}, u32[]{:S(2)}) collective-permute-start(bf16[100,512]{1,0:T(8,128)(2,1)} %pad_maximum_fusion.24), channel_id=1, source_target_pairs={{0,4},{4,0},{8,12},{12,8},{1,5},{5,1},{9,13},{13,9},{2,6},{6,2},{1... | collective-permute-start | bytes 307208 | tf_op jit(solution)/shard_map/ppermute | solution.py:174
  45.7 0.6 copy-start.6
  68.8 0.7 copy-start.1
  70.3 3.7 %collective-permute-start.5 = (bf16[13,256]{1,0:T(8,128)(2,1)S(1)}, bf16[13,256]{1,0:T(8,128)(2,1)S(1)}, u32[]{:S(2)}, u32[]{:S(2)}) collective-permute-start(bf16[13,256]{1,0:T(8,128)(2,1)S(1)} %pad_maximum_fusion.26), channel_id=1, source_target_pairs={{0,2},{2,0},{1,3},{3,1},{4,6},{6,4},{5,7},{7,5},{8,10},{10,8},{9,1... | collective-permute-start | bytes 19976 | tf_op jit(solution)/shard_map/ppermute | solution.py:174
  73.9 6.6 %copy-start.11 = (bf16[13,256]{1,0:T(8,128)(2,1)}, bf16[13,256]{1,0:T(8,128)(2,1)S(1)}, u32[]{:S(2)}) copy-start(bf16[13,256]{1,0:T(8,128)(2,1)S(1)} %collective-permute-done.5) | copy-start | bytes 19972
  88.6 5.1 %collective-permute-start.6 = (bf16[199,256]{1,0:T(8,128)(2,1)S(1)}, bf16[199,256]{1,0:T(8,128)(2,1)S(1)}, u32[]{:S(2)}, u32[]{:S(2)}) collective-permute-start(bf16[199,256]{1,0:T(8,128)(2,1)S(1)} %get-tuple-element.57), channel_id=1, source_target_pairs={{0,4},{4,0},{8,12},{12,8},{1,5},{5,1},{9,13},{13,9},{2,6},{6,2},{1... | collective-permute-start | bytes 305672 | tf_op jit(solution)/shard_map/ppermute | solution.py:174
  90.2 12.6 %collective-permute-start.8 = (f32[2,32]{1,0:T(2,128)S(1)}, f32[2,32]{1,0:T(2,128)}, u32[]{:S(2)}, u32[]{:S(2)}) collective-permute-start(f32[2,32]{1,0:T(2,128)S(1)} %get-tuple-element.24), channel_id=1, source_target_pairs={{0,8},{4,12},{8,0},{12,4},{1,9},{5,13},{9,1},{13,5},{2,10},{6,14},... | collective-permute-start | bytes 776 | tf_op jit(solution)/shard_map/ppermute | solution.py:174
  92.6 6.6 %collective-permute-start.7 = (bf16[199,256]{1,0:T(8,128)(2,1)S(1)}, bf16[199,256]{1,0:T(8,128)(2,1)S(1)}, u32[]{:S(2)}, u32[]{:S(2)}) collective-permute-start(bf16[199,256]{1,0:T(8,128)(2,1)S(1)} %get-tuple-element.58), channel_id=1, source_target_pairs={{0,12},{4,8},{8,4},{12,0},{1,13},{5,9},{9,5},{13,1},{2,14},{6,10},... | collective-permute-start | bytes 305672 | tf_op jit(solution)/shard_map/ppermute | solution.py:174
  93.6 0.6 copy-start.7
  99.1 0.6 copy-start.10
  118.6 2.5 %collective-permute-start.9 = (bf16[793,256]{1,0:T(8,128)(2,1)S(1)}, bf16[793,256]{1,0:T(8,128)(2,1)S(1)}, u32[]{:S(2)}, u32[]{:S(2)}) collective-permute-start(bf16[793,256]{1,0:T(8,128)(2,1)S(1)} %pad_maximum_fusion.8), channel_id=1, source_target_pairs={{0,1},{1,0},{2,3},{3,2},{4,5},{5,4},{6,7},{7,6},{8,9},{9,8},{10,11... | collective-permute-start | bytes 1218056 | tf_op jit(solution)/shard_map/ppermute | solution.py:174
  119.5 19.7 %copy-start.14 = (pred[6,66]{1,0:T(8,128)(4,1)}, pred[6,66]{1,0:T(8,128)(4,1)S(1)}, u32[]{:S(2)}) copy-start(pred[6,66]{1,0:T(8,128)(4,1)S(1)} %broadcast_and_fusion) | copy-start | bytes 1192
  121.2 0.8 copy-start.4
  143.4 0.7 copy-start.3
  149.2 3.7 %collective-permute-start.10 = (bf16[13,256]{1,0:T(8,128)(2,1)S(1)}, bf16[13,256]{1,0:T(8,128)(2,1)S(1)}, u32[]{:S(2)}, u32[]{:S(2)}) collective-permute-start(bf16[13,256]{1,0:T(8,128)(2,1)S(1)} %pad_maximum_fusion.27), channel_id=1, source_target_pairs={{0,2},{2,0},{1,3},{3,1},{4,6},{6,4},{5,7},{7,5},{8,10},{10,8},{9,1... | collective-permute-start | bytes 19976 | tf_op jit(solution)/shard_map/ppermute | solution.py:174
  152.8 6.7 %copy-start.13 = (bf16[13,256]{1,0:T(8,128)(2,1)}, bf16[13,256]{1,0:T(8,128)(2,1)S(1)}, u32[]{:S(2)}) copy-start(bf16[13,256]{1,0:T(8,128)(2,1)S(1)} %collective-permute-done.10) | copy-start | bytes 19972
  167.7 4.7 %collective-permute-start.11 = (bf16[199,256]{1,0:T(8,128)(2,1)S(1)}, bf16[199,256]{1,0:T(8,128)(2,1)S(1)}, u32[]{:S(2)}, u32[]{:S(2)}) collective-permute-start(bf16[199,256]{1,0:T(8,128)(2,1)S(1)} %get-tuple-element.51), channel_id=1, source_target_pairs={{0,4},{4,0},{8,12},{12,8},{1,5},{5,1},{9,13},{13,9},{2,6},{6,2},{1... | collective-permute-start | bytes 305672 | tf_op jit(solution)/shard_map/ppermute | solution.py:174
  168.5 11.2 %collective-permute-start.13 = (f32[2,32]{1,0:T(2,128)S(1)}, f32[2,32]{1,0:T(2,128)}, u32[]{:S(2)}, u32[]{:S(2)}) collective-permute-start(f32[2,32]{1,0:T(2,128)S(1)} %get-tuple-element.17), channel_id=1, source_target_pairs={{0,8},{4,12},{8,0},{12,4},{1,9},{5,13},{9,1},{13,5},{2,10},{6,14},... | collective-permute-start | bytes 776 | tf_op jit(solution)/shard_map/ppermute | solution.py:174
  169.4 6.6 %collective-permute-start.12 = (bf16[199,256]{1,0:T(8,128)(2,1)S(1)}, bf16[199,256]{1,0:T(8,128)(2,1)S(1)}, u32[]{:S(2)}, u32[]{:S(2)}) collective-permute-start(bf16[199,256]{1,0:T(8,128)(2,1)S(1)} %get-tuple-element.52), channel_id=1, source_target_pairs={{0,12},{4,8},{8,4},{12,0},{1,13},{5,9},{9,5},{13,1},{2,14},{6,10},... | collective-permute-start | bytes 305672 | tf_op jit(solution)/shard_map/ppermute | solution.py:174
  172.4 0.6 copy-start.8
  175.9 0.6 copy-start.9
  195.6 1.8 collective-permute-start.14
  197.4 0.8 copy-start.5
  212.7 2.3 %copy-start.2 = (bf16[3,2,2,64,256]{4,3,2,1,0:T(8,128)(2,1)S(1)}, bf16[3,2,2,64,256]{4,3,2,1,0:T(8,128)(2,1)}, u32[]{:S(2)}) copy-start(bf16[3,2,2,64,256]{4,3,2,1,0:T(8,128)(2,1)} %copy-done.1) | copy-start | bytes 1179652
  212.7 2.3 %copy-start.16 = (bf16[3,3,3,256,256]{4,3,2,1,0:T(8,128)(2,1)S(1)}, bf16[3,3,3,256,256]{4,3,2,1,0:T(8,128)(2,1)}, u32[]{:S(2)}) copy-start(bf16[3,3,3,256,256]{4,3,2,1,0:T(8,128)(2,1)} %param.19) | copy-start | bytes 10616836

commit v19 on v10

--- a/solution.py
+++ b/solution.py
@@ -237,20 +237,22 @@
     return sums, above, below
 
 
-def fast_conv_input(values):
+def fast_conv_input(values, gain, shift):
+    frames, height, across, _ = values.shape
     sums = local_sums(values.astype(jnp.float32))
+    sums = sums + swap(sums, "ta", 1)
     w = lax.axis_index("wa")
     s_w, beside = swap_with(sums, jnp.where(w == 0, values[:, :, -1:], values[:, :, :1]), "wa", 1)
     sums = sums + s_w
     x = jnp.concatenate([beside, values, beside], axis=2)
     sums, above, below = ha_round(sums, x[:, :1], x[:, -1:])
     x = jnp.concatenate([above, x, below], axis=1)
-    s_t, earlier = swap_with(sums, x[-2:], "ta", 1)
-    sums = sums + s_t
-    opening = jnp.concatenate([x[:1], x[:1]], axis=0)
+    act = activate(x.astype(jnp.float32), finish_stats(sums, values), gain, shift)
+    act = jnp.where(inside_mask(height + 2, across + 2, 1), act, 0.0).astype(jnp.bfloat16)
+    earlier = passed_along(act[-2:], "ta", 1)
+    opening = jnp.concatenate([act[:1], act[:1]], axis=0)
     earlier = jnp.where(lax.axis_index("ta") == 0, opening, earlier)
-    x = jnp.concatenate([earlier, x], axis=0)
-    return finish_stats(sums, values), x
+    return jnp.concatenate([earlier, act], axis=0)
 
 
 def fast_latent_input(values):
@@ -267,12 +269,12 @@
 def norm_conv(values, gain, shift, kernel):
     frames, height, across, _ = values.shape
     if fast_mesh():
-        stats, extended = fast_conv_input(values)
+        act = fast_conv_input(values, gain, shift)
     else:
         stats = group_stats(values.astype(jnp.float32))
         extended = conv_halo(values)
-    act = activate(extended.astype(jnp.float32), stats, gain, shift)
-    act = jnp.where(inside_mask(height + 2, across + 2, 1), act, 0.0).astype(jnp.bfloat16)
+        act = activate(extended.astype(jnp.float32), stats, gain, shift)
+        act = jnp.where(inside_mask(height + 2, across + 2, 1), act, 0.0).astype(jnp.bfloat16)
     return valid_conv(act, kernel, frames, height, across)
 
 

time: 77.8 us -> 78.2 us (level)
  local copies, waits for them, and re-layouts: 20.9 us -> 13 us
  starting transfers between devices: 18.3 us -> 22.9 us
  waiting for transfers between devices: 17.7 us -> 21.2 us
    unnamed x39 -> x15, local copies, waits for them, and re-layouts: 3.58 us -> 0.05 us
    ppermute x15, waiting for transfers between devices: 17.7 us -> 21.2 us  [swap(): return lax.ppermute(x, axis, [(i, i ^ distance) for i in range(size)])]
    unnamed x0 -> x16, other arithmetic: none -> 3.01 us
    slice x2, local copies, waits for them, and re-layouts: 7.42 us -> 4.43 us  [valid_conv(): kernel[step_t].reshape(9 * channels, -1)]
    ppermute x0 -> x2, starting transfers between devices: none -> 2.82 us  [passed_along(): return lax.ppermute(block, axis, route)]
    convert_element_type x2, other arithmetic: 3.58 us -> 1.24 us  [fast_conv_input(): jnp.where(inside_mask(height + 2, across + 2, 1), act, 0.0)]
    ppermute x15, starting transfers between devices: 18.3 us -> 20.1 us  [swap(): return lax.ppermute(x, axis, [(i, i ^ distance) for i in range(size)])]
  transfers between devices with their start and end apart: 15 -> 17, of which waited for: 10 -> 11; matrix products, arithmetic and copies ran while one was open for 14% -> 10% of each run, Pallas kernels for 0% -> 0%
where the time goes in v19:
time: 78.2 us; the launch traced here: 78 us
  starting transfers between devices  22.9 us (29%)
  waiting for transfers between devices  21.2 us (27%)
  local copies, waits for them, and re-layouts  13 us (17%)
  other arithmetic  11.4 us (15%)
  matrix products  8.58 us (11%)
  between operations  0.87 us (1%)
    ppermute x15, waiting for transfers between devices, swap(): return lax.ppermute(x, axis, [(i, i ^ distance) for i in range(size)])  21.2 us
    ppermute x15, starting transfers between devices, swap(): return lax.ppermute(x, axis, [(i, i ^ distance) for i in range(size)])  20.1 us
    dot_general x6, matrix products, valid_conv(): jnp.dot(window, kernel[step_t].reshape(9 * channels, -1), preferred_eleme...  6.51 us
    slice x2, local copies, waits for them, and re-layouts, valid_conv(): kernel[step_t].reshape(9 * channels, -1)  4.43 us
    unnamed x16, other arithmetic  3.01 us
    ppermute x2, starting transfers between devices, passed_along(): return lax.ppermute(block, axis, route)  2.82 us
    reduce_sum x5, other arithmetic, local_sums(): jnp.sum(grouped, axis=(0, 2))  2.18 us
    dot_general x4, matrix products, upsample(): dot = lambda v, w: jnp.dot(flat(v), w, preferred_element_type=jnp.float32)  2.07 us
  transfers between devices with their start and end apart: 17, of which 11 were waited for; matrix products, arithmetic and copies ran while one was open for 10% of the time, Pallas kernels for 0%

profile of v19, /device:TPU:0, one launch (start us, length us, event | category | flops | bytes accessed | tf_op | source)
XLA Modules:
  0.0 78.0 jit_solution(11662829536529329458)
XLA Ops:
  0.0 1.0 %convert_reduce_fusion.2 = (f32[512]{0:T(512)S(1)}, f32[512]{0:T(512)S(1)}) fusion(bf16[3,2,32,512]{3,2,1,0:T(8,128)(2,1)} %param.10), kind=kLoop, calls=%fused_computation.102 | loop fusion | flops 392192 | bytes 200704 | tf_op jit(solution)/shard_map/reduce_sum | solution.py:179
  1.4 0.5 collective-permute-start
  2.0 1.7 %slice_bitcast_fusion.7 = (bf16[512,256]{1,0:T(8,128)(2,1)S(1)}, bf16[512,256]{1,0:T(8,128)(2,1)S(1)}, bf16[512,256]{1,0:T(8,128)(2,1)S(1)}, bf16[512,256]{1,0:T...) fusion(bf16[3,3,512,256]{3,2,1,0:T(8,128)(2,1)} %param.13), kind=kLoop, calls=%fused_computation.117 | loop fusion | bytes 4194304 | tf_op jit(solution)/shard_map/squeeze | solution.py:129
  4.2 2.6 %collective-permute-start.1 = (bf16[7,512]{1,0:T(8,128)(2,1)S(1)}, bf16[7,512]{1,0:T(8,128)(2,1)S(1)}, u32[]{:S(2)}, u32[]{:S(2)}) collective-permute-start(bf16[7,512]{1,0:T(8,128)(2,1)S(1)} %pad_maximum_fusion.15), channel_id=1, source_target_pairs={{0,2},{2,0},{1,3},{3,1},{4,6},{6,4},{5,7},{7,5},{8,10},{10,8},{9,1... | collective-permute-start | bytes 21512 | tf_op jit(solution)/shard_map/ppermute | solution.py:170
  6.8 1.6 %collective-permute-done.1 = bf16[7,512]{1,0:T(8,128)(2,1)S(1)} collective-permute-done((bf16[7,512]{1,0:T(8,128)(2,1)S(1)}, bf16[7,512]{1,0:T(8,128)(2,1)S(1)}, u32[]{:S(2)}, u32[]{:S(2)}) %collective-permute-start.1) | collective-permute-done | bytes 7200 | tf_op jit(solution)/shard_map/ppermute | solution.py:170
  9.1 2.2 %collective-permute-start.2 = (bf16[100,512]{1,0:T(8,128)(2,1)S(1)}, bf16[100,512]{1,0:T(8,128)(2,1)S(1)}, u32[]{:S(2)}, u32[]{:S(2)}) collective-permute-start(bf16[100,512]{1,0:T(8,128)(2,1)S(1)} %pad_maximum_fusion.14), channel_id=1, source_target_pairs={{0,4},{4,0},{8,12},{12,8},{1,5},{5,1},{9,13},{13,9},{2,6},{6,2},{1... | collective-permute-start | bytes 307208 | tf_op jit(solution)/shard_map/ppermute | solution.py:170
  11.3 2.5 %collective-permute-start.3 = (bf16[100,512]{1,0:T(8,128)(2,1)S(1)}, bf16[100,512]{1,0:T(8,128)(2,1)S(1)}, u32[]{:S(2)}, u32[]{:S(2)}) collective-permute-start(bf16[100,512]{1,0:T(8,128)(2,1)S(1)} %pad_maximum_fusion.14), channel_id=1, source_target_pairs={{0,12},{4,8},{8,4},{12,0},{1,13},{5,9},{9,5},{13,1},{2,14},{6,10},... | collective-permute-start | bytes 307208 | tf_op jit(solution)/shard_map/ppermute | solution.py:170
  14.2 4.1 %collective-permute-done.3 = bf16[100,512]{1,0:T(8,128)(2,1)S(1)} collective-permute-done((bf16[100,512]{1,0:T(8,128)(2,1)S(1)}, bf16[100,512]{1,0:T(8,128)(2,1)S(1)}, u32[]{:S(2)}, u32[]{:S(2)}) %collective-permute-start.3) | collective-permute-done | bytes 102432 | tf_op jit(solution)/shard_map/ppermute | solution.py:170
  19.0 0.3 select_convert_fusion.2
  19.4 0.3 fusion.45
  19.7 0.3 fusion.49
  19.9 0.4 fusion.1
  20.7 1.2 %convolution_add_fusion.4 = bf16[192,256]{1,0:T(8,128)(2,1)S(1)} fusion(bf16[192,512]{1,0:T(8,128)(2,1)S(1)} %bitcast.118, bf16[3,3,512,256]{3,2,1,0:T(8,128)(2,1)} %param.13, f32[192,512]{1,0:T(8,128)S(1)} %fusion.49, f32[192,512]{1,0:T(8,128)S(1)} %fusion.45, f32[192,1024]{1,0:T(8,128)S(1)} %fusion.1), kind=kOutput, calls=%fused_computation.39 | convolution fusion | flops 50528256 | bytes 1146880 | tf_op jit(solution)/shard_map/dot_general | solution.py:123
  22.6 0.8 %convert_reduce_fusion.1 = (f32[256]{0:T(256)S(1)}, f32[256]{0:T(256)S(1)}, bf16[3,2,2,64,256]{4,1,3,0,2:T(2,128)(2,1)S(1)}) fusion(bf16[3,2,1,64,256]{4,1,3,0,2:T(2,128)(2,1)S(1)} %bitcast.121, bf16[3,2,1,64,256]{4,1,3,0,2:T(2,128)(2,1)S(1)} %bitcast.120), kind=kLoop, calls=%fused_computation.51 | loop fusion | flops 982528 | bytes 788480 | tf_op jit(solution)/shard_map/reduce_sum | solution.py:179
  24.0 1.1 %collective-permute-done.5 = f32[2,32]{1,0:T(2,128)S(1)} collective-permute-done((f32[2,32]{1,0:T(2,128)S(1)}, f32[2,32]{1,0:T(2,128)S(1)}, u32[]{:S(2)}, u32[]{:S(2)}) %collective-permute-start.5) | collective-permute-done | bytes 288 | tf_op jit(solution)/shard_map/ppermute | solution.py:170
  25.5 1.5 %collective-permute-start.6 = (bf16[13,256]{1,0:T(8,128)(2,1)S(1)}, bf16[13,256]{1,0:T(8,128)(2,1)S(1)}, u32[]{:S(2)}, u32[]{:S(2)}) collective-permute-start(bf16[13,256]{1,0:T(8,128)(2,1)S(1)} %pad_maximum_fusion.16), channel_id=1, source_target_pairs={{0,2},{2,0},{1,3},{3,1},{4,6},{6,4},{5,7},{7,5},{8,10},{10,8},{9,1... | collective-permute-start | bytes 19976 | tf_op jit(solution)/shard_map/ppermute | solution.py:170
  27.0 2.2 %collective-permute-done.6 = bf16[13,256]{1,0:T(8,128)(2,1)S(1)} collective-permute-done((bf16[13,256]{1,0:T(8,128)(2,1)S(1)}, bf16[13,256]{1,0:T(8,128)(2,1)S(1)}, u32[]{:S(2)}, u32[]{:S(2)}) %collective-permute-start.6) | collective-permute-done | bytes 6688 | tf_op jit(solution)/shard_map/ppermute | solution.py:170
  30.0 0.7 collective-permute-start.7
  30.7 2.6 %collective-permute-start.9 = (f32[2,32]{1,0:T(2,128)S(1)}, f32[2,32]{1,0:T(2,128)S(1)}, u32[]{:S(2)}, u32[]{:S(2)}) collective-permute-start(f32[2,32]{1,0:T(2,128)S(1)} %get-tuple-element.22), channel_id=1, source_target_pairs={{0,8},{4,12},{8,0},{12,4},{1,9},{5,13},{9,1},{13,5},{2,10},{6,14},... | collective-permute-start | bytes 776 | tf_op jit(solution)/shard_map/ppermute | solution.py:170
  33.3 1.2 %collective-permute-start.8 = (bf16[199,256]{1,0:T(8,128)(2,1)S(1)}, bf16[199,256]{1,0:T(8,128)(2,1)S(1)}, u32[]{:S(2)}, u32[]{:S(2)}) collective-permute-start(bf16[199,256]{1,0:T(8,128)(2,1)S(1)} %get-tuple-element.68), channel_id=1, source_target_pairs={{0,12},{4,8},{8,4},{12,0},{1,13},{5,9},{9,5},{13,1},{2,14},{6,10},... | collective-permute-start | bytes 305672 | tf_op jit(solution)/shard_map/ppermute | solution.py:170
  34.8 4.9 %collective-permute-done.8 = bf16[199,256]{1,0:T(8,128)(2,1)S(1)} collective-permute-done((bf16[199,256]{1,0:T(8,128)(2,1)S(1)}, bf16[199,256]{1,0:T(8,128)(2,1)S(1)}, u32[]{:S(2)}, u32[]{:S(2)}) %collective-permute-start.8) | collective-permute-done | bytes 101920 | tf_op jit(solution)/shard_map/ppermute | solution.py:170
  40.5 0.6 select_convert_fusion.1
  41.1 1.5 %collective-permute-start.10 = (bf16[2,6,66,256]{3,2,1,0:T(8,128)(2,1)S(1)}, bf16[2,6,66,256]{3,2,1,0:T(8,128)(2,1)S(1)}, u32[]{:S(2)}, u32[]{:S(2)}) collective-permute-start(bf16[2,6,66,256]{3,2,1,0:T(8,128)(2,1)S(1)} %slice.621), channel_id=1, source_target_pairs={{0,1},{2,3},{4,5},{6,7},{8,9},{10,11},{12,13},{14,15},{16,17},{18,... | collective-permute-start | bytes 1216520 | tf_op jit(solution)/shard_map/ppermute | solution.py:15
  42.7 2.2 %fusion.133 = (bf16[1,3,3,256,256]{4,3,2,1,0:T(8,128)(2,1)S(1)}, bf16[1,3,3,256,256]{4,3,2,1,0:T(8,128)(2,1)S(1)}, bf16[1,3,3,256,256]{4,3,2,1,0:T(8,128)(2,1)S(1)}) fusion(bf16[3,3,3,256,256]{4,3,2,1,0:T(8,128)(2,1)} %param.16), kind=kLoop, calls=%fused_computation.289 | loop fusion | bytes 7077888 | tf_op jit(solution)/shard_map/slice | solution.py:154
  45.0 0.3 fusion.32
  45.6 0.3 fusion.38
  46.8 1.0 %fusion.131 = (bf16[3,4,64,2304]{3,2,1,0:T(8,128)(2,1)S(1)}, bf16[3,4,64,2304]{3,2,1,0:T(8,128)(2,1)S(1)}, bf16[3,4,64,2304]{3,2,1,0:T(8,128)(2,1)S(1)}) fusion(bf16[5,4,64,2304]{3,2,1,0:T(8,128)(2,1)S(1)} %fusion.44), kind=kLoop, calls=%fused_computation.287 | loop fusion | bytes 21233664 | tf_op jit(solution)/shard_map/slice | solution.py:152
  47.8 1.1 %fusion.136 = f32[768,256]{1,0:T(8,128)S(1)} fusion(bf16[768,2304]{1,0:T(8,128)(2,1)S(1)} %bitcast.107, bf16[2304,256]{1,0:T(8,128)(2,1)S(1)} %bitcast.117), kind=kOutput, calls=%fused_computation.292 | convolution fusion | flops 905969664 | bytes 5505024 | tf_op jit(solution)/shard_map/dot_general | solution.py:153
  48.9 1.1 %convolution_add_fusion.3 = f32[768,256]{1,0:T(8,128)S(1)} fusion(f32[768,256]{1,0:T(8,128)S(1)} %fusion.136, bf16[768,2304]{1,0:T(8,128)(2,1)S(1)} %bitcast.105, bf16[2304,256]{1,0:T(8,128)(2,1)S(1)} %bitcast.115), kind=kOutput, calls=%fused_computation.37 | convolution fusion | flops 906166272 | bytes 6291456 | tf_op jit(solution)/shard_map/dot_general | solution.py:153
  50.0 1.1 %convert_reduce_fusion = (f32[256]{0:T(256)S(1)}, f32[256]{0:T(256)S(1)}, bf16[768,256]{1,0:T(8,128)(2,1)S(1)}) fusion(f32[768,256]{1,0:T(8,128)S(1)} %convolution_add_fusion.3, bf16[768,2304]{1,0:T(8,128)(2,1)S(1)} %bitcast.103, bf16[2304,256]{1,0:T(8,128)(2,1)S(1)} %bitcast.112), kind=kOutput, calls=%fused_computation.49 | convolution fusion | flops 907148800 | bytes 5900288 | tf_op jit(solution)/shard_map/dot_general | solution.py:153
  51.6 1.1 %collective-permute-done.11 = f32[2,32]{1,0:T(2,128)S(1)} collective-permute-done((f32[2,32]{1,0:T(2,128)S(1)}, f32[2,32]{1,0:T(2,128)S(1)}, u32[]{:S(2)}, u32[]{:S(2)}) %collective-permute-start.11) | collective-permute-done | bytes 288 | tf_op jit(solution)/shard_map/ppermute | solution.py:170
  53.1 1.5 %collective-permute-start.12 = (bf16[13,256]{1,0:T(8,128)(2,1)S(1)}, bf16[13,256]{1,0:T(8,128)(2,1)S(1)}, u32[]{:S(2)}, u32[]{:S(2)}) collective-permute-start(bf16[13,256]{1,0:T(8,128)(2,1)S(1)} %pad_maximum_fusion.17), channel_id=1, source_target_pairs={{0,2},{2,0},{1,3},{3,1},{4,6},{6,4},{5,7},{7,5},{8,10},{10,8},{9,1... | collective-permute-start | bytes 19976 | tf_op jit(solution)/shard_map/ppermute | solution.py:170
  54.6 2.2 %collective-permute-done.12 = bf16[13,256]{1,0:T(8,128)(2,1)S(1)} collective-permute-done((bf16[13,256]{1,0:T(8,128)(2,1)S(1)}, bf16[13,256]{1,0:T(8,128)(2,1)S(1)}, u32[]{:S(2)}, u32[]{:S(2)}) %collective-permute-start.12) | collective-permute-done | bytes 6688 | tf_op jit(solution)/shard_map/ppermute | solution.py:170
  57.7 1.8 %collective-permute-start.15 = (f32[2,32]{1,0:T(2,128)S(1)}, f32[2,32]{1,0:T(2,128)S(1)}, u32[]{:S(2)}, u32[]{:S(2)}) collective-permute-start(f32[2,32]{1,0:T(2,128)S(1)} %get-tuple-element.15), channel_id=1, source_target_pairs={{0,8},{4,12},{8,0},{12,4},{1,9},{5,13},{9,1},{13,5},{2,10},{6,14},... | collective-permute-start | bytes 776 | tf_op jit(solution)/shard_map/ppermute | solution.py:170
  59.5 2.6 %collective-permute-start.14 = (bf16[199,256]{1,0:T(8,128)(2,1)S(1)}, bf16[199,256]{1,0:T(8,128)(2,1)S(1)}, u32[]{:S(2)}, u32[]{:S(2)}) collective-permute-start(bf16[199,256]{1,0:T(8,128)(2,1)S(1)} %get-tuple-element.62), channel_id=1, source_target_pairs={{0,12},{4,8},{8,4},{12,0},{1,13},{5,9},{9,5},{13,1},{2,14},{6,10},... | collective-permute-start | bytes 305672 | tf_op jit(solution)/shard_map/ppermute | solution.py:170
  62.0 0.3 collective-permute-done.13
  62.5 3.4 %collective-permute-done.14 = bf16[199,256]{1,0:T(8,128)(2,1)S(1)} collective-permute-done((bf16[199,256]{1,0:T(8,128)(2,1)S(1)}, bf16[199,256]{1,0:T(8,128)(2,1)S(1)}, u32[]{:S(2)}, u32[]{:S(2)}) %collective-permute-start.14) | collective-permute-done | bytes 101920 | tf_op jit(solution)/shard_map/ppermute | solution.py:170
  66.7 0.6 select_convert_fusion
  67.3 1.3 %collective-permute-start.16 = (bf16[2,6,66,256]{3,2,1,0:T(8,128)(2,1)S(1)}, bf16[2,6,66,256]{3,2,1,0:T(8,128)(2,1)S(1)}, u32[]{:S(2)}, u32[]{:S(2)}) collective-permute-start(bf16[2,6,66,256]{3,2,1,0:T(8,128)(2,1)S(1)} %slice.659), channel_id=1, source_target_pairs={{0,1},{2,3},{4,5},{6,7},{8,9},{10,11},{12,13},{14,15},{16,17},{18,... | collective-permute-start | bytes 1216520 | tf_op jit(solution)/shard_map/ppermute | solution.py:15
  68.6 2.2 %fusion.132 = (bf16[1,3,3,256,256]{4,3,2,1,0:T(8,128)(2,1)S(1)}, bf16[1,3,3,256,256]{4,3,2,1,0:T(8,128)(2,1)S(1)}, bf16[1,3,3,256,256]{4,3,2,1,0:T(8,128)(2,1)S(1)}) fusion(bf16[3,3,3,256,256]{4,3,2,1,0:T(8,128)(2,1)} %param.19), kind=kLoop, calls=%fused_computation.288 | loop fusion | bytes 7077888 | tf_op jit(solution)/shard_map/slice | solution.py:154
  71.0 0.3 fusion.16
  71.6 0.3 fusion.22
  72.3 0.3 fusion.12
  72.8 1.0 %fusion.130 = (bf16[3,4,64,2304]{3,2,1,0:T(8,128)(2,1)S(1)}, bf16[3,4,64,2304]{3,2,1,0:T(8,128)(2,1)S(1)}, bf16[3,4,64,2304]{3,2,1,0:T(8,128)(2,1)S(1)}) fusion(bf16[5,4,64,2304]{3,2,1,0:T(8,128)(2,1)S(1)} %fusion.43), kind=kLoop, calls=%fused_computation.286 | loop fusion | bytes 21233664 | tf_op jit(solution)/shard_map/slice | solution.py:152
  73.8 1.1 %fusion.137 = f32[768,256]{1,0:T(8,128)S(1)} fusion(bf16[768,2304]{1,0:T(8,128)(2,1)S(1)} %bitcast.108, bf16[2304,256]{1,0:T(8,128)(2,1)S(1)} %bitcast.116), kind=kOutput, calls=%fused_computation.293 | convolution fusion | flops 905969664 | bytes 5505024 | tf_op jit(solution)/shard_map/dot_general | solution.py:153
  74.9 1.1 %convolution_add_fusion.1 = f32[768,256]{1,0:T(8,128)S(1)} fusion(f32[768,256]{1,0:T(8,128)S(1)} %fusion.137, bf16[768,2304]{1,0:T(8,128)(2,1)S(1)} %bitcast.106, bf16[2304,256]{1,0:T(8,128)(2,1)S(1)} %bitcast.114), kind=kOutput, calls=%fused_computation.35 | convolution fusion | flops 906166272 | bytes 6291456 | tf_op jit(solution)/shard_map/dot_general | solution.py:153
  76.0 1.1 %convolution_add_fusion = f32[768,256]{1,0:T(8,128)S(1)} fusion(f32[768,256]{1,0:T(8,128)S(1)} %convolution_add_fusion.1, bf16[768,2304]{1,0:T(8,128)(2,1)S(1)} %bitcast.104, bf16[2304,256]{1,0:T(8,128)(2,1)S(1)} %bitcast.113), kind=kOutput, calls=%fused_computation.34 | convolution fusion | flops 906166272 | bytes 6291456 | tf_op jit(solution)/shard_map/dot_general | solution.py:153
  77.1 0.9 %add_convert_fusion = bf16[3,4,64,256]{3,2,1,0:T(8,128)(2,1)} fusion(f32[3,4,64,256]{3,2,1,0:T(8,128)S(1)} %bitcast.119, bf16[3,4,64,256]{3,2,1,0:T(8,128)(2,1)S(1)} %bitcast.102), kind=kLoop, calls=%fused_computation.55 | loop fusion | flops 589824 | bytes 1572864 | tf_op jit(solution)/shard_map/convert_element_type | solution.py:304
  (200 shorter events, 11.6 us)
Async XLA Ops:
  1.4 2.4 %collective-permute-start = (f32[2,32]{1,0:T(2,128)S(1)}, f32[2,32]{1,0:T(2,128)S(1)}, u32[]{:S(2)}, u32[]{:S(2)}) collective-permute-start(f32[2,32]{1,0:T(2,128)S(1)} %pad_maximum_fusion.18), channel_id=1, source_target_pairs={{0,1},{1,0},{2,3},{3,2},{4,5},{5,4},{6,7},{7,6},{8,9},{9,8},{10,11... | collective-permute-start | bytes 776 | tf_op jit(solution)/shard_map/ppermute | solution.py:170
  1.9 1.8 %copy-start = (bf16[3,2,32,512]{3,2,1,0:T(8,128)(2,1)S(1)}, bf16[3,2,32,512]{3,2,1,0:T(8,128)(2,1)}, u32[]{:S(2)}) copy-start(bf16[3,2,32,512]{3,2,1,0:T(8,128)(2,1)} %param.10) | copy-start | bytes 589828
  3.6 15.3 %copy-start.1 = (f32[512]{0:T(512)S(1)}, f32[512]{0:T(512)}, u32[]{:S(2)}) copy-start(f32[512]{0:T(512)} %param.12) | copy-start | bytes 6148
  3.6 15.3 %copy-start.2 = (f32[512]{0:T(512)S(1)}, f32[512]{0:T(512)}, u32[]{:S(2)}) copy-start(f32[512]{0:T(512)} %param.11) | copy-start | bytes 6148
  4.2 4.2 %collective-permute-start.1 = (bf16[7,512]{1,0:T(8,128)(2,1)S(1)}, bf16[7,512]{1,0:T(8,128)(2,1)S(1)}, u32[]{:S(2)}, u32[]{:S(2)}) collective-permute-start(bf16[7,512]{1,0:T(8,128)(2,1)S(1)} %pad_maximum_fusion.15), channel_id=1, source_target_pairs={{0,2},{2,0},{1,3},{3,1},{4,6},{6,4},{5,7},{7,5},{8,10},{10,8},{9,1... | collective-permute-start | bytes 21512 | tf_op jit(solution)/shard_map/ppermute | solution.py:170
  9.1 5.0 %collective-permute-start.2 = (bf16[100,512]{1,0:T(8,128)(2,1)S(1)}, bf16[100,512]{1,0:T(8,128)(2,1)S(1)}, u32[]{:S(2)}, u32[]{:S(2)}) collective-permute-start(bf16[100,512]{1,0:T(8,128)(2,1)S(1)} %pad_maximum_fusion.14), channel_id=1, source_target_pairs={{0,4},{4,0},{8,12},{12,8},{1,5},{5,1},{9,13},{13,9},{2,6},{6,2},{1... | collective-permute-start | bytes 307208 | tf_op jit(solution)/shard_map/ppermute | solution.py:170
  11.3 7.0 %collective-permute-start.3 = (bf16[100,512]{1,0:T(8,128)(2,1)S(1)}, bf16[100,512]{1,0:T(8,128)(2,1)S(1)}, u32[]{:S(2)}, u32[]{:S(2)}) collective-permute-start(bf16[100,512]{1,0:T(8,128)(2,1)S(1)} %pad_maximum_fusion.14), channel_id=1, source_target_pairs={{0,12},{4,8},{8,4},{12,0},{1,13},{5,9},{9,5},{13,1},{2,14},{6,10},... | collective-permute-start | bytes 307208 | tf_op jit(solution)/shard_map/ppermute | solution.py:170
  13.7 4.8 %collective-permute-start.4 = (f32[2,32]{1,0:T(2,128)S(1)}, f32[2,32]{1,0:T(2,128)S(1)}, u32[]{:S(2)}, u32[]{:S(2)}) collective-permute-start(f32[2,32]{1,0:T(2,128)S(1)} %get-tuple-element.27), channel_id=1, source_target_pairs={{0,8},{4,12},{8,0},{12,4},{1,9},{5,13},{9,1},{13,5},{2,10},{6,14},... | collective-permute-start | bytes 776 | tf_op jit(solution)/shard_map/ppermute | solution.py:170
  23.9 1.2 %collective-permute-start.5 = (f32[2,32]{1,0:T(2,128)S(1)}, f32[2,32]{1,0:T(2,128)S(1)}, u32[]{:S(2)}, u32[]{:S(2)}) collective-permute-start(f32[2,32]{1,0:T(2,128)S(1)} %pad_maximum_fusion.19), channel_id=1, source_target_pairs={{0,1},{1,0},{2,3},{3,2},{4,5},{5,4},{6,7},{7,6},{8,9},{9,8},{10,11... | collective-permute-start | bytes 776 | tf_op jit(solution)/shard_map/ppermute | solution.py:170
  25.5 3.7 %collective-permute-start.6 = (bf16[13,256]{1,0:T(8,128)(2,1)S(1)}, bf16[13,256]{1,0:T(8,128)(2,1)S(1)}, u32[]{:S(2)}, u32[]{:S(2)}) collective-permute-start(bf16[13,256]{1,0:T(8,128)(2,1)S(1)} %pad_maximum_fusion.16), channel_id=1, source_target_pairs={{0,2},{2,0},{1,3},{3,1},{4,6},{6,4},{5,7},{7,5},{8,10},{10,8},{9,1... | collective-permute-start | bytes 19976 | tf_op jit(solution)/shard_map/ppermute | solution.py:170
  29.2 11.3 %copy-start.3 = (f32[256]{0:T(256)S(1)}, f32[256]{0:T(256)}, u32[]{:S(2)}) copy-start(f32[256]{0:T(256)} %param.15) | copy-start | bytes 3076
  29.2 11.3 %copy-start.4 = (f32[256]{0:T(256)S(1)}, f32[256]{0:T(256)}, u32[]{:S(2)}) copy-start(f32[256]{0:T(256)} %param.14) | copy-start | bytes 3076
  30.0 4.7 %collective-permute-start.7 = (bf16[199,256]{1,0:T(8,128)(2,1)S(1)}, bf16[199,256]{1,0:T(8,128)(2,1)S(1)}, u32[]{:S(2)}, u32[]{:S(2)}) collective-permute-start(bf16[199,256]{1,0:T(8,128)(2,1)S(1)} %get-tuple-element.67), channel_id=1, source_target_pairs={{0,4},{4,0},{8,12},{12,8},{1,5},{5,1},{9,13},{13,9},{2,6},{6,2},{1... | collective-permute-start | bytes 305672 | tf_op jit(solution)/shard_map/ppermute | solution.py:170
  30.7 9.3 %collective-permute-start.9 = (f32[2,32]{1,0:T(2,128)S(1)}, f32[2,32]{1,0:T(2,128)S(1)}, u32[]{:S(2)}, u32[]{:S(2)}) collective-permute-start(f32[2,32]{1,0:T(2,128)S(1)} %get-tuple-element.22), channel_id=1, source_target_pairs={{0,8},{4,12},{8,0},{12,4},{1,9},{5,13},{9,1},{13,5},{2,10},{6,14},... | collective-permute-start | bytes 776 | tf_op jit(solution)/shard_map/ppermute | solution.py:170
  33.3 6.5 %collective-permute-start.8 = (bf16[199,256]{1,0:T(8,128)(2,1)S(1)}, bf16[199,256]{1,0:T(8,128)(2,1)S(1)}, u32[]{:S(2)}, u32[]{:S(2)}) collective-permute-start(bf16[199,256]{1,0:T(8,128)(2,1)S(1)} %get-tuple-element.68), channel_id=1, source_target_pairs={{0,12},{4,8},{8,4},{12,0},{1,13},{5,9},{9,5},{13,1},{2,14},{6,10},... | collective-permute-start | bytes 305672 | tf_op jit(solution)/shard_map/ppermute | solution.py:170
  41.1 3.8 %collective-permute-start.10 = (bf16[2,6,66,256]{3,2,1,0:T(8,128)(2,1)S(1)}, bf16[2,6,66,256]{3,2,1,0:T(8,128)(2,1)S(1)}, u32[]{:S(2)}, u32[]{:S(2)}) collective-permute-start(bf16[2,6,66,256]{3,2,1,0:T(8,128)(2,1)S(1)} %slice.621), channel_id=1, source_target_pairs={{0,1},{2,3},{4,5},{6,7},{8,9},{10,11},{12,13},{14,15},{16,17},{18,... | collective-permute-start | bytes 1216520 | tf_op jit(solution)/shard_map/ppermute | solution.py:15
  51.5 1.2 %collective-permute-start.11 = (f32[2,32]{1,0:T(2,128)S(1)}, f32[2,32]{1,0:T(2,128)S(1)}, u32[]{:S(2)}, u32[]{:S(2)}) collective-permute-start(f32[2,32]{1,0:T(2,128)S(1)} %pad_maximum_fusion.20), channel_id=1, source_target_pairs={{0,1},{1,0},{2,3},{3,2},{4,5},{5,4},{6,7},{7,6},{8,9},{9,8},{10,11... | collective-permute-start | bytes 776 | tf_op jit(solution)/shard_map/ppermute | solution.py:170
  53.1 3.7 %collective-permute-start.12 = (bf16[13,256]{1,0:T(8,128)(2,1)S(1)}, bf16[13,256]{1,0:T(8,128)(2,1)S(1)}, u32[]{:S(2)}, u32[]{:S(2)}) collective-permute-start(bf16[13,256]{1,0:T(8,128)(2,1)S(1)} %pad_maximum_fusion.17), channel_id=1, source_target_pairs={{0,2},{2,0},{1,3},{3,1},{4,6},{6,4},{5,7},{7,5},{8,10},{10,8},{9,1... | collective-permute-start | bytes 19976 | tf_op jit(solution)/shard_map/ppermute | solution.py:170
  56.8 9.8 %copy-start.5 = (f32[256]{0:T(256)S(1)}, f32[256]{0:T(256)}, u32[]{:S(2)}) copy-start(f32[256]{0:T(256)} %param.18) | copy-start | bytes 3076
  56.8 9.8 %copy-start.6 = (f32[256]{0:T(256)S(1)}, f32[256]{0:T(256)}, u32[]{:S(2)}) copy-start(f32[256]{0:T(256)} %param.17) | copy-start | bytes 3076
  57.6 4.8 %collective-permute-start.13 = (bf16[199,256]{1,0:T(8,128)(2,1)S(1)}, bf16[199,256]{1,0:T(8,128)(2,1)S(1)}, u32[]{:S(2)}, u32[]{:S(2)}) collective-permute-start(bf16[199,256]{1,0:T(8,128)(2,1)S(1)} %get-tuple-element.61), channel_id=1, source_target_pairs={{0,4},{4,0},{8,12},{12,8},{1,5},{5,1},{9,13},{13,9},{2,6},{6,2},{1... | collective-permute-start | bytes 305672 | tf_op jit(solution)/shard_map/ppermute | solution.py:170
  57.7 8.5 %collective-permute-start.15 = (f32[2,32]{1,0:T(2,128)S(1)}, f32[2,32]{1,0:T(2,128)S(1)}, u32[]{:S(2)}, u32[]{:S(2)}) collective-permute-start(f32[2,32]{1,0:T(2,128)S(1)} %get-tuple-element.15), channel_id=1, source_target_pairs={{0,8},{4,12},{8,0},{12,4},{1,9},{5,13},{9,1},{13,5},{2,10},{6,14},... | collective-permute-start | bytes 776 | tf_op jit(solution)/shard_map/ppermute | solution.py:170
  59.5 6.5 %collective-permute-start.14 = (bf16[199,256]{1,0:T(8,128)(2,1)S(1)}, bf16[199,256]{1,0:T(8,128)(2,1)S(1)}, u32[]{:S(2)}, u32[]{:S(2)}) collective-permute-start(bf16[199,256]{1,0:T(8,128)(2,1)S(1)} %get-tuple-element.62), channel_id=1, source_target_pairs={{0,12},{4,8},{8,4},{12,0},{1,13},{5,9},{9,5},{13,1},{2,14},{6,10},... | collective-permute-start | bytes 305672 | tf_op jit(solution)/shard_map/ppermute | solution.py:170
  67.3 3.6 %collective-permute-start.16 = (bf16[2,6,66,256]{3,2,1,0:T(8,128)(2,1)S(1)}, bf16[2,6,66,256]{3,2,1,0:T(8,128)(2,1)S(1)}, u32[]{:S(2)}, u32[]{:S(2)}) collective-permute-start(bf16[2,6,66,256]{3,2,1,0:T(8,128)(2,1)S(1)} %slice.659), channel_id=1, source_target_pairs={{0,1},{2,3},{4,5},{6,7},{8,9},{10,11},{12,13},{14,15},{16,17},{18,... | collective-permute-start | bytes 1216520 | tf_op jit(solution)/shard_map/ppermute | solution.py:15

commit v20 on v10

--- a/solution.py
+++ b/solution.py
@@ -142,12 +142,11 @@
     return jnp.concatenate([even, odd], axis=2).reshape(frames, 2 * height, 2 * across, out)
 
 
-def valid_conv(padded, kernel, frames, height, across):
+def valid_conv(padded, kernel, frames, height, across, result=None):
     channels = padded.shape[-1]
     wide = jnp.concatenate(
         [padded[:, dy : dy + height, dx : dx + across] for dy in range(3) for dx in range(3)], axis=-1
     )
-    result = None
     for step_t in range(3):
         window = wide[step_t : step_t + frames].reshape(-1, 9 * channels)
         part = jnp.dot(
@@ -264,7 +263,7 @@
     return finish_stats(sums, values), x
 
 
-def norm_conv(values, gain, shift, kernel):
+def norm_conv(values, gain, shift, kernel, result=None):
     frames, height, across, _ = values.shape
     if fast_mesh():
         stats, extended = fast_conv_input(values)
@@ -273,7 +272,7 @@
         extended = conv_halo(values)
     act = activate(extended.astype(jnp.float32), stats, gain, shift)
     act = jnp.where(inside_mask(height + 2, across + 2, 1), act, 0.0).astype(jnp.bfloat16)
-    return valid_conv(act, kernel, frames, height, across)
+    return valid_conv(act, kernel, frames, height, across, result)
 
 
 def per_device(
@@ -298,8 +297,9 @@
     activated = jnp.where(inside_mask(height + 1, across + 1, 0), activated, 0.0)
     lifted = upsample(activated.astype(jnp.bfloat16), up_weight).astype(jnp.bfloat16)
     hidden = norm_conv(lifted, norm2_gain, norm2_shift, conv_a).astype(jnp.bfloat16)
-    branch = norm_conv(hidden, norm3_gain, norm3_shift, conv_b)
-    return (lifted.astype(jnp.float32) + branch).astype(jnp.bfloat16)
+    residual = lifted.astype(jnp.float32).reshape(-1, lifted.shape[-1])
+    decoded = norm_conv(hidden, norm3_gain, norm3_shift, conv_b, residual)
+    return decoded.astype(jnp.bfloat16)
 
 
 def solution(mesh):

time: 77.8 us -> 78.9 us (1.014)
  local copies, waits for them, and re-layouts: 20.9 us -> 22.1 us
  other arithmetic: 11 us -> 10.1 us
    convert_element_type x0 -> x1, local copies, waits for them, and re-layouts: none -> 0.97 us  [per_device(): residual = lifted.astype(jnp.float32).reshape(-1, lifted.shape[-1])]
    convert_element_type x1 -> x0, other arithmetic: 0.87 us -> none  [per_device(): return (lifted.astype(jnp.float32) + branch).astype(jnp.bfloat16)]
    unnamed x39 -> x41, local copies, waits for them, and re-layouts: 3.58 us -> 4.02 us
  transfers between devices with their start and end apart: 15 -> 15, of which waited for: 10 -> 10; matrix products, arithmetic and copies ran while one was open for 14% -> 15% of each run, Pallas kernels for 0% -> 0%
where the time goes in v20:
time: 78.9 us; the launch traced here: 78.5 us
  local copies, waits for them, and re-layouts  22.1 us (28%)
  starting transfers between devices  18.3 us (23%)
  waiting for transfers between devices  17.7 us (22%)
  other arithmetic  10.1 us (13%)
  matrix products  9.34 us (12%)
  between operations  0.9 us (1%)
    ppermute x15, starting transfers between devices, swap(): return lax.ppermute(x, axis, [(i, i ^ distance) for i in range(size)])  18.3 us
    ppermute x15, waiting for transfers between devices, swap(): return lax.ppermute(x, axis, [(i, i ^ distance) for i in range(size)])  17.7 us
    slice x2, local copies, waits for them, and re-layouts, valid_conv(): kernel[step_t].reshape(9 * channels, -1)  7.43 us
    dot_general x6, matrix products, valid_conv(): jnp.dot(window, kernel[step_t].reshape(9 * channels, -1), preferred_eleme...  7.27 us
    unnamed x41, local copies, waits for them, and re-layouts  4.02 us
    convert_element_type x2, other arithmetic, norm_conv(): jnp.where(inside_mask(height + 2, across + 2, 1), act, 0.0)  3.58 us
    reduce_sum x5, other arithmetic, local_sums(): jnp.sum(grouped, axis=(0, 2))  2.25 us
    dot_general x4, matrix products, upsample(): dot = lambda v, w: jnp.dot(flat(v), w, preferred_element_type=jnp.float32)  2.07 us
  transfers between devices with their start and end apart: 15, of which 10 were waited for; matrix products, arithmetic and copies ran while one was open for 15% of the time, Pallas kernels for 0%

profile of v20, /device:TPU:0, one launch (start us, length us, event | category | flops | bytes accessed | tf_op | source)
XLA Modules:
  0.0 78.5 jit_solution(12672295650752759467)
XLA Ops:
  0.0 1.1 %convert_reduce_fusion.1 = (f32[512]{0:T(512)S(1)}, f32[512]{0:T(512)S(1)}) fusion(bf16[3,2,32,512]{3,2,1,0:T(8,128)(2,1)} %param.10), kind=kLoop, calls=%fused_computation.51 | loop fusion | flops 392192 | bytes 200704 | tf_op jit(solution)/shard_map/reduce_sum | solution.py:178
  1.5 0.5 collective-permute-start
  2.0 1.6 %slice_bitcast_fusion.7 = (bf16[512,256]{1,0:T(8,128)(2,1)S(1)}, bf16[512,256]{1,0:T(8,128)(2,1)S(1)}, bf16[512,256]{1,0:T(8,128)(2,1)S(1)}, bf16[512,256]{1,0:T...) fusion(bf16[3,3,512,256]{3,2,1,0:T(8,128)(2,1)} %param.13), kind=kLoop, calls=%fused_computation.77 | loop fusion | bytes 4194304 | tf_op jit(solution)/shard_map/squeeze | solution.py:129
  4.2 2.6 %collective-permute-start.1 = (bf16[7,512]{1,0:T(8,128)(2,1)S(1)}, bf16[7,512]{1,0:T(8,128)(2,1)S(1)}, u32[]{:S(2)}, u32[]{:S(2)}) collective-permute-start(bf16[7,512]{1,0:T(8,128)(2,1)S(1)} %pad_maximum_fusion.25), channel_id=1, source_target_pairs={{0,2},{2,0},{1,3},{3,1},{4,6},{6,4},{5,7},{7,5},{8,10},{10,8},{9,1... | collective-permute-start | bytes 21512 | tf_op jit(solution)/shard_map/ppermute | solution.py:169
  6.9 1.6 %collective-permute-done.1 = bf16[7,512]{1,0:T(8,128)(2,1)S(1)} collective-permute-done((bf16[7,512]{1,0:T(8,128)(2,1)S(1)}, bf16[7,512]{1,0:T(8,128)(2,1)S(1)}, u32[]{:S(2)}, u32[]{:S(2)}) %collective-permute-start.1) | collective-permute-done | bytes 7200 | tf_op jit(solution)/shard_map/ppermute | solution.py:169
  9.1 2.2 %collective-permute-start.2 = (bf16[100,512]{1,0:T(8,128)(2,1)S(1)}, bf16[100,512]{1,0:T(8,128)(2,1)S(1)}, u32[]{:S(2)}, u32[]{:S(2)}) collective-permute-start(bf16[100,512]{1,0:T(8,128)(2,1)S(1)} %pad_maximum_fusion.24), channel_id=1, source_target_pairs={{0,4},{4,0},{8,12},{12,8},{1,5},{5,1},{9,13},{13,9},{2,6},{6,2},{1... | collective-permute-start | bytes 307208 | tf_op jit(solution)/shard_map/ppermute | solution.py:169
  11.3 2.5 %collective-permute-start.3 = (bf16[100,512]{1,0:T(8,128)(2,1)S(1)}, bf16[100,512]{1,0:T(8,128)(2,1)S(1)}, u32[]{:S(2)}, u32[]{:S(2)}) collective-permute-start(bf16[100,512]{1,0:T(8,128)(2,1)S(1)} %pad_maximum_fusion.24), channel_id=1, source_target_pairs={{0,12},{4,8},{8,4},{12,0},{1,13},{5,9},{9,5},{13,1},{2,14},{6,10},... | collective-permute-start | bytes 307208 | tf_op jit(solution)/shard_map/ppermute | solution.py:169
  14.3 4.1 %collective-permute-done.3 = bf16[100,512]{1,0:T(8,128)(2,1)S(1)} collective-permute-done((bf16[100,512]{1,0:T(8,128)(2,1)S(1)}, bf16[100,512]{1,0:T(8,128)(2,1)S(1)}, u32[]{:S(2)}, u32[]{:S(2)}) %collective-permute-start.3) | collective-permute-done | bytes 102432 | tf_op jit(solution)/shard_map/ppermute | solution.py:169
  19.0 0.3 select_convert_fusion.2
  19.4 0.3 fusion.11
  19.7 0.3 fusion.15
  20.0 0.4 fusion.2
  20.8 1.2 %convolution_add_fusion.5 = bf16[192,256]{1,0:T(8,128)(2,1)S(1)} fusion(bf16[192,512]{1,0:T(8,128)(2,1)S(1)} %bitcast.122, bf16[3,3,512,256]{3,2,1,0:T(8,128)(2,1)} %param.13, f32[192,512]{1,0:T(8,128)S(1)} %fusion.15, f32[192,512]{1,0:T(8,128)S(1)} %fusion.11, f32[192,1024]{1,0:T(8,128)S(1)} %fusion.2), kind=kOutput, calls=%fused_computation.9 | convolution fusion | flops 50528256 | bytes 1146880 | tf_op jit(solution)/shard_map/dot_general | solution.py:123
  22.0 0.3 pad_maximum_fusion.10
  22.3 0.3 pad_maximum_fusion.11
  22.6 0.8 %convert_reduce_fusion.2 = (f32[256]{0:T(256)S(1)}, f32[256]{0:T(256)S(1)}, bf16[3,2,2,64,256]{4,1,3,0,2:T(2,128)(2,1)S(1)}) fusion(bf16[3,2,1,64,256]{4,1,3,0,2:T(2,128)(2,1)S(1)} %bitcast.125, bf16[3,2,1,64,256]{4,1,3,0,2:T(2,128)(2,1)S(1)} %bitcast.124), kind=kLoop, calls=%fused_computation.67 | loop fusion | flops 982528 | bytes 788480 | tf_op jit(solution)/shard_map/reduce_sum | solution.py:178
  24.2 1.6 %collective-permute-start.5 = (bf16[13,256]{1,0:T(8,128)(2,1)S(1)}, bf16[13,256]{1,0:T(8,128)(2,1)S(1)}, u32[]{:S(2)}, u32[]{:S(2)}) collective-permute-start(bf16[13,256]{1,0:T(8,128)(2,1)S(1)} %pad_maximum_fusion.26), channel_id=1, source_target_pairs={{0,2},{2,0},{1,3},{3,1},{4,6},{6,4},{5,7},{7,5},{8,10},{10,8},{9,1... | collective-permute-start | bytes 19976 | tf_op jit(solution)/shard_map/ppermute | solution.py:169
  25.7 2.2 %collective-permute-done.5 = bf16[13,256]{1,0:T(8,128)(2,1)S(1)} collective-permute-done((bf16[13,256]{1,0:T(8,128)(2,1)S(1)}, bf16[13,256]{1,0:T(8,128)(2,1)S(1)}, u32[]{:S(2)}, u32[]{:S(2)}) %collective-permute-start.5) | collective-permute-done | bytes 6688 | tf_op jit(solution)/shard_map/ppermute | solution.py:169
  28.7 0.7 collective-permute-start.6
  29.3 2.8 %collective-permute-start.7 = (bf16[199,256]{1,0:T(8,128)(2,1)S(1)}, bf16[199,256]{1,0:T(8,128)(2,1)S(1)}, u32[]{:S(2)}, u32[]{:S(2)}) collective-permute-start(bf16[199,256]{1,0:T(8,128)(2,1)S(1)} %get-tuple-element.70), channel_id=1, source_target_pairs={{0,12},{4,8},{8,4},{12,0},{1,13},{5,9},{9,5},{13,1},{2,14},{6,10},... | collective-permute-start | bytes 305672 | tf_op jit(solution)/shard_map/ppermute | solution.py:169
  32.3 1.1 %collective-permute-done.6 = bf16[199,256]{1,0:T(8,128)(2,1)S(1)} collective-permute-done((bf16[199,256]{1,0:T(8,128)(2,1)S(1)}, bf16[199,256]{1,0:T(8,128)(2,1)S(1)}, u32[]{:S(2)}, u32[]{:S(2)}) %collective-permute-start.6) | collective-permute-done | bytes 101920 | tf_op jit(solution)/shard_map/ppermute | solution.py:169
  33.4 2.6 %collective-permute-done.7 = bf16[199,256]{1,0:T(8,128)(2,1)S(1)} collective-permute-done((bf16[199,256]{1,0:T(8,128)(2,1)S(1)}, bf16[199,256]{1,0:T(8,128)(2,1)S(1)}, u32[]{:S(2)}, u32[]{:S(2)}) %collective-permute-start.7) | collective-permute-done | bytes 101920 | tf_op jit(solution)/shard_map/ppermute | solution.py:169
  37.2 3.7 %fusion.117 = (bf16[1,3,3,256,256]{4,3,2,1,0:T(8,128)(2,1)S(1)}, bf16[1,3,3,256,256]{4,3,2,1,0:T(8,128)(2,1)}, bf16[1,3,3,256,256]{4,3,2,1,0:T(8,128)(2,1)}) fusion(bf16[3,3,3,256,256]{4,3,2,1,0:T(8,128)(2,1)} %param.16), kind=kLoop, calls=%fused_computation.281 | loop fusion | bytes 7077888 | tf_op jit(solution)/shard_map/slice | solution.py:153
  41.7 1.9 %select_convert_fusion.1 = bf16[5,6,66,256]{3,2,1,0:T(8,128)(2,1)S(1)} fusion(bf16[3,1,66,256]{3,2,1,0:T(8,128)(2,1)S(1)} %select_n.182, bf16[3,4,1,256]{3,2,1,0:T(2,128)(2,1)S(1)} %reshape.756, bf16[3,4,64,256]{3,2,1,0:T(8,128)(2,1)S(1)} %bitcast.104, bf16[3,1,66,256]{3,2,1,0:T(8,128)(2,1)S(1)} %select_n.179, ...), kind=kLoop, calls=%fused_computation.1 | loop fusion | flops 11151360 | bytes 2025868 | tf_op jit(solution)/shard_map/convert_element_type | solution.py:274
  43.7 0.2 slice_dynamic-update-slice_fusion.16
  43.9 0.2 slice_dynamic-update-slice_fusion.15
  45.4 1.0 %fusion.115 = (bf16[3,4,64,2304]{3,2,1,0:T(8,128)(2,1)S(1)}, bf16[3,4,64,2304]{3,2,1,0:T(8,128)(2,1)S(1)}, bf16[3,4,64,2304]{3,2,1,0:T(8,128)(2,1)S(1)}) fusion(bf16[5,4,64,2304]{3,2,1,0:T(8,128)(2,1)S(1)} %slice_dynamic-update-slice_fusion.9), kind=kLoop, calls=%fused_computation.279 | loop fusion | bytes 21233664 | tf_op jit(solution)/shard_map/slice | solution.py:151
  46.4 0.3 copy-done.3
  46.6 1.1 %fusion.120 = f32[768,256]{1,0:T(8,128)S(1)} fusion(bf16[768,2304]{1,0:T(8,128)(2,1)S(1)} %bitcast.115, bf16[2304,256]{1,0:T(8,128)(2,1)S(1)} %bitcast.121), kind=kOutput, calls=%fused_computation.284 | convolution fusion | flops 905969664 | bytes 5505024 | tf_op jit(solution)/shard_map/dot_general | solution.py:152
  47.9 1.1 %convolution_add_fusion.4 = f32[768,256]{1,0:T(8,128)S(1)} fusion(f32[768,256]{1,0:T(8,128)S(1)} %fusion.120, bf16[768,2304]{1,0:T(8,128)(2,1)S(1)} %bitcast.113, bf16[2304,256]{1,0:T(8,128)(2,1)S(1)} %bitcast.120), kind=kOutput, calls=%fused_computation.6 | convolution fusion | flops 906166272 | bytes 6291456 | tf_op jit(solution)/shard_map/dot_general | solution.py:152
  49.0 1.1 %convert_reduce_fusion = (f32[256]{0:T(256)S(1)}, f32[256]{0:T(256)S(1)}, bf16[768,256]{1,0:T(8,128)(2,1)S(1)}) fusion(f32[768,256]{1,0:T(8,128)S(1)} %convolution_add_fusion.4, bf16[768,2304]{1,0:T(8,128)(2,1)S(1)} %bitcast.110, bf16[2304,256]{1,0:T(8,128)(2,1)S(1)} %bitcast.117), kind=kOutput, calls=%fused_computation.19 | convolution fusion | flops 907148800 | bytes 5900288 | tf_op jit(solution)/shard_map/dot_general | solution.py:152
  50.8 1.6 %collective-permute-start.10 = (bf16[13,256]{1,0:T(8,128)(2,1)S(1)}, bf16[13,256]{1,0:T(8,128)(2,1)S(1)}, u32[]{:S(2)}, u32[]{:S(2)}) collective-permute-start(bf16[13,256]{1,0:T(8,128)(2,1)S(1)} %pad_maximum_fusion.27), channel_id=1, source_target_pairs={{0,2},{2,0},{1,3},{3,1},{4,6},{6,4},{5,7},{7,5},{8,10},{10,8},{9,1... | collective-permute-start | bytes 19976 | tf_op jit(solution)/shard_map/ppermute | solution.py:169
  52.4 2.2 %collective-permute-done.10 = bf16[13,256]{1,0:T(8,128)(2,1)S(1)} collective-permute-done((bf16[13,256]{1,0:T(8,128)(2,1)S(1)}, bf16[13,256]{1,0:T(8,128)(2,1)S(1)}, u32[]{:S(2)}, u32[]{:S(2)}) %collective-permute-start.10) | collective-permute-done | bytes 6688 | tf_op jit(solution)/shard_map/ppermute | solution.py:169
  55.3 0.4 collective-permute-start.11
  55.7 2.4 %collective-permute-start.12 = (bf16[199,256]{1,0:T(8,128)(2,1)S(1)}, bf16[199,256]{1,0:T(8,128)(2,1)S(1)}, u32[]{:S(2)}, u32[]{:S(2)}) collective-permute-start(bf16[199,256]{1,0:T(8,128)(2,1)S(1)} %get-tuple-element.64), channel_id=1, source_target_pairs={{0,12},{4,8},{8,4},{12,0},{1,13},{5,9},{9,5},{13,1},{2,14},{6,10},... | collective-permute-start | bytes 305672 | tf_op jit(solution)/shard_map/ppermute | solution.py:169
  58.1 0.8 %collective-permute-start.13 = (f32[2,32]{1,0:T(2,128)S(1)}, f32[2,32]{1,0:T(2,128)S(1)}, u32[]{:S(2)}, u32[]{:S(2)}) collective-permute-start(f32[2,32]{1,0:T(2,128)S(1)} %get-tuple-element.17), channel_id=1, source_target_pairs={{0,8},{4,12},{8,0},{12,4},{1,9},{5,13},{9,1},{13,5},{2,10},{6,14},... | collective-permute-start | bytes 776 | tf_op jit(solution)/shard_map/ppermute | solution.py:169
  58.9 2.2 %collective-permute-done.11 = bf16[199,256]{1,0:T(8,128)(2,1)S(1)} collective-permute-done((bf16[199,256]{1,0:T(8,128)(2,1)S(1)}, bf16[199,256]{1,0:T(8,128)(2,1)S(1)}, u32[]{:S(2)}, u32[]{:S(2)}) %collective-permute-start.11) | collective-permute-done | bytes 101920 | tf_op jit(solution)/shard_map/ppermute | solution.py:169
  61.1 1.6 %collective-permute-done.12 = bf16[199,256]{1,0:T(8,128)(2,1)S(1)} collective-permute-done((bf16[199,256]{1,0:T(8,128)(2,1)S(1)}, bf16[199,256]{1,0:T(8,128)(2,1)S(1)}, u32[]{:S(2)}, u32[]{:S(2)}) %collective-permute-start.12) | collective-permute-done | bytes 101920 | tf_op jit(solution)/shard_map/ppermute | solution.py:169
  63.8 3.7 %fusion.116 = (bf16[1,3,3,256,256]{4,3,2,1,0:T(8,128)(2,1)S(1)}, bf16[1,3,3,256,256]{4,3,2,1,0:T(8,128)(2,1)}, bf16[1,3,3,256,256]{4,3,2,1,0:T(8,128)(2,1)}) fusion(bf16[3,3,3,256,256]{4,3,2,1,0:T(8,128)(2,1)} %param.19), kind=kLoop, calls=%fused_computation.280 | loop fusion | bytes 7077888 | tf_op jit(solution)/shard_map/slice | solution.py:153
  67.5 1.0 %copy.41 = f32[3,2,2,64,256]{4,3,2,1,0:T(8,128)} copy(bf16[3,2,2,64,256]{4,1,3,0,2:T(2,128)(2,1)S(1)} %get-tuple-element.25) | data formatting | bytes 1179648 | tf_op jit(solution)/shard_map/convert_element_type | solution.py:300
  69.3 1.7 %select_convert_fusion = bf16[5,6,66,256]{3,2,1,0:T(8,128)(2,1)S(1)} fusion(bf16[3,1,66,256]{3,2,1,0:T(8,128)(2,1)S(1)} %select_n.191, bf16[3,4,1,256]{3,2,1,0:T(2,128)(2,1)S(1)} %reshape.757, bf16[3,4,64,256]{3,2,1,0:T(8,128)(2,1)S(1)} %bitcast.109, bf16[3,1,66,256]{3,2,1,0:T(8,128)(2,1)S(1)} %select_n.189, ...), kind=kLoop, calls=%fused_computation | loop fusion | flops 11151360 | bytes 2025868 | tf_op jit(solution)/shard_map/convert_element_type | solution.py:274
  71.1 0.2 slice_dynamic-update-slice_fusion.7
  71.4 0.2 slice_dynamic-update-slice_fusion.6
  72.8 1.0 %fusion.114 = (bf16[3,4,64,2304]{3,2,1,0:T(8,128)(2,1)S(1)}, bf16[3,4,64,2304]{3,2,1,0:T(8,128)(2,1)S(1)}, bf16[3,4,64,2304]{3,2,1,0:T(8,128)(2,1)S(1)}) fusion(bf16[5,4,64,2304]{3,2,1,0:T(8,128)(2,1)S(1)} %slice_dynamic-update-slice_fusion), kind=kLoop, calls=%fused_computation.278 | loop fusion | bytes 21233664 | tf_op jit(solution)/shard_map/slice | solution.py:151
  73.8 0.3 copy-done.1
  74.3 1.1 %convolution_add_fusion.2 = f32[768,256]{1,0:T(8,128)S(1)} fusion(f32[768,256]{1,0:T(8,128)S(1)} %bitcast.123, bf16[768,2304]{1,0:T(8,128)(2,1)S(1)} %bitcast.114, bf16[2304,256]{1,0:T(8,128)(2,1)S(1)} %bitcast.119), kind=kOutput, calls=%fused_computation.4 | convolution fusion | flops 906166272 | bytes 6291456 | tf_op jit(solution)/shard_map/dot_general | solution.py:152
  75.5 1.1 %convolution_add_fusion.1 = f32[768,256]{1,0:T(8,128)S(1)} fusion(f32[768,256]{1,0:T(8,128)S(1)} %convolution_add_fusion.2, bf16[768,2304]{1,0:T(8,128)(2,1)S(1)} %bitcast.112, bf16[2304,256]{1,0:T(8,128)(2,1)S(1)} %bitcast.118), kind=kOutput, calls=%fused_computation.3 | convolution fusion | flops 906166272 | bytes 6291456 | tf_op jit(solution)/shard_map/dot_general | solution.py:152
  76.6 1.8 %fusion.1 = bf16[768,256]{1,0:T(8,128)(2,1)} fusion(f32[768,256]{1,0:T(8,128)S(1)} %convolution_add_fusion.1, bf16[768,2304]{1,0:T(8,128)(2,1)S(1)} %bitcast.111, bf16[2304,256]{1,0:T(8,128)(2,1)S(1)} %bitcast.116), kind=kOutput, calls=%fused_computation.8 | convolution fusion | flops 906362880 | bytes 5898240 | tf_op jit(solution)/shard_map/dot_general | solution.py:152
  (228 shorter events, 13.1 us)
Async XLA Ops:
  0.0 3.8 %copy-start.4 = (bf16[3,2,32,512]{3,2,1,0:T(8,128)(2,1)S(1)}, bf16[3,2,32,512]{3,2,1,0:T(8,128)(2,1)}, u32[]{:S(2)}) copy-start(bf16[3,2,32,512]{3,2,1,0:T(8,128)(2,1)} %param.10) | copy-start | bytes 589828
  1.5 2.3 %collective-permute-start = (f32[2,32]{1,0:T(2,128)S(1)}, f32[2,32]{1,0:T(2,128)S(1)}, u32[]{:S(2)}, u32[]{:S(2)}) collective-permute-start(f32[2,32]{1,0:T(2,128)S(1)} %pad_maximum_fusion.28), channel_id=1, source_target_pairs={{0,1},{1,0},{2,3},{3,2},{4,5},{5,4},{6,7},{7,6},{8,9},{9,8},{10,11... | collective-permute-start | bytes 776 | tf_op jit(solution)/shard_map/ppermute | solution.py:169
  2.0 17.0 %copy-start.6 = (f32[512]{0:T(512)S(1)}, f32[512]{0:T(512)}, u32[]{:S(2)}) copy-start(f32[512]{0:T(512)} %param.12) | copy-start | bytes 6148
  2.0 17.0 %copy-start.7 = (f32[512]{0:T(512)S(1)}, f32[512]{0:T(512)}, u32[]{:S(2)}) copy-start(f32[512]{0:T(512)} %param.11) | copy-start | bytes 6148
  4.2 4.2 %collective-permute-start.1 = (bf16[7,512]{1,0:T(8,128)(2,1)S(1)}, bf16[7,512]{1,0:T(8,128)(2,1)S(1)}, u32[]{:S(2)}, u32[]{:S(2)}) collective-permute-start(bf16[7,512]{1,0:T(8,128)(2,1)S(1)} %pad_maximum_fusion.25), channel_id=1, source_target_pairs={{0,2},{2,0},{1,3},{3,1},{4,6},{6,4},{5,7},{7,5},{8,10},{10,8},{9,1... | collective-permute-start | bytes 21512 | tf_op jit(solution)/shard_map/ppermute | solution.py:169
  9.1 5.0 %collective-permute-start.2 = (bf16[100,512]{1,0:T(8,128)(2,1)S(1)}, bf16[100,512]{1,0:T(8,128)(2,1)S(1)}, u32[]{:S(2)}, u32[]{:S(2)}) collective-permute-start(bf16[100,512]{1,0:T(8,128)(2,1)S(1)} %pad_maximum_fusion.24), channel_id=1, source_target_pairs={{0,4},{4,0},{8,12},{12,8},{1,5},{5,1},{9,13},{13,9},{2,6},{6,2},{1... | collective-permute-start | bytes 307208 | tf_op jit(solution)/shard_map/ppermute | solution.py:169
  11.3 7.0 %collective-permute-start.3 = (bf16[100,512]{1,0:T(8,128)(2,1)S(1)}, bf16[100,512]{1,0:T(8,128)(2,1)S(1)}, u32[]{:S(2)}, u32[]{:S(2)}) collective-permute-start(bf16[100,512]{1,0:T(8,128)(2,1)S(1)} %pad_maximum_fusion.24), channel_id=1, source_target_pairs={{0,12},{4,8},{8,4},{12,0},{1,13},{5,9},{9,5},{13,1},{2,14},{6,10},... | collective-permute-start | bytes 307208 | tf_op jit(solution)/shard_map/ppermute | solution.py:169
  13.8 4.8 %collective-permute-start.4 = (f32[2,32]{1,0:T(2,128)S(1)}, f32[2,32]{1,0:T(2,128)S(1)}, u32[]{:S(2)}, u32[]{:S(2)}) collective-permute-start(f32[2,32]{1,0:T(2,128)S(1)} %get-tuple-element.27), channel_id=1, source_target_pairs={{0,8},{4,12},{8,0},{12,4},{1,9},{5,13},{9,1},{13,5},{2,10},{6,14},... | collective-permute-start | bytes 776 | tf_op jit(solution)/shard_map/ppermute | solution.py:169
  24.2 3.7 %collective-permute-start.5 = (bf16[13,256]{1,0:T(8,128)(2,1)S(1)}, bf16[13,256]{1,0:T(8,128)(2,1)S(1)}, u32[]{:S(2)}, u32[]{:S(2)}) collective-permute-start(bf16[13,256]{1,0:T(8,128)(2,1)S(1)} %pad_maximum_fusion.26), channel_id=1, source_target_pairs={{0,2},{2,0},{1,3},{3,1},{4,6},{6,4},{5,7},{7,5},{8,10},{10,8},{9,1... | collective-permute-start | bytes 19976 | tf_op jit(solution)/shard_map/ppermute | solution.py:169
  28.7 4.7 %collective-permute-start.6 = (bf16[199,256]{1,0:T(8,128)(2,1)S(1)}, bf16[199,256]{1,0:T(8,128)(2,1)S(1)}, u32[]{:S(2)}, u32[]{:S(2)}) collective-permute-start(bf16[199,256]{1,0:T(8,128)(2,1)S(1)} %get-tuple-element.69), channel_id=1, source_target_pairs={{0,4},{4,0},{8,12},{12,8},{1,5},{5,1},{9,13},{13,9},{2,6},{6,2},{1... | collective-permute-start | bytes 305672 | tf_op jit(solution)/shard_map/ppermute | solution.py:169
  29.3 6.6 %collective-permute-start.7 = (bf16[199,256]{1,0:T(8,128)(2,1)S(1)}, bf16[199,256]{1,0:T(8,128)(2,1)S(1)}, u32[]{:S(2)}, u32[]{:S(2)}) collective-permute-start(bf16[199,256]{1,0:T(8,128)(2,1)S(1)} %get-tuple-element.70), channel_id=1, source_target_pairs={{0,12},{4,8},{8,4},{12,0},{1,13},{5,9},{9,5},{13,1},{2,14},{6,10},... | collective-permute-start | bytes 305672 | tf_op jit(solution)/shard_map/ppermute | solution.py:169
  32.2 4.5 %collective-permute-start.8 = (f32[2,32]{1,0:T(2,128)S(1)}, f32[2,32]{1,0:T(2,128)S(1)}, u32[]{:S(2)}, u32[]{:S(2)}) collective-permute-start(f32[2,32]{1,0:T(2,128)S(1)} %get-tuple-element.24), channel_id=1, source_target_pairs={{0,8},{4,12},{8,0},{12,4},{1,9},{5,13},{9,1},{13,5},{2,10},{6,14},... | collective-permute-start | bytes 776 | tf_op jit(solution)/shard_map/ppermute | solution.py:169
  37.1 3.8 %collective-permute-start.9 = (bf16[793,256]{1,0:T(8,128)(2,1)S(1)}, bf16[793,256]{1,0:T(8,128)(2,1)S(1)}, u32[]{:S(2)}, u32[]{:S(2)}) collective-permute-start(bf16[793,256]{1,0:T(8,128)(2,1)S(1)} %pad_maximum_fusion.8), channel_id=1, source_target_pairs={{0,1},{1,0},{2,3},{3,2},{4,5},{5,4},{6,7},{7,6},{8,9},{9,8},{10,11... | collective-permute-start | bytes 1218056 | tf_op jit(solution)/shard_map/ppermute | solution.py:169
  40.9 0.8 %copy-start.8 = (f32[256]{0:T(256)S(1)}, f32[256]{0:T(256)}, u32[]{:S(2)}) copy-start(f32[256]{0:T(256)} %param.15) | copy-start | bytes 3076
  40.9 0.8 %copy-start.9 = (f32[256]{0:T(256)S(1)}, f32[256]{0:T(256)}, u32[]{:S(2)}) copy-start(f32[256]{0:T(256)} %param.14) | copy-start | bytes 3076
  45.4 1.3 %copy-start.3 = (bf16[1,3,3,256,256]{4,3,2,1,0:T(8,128)(2,1)S(1)}, bf16[1,3,3,256,256]{4,3,2,1,0:T(8,128)(2,1)}, u32[]{:S(2)}) copy-start(bf16[1,3,3,256,256]{4,3,2,1,0:T(8,128)(2,1)} %get-tuple-element.40) | copy-start | bytes 3538948
  46.6 1.3 %copy-start.2 = (bf16[1,3,3,256,256]{4,3,2,1,0:T(8,128)(2,1)S(1)}, bf16[1,3,3,256,256]{4,3,2,1,0:T(8,128)(2,1)}, u32[]{:S(2)}) copy-start(bf16[1,3,3,256,256]{4,3,2,1,0:T(8,128)(2,1)} %get-tuple-element.41) | copy-start | bytes 3538948
  50.8 3.7 %collective-permute-start.10 = (bf16[13,256]{1,0:T(8,128)(2,1)S(1)}, bf16[13,256]{1,0:T(8,128)(2,1)S(1)}, u32[]{:S(2)}, u32[]{:S(2)}) collective-permute-start(bf16[13,256]{1,0:T(8,128)(2,1)S(1)} %pad_maximum_fusion.27), channel_id=1, source_target_pairs={{0,2},{2,0},{1,3},{3,1},{4,6},{6,4},{5,7},{7,5},{8,10},{10,8},{9,1... | collective-permute-start | bytes 19976 | tf_op jit(solution)/shard_map/ppermute | solution.py:169
  55.3 5.8 %collective-permute-start.11 = (bf16[199,256]{1,0:T(8,128)(2,1)S(1)}, bf16[199,256]{1,0:T(8,128)(2,1)S(1)}, u32[]{:S(2)}, u32[]{:S(2)}) collective-permute-start(bf16[199,256]{1,0:T(8,128)(2,1)S(1)} %get-tuple-element.63), channel_id=1, source_target_pairs={{0,4},{4,0},{8,12},{12,8},{1,5},{5,1},{9,13},{13,9},{2,6},{6,2},{1... | collective-permute-start | bytes 305672 | tf_op jit(solution)/shard_map/ppermute | solution.py:169
  55.7 7.0 %collective-permute-start.12 = (bf16[199,256]{1,0:T(8,128)(2,1)S(1)}, bf16[199,256]{1,0:T(8,128)(2,1)S(1)}, u32[]{:S(2)}, u32[]{:S(2)}) collective-permute-start(bf16[199,256]{1,0:T(8,128)(2,1)S(1)} %get-tuple-element.64), channel_id=1, source_target_pairs={{0,12},{4,8},{8,4},{12,0},{1,13},{5,9},{9,5},{13,1},{2,14},{6,10},... | collective-permute-start | bytes 305672 | tf_op jit(solution)/shard_map/ppermute | solution.py:169
  58.1 5.3 %collective-permute-start.13 = (f32[2,32]{1,0:T(2,128)S(1)}, f32[2,32]{1,0:T(2,128)S(1)}, u32[]{:S(2)}, u32[]{:S(2)}) collective-permute-start(f32[2,32]{1,0:T(2,128)S(1)} %get-tuple-element.17), channel_id=1, source_target_pairs={{0,8},{4,12},{8,0},{12,4},{1,9},{5,13},{9,1},{13,5},{2,10},{6,14},... | collective-permute-start | bytes 776 | tf_op jit(solution)/shard_map/ppermute | solution.py:169
  63.7 4.8 %collective-permute-start.14 = (bf16[793,256]{1,0:T(8,128)(2,1)S(1)}, bf16[793,256]{1,0:T(8,128)(2,1)S(1)}, u32[]{:S(2)}, u32[]{:S(2)}) collective-permute-start(bf16[793,256]{1,0:T(8,128)(2,1)S(1)} %pad_maximum_fusion.9), channel_id=1, source_target_pairs={{0,1},{1,0},{2,3},{3,2},{4,5},{5,4},{6,7},{7,6},{8,9},{9,8},{10,11... | collective-permute-start | bytes 1218056 | tf_op jit(solution)/shard_map/ppermute | solution.py:169
  67.5 1.8 %copy-start.10 = (f32[256]{0:T(256)S(1)}, f32[256]{0:T(256)}, u32[]{:S(2)}) copy-start(f32[256]{0:T(256)} %param.18) | copy-start | bytes 3076
  67.5 1.8 %copy-start.11 = (f32[256]{0:T(256)S(1)}, f32[256]{0:T(256)}, u32[]{:S(2)}) copy-start(f32[256]{0:T(256)} %param.17) | copy-start | bytes 3076
  72.8 1.3 %copy-start.1 = (bf16[1,3,3,256,256]{4,3,2,1,0:T(8,128)(2,1)S(1)}, bf16[1,3,3,256,256]{4,3,2,1,0:T(8,128)(2,1)}, u32[]{:S(2)}) copy-start(bf16[1,3,3,256,256]{4,3,2,1,0:T(8,128)(2,1)} %get-tuple-element.37) | copy-start | bytes 3538948
  72.8 1.5 %copy-start.5 = (f32[3,2,2,64,256]{4,3,2,1,0:T(8,128)S(1)}, f32[3,2,2,64,256]{4,3,2,1,0:T(8,128)}, u32[]{:S(2)}) copy-start(f32[3,2,2,64,256]{4,3,2,1,0:T(8,128)} %copy.41) | copy-start | bytes 2359300
  74.3 1.3 %copy-start = (bf16[1,3,3,256,256]{4,3,2,1,0:T(8,128)(2,1)S(1)}, bf16[1,3,3,256,256]{4,3,2,1,0:T(8,128)(2,1)}, u32[]{:S(2)}) copy-start(bf16[1,3,3,256,256]{4,3,2,1,0:T(8,128)(2,1)} %get-tuple-element.38) | copy-start | bytes 3538948

commit v21 on v17

--- a/solution.py
+++ b/solution.py
@@ -239,12 +239,12 @@
 
 def fast_conv_input(values):
     sums = local_sums(values.astype(jnp.float32))
-    sums, above, below = ha_round(sums, values[:, :1], values[:, -1:])
-    x = jnp.concatenate([above, values, below], axis=1)
     w = lax.axis_index("wa")
-    s_w, beside = swap_with(sums, jnp.where(w == 0, x[:, :, -1:], x[:, :, :1]), "wa", 1)
+    s_w, beside = swap_with(sums, jnp.where(w == 0, values[:, :, -1:], values[:, :, :1]), "wa", 1)
     sums = sums + s_w
-    x = jnp.concatenate([beside, x, beside], axis=2)
+    x = jnp.concatenate([beside, values, beside], axis=2)
+    sums, above, below = ha_round(sums, x[:, :1], x[:, -1:])
+    x = jnp.concatenate([above, x, below], axis=1)
     s_t, earlier = swap_with(sums, x[-2:], "ta", 1)
     sums = sums + s_t
     opening = jnp.concatenate([x[:1], x[:1]], axis=0)

time: 83.2 us -> 80.6 us (0.969)
  starting transfers between devices: 19.5 us -> 17.7 us
  waiting for transfers between devices: 21 us -> 19.4 us
  local copies, waits for them, and re-layouts: 21.8 us -> 22.7 us
    ppermute x15, starting transfers between devices: 19.5 us -> 17.7 us  [swap(): return lax.ppermute(x, axis, [(i, i ^ distance) for i in range(size)])]
    ppermute x15, waiting for transfers between devices: 21 us -> 19.4 us  [swap(): return lax.ppermute(x, axis, [(i, i ^ distance) for i in range(size)])]
  transfers between devices with their start and end apart: 15 -> 15, of which waited for: 9 -> 9; matrix products, arithmetic and copies ran while one was open for 13% -> 14% of each run, Pallas kernels for 0% -> 0%
where the time goes in v21:
time: 80.6 us; the launch traced here: 80.2 us
  local copies, waits for them, and re-layouts  22.7 us (28%)
  waiting for transfers between devices  19.4 us (24%)
  starting transfers between devices  17.7 us (22%)
  other arithmetic  11 us (14%)
  matrix products  8.6 us (11%)
  between operations  0.84 us (1%)
    ppermute x15, waiting for transfers between devices, swap(): return lax.ppermute(x, axis, [(i, i ^ distance) for i in range(size)])  19.4 us
    ppermute x15, starting transfers between devices, swap(): return lax.ppermute(x, axis, [(i, i ^ distance) for i in range(size)])  17.7 us
    slice x2, local copies, waits for them, and re-layouts, valid_conv(): kernel[step_t].reshape(9 * channels, -1)  7.55 us
    dot_general x6, matrix products, valid_conv(): jnp.dot(window, kernel[step_t].reshape(9 * channels, -1), preferred_eleme...  6.54 us
    unnamed x40, local copies, waits for them, and re-layouts  4.3 us
    convert_element_type x2, other arithmetic, norm_conv(): jnp.where(inside_mask(height + 2, across + 2, 1), act, 0.0)  3.58 us
    slice x2, local copies, waits for them, and re-layouts, valid_conv(): window = wide[step_t:step_t + frames].reshape(-1, 9 * channels)  2.19 us
    reduce_sum x5, other arithmetic, local_sums(): jnp.sum(grouped, axis=(0, 2))  2.18 us
  transfers between devices with their start and end apart: 15, of which 9 were waited for; matrix products, arithmetic and copies ran while one was open for 14% of the time, Pallas kernels for 0%

profile of v21, /device:TPU:0, one launch (start us, length us, event | category | flops | bytes accessed | tf_op | source)
XLA Modules:
  0.0 80.2 jit_solution(6217342622208605743)
XLA Ops:
  0.0 1.0 %convert_reduce_fusion.2 = (f32[512]{0:T(512)S(1)}, f32[512]{0:T(512)S(1)}) fusion(bf16[3,2,32,512]{3,2,1,0:T(8,128)(2,1)} %param.10), kind=kLoop, calls=%fused_computation.52 | loop fusion | flops 392192 | bytes 200704 | tf_op jit(solution)/shard_map/reduce_sum | solution.py:179
  1.4 0.5 collective-permute-start
  2.0 1.7 %slice_bitcast_fusion.7 = (bf16[512,256]{1,0:T(8,128)(2,1)S(1)}, bf16[512,256]{1,0:T(8,128)(2,1)S(1)}, bf16[512,256]{1,0:T(8,128)(2,1)S(1)}, bf16[512,256]{1,0:T...) fusion(bf16[3,3,512,256]{3,2,1,0:T(8,128)(2,1)} %param.13), kind=kLoop, calls=%fused_computation.77 | loop fusion | bytes 4194304 | tf_op jit(solution)/shard_map/squeeze | solution.py:129
  4.1 2.7 %collective-permute-start.1 = (bf16[97,512]{1,0:T(8,128)(2,1)S(1)}, bf16[97,512]{1,0:T(8,128)(2,1)S(1)}, u32[]{:S(2)}, u32[]{:S(2)}) collective-permute-start(bf16[97,512]{1,0:T(8,128)(2,1)S(1)} %pad_maximum_fusion.24), channel_id=1, source_target_pairs={{0,4},{4,0},{8,12},{12,8},{1,5},{5,1},{9,13},{13,9},{2,6},{6,2},{1... | collective-permute-start | bytes 297992 | tf_op jit(solution)/shard_map/ppermute | solution.py:170
  6.9 2.5 %collective-permute-start.2 = (bf16[97,512]{1,0:T(8,128)(2,1)S(1)}, bf16[97,512]{1,0:T(8,128)(2,1)S(1)}, u32[]{:S(2)}, u32[]{:S(2)}) collective-permute-start(bf16[97,512]{1,0:T(8,128)(2,1)S(1)} %pad_maximum_fusion.24), channel_id=1, source_target_pairs={{0,12},{4,8},{8,4},{12,0},{1,13},{5,9},{9,5},{13,1},{2,14},{6,10},... | collective-permute-start | bytes 297992 | tf_op jit(solution)/shard_map/ppermute | solution.py:170
  9.5 0.9 %collective-permute-done.1 = bf16[97,512]{1,0:T(8,128)(2,1)S(1)} collective-permute-done((bf16[97,512]{1,0:T(8,128)(2,1)S(1)}, bf16[97,512]{1,0:T(8,128)(2,1)S(1)}, u32[]{:S(2)}, u32[]{:S(2)}) %collective-permute-start.1) | collective-permute-done | bytes 99360 | tf_op jit(solution)/shard_map/ppermute | solution.py:170
  10.5 4.5 %collective-permute-done.2 = bf16[97,512]{1,0:T(8,128)(2,1)S(1)} collective-permute-done((bf16[97,512]{1,0:T(8,128)(2,1)S(1)}, bf16[97,512]{1,0:T(8,128)(2,1)S(1)}, u32[]{:S(2)}, u32[]{:S(2)}) %collective-permute-start.2) | collective-permute-done | bytes 99360 | tf_op jit(solution)/shard_map/ppermute | solution.py:170
  15.7 1.6 %collective-permute-start.4 = (bf16[10,512]{1,0:T(8,128)(2,1)S(1)}, bf16[10,512]{1,0:T(8,128)(2,1)S(1)}, u32[]{:S(2)}, u32[]{:S(2)}) collective-permute-start(bf16[10,512]{1,0:T(8,128)(2,1)S(1)} %pad_maximum_fusion.26), channel_id=1, source_target_pairs={{0,2},{2,0},{1,3},{3,1},{4,6},{6,4},{5,7},{7,5},{8,10},{10,8},{9,1... | collective-permute-start | bytes 30728 | tf_op jit(solution)/shard_map/ppermute | solution.py:170
  17.3 2.2 %collective-permute-done.4 = bf16[10,512]{1,0:T(8,128)(2,1)S(1)} collective-permute-done((bf16[10,512]{1,0:T(8,128)(2,1)S(1)}, bf16[10,512]{1,0:T(8,128)(2,1)S(1)}, u32[]{:S(2)}, u32[]{:S(2)}) %collective-permute-start.4) | collective-permute-done | bytes 10272 | tf_op jit(solution)/shard_map/ppermute | solution.py:170
  20.1 0.3 select_convert_fusion.2
  20.5 0.3 fusion.11
  20.7 0.3 fusion.15
  21.0 0.4 fusion.1
  21.8 1.2 %convolution_add_fusion.4 = bf16[192,256]{1,0:T(8,128)(2,1)S(1)} fusion(bf16[192,512]{1,0:T(8,128)(2,1)S(1)} %bitcast.127, bf16[3,3,512,256]{3,2,1,0:T(8,128)(2,1)} %param.13, f32[192,512]{1,0:T(8,128)S(1)} %fusion.15, f32[192,512]{1,0:T(8,128)S(1)} %fusion.11, f32[192,1024]{1,0:T(8,128)S(1)} %fusion.1), kind=kOutput, calls=%fused_computation.7 | convolution fusion | flops 50528256 | bytes 1146880 | tf_op jit(solution)/shard_map/dot_general | solution.py:123
  23.1 0.3 pad_maximum_fusion.10
  23.4 0.3 pad_maximum_fusion.11
  23.6 0.8 %convert_reduce_fusion.1 = (f32[256]{0:T(256)S(1)}, f32[256]{0:T(256)S(1)}, bf16[3,2,2,64,256]{4,1,3,0,2:T(2,128)(2,1)S(1)}) fusion(bf16[3,2,1,64,256]{4,1,3,0,2:T(2,128)(2,1)S(1)} %bitcast.130, bf16[3,2,1,64,256]{4,1,3,0,2:T(2,128)(2,1)S(1)} %bitcast.129), kind=kLoop, calls=%fused_computation.19 | loop fusion | flops 982528 | bytes 788480 | tf_op jit(solution)/shard_map/reduce_sum | solution.py:179
  25.2 1.6 %collective-permute-start.5 = (bf16[13,256]{1,0:T(8,128)(2,1)S(1)}, bf16[13,256]{1,0:T(8,128)(2,1)S(1)}, u32[]{:S(2)}, u32[]{:S(2)}) collective-permute-start(bf16[13,256]{1,0:T(8,128)(2,1)S(1)} %pad_maximum_fusion.27), channel_id=1, source_target_pairs={{0,2},{2,0},{1,3},{3,1},{4,6},{6,4},{5,7},{7,5},{8,10},{10,8},{9,1... | collective-permute-start | bytes 19976 | tf_op jit(solution)/shard_map/ppermute | solution.py:170
  26.8 2.2 %collective-permute-done.5 = bf16[13,256]{1,0:T(8,128)(2,1)S(1)} collective-permute-done((bf16[13,256]{1,0:T(8,128)(2,1)S(1)}, bf16[13,256]{1,0:T(8,128)(2,1)S(1)}, u32[]{:S(2)}, u32[]{:S(2)}) %collective-permute-start.5) | collective-permute-done | bytes 6688 | tf_op jit(solution)/shard_map/ppermute | solution.py:170
  29.7 0.7 collective-permute-start.6
  30.5 2.6 %collective-permute-start.7 = (bf16[199,256]{1,0:T(8,128)(2,1)S(1)}, bf16[199,256]{1,0:T(8,128)(2,1)S(1)}, u32[]{:S(2)}, u32[]{:S(2)}) collective-permute-start(bf16[199,256]{1,0:T(8,128)(2,1)S(1)} %get-tuple-element.70), channel_id=1, source_target_pairs={{0,12},{4,8},{8,4},{12,0},{1,13},{5,9},{9,5},{13,1},{2,14},{6,10},... | collective-permute-start | bytes 305672 | tf_op jit(solution)/shard_map/ppermute | solution.py:170
  33.3 1.1 %collective-permute-done.6 = bf16[199,256]{1,0:T(8,128)(2,1)S(1)} collective-permute-done((bf16[199,256]{1,0:T(8,128)(2,1)S(1)}, bf16[199,256]{1,0:T(8,128)(2,1)S(1)}, u32[]{:S(2)}, u32[]{:S(2)}) %collective-permute-start.6) | collective-permute-done | bytes 101920 | tf_op jit(solution)/shard_map/ppermute | solution.py:170
  34.4 2.6 %collective-permute-done.7 = bf16[199,256]{1,0:T(8,128)(2,1)S(1)} collective-permute-done((bf16[199,256]{1,0:T(8,128)(2,1)S(1)}, bf16[199,256]{1,0:T(8,128)(2,1)S(1)}, u32[]{:S(2)}, u32[]{:S(2)}) %collective-permute-start.7) | collective-permute-done | bytes 101920 | tf_op jit(solution)/shard_map/ppermute | solution.py:170
  38.2 3.8 %fusion.118 = (bf16[1,3,3,256,256]{4,3,2,1,0:T(8,128)(2,1)S(1)}, bf16[1,3,3,256,256]{4,3,2,1,0:T(8,128)(2,1)}, bf16[1,3,3,256,256]{4,3,2,1,0:T(8,128)(2,1)}) fusion(bf16[3,3,3,256,256]{4,3,2,1,0:T(8,128)(2,1)} %param.16), kind=kLoop, calls=%fused_computation.280 | loop fusion | bytes 7077888 | tf_op jit(solution)/shard_map/slice | solution.py:154
  42.8 1.9 %select_convert_fusion.1 = bf16[5,6,66,256]{3,2,1,0:T(8,128)(2,1)S(1)} fusion(bf16[3,1,66,256]{3,2,1,0:T(8,128)(2,1)S(1)} %select_n.182, bf16[3,4,1,256]{3,2,1,0:T(2,128)(2,1)S(1)} %reshape.752, bf16[3,4,64,256]{3,2,1,0:T(8,128)(2,1)S(1)} %bitcast.105, bf16[3,1,66,256]{3,2,1,0:T(8,128)(2,1)S(1)} %select_n.179, ...), kind=kLoop, calls=%fused_computation.1 | loop fusion | flops 11151360 | bytes 2025868 | tf_op jit(solution)/shard_map/convert_element_type | solution.py:275
  44.7 0.2 slice_dynamic-update-slice_fusion.16
  45.9 0.2 slice_dynamic-update-slice_fusion.10
  46.4 1.0 %fusion.116 = (bf16[3,4,64,2304]{3,2,1,0:T(8,128)(2,1)S(1)}, bf16[3,4,64,2304]{3,2,1,0:T(8,128)(2,1)S(1)}, bf16[3,4,64,2304]{3,2,1,0:T(8,128)(2,1)S(1)}) fusion(bf16[5,4,64,2304]{3,2,1,0:T(8,128)(2,1)S(1)} %slice_dynamic-update-slice_fusion.9), kind=kLoop, calls=%fused_computation.278 | loop fusion | bytes 21233664 | tf_op jit(solution)/shard_map/slice | solution.py:152
  47.4 0.3 copy-done.4
  47.7 1.1 %fusion.121 = f32[768,256]{1,0:T(8,128)S(1)} fusion(bf16[768,2304]{1,0:T(8,128)(2,1)S(1)} %bitcast.116, bf16[2304,256]{1,0:T(8,128)(2,1)S(1)} %bitcast.124), kind=kOutput, calls=%fused_computation.283 | convolution fusion | flops 905969664 | bytes 5505024 | tf_op jit(solution)/shard_map/dot_general | solution.py:153
  48.9 1.1 %convolution_add_fusion.3 = f32[768,256]{1,0:T(8,128)S(1)} fusion(f32[768,256]{1,0:T(8,128)S(1)} %fusion.121, bf16[768,2304]{1,0:T(8,128)(2,1)S(1)} %bitcast.114, bf16[2304,256]{1,0:T(8,128)(2,1)S(1)} %bitcast.123), kind=kOutput, calls=%fused_computation.5 | convolution fusion | flops 906166272 | bytes 6291456 | tf_op jit(solution)/shard_map/dot_general | solution.py:153
  50.0 1.1 %convert_reduce_fusion = (f32[256]{0:T(256)S(1)}, f32[256]{0:T(256)S(1)}, bf16[768,256]{1,0:T(8,128)(2,1)S(1)}) fusion(f32[768,256]{1,0:T(8,128)S(1)} %convolution_add_fusion.3, bf16[768,2304]{1,0:T(8,128)(2,1)S(1)} %bitcast.112, bf16[2304,256]{1,0:T(8,128)(2,1)S(1)} %bitcast.119), kind=kOutput, calls=%fused_computation.17 | convolution fusion | flops 907148800 | bytes 5900288 | tf_op jit(solution)/shard_map/dot_general | solution.py:153
  51.9 1.6 %collective-permute-start.10 = (bf16[13,256]{1,0:T(8,128)(2,1)S(1)}, bf16[13,256]{1,0:T(8,128)(2,1)S(1)}, u32[]{:S(2)}, u32[]{:S(2)}) collective-permute-start(bf16[13,256]{1,0:T(8,128)(2,1)S(1)} %pad_maximum_fusion.28), channel_id=1, source_target_pairs={{0,2},{2,0},{1,3},{3,1},{4,6},{6,4},{5,7},{7,5},{8,10},{10,8},{9,1... | collective-permute-start | bytes 19976 | tf_op jit(solution)/shard_map/ppermute | solution.py:170
  53.4 2.2 %collective-permute-done.10 = bf16[13,256]{1,0:T(8,128)(2,1)S(1)} collective-permute-done((bf16[13,256]{1,0:T(8,128)(2,1)S(1)}, bf16[13,256]{1,0:T(8,128)(2,1)S(1)}, u32[]{:S(2)}, u32[]{:S(2)}) %collective-permute-start.10) | collective-permute-done | bytes 6688 | tf_op jit(solution)/shard_map/ppermute | solution.py:170
  56.6 2.5 %collective-permute-start.12 = (bf16[199,256]{1,0:T(8,128)(2,1)S(1)}, bf16[199,256]{1,0:T(8,128)(2,1)S(1)}, u32[]{:S(2)}, u32[]{:S(2)}) collective-permute-start(bf16[199,256]{1,0:T(8,128)(2,1)S(1)} %get-tuple-element.64), channel_id=1, source_target_pairs={{0,12},{4,8},{8,4},{12,0},{1,13},{5,9},{9,5},{13,1},{2,14},{6,10},... | collective-permute-start | bytes 305672 | tf_op jit(solution)/shard_map/ppermute | solution.py:170
  59.1 0.8 %collective-permute-start.13 = (f32[2,32]{1,0:T(2,128)S(1)}, f32[2,32]{1,0:T(2,128)S(1)}, u32[]{:S(2)}, u32[]{:S(2)}) collective-permute-start(f32[2,32]{1,0:T(2,128)S(1)} %get-tuple-element.17), channel_id=1, source_target_pairs={{0,8},{4,12},{8,0},{12,4},{1,9},{5,13},{9,1},{13,5},{2,10},{6,14},... | collective-permute-start | bytes 776 | tf_op jit(solution)/shard_map/ppermute | solution.py:170
  59.9 2.3 %collective-permute-done.11 = bf16[199,256]{1,0:T(8,128)(2,1)S(1)} collective-permute-done((bf16[199,256]{1,0:T(8,128)(2,1)S(1)}, bf16[199,256]{1,0:T(8,128)(2,1)S(1)}, u32[]{:S(2)}, u32[]{:S(2)}) %collective-permute-start.11) | collective-permute-done | bytes 101920 | tf_op jit(solution)/shard_map/ppermute | solution.py:170
  62.2 1.4 %collective-permute-done.12 = bf16[199,256]{1,0:T(8,128)(2,1)S(1)} collective-permute-done((bf16[199,256]{1,0:T(8,128)(2,1)S(1)}, bf16[199,256]{1,0:T(8,128)(2,1)S(1)}, u32[]{:S(2)}, u32[]{:S(2)}) %collective-permute-start.12) | collective-permute-done | bytes 101920 | tf_op jit(solution)/shard_map/ppermute | solution.py:170
  64.8 3.8 %fusion.117 = (bf16[1,3,3,256,256]{4,3,2,1,0:T(8,128)(2,1)S(1)}, bf16[1,3,3,256,256]{4,3,2,1,0:T(8,128)(2,1)}, bf16[1,3,3,256,256]{4,3,2,1,0:T(8,128)(2,1)}) fusion(bf16[3,3,3,256,256]{4,3,2,1,0:T(8,128)(2,1)} %param.19), kind=kLoop, calls=%fused_computation.279 | loop fusion | bytes 7077888 | tf_op jit(solution)/shard_map/slice | solution.py:154
  68.7 0.7 copy-done.5
  69.9 1.0 %slice.717 = bf16[792,256]{1,0:T(8,128)(2,1)S(1)} slice(bf16[793,256]{1,0:T(8,128)(2,1)} %copy-done.5), slice={[0:792], [0:256]} | slice | bytes 811008 | tf_op jit(solution)/shard_map/slice | solution.py:224
  71.2 1.7 %select_convert_fusion = bf16[5,6,66,256]{3,2,1,0:T(8,128)(2,1)S(1)} fusion(bf16[3,1,66,256]{3,2,1,0:T(8,128)(2,1)S(1)} %select_n.191, bf16[3,4,1,256]{3,2,1,0:T(2,128)(2,1)S(1)} %reshape.753, bf16[3,4,64,256]{3,2,1,0:T(8,128)(2,1)S(1)} %bitcast.111, bf16[3,1,66,256]{3,2,1,0:T(8,128)(2,1)S(1)} %select_n.189, ...), kind=kLoop, calls=%fused_computation | loop fusion | flops 11151360 | bytes 2025868 | tf_op jit(solution)/shard_map/convert_element_type | solution.py:275
  74.1 0.2 slice_dynamic-update-slice_fusion.1
  74.6 1.2 %fusion.115 = (bf16[3,4,64,2304]{3,2,1,0:T(8,128)(2,1)S(1)}, bf16[3,4,64,2304]{3,2,1,0:T(8,128)(2,1)S(1)}, bf16[3,4,64,2304]{3,2,1,0:T(8,128)(2,1)S(1)}) fusion(bf16[5,4,64,2304]{3,2,1,0:T(8,128)(2,1)S(1)} %slice_dynamic-update-slice_fusion), kind=kLoop, calls=%fused_computation.277 | loop fusion | bytes 21233664 | tf_op jit(solution)/shard_map/slice | solution.py:152
  75.9 1.1 %fusion.122 = f32[768,256]{1,0:T(8,128)S(1)} fusion(bf16[768,2304]{1,0:T(8,128)(2,1)S(1)} %bitcast.117, bf16[2304,256]{1,0:T(8,128)(2,1)S(1)} %bitcast.122), kind=kOutput, calls=%fused_computation.284 | convolution fusion | flops 905969664 | bytes 5505024 | tf_op jit(solution)/shard_map/dot_general | solution.py:153
  77.1 1.1 %convolution_add_fusion.1 = f32[768,256]{1,0:T(8,128)S(1)} fusion(f32[768,256]{1,0:T(8,128)S(1)} %fusion.122, bf16[768,2304]{1,0:T(8,128)(2,1)S(1)} %bitcast.115, bf16[2304,256]{1,0:T(8,128)(2,1)S(1)} %bitcast.121), kind=kOutput, calls=%fused_computation.3 | convolution fusion | flops 906166272 | bytes 6291456 | tf_op jit(solution)/shard_map/dot_general | solution.py:153
  78.2 1.1 %convolution_add_fusion = f32[768,256]{1,0:T(8,128)S(1)} fusion(f32[768,256]{1,0:T(8,128)S(1)} %convolution_add_fusion.1, bf16[768,2304]{1,0:T(8,128)(2,1)S(1)} %bitcast.113, bf16[2304,256]{1,0:T(8,128)(2,1)S(1)} %bitcast.120), kind=kOutput, calls=%fused_computation.2 | convolution fusion | flops 906166272 | bytes 6291456 | tf_op jit(solution)/shard_map/dot_general | solution.py:153
  79.3 0.8 %add_convert_fusion = bf16[3,4,64,256]{3,2,1,0:T(8,128)(2,1)} fusion(f32[3,4,64,256]{3,2,1,0:T(8,128)S(1)} %bitcast.128, bf16[3,4,64,256]{3,2,1,0:T(8,128)(2,1)S(1)} %bitcast.106), kind=kLoop, calls=%fused_computation.23 | loop fusion | flops 589824 | bytes 1572864 | tf_op jit(solution)/shard_map/convert_element_type | solution.py:302
  (225 shorter events, 13.0 us)
Async XLA Ops:
  1.4 2.3 %collective-permute-start = (f32[2,32]{1,0:T(2,128)S(1)}, f32[2,32]{1,0:T(2,128)S(1)}, u32[]{:S(2)}, u32[]{:S(2)}) collective-permute-start(f32[2,32]{1,0:T(2,128)S(1)} %pad_maximum_fusion.29), channel_id=1, source_target_pairs={{0,1},{1,0},{2,3},{3,2},{4,5},{5,4},{6,7},{7,6},{8,9},{9,8},{10,11... | collective-permute-start | bytes 776 | tf_op jit(solution)/shard_map/ppermute | solution.py:170
  1.9 2.1 %slice-start = ((bf16[3,2,32,512]{3,2,1,0:T(8,128)(2,1)}), bf16[3,1,32,512]{3,2,1,0:T(8,128)(2,1)S(1)}, s32[]{:S(2)}) async-start(bf16[3,2,32,512]{3,2,1,0:T(8,128)(2,1)} %param.10), calls=%async_computation | async-start | bytes 196608 | tf_op jit(solution)/shard_map/slice | solution.py:259
  1.9 13.1 %copy-start = (bf16[3,2,32,512]{3,2,1,0:T(8,128)(2,1)S(1)}, bf16[3,2,32,512]{3,2,1,0:T(8,128)(2,1)}, u32[]{:S(2)}) copy-start(bf16[3,2,32,512]{3,2,1,0:T(8,128)(2,1)} %param.10) | copy-start | bytes 589828
  1.9 18.1 %copy-start.6 = (f32[512]{0:T(512)S(1)}, f32[512]{0:T(512)}, u32[]{:S(2)}) copy-start(f32[512]{0:T(512)} %param.12) | copy-start | bytes 6148
  2.0 18.1 %copy-start.7 = (f32[512]{0:T(512)S(1)}, f32[512]{0:T(512)}, u32[]{:S(2)}) copy-start(f32[512]{0:T(512)} %param.11) | copy-start | bytes 6148
  4.1 6.3 %collective-permute-start.1 = (bf16[97,512]{1,0:T(8,128)(2,1)S(1)}, bf16[97,512]{1,0:T(8,128)(2,1)S(1)}, u32[]{:S(2)}, u32[]{:S(2)}) collective-permute-start(bf16[97,512]{1,0:T(8,128)(2,1)S(1)} %pad_maximum_fusion.24), channel_id=1, source_target_pairs={{0,4},{4,0},{8,12},{12,8},{1,5},{5,1},{9,13},{13,9},{2,6},{6,2},{1... | collective-permute-start | bytes 297992 | tf_op jit(solution)/shard_map/ppermute | solution.py:170
  6.9 8.1 %collective-permute-start.2 = (bf16[97,512]{1,0:T(8,128)(2,1)S(1)}, bf16[97,512]{1,0:T(8,128)(2,1)S(1)}, u32[]{:S(2)}, u32[]{:S(2)}) collective-permute-start(bf16[97,512]{1,0:T(8,128)(2,1)S(1)} %pad_maximum_fusion.24), channel_id=1, source_target_pairs={{0,12},{4,8},{8,4},{12,0},{1,13},{5,9},{9,5},{13,1},{2,14},{6,10},... | collective-permute-start | bytes 297992 | tf_op jit(solution)/shard_map/ppermute | solution.py:170
  9.3 6.0 %collective-permute-start.3 = (f32[2,32]{1,0:T(2,128)S(1)}, f32[2,32]{1,0:T(2,128)S(1)}, u32[]{:S(2)}, u32[]{:S(2)}) collective-permute-start(f32[2,32]{1,0:T(2,128)S(1)} %get-tuple-element.29), channel_id=1, source_target_pairs={{0,8},{4,12},{8,0},{12,4},{1,9},{5,13},{9,1},{13,5},{2,10},{6,14},... | collective-permute-start | bytes 776 | tf_op jit(solution)/shard_map/ppermute | solution.py:170
  15.7 3.8 %collective-permute-start.4 = (bf16[10,512]{1,0:T(8,128)(2,1)S(1)}, bf16[10,512]{1,0:T(8,128)(2,1)S(1)}, u32[]{:S(2)}, u32[]{:S(2)}) collective-permute-start(bf16[10,512]{1,0:T(8,128)(2,1)S(1)} %pad_maximum_fusion.26), channel_id=1, source_target_pairs={{0,2},{2,0},{1,3},{3,1},{4,6},{6,4},{5,7},{7,5},{8,10},{10,8},{9,1... | collective-permute-start | bytes 30728 | tf_op jit(solution)/shard_map/ppermute | solution.py:170
  25.2 3.7 %collective-permute-start.5 = (bf16[13,256]{1,0:T(8,128)(2,1)S(1)}, bf16[13,256]{1,0:T(8,128)(2,1)S(1)}, u32[]{:S(2)}, u32[]{:S(2)}) collective-permute-start(bf16[13,256]{1,0:T(8,128)(2,1)S(1)} %pad_maximum_fusion.27), channel_id=1, source_target_pairs={{0,2},{2,0},{1,3},{3,1},{4,6},{6,4},{5,7},{7,5},{8,10},{10,8},{9,1... | collective-permute-start | bytes 19976 | tf_op jit(solution)/shard_map/ppermute | solution.py:170
  29.7 4.7 %collective-permute-start.6 = (bf16[199,256]{1,0:T(8,128)(2,1)S(1)}, bf16[199,256]{1,0:T(8,128)(2,1)S(1)}, u32[]{:S(2)}, u32[]{:S(2)}) collective-permute-start(bf16[199,256]{1,0:T(8,128)(2,1)S(1)} %get-tuple-element.69), channel_id=1, source_target_pairs={{0,4},{4,0},{8,12},{12,8},{1,5},{5,1},{9,13},{13,9},{2,6},{6,2},{1... | collective-permute-start | bytes 305672 | tf_op jit(solution)/shard_map/ppermute | solution.py:170
  30.5 6.5 %collective-permute-start.7 = (bf16[199,256]{1,0:T(8,128)(2,1)S(1)}, bf16[199,256]{1,0:T(8,128)(2,1)S(1)}, u32[]{:S(2)}, u32[]{:S(2)}) collective-permute-start(bf16[199,256]{1,0:T(8,128)(2,1)S(1)} %get-tuple-element.70), channel_id=1, source_target_pairs={{0,12},{4,8},{8,4},{12,0},{1,13},{5,9},{9,5},{13,1},{2,14},{6,10},... | collective-permute-start | bytes 305672 | tf_op jit(solution)/shard_map/ppermute | solution.py:170
  33.2 4.5 %collective-permute-start.8 = (f32[2,32]{1,0:T(2,128)S(1)}, f32[2,32]{1,0:T(2,128)S(1)}, u32[]{:S(2)}, u32[]{:S(2)}) collective-permute-start(f32[2,32]{1,0:T(2,128)S(1)} %get-tuple-element.24), channel_id=1, source_target_pairs={{0,8},{4,12},{8,0},{12,4},{1,9},{5,13},{9,1},{13,5},{2,10},{6,14},... | collective-permute-start | bytes 776 | tf_op jit(solution)/shard_map/ppermute | solution.py:170
  38.1 3.9 %collective-permute-start.9 = (bf16[793,256]{1,0:T(8,128)(2,1)S(1)}, bf16[793,256]{1,0:T(8,128)(2,1)S(1)}, u32[]{:S(2)}, u32[]{:S(2)}) collective-permute-start(bf16[793,256]{1,0:T(8,128)(2,1)S(1)} %pad_maximum_fusion.8), channel_id=1, source_target_pairs={{0,1},{1,0},{2,3},{3,2},{4,5},{5,4},{6,7},{7,6},{8,9},{9,8},{10,11... | collective-permute-start | bytes 1218056 | tf_op jit(solution)/shard_map/ppermute | solution.py:170
  41.9 0.8 %copy-start.8 = (f32[256]{0:T(256)S(1)}, f32[256]{0:T(256)}, u32[]{:S(2)}) copy-start(f32[256]{0:T(256)} %param.15) | copy-start | bytes 3076
  41.9 0.8 %copy-start.9 = (f32[256]{0:T(256)S(1)}, f32[256]{0:T(256)}, u32[]{:S(2)}) copy-start(f32[256]{0:T(256)} %param.14) | copy-start | bytes 3076
  46.4 1.3 %copy-start.4 = (bf16[1,3,3,256,256]{4,3,2,1,0:T(8,128)(2,1)S(1)}, bf16[1,3,3,256,256]{4,3,2,1,0:T(8,128)(2,1)}, u32[]{:S(2)}) copy-start(bf16[1,3,3,256,256]{4,3,2,1,0:T(8,128)(2,1)} %get-tuple-element.40) | copy-start | bytes 3538948
  47.7 1.3 %copy-start.3 = (bf16[1,3,3,256,256]{4,3,2,1,0:T(8,128)(2,1)S(1)}, bf16[1,3,3,256,256]{4,3,2,1,0:T(8,128)(2,1)}, u32[]{:S(2)}) copy-start(bf16[1,3,3,256,256]{4,3,2,1,0:T(8,128)(2,1)} %get-tuple-element.41) | copy-start | bytes 3538948
  51.9 3.7 %collective-permute-start.10 = (bf16[13,256]{1,0:T(8,128)(2,1)S(1)}, bf16[13,256]{1,0:T(8,128)(2,1)S(1)}, u32[]{:S(2)}, u32[]{:S(2)}) collective-permute-start(bf16[13,256]{1,0:T(8,128)(2,1)S(1)} %pad_maximum_fusion.28), channel_id=1, source_target_pairs={{0,2},{2,0},{1,3},{3,1},{4,6},{6,4},{5,7},{7,5},{8,10},{10,8},{9,1... | collective-permute-start | bytes 19976 | tf_op jit(solution)/shard_map/ppermute | solution.py:170
  56.4 5.8 %collective-permute-start.11 = (bf16[199,256]{1,0:T(8,128)(2,1)S(1)}, bf16[199,256]{1,0:T(8,128)(2,1)S(1)}, u32[]{:S(2)}, u32[]{:S(2)}) collective-permute-start(bf16[199,256]{1,0:T(8,128)(2,1)S(1)} %get-tuple-element.63), channel_id=1, source_target_pairs={{0,4},{4,0},{8,12},{12,8},{1,5},{5,1},{9,13},{13,9},{2,6},{6,2},{1... | collective-permute-start | bytes 305672 | tf_op jit(solution)/shard_map/ppermute | solution.py:170
  56.6 7.1 %collective-permute-start.12 = (bf16[199,256]{1,0:T(8,128)(2,1)S(1)}, bf16[199,256]{1,0:T(8,128)(2,1)S(1)}, u32[]{:S(2)}, u32[]{:S(2)}) collective-permute-start(bf16[199,256]{1,0:T(8,128)(2,1)S(1)} %get-tuple-element.64), channel_id=1, source_target_pairs={{0,12},{4,8},{8,4},{12,0},{1,13},{5,9},{9,5},{13,1},{2,14},{6,10},... | collective-permute-start | bytes 305672 | tf_op jit(solution)/shard_map/ppermute | solution.py:170
  59.1 5.3 %collective-permute-start.13 = (f32[2,32]{1,0:T(2,128)S(1)}, f32[2,32]{1,0:T(2,128)S(1)}, u32[]{:S(2)}, u32[]{:S(2)}) collective-permute-start(f32[2,32]{1,0:T(2,128)S(1)} %get-tuple-element.17), channel_id=1, source_target_pairs={{0,8},{4,12},{8,0},{12,4},{1,9},{5,13},{9,1},{13,5},{2,10},{6,14},... | collective-permute-start | bytes 776 | tf_op jit(solution)/shard_map/ppermute | solution.py:170
  64.7 3.9 %collective-permute-start.14 = (bf16[793,256]{1,0:T(8,128)(2,1)S(1)}, bf16[793,256]{1,0:T(8,128)(2,1)S(1)}, u32[]{:S(2)}, u32[]{:S(2)}) collective-permute-start(bf16[793,256]{1,0:T(8,128)(2,1)S(1)} %pad_maximum_fusion.9), channel_id=1, source_target_pairs={{0,1},{1,0},{2,3},{3,2},{4,5},{5,4},{6,7},{7,6},{8,9},{9,8},{10,11... | collective-permute-start | bytes 1218056 | tf_op jit(solution)/shard_map/ppermute | solution.py:170
  68.6 2.6 %copy-start.10 = (f32[256]{0:T(256)S(1)}, f32[256]{0:T(256)}, u32[]{:S(2)}) copy-start(f32[256]{0:T(256)} %param.18) | copy-start | bytes 3076
  68.6 2.6 %copy-start.11 = (f32[256]{0:T(256)S(1)}, f32[256]{0:T(256)}, u32[]{:S(2)}) copy-start(f32[256]{0:T(256)} %param.17) | copy-start | bytes 3076
  68.6 0.8 copy-start.5
  74.6 1.3 %copy-start.2 = (bf16[1,3,3,256,256]{4,3,2,1,0:T(8,128)(2,1)S(1)}, bf16[1,3,3,256,256]{4,3,2,1,0:T(8,128)(2,1)}, u32[]{:S(2)}) copy-start(bf16[1,3,3,256,256]{4,3,2,1,0:T(8,128)(2,1)} %get-tuple-element.37) | copy-start | bytes 3538948
  75.9 1.3 %copy-start.1 = (bf16[1,3,3,256,256]{4,3,2,1,0:T(8,128)(2,1)S(1)}, bf16[1,3,3,256,256]{4,3,2,1,0:T(8,128)(2,1)}, u32[]{:S(2)}) copy-start(bf16[1,3,3,256,256]{4,3,2,1,0:T(8,128)(2,1)} %get-tuple-element.38) | copy-start | bytes 3538948

commit v22 on v19

--- a/solution.py
+++ b/solution.py
@@ -84,7 +84,7 @@
 def activate(values, stats, scale_vec, shift_vec):
     average, scaling = stats
     normed = (values - average) * scaling * scale_vec + shift_vec
-    return jax.nn.silu(normed)
+    return 0.5 * normed * (1.0 + jnp.tanh(0.5 * normed))
 
 
 def inside_mask(rows, cols, low_pad):
@@ -142,12 +142,11 @@
     return jnp.concatenate([even, odd], axis=2).reshape(frames, 2 * height, 2 * across, out)
 
 
-def valid_conv(padded, kernel, frames, height, across):
+def valid_conv(padded, kernel, frames, height, across, result=None):
     channels = padded.shape[-1]
     wide = jnp.concatenate(
         [padded[:, dy : dy + height, dx : dx + across] for dy in range(3) for dx in range(3)], axis=-1
     )
-    result = None
     for step_t in range(3):
         window = wide[step_t : step_t + frames].reshape(-1, 9 * channels)
         part = jnp.dot(
@@ -266,7 +265,7 @@
     return finish_stats(sums, values), x
 
 
-def norm_conv(values, gain, shift, kernel):
+def norm_conv(values, gain, shift, kernel, result=None):
     frames, height, across, _ = values.shape
     if fast_mesh():
         act = fast_conv_input(values, gain, shift)
@@ -275,7 +274,7 @@
         extended = conv_halo(values)
         act = activate(extended.astype(jnp.float32), stats, gain, shift)
         act = jnp.where(inside_mask(height + 2, across + 2, 1), act, 0.0).astype(jnp.bfloat16)
-    return valid_conv(act, kernel, frames, height, across)
+    return valid_conv(act, kernel, frames, height, across, result)
 
 
 def per_device(
@@ -300,8 +299,9 @@
     activated = jnp.where(inside_mask(height + 1, across + 1, 0), activated, 0.0)
     lifted = upsample(activated.astype(jnp.bfloat16), up_weight).astype(jnp.bfloat16)
     hidden = norm_conv(lifted, norm2_gain, norm2_shift, conv_a).astype(jnp.bfloat16)
-    branch = norm_conv(hidden, norm3_gain, norm3_shift, conv_b)
-    return (lifted.astype(jnp.float32) + branch).astype(jnp.bfloat16)
+    residual = lifted.astype(jnp.float32).reshape(-1, lifted.shape[-1])
+    decoded = norm_conv(hidden, norm3_gain, norm3_shift, conv_b, residual)
+    return decoded.astype(jnp.bfloat16)
 
 
 def solution(mesh):

time: 78.2 us -> 105 us (1.34)
  local copies, waits for them, and re-layouts: 13 us -> 29.5 us
  other arithmetic: 11.4 us -> 20.7 us
    reshape x8, local copies, waits for them, and re-layouts: 0.2 us -> 3.42 us  [swap_with(): message = jnp.concatenate([payload.reshape(-1, width), packed], axis=0)]
    add x9, local copies, waits for them, and re-layouts: 0.74 us -> 3.7 us  [unpack_sums(): return flat[0] + flat[1] + flat[2]]
    slice x2, local copies, waits for them, and re-layouts: 4.43 us -> 2.45 us  [valid_conv(): kernel[step_t].reshape(9 * channels, -1)]
    unnamed x15 -> x29, local copies, waits for them, and re-layouts: 0.05 us -> 1.92 us
    broadcast_in_dim x6, local copies, waits for them, and re-layouts: 0.42 us -> 2.21 us  [finish_stats(): return (jnp.repeat(average, group_width), jnp.repeat(scaling, group_width))]
    another operation x12, other arithmetic: 0.15 us -> 1.87 us
    select_n x2, other arithmetic: 0.05 us -> 1.65 us  [ha_round(): above = jnp.where(h % 2 == 1, got_first, got_third)]
    select_n x3, local copies, waits for them, and re-layouts: 0.09 us -> 1.63 us  [ha_round(): below = jnp.where(h % 2 == 0, got_first, got_third)]
  transfers between devices with their start and end apart: 17 -> 17, of which waited for: 11 -> 12; matrix products, arithmetic and copies ran while one was open for 10% -> 9% of each run, Pallas kernels for 0% -> 0%
where the time goes in v22:
time: 105 us; the launch traced here: 104 us
  local copies, waits for them, and re-layouts  29.5 us (28%)
  starting transfers between devices  23 us (22%)
  waiting for transfers between devices  21 us (20%)
  other arithmetic  20.7 us (20%)
  matrix products  9.31 us (9%)
    ppermute x15, starting transfers between devices, swap(): return lax.ppermute(x, axis, [(i, i ^ distance) for i in range(size)])  20.1 us
    ppermute x15, waiting for transfers between devices, swap(): return lax.ppermute(x, axis, [(i, i ^ distance) for i in range(size)])  20 us
    dot_general x6, matrix products, valid_conv(): jnp.dot(window, kernel[step_t].reshape(9 * channels, -1), preferred_eleme...  7.24 us
    add x9, local copies, waits for them, and re-layouts, unpack_sums(): return flat[0] + flat[1] + flat[2]  3.7 us
    reshape x8, local copies, waits for them, and re-layouts, swap_with(): message = jnp.concatenate([payload.reshape(-1, width), packed], axis=0)  3.42 us
    unnamed x16, other arithmetic  3.03 us
    ppermute x2, starting transfers between devices, passed_along(): return lax.ppermute(block, axis, route)  2.95 us
    slice x2, local copies, waits for them, and re-layouts, valid_conv(): kernel[step_t].reshape(9 * channels, -1)  2.45 us
  transfers between devices with their start and end apart: 17, of which 12 were waited for; matrix products, arithmetic and copies ran while one was open for 9% of the time, Pallas kernels for 0%

profile of v22, /device:TPU:0, one launch (start us, length us, event | category | flops | bytes accessed | tf_op | source)
XLA Modules:
  0.0 104.4 jit_solution(4697807801787259195)
XLA Ops:
  0.0 1.0 convert_reduce_fusion.1
  2.0 1.7 %slice_bitcast_fusion.7 = (bf16[512,256]{1,0:T(8,128)(2,1)S(1)}, bf16[512,256]{1,0:T(8,128)(2,1)S(1)}, bf16[512,256]{1,0:T(8,128)(2,1)S(1)}, bf16[512,256]{1,0:T...) fusion(bf16[3,3,512,256]{3,2,1,0:T(8,128)(2,1)} %param.13), kind=kLoop, calls=%fused_computation.117 | loop fusion | bytes 4194304 | tf_op jit(solution)/shard_map/squeeze | solution.py:129
  4.2 2.6 %collective-permute-start.1 = (bf16[7,512]{1,0:T(8,128)(2,1)S(1)}, bf16[7,512]{1,0:T(8,128)(2,1)S(1)}, u32[]{:S(2)}, u32[]{:S(2)}) collective-permute-start(bf16[7,512]{1,0:T(8,128)(2,1)S(1)} %pad_maximum_fusion.15), channel_id=1, source_target_pairs={{0,2},{2,0},{1,3},{3,1},{4,6},{6,4},{5,7},{7,5},{8,10},{10,8},{9,1... | collective-permute-start | bytes 21512 | tf_op jit(solution)/shard_map/ppermute | solution.py:169
  6.8 1.6 %collective-permute-done.1 = bf16[7,512]{1,0:T(8,128)(2,1)S(1)} collective-permute-done((bf16[7,512]{1,0:T(8,128)(2,1)S(1)}, bf16[7,512]{1,0:T(8,128)(2,1)S(1)}, u32[]{:S(2)}, u32[]{:S(2)}) %collective-permute-start.1) | collective-permute-done | bytes 7200 | tf_op jit(solution)/shard_map/ppermute | solution.py:169
  9.1 2.2 %collective-permute-start.2 = (bf16[100,512]{1,0:T(8,128)(2,1)S(1)}, bf16[100,512]{1,0:T(8,128)(2,1)S(1)}, u32[]{:S(2)}, u32[]{:S(2)}) collective-permute-start(bf16[100,512]{1,0:T(8,128)(2,1)S(1)} %pad_maximum_fusion.14), channel_id=1, source_target_pairs={{0,4},{4,0},{8,12},{12,8},{1,5},{5,1},{9,13},{13,9},{2,6},{6,2},{1... | collective-permute-start | bytes 307208 | tf_op jit(solution)/shard_map/ppermute | solution.py:169
  11.3 2.5 %collective-permute-start.3 = (bf16[100,512]{1,0:T(8,128)(2,1)S(1)}, bf16[100,512]{1,0:T(8,128)(2,1)S(1)}, u32[]{:S(2)}, u32[]{:S(2)}) collective-permute-start(bf16[100,512]{1,0:T(8,128)(2,1)S(1)} %pad_maximum_fusion.14), channel_id=1, source_target_pairs={{0,12},{4,8},{8,4},{12,0},{1,13},{5,9},{9,5},{13,1},{2,14},{6,10},... | collective-permute-start | bytes 307208 | tf_op jit(solution)/shard_map/ppermute | solution.py:169
  14.2 4.1 %collective-permute-done.3 = bf16[100,512]{1,0:T(8,128)(2,1)S(1)} collective-permute-done((bf16[100,512]{1,0:T(8,128)(2,1)S(1)}, bf16[100,512]{1,0:T(8,128)(2,1)S(1)}, u32[]{:S(2)}, u32[]{:S(2)}) %collective-permute-start.3) | collective-permute-done | bytes 102432 | tf_op jit(solution)/shard_map/ppermute | solution.py:169
  20.7 1.2 %convolution_add_fusion.5 = bf16[192,256]{1,0:T(8,128)(2,1)S(1)} fusion(bf16[192,512]{1,0:T(8,128)(2,1)S(1)} %bitcast.118, bf16[3,3,512,256]{3,2,1,0:T(8,128)(2,1)} %param.13, f32[192,512]{1,0:T(8,128)S(1)} %fusion.49, f32[192,512]{1,0:T(8,128)S(1)} %fusion.45, f32[192,1024]{1,0:T(8,128)S(1)} %fusion.2), kind=kOutput, calls=%fused_computation.41 | convolution fusion | flops 50528256 | bytes 1146880 | tf_op jit(solution)/shard_map/dot_general | solution.py:123
  22.5 0.8 convert_reduce_fusion.2
  24.0 1.0 collective-permute-done.5
  25.4 1.6 %collective-permute-start.6 = (bf16[13,256]{1,0:T(8,128)(2,1)S(1)}, bf16[13,256]{1,0:T(8,128)(2,1)S(1)}, u32[]{:S(2)}, u32[]{:S(2)}) collective-permute-start(bf16[13,256]{1,0:T(8,128)(2,1)S(1)} %pad_maximum_fusion.16), channel_id=1, source_target_pairs={{0,2},{2,0},{1,3},{3,1},{4,6},{6,4},{5,7},{7,5},{8,10},{10,8},{9,1... | collective-permute-start | bytes 19976 | tf_op jit(solution)/shard_map/ppermute | solution.py:169
  27.0 2.1 %collective-permute-done.6 = bf16[13,256]{1,0:T(8,128)(2,1)S(1)} collective-permute-done((bf16[13,256]{1,0:T(8,128)(2,1)S(1)}, bf16[13,256]{1,0:T(8,128)(2,1)S(1)}, u32[]{:S(2)}, u32[]{:S(2)}) %collective-permute-start.6) | collective-permute-done | bytes 6688 | tf_op jit(solution)/shard_map/ppermute | solution.py:169
  30.7 2.6 %collective-permute-start.9 = (f32[2,32]{1,0:T(2,128)S(1)}, f32[2,32]{1,0:T(2,128)S(1)}, u32[]{:S(2)}, u32[]{:S(2)}) collective-permute-start(f32[2,32]{1,0:T(2,128)S(1)} %get-tuple-element.22), channel_id=1, source_target_pairs={{0,8},{4,12},{8,0},{12,4},{1,9},{5,13},{9,1},{13,5},{2,10},{6,14},... | collective-permute-start | bytes 776 | tf_op jit(solution)/shard_map/ppermute | solution.py:169
  33.2 1.2 %collective-permute-start.8 = (bf16[199,256]{1,0:T(8,128)(2,1)S(1)}, bf16[199,256]{1,0:T(8,128)(2,1)S(1)}, u32[]{:S(2)}, u32[]{:S(2)}) collective-permute-start(bf16[199,256]{1,0:T(8,128)(2,1)S(1)} %get-tuple-element.68), channel_id=1, source_target_pairs={{0,12},{4,8},{8,4},{12,0},{1,13},{5,9},{9,5},{13,1},{2,14},{6,10},... | collective-permute-start | bytes 305672 | tf_op jit(solution)/shard_map/ppermute | solution.py:169
  34.7 4.9 %collective-permute-done.8 = bf16[199,256]{1,0:T(8,128)(2,1)S(1)} collective-permute-done((bf16[199,256]{1,0:T(8,128)(2,1)S(1)}, bf16[199,256]{1,0:T(8,128)(2,1)S(1)}, u32[]{:S(2)}, u32[]{:S(2)}) %collective-permute-start.8) | collective-permute-done | bytes 101920 | tf_op jit(solution)/shard_map/ppermute | solution.py:169
  41.0 1.5 %collective-permute-start.10 = (bf16[2,6,66,256]{3,2,1,0:T(8,128)(2,1)S(1)}, bf16[2,6,66,256]{3,2,1,0:T(8,128)(2,1)S(1)}, u32[]{:S(2)}, u32[]{:S(2)}) collective-permute-start(bf16[2,6,66,256]{3,2,1,0:T(8,128)(2,1)S(1)} %slice.621), channel_id=1, source_target_pairs={{0,1},{2,3},{4,5},{6,7},{8,9},{10,11},{12,13},{14,15},{16,17},{18,... | collective-permute-start | bytes 1216520 | tf_op jit(solution)/shard_map/ppermute | solution.py:15
  42.6 2.2 %fusion.133 = (bf16[1,3,3,256,256]{4,3,2,1,0:T(8,128)(2,1)S(1)}, bf16[1,3,3,256,256]{4,3,2,1,0:T(8,128)(2,1)S(1)}, bf16[1,3,3,256,256]{4,3,2,1,0:T(8,128)(2,1)S(1)}) fusion(bf16[3,3,3,256,256]{4,3,2,1,0:T(8,128)(2,1)} %param.16), kind=kLoop, calls=%fused_computation.289 | loop fusion | bytes 7077888 | tf_op jit(solution)/shard_map/slice | solution.py:153
  46.7 1.0 fusion.131
  47.7 1.1 %fusion.136 = f32[768,256]{1,0:T(8,128)S(1)} fusion(bf16[768,2304]{1,0:T(8,128)(2,1)S(1)} %bitcast.108, bf16[2304,256]{1,0:T(8,128)(2,1)S(1)} %bitcast.117), kind=kOutput, calls=%fused_computation.292 | convolution fusion | flops 905969664 | bytes 5505024 | tf_op jit(solution)/shard_map/dot_general | solution.py:152
  48.8 1.1 %convolution_add_fusion.4 = f32[768,256]{1,0:T(8,128)S(1)} fusion(f32[768,256]{1,0:T(8,128)S(1)} %fusion.136, bf16[768,2304]{1,0:T(8,128)(2,1)S(1)} %bitcast.106, bf16[2304,256]{1,0:T(8,128)(2,1)S(1)} %bitcast.116), kind=kOutput, calls=%fused_computation.38 | convolution fusion | flops 906166272 | bytes 6291456 | tf_op jit(solution)/shard_map/dot_general | solution.py:152
  49.9 1.1 %convert_reduce_fusion = (f32[256]{0:T(256)S(1)}, f32[256]{0:T(256)S(1)}, bf16[768,256]{1,0:T(8,128)(2,1)S(1)}) fusion(f32[768,256]{1,0:T(8,128)S(1)} %convolution_add_fusion.4, bf16[768,2304]{1,0:T(8,128)(2,1)S(1)} %bitcast.103, bf16[2304,256]{1,0:T(8,128)(2,1)S(1)} %bitcast.113), kind=kOutput, calls=%fused_computation.51 | convolution fusion | flops 907148800 | bytes 5900288 | tf_op jit(solution)/shard_map/dot_general | solution.py:152
  51.6 1.1 %collective-permute-done.11 = f32[2,32]{1,0:T(2,128)S(1)} collective-permute-done((f32[2,32]{1,0:T(2,128)S(1)}, f32[2,32]{1,0:T(2,128)S(1)}, u32[]{:S(2)}, u32[]{:S(2)}) %collective-permute-start.11) | collective-permute-done | bytes 288 | tf_op jit(solution)/shard_map/ppermute | solution.py:169
  53.6 1.5 %collective-permute-start.12 = (bf16[13,256]{1,0:T(8,128)(2,1)S(1)}, bf16[13,256]{1,0:T(8,128)(2,1)S(1)}, u32[]{:S(2)}, u32[]{:S(2)}) collective-permute-start(bf16[13,256]{1,0:T(8,128)(2,1)S(1)} %pad_maximum_fusion.17), channel_id=1, source_target_pairs={{0,2},{2,0},{1,3},{3,1},{4,6},{6,4},{5,7},{7,5},{8,10},{10,8},{9,1... | collective-permute-start | bytes 19976 | tf_op jit(solution)/shard_map/ppermute | solution.py:169
  55.1 2.2 %collective-permute-done.12 = bf16[13,256]{1,0:T(8,128)(2,1)S(1)} collective-permute-done((bf16[13,256]{1,0:T(8,128)(2,1)S(1)}, bf16[13,256]{1,0:T(8,128)(2,1)S(1)}, u32[]{:S(2)}, u32[]{:S(2)}) %collective-permute-start.12) | collective-permute-done | bytes 6688 | tf_op jit(solution)/shard_map/ppermute | solution.py:169
  58.7 1.7 %reshape.672 = bf16[198,256]{1,0:T(8,128)(2,1)} reshape(bf16[3,1,66,256]{3,2,1,0:T(8,128)(2,1)} %broadcast_select_fusion) | data formatting | bytes 202752 | tf_op jit(solution)/shard_map/reshape | solution.py:220
  60.4 1.6 %reshape.667 = bf16[198,256]{1,0:T(8,128)(2,1)} reshape(bf16[3,1,66,256]{3,2,1,0:T(8,128)(2,1)} %get-tuple-element.11) | data formatting | bytes 202752 | tf_op jit(solution)/shard_map/reshape | solution.py:220
  63.4 1.2 %fusion.96 = (bf16[2,32]{1,0:T(2,128)(2,1)}, f32[2,32]{1,0:T(2,128)S(1)}) fusion(f32[2,32]{1,0:T(2,128)} %copy-done.8, f32[2,32]{1,0:T(2,128)} %add.281), kind=kLoop, calls=%fused_computation.231 | loop fusion | flops 320 | bytes 896 | tf_op jit(solution)/shard_map/convert.6
  65.2 1.3 %reshape.669 = bf16[64]{0:T(256)(128)(2,1)} reshape(bf16[2,32]{1,0:T(2,128)(2,1)} %get-tuple-element.63) | data formatting | bytes 256 | tf_op jit(solution)/shard_map/reshape | solution.py:206
  66.4 1.3 %reshape.670 = bf16[64]{0:T(256)(128)(2,1)} reshape(bf16[2,32]{1,0:T(2,128)(2,1)} %get-tuple-element.64) | data formatting | bytes 256 | tf_op jit(solution)/shard_map/reshape | solution.py:206
  67.8 1.2 %reshape.668 = bf16[64]{0:T(256)(128)(2,1)} reshape(bf16[2,32]{1,0:T(2,128)(2,1)} %get-tuple-element.14) | data formatting | bytes 256 | tf_op jit(solution)/shard_map/reshape | solution.py:206
  69.7 1.0 pad_maximum_fusion.7
  70.8 1.8 %collective-permute-start.15 = (f32[2,32]{1,0:T(2,128)S(1)}, f32[2,32]{1,0:T(2,128)}, u32[]{:S(2)}, u32[]{:S(2)}) collective-permute-start(f32[2,32]{1,0:T(2,128)S(1)} %get-tuple-element.15), channel_id=1, source_target_pairs={{0,8},{4,12},{8,0},{12,4},{1,9},{5,13},{9,1},{13,5},{2,10},{6,14},... | collective-permute-start | bytes 776 | tf_op jit(solution)/shard_map/ppermute | solution.py:169
  72.6 2.6 %collective-permute-start.14 = (bf16[199,256]{1,0:T(8,128)(2,1)S(1)}, bf16[199,256]{1,0:T(8,128)(2,1)S(1)}, u32[]{:S(2)}, u32[]{:S(2)}) collective-permute-start(bf16[199,256]{1,0:T(8,128)(2,1)S(1)} %get-tuple-element.62), channel_id=1, source_target_pairs={{0,12},{4,8},{8,4},{12,0},{1,13},{5,9},{9,5},{13,1},{2,14},{6,10},... | collective-permute-start | bytes 305672 | tf_op jit(solution)/shard_map/ppermute | solution.py:169
  76.7 2.3 %collective-permute-done.14 = bf16[199,256]{1,0:T(8,128)(2,1)S(1)} collective-permute-done((bf16[199,256]{1,0:T(8,128)(2,1)S(1)}, bf16[199,256]{1,0:T(8,128)(2,1)S(1)}, u32[]{:S(2)}, u32[]{:S(2)}) %collective-permute-start.14) | collective-permute-done | bytes 101920 | tf_op jit(solution)/shard_map/ppermute | solution.py:169
  80.3 1.3 %add.285 = f32[2,32]{1,0:T(2,128)} reshape(f32[64]{0:T(128)} %fusion.107) | data formatting | bytes 512 | tf_op jit(solution)/shard_map/add | solution.py:214
  81.6 1.3 %add.289 = f32[2,32]{1,0:T(2,128)} reshape(f32[64]{0:T(128)} %fusion.106) | data formatting | bytes 512 | tf_op jit(solution)/shard_map/add | solution.py:214
  85.6 1.3 %broadcast_in_dim.69 = f32[32,8]{1,0:T(8,128)} broadcast(f32[32]{0:T(128)} %multiply_bitcast_fusion), dimensions={0} | broadcast | bytes 1152 | tf_op jit(solution)/shard_map/broadcast_in_dim | solution.py:193
  86.8 1.4 %sub.209 = f32[256]{0:T(256)} reshape(f32[32,8]{1,0:T(8,128)} %broadcast_in_dim.69) | data formatting | bytes 2048 | tf_op jit(solution)/shard_map/sub | solution.py:86
  88.2 1.6 %broadcast_select_fusion.6 = (bf16[198,256]{1,0:T(8,128)(2,1)}, bf16[198,256]{1,0:T(8,128)(2,1)}) fusion(pred[]{:T(512)S(6)} %eq.36, bf16[199,256]{1,0:T(8,128)(2,1)} %copy-done.6, bf16[199,256]{1,0:T(8,128)(2,1)} %copy-done.5, pred[]{:T(512)S(6)} %eq.34), kind=kLoop, calls=%fused_computation.140 | loop fusion | flops 101376 | bytes 405506 | tf_op jit(solution)/shard_map/jit(_where)/select_n | solution.py:234
  89.8 1.6 %select_n.189 = bf16[3,1,66,256]{3,2,1,0:T(8,128)(2,1)} reshape(bf16[198,256]{1,0:T(8,128)(2,1)} %get-tuple-element.57) | data formatting | bytes 202752 | tf_op jit(solution)/shard_map/jit(_where)/select_n | solution.py:234
  91.4 1.6 %select_n.191 = bf16[3,1,66,256]{3,2,1,0:T(8,128)(2,1)} reshape(bf16[198,256]{1,0:T(8,128)(2,1)} %get-tuple-element.58) | data formatting | bytes 202752 | tf_op jit(solution)/shard_map/jit(_where)/select_n | solution.py:235
  93.0 1.6 %select_convert_fusion = bf16[3,6,66,256]{3,2,1,0:T(8,128)(2,1)S(1)} fusion(bf16[3,1,66,256]{3,2,1,0:T(8,128)(2,1)} %select_n.191, bf16[3,4,1,256]{3,2,1,0:T(2,128)(2,1)S(1)} %reshape.679, bf16[3,4,64,256]{3,2,1,0:T(8,128)(2,1)} %bitcast.111, bf16[3,1,66,256]{3,2,1,0:T(8,128)(2,1)} %select_n.189, f32[256]{0:T(256)} %param.18, f32[256]{0:T(256)} %param.17, ...), kind=kLoop, calls=%fused_computation.32 | loop fusion | flops 5778432 | bytes 1214860 | tf_op jit(solution)/shard_map/convert_element_type | solution.py:250
  94.7 1.4 %collective-permute-start.16 = (bf16[2,6,66,256]{3,2,1,0:T(8,128)(2,1)S(1)}, bf16[2,6,66,256]{3,2,1,0:T(8,128)(2,1)S(1)}, u32[]{:S(2)}, u32[]{:S(2)}) collective-permute-start(bf16[2,6,66,256]{3,2,1,0:T(8,128)(2,1)S(1)} %slice.659), channel_id=1, source_target_pairs={{0,1},{2,3},{4,5},{6,7},{8,9},{10,11},{12,13},{14,15},{16,17},{18,... | collective-permute-start | bytes 1216520 | tf_op jit(solution)/shard_map/ppermute | solution.py:15
  96.5 1.0 collective-permute-done.16
  99.4 1.0 fusion.130
  100.4 1.1 %convolution_add_fusion.2 = f32[768,256]{1,0:T(8,128)S(1)} fusion(f32[768,256]{1,0:T(8,128)S(1)} %bitcast.119, bf16[768,2304]{1,0:T(8,128)(2,1)S(1)} %bitcast.107, bf16[2304,256]{1,0:T(8,128)(2,1)S(1)} %bitcast.115), kind=kOutput, calls=%fused_computation.36 | convolution fusion | flops 906166272 | bytes 6291456 | tf_op jit(solution)/shard_map/dot_general | solution.py:152
  101.5 1.1 %convolution_add_fusion.1 = f32[768,256]{1,0:T(8,128)S(1)} fusion(f32[768,256]{1,0:T(8,128)S(1)} %convolution_add_fusion.2, bf16[768,2304]{1,0:T(8,128)(2,1)S(1)} %bitcast.105, bf16[2304,256]{1,0:T(8,128)(2,1)S(1)} %bitcast.114), kind=kOutput, calls=%fused_computation.35 | convolution fusion | flops 906166272 | bytes 6291456 | tf_op jit(solution)/shard_map/dot_general | solution.py:152
  102.6 1.8 %fusion.1 = bf16[768,256]{1,0:T(8,128)(2,1)} fusion(f32[768,256]{1,0:T(8,128)S(1)} %convolution_add_fusion.1, bf16[768,2304]{1,0:T(8,128)(2,1)S(1)} %bitcast.104, bf16[2304,256]{1,0:T(8,128)(2,1)S(1)} %bitcast.112), kind=kOutput, calls=%fused_computation.40 | convolution fusion | flops 906362880 | bytes 5898240 | tf_op jit(solution)/shard_map/dot_general | solution.py:152
  (214 shorter events, 24.9 us)
Async XLA Ops:
  1.4 2.4 %collective-permute-start = (f32[2,32]{1,0:T(2,128)S(1)}, f32[2,32]{1,0:T(2,128)S(1)}, u32[]{:S(2)}, u32[]{:S(2)}) collective-permute-start(f32[2,32]{1,0:T(2,128)S(1)} %pad_maximum_fusion.18), channel_id=1, source_target_pairs={{0,1},{1,0},{2,3},{3,2},{4,5},{5,4},{6,7},{7,6},{8,9},{9,8},{10,11... | collective-permute-start | bytes 776 | tf_op jit(solution)/shard_map/ppermute | solution.py:169
  1.9 1.8 %copy-start.4 = (bf16[3,2,32,512]{3,2,1,0:T(8,128)(2,1)S(1)}, bf16[3,2,32,512]{3,2,1,0:T(8,128)(2,1)}, u32[]{:S(2)}) copy-start(bf16[3,2,32,512]{3,2,1,0:T(8,128)(2,1)} %param.10) | copy-start | bytes 589828
  3.6 15.3 %copy-start.10 = (f32[512]{0:T(512)S(1)}, f32[512]{0:T(512)}, u32[]{:S(2)}) copy-start(f32[512]{0:T(512)} %param.12) | copy-start | bytes 6148
  3.6 15.3 %copy-start.11 = (f32[512]{0:T(512)S(1)}, f32[512]{0:T(512)}, u32[]{:S(2)}) copy-start(f32[512]{0:T(512)} %param.11) | copy-start | bytes 6148
  4.2 4.2 %collective-permute-start.1 = (bf16[7,512]{1,0:T(8,128)(2,1)S(1)}, bf16[7,512]{1,0:T(8,128)(2,1)S(1)}, u32[]{:S(2)}, u32[]{:S(2)}) collective-permute-start(bf16[7,512]{1,0:T(8,128)(2,1)S(1)} %pad_maximum_fusion.15), channel_id=1, source_target_pairs={{0,2},{2,0},{1,3},{3,1},{4,6},{6,4},{5,7},{7,5},{8,10},{10,8},{9,1... | collective-permute-start | bytes 21512 | tf_op jit(solution)/shard_map/ppermute | solution.py:169
  9.1 5.0 %collective-permute-start.2 = (bf16[100,512]{1,0:T(8,128)(2,1)S(1)}, bf16[100,512]{1,0:T(8,128)(2,1)S(1)}, u32[]{:S(2)}, u32[]{:S(2)}) collective-permute-start(bf16[100,512]{1,0:T(8,128)(2,1)S(1)} %pad_maximum_fusion.14), channel_id=1, source_target_pairs={{0,4},{4,0},{8,12},{12,8},{1,5},{5,1},{9,13},{13,9},{2,6},{6,2},{1... | collective-permute-start | bytes 307208 | tf_op jit(solution)/shard_map/ppermute | solution.py:169
  11.3 7.0 %collective-permute-start.3 = (bf16[100,512]{1,0:T(8,128)(2,1)S(1)}, bf16[100,512]{1,0:T(8,128)(2,1)S(1)}, u32[]{:S(2)}, u32[]{:S(2)}) collective-permute-start(bf16[100,512]{1,0:T(8,128)(2,1)S(1)} %pad_maximum_fusion.14), channel_id=1, source_target_pairs={{0,12},{4,8},{8,4},{12,0},{1,13},{5,9},{9,5},{13,1},{2,14},{6,10},... | collective-permute-start | bytes 307208 | tf_op jit(solution)/shard_map/ppermute | solution.py:169
  13.7 4.8 %collective-permute-start.4 = (f32[2,32]{1,0:T(2,128)S(1)}, f32[2,32]{1,0:T(2,128)S(1)}, u32[]{:S(2)}, u32[]{:S(2)}) collective-permute-start(f32[2,32]{1,0:T(2,128)S(1)} %get-tuple-element.27), channel_id=1, source_target_pairs={{0,8},{4,12},{8,0},{12,4},{1,9},{5,13},{9,1},{13,5},{2,10},{6,14},... | collective-permute-start | bytes 776 | tf_op jit(solution)/shard_map/ppermute | solution.py:169
  23.4 6.5 %copy-start.1 = (bf16[3,2,2,64,256]{4,1,3,0,2:T(2,128)(2,1)}, bf16[3,2,2,64,256]{4,1,3,0,2:T(2,128)(2,1)S(1)}, u32[]{:S(2)}) copy-start(bf16[3,2,2,64,256]{4,1,3,0,2:T(2,128)(2,1)S(1)} %get-tuple-element.25) | copy-start | bytes 1179652
  23.8 1.2 %collective-permute-start.5 = (f32[2,32]{1,0:T(2,128)S(1)}, f32[2,32]{1,0:T(2,128)S(1)}, u32[]{:S(2)}, u32[]{:S(2)}) collective-permute-start(f32[2,32]{1,0:T(2,128)S(1)} %pad_maximum_fusion.19), channel_id=1, source_target_pairs={{0,1},{1,0},{2,3},{3,2},{4,5},{5,4},{6,7},{7,6},{8,9},{9,8},{10,11... | collective-permute-start | bytes 776 | tf_op jit(solution)/shard_map/ppermute | solution.py:169
  25.4 3.7 %collective-permute-start.6 = (bf16[13,256]{1,0:T(8,128)(2,1)S(1)}, bf16[13,256]{1,0:T(8,128)(2,1)S(1)}, u32[]{:S(2)}, u32[]{:S(2)}) collective-permute-start(bf16[13,256]{1,0:T(8,128)(2,1)S(1)} %pad_maximum_fusion.16), channel_id=1, source_target_pairs={{0,2},{2,0},{1,3},{3,1},{4,6},{6,4},{5,7},{7,5},{8,10},{10,8},{9,1... | collective-permute-start | bytes 19976 | tf_op jit(solution)/shard_map/ppermute | solution.py:169
  29.1 11.3 %copy-start.12 = (f32[256]{0:T(256)S(1)}, f32[256]{0:T(256)}, u32[]{:S(2)}) copy-start(f32[256]{0:T(256)} %param.15) | copy-start | bytes 3076
  29.1 11.3 %copy-start.13 = (f32[256]{0:T(256)S(1)}, f32[256]{0:T(256)}, u32[]{:S(2)}) copy-start(f32[256]{0:T(256)} %param.14) | copy-start | bytes 3076
  29.9 4.7 %collective-permute-start.7 = (bf16[199,256]{1,0:T(8,128)(2,1)S(1)}, bf16[199,256]{1,0:T(8,128)(2,1)S(1)}, u32[]{:S(2)}, u32[]{:S(2)}) collective-permute-start(bf16[199,256]{1,0:T(8,128)(2,1)S(1)} %get-tuple-element.67), channel_id=1, source_target_pairs={{0,4},{4,0},{8,12},{12,8},{1,5},{5,1},{9,13},{13,9},{2,6},{6,2},{1... | collective-permute-start | bytes 305672 | tf_op jit(solution)/shard_map/ppermute | solution.py:169
  30.6 9.7 %copy-start.9 = (pred[6,66]{1,0:T(8,128)(4,1)}, pred[6,66]{1,0:T(8,128)(4,1)S(1)}, u32[]{:S(2)}) copy-start(pred[6,66]{1,0:T(8,128)(4,1)S(1)} %broadcast_and_fusion) | copy-start | bytes 1192
  30.7 9.3 %collective-permute-start.9 = (f32[2,32]{1,0:T(2,128)S(1)}, f32[2,32]{1,0:T(2,128)S(1)}, u32[]{:S(2)}, u32[]{:S(2)}) collective-permute-start(f32[2,32]{1,0:T(2,128)S(1)} %get-tuple-element.22), channel_id=1, source_target_pairs={{0,8},{4,12},{8,0},{12,4},{1,9},{5,13},{9,1},{13,5},{2,10},{6,14},... | collective-permute-start | bytes 776 | tf_op jit(solution)/shard_map/ppermute | solution.py:169
  33.2 6.5 %collective-permute-start.8 = (bf16[199,256]{1,0:T(8,128)(2,1)S(1)}, bf16[199,256]{1,0:T(8,128)(2,1)S(1)}, u32[]{:S(2)}, u32[]{:S(2)}) collective-permute-start(bf16[199,256]{1,0:T(8,128)(2,1)S(1)} %get-tuple-element.68), channel_id=1, source_target_pairs={{0,12},{4,8},{8,4},{12,0},{1,13},{5,9},{9,5},{13,1},{2,14},{6,10},... | collective-permute-start | bytes 305672 | tf_op jit(solution)/shard_map/ppermute | solution.py:169
  41.0 3.8 %collective-permute-start.10 = (bf16[2,6,66,256]{3,2,1,0:T(8,128)(2,1)S(1)}, bf16[2,6,66,256]{3,2,1,0:T(8,128)(2,1)S(1)}, u32[]{:S(2)}, u32[]{:S(2)}) collective-permute-start(bf16[2,6,66,256]{3,2,1,0:T(8,128)(2,1)S(1)} %slice.621), channel_id=1, source_target_pairs={{0,1},{2,3},{4,5},{6,7},{8,9},{10,11},{12,13},{14,15},{16,17},{18,... | collective-permute-start | bytes 1216520 | tf_op jit(solution)/shard_map/ppermute | solution.py:15
  51.0 7.0 %copy-start.3 = (bf16[768,256]{1,0:T(8,128)(2,1)}, bf16[768,256]{1,0:T(8,128)(2,1)S(1)}, u32[]{:S(2)}) copy-start(bf16[768,256]{1,0:T(8,128)(2,1)S(1)} %get-tuple-element.77) | copy-start | bytes 1179652
  51.4 1.2 %collective-permute-start.11 = (f32[2,32]{1,0:T(2,128)S(1)}, f32[2,32]{1,0:T(2,128)S(1)}, u32[]{:S(2)}, u32[]{:S(2)}) collective-permute-start(f32[2,32]{1,0:T(2,128)S(1)} %pad_maximum_fusion.20), channel_id=1, source_target_pairs={{0,1},{1,0},{2,3},{3,2},{4,5},{5,4},{6,7},{7,6},{8,9},{9,8},{10,11... | collective-permute-start | bytes 776 | tf_op jit(solution)/shard_map/ppermute | solution.py:169
  52.6 0.6 copy-start.8
  53.6 3.7 %collective-permute-start.12 = (bf16[13,256]{1,0:T(8,128)(2,1)S(1)}, bf16[13,256]{1,0:T(8,128)(2,1)S(1)}, u32[]{:S(2)}, u32[]{:S(2)}) collective-permute-start(bf16[13,256]{1,0:T(8,128)(2,1)S(1)} %pad_maximum_fusion.17), channel_id=1, source_target_pairs={{0,2},{2,0},{1,3},{3,1},{4,6},{6,4},{5,7},{7,5},{8,10},{10,8},{9,1... | collective-permute-start | bytes 19976 | tf_op jit(solution)/shard_map/ppermute | solution.py:169
  57.3 0.7 copy-start.7
  58.7 37.4 %copy-start = (bf16[3,3,3,256,256]{4,3,2,1,0:T(8,128)(2,1)S(1)}, bf16[3,3,3,256,256]{4,3,2,1,0:T(8,128)(2,1)}, u32[]{:S(2)}) copy-start(bf16[3,3,3,256,256]{4,3,2,1,0:T(8,128)(2,1)} %param.19) | copy-start | bytes 10616836
  70.7 4.7 %collective-permute-start.13 = (bf16[199,256]{1,0:T(8,128)(2,1)S(1)}, bf16[199,256]{1,0:T(8,128)(2,1)S(1)}, u32[]{:S(2)}, u32[]{:S(2)}) collective-permute-start(bf16[199,256]{1,0:T(8,128)(2,1)S(1)} %get-tuple-element.61), channel_id=1, source_target_pairs={{0,4},{4,0},{8,12},{12,8},{1,5},{5,1},{9,13},{13,9},{2,6},{6,2},{1... | collective-permute-start | bytes 305672 | tf_op jit(solution)/shard_map/ppermute | solution.py:169
  70.8 12.1 %collective-permute-start.15 = (f32[2,32]{1,0:T(2,128)S(1)}, f32[2,32]{1,0:T(2,128)}, u32[]{:S(2)}, u32[]{:S(2)}) collective-permute-start(f32[2,32]{1,0:T(2,128)S(1)} %get-tuple-element.15), channel_id=1, source_target_pairs={{0,8},{4,12},{8,0},{12,4},{1,9},{5,13},{9,1},{13,5},{2,10},{6,14},... | collective-permute-start | bytes 776 | tf_op jit(solution)/shard_map/ppermute | solution.py:169
  72.6 6.5 %collective-permute-start.14 = (bf16[199,256]{1,0:T(8,128)(2,1)S(1)}, bf16[199,256]{1,0:T(8,128)(2,1)S(1)}, u32[]{:S(2)}, u32[]{:S(2)}) collective-permute-start(bf16[199,256]{1,0:T(8,128)(2,1)S(1)} %get-tuple-element.62), channel_id=1, source_target_pairs={{0,12},{4,8},{8,4},{12,0},{1,13},{5,9},{9,5},{13,1},{2,14},{6,10},... | collective-permute-start | bytes 305672 | tf_op jit(solution)/shard_map/ppermute | solution.py:169
  75.4 0.6 copy-start.5
  79.0 0.6 copy-start.6
  94.6 1.7 %copy-start.2 = (bf16[3,2,2,64,256]{4,1,3,0,2:T(2,128)(2,1)S(1)}, bf16[3,2,2,64,256]{4,1,3,0,2:T(2,128)(2,1)}, u32[]{:S(2)}) copy-start(bf16[3,2,2,64,256]{4,1,3,0,2:T(2,128)(2,1)} %copy-done.1) | copy-start | bytes 1179652
  94.7 2.8 %collective-permute-start.16 = (bf16[2,6,66,256]{3,2,1,0:T(8,128)(2,1)S(1)}, bf16[2,6,66,256]{3,2,1,0:T(8,128)(2,1)S(1)}, u32[]{:S(2)}, u32[]{:S(2)}) collective-permute-start(bf16[2,6,66,256]{3,2,1,0:T(8,128)(2,1)S(1)} %slice.659), channel_id=1, source_target_pairs={{0,1},{2,3},{4,5},{6,7},{8,9},{10,11},{12,13},{14,15},{16,17},{18,... | collective-permute-start | bytes 1216520 | tf_op jit(solution)/shard_map/ppermute | solution.py:15
